TPU v7x, 32 devices: a whole 2x2x4 slice. The times are simulated.
32 devices in a mesh: pipe: 2 (over core), dp: 8 (over z, x), tensor: 2 (over y).
Axes of the slice: x: 2, y: 2, z: 4, core: 2. Of those that a mesh axis runs over, the one named last changes fastest.
Arguments:
- normed_input: bfloat16 [2, 8, 1024, 4096], P('pipe', None, 'dp')
- key_grad: bfloat16 [2, 8, 1024, 512], P('pipe', None, 'dp', 'tensor')
- live_slots: int32 [2, 8], P('pipe'), may hold values from 0 to 1, as said below
- master: float32 [2, 4096, 512], P('pipe', 'dp', 'tensor'), may hold values from -4 to 4
- first_moment: float32 [2, 4096, 512], P('pipe', 'dp', 'tensor'), may hold values from -0.0009765625 to 0.0009765625
- second_moment: float32 [2, 4096, 512], P('pipe', 'dp', 'tensor'), as said below
Outputs:
- update: bfloat16 [2, 4096, 512], P('pipe', None, 'tensor')
Inputs may be any that keep to these rules, and one draw needn't show every extreme that they name: `live_slots`: in every draw exactly one section has all 8 slots live; every other section has at least one live and at least one dead slot. `second_moment`: every entry is positive.
All inputs are finite; a program needn't handle non-finite values.
Results may differ from a plain program's by a relative error of at most 0.0004.
Values may be sent and summed in bfloat16 or wider, within the bound.
No kernel may reach another device: no remote copies, remote signals or barrier semaphores. Data moves between devices by JAX's collectives and lax.ppermute only.
A program may use at most 64 MiB of HBM per device.

v0:
```python
import jax
import jax.numpy as jnp
from jax import lax
from jax.sharding import PartitionSpec as P

MOMENT_DECAY = 0.9
SQUARE_DECAY = 0.95
FIRST_CORRECTION = 1.0 - 0.9**20
SECOND_CORRECTION = 1.0 - 0.95**20
WEIGHT_DECAY = 0.1
CLIP_NORM = 1.0
EPSILON = 1e-08


def slot_term(inputs, key_grads, live_row, column_count):
    keep_mask = live_row.astype(key_grads.dtype)
    weighted = (key_grads * keep_mask[:, None, None]).reshape(-1, key_grads.shape[2])
    columns = inputs.reshape(-1, column_count)
    return lax.dot_general(
        columns, weighted, (((0,), (0,)), ((), ())), preferred_element_type=jnp.float32
    )


def local(normed_input, key_grad, live_slots, master, first_moment, second_moment):
    inputs = normed_input[0]
    key_grads = key_grad[0]
    live_row = live_slots[0]
    live_count = jnp.sum(live_row)
    features = inputs.shape[2]
    summed = lax.psum_scatter(
        slot_term(inputs, key_grads, live_row, features), "dp", scatter_dimension=0, tiled=True
    )
    tokens_total = (live_count * (inputs.shape[1] * lax.axis_size("dp"))).astype(jnp.float32)
    grad_shard = summed / tokens_total
    squares = lax.psum(jnp.sum(grad_shard * grad_shard), ("pipe", "dp", "tensor"))
    clip_factor = jnp.minimum(1.0, CLIP_NORM / jnp.sqrt(squares))
    clipped = clip_factor * grad_shard
    moment1 = MOMENT_DECAY * first_moment[0] + (1.0 - MOMENT_DECAY) * clipped
    moment2 = SQUARE_DECAY * second_moment[0] + (1.0 - SQUARE_DECAY) * clipped * clipped
    update = (
        moment1 / FIRST_CORRECTION / (jnp.sqrt(moment2 / SECOND_CORRECTION) + EPSILON)
        + WEIGHT_DECAY * master[0]
    )
    update_rows = update.astype(jnp.bfloat16)[None]
    return lax.all_gather(update_rows, "dp", axis=1, tiled=True)


def solution(mesh):
    in_specs = (
        P("pipe", None, "dp", None),
        P("pipe", None, "dp", "tensor"),
        P("pipe", None),
        P("pipe", "dp", "tensor"),
        P("pipe", "dp", "tensor"),
        P("pipe", "dp", "tensor"),
    )
    out_specs = P("pipe", None, "tensor")
    return jax.shard_map(local, mesh=mesh, in_specs=in_specs, out_specs=out_specs, check_vma=False)
```

profile of v0, /device:TPU:0, one launch (start us, length us, event | category | flops | bytes accessed | tf_op | source)
XLA Modules:
  0.0 214.4 jit_solution(13043117699963963438)
XLA Ops:
  6.5 0.0 reduce-scatter.2.cloned.1.call-start
  6.5 1.4 fusion.16
  7.9 0.0 copy-start
  7.9 0.0 copy-start.1
  7.9 0.0 copy-start.2
  7.9 8.0 %fusion.2 = f32[4096,256]{0,1:T(8,128)} fusion(bf16[1,8,128,4096]{3,2,1,0:T(8,128)(2,1)} %param.6, bf16[1,8,128,256]{3,2,1,0:T(8,128)(2,1)} %param.7, bf16[8]{0:T(256)(128)(2,1)S(1)} %get-tuple-element.6), kind=kOutput, calls=%fused_computation.2 | convolution fusion | flops 2147745792 | bytes 13107216 | tf_op jit(solution)/shard_map/dot_general | solution.py:19
  15.9 0.0 reduce-scatter.2.cloned.1.call-update
  16.0 0.0 all-gather.3.cloned.1.call-start
  16.7 0.0 copy-done
  16.7 0.2 copy.10
  16.9 0.0 copy-done.1
  16.9 0.2 copy.7
  17.1 90.0 %reduce-scatter.2.cloned.1.call-done = f32[512,256]{0,1:T(8,128)} async-done(((f32[4096,256]{0,1:T(8,128)}), f32[512,256]{0,1:T(8,128)}) %reduce-scatter.2.cloned.1.call-update) | async-done | bytes 524304 | tf_op jit(solution)/shard_map/reduce_scatter | solution.py:30
  107.1 1.8 multiply_reduce_fusion
  108.9 0.0 copy-done.2
  108.9 0.2 copy.9
  109.1 40.6 %psum.7 = f32[]{:T(128)} all-reduce(f32[]{:T(128)} %multiply_reduce_fusion), channel_id=1, replica_groups=mesh['pipe'=2,'dp'=8,'tensor'=2] {'pipe','dp','tensor'}, use_global_device_ids=true, to_apply=%region_3.0 | all-reduce | flops 1 | bytes 8 | tf_op jit(solution)/shard_map/psum | solution.py:35
  150.4 2.2 %fusion.14 = bf16[512,256]{0,1:T(8,128)(2,1)} fusion(f32[1,512,256]{1,2,0:T(8,128)S(1)} %copy.10, f32[1,512,256]{1,2,0:T(8,128)S(1)} %copy.9, f32[1,512,256]{1,2,0:T(8,128)S(1)} %copy.7, f32[]{:T(128)S(6)} %min.3, f32[512,256]{0,1:T(8,128)} %reduce-scatter.2.cloned.1.call-done, f32[]{:T(128)S(6)} %convert_element_type.18), kind=kLoop, calls=%fused_computation.15 | loop fusion | flops 2097152 | bytes 2359304 | tf_op jit(solution)/shard_map/convert_element_type | solution.py:44
  152.6 0.0 all-gather.3.cloned.1.call-update
  152.6 50.9 %all-gather.3.cloned.1.call-done = bf16[4096,256]{0,1:T(8,128)(2,1)} async-done(((bf16[512,256]{0,1:T(8,128)(2,1)}), bf16[4096,256]{0,1:T(8,128)(2,1)}) %all-gather.3.cloned.1.call-update) | async-done | bytes 2097168 | tf_op jit(solution)/shard_map/all_gather | solution.py:45
  203.5 4.1 %copy.11 = bf16[1,4096,256]{2,1,0:T(8,128)(2,1)} copy(bf16[1,4096,256]{1,2,0:T(8,128)(2,1)} %bitcast.31) | data formatting | bytes 4194304 | tf_op jit(solution)/shard_map/all_gather | solution.py:45
Async XLA Ops:
  6.5 100.6 %reduce-scatter.2.cloned.1.call-start = ((), (), s32[]{:S(2)}) async-start(), calls=%async_computation.1 | async-start | bytes 4718592 | tf_op jit(solution)/shard_map/reduce_scatter | solution.py:30
  7.9 8.8 %copy-start = (f32[1,512,256]{2,1,0:T(8,128)S(1)}, f32[1,512,256]{2,1,0:T(8,128)}, u32[]{:S(2)}) copy-start(f32[1,512,256]{2,1,0:T(8,128)} %param.9) | copy-start | bytes 1572868
  7.9 9.0 %copy-start.1 = (f32[1,512,256]{2,1,0:T(8,128)S(1)}, f32[1,512,256]{2,1,0:T(8,128)}, u32[]{:S(2)}) copy-start(f32[1,512,256]{2,1,0:T(8,128)} %param.10) | copy-start | bytes 1572868
  7.9 101.0 %copy-start.2 = (f32[1,512,256]{2,1,0:T(8,128)S(1)}, f32[1,512,256]{2,1,0:T(8,128)}, u32[]{:S(2)}) copy-start(f32[1,512,256]{2,1,0:T(8,128)} %param.11) | copy-start | bytes 1572868
  16.0 187.5 %all-gather.3.cloned.1.call-start = ((), (), s32[]{:S(2)}) async-start(), calls=%async_computation.2 | async-start | bytes 2359296 | tf_op jit(solution)/shard_map/all_gather | solution.py:45
Sparse Core Ops, SparseCore 0:
  16.1 90.9 reduce-scatter.1
  152.7 50.7 all-gather.2
where the time goes:
time: 215 us; the launch traced here: 214 us
  waiting for transfers between devices  141 us (66%)
  blocking collectives  40.6 us (19%)
  between operations  14.8 us (7%)
  matrix products  8.04 us (4%)
  other arithmetic  5.32 us (2%)
  local copies, waits for them, and re-layouts  4.66 us (2%)
    reduce_scatter x1, waiting for transfers between devices, local(): lax.psum_scatter(slot_term(inputs, key_grads, live_row, features), 'dp',...  90 us
    all_gather x1, waiting for transfers between devices, local(): return lax.all_gather(update_rows, 'dp', axis=1, tiled=True)  50.9 us
    psum x1, blocking collectives, local(): lax.psum(jnp.sum(grad_shard * grad_shard), ('pipe', 'dp', 'tensor'))  40.6 us
    dot_general x1, matrix products, slot_term(): lax.dot_general(columns, weighted, (((0,), (0,)), ((), ())), preferred_el...  8.04 us
  transfers between devices with their start and end apart: 2, of which 2 were waited for; matrix products, arithmetic and copies ran while one was open for 0% of the time, Pallas kernels for 0%

commit v1 on v0

--- a/solution.py
+++ b/solution.py
@@ -21,6 +21,20 @@
     )
 
 
+def butterfly_sum(value, axes):
+    for axis in axes:
+        size = lax.axis_size(axis)
+        if size & (size - 1):
+            value = lax.psum(value, axis)
+            continue
+        bit = 1
+        while bit < size:
+            pairs = [(i, i ^ bit) for i in range(size)]
+            value = value + lax.ppermute(value, axis, pairs)
+            bit *= 2
+    return value
+
+
 def local(normed_input, key_grad, live_slots, master, first_moment, second_moment):
     inputs = normed_input[0]
     key_grads = key_grad[0]
@@ -32,7 +46,7 @@
     )
     tokens_total = (live_count * (inputs.shape[1] * lax.axis_size("dp"))).astype(jnp.float32)
     grad_shard = summed / tokens_total
-    squares = lax.psum(jnp.sum(grad_shard * grad_shard), ("pipe", "dp", "tensor"))
+    squares = butterfly_sum(jnp.sum(grad_shard * grad_shard), ("pipe", "tensor", "dp"))
     clip_factor = jnp.minimum(1.0, CLIP_NORM / jnp.sqrt(squares))
     clipped = clip_factor * grad_shard
     moment1 = MOMENT_DECAY * first_moment[0] + (1.0 - MOMENT_DECAY) * clipped

time: 215 us -> 194 us (0.902)
  blocking collectives: 40.6 us -> 0 us
  starting transfers between devices: 0.04 us -> 12.2 us
  waiting for transfers between devices: 141 us -> 145 us
  between operations: 14.8 us -> 18.3 us
    psum x1 -> x0, blocking collectives: 40.6 us -> none  [local(): lax.psum(jnp.sum(grad_shard * grad_shard), ('pipe', 'dp', 'tensor'))]
    ppermute x0 -> x5, starting transfers between devices: none -> 12.2 us  [butterfly_sum(): value = value + lax.ppermute(value, axis, pairs)]
    ppermute x0 -> x5, waiting for transfers between devices: none -> 4.16 us  [butterfly_sum(): value = value + lax.ppermute(value, axis, pairs)]
  transfers between devices with their start and end apart: 2 -> 7, of which waited for: 2 -> 7; matrix products, arithmetic and copies ran while one was open for 0% -> 0% of each run, Pallas kernels for 0% -> 0%
where the time goes in v1:
time: 194 us
  waiting for transfers between devices  145 us (75%)
  between operations  18.3 us (9%)
  starting transfers between devices  12.2 us (6%)
  matrix products  8.06 us (4%)
  other arithmetic  5.32 us (3%)
  local copies, waits for them, and re-layouts  4.66 us (2%)
    reduce_scatter x1, waiting for transfers between devices, local(): lax.psum_scatter(slot_term(inputs, key_grads, live_row, features), 'dp',...  90 us
    all_gather x1, waiting for transfers between devices, local(): return lax.all_gather(update_rows, 'dp', axis=1, tiled=True)  51 us
    ppermute x5, starting transfers between devices, butterfly_sum(): value = value + lax.ppermute(value, axis, pairs)  12.2 us
    dot_general x1, matrix products, slot_term(): lax.dot_general(columns, weighted, (((0,), (0,)), ((), ())), preferred_el...  8.06 us
    ppermute x5, waiting for transfers between devices, butterfly_sum(): value = value + lax.ppermute(value, axis, pairs)  4.16 us
    all_gather x1, local copies, waits for them, and re-layouts, local(): return lax.all_gather(update_rows, 'dp', axis=1, tiled=True)  4.06 us
  transfers between devices with their start and end apart: 7, of which 7 were waited for; matrix products, arithmetic and copies ran while one was open for 0% of the time, Pallas kernels for 0%

profile of v1, /device:TPU:0, one launch (start us, length us, event | category | flops | bytes accessed | tf_op | source)
XLA Modules:
  0.0 193.7 jit_solution(4177032211234704478)
XLA Ops:
  6.5 0.0 reduce-scatter.2.cloned.1.call-start
  6.5 1.4 fusion.16
  7.9 0.0 copy-start
  7.9 0.0 copy-start.1
  7.9 0.0 copy-start.2
  7.9 8.1 %fusion.2 = f32[4096,256]{0,1:T(8,128)} fusion(bf16[1,8,128,4096]{3,2,1,0:T(8,128)(2,1)} %param.6, bf16[1,8,128,256]{3,2,1,0:T(8,128)(2,1)} %param.7, bf16[8]{0:T(256)(128)(2,1)S(1)} %get-tuple-element.6), kind=kOutput, calls=%fused_computation.2 | convolution fusion | flops 2147745792 | bytes 13107216 | tf_op jit(solution)/shard_map/dot_general | solution.py:19
  16.0 0.0 reduce-scatter.2.cloned.1.call-update
  16.0 0.0 all-gather.3.cloned.1.call-start
  16.7 0.0 copy-done
  16.7 0.2 copy.10
  16.9 0.0 copy-done.1
  16.9 0.2 copy.7
  17.1 0.0 copy-done.2
  17.1 0.2 copy.9
  17.3 90.0 %reduce-scatter.2.cloned.1.call-done = f32[512,256]{0,1:T(8,128)} async-done(((f32[4096,256]{0,1:T(8,128)}), f32[512,256]{0,1:T(8,128)}) %reduce-scatter.2.cloned.1.call-update) | async-done | bytes 524304 | tf_op jit(solution)/shard_map/reduce_scatter | solution.py:44
  107.3 1.8 multiply_reduce_fusion
  109.1 0.0 collective-permute-start
  109.1 1.2 collective-permute-done
  111.7 2.8 %collective-permute-start.1 = (f32[]{:T(128)}, f32[]{:T(128)}, u32[]{:S(2)}, u32[]{:S(2)}) collective-permute-start(f32[]{:T(128)} %add.32), channel_id=1, source_target_pairs={{0,1},{1,0},{2,3},{3,2},{4,5},{5,4},{6,7},{7,6},{8,9},{9,8},{10,11... | collective-permute-start | bytes 20 | tf_op jit(solution)/shard_map/ppermute | solution.py:33
  114.5 0.7 collective-permute-done.1
  115.9 2.8 %collective-permute-start.2 = (f32[]{:T(128)}, f32[]{:T(128)}, u32[]{:S(2)}, u32[]{:S(2)}) collective-permute-start(f32[]{:T(128)} %add.33), channel_id=1, source_target_pairs={{0,2},{2,0},{4,6},{6,4},{8,10},{10,8},{12,14},{14,12},{1,3},{3,1},... | collective-permute-start | bytes 20 | tf_op jit(solution)/shard_map/ppermute | solution.py:33
  118.7 0.7 collective-permute-done.2
  120.2 3.0 %collective-permute-start.3 = (f32[]{:T(128)}, f32[]{:T(128)}, u32[]{:S(2)}, u32[]{:S(2)}) collective-permute-start(f32[]{:T(128)} %add.34), channel_id=1, source_target_pairs={{0,4},{2,6},{4,0},{6,2},{8,12},{10,14},{12,8},{14,10},{1,5},{3,7},... | collective-permute-start | bytes 20 | tf_op jit(solution)/shard_map/ppermute | solution.py:33
  123.2 0.5 collective-permute-done.3
  124.4 3.5 %collective-permute-start.4 = (f32[]{:T(128)}, f32[]{:T(128)}, u32[]{:S(2)}, u32[]{:S(2)}) collective-permute-start(f32[]{:T(128)} %add.35), channel_id=1, source_target_pairs={{0,8},{2,10},{4,12},{6,14},{8,0},{10,2},{12,4},{14,6},{1,9},{3,11}... | collective-permute-start | bytes 20 | tf_op jit(solution)/shard_map/ppermute | solution.py:33
  127.9 0.9 collective-permute-done.4
  129.6 2.2 %fusion.14 = bf16[512,256]{0,1:T(8,128)(2,1)} fusion(f32[1,512,256]{1,2,0:T(8,128)S(1)} %copy.10, f32[1,512,256]{1,2,0:T(8,128)S(1)} %copy.9, f32[1,512,256]{1,2,0:T(8,128)S(1)} %copy.7, f32[]{:T(128)S(6)} %min.3, f32[512,256]{0,1:T(8,128)} %reduce-scatter.2.cloned.1.call-done, f32[]{:T(128)S(6)} %convert_element_type.18), kind=kLoop, calls=%fused_computation.15 | loop fusion | flops 2097152 | bytes 2359304 | tf_op jit(solution)/shard_map/convert_element_type | solution.py:58
  131.8 0.0 all-gather.3.cloned.1.call-update
  131.8 51.0 %all-gather.3.cloned.1.call-done = bf16[4096,256]{0,1:T(8,128)(2,1)} async-done(((bf16[512,256]{0,1:T(8,128)(2,1)}), bf16[4096,256]{0,1:T(8,128)(2,1)}) %all-gather.3.cloned.1.call-update) | async-done | bytes 2097168 | tf_op jit(solution)/shard_map/all_gather | solution.py:59
  182.8 4.1 %copy.11 = bf16[1,4096,256]{2,1,0:T(8,128)(2,1)} copy(bf16[1,4096,256]{1,2,0:T(8,128)(2,1)} %bitcast.31) | data formatting | bytes 4194304 | tf_op jit(solution)/shard_map/all_gather | solution.py:59
Async XLA Ops:
  6.5 100.8 %reduce-scatter.2.cloned.1.call-start = ((), (), s32[]{:S(2)}) async-start(), calls=%async_computation.1 | async-start | bytes 4718592 | tf_op jit(solution)/shard_map/reduce_scatter | solution.py:44
  7.9 8.8 %copy-start = (f32[1,512,256]{2,1,0:T(8,128)S(1)}, f32[1,512,256]{2,1,0:T(8,128)}, u32[]{:S(2)}) copy-start(f32[1,512,256]{2,1,0:T(8,128)} %param.9) | copy-start | bytes 1572868
  7.9 9.0 %copy-start.1 = (f32[1,512,256]{2,1,0:T(8,128)S(1)}, f32[1,512,256]{2,1,0:T(8,128)}, u32[]{:S(2)}) copy-start(f32[1,512,256]{2,1,0:T(8,128)} %param.10) | copy-start | bytes 1572868
  7.9 9.2 %copy-start.2 = (f32[1,512,256]{2,1,0:T(8,128)S(1)}, f32[1,512,256]{2,1,0:T(8,128)}, u32[]{:S(2)}) copy-start(f32[1,512,256]{2,1,0:T(8,128)} %param.11) | copy-start | bytes 1572868
  16.0 166.8 %all-gather.3.cloned.1.call-start = ((), (), s32[]{:S(2)}) async-start(), calls=%async_computation.2 | async-start | bytes 2359296 | tf_op jit(solution)/shard_map/all_gather | solution.py:59
  109.1 1.2 collective-permute-start
  111.7 3.6 %collective-permute-start.1 = (f32[]{:T(128)}, f32[]{:T(128)}, u32[]{:S(2)}, u32[]{:S(2)}) collective-permute-start(f32[]{:T(128)} %add.32), channel_id=1, source_target_pairs={{0,1},{1,0},{2,3},{3,2},{4,5},{5,4},{6,7},{7,6},{8,9},{9,8},{10,11... | collective-permute-start | bytes 20 | tf_op jit(solution)/shard_map/ppermute | solution.py:33
  115.9 3.6 %collective-permute-start.2 = (f32[]{:T(128)}, f32[]{:T(128)}, u32[]{:S(2)}, u32[]{:S(2)}) collective-permute-start(f32[]{:T(128)} %add.33), channel_id=1, source_target_pairs={{0,2},{2,0},{4,6},{6,4},{8,10},{10,8},{12,14},{14,12},{1,3},{3,1},... | collective-permute-start | bytes 20 | tf_op jit(solution)/shard_map/ppermute | solution.py:33
  120.2 3.6 %collective-permute-start.3 = (f32[]{:T(128)}, f32[]{:T(128)}, u32[]{:S(2)}, u32[]{:S(2)}) collective-permute-start(f32[]{:T(128)} %add.34), channel_id=1, source_target_pairs={{0,4},{2,6},{4,0},{6,2},{8,12},{10,14},{12,8},{14,10},{1,5},{3,7},... | collective-permute-start | bytes 20 | tf_op jit(solution)/shard_map/ppermute | solution.py:33
  124.4 4.5 %collective-permute-start.4 = (f32[]{:T(128)}, f32[]{:T(128)}, u32[]{:S(2)}, u32[]{:S(2)}) collective-permute-start(f32[]{:T(128)} %add.35), channel_id=1, source_target_pairs={{0,8},{2,10},{4,12},{6,14},{8,0},{10,2},{12,4},{14,6},{1,9},{3,11}... | collective-permute-start | bytes 20 | tf_op jit(solution)/shard_map/ppermute | solution.py:33
Sparse Core Ops, SparseCore 0:
  16.1 91.1 reduce-scatter.1
  131.9 50.8 all-gather.2

commit v2 on v1

--- a/solution.py
+++ b/solution.py
@@ -35,15 +35,88 @@
     return value
 
 
+def bit_orders(size):
+    bits = list(range(size.bit_length() - 1))
+    return bits, bits[1:] + bits[:1]
+
+
+def halving_scatter(partial, axis, order):
+    size = lax.axis_size(axis)
+    levels = size.bit_length() - 1
+    index = lax.axis_index(axis)
+    rows, cols = partial.shape
+    blocks = partial.reshape((2,) * levels + (rows // size, cols))
+    for step, bit in enumerate(order):
+        dim = levels - 1 - bit
+        dim -= sum(1 for done in order[:step] if levels - 1 - done < dim)
+        mine = (index >> bit) & 1
+        low = lax.index_in_dim(blocks, 0, dim, keepdims=False)
+        high = lax.index_in_dim(blocks, 1, dim, keepdims=False)
+        keep = jnp.where(mine == 1, high, low)
+        send = jnp.where(mine == 1, low, high)
+        pairs = [(i, i ^ (1 << bit)) for i in range(size)]
+        blocks = keep + lax.ppermute(send, axis, pairs)
+    return blocks.reshape(rows // size, cols)
+
+
+def doubling_gather(part, axis, order):
+    size = lax.axis_size(axis)
+    levels = size.bit_length() - 1
+    index = lax.axis_index(axis)
+    placed = []
+    current = part
+    for bit in order:
+        mine = (index >> bit) & 1
+        pairs = [(i, i ^ (1 << bit)) for i in range(size)]
+        other = lax.ppermute(current, axis, pairs)
+        low = jnp.where(mine == 1, other, current)
+        high = jnp.where(mine == 1, current, other)
+        current = jnp.stack([low, high], axis=0)
+        placed.insert(0, bit)
+    perm = [placed.index(bit) for bit in range(levels - 1, -1, -1)]
+    current = jnp.transpose(current, perm + list(range(levels, current.ndim)))
+    return current.reshape((-1,) + part.shape[1:])
+
+
+def scatter_rows(partial, axis):
+    size = lax.axis_size(axis)
+    cols = partial.shape[1]
+    if size & (size - 1) or size == 1 or cols % 2:
+        return lax.psum_scatter(partial, axis, scatter_dimension=0, tiled=True)
+    first, second = bit_orders(size)
+    half = cols // 2
+    return jnp.concatenate(
+        [
+            halving_scatter(partial[:, :half], axis, first),
+            halving_scatter(partial[:, half:], axis, second),
+        ],
+        axis=1,
+    )
+
+
+def gather_rows(part, axis):
+    size = lax.axis_size(axis)
+    cols = part.shape[1]
+    if size & (size - 1) or size == 1 or cols % 2:
+        return lax.all_gather(part, axis, axis=0, tiled=True)
+    first, second = bit_orders(size)
+    half = cols // 2
+    return jnp.concatenate(
+        [
+            doubling_gather(part[:, :half], axis, first[::-1]),
+            doubling_gather(part[:, half:], axis, second[::-1]),
+        ],
+        axis=1,
+    )
+
+
 def local(normed_input, key_grad, live_slots, master, first_moment, second_moment):
     inputs = normed_input[0]
     key_grads = key_grad[0]
     live_row = live_slots[0]
     live_count = jnp.sum(live_row)
     features = inputs.shape[2]
-    summed = lax.psum_scatter(
-        slot_term(inputs, key_grads, live_row, features), "dp", scatter_dimension=0, tiled=True
-    )
+    summed = scatter_rows(slot_term(inputs, key_grads, live_row, features), "dp")
     tokens_total = (live_count * (inputs.shape[1] * lax.axis_size("dp"))).astype(jnp.float32)
     grad_shard = summed / tokens_total
     squares = butterfly_sum(jnp.sum(grad_shard * grad_shard), ("pipe", "tensor", "dp"))
@@ -55,8 +128,7 @@
         moment1 / FIRST_CORRECTION / (jnp.sqrt(moment2 / SECOND_CORRECTION) + EPSILON)
         + WEIGHT_DECAY * master[0]
     )
-    update_rows = update.astype(jnp.bfloat16)[None]
-    return lax.all_gather(update_rows, "dp", axis=1, tiled=True)
+    return gather_rows(update.astype(jnp.bfloat16), "dp")[None]
 
 
 def solution(mesh):

time: 194 us -> 157 us (0.81)
  waiting for transfers between devices: 145 us -> 82.5 us
  local copies, waits for them, and re-layouts: 4.66 us -> 24.9 us
  starting transfers between devices: 12.2 us -> 26.7 us
  between operations: 18.3 us -> 4.66 us
  other arithmetic: 5.32 us -> 12.1 us
  matrix products: 8.06 us -> 6.02 us
    reduce_scatter x1 -> x0, waiting for transfers between devices: 90 us -> none  [local(): lax.psum_scatter(slot_term(inputs, key_grads, live_row, features), 'dp',...]
    ppermute x0 -> x12, waiting for transfers between devices: none -> 74.3 us  [the longest x6 48.5 us: halving_scatter(): blocks = keep + lax.ppermute(send, axis, pairs)]
    all_gather x1 -> x0, waiting for transfers between devices: 51 us -> none  [local(): return lax.all_gather(update_rows, 'dp', axis=1, tiled=True)]
    ppermute x0 -> x12, starting transfers between devices: none -> 17.7 us  [the longest x6 9.28 us: halving_scatter(): blocks = keep + lax.ppermute(send, axis, pairs)]
    slice x0 -> x4, local copies, waits for them, and re-layouts: none -> 9.79 us  [the longest x2 7.45 us: halving_scatter(): high = lax.index_in_dim(blocks, 1, dim, keepdims=False)]
    unnamed x9 -> x12, local copies, waits for them, and re-layouts: 0.6 us -> 7.95 us
    reshape x0 -> x2, local copies, waits for them, and re-layouts: none -> 7.01 us  [halving_scatter(): blocks = partial.reshape((2,) * levels + (rows // size, cols))]
    select_n x0 -> x6, other arithmetic: none -> 4.27 us  [halving_scatter(): send = jnp.where(mine == 1, low, high)]
  transfers between devices with their start and end apart: 7 -> 17, of which waited for: 7 -> 15; matrix products, arithmetic and copies ran while one was open for 0% -> 14% of each run, Pallas kernels for 0% -> 0%
where the time goes in v2:
time: 157 us
  waiting for transfers between devices  82.5 us (53%)
  starting transfers between devices  26.7 us (17%)
  local copies, waits for them, and re-layouts  24.9 us (16%)
  other arithmetic  12.1 us (8%)
  matrix products  6.02 us (4%)
  between operations  4.66 us (3%)
    ppermute x6, waiting for transfers between devices, halving_scatter(): blocks = keep + lax.ppermute(send, axis, pairs)  48.5 us
    ppermute x6, waiting for transfers between devices, doubling_gather(): other = lax.ppermute(current, axis, pairs)  25.9 us
    ppermute x6, starting transfers between devices, halving_scatter(): blocks = keep + lax.ppermute(send, axis, pairs)  9.28 us
    ppermute x5, starting transfers between devices, butterfly_sum(): value = value + lax.ppermute(value, axis, pairs)  9.02 us
    ppermute x6, starting transfers between devices, doubling_gather(): other = lax.ppermute(current, axis, pairs)  8.4 us
    ppermute x5, waiting for transfers between devices, butterfly_sum(): value = value + lax.ppermute(value, axis, pairs)  8.13 us
    unnamed x12, local copies, waits for them, and re-layouts  7.95 us
    slice x2, local copies, waits for them, and re-layouts, halving_scatter(): high = lax.index_in_dim(blocks, 1, dim, keepdims=False)  7.45 us
  transfers between devices with their start and end apart: 17, of which 15 were waited for; matrix products, arithmetic and copies ran while one was open for 14% of the time, Pallas kernels for 0%

profile of v2, /device:TPU:0, one launch (start us, length us, event | category | flops | bytes accessed | tf_op | source)
XLA Modules:
  0.0 156.9 jit_solution(12215113966081065010)
XLA Ops:
  1.4 6.0 %fusion.2 = f32[4096,256]{0,1:T(8,128)S(1)} fusion(bf16[1,8,128,4096]{3,2,1,0:T(8,128)(2,1)} %param.6, bf16[1,8,128,256]{3,2,1,0:T(8,128)(2,1)} %param.7, bf16[8]{0:T(256)(128)(2,1)S(1)} %get-tuple-element.27), kind=kOutput, calls=%fused_computation.2 | convolution fusion | flops 2147745792 | bytes 13107216 | tf_op jit(solution)/shard_map/dot_general | solution.py:19
  7.4 2.3 %fusion.16 = (f32[4096,128]{0,1:T(8,128)}, f32[4096,128]{0,1:T(8,128)}) fusion(f32[4096,256]{0,1:T(8,128)S(1)} %fusion.2), kind=kLoop, calls=%fused_computation.50 | loop fusion | bytes 8388608 | tf_op jit(solution)/shard_map/slice | solution.py:90
  9.7 3.0 %reshape.66 = f32[2,2,2,512,128]{3,2,1,0,4:T(2,128)S(1)} reshape(f32[4096,128]{0,1:T(8,128)} %get-tuple-element.6) | data formatting | bytes 4194304 | tf_op jit(solution)/shard_map/reshape | solution.py:48
  12.7 1.8 %fusion.18 = (f32[2,1,2,512,128]{3,2,1,0,4:T(2,128)S(1)}, f32[2,1,2,512,128]{3,2,1,0,4:T(2,128)}) fusion(f32[2,2,2,512,128]{3,2,1,0,4:T(2,128)S(1)} %reshape.66), kind=kLoop, calls=%fused_computation.52 | loop fusion | bytes 4194304 | tf_op jit(solution)/shard_map/slice | solution.py:54
  14.5 1.5 copy.18
  17.6 3.0 %collective-permute-start.3 = (f32[2,2,512,128]{3,2,1,0:T(8,128)}, f32[2,2,512,128]{3,2,1,0:T(8,128)}, u32[]{:S(2)}, u32[]{:S(2)}) collective-permute-start(f32[2,2,512,128]{3,2,1,0:T(8,128)} %select_bitcast_fusion), channel_id=1, source_target_pairs={{0,4},{2,6},{4,0},{6,2},{8,12},{10,14},{12,8},{14,10},{1,5},{3,7},... | collective-permute-start | bytes 3145736 | tf_op jit(solution)/shard_map/ppermute | solution.py:58
  20.6 4.0 %reshape.65 = f32[2,2,2,512,128]{3,2,1,0,4:T(2,128)} reshape(f32[4096,128]{0,1:T(8,128)} %get-tuple-element.5) | data formatting | bytes 4194304 | tf_op jit(solution)/shard_map/reshape | solution.py:48
  24.6 5.7 %fusion.17 = (f32[2,2,1,512,128]{3,2,1,0,4:T(1,128)}, f32[2,2,1,512,128]{3,2,1,0,4:T(1,128)}) fusion(f32[2,2,2,512,128]{3,2,1,0,4:T(2,128)} %reshape.65), kind=kLoop, calls=%fused_computation.51 | loop fusion | bytes 4194304 | tf_op jit(solution)/shard_map/slice | solution.py:54
  30.3 2.3 %copy.16 = f32[2,2,1,512,128]{4,3,0,1,2:T(8,128)S(1)} copy(f32[2,2,1,512,128]{3,2,1,0,4:T(1,128)} %get-tuple-element.8) | data formatting | bytes 2097152
  32.6 3.6 %copy.15 = f32[2,2,1,512,128]{4,3,0,1,2:T(8,128)} copy(f32[2,2,1,512,128]{3,2,1,0,4:T(1,128)} %get-tuple-element.7) | data formatting | bytes 2097152
  36.3 2.3 %select_bitcast_fusion.1 = f32[2,2,512,128]{3,2,0,1:T(8,128)} fusion(f32[2,2,1,512,128]{4,3,0,1,2:T(8,128)S(1)} %copy.16, f32[2,2,1,512,128]{4,3,0,1,2:T(8,128)} %copy.15, pred[]{:T(512)S(6)} %eq.6), kind=kLoop, calls=%fused_computation.9 | loop fusion | flops 262144 | bytes 3145729 | tf_op jit(solution)/shard_map/jit(_where)/select_n | solution.py:56
  38.8 5.3 %collective-permute-done.3 = f32[2,2,512,128]{3,2,1,0:T(8,128)} collective-permute-done((f32[2,2,512,128]{3,2,1,0:T(8,128)}, f32[2,2,512,128]{3,2,1,0:T(8,128)}, u32[]{:S(2)}, u32[]{:S(2)}) %collective-permute-start.3) | collective-permute-done | bytes 1048608 | tf_op jit(solution)/shard_map/ppermute | solution.py:58
  45.5 2.8 %collective-permute-start.4 = (f32[2,512,128]{2,1,0:T(8,128)S(1)}, f32[2,512,128]{2,1,0:T(8,128)S(1)}, u32[]{:S(2)}, u32[]{:S(2)}) collective-permute-start(f32[2,512,128]{2,1,0:T(8,128)S(1)} %select_bitcast_fusion.6), channel_id=1, source_target_pairs={{0,8},{2,10},{4,12},{6,14},{8,0},{10,2},{12,4},{14,6},{1,9},{3,11}... | collective-permute-start | bytes 1572872 | tf_op jit(solution)/shard_map/ppermute | solution.py:58
  48.4 15.1 %collective-permute-done = f32[2,2,512,128]{3,2,0,1:T(8,128)} collective-permute-done((f32[2,2,512,128]{3,2,0,1:T(8,128)}, f32[2,2,512,128]{3,2,0,1:T(8,128)}, u32[]{:S(2)}, u32[]{:S(2)}) %collective-permute-start) | collective-permute-done | bytes 1048608 | tf_op jit(solution)/shard_map/ppermute | solution.py:58
  65.4 5.6 %collective-permute-done.4 = f32[2,512,128]{2,1,0:T(8,128)S(1)} collective-permute-done((f32[2,512,128]{2,1,0:T(8,128)S(1)}, f32[2,512,128]{2,1,0:T(8,128)S(1)}, u32[]{:S(2)}, u32[]{:S(2)}) %collective-permute-start.4) | collective-permute-done | bytes 524320 | tf_op jit(solution)/shard_map/ppermute | solution.py:58
  72.5 9.6 %collective-permute-done.1 = f32[2,512,128]{2,1,0:T(8,128)S(1)} collective-permute-done((f32[2,512,128]{2,1,0:T(8,128)S(1)}, f32[2,512,128]{2,1,0:T(8,128)S(1)}, u32[]{:S(2)}, u32[]{:S(2)}) %collective-permute-start.1) | collective-permute-done | bytes 524320 | tf_op jit(solution)/shard_map/ppermute | solution.py:58
  85.0 12.9 %collective-permute-done.2 = f32[512,128]{1,0:T(8,128)S(1)} collective-permute-done((f32[512,128]{1,0:T(8,128)}, f32[512,128]{1,0:T(8,128)S(1)}, u32[]{:S(2)}, u32[]{:S(2)}) %collective-permute-start.2) | collective-permute-done | bytes 262176 | tf_op jit(solution)/shard_map/ppermute | solution.py:58
  101.4 2.7 %collective-permute-start.7 = (f32[]{:T(128)}, f32[]{:T(128)}, u32[]{:S(2)}, u32[]{:S(2)}) collective-permute-start(f32[]{:T(128)} %add.54), channel_id=1, source_target_pairs={{0,1},{1,0},{2,3},{3,2},{4,5},{5,4},{6,7},{7,6},{8,9},{9,8},{10,11... | collective-permute-start | bytes 20 | tf_op jit(solution)/shard_map/ppermute | solution.py:33
  105.7 2.7 %collective-permute-start.8 = (f32[]{:T(128)}, f32[]{:T(128)}, u32[]{:S(2)}, u32[]{:S(2)}) collective-permute-start(f32[]{:T(128)} %add.55), channel_id=1, source_target_pairs={{0,2},{2,0},{4,6},{6,4},{8,10},{10,8},{12,14},{14,12},{1,3},{3,1},... | collective-permute-start | bytes 20 | tf_op jit(solution)/shard_map/ppermute | solution.py:33
  111.4 2.3 %collective-permute-done.9 = f32[]{:T(128)} collective-permute-done((f32[]{:T(128)}, f32[]{:T(128)}, u32[]{:S(2)}, u32[]{:S(2)}) %collective-permute-start.9) | collective-permute-done | bytes 36 | tf_op jit(solution)/shard_map/ppermute | solution.py:33
  114.4 2.2 %collective-permute-start.10 = (f32[]{:T(128)}, f32[]{:T(128)}, u32[]{:S(2)}, u32[]{:S(2)}) collective-permute-start(f32[]{:T(128)} %add.57), channel_id=1, source_target_pairs={{0,8},{2,10},{4,12},{6,14},{8,0},{10,2},{12,4},{14,6},{1,9},{3,11}... | collective-permute-start | bytes 20 | tf_op jit(solution)/shard_map/ppermute | solution.py:33
  116.6 2.4 %collective-permute-done.10 = f32[]{:T(128)} collective-permute-done((f32[]{:T(128)}, f32[]{:T(128)}, u32[]{:S(2)}, u32[]{:S(2)}) %collective-permute-start.10) | collective-permute-done | bytes 36 | tf_op jit(solution)/shard_map/ppermute | solution.py:33
  121.1 1.5 collective-permute-start.14
  122.6 8.6 %collective-permute-done.11 = bf16[512,128]{1,0:T(8,128)(2,1)S(1)} collective-permute-done((bf16[512,128]{1,0:T(8,128)(2,1)S(1)}, bf16[512,128]{1,0:T(8,128)(2,1)S(1)}, u32[]{:S(2)}, u32[]{:S(2)}) %collective-permute-start.11) | collective-permute-done | bytes 131104 | tf_op jit(solution)/shard_map/ppermute | solution.py:71
  131.4 2.7 %collective-permute-start.12 = (bf16[2,512,128]{2,1,0:T(8,128)(2,1)S(1)}, bf16[2,512,128]{2,1,0:T(8,128)(2,1)S(1)}, u32[]{:S(2)}, u32[]{:S(2)}) collective-permute-start(bf16[2,512,128]{2,1,0:T(8,128)(2,1)S(1)} %pad_maximum_fusion.2), channel_id=1, source_target_pairs={{0,4},{2,6},{4,0},{6,2},{8,12},{10,14},{12,8},{14,10},{1,5},{3,7},... | collective-permute-start | bytes 786440 | tf_op jit(solution)/shard_map/ppermute | solution.py:71
  134.1 6.8 %collective-permute-done.15 = bf16[2,512,128]{2,1,0:T(8,128)(2,1)S(1)} collective-permute-done((bf16[2,512,128]{2,1,0:T(8,128)(2,1)S(1)}, bf16[2,512,128]{2,1,0:T(8,128)(2,1)S(1)}, u32[]{:S(2)}, u32[]{:S(2)}) %collective-permute-start.15) | collective-permute-done | bytes 262176 | tf_op jit(solution)/shard_map/ppermute | solution.py:71
  140.8 3.1 %collective-permute-done.12 = bf16[2,512,128]{2,1,0:T(8,128)(2,1)S(1)} collective-permute-done((bf16[2,512,128]{2,1,0:T(8,128)(2,1)S(1)}, bf16[2,512,128]{2,1,0:T(8,128)(2,1)S(1)}, u32[]{:S(2)}, u32[]{:S(2)}) %collective-permute-start.12) | collective-permute-done | bytes 262176 | tf_op jit(solution)/shard_map/ppermute | solution.py:71
  144.1 1.7 %collective-permute-start.16 = (bf16[2,2,512,128]{3,2,1,0:T(8,128)(2,1)S(1)}, bf16[2,2,512,128]{3,2,1,0:T(8,128)(2,1)S(1)}, u32[]{:S(2)}, u32[]{:S(2)}) collective-permute-start(bf16[2,2,512,128]{3,2,1,0:T(8,128)(2,1)S(1)} %pad_maximum_fusion.1), channel_id=1, source_target_pairs={{0,4},{2,6},{4,0},{6,2},{8,12},{10,14},{12,8},{14,10},{1,5},{3,7},... | collective-permute-start | bytes 1572872 | tf_op jit(solution)/shard_map/ppermute | solution.py:71
  145.8 1.5 collective-permute-start.13
  147.4 6.0 %collective-permute-done.16 = bf16[2,2,512,128]{3,2,1,0:T(8,128)(2,1)S(1)} collective-permute-done((bf16[2,2,512,128]{3,2,1,0:T(8,128)(2,1)S(1)}, bf16[2,2,512,128]{3,2,1,0:T(8,128)(2,1)S(1)}, u32[]{:S(2)}, u32[]{:S(2)}) %collective-permute-start.16) | collective-permute-done | bytes 524320 | tf_op jit(solution)/shard_map/ppermute | solution.py:71
  153.6 1.5 collective-permute-done.13
  155.3 1.5 maximum_bitcast_fusion
  (49 shorter events, 18.1 us)
Async XLA Ops:
  17.6 26.5 %collective-permute-start.3 = (f32[2,2,512,128]{3,2,1,0:T(8,128)}, f32[2,2,512,128]{3,2,1,0:T(8,128)}, u32[]{:S(2)}, u32[]{:S(2)}) collective-permute-start(f32[2,2,512,128]{3,2,1,0:T(8,128)} %select_bitcast_fusion), channel_id=1, source_target_pairs={{0,4},{2,6},{4,0},{6,2},{8,12},{10,14},{12,8},{14,10},{1,5},{3,7},... | collective-permute-start | bytes 3145736 | tf_op jit(solution)/shard_map/ppermute | solution.py:58
  38.6 24.9 %collective-permute-start = (f32[2,2,512,128]{3,2,0,1:T(8,128)}, f32[2,2,512,128]{3,2,0,1:T(8,128)}, u32[]{:S(2)}, u32[]{:S(2)}) collective-permute-start(f32[2,2,512,128]{3,2,0,1:T(8,128)} %select_bitcast_fusion.1), channel_id=1, source_target_pairs={{0,2},{2,0},{4,6},{6,4},{8,10},{10,8},{12,14},{14,12},{1,3},{3,1},... | collective-permute-start | bytes 3145736 | tf_op jit(solution)/shard_map/ppermute | solution.py:58
  38.8 24.7 %copy-start = (f32[2,2,1,512,128]{4,3,0,1,2:T(8,128)S(1)}, f32[2,2,1,512,128]{4,3,0,1,2:T(8,128)}, u32[]{:S(2)}) copy-start(f32[2,2,1,512,128]{4,3,0,1,2:T(8,128)} %copy.15) | copy-start | bytes 3145732
  45.5 25.4 %collective-permute-start.4 = (f32[2,512,128]{2,1,0:T(8,128)S(1)}, f32[2,512,128]{2,1,0:T(8,128)S(1)}, u32[]{:S(2)}, u32[]{:S(2)}) collective-permute-start(f32[2,512,128]{2,1,0:T(8,128)S(1)} %select_bitcast_fusion.6), channel_id=1, source_target_pairs={{0,8},{2,10},{4,12},{6,14},{8,0},{10,2},{12,4},{14,6},{1,9},{3,11}... | collective-permute-start | bytes 1572872 | tf_op jit(solution)/shard_map/ppermute | solution.py:58
  65.0 17.0 %collective-permute-start.1 = (f32[2,512,128]{2,1,0:T(8,128)S(1)}, f32[2,512,128]{2,1,0:T(8,128)S(1)}, u32[]{:S(2)}, u32[]{:S(2)}) collective-permute-start(f32[2,512,128]{2,1,0:T(8,128)S(1)} %select_bitcast_fusion.7), channel_id=1, source_target_pairs={{0,4},{2,6},{4,0},{6,2},{8,12},{10,14},{12,8},{14,10},{1,5},{3,7},... | collective-permute-start | bytes 1572872 | tf_op jit(solution)/shard_map/ppermute | solution.py:58
  71.1 13.9 %collective-permute-start.5 = (f32[512,128]{1,0:T(8,128)S(1)}, f32[512,128]{1,0:T(8,128)S(1)}, u32[]{:S(2)}, u32[]{:S(2)}) collective-permute-start(f32[512,128]{1,0:T(8,128)S(1)} %select_bitcast_fusion.12), channel_id=1, source_target_pairs={{0,2},{2,0},{4,6},{6,4},{8,10},{10,8},{12,14},{14,12},{1,3},{3,1},... | collective-permute-start | bytes 786440 | tf_op jit(solution)/shard_map/ppermute | solution.py:58
  82.2 37.5 %copy-start.1 = (f32[1,512,256]{2,1,0:T(8,128)S(1)}, f32[1,512,256]{2,1,0:T(8,128)}, u32[]{:S(2)}) copy-start(f32[1,512,256]{2,1,0:T(8,128)} %param.9) | copy-start | bytes 1572868
  82.2 37.5 %copy-start.2 = (f32[1,512,256]{2,1,0:T(8,128)S(1)}, f32[1,512,256]{2,1,0:T(8,128)}, u32[]{:S(2)}) copy-start(f32[1,512,256]{2,1,0:T(8,128)} %param.11) | copy-start | bytes 1572868
  82.2 37.5 %copy-start.3 = (f32[1,512,256]{2,1,0:T(8,128)S(1)}, f32[1,512,256]{2,1,0:T(8,128)}, u32[]{:S(2)}) copy-start(f32[1,512,256]{2,1,0:T(8,128)} %param.10) | copy-start | bytes 1572868
  83.0 15.0 %collective-permute-start.2 = (f32[512,128]{1,0:T(8,128)}, f32[512,128]{1,0:T(8,128)S(1)}, u32[]{:S(2)}, u32[]{:S(2)}) collective-permute-start(f32[512,128]{1,0:T(8,128)} %select_bitcast_fusion.13), channel_id=1, source_target_pairs={{0,8},{2,10},{4,12},{6,14},{8,0},{10,2},{12,4},{14,6},{1,9},{3,11}... | collective-permute-start | bytes 786440 | tf_op jit(solution)/shard_map/ppermute | solution.py:58
  98.7 1.4 collective-permute-start.6
  101.4 3.7 %collective-permute-start.7 = (f32[]{:T(128)}, f32[]{:T(128)}, u32[]{:S(2)}, u32[]{:S(2)}) collective-permute-start(f32[]{:T(128)} %add.54), channel_id=1, source_target_pairs={{0,1},{1,0},{2,3},{3,2},{4,5},{5,4},{6,7},{7,6},{8,9},{9,8},{10,11... | collective-permute-start | bytes 20 | tf_op jit(solution)/shard_map/ppermute | solution.py:33
  105.7 3.7 %collective-permute-start.8 = (f32[]{:T(128)}, f32[]{:T(128)}, u32[]{:S(2)}, u32[]{:S(2)}) collective-permute-start(f32[]{:T(128)} %add.55), channel_id=1, source_target_pairs={{0,2},{2,0},{4,6},{6,4},{8,10},{10,8},{12,14},{14,12},{1,3},{3,1},... | collective-permute-start | bytes 20 | tf_op jit(solution)/shard_map/ppermute | solution.py:33
  110.1 3.7 %collective-permute-start.9 = (f32[]{:T(128)}, f32[]{:T(128)}, u32[]{:S(2)}, u32[]{:S(2)}) collective-permute-start(f32[]{:T(128)} %add.56), channel_id=1, source_target_pairs={{0,4},{2,6},{4,0},{6,2},{8,12},{10,14},{12,8},{14,10},{1,5},{3,7},... | collective-permute-start | bytes 20 | tf_op jit(solution)/shard_map/ppermute | solution.py:33
  114.4 4.6 %collective-permute-start.10 = (f32[]{:T(128)}, f32[]{:T(128)}, u32[]{:S(2)}, u32[]{:S(2)}) collective-permute-start(f32[]{:T(128)} %add.57), channel_id=1, source_target_pairs={{0,8},{2,10},{4,12},{6,14},{8,0},{10,2},{12,4},{14,6},{1,9},{3,11}... | collective-permute-start | bytes 20 | tf_op jit(solution)/shard_map/ppermute | solution.py:33
  120.2 11.0 %collective-permute-start.11 = (bf16[512,128]{1,0:T(8,128)(2,1)S(1)}, bf16[512,128]{1,0:T(8,128)(2,1)S(1)}, u32[]{:S(2)}, u32[]{:S(2)}) collective-permute-start(bf16[512,128]{1,0:T(8,128)(2,1)S(1)} %get-tuple-element.25), channel_id=1, source_target_pairs={{0,8},{2,10},{4,12},{6,14},{8,0},{10,2},{12,4},{14,6},{1,9},{3,11}... | collective-permute-start | bytes 393224 | tf_op jit(solution)/shard_map/ppermute | solution.py:71
  121.1 10.1 %collective-permute-start.14 = (bf16[512,128]{1,0:T(8,128)(2,1)S(1)}, bf16[512,128]{1,0:T(8,128)(2,1)S(1)}, u32[]{:S(2)}, u32[]{:S(2)}) collective-permute-start(bf16[512,128]{1,0:T(8,128)(2,1)S(1)} %get-tuple-element.26), channel_id=1, source_target_pairs={{0,2},{2,0},{4,6},{6,4},{8,10},{10,8},{12,14},{14,12},{1,3},{3,1},... | collective-permute-start | bytes 393224 | tf_op jit(solution)/shard_map/ppermute | solution.py:71
  131.2 9.6 %collective-permute-start.15 = (bf16[2,512,128]{2,1,0:T(8,128)(2,1)S(1)}, bf16[2,512,128]{2,1,0:T(8,128)(2,1)S(1)}, u32[]{:S(2)}, u32[]{:S(2)}) collective-permute-start(bf16[2,512,128]{2,1,0:T(8,128)(2,1)S(1)} %pad_maximum_fusion.3), channel_id=1, source_target_pairs={{0,8},{2,10},{4,12},{6,14},{8,0},{10,2},{12,4},{14,6},{1,9},{3,11}... | collective-permute-start | bytes 786440 | tf_op jit(solution)/shard_map/ppermute | solution.py:71
  131.4 12.6 %collective-permute-start.12 = (bf16[2,512,128]{2,1,0:T(8,128)(2,1)S(1)}, bf16[2,512,128]{2,1,0:T(8,128)(2,1)S(1)}, u32[]{:S(2)}, u32[]{:S(2)}) collective-permute-start(bf16[2,512,128]{2,1,0:T(8,128)(2,1)S(1)} %pad_maximum_fusion.2), channel_id=1, source_target_pairs={{0,4},{2,6},{4,0},{6,2},{8,12},{10,14},{12,8},{14,10},{1,5},{3,7},... | collective-permute-start | bytes 786440 | tf_op jit(solution)/shard_map/ppermute | solution.py:71
  144.1 9.2 %collective-permute-start.16 = (bf16[2,2,512,128]{3,2,1,0:T(8,128)(2,1)S(1)}, bf16[2,2,512,128]{3,2,1,0:T(8,128)(2,1)S(1)}, u32[]{:S(2)}, u32[]{:S(2)}) collective-permute-start(bf16[2,2,512,128]{3,2,1,0:T(8,128)(2,1)S(1)} %pad_maximum_fusion.1), channel_id=1, source_target_pairs={{0,4},{2,6},{4,0},{6,2},{8,12},{10,14},{12,8},{14,10},{1,5},{3,7},... | collective-permute-start | bytes 1572872 | tf_op jit(solution)/shard_map/ppermute | solution.py:71
  145.8 9.2 %collective-permute-start.13 = (bf16[2,2,512,128]{3,2,1,0:T(8,128)(2,1)S(1)}, bf16[2,2,512,128]{3,2,1,0:T(8,128)(2,1)S(1)}, u32[]{:S(2)}, u32[]{:S(2)}) collective-permute-start(bf16[2,2,512,128]{3,2,1,0:T(8,128)(2,1)S(1)} %pad_maximum_fusion), channel_id=1, source_target_pairs={{0,2},{2,0},{4,6},{6,4},{8,10},{10,8},{12,14},{14,12},{1,3},{3,1},... | collective-permute-start | bytes 1572872 | tf_op jit(solution)/shard_map/ppermute | solution.py:71

commit v3 on v2

--- a/solution.py
+++ b/solution.py
@@ -17,7 +17,7 @@
     weighted = (key_grads * keep_mask[:, None, None]).reshape(-1, key_grads.shape[2])
     columns = inputs.reshape(-1, column_count)
     return lax.dot_general(
-        columns, weighted, (((0,), (0,)), ((), ())), preferred_element_type=jnp.float32
+        weighted, columns, (((0,), (0,)), ((), ())), preferred_element_type=jnp.float32
     )
 
 
@@ -42,21 +42,22 @@
 
 def halving_scatter(partial, axis, order):
     size = lax.axis_size(axis)
-    levels = size.bit_length() - 1
     index = lax.axis_index(axis)
-    rows, cols = partial.shape
-    blocks = partial.reshape((2,) * levels + (rows // size, cols))
-    for step, bit in enumerate(order):
-        dim = levels - 1 - bit
-        dim -= sum(1 for done in order[:step] if levels - 1 - done < dim)
+    width = partial.shape[1] // size
+    held = list(range(size))
+    blocks = partial
+    for bit in order:
         mine = (index >> bit) & 1
-        low = lax.index_in_dim(blocks, 0, dim, keepdims=False)
-        high = lax.index_in_dim(blocks, 1, dim, keepdims=False)
-        keep = jnp.where(mine == 1, high, low)
-        send = jnp.where(mine == 1, low, high)
+        low = [k for k, block in enumerate(held) if not (block >> bit) & 1]
+        high = [k for k, block in enumerate(held) if (block >> bit) & 1]
+        low_part = jnp.concatenate([blocks[:, k * width:(k + 1) * width] for k in low], axis=1)
+        high_part = jnp.concatenate([blocks[:, k * width:(k + 1) * width] for k in high], axis=1)
+        keep = jnp.where(mine == 1, high_part, low_part)
+        send = jnp.where(mine == 1, low_part, high_part)
         pairs = [(i, i ^ (1 << bit)) for i in range(size)]
         blocks = keep + lax.ppermute(send, axis, pairs)
-    return blocks.reshape(rows // size, cols)
+        held = [held[k] & ~(1 << bit) for k in low]
+    return blocks
 
 
 def doubling_gather(part, axis, order):
@@ -78,19 +79,19 @@
     return current.reshape((-1,) + part.shape[1:])
 
 
-def scatter_rows(partial, axis):
+def scatter_rows(partial_t, axis):
     size = lax.axis_size(axis)
-    cols = partial.shape[1]
+    cols = partial_t.shape[0]
     if size & (size - 1) or size == 1 or cols % 2:
-        return lax.psum_scatter(partial, axis, scatter_dimension=0, tiled=True)
+        return lax.psum_scatter(partial_t, axis, scatter_dimension=1, tiled=True)
     first, second = bit_orders(size)
     half = cols // 2
     return jnp.concatenate(
         [
-            halving_scatter(partial[:, :half], axis, first),
-            halving_scatter(partial[:, half:], axis, second),
+            halving_scatter(partial_t[:half], axis, first),
+            halving_scatter(partial_t[half:], axis, second),
         ],
-        axis=1,
+        axis=0,
     )
 
 
@@ -122,13 +123,13 @@
     squares = butterfly_sum(jnp.sum(grad_shard * grad_shard), ("pipe", "tensor", "dp"))
     clip_factor = jnp.minimum(1.0, CLIP_NORM / jnp.sqrt(squares))
     clipped = clip_factor * grad_shard
-    moment1 = MOMENT_DECAY * first_moment[0] + (1.0 - MOMENT_DECAY) * clipped
-    moment2 = SQUARE_DECAY * second_moment[0] + (1.0 - SQUARE_DECAY) * clipped * clipped
+    moment1 = MOMENT_DECAY * first_moment[0].T + (1.0 - MOMENT_DECAY) * clipped
+    moment2 = SQUARE_DECAY * second_moment[0].T + (1.0 - SQUARE_DECAY) * clipped * clipped
     update = (
         moment1 / FIRST_CORRECTION / (jnp.sqrt(moment2 / SECOND_CORRECTION) + EPSILON)
-        + WEIGHT_DECAY * master[0]
+        + WEIGHT_DECAY * master[0].T
     )
-    return gather_rows(update.astype(jnp.bfloat16), "dp")[None]
+    return gather_rows(update.astype(jnp.bfloat16).T, "dp")[None]
 
 
 def solution(mesh):

time: 157 us -> 139 us (0.89)
  local copies, waits for them, and re-layouts: 24.9 us -> 5.83 us
  waiting for transfers between devices: 82.5 us -> 77 us
  starting transfers between devices: 26.7 us -> 31.1 us
  other arithmetic: 12.1 us -> 13.8 us
    slice x3, local copies, waits for them, and re-layouts: 9.77 us -> 1.92 us  [halving_scatter(): blocks[:, k * width:(k + 1) * width]]
    reshape x2 -> x0, local copies, waits for them, and re-layouts: 7.01 us -> none  [halving_scatter(): blocks = partial.reshape((2,) * levels + (rows // size, cols))]
    unnamed x12 -> x17, local copies, waits for them, and re-layouts: 7.95 us -> 2.56 us
    ppermute x6, waiting for transfers between devices: 25.9 us -> 21 us  [doubling_gather(): other = lax.ppermute(current, axis, pairs)]
    ppermute x5, waiting for transfers between devices: 8.13 us -> 3.71 us  [butterfly_sum(): value = value + lax.ppermute(value, axis, pairs)]
    ppermute x5, starting transfers between devices: 9.02 us -> 13 us  [butterfly_sum(): value = value + lax.ppermute(value, axis, pairs)]
    ppermute x6, waiting for transfers between devices: 48.5 us -> 52.4 us  [halving_scatter(): blocks = keep + lax.ppermute(send, axis, pairs)]
    add x6, other arithmetic: 3.17 us -> 5.18 us  [halving_scatter(): blocks = keep + lax.ppermute(send, axis, pairs)]
  transfers between devices with their start and end apart: 17 -> 17, of which waited for: 15 -> 17; matrix products, arithmetic and copies ran while one was open for 14% -> 7% of each run, Pallas kernels for 0% -> 0%
where the time goes in v3:
time: 139 us
  waiting for transfers between devices  77 us (55%)
  starting transfers between devices  31.1 us (22%)
  other arithmetic  13.8 us (10%)
  matrix products  6.18 us (4%)
  local copies, waits for them, and re-layouts  5.83 us (4%)
  between operations  4.91 us (4%)
    ppermute x6, waiting for transfers between devices, halving_scatter(): blocks = keep + lax.ppermute(send, axis, pairs)  52.4 us
    ppermute x6, waiting for transfers between devices, doubling_gather(): other = lax.ppermute(current, axis, pairs)  21 us
    ppermute x5, starting transfers between devices, butterfly_sum(): value = value + lax.ppermute(value, axis, pairs)  13 us
    ppermute x6, starting transfers between devices, halving_scatter(): blocks = keep + lax.ppermute(send, axis, pairs)  10.1 us
    ppermute x6, starting transfers between devices, doubling_gather(): other = lax.ppermute(current, axis, pairs)  8.08 us
    dot_general x1, matrix products, slot_term(): lax.dot_general(weighted, columns, (((0,), (0,)), ((), ())), preferred_el...  6.18 us
    add x6, other arithmetic, halving_scatter(): blocks = keep + lax.ppermute(send, axis, pairs)  5.18 us
    ppermute x5, waiting for transfers between devices, butterfly_sum(): value = value + lax.ppermute(value, axis, pairs)  3.71 us
  transfers between devices with their start and end apart: 17, of which 17 were waited for; matrix products, arithmetic and copies ran while one was open for 7% of the time, Pallas kernels for 0%

profile of v3, /device:TPU:0, one launch (start us, length us, event | category | flops | bytes accessed | tf_op | source)
XLA Modules:
  0.0 138.9 jit_solution(18420683884368699981)
XLA Ops:
  0.0 1.3 convert_bitcast_fusion
  1.3 6.2 %fusion.2 = f32[256,4096]{1,0:T(8,128)S(1)} fusion(bf16[1,8,128,4096]{3,2,1,0:T(8,128)(2,1)} %param.6, bf16[1,8,128,256]{3,2,1,0:T(8,128)(2,1)} %param.7, bf16[8]{0:T(256)(128)(2,1)S(1)} %get-tuple-element.37), kind=kOutput, calls=%fused_computation.2 | convolution fusion | flops 2147745792 | bytes 13107216 | tf_op jit(solution)/shard_map/dot_general | solution.py:19
  7.5 1.9 %copy-done = f32[256,4096]{1,0:T(8,128)} copy-done((f32[256,4096]{1,0:T(8,128)}, f32[256,4096]{1,0:T(8,128)S(1)}, u32[]{:S(2)}) %copy-start) | copy-done | bytes 4194328
  9.7 1.2 fusion.6
  10.9 2.9 %collective-permute-start = (f32[128,2048]{1,0:T(8,128)}, f32[128,2048]{1,0:T(8,128)}, u32[]{:S(2)}, u32[]{:S(2)}) collective-permute-start(f32[128,2048]{1,0:T(8,128)} %fusion.6), channel_id=1, source_target_pairs={{0,2},{2,0},{4,6},{6,4},{8,10},{10,8},{12,14},{14,12},{1,3},{3,1},... | collective-permute-start | bytes 3145736 | tf_op jit(solution)/shard_map/ppermute | solution.py:58
  13.9 1.7 %fusion.21 = (f32[128,1024]{1,0:T(8,128)S(1)}, f32[128,1024]{1,0:T(8,128)S(1)}, f32[128,1024]{1,0:T(8,128)S(1)}, f32[128,1024]{1,0:T(8,128)S(1)}) fusion(f32[256,4096]{1,0:T(8,128)} %copy-done), kind=kLoop, calls=%fused_computation.58 | loop fusion | bytes 4194304 | tf_op jit(solution)/shard_map/slice | solution.py:54
  15.5 1.1 fusion.5
  16.6 1.6 %collective-permute-start.3 = (f32[128,2048]{1,0:T(8,128)}, f32[128,2048]{1,0:T(8,128)}, u32[]{:S(2)}, u32[]{:S(2)}) collective-permute-start(f32[128,2048]{1,0:T(8,128)} %fusion.5), channel_id=1, source_target_pairs={{0,4},{2,6},{4,0},{6,2},{8,12},{10,14},{12,8},{14,10},{1,5},{3,7},... | collective-permute-start | bytes 3145736 | tf_op jit(solution)/shard_map/ppermute | solution.py:58
  18.2 19.1 %collective-permute-done = f32[128,2048]{1,0:T(8,128)} collective-permute-done((f32[128,2048]{1,0:T(8,128)}, f32[128,2048]{1,0:T(8,128)}, u32[]{:S(2)}, u32[]{:S(2)}) %collective-permute-start) | collective-permute-done | bytes 1048608 | tf_op jit(solution)/shard_map/ppermute | solution.py:58
  37.3 1.6 %select_add_fusion.1 = f32[128,2048]{1,0:T(8,128)S(1)} fusion(f32[128,2048]{1,0:T(8,128)} %collective-permute-done, f32[128,512]{1,0:T(8,128)S(1)} %get-tuple-element.6, f32[128,512]{1,0:T(8,128)S(1)} %get-tuple-element.7, f32[128,512]{1,0:T(8,128)S(1)} %get-tuple-element.8, f32[128,512]{1,0:T(8,128)S(1)} %get-tuple-element.9, f32[128,512]{1,0:T(8,128)} %copy-done.1, ...), kind=kLoop, calls=%fused_computation.11 | loop fusion | flops 2097152 | bytes 4194305 | tf_op jit(solution)/shard_map/add | solution.py:58
  39.1 1.9 %collective-permute-start.1 = (f32[128,1024]{1,0:T(8,128)S(1)}, f32[128,1024]{1,0:T(8,128)S(1)}, u32[]{:S(2)}, u32[]{:S(2)}) collective-permute-start(f32[128,1024]{1,0:T(8,128)S(1)} %fusion.17), channel_id=1, source_target_pairs={{0,4},{2,6},{4,0},{6,2},{8,12},{10,14},{12,8},{14,10},{1,5},{3,7},... | collective-permute-start | bytes 1572872 | tf_op jit(solution)/shard_map/ppermute | solution.py:58
  41.9 1.4 select_add_fusion
  43.4 2.7 %collective-permute-start.4 = (f32[128,1024]{1,0:T(8,128)S(1)}, f32[128,1024]{1,0:T(8,128)S(1)}, u32[]{:S(2)}, u32[]{:S(2)}) collective-permute-start(f32[128,1024]{1,0:T(8,128)S(1)} %slice_select_fusion), channel_id=1, source_target_pairs={{0,8},{2,10},{4,12},{6,14},{8,0},{10,2},{12,4},{14,6},{1,9},{3,11}... | collective-permute-start | bytes 1572872 | tf_op jit(solution)/shard_map/ppermute | solution.py:58
  46.1 16.1 %collective-permute-done.1 = f32[128,1024]{1,0:T(8,128)S(1)} collective-permute-done((f32[128,1024]{1,0:T(8,128)S(1)}, f32[128,1024]{1,0:T(8,128)S(1)}, u32[]{:S(2)}, u32[]{:S(2)}) %collective-permute-start.1) | collective-permute-done | bytes 524320 | tf_op jit(solution)/shard_map/ppermute | solution.py:58
  62.4 12.6 %collective-permute-done.4 = f32[128,1024]{1,0:T(8,128)S(1)} collective-permute-done((f32[128,1024]{1,0:T(8,128)S(1)}, f32[128,1024]{1,0:T(8,128)S(1)}, u32[]{:S(2)}, u32[]{:S(2)}) %collective-permute-start.4) | collective-permute-done | bytes 524320 | tf_op jit(solution)/shard_map/ppermute | solution.py:58
  78.0 1.1 collective-permute-done.2
  80.1 2.5 %collective-permute-done.5 = f32[128,512]{1,0:T(8,128)} collective-permute-done((f32[128,512]{1,0:T(8,128)}, f32[128,512]{1,0:T(8,128)}, u32[]{:S(2)}, u32[]{:S(2)}) %collective-permute-start.5) | collective-permute-done | bytes 262176 | tf_op jit(solution)/shard_map/ppermute | solution.py:58
  84.3 1.2 collective-permute-done.6
  86.9 2.9 %collective-permute-start.7 = (f32[]{:T(128)}, f32[]{:T(128)}, u32[]{:S(2)}, u32[]{:S(2)}) collective-permute-start(f32[]{:T(128)} %add.54), channel_id=1, source_target_pairs={{0,1},{1,0},{2,3},{3,2},{4,5},{5,4},{6,7},{7,6},{8,9},{9,8},{10,11... | collective-permute-start | bytes 20 | tf_op jit(solution)/shard_map/ppermute | solution.py:33
  91.1 2.2 %collective-permute-start.8 = (f32[]{:T(128)}, f32[]{:T(128)}, u32[]{:S(2)}, u32[]{:S(2)}) collective-permute-start(f32[]{:T(128)} %add.55), channel_id=1, source_target_pairs={{0,2},{2,0},{4,6},{6,4},{8,10},{10,8},{12,14},{14,12},{1,3},{3,1},... | collective-permute-start | bytes 20 | tf_op jit(solution)/shard_map/ppermute | solution.py:33
  93.4 1.3 collective-permute-done.8
  95.3 3.3 %collective-permute-start.9 = (f32[]{:T(128)}, f32[]{:T(128)}, u32[]{:S(2)}, u32[]{:S(2)}) collective-permute-start(f32[]{:T(128)} %add.56), channel_id=1, source_target_pairs={{0,4},{2,6},{4,0},{6,2},{8,12},{10,14},{12,8},{14,10},{1,5},{3,7},... | collective-permute-start | bytes 20 | tf_op jit(solution)/shard_map/ppermute | solution.py:33
  99.6 4.6 %collective-permute-start.10 = (f32[]{:T(128)}, f32[]{:T(128)}, u32[]{:S(2)}, u32[]{:S(2)}) collective-permute-start(f32[]{:T(128)} %add.57), channel_id=1, source_target_pairs={{0,8},{2,10},{4,12},{6,14},{8,0},{10,2},{12,4},{14,6},{1,9},{3,11}... | collective-permute-start | bytes 20 | tf_op jit(solution)/shard_map/ppermute | solution.py:33
  105.6 3.0 %collective-permute-start.11 = (bf16[512,128]{0,1:T(8,128)(2,1)S(1)}, bf16[512,128]{0,1:T(8,128)(2,1)S(1)}, u32[]{:S(2)}, u32[]{:S(2)}) collective-permute-start(bf16[512,128]{0,1:T(8,128)(2,1)S(1)} %get-tuple-element.35), channel_id=1, source_target_pairs={{0,8},{2,10},{4,12},{6,14},{8,0},{10,2},{12,4},{14,6},{1,9},{3,11}... | collective-permute-start | bytes 393224 | tf_op jit(solution)/shard_map/ppermute | solution.py:72
  108.6 2.9 %collective-permute-done.11 = bf16[512,128]{0,1:T(8,128)(2,1)S(1)} collective-permute-done((bf16[512,128]{0,1:T(8,128)(2,1)S(1)}, bf16[512,128]{0,1:T(8,128)(2,1)S(1)}, u32[]{:S(2)}, u32[]{:S(2)}) %collective-permute-start.11) | collective-permute-done | bytes 131104 | tf_op jit(solution)/shard_map/ppermute | solution.py:72
  111.5 2.0 %collective-permute-done.14 = bf16[512,128]{0,1:T(8,128)(2,1)S(1)} collective-permute-done((bf16[512,128]{0,1:T(8,128)(2,1)S(1)}, bf16[512,128]{0,1:T(8,128)(2,1)S(1)}, u32[]{:S(2)}, u32[]{:S(2)}) %collective-permute-start.14) | collective-permute-done | bytes 131104 | tf_op jit(solution)/shard_map/ppermute | solution.py:72
  113.6 2.1 %collective-permute-start.12 = (bf16[2,512,128]{1,2,0:T(8,128)(2,1)S(1)}, bf16[2,512,128]{1,2,0:T(8,128)(2,1)S(1)}, u32[]{:S(2)}, u32[]{:S(2)}) collective-permute-start(bf16[2,512,128]{1,2,0:T(8,128)(2,1)S(1)} %pad_maximum_fusion.8), channel_id=1, source_target_pairs={{0,4},{2,6},{4,0},{6,2},{8,12},{10,14},{12,8},{14,10},{1,5},{3,7},... | collective-permute-start | bytes 786440 | tf_op jit(solution)/shard_map/ppermute | solution.py:72
  115.7 2.7 %collective-permute-start.15 = (bf16[2,512,128]{1,2,0:T(8,128)(2,1)S(1)}, bf16[2,512,128]{1,2,0:T(8,128)(2,1)S(1)}, u32[]{:S(2)}, u32[]{:S(2)}) collective-permute-start(bf16[2,512,128]{1,2,0:T(8,128)(2,1)S(1)} %pad_maximum_fusion.9), channel_id=1, source_target_pairs={{0,8},{2,10},{4,12},{6,14},{8,0},{10,2},{12,4},{14,6},{1,9},{3,11}... | collective-permute-start | bytes 786440 | tf_op jit(solution)/shard_map/ppermute | solution.py:72
  118.4 4.2 %collective-permute-done.12 = bf16[2,512,128]{1,2,0:T(8,128)(2,1)S(1)} collective-permute-done((bf16[2,512,128]{1,2,0:T(8,128)(2,1)S(1)}, bf16[2,512,128]{1,2,0:T(8,128)(2,1)S(1)}, u32[]{:S(2)}, u32[]{:S(2)}) %collective-permute-start.12) | collective-permute-done | bytes 262176 | tf_op jit(solution)/shard_map/ppermute | solution.py:72
  122.6 3.4 %collective-permute-done.15 = bf16[2,512,128]{1,2,0:T(8,128)(2,1)S(1)} collective-permute-done((bf16[2,512,128]{1,2,0:T(8,128)(2,1)S(1)}, bf16[2,512,128]{1,2,0:T(8,128)(2,1)S(1)}, u32[]{:S(2)}, u32[]{:S(2)}) %collective-permute-start.15) | collective-permute-done | bytes 262176 | tf_op jit(solution)/shard_map/ppermute | solution.py:72
  127.1 8.2 %collective-permute-done.13 = bf16[2,2,512,128]{2,3,1,0:T(8,128)(2,1)S(1)} collective-permute-done((bf16[2,2,512,128]{2,3,1,0:T(8,128)(2,1)S(1)}, bf16[2,2,512,128]{2,3,1,0:T(8,128)(2,1)S(1)}, u32[]{:S(2)}, u32[]{:S(2)}) %collective-permute-start.13) | collective-permute-done | bytes 524320 | tf_op jit(solution)/shard_map/ppermute | solution.py:72
  137.4 1.5 %maximum_bitcast_fusion = bf16[1,4096,256]{2,1,0:T(8,128)(2,1)} fusion(bf16[4096,128]{1,0:T(8,128)(2,1)S(1)} %bitcast.75, bf16[4096,128]{1,0:T(8,128)(2,1)S(1)} %bitcast.74), kind=kLoop, calls=%fused_computation.3 | loop fusion | flops 4194304 | bytes 4194304 | tf_op jit(solution)/shard_map/broadcast_in_dim | solution.py:132
  (52 shorter events, 11.6 us)
Async XLA Ops:
  7.5 2.0 %copy-start = (f32[256,4096]{1,0:T(8,128)}, f32[256,4096]{1,0:T(8,128)S(1)}, u32[]{:S(2)}) copy-start(f32[256,4096]{1,0:T(8,128)S(1)} %fusion.2) | copy-start | bytes 12582916
  9.7 4.2 %copy-start.1 = (f32[128,512]{1,0:T(8,128)}, f32[128,512]{1,0:T(8,128)S(1)}, u32[]{:S(2)}) copy-start(f32[128,512]{1,0:T(8,128)S(1)} %get-tuple-element.10) | copy-start | bytes 786436
  9.7 4.2 %copy-start.2 = (f32[128,512]{1,0:T(8,128)}, f32[128,512]{1,0:T(8,128)S(1)}, u32[]{:S(2)}) copy-start(f32[128,512]{1,0:T(8,128)S(1)} %get-tuple-element.11) | copy-start | bytes 786436
  9.7 4.2 %copy-start.3 = (f32[128,512]{1,0:T(8,128)}, f32[128,512]{1,0:T(8,128)S(1)}, u32[]{:S(2)}) copy-start(f32[128,512]{1,0:T(8,128)S(1)} %get-tuple-element.12) | copy-start | bytes 786436
  10.9 26.4 %collective-permute-start = (f32[128,2048]{1,0:T(8,128)}, f32[128,2048]{1,0:T(8,128)}, u32[]{:S(2)}, u32[]{:S(2)}) collective-permute-start(f32[128,2048]{1,0:T(8,128)} %fusion.6), channel_id=1, source_target_pairs={{0,2},{2,0},{4,6},{6,4},{8,10},{10,8},{12,14},{14,12},{1,3},{3,1},... | collective-permute-start | bytes 3145736 | tf_op jit(solution)/shard_map/ppermute | solution.py:58
  16.6 25.3 %collective-permute-start.3 = (f32[128,2048]{1,0:T(8,128)}, f32[128,2048]{1,0:T(8,128)}, u32[]{:S(2)}, u32[]{:S(2)}) collective-permute-start(f32[128,2048]{1,0:T(8,128)} %fusion.5), channel_id=1, source_target_pairs={{0,4},{2,6},{4,0},{6,2},{8,12},{10,14},{12,8},{14,10},{1,5},{3,7},... | collective-permute-start | bytes 3145736 | tf_op jit(solution)/shard_map/ppermute | solution.py:58
  39.1 23.1 %collective-permute-start.1 = (f32[128,1024]{1,0:T(8,128)S(1)}, f32[128,1024]{1,0:T(8,128)S(1)}, u32[]{:S(2)}, u32[]{:S(2)}) collective-permute-start(f32[128,1024]{1,0:T(8,128)S(1)} %fusion.17), channel_id=1, source_target_pairs={{0,4},{2,6},{4,0},{6,2},{8,12},{10,14},{12,8},{14,10},{1,5},{3,7},... | collective-permute-start | bytes 1572872 | tf_op jit(solution)/shard_map/ppermute | solution.py:58
  43.3 34.0 %copy-start.4 = (f32[1,512,256]{2,1,0:T(8,128)S(1)}, f32[1,512,256]{2,1,0:T(8,128)}, u32[]{:S(2)}) copy-start(f32[1,512,256]{2,1,0:T(8,128)} %param.10) | copy-start | bytes 1572868
  43.3 34.2 %copy-start.5 = (f32[1,512,256]{2,1,0:T(8,128)S(1)}, f32[1,512,256]{2,1,0:T(8,128)}, u32[]{:S(2)}) copy-start(f32[1,512,256]{2,1,0:T(8,128)} %param.11) | copy-start | bytes 1572868
  43.4 34.4 %copy-start.6 = (f32[1,512,256]{2,1,0:T(8,128)S(1)}, f32[1,512,256]{2,1,0:T(8,128)}, u32[]{:S(2)}) copy-start(f32[1,512,256]{2,1,0:T(8,128)} %param.9) | copy-start | bytes 1572868
  43.4 31.6 %collective-permute-start.4 = (f32[128,1024]{1,0:T(8,128)S(1)}, f32[128,1024]{1,0:T(8,128)S(1)}, u32[]{:S(2)}, u32[]{:S(2)}) collective-permute-start(f32[128,1024]{1,0:T(8,128)S(1)} %slice_select_fusion), channel_id=1, source_target_pairs={{0,8},{2,10},{4,12},{6,14},{8,0},{10,2},{12,4},{14,6},{1,9},{3,11}... | collective-permute-start | bytes 1572872 | tf_op jit(solution)/shard_map/ppermute | solution.py:58
  62.3 16.8 %collective-permute-start.2 = (f32[128,512]{1,0:T(8,128)S(1)}, f32[128,512]{1,0:T(8,128)}, u32[]{:S(2)}, u32[]{:S(2)}) collective-permute-start(f32[128,512]{1,0:T(8,128)S(1)} %slice_select_fusion.2), channel_id=1, source_target_pairs={{0,8},{2,10},{4,12},{6,14},{8,0},{10,2},{12,4},{14,6},{1,9},{3,11}... | collective-permute-start | bytes 786440 | tf_op jit(solution)/shard_map/ppermute | solution.py:58
  75.9 6.7 %collective-permute-start.5 = (f32[128,512]{1,0:T(8,128)}, f32[128,512]{1,0:T(8,128)}, u32[]{:S(2)}, u32[]{:S(2)}) collective-permute-start(f32[128,512]{1,0:T(8,128)} %slice_select_fusion.1), channel_id=1, source_target_pairs={{0,2},{2,0},{4,6},{6,4},{8,10},{10,8},{12,14},{14,12},{1,3},{3,1},... | collective-permute-start | bytes 786440 | tf_op jit(solution)/shard_map/ppermute | solution.py:58
  84.3 1.2 collective-permute-start.6
  86.9 3.6 %collective-permute-start.7 = (f32[]{:T(128)}, f32[]{:T(128)}, u32[]{:S(2)}, u32[]{:S(2)}) collective-permute-start(f32[]{:T(128)} %add.54), channel_id=1, source_target_pairs={{0,1},{1,0},{2,3},{3,2},{4,5},{5,4},{6,7},{7,6},{8,9},{9,8},{10,11... | collective-permute-start | bytes 20 | tf_op jit(solution)/shard_map/ppermute | solution.py:33
  91.1 3.6 %collective-permute-start.8 = (f32[]{:T(128)}, f32[]{:T(128)}, u32[]{:S(2)}, u32[]{:S(2)}) collective-permute-start(f32[]{:T(128)} %add.55), channel_id=1, source_target_pairs={{0,2},{2,0},{4,6},{6,4},{8,10},{10,8},{12,14},{14,12},{1,3},{3,1},... | collective-permute-start | bytes 20 | tf_op jit(solution)/shard_map/ppermute | solution.py:33
  95.3 3.6 %collective-permute-start.9 = (f32[]{:T(128)}, f32[]{:T(128)}, u32[]{:S(2)}, u32[]{:S(2)}) collective-permute-start(f32[]{:T(128)} %add.56), channel_id=1, source_target_pairs={{0,4},{2,6},{4,0},{6,2},{8,12},{10,14},{12,8},{14,10},{1,5},{3,7},... | collective-permute-start | bytes 20 | tf_op jit(solution)/shard_map/ppermute | solution.py:33
  99.6 4.8 %collective-permute-start.10 = (f32[]{:T(128)}, f32[]{:T(128)}, u32[]{:S(2)}, u32[]{:S(2)}) collective-permute-start(f32[]{:T(128)} %add.57), channel_id=1, source_target_pairs={{0,8},{2,10},{4,12},{6,14},{8,0},{10,2},{12,4},{14,6},{1,9},{3,11}... | collective-permute-start | bytes 20 | tf_op jit(solution)/shard_map/ppermute | solution.py:33
  105.6 5.9 %collective-permute-start.11 = (bf16[512,128]{0,1:T(8,128)(2,1)S(1)}, bf16[512,128]{0,1:T(8,128)(2,1)S(1)}, u32[]{:S(2)}, u32[]{:S(2)}) collective-permute-start(bf16[512,128]{0,1:T(8,128)(2,1)S(1)} %get-tuple-element.35), channel_id=1, source_target_pairs={{0,8},{2,10},{4,12},{6,14},{8,0},{10,2},{12,4},{14,6},{1,9},{3,11}... | collective-permute-start | bytes 393224 | tf_op jit(solution)/shard_map/ppermute | solution.py:72
  108.5 5.0 %collective-permute-start.14 = (bf16[512,128]{0,1:T(8,128)(2,1)S(1)}, bf16[512,128]{0,1:T(8,128)(2,1)S(1)}, u32[]{:S(2)}, u32[]{:S(2)}) collective-permute-start(bf16[512,128]{0,1:T(8,128)(2,1)S(1)} %get-tuple-element.36), channel_id=1, source_target_pairs={{0,2},{2,0},{4,6},{6,4},{8,10},{10,8},{12,14},{14,12},{1,3},{3,1},... | collective-permute-start | bytes 393224 | tf_op jit(solution)/shard_map/ppermute | solution.py:72
  113.6 9.1 %collective-permute-start.12 = (bf16[2,512,128]{1,2,0:T(8,128)(2,1)S(1)}, bf16[2,512,128]{1,2,0:T(8,128)(2,1)S(1)}, u32[]{:S(2)}, u32[]{:S(2)}) collective-permute-start(bf16[2,512,128]{1,2,0:T(8,128)(2,1)S(1)} %pad_maximum_fusion.8), channel_id=1, source_target_pairs={{0,4},{2,6},{4,0},{6,2},{8,12},{10,14},{12,8},{14,10},{1,5},{3,7},... | collective-permute-start | bytes 786440 | tf_op jit(solution)/shard_map/ppermute | solution.py:72
  115.7 10.3 %collective-permute-start.15 = (bf16[2,512,128]{1,2,0:T(8,128)(2,1)S(1)}, bf16[2,512,128]{1,2,0:T(8,128)(2,1)S(1)}, u32[]{:S(2)}, u32[]{:S(2)}) collective-permute-start(bf16[2,512,128]{1,2,0:T(8,128)(2,1)S(1)} %pad_maximum_fusion.9), channel_id=1, source_target_pairs={{0,8},{2,10},{4,12},{6,14},{8,0},{10,2},{12,4},{14,6},{1,9},{3,11}... | collective-permute-start | bytes 786440 | tf_op jit(solution)/shard_map/ppermute | solution.py:72
  126.1 9.2 %collective-permute-start.13 = (bf16[2,2,512,128]{2,3,1,0:T(8,128)(2,1)S(1)}, bf16[2,2,512,128]{2,3,1,0:T(8,128)(2,1)S(1)}, u32[]{:S(2)}, u32[]{:S(2)}) collective-permute-start(bf16[2,2,512,128]{2,3,1,0:T(8,128)(2,1)S(1)} %pad_maximum_fusion.6), channel_id=1, source_target_pairs={{0,2},{2,0},{4,6},{6,4},{8,10},{10,8},{12,14},{14,12},{1,3},{3,1},... | collective-permute-start | bytes 1572872 | tf_op jit(solution)/shard_map/ppermute | solution.py:72
  127.1 9.4 %collective-permute-start.16 = (bf16[2,2,512,128]{2,3,1,0:T(8,128)(2,1)}, bf16[2,2,512,128]{2,3,1,0:T(8,128)(2,1)S(1)}, u32[]{:S(2)}, u32[]{:S(2)}) collective-permute-start(bf16[2,2,512,128]{2,3,1,0:T(8,128)(2,1)} %pad_maximum_fusion.7), channel_id=1, source_target_pairs={{0,4},{2,6},{4,0},{6,2},{8,12},{10,14},{12,8},{14,10},{1,5},{3,7},... | collective-permute-start | bytes 1572872 | tf_op jit(solution)/shard_map/ppermute | solution.py:72

commit v4 on v3

--- a/solution.py
+++ b/solution.py
@@ -37,7 +37,7 @@
 
 def bit_orders(size):
     bits = list(range(size.bit_length() - 1))
-    return bits, bits[1:] + bits[:1]
+    return bits, bits[1:2] + bits[:1] + bits[2:]
 
 
 def halving_scatter(partial, axis, order):

time: 139 us -> 136 us (0.978)
  other arithmetic: 13.8 us -> 10 us
  starting transfers between devices: 31.1 us -> 27.6 us
  local copies, waits for them, and re-layouts: 5.83 us -> 9.08 us
    ppermute x6, waiting for transfers between devices: 52.4 us -> 45 us  [halving_scatter(): blocks = keep + lax.ppermute(send, axis, pairs)]
    ppermute x6, waiting for transfers between devices: 21 us -> 25.7 us  [doubling_gather(): other = lax.ppermute(current, axis, pairs)]
    ppermute x5, starting transfers between devices: 13 us -> 9.36 us  [butterfly_sum(): value = value + lax.ppermute(value, axis, pairs)]
    add x6, other arithmetic: 5.18 us -> 1.64 us  [halving_scatter(): blocks = keep + lax.ppermute(send, axis, pairs)]
    ppermute x5, waiting for transfers between devices: 3.71 us -> 7 us  [butterfly_sum(): value = value + lax.ppermute(value, axis, pairs)]
    unnamed x17 -> x5, local copies, waits for them, and re-layouts: 2.56 us -> 5.64 us
    ppermute x6, starting transfers between devices: 10.1 us -> 11.6 us  [halving_scatter(): blocks = keep + lax.ppermute(send, axis, pairs)]
    ppermute x6, starting transfers between devices: 8.08 us -> 6.66 us  [doubling_gather(): other = lax.ppermute(current, axis, pairs)]
  transfers between devices with their start and end apart: 17 -> 17, of which waited for: 17 -> 16; matrix products, arithmetic and copies ran while one was open for 7% -> 8% of each run, Pallas kernels for 0% -> 0%
where the time goes in v4:
time: 136 us; the launch traced here: 135 us
  waiting for transfers between devices  77.6 us (57%)
  starting transfers between devices  27.6 us (20%)
  other arithmetic  10 us (7%)
  local copies, waits for them, and re-layouts  9.08 us (7%)
  matrix products  6.18 us (5%)
  between operations  4.64 us (3%)
    ppermute x6, waiting for transfers between devices, halving_scatter(): blocks = keep + lax.ppermute(send, axis, pairs)  45 us
    ppermute x6, waiting for transfers between devices, doubling_gather(): other = lax.ppermute(current, axis, pairs)  25.7 us
    ppermute x6, starting transfers between devices, halving_scatter(): blocks = keep + lax.ppermute(send, axis, pairs)  11.6 us
    ppermute x5, starting transfers between devices, butterfly_sum(): value = value + lax.ppermute(value, axis, pairs)  9.36 us
    ppermute x5, waiting for transfers between devices, butterfly_sum(): value = value + lax.ppermute(value, axis, pairs)  7 us
    ppermute x6, starting transfers between devices, doubling_gather(): other = lax.ppermute(current, axis, pairs)  6.66 us
    dot_general x1, matrix products, slot_term(): lax.dot_general(weighted, columns, (((0,), (0,)), ((), ())), preferred_el...  6.18 us
    unnamed x5, local copies, waits for them, and re-layouts  5.64 us
  transfers between devices with their start and end apart: 17, of which 16 were waited for; matrix products, arithmetic and copies ran while one was open for 8% of the time, Pallas kernels for 0%

profile of v4, /device:TPU:0, one launch (start us, length us, event | category | flops | bytes accessed | tf_op | source)
XLA Modules:
  0.0 135.2 jit_solution(14781293018466290864)
XLA Ops:
  0.0 1.4 %convert_bitcast_fusion = (bf16[8]{0:T(256)(128)(2,1)S(1)}, s32[]{:T(128)}) fusion(s32[1,8]{1,0:T(1,128)} %param.8), kind=kLoop, calls=%fused_computation.58 | loop fusion | flops 15 | bytes 52 | tf_op jit(solution)/shard_map/convert_element_type | solution.py:16
  1.4 6.2 %fusion.2 = f32[256,4096]{1,0:T(8,128)S(1)} fusion(bf16[1,8,128,4096]{3,2,1,0:T(8,128)(2,1)} %param.6, bf16[1,8,128,256]{3,2,1,0:T(8,128)(2,1)} %param.7, bf16[8]{0:T(256)(128)(2,1)S(1)} %get-tuple-element.38), kind=kOutput, calls=%fused_computation.2 | convolution fusion | flops 2147745792 | bytes 13107216 | tf_op jit(solution)/shard_map/dot_general | solution.py:19
  7.6 1.9 %copy-done = f32[256,4096]{1,0:T(8,128)} copy-done((f32[256,4096]{1,0:T(8,128)}, f32[256,4096]{1,0:T(8,128)S(1)}, u32[]{:S(2)}) %copy-start) | copy-done | bytes 4194328
  10.8 2.9 %collective-permute-start = (f32[128,2048]{1,0:T(8,128)}, f32[128,2048]{1,0:T(8,128)S(1)}, u32[]{:S(2)}, u32[]{:S(2)}) collective-permute-start(f32[128,2048]{1,0:T(8,128)} %fusion.6), channel_id=1, source_target_pairs={{0,2},{2,0},{4,6},{6,4},{8,10},{10,8},{12,14},{14,12},{1,3},{3,1},... | collective-permute-start | bytes 3145736 | tf_op jit(solution)/shard_map/ppermute | solution.py:58
  13.7 1.8 %fusion.22 = (f32[128,1024]{1,0:T(8,128)S(1)}, f32[128,1024]{1,0:T(8,128)S(1)}, f32[128,1024]{1,0:T(8,128)S(1)}, f32[128,1024]{1,0:T(8,128)S(1)}) fusion(f32[256,4096]{1,0:T(8,128)} %copy-done), kind=kLoop, calls=%fused_computation.60 | loop fusion | bytes 4194304 | tf_op jit(solution)/shard_map/slice | solution.py:54
  15.6 1.6 %collective-permute-start.3 = (f32[128,2048]{1,0:T(8,128)S(1)}, f32[128,2048]{1,0:T(8,128)S(1)}, u32[]{:S(2)}, u32[]{:S(2)}) collective-permute-start(f32[128,2048]{1,0:T(8,128)S(1)} %fusion.5), channel_id=1, source_target_pairs={{0,4},{2,6},{4,0},{6,2},{8,12},{10,14},{12,8},{14,10},{1,5},{3,7},... | collective-permute-start | bytes 3145736 | tf_op jit(solution)/shard_map/ppermute | solution.py:58
  17.3 19.8 %collective-permute-done = f32[128,2048]{1,0:T(8,128)S(1)} collective-permute-done((f32[128,2048]{1,0:T(8,128)}, f32[128,2048]{1,0:T(8,128)S(1)}, u32[]{:S(2)}, u32[]{:S(2)}) %collective-permute-start) | collective-permute-done | bytes 1048608 | tf_op jit(solution)/shard_map/ppermute | solution.py:58
  37.4 1.9 %collective-permute-start.1 = (f32[128,1024]{1,0:T(8,128)S(1)}, f32[128,1024]{1,0:T(8,128)S(1)}, u32[]{:S(2)}, u32[]{:S(2)}) collective-permute-start(f32[128,1024]{1,0:T(8,128)S(1)} %fusion.18), channel_id=1, source_target_pairs={{0,4},{2,6},{4,0},{6,2},{8,12},{10,14},{12,8},{14,10},{1,5},{3,7},... | collective-permute-start | bytes 1572872 | tf_op jit(solution)/shard_map/ppermute | solution.py:58
  39.3 1.9 %collective-permute-done.3 = f32[128,2048]{1,0:T(8,128)S(1)} collective-permute-done((f32[128,2048]{1,0:T(8,128)S(1)}, f32[128,2048]{1,0:T(8,128)S(1)}, u32[]{:S(2)}, u32[]{:S(2)}) %collective-permute-start.3) | collective-permute-done | bytes 1048608 | tf_op jit(solution)/shard_map/ppermute | solution.py:58
  42.3 9.2 %collective-permute-done.1 = f32[128,1024]{1,0:T(8,128)S(1)} collective-permute-done((f32[128,1024]{1,0:T(8,128)S(1)}, f32[128,1024]{1,0:T(8,128)S(1)}, u32[]{:S(2)}, u32[]{:S(2)}) %collective-permute-start.1) | collective-permute-done | bytes 524320 | tf_op jit(solution)/shard_map/ppermute | solution.py:58
  51.7 2.7 %collective-permute-start.2 = (f32[128,512]{1,0:T(8,128)S(1)}, f32[128,512]{1,0:T(8,128)S(1)}, u32[]{:S(2)}, u32[]{:S(2)}) collective-permute-start(f32[128,512]{1,0:T(8,128)S(1)} %slice_select_fusion.1), channel_id=1, source_target_pairs={{0,8},{2,10},{4,12},{6,14},{8,0},{10,2},{12,4},{14,6},{1,9},{3,11}... | collective-permute-start | bytes 786440 | tf_op jit(solution)/shard_map/ppermute | solution.py:58
  56.2 2.4 %collective-permute-start.5 = (f32[128,512]{1,0:T(8,128)}, f32[128,512]{1,0:T(8,128)S(1)}, u32[]{:S(2)}, u32[]{:S(2)}) collective-permute-start(f32[128,512]{1,0:T(8,128)} %slice_select_fusion), channel_id=1, source_target_pairs={{0,8},{2,10},{4,12},{6,14},{8,0},{10,2},{12,4},{14,6},{1,9},{3,11}... | collective-permute-start | bytes 786440 | tf_op jit(solution)/shard_map/ppermute | solution.py:58
  59.2 1.2 copy.11
  60.5 1.2 copy.13
  61.7 1.2 copy.14
  63.0 9.5 %collective-permute-done.2 = f32[128,512]{1,0:T(8,128)S(1)} collective-permute-done((f32[128,512]{1,0:T(8,128)S(1)}, f32[128,512]{1,0:T(8,128)S(1)}, u32[]{:S(2)}, u32[]{:S(2)}) %collective-permute-start.2) | collective-permute-done | bytes 262176 | tf_op jit(solution)/shard_map/ppermute | solution.py:58
  72.5 4.5 %collective-permute-done.5 = f32[128,512]{1,0:T(8,128)S(1)} collective-permute-done((f32[128,512]{1,0:T(8,128)}, f32[128,512]{1,0:T(8,128)S(1)}, u32[]{:S(2)}, u32[]{:S(2)}) %collective-permute-start.5) | collective-permute-done | bytes 262176 | tf_op jit(solution)/shard_map/ppermute | solution.py:58
  80.3 2.7 %collective-permute-start.7 = (f32[]{:T(128)}, f32[]{:T(128)}, u32[]{:S(2)}, u32[]{:S(2)}) collective-permute-start(f32[]{:T(128)} %add.54), channel_id=1, source_target_pairs={{0,1},{1,0},{2,3},{3,2},{4,5},{5,4},{6,7},{7,6},{8,9},{9,8},{10,11... | collective-permute-start | bytes 20 | tf_op jit(solution)/shard_map/ppermute | solution.py:33
  84.5 1.4 %collective-permute-start.8 = (f32[]{:T(128)}, f32[]{:T(128)}, u32[]{:S(2)}, u32[]{:S(2)}) collective-permute-start(f32[]{:T(128)} %add.55), channel_id=1, source_target_pairs={{0,2},{2,0},{4,6},{6,4},{8,10},{10,8},{12,14},{14,12},{1,3},{3,1},... | collective-permute-start | bytes 20 | tf_op jit(solution)/shard_map/ppermute | solution.py:33
  85.9 2.2 %collective-permute-done.8 = f32[]{:T(128)} collective-permute-done((f32[]{:T(128)}, f32[]{:T(128)}, u32[]{:S(2)}, u32[]{:S(2)}) %collective-permute-start.8) | collective-permute-done | bytes 36 | tf_op jit(solution)/shard_map/ppermute | solution.py:33
  88.7 2.0 %collective-permute-start.9 = (f32[]{:T(128)}, f32[]{:T(128)}, u32[]{:S(2)}, u32[]{:S(2)}) collective-permute-start(f32[]{:T(128)} %add.56), channel_id=1, source_target_pairs={{0,4},{2,6},{4,0},{6,2},{8,12},{10,14},{12,8},{14,10},{1,5},{3,7},... | collective-permute-start | bytes 20 | tf_op jit(solution)/shard_map/ppermute | solution.py:33
  90.7 1.6 %collective-permute-done.9 = f32[]{:T(128)} collective-permute-done((f32[]{:T(128)}, f32[]{:T(128)}, u32[]{:S(2)}, u32[]{:S(2)}) %collective-permute-start.9) | collective-permute-done | bytes 36 | tf_op jit(solution)/shard_map/ppermute | solution.py:33
  92.9 3.3 %collective-permute-start.10 = (f32[]{:T(128)}, f32[]{:T(128)}, u32[]{:S(2)}, u32[]{:S(2)}) collective-permute-start(f32[]{:T(128)} %add.57), channel_id=1, source_target_pairs={{0,8},{2,10},{4,12},{6,14},{8,0},{10,2},{12,4},{14,6},{1,9},{3,11}... | collective-permute-start | bytes 20 | tf_op jit(solution)/shard_map/ppermute | solution.py:33
  98.5 2.0 %collective-permute-start.11 = (bf16[512,128]{0,1:T(8,128)(2,1)S(1)}, bf16[512,128]{0,1:T(8,128)(2,1)S(1)}, u32[]{:S(2)}, u32[]{:S(2)}) collective-permute-start(bf16[512,128]{0,1:T(8,128)(2,1)S(1)} %slice.154), channel_id=1, source_target_pairs={{0,8},{2,10},{4,12},{6,14},{8,0},{10,2},{12,4},{14,6},{1,9},{3,11}... | collective-permute-start | bytes 393224 | tf_op jit(solution)/shard_map/ppermute | solution.py:72
  100.4 7.7 %collective-permute-done.11 = bf16[512,128]{0,1:T(8,128)(2,1)S(1)} collective-permute-done((bf16[512,128]{0,1:T(8,128)(2,1)S(1)}, bf16[512,128]{0,1:T(8,128)(2,1)S(1)}, u32[]{:S(2)}, u32[]{:S(2)}) %collective-permute-start.11) | collective-permute-done | bytes 131104 | tf_op jit(solution)/shard_map/ppermute | solution.py:72
  108.3 3.9 %collective-permute-start.12 = (bf16[2,512,128]{1,2,0:T(8,128)(2,1)S(1)}, bf16[2,512,128]{1,2,0:T(8,128)(2,1)S(1)}, u32[]{:S(2)}, u32[]{:S(2)}) collective-permute-start(bf16[2,512,128]{1,2,0:T(8,128)(2,1)S(1)} %pad_maximum_fusion.10), channel_id=1, source_target_pairs={{0,4},{2,6},{4,0},{6,2},{8,12},{10,14},{12,8},{14,10},{1,5},{3,7},... | collective-permute-start | bytes 786440 | tf_op jit(solution)/shard_map/ppermute | solution.py:72
  112.1 3.4 %collective-permute-done.14 = bf16[512,128]{0,1:T(8,128)(2,1)S(1)} collective-permute-done((bf16[512,128]{0,1:T(8,128)(2,1)S(1)}, bf16[512,128]{0,1:T(8,128)(2,1)S(1)}, u32[]{:S(2)}, u32[]{:S(2)}) %collective-permute-start.14) | collective-permute-done | bytes 131104 | tf_op jit(solution)/shard_map/ppermute | solution.py:72
  115.7 1.7 %collective-permute-done.12 = bf16[2,512,128]{1,2,0:T(8,128)(2,1)S(1)} collective-permute-done((bf16[2,512,128]{1,2,0:T(8,128)(2,1)S(1)}, bf16[2,512,128]{1,2,0:T(8,128)(2,1)S(1)}, u32[]{:S(2)}, u32[]{:S(2)}) %collective-permute-start.12) | collective-permute-done | bytes 262176 | tf_op jit(solution)/shard_map/ppermute | solution.py:72
  117.9 4.6 %collective-permute-done.15 = bf16[2,512,128]{1,2,0:T(8,128)(2,1)S(1)} collective-permute-done((bf16[2,512,128]{1,2,0:T(8,128)(2,1)S(1)}, bf16[2,512,128]{1,2,0:T(8,128)(2,1)S(1)}, u32[]{:S(2)}, u32[]{:S(2)}) %collective-permute-start.15) | collective-permute-done | bytes 262176 | tf_op jit(solution)/shard_map/ppermute | solution.py:72
  123.7 4.4 %collective-permute-done.13 = bf16[2,2,512,128]{2,3,1,0:T(8,128)(2,1)S(1)} collective-permute-done((bf16[2,2,512,128]{2,3,1,0:T(8,128)(2,1)S(1)}, bf16[2,2,512,128]{2,3,1,0:T(8,128)(2,1)S(1)}, u32[]{:S(2)}, u32[]{:S(2)}) %collective-permute-start.13) | collective-permute-done | bytes 524320 | tf_op jit(solution)/shard_map/ppermute | solution.py:72
  129.0 3.8 %collective-permute-done.16 = bf16[2,2,512,128]{2,3,1,0:T(8,128)(2,1)S(1)} collective-permute-done((bf16[2,2,512,128]{2,3,1,0:T(8,128)(2,1)}, bf16[2,2,512,128]{2,3,1,0:T(8,128)(2,1)S(1)}, u32[]{:S(2)}, u32[]{:S(2)}) %collective-permute-start.16) | collective-permute-done | bytes 524320 | tf_op jit(solution)/shard_map/ppermute | solution.py:72
  133.6 1.5 %maximum_bitcast_fusion = bf16[1,4096,256]{2,1,0:T(8,128)(2,1)} fusion(bf16[4096,128]{1,0:T(8,128)(2,1)S(1)} %bitcast.75, bf16[4096,128]{1,0:T(8,128)(2,1)S(1)} %bitcast.74), kind=kLoop, calls=%fused_computation.3 | loop fusion | flops 4194304 | bytes 4194304 | tf_op jit(solution)/shard_map/broadcast_in_dim | solution.py:132
  (43 shorter events, 12.9 us)
Async XLA Ops:
  7.6 1.9 %copy-start = (f32[256,4096]{1,0:T(8,128)}, f32[256,4096]{1,0:T(8,128)S(1)}, u32[]{:S(2)}) copy-start(f32[256,4096]{1,0:T(8,128)S(1)} %fusion.2) | copy-start | bytes 12582916
  10.8 26.3 %collective-permute-start = (f32[128,2048]{1,0:T(8,128)}, f32[128,2048]{1,0:T(8,128)S(1)}, u32[]{:S(2)}, u32[]{:S(2)}) collective-permute-start(f32[128,2048]{1,0:T(8,128)} %fusion.6), channel_id=1, source_target_pairs={{0,2},{2,0},{4,6},{6,4},{8,10},{10,8},{12,14},{14,12},{1,3},{3,1},... | collective-permute-start | bytes 3145736 | tf_op jit(solution)/shard_map/ppermute | solution.py:58
  15.6 25.6 %collective-permute-start.3 = (f32[128,2048]{1,0:T(8,128)S(1)}, f32[128,2048]{1,0:T(8,128)S(1)}, u32[]{:S(2)}, u32[]{:S(2)}) collective-permute-start(f32[128,2048]{1,0:T(8,128)S(1)} %fusion.5), channel_id=1, source_target_pairs={{0,4},{2,6},{4,0},{6,2},{8,12},{10,14},{12,8},{14,10},{1,5},{3,7},... | collective-permute-start | bytes 3145736 | tf_op jit(solution)/shard_map/ppermute | solution.py:58
  37.4 14.1 %collective-permute-start.1 = (f32[128,1024]{1,0:T(8,128)S(1)}, f32[128,1024]{1,0:T(8,128)S(1)}, u32[]{:S(2)}, u32[]{:S(2)}) collective-permute-start(f32[128,1024]{1,0:T(8,128)S(1)} %fusion.18), channel_id=1, source_target_pairs={{0,4},{2,6},{4,0},{6,2},{8,12},{10,14},{12,8},{14,10},{1,5},{3,7},... | collective-permute-start | bytes 1572872 | tf_op jit(solution)/shard_map/ppermute | solution.py:58
  42.3 12.0 %collective-permute-start.4 = (f32[128,1024]{1,0:T(8,128)}, f32[128,1024]{1,0:T(8,128)}, u32[]{:S(2)}, u32[]{:S(2)}) collective-permute-start(f32[128,1024]{1,0:T(8,128)} %fusion.17), channel_id=1, source_target_pairs={{0,2},{2,0},{4,6},{6,4},{8,10},{10,8},{12,14},{14,12},{1,3},{3,1},... | collective-permute-start | bytes 1572872 | tf_op jit(solution)/shard_map/ppermute | solution.py:58
  51.7 20.8 %collective-permute-start.2 = (f32[128,512]{1,0:T(8,128)S(1)}, f32[128,512]{1,0:T(8,128)S(1)}, u32[]{:S(2)}, u32[]{:S(2)}) collective-permute-start(f32[128,512]{1,0:T(8,128)S(1)} %slice_select_fusion.1), channel_id=1, source_target_pairs={{0,8},{2,10},{4,12},{6,14},{8,0},{10,2},{12,4},{14,6},{1,9},{3,11}... | collective-permute-start | bytes 786440 | tf_op jit(solution)/shard_map/ppermute | solution.py:58
  56.2 20.8 %collective-permute-start.5 = (f32[128,512]{1,0:T(8,128)}, f32[128,512]{1,0:T(8,128)S(1)}, u32[]{:S(2)}, u32[]{:S(2)}) collective-permute-start(f32[128,512]{1,0:T(8,128)} %slice_select_fusion), channel_id=1, source_target_pairs={{0,8},{2,10},{4,12},{6,14},{8,0},{10,2},{12,4},{14,6},{1,9},{3,11}... | collective-permute-start | bytes 786440 | tf_op jit(solution)/shard_map/ppermute | solution.py:58
  77.8 1.2 collective-permute-start.6
  80.3 3.6 %collective-permute-start.7 = (f32[]{:T(128)}, f32[]{:T(128)}, u32[]{:S(2)}, u32[]{:S(2)}) collective-permute-start(f32[]{:T(128)} %add.54), channel_id=1, source_target_pairs={{0,1},{1,0},{2,3},{3,2},{4,5},{5,4},{6,7},{7,6},{8,9},{9,8},{10,11... | collective-permute-start | bytes 20 | tf_op jit(solution)/shard_map/ppermute | solution.py:33
  84.5 3.6 %collective-permute-start.8 = (f32[]{:T(128)}, f32[]{:T(128)}, u32[]{:S(2)}, u32[]{:S(2)}) collective-permute-start(f32[]{:T(128)} %add.55), channel_id=1, source_target_pairs={{0,2},{2,0},{4,6},{6,4},{8,10},{10,8},{12,14},{14,12},{1,3},{3,1},... | collective-permute-start | bytes 20 | tf_op jit(solution)/shard_map/ppermute | solution.py:33
  88.7 3.6 %collective-permute-start.9 = (f32[]{:T(128)}, f32[]{:T(128)}, u32[]{:S(2)}, u32[]{:S(2)}) collective-permute-start(f32[]{:T(128)} %add.56), channel_id=1, source_target_pairs={{0,4},{2,6},{4,0},{6,2},{8,12},{10,14},{12,8},{14,10},{1,5},{3,7},... | collective-permute-start | bytes 20 | tf_op jit(solution)/shard_map/ppermute | solution.py:33
  92.9 4.5 %collective-permute-start.10 = (f32[]{:T(128)}, f32[]{:T(128)}, u32[]{:S(2)}, u32[]{:S(2)}) collective-permute-start(f32[]{:T(128)} %add.57), channel_id=1, source_target_pairs={{0,8},{2,10},{4,12},{6,14},{8,0},{10,2},{12,4},{14,6},{1,9},{3,11}... | collective-permute-start | bytes 20 | tf_op jit(solution)/shard_map/ppermute | solution.py:33
  98.5 9.7 %collective-permute-start.11 = (bf16[512,128]{0,1:T(8,128)(2,1)S(1)}, bf16[512,128]{0,1:T(8,128)(2,1)S(1)}, u32[]{:S(2)}, u32[]{:S(2)}) collective-permute-start(bf16[512,128]{0,1:T(8,128)(2,1)S(1)} %slice.154), channel_id=1, source_target_pairs={{0,8},{2,10},{4,12},{6,14},{8,0},{10,2},{12,4},{14,6},{1,9},{3,11}... | collective-permute-start | bytes 393224 | tf_op jit(solution)/shard_map/ppermute | solution.py:72
  108.1 7.4 %collective-permute-start.14 = (bf16[512,128]{0,1:T(8,128)(2,1)S(1)}, bf16[512,128]{0,1:T(8,128)(2,1)S(1)}, u32[]{:S(2)}, u32[]{:S(2)}) collective-permute-start(bf16[512,128]{0,1:T(8,128)(2,1)S(1)} %get-tuple-element.37), channel_id=1, source_target_pairs={{0,8},{2,10},{4,12},{6,14},{8,0},{10,2},{12,4},{14,6},{1,9},{3,11}... | collective-permute-start | bytes 393224 | tf_op jit(solution)/shard_map/ppermute | solution.py:72
  108.3 9.2 %collective-permute-start.12 = (bf16[2,512,128]{1,2,0:T(8,128)(2,1)S(1)}, bf16[2,512,128]{1,2,0:T(8,128)(2,1)S(1)}, u32[]{:S(2)}, u32[]{:S(2)}) collective-permute-start(bf16[2,512,128]{1,2,0:T(8,128)(2,1)S(1)} %pad_maximum_fusion.10), channel_id=1, source_target_pairs={{0,4},{2,6},{4,0},{6,2},{8,12},{10,14},{12,8},{14,10},{1,5},{3,7},... | collective-permute-start | bytes 786440 | tf_op jit(solution)/shard_map/ppermute | solution.py:72
  115.7 6.8 %collective-permute-start.15 = (bf16[2,512,128]{1,2,0:T(8,128)(2,1)S(1)}, bf16[2,512,128]{1,2,0:T(8,128)(2,1)S(1)}, u32[]{:S(2)}, u32[]{:S(2)}) collective-permute-start(bf16[2,512,128]{1,2,0:T(8,128)(2,1)S(1)} %pad_maximum_fusion.11), channel_id=1, source_target_pairs={{0,2},{2,0},{4,6},{6,4},{8,10},{10,8},{12,14},{14,12},{1,3},{3,1},... | collective-permute-start | bytes 786440 | tf_op jit(solution)/shard_map/ppermute | solution.py:72
  117.5 10.6 %collective-permute-start.13 = (bf16[2,2,512,128]{2,3,1,0:T(8,128)(2,1)S(1)}, bf16[2,2,512,128]{2,3,1,0:T(8,128)(2,1)S(1)}, u32[]{:S(2)}, u32[]{:S(2)}) collective-permute-start(bf16[2,2,512,128]{2,3,1,0:T(8,128)(2,1)S(1)} %pad_maximum_fusion.8), channel_id=1, source_target_pairs={{0,2},{2,0},{4,6},{6,4},{8,10},{10,8},{12,14},{14,12},{1,3},{3,1},... | collective-permute-start | bytes 1572872 | tf_op jit(solution)/shard_map/ppermute | solution.py:72
  123.4 9.4 %collective-permute-start.16 = (bf16[2,2,512,128]{2,3,1,0:T(8,128)(2,1)}, bf16[2,2,512,128]{2,3,1,0:T(8,128)(2,1)S(1)}, u32[]{:S(2)}, u32[]{:S(2)}) collective-permute-start(bf16[2,2,512,128]{2,3,1,0:T(8,128)(2,1)} %pad_maximum_fusion.9), channel_id=1, source_target_pairs={{0,4},{2,6},{4,0},{6,2},{8,12},{10,14},{12,8},{14,10},{1,5},{3,7},... | collective-permute-start | bytes 1572872 | tf_op jit(solution)/shard_map/ppermute | solution.py:72

commit v5 on v4

--- a/solution.py
+++ b/solution.py
@@ -12,10 +12,13 @@
 EPSILON = 1e-08
 
 
-def slot_term(inputs, key_grads, live_row, column_count):
+def slot_operands(inputs, key_grads, live_row, column_count):
     keep_mask = live_row.astype(key_grads.dtype)
     weighted = (key_grads * keep_mask[:, None, None]).reshape(-1, key_grads.shape[2])
-    columns = inputs.reshape(-1, column_count)
+    return weighted, inputs.reshape(-1, column_count)
+
+
+def slot_term(weighted, columns):
     return lax.dot_general(
         weighted, columns, (((0,), (0,)), ((), ())), preferred_element_type=jnp.float32
     )
@@ -79,17 +82,18 @@
     return current.reshape((-1,) + part.shape[1:])
 
 
-def scatter_rows(partial_t, axis):
+def scatter_rows(weighted, columns, axis):
     size = lax.axis_size(axis)
-    cols = partial_t.shape[0]
+    cols = weighted.shape[1]
     if size & (size - 1) or size == 1 or cols % 2:
+        partial_t = slot_term(weighted, columns)
         return lax.psum_scatter(partial_t, axis, scatter_dimension=1, tiled=True)
     first, second = bit_orders(size)
     half = cols // 2
     return jnp.concatenate(
         [
-            halving_scatter(partial_t[:half], axis, first),
-            halving_scatter(partial_t[half:], axis, second),
+            halving_scatter(slot_term(weighted[:, :half], columns), axis, first),
+            halving_scatter(slot_term(weighted[:, half:], columns), axis, second),
         ],
         axis=0,
     )
@@ -117,7 +121,8 @@
     live_row = live_slots[0]
     live_count = jnp.sum(live_row)
     features = inputs.shape[2]
-    summed = scatter_rows(slot_term(inputs, key_grads, live_row, features), "dp")
+    weighted, columns = slot_operands(inputs, key_grads, live_row, features)
+    summed = scatter_rows(weighted, columns, "dp")
     tokens_total = (live_count * (inputs.shape[1] * lax.axis_size("dp"))).astype(jnp.float32)
     grad_shard = summed / tokens_total
     squares = butterfly_sum(jnp.sum(grad_shard * grad_shard), ("pipe", "tensor", "dp"))

time: 136 us -> 136 us (level)
  waiting for transfers between devices: 77.6 us -> 72.5 us
  local copies, waits for them, and re-layouts: 9.08 us -> 5.71 us
  starting transfers between devices: 27.6 us -> 30.8 us
  matrix products: 6.18 us -> 9.33 us
  other arithmetic: 10 us -> 12.6 us
    dot_general x1 -> x2, matrix products: 6.18 us -> 9.33 us  [slot_term(): lax.dot_general(weighted, columns, (((0,), (0,)), ((), ())), preferred_el...]
    ppermute x6, waiting for transfers between devices: 45 us -> 43 us  [halving_scatter(): blocks = keep + lax.ppermute(send, axis, pairs)]
    ppermute x6, starting transfers between devices: 6.66 us -> 8.66 us  [doubling_gather(): other = lax.ppermute(current, axis, pairs)]
    ppermute x6, waiting for transfers between devices: 25.7 us -> 23.7 us  [doubling_gather(): other = lax.ppermute(current, axis, pairs)]
    unnamed x5 -> x3, local copies, waits for them, and re-layouts: 5.64 us -> 3.72 us
    slice x4, local copies, waits for them, and re-layouts: 2.1 us -> 0.59 us  [halving_scatter(): blocks[:, k * width:(k + 1) * width]]
  transfers between devices with their start and end apart: 17 -> 17, of which waited for: 16 -> 16; matrix products, arithmetic and copies ran while one was open for 8% -> 11% of each run, Pallas kernels for 0% -> 0%
where the time goes in v5:
time: 136 us
  waiting for transfers between devices  72.5 us (53%)
  starting transfers between devices  30.8 us (23%)
  other arithmetic  12.6 us (9%)
  matrix products  9.33 us (7%)
  local copies, waits for them, and re-layouts  5.71 us (4%)
  between operations  4.77 us (4%)
    ppermute x6, waiting for transfers between devices, halving_scatter(): blocks = keep + lax.ppermute(send, axis, pairs)  43 us
    ppermute x6, waiting for transfers between devices, doubling_gather(): other = lax.ppermute(current, axis, pairs)  23.7 us
    ppermute x6, starting transfers between devices, halving_scatter(): blocks = keep + lax.ppermute(send, axis, pairs)  11.6 us
    ppermute x5, starting transfers between devices, butterfly_sum(): value = value + lax.ppermute(value, axis, pairs)  10.5 us
    dot_general x2, matrix products, slot_term(): lax.dot_general(weighted, columns, (((0,), (0,)), ((), ())), preferred_el...  9.33 us
    ppermute x6, starting transfers between devices, doubling_gather(): other = lax.ppermute(current, axis, pairs)  8.66 us
    ppermute x5, waiting for transfers between devices, butterfly_sum(): value = value + lax.ppermute(value, axis, pairs)  5.86 us
    unnamed x3, local copies, waits for them, and re-layouts  3.72 us
  transfers between devices with their start and end apart: 17, of which 16 were waited for; matrix products, arithmetic and copies ran while one was open for 11% of the time, Pallas kernels for 0%

profile of v5, /device:TPU:0, one launch (start us, length us, event | category | flops | bytes accessed | tf_op | source)
XLA Modules:
  0.0 135.7 jit_solution(16413645083861490348)
XLA Ops:
  0.0 1.4 %convert_bitcast_fusion = (bf16[8]{0:T(256)(128)(2,1)S(1)}, s32[]{:T(128)}) fusion(s32[1,8]{1,0:T(1,128)} %param.8), kind=kLoop, calls=%fused_computation.58 | loop fusion | flops 15 | bytes 52 | tf_op jit(solution)/shard_map/convert_element_type | solution.py:16
  1.5 1.2 bitcast_multiply_fusion
  2.7 4.7 %fusion.14 = f32[128,4096]{1,0:T(8,128)S(1)} fusion(bf16[1024,4096]{1,0:T(8,128)(2,1)} %bitcast.71, bf16[1024,256]{1,0:T(8,128)(2,1)S(1)} %bitcast_multiply_fusion), kind=kOutput, calls=%fused_computation.40 | convolution fusion | flops 1073741824 | bytes 10747904 | tf_op jit(solution)/shard_map/dot_general | solution.py:22
  8.7 2.9 %collective-permute-start = (f32[128,2048]{1,0:T(8,128)}, f32[128,2048]{1,0:T(8,128)}, u32[]{:S(2)}, u32[]{:S(2)}) collective-permute-start(f32[128,2048]{1,0:T(8,128)} %fusion.1), channel_id=1, source_target_pairs={{0,2},{2,0},{4,6},{6,4},{8,10},{10,8},{12,14},{14,12},{1,3},{3,1},... | collective-permute-start | bytes 3145736 | tf_op jit(solution)/shard_map/ppermute | solution.py:61
  11.7 4.7 %fusion.12 = f32[128,4096]{1,0:T(8,128)S(1)} fusion(bf16[1024,4096]{1,0:T(8,128)(2,1)} %bitcast.72, bf16[1024,256]{1,0:T(8,128)(2,1)S(1)} %bitcast_multiply_fusion), kind=kOutput, calls=%fused_computation.38 | convolution fusion | flops 1073741824 | bytes 10747904 | tf_op jit(solution)/shard_map/dot_general | solution.py:22
  16.7 1.6 %collective-permute-start.3 = (f32[128,2048]{1,0:T(8,128)S(1)}, f32[128,2048]{1,0:T(8,128)S(1)}, u32[]{:S(2)}, u32[]{:S(2)}) collective-permute-start(f32[128,2048]{1,0:T(8,128)S(1)} %fusion), channel_id=1, source_target_pairs={{0,4},{2,6},{4,0},{6,2},{8,12},{10,14},{12,8},{14,10},{1,5},{3,7},... | collective-permute-start | bytes 3145736 | tf_op jit(solution)/shard_map/ppermute | solution.py:61
  18.3 16.8 %collective-permute-done = f32[128,2048]{1,0:T(8,128)} collective-permute-done((f32[128,2048]{1,0:T(8,128)}, f32[128,2048]{1,0:T(8,128)}, u32[]{:S(2)}, u32[]{:S(2)}) %collective-permute-start) | collective-permute-done | bytes 1048608 | tf_op jit(solution)/shard_map/ppermute | solution.py:61
  35.1 1.4 %select_add_fusion.1 = f32[128,2048]{1,0:T(8,128)S(1)} fusion(f32[128,2048]{1,0:T(8,128)} %collective-permute-done, f32[128,512]{1,0:T(8,128)S(1)} %get-tuple-element.6, f32[128,512]{1,0:T(8,128)S(1)} %get-tuple-element.7, f32[128,512]{1,0:T(8,128)S(1)} %get-tuple-element.8, f32[128,512]{1,0:T(8,128)S(1)} %get-tuple-element.9, ...), kind=kLoop, calls=%fused_computation.8 | loop fusion | flops 2097152 | bytes 4194305 | tf_op jit(solution)/shard_map/add | solution.py:61
  36.7 1.9 %collective-permute-start.1 = (f32[128,1024]{1,0:T(8,128)S(1)}, f32[128,1024]{1,0:T(8,128)S(1)}, u32[]{:S(2)}, u32[]{:S(2)}) collective-permute-start(f32[128,1024]{1,0:T(8,128)S(1)} %fusion.11), channel_id=1, source_target_pairs={{0,4},{2,6},{4,0},{6,2},{8,12},{10,14},{12,8},{14,10},{1,5},{3,7},... | collective-permute-start | bytes 1572872 | tf_op jit(solution)/shard_map/ppermute | solution.py:61
  38.6 4.3 %collective-permute-done.3 = f32[128,2048]{1,0:T(8,128)S(1)} collective-permute-done((f32[128,2048]{1,0:T(8,128)S(1)}, f32[128,2048]{1,0:T(8,128)S(1)}, u32[]{:S(2)}, u32[]{:S(2)}) %collective-permute-start.3) | collective-permute-done | bytes 1048608 | tf_op jit(solution)/shard_map/ppermute | solution.py:61
  44.0 8.6 %collective-permute-done.1 = f32[128,1024]{1,0:T(8,128)S(1)} collective-permute-done((f32[128,1024]{1,0:T(8,128)S(1)}, f32[128,1024]{1,0:T(8,128)S(1)}, u32[]{:S(2)}, u32[]{:S(2)}) %collective-permute-start.1) | collective-permute-done | bytes 524320 | tf_op jit(solution)/shard_map/ppermute | solution.py:61
  52.8 2.7 %collective-permute-start.2 = (f32[128,512]{1,0:T(8,128)S(1)}, f32[128,512]{1,0:T(8,128)S(1)}, u32[]{:S(2)}, u32[]{:S(2)}) collective-permute-start(f32[128,512]{1,0:T(8,128)S(1)} %slice_select_fusion.1), channel_id=1, source_target_pairs={{0,8},{2,10},{4,12},{6,14},{8,0},{10,2},{12,4},{14,6},{1,9},{3,11}... | collective-permute-start | bytes 786440 | tf_op jit(solution)/shard_map/ppermute | solution.py:61
  57.3 2.5 %collective-permute-start.5 = (f32[128,512]{1,0:T(8,128)}, f32[128,512]{1,0:T(8,128)S(1)}, u32[]{:S(2)}, u32[]{:S(2)}) collective-permute-start(f32[128,512]{1,0:T(8,128)} %slice_select_fusion), channel_id=1, source_target_pairs={{0,8},{2,10},{4,12},{6,14},{8,0},{10,2},{12,4},{14,6},{1,9},{3,11}... | collective-permute-start | bytes 786440 | tf_op jit(solution)/shard_map/ppermute | solution.py:61
  60.4 1.2 copy.10
  61.7 1.2 copy.11
  62.9 1.2 copy.12
  64.2 8.9 %collective-permute-done.2 = f32[128,512]{1,0:T(8,128)S(1)} collective-permute-done((f32[128,512]{1,0:T(8,128)S(1)}, f32[128,512]{1,0:T(8,128)S(1)}, u32[]{:S(2)}, u32[]{:S(2)}) %collective-permute-start.2) | collective-permute-done | bytes 262176 | tf_op jit(solution)/shard_map/ppermute | solution.py:61
  73.2 4.4 %collective-permute-done.5 = f32[128,512]{1,0:T(8,128)S(1)} collective-permute-done((f32[128,512]{1,0:T(8,128)}, f32[128,512]{1,0:T(8,128)S(1)}, u32[]{:S(2)}, u32[]{:S(2)}) %collective-permute-start.5) | collective-permute-done | bytes 262176 | tf_op jit(solution)/shard_map/ppermute | solution.py:61
  80.8 2.9 %collective-permute-start.7 = (f32[]{:T(128)}, f32[]{:T(128)}, u32[]{:S(2)}, u32[]{:S(2)}) collective-permute-start(f32[]{:T(128)} %add.54), channel_id=1, source_target_pairs={{0,1},{1,0},{2,3},{3,2},{4,5},{5,4},{6,7},{7,6},{8,9},{9,8},{10,11... | collective-permute-start | bytes 20 | tf_op jit(solution)/shard_map/ppermute | solution.py:36
  85.0 2.1 %collective-permute-start.8 = (f32[]{:T(128)}, f32[]{:T(128)}, u32[]{:S(2)}, u32[]{:S(2)}) collective-permute-start(f32[]{:T(128)} %add.55), channel_id=1, source_target_pairs={{0,2},{2,0},{4,6},{6,4},{8,10},{10,8},{12,14},{14,12},{1,3},{3,1},... | collective-permute-start | bytes 20 | tf_op jit(solution)/shard_map/ppermute | solution.py:36
  87.1 1.5 %collective-permute-done.8 = f32[]{:T(128)} collective-permute-done((f32[]{:T(128)}, f32[]{:T(128)}, u32[]{:S(2)}, u32[]{:S(2)}) %collective-permute-start.8) | collective-permute-done | bytes 36 | tf_op jit(solution)/shard_map/ppermute | solution.py:36
  89.2 2.1 %collective-permute-start.9 = (f32[]{:T(128)}, f32[]{:T(128)}, u32[]{:S(2)}, u32[]{:S(2)}) collective-permute-start(f32[]{:T(128)} %add.56), channel_id=1, source_target_pairs={{0,4},{2,6},{4,0},{6,2},{8,12},{10,14},{12,8},{14,10},{1,5},{3,7},... | collective-permute-start | bytes 20 | tf_op jit(solution)/shard_map/ppermute | solution.py:36
  91.4 1.4 %collective-permute-done.9 = f32[]{:T(128)} collective-permute-done((f32[]{:T(128)}, f32[]{:T(128)}, u32[]{:S(2)}, u32[]{:S(2)}) %collective-permute-start.9) | collective-permute-done | bytes 36 | tf_op jit(solution)/shard_map/ppermute | solution.py:36
  93.4 3.4 %collective-permute-start.10 = (f32[]{:T(128)}, f32[]{:T(128)}, u32[]{:S(2)}, u32[]{:S(2)}) collective-permute-start(f32[]{:T(128)} %add.57), channel_id=1, source_target_pairs={{0,8},{2,10},{4,12},{6,14},{8,0},{10,2},{12,4},{14,6},{1,9},{3,11}... | collective-permute-start | bytes 20 | tf_op jit(solution)/shard_map/ppermute | solution.py:36
  99.0 2.1 %collective-permute-start.11 = (bf16[512,128]{0,1:T(8,128)(2,1)S(1)}, bf16[512,128]{0,1:T(8,128)(2,1)S(1)}, u32[]{:S(2)}, u32[]{:S(2)}) collective-permute-start(bf16[512,128]{0,1:T(8,128)(2,1)S(1)} %slice.146), channel_id=1, source_target_pairs={{0,8},{2,10},{4,12},{6,14},{8,0},{10,2},{12,4},{14,6},{1,9},{3,11}... | collective-permute-start | bytes 393224 | tf_op jit(solution)/shard_map/ppermute | solution.py:75
  101.1 7.4 %collective-permute-done.11 = bf16[512,128]{0,1:T(8,128)(2,1)S(1)} collective-permute-done((bf16[512,128]{0,1:T(8,128)(2,1)S(1)}, bf16[512,128]{0,1:T(8,128)(2,1)S(1)}, u32[]{:S(2)}, u32[]{:S(2)}) %collective-permute-start.11) | collective-permute-done | bytes 131104 | tf_op jit(solution)/shard_map/ppermute | solution.py:75
  108.7 4.2 %collective-permute-start.12 = (bf16[2,512,128]{1,2,0:T(8,128)(2,1)S(1)}, bf16[2,512,128]{1,2,0:T(8,128)(2,1)S(1)}, u32[]{:S(2)}, u32[]{:S(2)}) collective-permute-start(bf16[2,512,128]{1,2,0:T(8,128)(2,1)S(1)} %pad_maximum_fusion.10), channel_id=1, source_target_pairs={{0,4},{2,6},{4,0},{6,2},{8,12},{10,14},{12,8},{14,10},{1,5},{3,7},... | collective-permute-start | bytes 786440 | tf_op jit(solution)/shard_map/ppermute | solution.py:75
  112.9 3.1 %collective-permute-done.14 = bf16[512,128]{0,1:T(8,128)(2,1)S(1)} collective-permute-done((bf16[512,128]{0,1:T(8,128)(2,1)S(1)}, bf16[512,128]{0,1:T(8,128)(2,1)S(1)}, u32[]{:S(2)}, u32[]{:S(2)}) %collective-permute-start.14) | collective-permute-done | bytes 131104 | tf_op jit(solution)/shard_map/ppermute | solution.py:75
  118.9 4.2 %collective-permute-done.15 = bf16[2,512,128]{1,2,0:T(8,128)(2,1)S(1)} collective-permute-done((bf16[2,512,128]{1,2,0:T(8,128)(2,1)S(1)}, bf16[2,512,128]{1,2,0:T(8,128)(2,1)S(1)}, u32[]{:S(2)}, u32[]{:S(2)}) %collective-permute-start.15) | collective-permute-done | bytes 262176 | tf_op jit(solution)/shard_map/ppermute | solution.py:75
  124.4 4.3 %collective-permute-done.13 = bf16[2,2,512,128]{2,3,1,0:T(8,128)(2,1)S(1)} collective-permute-done((bf16[2,2,512,128]{2,3,1,0:T(8,128)(2,1)S(1)}, bf16[2,2,512,128]{2,3,1,0:T(8,128)(2,1)S(1)}, u32[]{:S(2)}, u32[]{:S(2)}) %collective-permute-start.13) | collective-permute-done | bytes 524320 | tf_op jit(solution)/shard_map/ppermute | solution.py:75
  129.5 3.8 %collective-permute-done.16 = bf16[2,2,512,128]{2,3,1,0:T(8,128)(2,1)S(1)} collective-permute-done((bf16[2,2,512,128]{2,3,1,0:T(8,128)(2,1)}, bf16[2,2,512,128]{2,3,1,0:T(8,128)(2,1)S(1)}, u32[]{:S(2)}, u32[]{:S(2)}) %collective-permute-start.16) | collective-permute-done | bytes 524320 | tf_op jit(solution)/shard_map/ppermute | solution.py:75
  134.2 1.5 %maximum_bitcast_fusion = bf16[1,4096,256]{2,1,0:T(8,128)(2,1)} fusion(bf16[4096,128]{1,0:T(8,128)(2,1)S(1)} %bitcast.74, bf16[4096,128]{1,0:T(8,128)(2,1)S(1)} %bitcast.73), kind=kLoop, calls=%fused_computation | loop fusion | flops 4194304 | bytes 4194304 | tf_op jit(solution)/shard_map/broadcast_in_dim | solution.py:137
  (44 shorter events, 15.2 us)
Async XLA Ops:
  8.7 26.4 %collective-permute-start = (f32[128,2048]{1,0:T(8,128)}, f32[128,2048]{1,0:T(8,128)}, u32[]{:S(2)}, u32[]{:S(2)}) collective-permute-start(f32[128,2048]{1,0:T(8,128)} %fusion.1), channel_id=1, source_target_pairs={{0,2},{2,0},{4,6},{6,4},{8,10},{10,8},{12,14},{14,12},{1,3},{3,1},... | collective-permute-start | bytes 3145736 | tf_op jit(solution)/shard_map/ppermute | solution.py:61
  16.7 26.1 %collective-permute-start.3 = (f32[128,2048]{1,0:T(8,128)S(1)}, f32[128,2048]{1,0:T(8,128)S(1)}, u32[]{:S(2)}, u32[]{:S(2)}) collective-permute-start(f32[128,2048]{1,0:T(8,128)S(1)} %fusion), channel_id=1, source_target_pairs={{0,4},{2,6},{4,0},{6,2},{8,12},{10,14},{12,8},{14,10},{1,5},{3,7},... | collective-permute-start | bytes 3145736 | tf_op jit(solution)/shard_map/ppermute | solution.py:61
  36.7 16.0 %collective-permute-start.1 = (f32[128,1024]{1,0:T(8,128)S(1)}, f32[128,1024]{1,0:T(8,128)S(1)}, u32[]{:S(2)}, u32[]{:S(2)}) collective-permute-start(f32[128,1024]{1,0:T(8,128)S(1)} %fusion.11), channel_id=1, source_target_pairs={{0,4},{2,6},{4,0},{6,2},{8,12},{10,14},{12,8},{14,10},{1,5},{3,7},... | collective-permute-start | bytes 1572872 | tf_op jit(solution)/shard_map/ppermute | solution.py:61
  44.0 11.4 %collective-permute-start.4 = (f32[128,1024]{1,0:T(8,128)}, f32[128,1024]{1,0:T(8,128)}, u32[]{:S(2)}, u32[]{:S(2)}) collective-permute-start(f32[128,1024]{1,0:T(8,128)} %fusion.10), channel_id=1, source_target_pairs={{0,2},{2,0},{4,6},{6,4},{8,10},{10,8},{12,14},{14,12},{1,3},{3,1},... | collective-permute-start | bytes 1572872 | tf_op jit(solution)/shard_map/ppermute | solution.py:61
  52.8 20.3 %collective-permute-start.2 = (f32[128,512]{1,0:T(8,128)S(1)}, f32[128,512]{1,0:T(8,128)S(1)}, u32[]{:S(2)}, u32[]{:S(2)}) collective-permute-start(f32[128,512]{1,0:T(8,128)S(1)} %slice_select_fusion.1), channel_id=1, source_target_pairs={{0,8},{2,10},{4,12},{6,14},{8,0},{10,2},{12,4},{14,6},{1,9},{3,11}... | collective-permute-start | bytes 786440 | tf_op jit(solution)/shard_map/ppermute | solution.py:61
  57.3 20.2 %collective-permute-start.5 = (f32[128,512]{1,0:T(8,128)}, f32[128,512]{1,0:T(8,128)S(1)}, u32[]{:S(2)}, u32[]{:S(2)}) collective-permute-start(f32[128,512]{1,0:T(8,128)} %slice_select_fusion), channel_id=1, source_target_pairs={{0,8},{2,10},{4,12},{6,14},{8,0},{10,2},{12,4},{14,6},{1,9},{3,11}... | collective-permute-start | bytes 786440 | tf_op jit(solution)/shard_map/ppermute | solution.py:61
  78.3 1.2 collective-permute-start.6
  80.8 3.6 %collective-permute-start.7 = (f32[]{:T(128)}, f32[]{:T(128)}, u32[]{:S(2)}, u32[]{:S(2)}) collective-permute-start(f32[]{:T(128)} %add.54), channel_id=1, source_target_pairs={{0,1},{1,0},{2,3},{3,2},{4,5},{5,4},{6,7},{7,6},{8,9},{9,8},{10,11... | collective-permute-start | bytes 20 | tf_op jit(solution)/shard_map/ppermute | solution.py:36
  85.0 3.6 %collective-permute-start.8 = (f32[]{:T(128)}, f32[]{:T(128)}, u32[]{:S(2)}, u32[]{:S(2)}) collective-permute-start(f32[]{:T(128)} %add.55), channel_id=1, source_target_pairs={{0,2},{2,0},{4,6},{6,4},{8,10},{10,8},{12,14},{14,12},{1,3},{3,1},... | collective-permute-start | bytes 20 | tf_op jit(solution)/shard_map/ppermute | solution.py:36
  89.2 3.6 %collective-permute-start.9 = (f32[]{:T(128)}, f32[]{:T(128)}, u32[]{:S(2)}, u32[]{:S(2)}) collective-permute-start(f32[]{:T(128)} %add.56), channel_id=1, source_target_pairs={{0,4},{2,6},{4,0},{6,2},{8,12},{10,14},{12,8},{14,10},{1,5},{3,7},... | collective-permute-start | bytes 20 | tf_op jit(solution)/shard_map/ppermute | solution.py:36
  93.4 4.5 %collective-permute-start.10 = (f32[]{:T(128)}, f32[]{:T(128)}, u32[]{:S(2)}, u32[]{:S(2)}) collective-permute-start(f32[]{:T(128)} %add.57), channel_id=1, source_target_pairs={{0,8},{2,10},{4,12},{6,14},{8,0},{10,2},{12,4},{14,6},{1,9},{3,11}... | collective-permute-start | bytes 20 | tf_op jit(solution)/shard_map/ppermute | solution.py:36
  99.0 9.5 %collective-permute-start.11 = (bf16[512,128]{0,1:T(8,128)(2,1)S(1)}, bf16[512,128]{0,1:T(8,128)(2,1)S(1)}, u32[]{:S(2)}, u32[]{:S(2)}) collective-permute-start(bf16[512,128]{0,1:T(8,128)(2,1)S(1)} %slice.146), channel_id=1, source_target_pairs={{0,8},{2,10},{4,12},{6,14},{8,0},{10,2},{12,4},{14,6},{1,9},{3,11}... | collective-permute-start | bytes 393224 | tf_op jit(solution)/shard_map/ppermute | solution.py:75
  108.5 7.4 %collective-permute-start.14 = (bf16[512,128]{0,1:T(8,128)(2,1)S(1)}, bf16[512,128]{0,1:T(8,128)(2,1)S(1)}, u32[]{:S(2)}, u32[]{:S(2)}) collective-permute-start(bf16[512,128]{0,1:T(8,128)(2,1)S(1)} %get-tuple-element.37), channel_id=1, source_target_pairs={{0,8},{2,10},{4,12},{6,14},{8,0},{10,2},{12,4},{14,6},{1,9},{3,11}... | collective-permute-start | bytes 393224 | tf_op jit(solution)/shard_map/ppermute | solution.py:75
  108.7 9.2 %collective-permute-start.12 = (bf16[2,512,128]{1,2,0:T(8,128)(2,1)S(1)}, bf16[2,512,128]{1,2,0:T(8,128)(2,1)S(1)}, u32[]{:S(2)}, u32[]{:S(2)}) collective-permute-start(bf16[2,512,128]{1,2,0:T(8,128)(2,1)S(1)} %pad_maximum_fusion.10), channel_id=1, source_target_pairs={{0,4},{2,6},{4,0},{6,2},{8,12},{10,14},{12,8},{14,10},{1,5},{3,7},... | collective-permute-start | bytes 786440 | tf_op jit(solution)/shard_map/ppermute | solution.py:75
  116.1 7.0 %collective-permute-start.15 = (bf16[2,512,128]{1,2,0:T(8,128)(2,1)S(1)}, bf16[2,512,128]{1,2,0:T(8,128)(2,1)S(1)}, u32[]{:S(2)}, u32[]{:S(2)}) collective-permute-start(bf16[2,512,128]{1,2,0:T(8,128)(2,1)S(1)} %pad_maximum_fusion.11), channel_id=1, source_target_pairs={{0,2},{2,0},{4,6},{6,4},{8,10},{10,8},{12,14},{14,12},{1,3},{3,1},... | collective-permute-start | bytes 786440 | tf_op jit(solution)/shard_map/ppermute | solution.py:75
  117.9 10.7 %collective-permute-start.13 = (bf16[2,2,512,128]{2,3,1,0:T(8,128)(2,1)S(1)}, bf16[2,2,512,128]{2,3,1,0:T(8,128)(2,1)S(1)}, u32[]{:S(2)}, u32[]{:S(2)}) collective-permute-start(bf16[2,2,512,128]{2,3,1,0:T(8,128)(2,1)S(1)} %pad_maximum_fusion.8), channel_id=1, source_target_pairs={{0,2},{2,0},{4,6},{6,4},{8,10},{10,8},{12,14},{14,12},{1,3},{3,1},... | collective-permute-start | bytes 1572872 | tf_op jit(solution)/shard_map/ppermute | solution.py:75
  123.9 9.4 %collective-permute-start.16 = (bf16[2,2,512,128]{2,3,1,0:T(8,128)(2,1)}, bf16[2,2,512,128]{2,3,1,0:T(8,128)(2,1)S(1)}, u32[]{:S(2)}, u32[]{:S(2)}) collective-permute-start(bf16[2,2,512,128]{2,3,1,0:T(8,128)(2,1)} %pad_maximum_fusion.9), channel_id=1, source_target_pairs={{0,4},{2,6},{4,0},{6,2},{8,12},{10,14},{12,8},{14,10},{1,5},{3,7},... | collective-permute-start | bytes 1572872 | tf_op jit(solution)/shard_map/ppermute | solution.py:75

commit v6 on v4

--- a/solution.py
+++ b/solution.py
@@ -79,17 +79,17 @@
     return current.reshape((-1,) + part.shape[1:])
 
 
-def scatter_rows(partial_t, axis):
+def scatter_rows(partial_t, axis, parts=4):
     size = lax.axis_size(axis)
     cols = partial_t.shape[0]
-    if size & (size - 1) or size == 1 or cols % 2:
+    if size & (size - 1) or size == 1 or cols % (8 * parts):
         return lax.psum_scatter(partial_t, axis, scatter_dimension=1, tiled=True)
-    first, second = bit_orders(size)
-    half = cols // 2
+    orders = bit_orders(size)
+    width = cols // parts
     return jnp.concatenate(
         [
-            halving_scatter(partial_t[:half], axis, first),
-            halving_scatter(partial_t[half:], axis, second),
+            halving_scatter(partial_t[k * width:(k + 1) * width], axis, orders[k % 2])
+            for k in range(parts)
         ],
         axis=0,
     )

time: 136 us -> 131 us (0.963)
  waiting for transfers between devices: 77.6 us -> 64.5 us
  other arithmetic: 10 us -> 14.5 us
  starting transfers between devices: 27.6 us -> 30.7 us
    ppermute x6 -> x12, waiting for transfers between devices: 45 us -> 29.9 us  [halving_scatter(): blocks = keep + lax.ppermute(send, axis, pairs)]
    ppermute x6 -> x12, starting transfers between devices: 11.6 us -> 16.7 us  [halving_scatter(): blocks = keep + lax.ppermute(send, axis, pairs)]
    add x6 -> x12, other arithmetic: 1.64 us -> 5.12 us  [halving_scatter(): blocks = keep + lax.ppermute(send, axis, pairs)]
    select_n x6 -> x12, other arithmetic: 2.9 us -> 3.86 us  [halving_scatter(): send = jnp.where(mine == 1, low_part, high_part)]
    unnamed x5 -> x43, local copies, waits for them, and re-layouts: 5.64 us -> 6.54 us
  transfers between devices with their start and end apart: 17 -> 23, of which waited for: 16 -> 20; matrix products, arithmetic and copies ran while one was open for 8% -> 12% of each run, Pallas kernels for 0% -> 0%
where the time goes in v6:
time: 131 us
  waiting for transfers between devices  64.5 us (49%)
  starting transfers between devices  30.7 us (23%)
  other arithmetic  14.5 us (11%)
  local copies, waits for them, and re-layouts  9.88 us (8%)
  matrix products  6.18 us (5%)
  between operations  4.97 us (4%)
    ppermute x12, waiting for transfers between devices, halving_scatter(): blocks = keep + lax.ppermute(send, axis, pairs)  29.9 us
    ppermute x6, waiting for transfers between devices, doubling_gather(): other = lax.ppermute(current, axis, pairs)  26.7 us
    ppermute x12, starting transfers between devices, halving_scatter(): blocks = keep + lax.ppermute(send, axis, pairs)  16.7 us
    ppermute x5, starting transfers between devices, butterfly_sum(): value = value + lax.ppermute(value, axis, pairs)  8.59 us
    ppermute x5, waiting for transfers between devices, butterfly_sum(): value = value + lax.ppermute(value, axis, pairs)  7.85 us
    unnamed x43, local copies, waits for them, and re-layouts  6.54 us
    dot_general x1, matrix products, slot_term(): lax.dot_general(weighted, columns, (((0,), (0,)), ((), ())), preferred_el...  6.18 us
    ppermute x6, starting transfers between devices, doubling_gather(): other = lax.ppermute(current, axis, pairs)  5.38 us
  transfers between devices with their start and end apart: 23, of which 20 were waited for; matrix products, arithmetic and copies ran while one was open for 12% of the time, Pallas kernels for 0%

profile of v6, /device:TPU:0, one launch (start us, length us, event | category | flops | bytes accessed | tf_op | source)
XLA Modules:
  0.0 130.7 jit_solution(7952274294555620504)
XLA Ops:
  1.4 6.2 %fusion.2 = f32[256,4096]{1,0:T(8,128)S(1)} fusion(bf16[1,8,128,4096]{3,2,1,0:T(8,128)(2,1)} %param.6, bf16[1,8,128,256]{3,2,1,0:T(8,128)(2,1)} %param.7, bf16[8]{0:T(256)(128)(2,1)S(1)} %get-tuple-element.58), kind=kOutput, calls=%fused_computation.2 | convolution fusion | flops 2147745792 | bytes 13107216 | tf_op jit(solution)/shard_map/dot_general | solution.py:19
  7.6 1.9 %copy-done = f32[256,4096]{1,0:T(8,128)} copy-done((f32[256,4096]{1,0:T(8,128)}, f32[256,4096]{1,0:T(8,128)S(1)}, u32[]{:S(2)}) %copy-start) | copy-done | bytes 4194328
  10.9 2.9 %collective-permute-start = (f32[64,2048]{1,0:T(8,128)}, f32[64,2048]{1,0:T(8,128)}, u32[]{:S(2)}, u32[]{:S(2)}) collective-permute-start(f32[64,2048]{1,0:T(8,128)} %fusion.18), channel_id=1, source_target_pairs={{0,2},{2,0},{4,6},{6,4},{8,10},{10,8},{12,14},{14,12},{1,3},{3,1},... | collective-permute-start | bytes 1572872 | tf_op jit(solution)/shard_map/ppermute | solution.py:58
  13.9 1.6 %fusion.26 = (f32[64,1024]{1,0:T(8,128)S(1)}, f32[64,1024]{1,0:T(8,128)S(1)}, f32[64,1024]{1,0:T(8,128)S(1)}, f32[64,1024]{1,0:T(8,128)S(1)}, f32[64,1024]{1,0:T...) fusion(f32[256,4096]{1,0:T(8,128)} %copy-done), kind=kLoop, calls=%fused_computation.80 | loop fusion | bytes 4194304 | tf_op jit(solution)/shard_map/slice | solution.py:54
  16.4 1.6 %collective-permute-start.3 = (f32[64,2048]{1,0:T(8,128)}, f32[64,2048]{1,0:T(8,128)}, u32[]{:S(2)}, u32[]{:S(2)}) collective-permute-start(f32[64,2048]{1,0:T(8,128)} %fusion.16), channel_id=1, source_target_pairs={{0,4},{2,6},{4,0},{6,2},{8,12},{10,14},{12,8},{14,10},{1,5},{3,7},... | collective-permute-start | bytes 1572872 | tf_op jit(solution)/shard_map/ppermute | solution.py:58
  23.5 2.0 %copy.14 = f32[1,512,256]{1,2,0:T(8,128)} copy(f32[1,512,256]{2,1,0:T(8,128)} %param.9) | data formatting | bytes 1048576 | tf_op args[3]
  25.6 1.4 %collective-permute-done = f32[64,2048]{1,0:T(8,128)} collective-permute-done((f32[64,2048]{1,0:T(8,128)}, f32[64,2048]{1,0:T(8,128)}, u32[]{:S(2)}, u32[]{:S(2)}) %collective-permute-start) | collective-permute-done | bytes 524320 | tf_op jit(solution)/shard_map/ppermute | solution.py:58
  26.9 1.4 %select_add_fusion.3 = f32[64,2048]{1,0:T(8,128)S(1)} fusion(f32[64,2048]{1,0:T(8,128)} %collective-permute-done, f32[64,512]{1,0:T(8,128)} %copy-done.13, f32[64,512]{1,0:T(8,128)} %copy-done.14, f32[64,512]{1,0:T(8,128)} %copy-done.15, f32[64,512]{1,0:T(8,128)} %copy-done.16, f32[64,512]{1,0:T(8,128)} %copy-done.17, f32[64,512]{1,0:T(8,128)} %copy-done.18, ...), kind=kLoop, calls=%fused_computation.35 | loop fusion | flops 1048576 | bytes 2097153 | tf_op jit(solution)/shard_map/add | solution.py:58
  28.4 2.2 %collective-permute-start.1 = (f32[64,1024]{1,0:T(8,128)S(1)}, f32[64,1024]{1,0:T(8,128)S(1)}, u32[]{:S(2)}, u32[]{:S(2)}) collective-permute-start(f32[64,1024]{1,0:T(8,128)S(1)} %fusion.24), channel_id=1, source_target_pairs={{0,4},{2,6},{4,0},{6,2},{8,12},{10,14},{12,8},{14,10},{1,5},{3,7},... | collective-permute-start | bytes 786440 | tf_op jit(solution)/shard_map/ppermute | solution.py:58
  33.4 4.7 %collective-permute-done.6 = f32[64,2048]{1,0:T(8,128)} collective-permute-done((f32[64,2048]{1,0:T(8,128)}, f32[64,2048]{1,0:T(8,128)}, u32[]{:S(2)}, u32[]{:S(2)}) %collective-permute-start.6) | collective-permute-done | bytes 524320 | tf_op jit(solution)/shard_map/ppermute | solution.py:58
  39.4 2.2 %collective-permute-start.7 = (f32[64,1024]{1,0:T(8,128)S(1)}, f32[64,1024]{1,0:T(8,128)S(1)}, u32[]{:S(2)}, u32[]{:S(2)}) collective-permute-start(f32[64,1024]{1,0:T(8,128)S(1)} %fusion.22), channel_id=1, source_target_pairs={{0,4},{2,6},{4,0},{6,2},{8,12},{10,14},{12,8},{14,10},{1,5},{3,7},... | collective-permute-start | bytes 786440 | tf_op jit(solution)/shard_map/ppermute | solution.py:58
  44.4 3.9 %collective-permute-done.1 = f32[64,1024]{1,0:T(8,128)S(1)} collective-permute-done((f32[64,1024]{1,0:T(8,128)S(1)}, f32[64,1024]{1,0:T(8,128)S(1)}, u32[]{:S(2)}, u32[]{:S(2)}) %collective-permute-start.1) | collective-permute-done | bytes 262176 | tf_op jit(solution)/shard_map/ppermute | solution.py:58
  48.4 2.7 %collective-permute-start.2 = (f32[64,512]{1,0:T(8,128)S(1)}, f32[64,512]{1,0:T(8,128)S(1)}, u32[]{:S(2)}, u32[]{:S(2)}) collective-permute-start(f32[64,512]{1,0:T(8,128)S(1)} %slice_select_fusion.3), channel_id=1, source_target_pairs={{0,8},{2,10},{4,12},{6,14},{8,0},{10,2},{12,4},{14,6},{1,9},{3,11}... | collective-permute-start | bytes 393224 | tf_op jit(solution)/shard_map/ppermute | solution.py:58
  51.5 5.3 %collective-permute-done.7 = f32[64,1024]{1,0:T(8,128)S(1)} collective-permute-done((f32[64,1024]{1,0:T(8,128)S(1)}, f32[64,1024]{1,0:T(8,128)S(1)}, u32[]{:S(2)}, u32[]{:S(2)}) %collective-permute-start.7) | collective-permute-done | bytes 262176 | tf_op jit(solution)/shard_map/ppermute | solution.py:58
  57.5 2.5 %collective-permute-start.11 = (f32[64,512]{1,0:T(8,128)S(1)}, f32[64,512]{1,0:T(8,128)S(1)}, u32[]{:S(2)}, u32[]{:S(2)}) collective-permute-start(f32[64,512]{1,0:T(8,128)S(1)} %slice_select_fusion), channel_id=1, source_target_pairs={{0,8},{2,10},{4,12},{6,14},{8,0},{10,2},{12,4},{14,6},{1,9},{3,11}... | collective-permute-start | bytes 393224 | tf_op jit(solution)/shard_map/ppermute | solution.py:58
  60.1 8.2 %collective-permute-done.5 = f32[64,512]{1,0:T(8,128)S(1)} collective-permute-done((f32[64,512]{1,0:T(8,128)S(1)}, f32[64,512]{1,0:T(8,128)S(1)}, u32[]{:S(2)}, u32[]{:S(2)}) %collective-permute-start.5) | collective-permute-done | bytes 131104 | tf_op jit(solution)/shard_map/ppermute | solution.py:58
  68.3 2.8 %collective-permute-done.8 = f32[64,512]{1,0:T(8,128)S(1)} collective-permute-done((f32[64,512]{1,0:T(8,128)S(1)}, f32[64,512]{1,0:T(8,128)S(1)}, u32[]{:S(2)}, u32[]{:S(2)}) %collective-permute-start.8) | collective-permute-done | bytes 131104 | tf_op jit(solution)/shard_map/ppermute | solution.py:58
  71.1 1.6 %collective-permute-done.11 = f32[64,512]{1,0:T(8,128)S(1)} collective-permute-done((f32[64,512]{1,0:T(8,128)S(1)}, f32[64,512]{1,0:T(8,128)S(1)}, u32[]{:S(2)}, u32[]{:S(2)}) %collective-permute-start.11) | collective-permute-done | bytes 131104 | tf_op jit(solution)/shard_map/ppermute | solution.py:58
  76.1 2.9 %collective-permute-start.13 = (f32[]{:T(128)}, f32[]{:T(128)}, u32[]{:S(2)}, u32[]{:S(2)}) collective-permute-start(f32[]{:T(128)} %add.78), channel_id=1, source_target_pairs={{0,1},{1,0},{2,3},{3,2},{4,5},{5,4},{6,7},{7,6},{8,9},{9,8},{10,11... | collective-permute-start | bytes 20 | tf_op jit(solution)/shard_map/ppermute | solution.py:33
  80.3 1.9 %collective-permute-start.14 = (f32[]{:T(128)}, f32[]{:T(128)}, u32[]{:S(2)}, u32[]{:S(2)}) collective-permute-start(f32[]{:T(128)} %add.79), channel_id=1, source_target_pairs={{0,2},{2,0},{4,6},{6,4},{8,10},{10,8},{12,14},{14,12},{1,3},{3,1},... | collective-permute-start | bytes 20 | tf_op jit(solution)/shard_map/ppermute | solution.py:33
  82.2 1.7 %collective-permute-done.14 = f32[]{:T(128)} collective-permute-done((f32[]{:T(128)}, f32[]{:T(128)}, u32[]{:S(2)}, u32[]{:S(2)}) %collective-permute-start.14) | collective-permute-done | bytes 36 | tf_op jit(solution)/shard_map/ppermute | solution.py:33
  84.5 1.4 %collective-permute-start.15 = (f32[]{:T(128)}, f32[]{:T(128)}, u32[]{:S(2)}, u32[]{:S(2)}) collective-permute-start(f32[]{:T(128)} %add.80), channel_id=1, source_target_pairs={{0,4},{2,6},{4,0},{6,2},{8,12},{10,14},{12,8},{14,10},{1,5},{3,7},... | collective-permute-start | bytes 20 | tf_op jit(solution)/shard_map/ppermute | solution.py:33
  85.8 2.2 %collective-permute-done.15 = f32[]{:T(128)} collective-permute-done((f32[]{:T(128)}, f32[]{:T(128)}, u32[]{:S(2)}, u32[]{:S(2)}) %collective-permute-start.15) | collective-permute-done | bytes 36 | tf_op jit(solution)/shard_map/ppermute | solution.py:33
  88.6 2.4 %collective-permute-start.16 = (f32[]{:T(128)}, f32[]{:T(128)}, u32[]{:S(2)}, u32[]{:S(2)}) collective-permute-start(f32[]{:T(128)} %add.81), channel_id=1, source_target_pairs={{0,8},{2,10},{4,12},{6,14},{8,0},{10,2},{12,4},{14,6},{1,9},{3,11}... | collective-permute-start | bytes 20 | tf_op jit(solution)/shard_map/ppermute | solution.py:33
  91.1 2.0 %collective-permute-done.16 = f32[]{:T(128)} collective-permute-done((f32[]{:T(128)}, f32[]{:T(128)}, u32[]{:S(2)}, u32[]{:S(2)}) %collective-permute-start.16) | collective-permute-done | bytes 36 | tf_op jit(solution)/shard_map/ppermute | solution.py:33
  95.4 8.6 %collective-permute-done.17 = bf16[512,128]{0,1:T(8,128)(2,1)S(1)} collective-permute-done((bf16[512,128]{0,1:T(8,128)(2,1)S(1)}, bf16[512,128]{0,1:T(8,128)(2,1)S(1)}, u32[]{:S(2)}, u32[]{:S(2)}) %collective-permute-start.17) | collective-permute-done | bytes 131104 | tf_op jit(solution)/shard_map/ppermute | solution.py:72
  104.1 3.0 %collective-permute-start.18 = (bf16[2,512,128]{1,2,0:T(8,128)(2,1)S(1)}, bf16[2,512,128]{1,2,0:T(8,128)(2,1)S(1)}, u32[]{:S(2)}, u32[]{:S(2)}) collective-permute-start(bf16[2,512,128]{1,2,0:T(8,128)(2,1)S(1)} %pad_maximum_fusion.18), channel_id=1, source_target_pairs={{0,4},{2,6},{4,0},{6,2},{8,12},{10,14},{12,8},{14,10},{1,5},{3,7},... | collective-permute-start | bytes 786440 | tf_op jit(solution)/shard_map/ppermute | solution.py:72
  107.1 3.8 %collective-permute-done.20 = bf16[512,128]{0,1:T(8,128)(2,1)S(1)} collective-permute-done((bf16[512,128]{0,1:T(8,128)(2,1)S(1)}, bf16[512,128]{0,1:T(8,128)(2,1)S(1)}, u32[]{:S(2)}, u32[]{:S(2)}) %collective-permute-start.20) | collective-permute-done | bytes 131104 | tf_op jit(solution)/shard_map/ppermute | solution.py:72
  113.6 4.5 %collective-permute-done.21 = bf16[2,512,128]{1,2,0:T(8,128)(2,1)S(1)} collective-permute-done((bf16[2,512,128]{1,2,0:T(8,128)(2,1)S(1)}, bf16[2,512,128]{1,2,0:T(8,128)(2,1)S(1)}, u32[]{:S(2)}, u32[]{:S(2)}) %collective-permute-start.21) | collective-permute-done | bytes 262176 | tf_op jit(solution)/shard_map/ppermute | solution.py:72
  118.9 4.7 %collective-permute-done.19 = bf16[2,2,512,128]{2,3,1,0:T(8,128)(2,1)S(1)} collective-permute-done((bf16[2,2,512,128]{2,3,1,0:T(8,128)(2,1)S(1)}, bf16[2,2,512,128]{2,3,1,0:T(8,128)(2,1)S(1)}, u32[]{:S(2)}, u32[]{:S(2)}) %collective-permute-start.19) | collective-permute-done | bytes 524320 | tf_op jit(solution)/shard_map/ppermute | solution.py:72
  124.5 3.8 %collective-permute-done.22 = bf16[2,2,512,128]{2,3,1,0:T(8,128)(2,1)S(1)} collective-permute-done((bf16[2,2,512,128]{2,3,1,0:T(8,128)(2,1)}, bf16[2,2,512,128]{2,3,1,0:T(8,128)(2,1)S(1)}, u32[]{:S(2)}, u32[]{:S(2)}) %collective-permute-start.22) | collective-permute-done | bytes 524320 | tf_op jit(solution)/shard_map/ppermute | solution.py:72
  129.1 1.5 %maximum_bitcast_fusion = bf16[1,4096,256]{2,1,0:T(8,128)(2,1)} fusion(bf16[4096,128]{1,0:T(8,128)(2,1)S(1)} %bitcast.75, bf16[4096,128]{1,0:T(8,128)(2,1)S(1)} %bitcast.74), kind=kLoop, calls=%fused_computation.3 | loop fusion | flops 4194304 | bytes 4194304 | tf_op jit(solution)/shard_map/broadcast_in_dim | solution.py:132
  (107 shorter events, 26.2 us)
Async XLA Ops:
  9.8 11.2 %copy-start.12 = (f32[64,512]{1,0:T(8,128)}, f32[64,512]{1,0:T(8,128)S(1)}, u32[]{:S(2)}) copy-start(f32[64,512]{1,0:T(8,128)S(1)} %get-tuple-element.5) | copy-start | bytes 393220
  9.8 11.2 %copy-start.13 = (f32[64,512]{1,0:T(8,128)}, f32[64,512]{1,0:T(8,128)S(1)}, u32[]{:S(2)}) copy-start(f32[64,512]{1,0:T(8,128)S(1)} %get-tuple-element.14) | copy-start | bytes 393220
  9.8 11.2 %copy-start.14 = (f32[64,512]{1,0:T(8,128)}, f32[64,512]{1,0:T(8,128)S(1)}, u32[]{:S(2)}) copy-start(f32[64,512]{1,0:T(8,128)S(1)} %get-tuple-element.15) | copy-start | bytes 393220
  10.9 16.0 %collective-permute-start = (f32[64,2048]{1,0:T(8,128)}, f32[64,2048]{1,0:T(8,128)}, u32[]{:S(2)}, u32[]{:S(2)}) collective-permute-start(f32[64,2048]{1,0:T(8,128)} %fusion.18), channel_id=1, source_target_pairs={{0,2},{2,0},{4,6},{6,4},{8,10},{10,8},{12,14},{14,12},{1,3},{3,1},... | collective-permute-start | bytes 1572872 | tf_op jit(solution)/shard_map/ppermute | solution.py:58
  16.4 15.2 %collective-permute-start.3 = (f32[64,2048]{1,0:T(8,128)}, f32[64,2048]{1,0:T(8,128)}, u32[]{:S(2)}, u32[]{:S(2)}) collective-permute-start(f32[64,2048]{1,0:T(8,128)} %fusion.16), channel_id=1, source_target_pairs={{0,4},{2,6},{4,0},{6,2},{8,12},{10,14},{12,8},{14,10},{1,5},{3,7},... | collective-permute-start | bytes 1572872 | tf_op jit(solution)/shard_map/ppermute | solution.py:58
  18.9 19.3 %collective-permute-start.6 = (f32[64,2048]{1,0:T(8,128)}, f32[64,2048]{1,0:T(8,128)}, u32[]{:S(2)}, u32[]{:S(2)}) collective-permute-start(f32[64,2048]{1,0:T(8,128)} %fusion.17), channel_id=1, source_target_pairs={{0,2},{2,0},{4,6},{6,4},{8,10},{10,8},{12,14},{14,12},{1,3},{3,1},... | collective-permute-start | bytes 1572872 | tf_op jit(solution)/shard_map/ppermute | solution.py:58
  20.3 22.5 %collective-permute-start.9 = (f32[64,2048]{1,0:T(8,128)}, f32[64,2048]{1,0:T(8,128)}, u32[]{:S(2)}, u32[]{:S(2)}) collective-permute-start(f32[64,2048]{1,0:T(8,128)} %fusion.15), channel_id=1, source_target_pairs={{0,4},{2,6},{4,0},{6,2},{8,12},{10,14},{12,8},{14,10},{1,5},{3,7},... | collective-permute-start | bytes 1572872 | tf_op jit(solution)/shard_map/ppermute | solution.py:58
  25.6 12.6 %copy-start.3 = (f32[64,512]{1,0:T(8,128)S(1)}, f32[64,512]{1,0:T(8,128)}, u32[]{:S(2)}) copy-start(f32[64,512]{1,0:T(8,128)} %copy-done.2) | copy-start | bytes 393220
  25.6 12.6 %copy-start.5 = (f32[64,512]{1,0:T(8,128)S(1)}, f32[64,512]{1,0:T(8,128)}, u32[]{:S(2)}) copy-start(f32[64,512]{1,0:T(8,128)} %copy-done.4) | copy-start | bytes 393220
  25.6 12.6 %copy-start.7 = (f32[64,512]{1,0:T(8,128)S(1)}, f32[64,512]{1,0:T(8,128)}, u32[]{:S(2)}) copy-start(f32[64,512]{1,0:T(8,128)} %copy-done.6) | copy-start | bytes 393220
  25.6 12.6 %copy-start.9 = (f32[64,512]{1,0:T(8,128)S(1)}, f32[64,512]{1,0:T(8,128)}, u32[]{:S(2)}) copy-start(f32[64,512]{1,0:T(8,128)} %copy-done.8) | copy-start | bytes 393220
  25.6 12.6 %copy-start.11 = (f32[64,512]{1,0:T(8,128)S(1)}, f32[64,512]{1,0:T(8,128)}, u32[]{:S(2)}) copy-start(f32[64,512]{1,0:T(8,128)} %copy-done.10) | copy-start | bytes 393220
  28.4 19.9 %collective-permute-start.1 = (f32[64,1024]{1,0:T(8,128)S(1)}, f32[64,1024]{1,0:T(8,128)S(1)}, u32[]{:S(2)}, u32[]{:S(2)}) collective-permute-start(f32[64,1024]{1,0:T(8,128)S(1)} %fusion.24), channel_id=1, source_target_pairs={{0,4},{2,6},{4,0},{6,2},{8,12},{10,14},{12,8},{14,10},{1,5},{3,7},... | collective-permute-start | bytes 786440 | tf_op jit(solution)/shard_map/ppermute | solution.py:58
  32.8 18.3 %collective-permute-start.4 = (f32[64,1024]{1,0:T(8,128)S(1)}, f32[64,1024]{1,0:T(8,128)S(1)}, u32[]{:S(2)}, u32[]{:S(2)}) collective-permute-start(f32[64,1024]{1,0:T(8,128)S(1)} %fusion.23), channel_id=1, source_target_pairs={{0,2},{2,0},{4,6},{6,4},{8,10},{10,8},{12,14},{14,12},{1,3},{3,1},... | collective-permute-start | bytes 786440 | tf_op jit(solution)/shard_map/ppermute | solution.py:58
  39.4 17.4 %collective-permute-start.7 = (f32[64,1024]{1,0:T(8,128)S(1)}, f32[64,1024]{1,0:T(8,128)S(1)}, u32[]{:S(2)}, u32[]{:S(2)}) collective-permute-start(f32[64,1024]{1,0:T(8,128)S(1)} %fusion.22), channel_id=1, source_target_pairs={{0,4},{2,6},{4,0},{6,2},{8,12},{10,14},{12,8},{14,10},{1,5},{3,7},... | collective-permute-start | bytes 786440 | tf_op jit(solution)/shard_map/ppermute | solution.py:58
  44.0 49.7 %copy-start.1 = (f32[1,512,256]{1,2,0:T(8,128)S(1)}, f32[1,512,256]{1,2,0:T(8,128)}, u32[]{:S(2)}) copy-start(f32[1,512,256]{1,2,0:T(8,128)} %copy.14) | copy-start | bytes 1572868
  44.0 13.4 %collective-permute-start.10 = (f32[64,1024]{1,0:T(8,128)S(1)}, f32[64,1024]{1,0:T(8,128)S(1)}, u32[]{:S(2)}, u32[]{:S(2)}) collective-permute-start(f32[64,1024]{1,0:T(8,128)S(1)} %fusion.21), channel_id=1, source_target_pairs={{0,2},{2,0},{4,6},{6,4},{8,10},{10,8},{12,14},{14,12},{1,3},{3,1},... | collective-permute-start | bytes 786440 | tf_op jit(solution)/shard_map/ppermute | solution.py:58
  48.4 11.6 %collective-permute-start.2 = (f32[64,512]{1,0:T(8,128)S(1)}, f32[64,512]{1,0:T(8,128)S(1)}, u32[]{:S(2)}, u32[]{:S(2)}) collective-permute-start(f32[64,512]{1,0:T(8,128)S(1)} %slice_select_fusion.3), channel_id=1, source_target_pairs={{0,8},{2,10},{4,12},{6,14},{8,0},{10,2},{12,4},{14,6},{1,9},{3,11}... | collective-permute-start | bytes 393224 | tf_op jit(solution)/shard_map/ppermute | solution.py:58
  51.1 17.1 %collective-permute-start.5 = (f32[64,512]{1,0:T(8,128)S(1)}, f32[64,512]{1,0:T(8,128)S(1)}, u32[]{:S(2)}, u32[]{:S(2)}) collective-permute-start(f32[64,512]{1,0:T(8,128)S(1)} %slice_select_fusion.2), channel_id=1, source_target_pairs={{0,8},{2,10},{4,12},{6,14},{8,0},{10,2},{12,4},{14,6},{1,9},{3,11}... | collective-permute-start | bytes 393224 | tf_op jit(solution)/shard_map/ppermute | solution.py:58
  56.9 14.2 %collective-permute-start.8 = (f32[64,512]{1,0:T(8,128)S(1)}, f32[64,512]{1,0:T(8,128)S(1)}, u32[]{:S(2)}, u32[]{:S(2)}) collective-permute-start(f32[64,512]{1,0:T(8,128)S(1)} %slice_select_fusion.1), channel_id=1, source_target_pairs={{0,8},{2,10},{4,12},{6,14},{8,0},{10,2},{12,4},{14,6},{1,9},{3,11}... | collective-permute-start | bytes 393224 | tf_op jit(solution)/shard_map/ppermute | solution.py:58
  57.5 15.2 %collective-permute-start.11 = (f32[64,512]{1,0:T(8,128)S(1)}, f32[64,512]{1,0:T(8,128)S(1)}, u32[]{:S(2)}, u32[]{:S(2)}) collective-permute-start(f32[64,512]{1,0:T(8,128)S(1)} %slice_select_fusion), channel_id=1, source_target_pairs={{0,8},{2,10},{4,12},{6,14},{8,0},{10,2},{12,4},{14,6},{1,9},{3,11}... | collective-permute-start | bytes 393224 | tf_op jit(solution)/shard_map/ppermute | solution.py:58
  73.5 1.3 %collective-permute-start.12 = (f32[]{:T(128)}, f32[]{:T(128)}, u32[]{:S(2)}, u32[]{:S(2)}) collective-permute-start(f32[]{:T(128)} %multiply_reduce_fusion), channel_id=1, source_target_pairs={{0,16},{16,0},{1,17},{17,1},{2,18},{18,2},{3,19},{19,3},{4,20},{20... | collective-permute-start | bytes 20 | tf_op jit(solution)/shard_map/ppermute | solution.py:33
  76.1 3.6 %collective-permute-start.13 = (f32[]{:T(128)}, f32[]{:T(128)}, u32[]{:S(2)}, u32[]{:S(2)}) collective-permute-start(f32[]{:T(128)} %add.78), channel_id=1, source_target_pairs={{0,1},{1,0},{2,3},{3,2},{4,5},{5,4},{6,7},{7,6},{8,9},{9,8},{10,11... | collective-permute-start | bytes 20 | tf_op jit(solution)/shard_map/ppermute | solution.py:33
  80.3 3.6 %collective-permute-start.14 = (f32[]{:T(128)}, f32[]{:T(128)}, u32[]{:S(2)}, u32[]{:S(2)}) collective-permute-start(f32[]{:T(128)} %add.79), channel_id=1, source_target_pairs={{0,2},{2,0},{4,6},{6,4},{8,10},{10,8},{12,14},{14,12},{1,3},{3,1},... | collective-permute-start | bytes 20 | tf_op jit(solution)/shard_map/ppermute | solution.py:33
  84.5 3.6 %collective-permute-start.15 = (f32[]{:T(128)}, f32[]{:T(128)}, u32[]{:S(2)}, u32[]{:S(2)}) collective-permute-start(f32[]{:T(128)} %add.80), channel_id=1, source_target_pairs={{0,4},{2,6},{4,0},{6,2},{8,12},{10,14},{12,8},{14,10},{1,5},{3,7},... | collective-permute-start | bytes 20 | tf_op jit(solution)/shard_map/ppermute | solution.py:33
  88.6 4.5 %collective-permute-start.16 = (f32[]{:T(128)}, f32[]{:T(128)}, u32[]{:S(2)}, u32[]{:S(2)}) collective-permute-start(f32[]{:T(128)} %add.81), channel_id=1, source_target_pairs={{0,8},{2,10},{4,12},{6,14},{8,0},{10,2},{12,4},{14,6},{1,9},{3,11}... | collective-permute-start | bytes 20 | tf_op jit(solution)/shard_map/ppermute | solution.py:33
  94.2 9.8 %collective-permute-start.17 = (bf16[512,128]{0,1:T(8,128)(2,1)S(1)}, bf16[512,128]{0,1:T(8,128)(2,1)S(1)}, u32[]{:S(2)}, u32[]{:S(2)}) collective-permute-start(bf16[512,128]{0,1:T(8,128)(2,1)S(1)} %slice.300), channel_id=1, source_target_pairs={{0,8},{2,10},{4,12},{6,14},{8,0},{10,2},{12,4},{14,6},{1,9},{3,11}... | collective-permute-start | bytes 393224 | tf_op jit(solution)/shard_map/ppermute | solution.py:72
  104.0 6.9 %collective-permute-start.20 = (bf16[512,128]{0,1:T(8,128)(2,1)S(1)}, bf16[512,128]{0,1:T(8,128)(2,1)S(1)}, u32[]{:S(2)}, u32[]{:S(2)}) collective-permute-start(bf16[512,128]{0,1:T(8,128)(2,1)S(1)} %get-tuple-element.57), channel_id=1, source_target_pairs={{0,8},{2,10},{4,12},{6,14},{8,0},{10,2},{12,4},{14,6},{1,9},{3,11}... | collective-permute-start | bytes 393224 | tf_op jit(solution)/shard_map/ppermute | solution.py:72
  104.1 8.7 %collective-permute-start.18 = (bf16[2,512,128]{1,2,0:T(8,128)(2,1)S(1)}, bf16[2,512,128]{1,2,0:T(8,128)(2,1)S(1)}, u32[]{:S(2)}, u32[]{:S(2)}) collective-permute-start(bf16[2,512,128]{1,2,0:T(8,128)(2,1)S(1)} %pad_maximum_fusion.18), channel_id=1, source_target_pairs={{0,4},{2,6},{4,0},{6,2},{8,12},{10,14},{12,8},{14,10},{1,5},{3,7},... | collective-permute-start | bytes 786440 | tf_op jit(solution)/shard_map/ppermute | solution.py:72
  111.0 7.0 %collective-permute-start.21 = (bf16[2,512,128]{1,2,0:T(8,128)(2,1)S(1)}, bf16[2,512,128]{1,2,0:T(8,128)(2,1)S(1)}, u32[]{:S(2)}, u32[]{:S(2)}) collective-permute-start(bf16[2,512,128]{1,2,0:T(8,128)(2,1)S(1)} %pad_maximum_fusion.19), channel_id=1, source_target_pairs={{0,2},{2,0},{4,6},{6,4},{8,10},{10,8},{12,14},{14,12},{1,3},{3,1},... | collective-permute-start | bytes 786440 | tf_op jit(solution)/shard_map/ppermute | solution.py:72
  113.0 10.7 %collective-permute-start.19 = (bf16[2,2,512,128]{2,3,1,0:T(8,128)(2,1)S(1)}, bf16[2,2,512,128]{2,3,1,0:T(8,128)(2,1)S(1)}, u32[]{:S(2)}, u32[]{:S(2)}) collective-permute-start(bf16[2,2,512,128]{2,3,1,0:T(8,128)(2,1)S(1)} %pad_maximum_fusion.8), channel_id=1, source_target_pairs={{0,2},{2,0},{4,6},{6,4},{8,10},{10,8},{12,14},{14,12},{1,3},{3,1},... | collective-permute-start | bytes 1572872 | tf_op jit(solution)/shard_map/ppermute | solution.py:72
  118.9 9.4 %collective-permute-start.22 = (bf16[2,2,512,128]{2,3,1,0:T(8,128)(2,1)}, bf16[2,2,512,128]{2,3,1,0:T(8,128)(2,1)S(1)}, u32[]{:S(2)}, u32[]{:S(2)}) collective-permute-start(bf16[2,2,512,128]{2,3,1,0:T(8,128)(2,1)} %pad_maximum_fusion.9), channel_id=1, source_target_pairs={{0,4},{2,6},{4,0},{6,2},{8,12},{10,14},{12,8},{14,10},{1,5},{3,7},... | collective-permute-start | bytes 1572872 | tf_op jit(solution)/shard_map/ppermute | solution.py:72
  (11 other events, 68.0 us)

commit v7 on v6

--- a/solution.py
+++ b/solution.py
@@ -79,7 +79,7 @@
     return current.reshape((-1,) + part.shape[1:])
 
 
-def scatter_rows(partial_t, axis, parts=4):
+def scatter_rows(partial_t, axis, parts=8):
     size = lax.axis_size(axis)
     cols = partial_t.shape[0]
     if size & (size - 1) or size == 1 or cols % (8 * parts):

time: 131 us -> 145 us (1.11)
  starting transfers between devices: 30.7 us -> 41.3 us
  other arithmetic: 14.5 us -> 17.9 us
  waiting for transfers between devices: 64.5 us -> 62 us
    ppermute x12 -> x24, starting transfers between devices: 16.7 us -> 28.4 us  [halving_scatter(): blocks = keep + lax.ppermute(send, axis, pairs)]
    ppermute x12 -> x24, waiting for transfers between devices: 29.9 us -> 26.1 us  [halving_scatter(): blocks = keep + lax.ppermute(send, axis, pairs)]
    select_n x12 -> x24, other arithmetic: 3.86 us -> 6.85 us  [halving_scatter(): send = jnp.where(mine == 1, low_part, high_part)]
    slice x6 -> x11, local copies, waits for them, and re-layouts: 2 us -> 3.73 us  [halving_scatter(): blocks[:, k * width:(k + 1) * width]]
    unnamed x43 -> x103, local copies, waits for them, and re-layouts: 6.54 us -> 5.93 us
    add x12 -> x16, other arithmetic: 5.12 us -> 5.46 us  [halving_scatter(): blocks = keep + lax.ppermute(send, axis, pairs)]
  transfers between devices with their start and end apart: 23 -> 35, of which waited for: 20 -> 18; matrix products, arithmetic and copies ran while one was open for 12% -> 14% of each run, Pallas kernels for 0% -> 0%
where the time goes in v7:
time: 145 us; the launch traced here: 144 us
  waiting for transfers between devices  62 us (43%)
  starting transfers between devices  41.3 us (28%)
  other arithmetic  17.9 us (12%)
  local copies, waits for them, and re-layouts  11 us (8%)
  matrix products  6.18 us (4%)
  between operations  5.71 us (4%)
    ppermute x24, starting transfers between devices, halving_scatter(): blocks = keep + lax.ppermute(send, axis, pairs)  28.4 us
    ppermute x6, waiting for transfers between devices, doubling_gather(): other = lax.ppermute(current, axis, pairs)  26.9 us
    ppermute x24, waiting for transfers between devices, halving_scatter(): blocks = keep + lax.ppermute(send, axis, pairs)  26.1 us
    ppermute x5, waiting for transfers between devices, butterfly_sum(): value = value + lax.ppermute(value, axis, pairs)  9.06 us
    ppermute x5, starting transfers between devices, butterfly_sum(): value = value + lax.ppermute(value, axis, pairs)  8.11 us
    select_n x24, other arithmetic, halving_scatter(): send = jnp.where(mine == 1, low_part, high_part)  6.85 us
    dot_general x1, matrix products, slot_term(): lax.dot_general(weighted, columns, (((0,), (0,)), ((), ())), preferred_el...  6.18 us
    unnamed x103, local copies, waits for them, and re-layouts  5.93 us
  transfers between devices with their start and end apart: 35, of which 18 were waited for; matrix products, arithmetic and copies ran while one was open for 14% of the time, Pallas kernels for 0%

profile of v7, /device:TPU:0, one launch (start us, length us, event | category | flops | bytes accessed | tf_op | source)
XLA Modules:
  0.0 144.1 jit_solution(6125678754339929876)
XLA Ops:
  1.3 6.2 %fusion.2 = f32[256,4096]{1,0:T(8,128)S(1)} fusion(bf16[1,8,128,4096]{3,2,1,0:T(8,128)(2,1)} %param.6, bf16[1,8,128,256]{3,2,1,0:T(8,128)(2,1)} %param.7, bf16[8]{0:T(256)(128)(2,1)S(1)} %get-tuple-element.99), kind=kOutput, calls=%fused_computation.2 | convolution fusion | flops 2147745792 | bytes 13107216 | tf_op jit(solution)/shard_map/dot_general | solution.py:19
  7.5 2.0 %copy-done = f32[256,4096]{1,0:T(8,128)} copy-done((f32[256,4096]{1,0:T(8,128)}, f32[256,4096]{1,0:T(8,128)S(1)}, u32[]{:S(2)}) %copy-start) | copy-done | bytes 4194328
  10.4 3.0 %collective-permute-start.21 = (f32[32,2048]{1,0:T(8,128)}, f32[32,2048]{1,0:T(8,128)}, u32[]{:S(2)}, u32[]{:S(2)}) collective-permute-start(f32[32,2048]{1,0:T(8,128)} %fusion.17), channel_id=1, source_target_pairs={{0,4},{2,6},{4,0},{6,2},{8,12},{10,14},{12,8},{14,10},{1,5},{3,7},... | collective-permute-start | bytes 786440 | tf_op jit(solution)/shard_map/ppermute | solution.py:58
  16.0 1.5 %collective-permute-start.18 = (f32[32,2048]{1,0:T(8,128)}, f32[32,2048]{1,0:T(8,128)}, u32[]{:S(2)}, u32[]{:S(2)}) collective-permute-start(f32[32,2048]{1,0:T(8,128)} %fusion.21), channel_id=1, source_target_pairs={{0,2},{2,0},{4,6},{6,4},{8,10},{10,8},{12,14},{14,12},{1,3},{3,1},... | collective-permute-start | bytes 786440 | tf_op jit(solution)/shard_map/ppermute | solution.py:58
  20.3 2.0 %collective-permute-start.9 = (f32[32,2048]{1,0:T(8,128)}, f32[32,2048]{1,0:T(8,128)}, u32[]{:S(2)}, u32[]{:S(2)}) collective-permute-start(f32[32,2048]{1,0:T(8,128)} %fusion.19), channel_id=1, source_target_pairs={{0,4},{2,6},{4,0},{6,2},{8,12},{10,14},{12,8},{14,10},{1,5},{3,7},... | collective-permute-start | bytes 786440 | tf_op jit(solution)/shard_map/ppermute | solution.py:58
  22.3 2.0 %fusion.35 = (f32[32,512]{1,0:T(8,128)S(1)}, f32[32,512]{1,0:T(8,128)S(1)}, f32[32,512]{1,0:T(8,128)S(1)}, f32[32,512]{1,0:T(8,128)S(1)}, f32[32,512]{1,0:T(8,12...) fusion(f32[256,4096]{1,0:T(8,128)} %copy-done), kind=kLoop, calls=%fused_computation.121 | loop fusion | bytes 1703936 | tf_op jit(solution)/shard_map/slice | solution.py:54
  31.7 1.6 %collective-permute-start.6 = (f32[32,2048]{1,0:T(8,128)}, f32[32,2048]{1,0:T(8,128)S(1)}, u32[]{:S(2)}, u32[]{:S(2)}) collective-permute-start(f32[32,2048]{1,0:T(8,128)} %fusion.23), channel_id=1, source_target_pairs={{0,2},{2,0},{4,6},{6,4},{8,10},{10,8},{12,14},{14,12},{1,3},{3,1},... | collective-permute-start | bytes 786440 | tf_op jit(solution)/shard_map/ppermute | solution.py:58
  37.5 1.9 %collective-permute-start.22 = (f32[32,1024]{1,0:T(8,128)S(1)}, f32[32,1024]{1,0:T(8,128)S(1)}, u32[]{:S(2)}, u32[]{:S(2)}) collective-permute-start(f32[32,1024]{1,0:T(8,128)S(1)} %fusion.25), channel_id=1, source_target_pairs={{0,2},{2,0},{4,6},{6,4},{8,10},{10,8},{12,14},{14,12},{1,3},{3,1},... | collective-permute-start | bytes 393224 | tf_op jit(solution)/shard_map/ppermute | solution.py:58
  40.5 1.6 %collective-permute-start.19 = (f32[32,1024]{1,0:T(8,128)S(1)}, f32[32,1024]{1,0:T(8,128)S(1)}, u32[]{:S(2)}, u32[]{:S(2)}) collective-permute-start(f32[32,1024]{1,0:T(8,128)S(1)} %fusion.26), channel_id=1, source_target_pairs={{0,4},{2,6},{4,0},{6,2},{8,12},{10,14},{12,8},{14,10},{1,5},{3,7},... | collective-permute-start | bytes 393224 | tf_op jit(solution)/shard_map/ppermute | solution.py:58
  44.2 2.0 %collective-permute-done = f32[32,2048]{1,0:T(8,128)S(1)} collective-permute-done((f32[32,2048]{1,0:T(8,128)S(1)}, f32[32,2048]{1,0:T(8,128)S(1)}, u32[]{:S(2)}, u32[]{:S(2)}) %collective-permute-start) | collective-permute-done | bytes 262176 | tf_op jit(solution)/shard_map/ppermute | solution.py:58
  46.2 2.1 %collective-permute-start.10 = (f32[32,1024]{1,0:T(8,128)S(1)}, f32[32,1024]{1,0:T(8,128)S(1)}, u32[]{:S(2)}, u32[]{:S(2)}) collective-permute-start(f32[32,1024]{1,0:T(8,128)S(1)} %fusion.29), channel_id=1, source_target_pairs={{0,2},{2,0},{4,6},{6,4},{8,10},{10,8},{12,14},{14,12},{1,3},{3,1},... | collective-permute-start | bytes 393224 | tf_op jit(solution)/shard_map/ppermute | solution.py:58
  51.8 1.6 %collective-permute-start.1 = (f32[32,1024]{1,0:T(8,128)S(1)}, f32[32,1024]{1,0:T(8,128)S(1)}, u32[]{:S(2)}, u32[]{:S(2)}) collective-permute-start(f32[32,1024]{1,0:T(8,128)S(1)} %fusion.32), channel_id=1, source_target_pairs={{0,4},{2,6},{4,0},{6,2},{8,12},{10,14},{12,8},{14,10},{1,5},{3,7},... | collective-permute-start | bytes 393224 | tf_op jit(solution)/shard_map/ppermute | solution.py:58
  53.5 2.7 %collective-permute-start.23 = (f32[32,512]{1,0:T(8,128)S(1)}, f32[32,512]{1,0:T(8,128)S(1)}, u32[]{:S(2)}, u32[]{:S(2)}) collective-permute-start(f32[32,512]{1,0:T(8,128)S(1)} %slice_select_fusion), channel_id=1, source_target_pairs={{0,8},{2,10},{4,12},{6,14},{8,0},{10,2},{12,4},{14,6},{1,9},{3,11}... | collective-permute-start | bytes 196616 | tf_op jit(solution)/shard_map/ppermute | solution.py:58
  56.7 2.6 %collective-permute-start.17 = (f32[32,512]{1,0:T(8,128)S(1)}, f32[32,512]{1,0:T(8,128)S(1)}, u32[]{:S(2)}, u32[]{:S(2)}) collective-permute-start(f32[32,512]{1,0:T(8,128)S(1)} %slice_select_fusion.2), channel_id=1, source_target_pairs={{0,8},{2,10},{4,12},{6,14},{8,0},{10,2},{12,4},{14,6},{1,9},{3,11}... | collective-permute-start | bytes 196616 | tf_op jit(solution)/shard_map/ppermute | solution.py:58
  60.7 1.8 %collective-permute-start.2 = (f32[32,512]{1,0:T(8,128)S(1)}, f32[32,512]{1,0:T(8,128)S(1)}, u32[]{:S(2)}, u32[]{:S(2)}) collective-permute-start(f32[32,512]{1,0:T(8,128)S(1)} %slice_select_fusion.7), channel_id=1, source_target_pairs={{0,8},{2,10},{4,12},{6,14},{8,0},{10,2},{12,4},{14,6},{1,9},{3,11}... | collective-permute-start | bytes 196616 | tf_op jit(solution)/shard_map/ppermute | solution.py:58
  62.5 6.1 %collective-permute-done.2 = f32[32,512]{1,0:T(8,128)S(1)} collective-permute-done((f32[32,512]{1,0:T(8,128)S(1)}, f32[32,512]{1,0:T(8,128)S(1)}, u32[]{:S(2)}, u32[]{:S(2)}) %collective-permute-start.2) | collective-permute-done | bytes 65568 | tf_op jit(solution)/shard_map/ppermute | solution.py:58
  68.6 6.1 %collective-permute-done.5 = f32[32,512]{1,0:T(8,128)S(1)} collective-permute-done((f32[32,512]{1,0:T(8,128)S(1)}, f32[32,512]{1,0:T(8,128)S(1)}, u32[]{:S(2)}, u32[]{:S(2)}) %collective-permute-start.5) | collective-permute-done | bytes 65568 | tf_op jit(solution)/shard_map/ppermute | solution.py:58
  74.7 5.8 %collective-permute-done.8 = f32[32,512]{1,0:T(8,128)S(1)} collective-permute-done((f32[32,512]{1,0:T(8,128)S(1)}, f32[32,512]{1,0:T(8,128)S(1)}, u32[]{:S(2)}, u32[]{:S(2)}) %collective-permute-start.8) | collective-permute-done | bytes 65568 | tf_op jit(solution)/shard_map/ppermute | solution.py:58
  80.5 5.1 %collective-permute-done.11 = f32[32,512]{1,0:T(8,128)S(1)} collective-permute-done((f32[32,512]{1,0:T(8,128)S(1)}, f32[32,512]{1,0:T(8,128)S(1)}, u32[]{:S(2)}, u32[]{:S(2)}) %collective-permute-start.11) | collective-permute-done | bytes 65568 | tf_op jit(solution)/shard_map/ppermute | solution.py:58
  89.2 2.9 %collective-permute-start.25 = (f32[]{:T(128)}, f32[]{:T(128)}, u32[]{:S(2)}, u32[]{:S(2)}) collective-permute-start(f32[]{:T(128)} %add.126), channel_id=1, source_target_pairs={{0,1},{1,0},{2,3},{3,2},{4,5},{5,4},{6,7},{7,6},{8,9},{9,8},{10,11... | collective-permute-start | bytes 20 | tf_op jit(solution)/shard_map/ppermute | solution.py:33
  93.5 2.2 %collective-permute-start.26 = (f32[]{:T(128)}, f32[]{:T(128)}, u32[]{:S(2)}, u32[]{:S(2)}) collective-permute-start(f32[]{:T(128)} %add.127), channel_id=1, source_target_pairs={{0,2},{2,0},{4,6},{6,4},{8,10},{10,8},{12,14},{14,12},{1,3},{3,1},... | collective-permute-start | bytes 20 | tf_op jit(solution)/shard_map/ppermute | solution.py:33
  95.7 1.6 %collective-permute-done.26 = f32[]{:T(128)} collective-permute-done((f32[]{:T(128)}, f32[]{:T(128)}, u32[]{:S(2)}, u32[]{:S(2)}) %collective-permute-start.26) | collective-permute-done | bytes 36 | tf_op jit(solution)/shard_map/ppermute | solution.py:33
  99.3 2.3 %collective-permute-done.27 = f32[]{:T(128)} collective-permute-done((f32[]{:T(128)}, f32[]{:T(128)}, u32[]{:S(2)}, u32[]{:S(2)}) %collective-permute-start.27) | collective-permute-done | bytes 36 | tf_op jit(solution)/shard_map/ppermute | solution.py:33
  102.2 1.7 %collective-permute-start.28 = (f32[]{:T(128)}, f32[]{:T(128)}, u32[]{:S(2)}, u32[]{:S(2)}) collective-permute-start(f32[]{:T(128)} %add.129), channel_id=1, source_target_pairs={{0,8},{2,10},{4,12},{6,14},{8,0},{10,2},{12,4},{14,6},{1,9},{3,11}... | collective-permute-start | bytes 20 | tf_op jit(solution)/shard_map/ppermute | solution.py:33
  103.9 3.0 %collective-permute-done.28 = f32[]{:T(128)} collective-permute-done((f32[]{:T(128)}, f32[]{:T(128)}, u32[]{:S(2)}, u32[]{:S(2)}) %collective-permute-start.28) | collective-permute-done | bytes 36 | tf_op jit(solution)/shard_map/ppermute | solution.py:33
  108.4 9.0 %collective-permute-done.29 = bf16[512,128]{0,1:T(8,128)(2,1)S(1)} collective-permute-done((bf16[512,128]{0,1:T(8,128)(2,1)S(1)}, bf16[512,128]{0,1:T(8,128)(2,1)S(1)}, u32[]{:S(2)}, u32[]{:S(2)}) %collective-permute-start.29) | collective-permute-done | bytes 131104 | tf_op jit(solution)/shard_map/ppermute | solution.py:72
  117.5 2.6 %collective-permute-start.30 = (bf16[2,512,128]{1,2,0:T(8,128)(2,1)S(1)}, bf16[2,512,128]{1,2,0:T(8,128)(2,1)S(1)}, u32[]{:S(2)}, u32[]{:S(2)}) collective-permute-start(bf16[2,512,128]{1,2,0:T(8,128)(2,1)S(1)} %pad_maximum_fusion.18), channel_id=1, source_target_pairs={{0,4},{2,6},{4,0},{6,2},{8,12},{10,14},{12,8},{14,10},{1,5},{3,7},... | collective-permute-start | bytes 786440 | tf_op jit(solution)/shard_map/ppermute | solution.py:72
  120.2 3.8 %collective-permute-done.32 = bf16[512,128]{0,1:T(8,128)(2,1)S(1)} collective-permute-done((bf16[512,128]{0,1:T(8,128)(2,1)S(1)}, bf16[512,128]{0,1:T(8,128)(2,1)S(1)}, u32[]{:S(2)}, u32[]{:S(2)}) %collective-permute-start.32) | collective-permute-done | bytes 131104 | tf_op jit(solution)/shard_map/ppermute | solution.py:72
  126.9 4.5 %collective-permute-done.33 = bf16[2,512,128]{1,2,0:T(8,128)(2,1)S(1)} collective-permute-done((bf16[2,512,128]{1,2,0:T(8,128)(2,1)S(1)}, bf16[2,512,128]{1,2,0:T(8,128)(2,1)S(1)}, u32[]{:S(2)}, u32[]{:S(2)}) %collective-permute-start.33) | collective-permute-done | bytes 262176 | tf_op jit(solution)/shard_map/ppermute | solution.py:72
  132.3 4.7 %collective-permute-done.31 = bf16[2,2,512,128]{2,3,1,0:T(8,128)(2,1)S(1)} collective-permute-done((bf16[2,2,512,128]{2,3,1,0:T(8,128)(2,1)S(1)}, bf16[2,2,512,128]{2,3,1,0:T(8,128)(2,1)S(1)}, u32[]{:S(2)}, u32[]{:S(2)}) %collective-permute-start.31) | collective-permute-done | bytes 524320 | tf_op jit(solution)/shard_map/ppermute | solution.py:72
  137.9 3.8 %collective-permute-done.34 = bf16[2,2,512,128]{2,3,1,0:T(8,128)(2,1)S(1)} collective-permute-done((bf16[2,2,512,128]{2,3,1,0:T(8,128)(2,1)}, bf16[2,2,512,128]{2,3,1,0:T(8,128)(2,1)S(1)}, u32[]{:S(2)}, u32[]{:S(2)}) %collective-permute-start.34) | collective-permute-done | bytes 524320 | tf_op jit(solution)/shard_map/ppermute | solution.py:72
  142.5 1.5 %maximum_bitcast_fusion = bf16[1,4096,256]{2,1,0:T(8,128)(2,1)} fusion(bf16[4096,128]{1,0:T(8,128)(2,1)S(1)} %bitcast.75, bf16[4096,128]{1,0:T(8,128)(2,1)S(1)} %bitcast.74), kind=kLoop, calls=%fused_computation.3 | loop fusion | flops 4194304 | bytes 4194304 | tf_op jit(solution)/shard_map/broadcast_in_dim | solution.py:132
  (220 shorter events, 37.2 us)
Async XLA Ops:
  10.4 21.2 %collective-permute-start.21 = (f32[32,2048]{1,0:T(8,128)}, f32[32,2048]{1,0:T(8,128)}, u32[]{:S(2)}, u32[]{:S(2)}) collective-permute-start(f32[32,2048]{1,0:T(8,128)} %fusion.17), channel_id=1, source_target_pairs={{0,4},{2,6},{4,0},{6,2},{8,12},{10,14},{12,8},{14,10},{1,5},{3,7},... | collective-permute-start | bytes 786440 | tf_op jit(solution)/shard_map/ppermute | solution.py:58
  16.0 18.3 %collective-permute-start.18 = (f32[32,2048]{1,0:T(8,128)}, f32[32,2048]{1,0:T(8,128)}, u32[]{:S(2)}, u32[]{:S(2)}) collective-permute-start(f32[32,2048]{1,0:T(8,128)} %fusion.21), channel_id=1, source_target_pairs={{0,2},{2,0},{4,6},{6,4},{8,10},{10,8},{12,14},{14,12},{1,3},{3,1},... | collective-permute-start | bytes 786440 | tf_op jit(solution)/shard_map/ppermute | solution.py:58
  18.3 17.8 %collective-permute-start.15 = (f32[32,2048]{1,0:T(8,128)}, f32[32,2048]{1,0:T(8,128)}, u32[]{:S(2)}, u32[]{:S(2)}) collective-permute-start(f32[32,2048]{1,0:T(8,128)} %fusion.18), channel_id=1, source_target_pairs={{0,4},{2,6},{4,0},{6,2},{8,12},{10,14},{12,8},{14,10},{1,5},{3,7},... | collective-permute-start | bytes 786440 | tf_op jit(solution)/shard_map/ppermute | solution.py:58
  19.5 18.0 %collective-permute-start.12 = (f32[32,2048]{1,0:T(8,128)}, f32[32,2048]{1,0:T(8,128)}, u32[]{:S(2)}, u32[]{:S(2)}) collective-permute-start(f32[32,2048]{1,0:T(8,128)} %fusion.22), channel_id=1, source_target_pairs={{0,2},{2,0},{4,6},{6,4},{8,10},{10,8},{12,14},{14,12},{1,3},{3,1},... | collective-permute-start | bytes 786440 | tf_op jit(solution)/shard_map/ppermute | solution.py:58
  20.3 20.2 %collective-permute-start.9 = (f32[32,2048]{1,0:T(8,128)}, f32[32,2048]{1,0:T(8,128)}, u32[]{:S(2)}, u32[]{:S(2)}) collective-permute-start(f32[32,2048]{1,0:T(8,128)} %fusion.19), channel_id=1, source_target_pairs={{0,4},{2,6},{4,0},{6,2},{8,12},{10,14},{12,8},{14,10},{1,5},{3,7},... | collective-permute-start | bytes 786440 | tf_op jit(solution)/shard_map/ppermute | solution.py:58
  31.7 11.5 %collective-permute-start.6 = (f32[32,2048]{1,0:T(8,128)}, f32[32,2048]{1,0:T(8,128)S(1)}, u32[]{:S(2)}, u32[]{:S(2)}) collective-permute-start(f32[32,2048]{1,0:T(8,128)} %fusion.23), channel_id=1, source_target_pairs={{0,2},{2,0},{4,6},{6,4},{8,10},{10,8},{12,14},{14,12},{1,3},{3,1},... | collective-permute-start | bytes 786440 | tf_op jit(solution)/shard_map/ppermute | solution.py:58
  34.4 9.6 %collective-permute-start.3 = (f32[32,2048]{1,0:T(8,128)}, f32[32,2048]{1,0:T(8,128)S(1)}, u32[]{:S(2)}, u32[]{:S(2)}) collective-permute-start(f32[32,2048]{1,0:T(8,128)} %fusion.20), channel_id=1, source_target_pairs={{0,4},{2,6},{4,0},{6,2},{8,12},{10,14},{12,8},{14,10},{1,5},{3,7},... | collective-permute-start | bytes 786440 | tf_op jit(solution)/shard_map/ppermute | solution.py:58
  36.1 10.1 %collective-permute-start = (f32[32,2048]{1,0:T(8,128)S(1)}, f32[32,2048]{1,0:T(8,128)S(1)}, u32[]{:S(2)}, u32[]{:S(2)}) collective-permute-start(f32[32,2048]{1,0:T(8,128)S(1)} %fusion.24), channel_id=1, source_target_pairs={{0,2},{2,0},{4,6},{6,4},{8,10},{10,8},{12,14},{14,12},{1,3},{3,1},... | collective-permute-start | bytes 786440 | tf_op jit(solution)/shard_map/ppermute | solution.py:58
  37.5 11.5 %collective-permute-start.22 = (f32[32,1024]{1,0:T(8,128)S(1)}, f32[32,1024]{1,0:T(8,128)S(1)}, u32[]{:S(2)}, u32[]{:S(2)}) collective-permute-start(f32[32,1024]{1,0:T(8,128)S(1)} %fusion.25), channel_id=1, source_target_pairs={{0,2},{2,0},{4,6},{6,4},{8,10},{10,8},{12,14},{14,12},{1,3},{3,1},... | collective-permute-start | bytes 393224 | tf_op jit(solution)/shard_map/ppermute | solution.py:58
  40.5 9.3 %collective-permute-start.19 = (f32[32,1024]{1,0:T(8,128)S(1)}, f32[32,1024]{1,0:T(8,128)S(1)}, u32[]{:S(2)}, u32[]{:S(2)}) collective-permute-start(f32[32,1024]{1,0:T(8,128)S(1)} %fusion.26), channel_id=1, source_target_pairs={{0,4},{2,6},{4,0},{6,2},{8,12},{10,14},{12,8},{14,10},{1,5},{3,7},... | collective-permute-start | bytes 393224 | tf_op jit(solution)/shard_map/ppermute | solution.py:58
  43.2 8.6 %collective-permute-start.16 = (f32[32,1024]{1,0:T(8,128)S(1)}, f32[32,1024]{1,0:T(8,128)S(1)}, u32[]{:S(2)}, u32[]{:S(2)}) collective-permute-start(f32[32,1024]{1,0:T(8,128)S(1)} %fusion.27), channel_id=1, source_target_pairs={{0,2},{2,0},{4,6},{6,4},{8,10},{10,8},{12,14},{14,12},{1,3},{3,1},... | collective-permute-start | bytes 393224 | tf_op jit(solution)/shard_map/ppermute | solution.py:58
  44.0 9.5 %collective-permute-start.13 = (f32[32,1024]{1,0:T(8,128)S(1)}, f32[32,1024]{1,0:T(8,128)S(1)}, u32[]{:S(2)}, u32[]{:S(2)}) collective-permute-start(f32[32,1024]{1,0:T(8,128)S(1)} %fusion.28), channel_id=1, source_target_pairs={{0,4},{2,6},{4,0},{6,2},{8,12},{10,14},{12,8},{14,10},{1,5},{3,7},... | collective-permute-start | bytes 393224 | tf_op jit(solution)/shard_map/ppermute | solution.py:58
  46.2 10.0 %collective-permute-start.10 = (f32[32,1024]{1,0:T(8,128)S(1)}, f32[32,1024]{1,0:T(8,128)S(1)}, u32[]{:S(2)}, u32[]{:S(2)}) collective-permute-start(f32[32,1024]{1,0:T(8,128)S(1)} %fusion.29), channel_id=1, source_target_pairs={{0,2},{2,0},{4,6},{6,4},{8,10},{10,8},{12,14},{14,12},{1,3},{3,1},... | collective-permute-start | bytes 393224 | tf_op jit(solution)/shard_map/ppermute | solution.py:58
  49.0 7.7 %collective-permute-start.7 = (f32[32,1024]{1,0:T(8,128)S(1)}, f32[32,1024]{1,0:T(8,128)S(1)}, u32[]{:S(2)}, u32[]{:S(2)}) collective-permute-start(f32[32,1024]{1,0:T(8,128)S(1)} %fusion.30), channel_id=1, source_target_pairs={{0,4},{2,6},{4,0},{6,2},{8,12},{10,14},{12,8},{14,10},{1,5},{3,7},... | collective-permute-start | bytes 393224 | tf_op jit(solution)/shard_map/ppermute | solution.py:58
  49.9 10.8 %collective-permute-start.4 = (f32[32,1024]{1,0:T(8,128)S(1)}, f32[32,1024]{1,0:T(8,128)S(1)}, u32[]{:S(2)}, u32[]{:S(2)}) collective-permute-start(f32[32,1024]{1,0:T(8,128)S(1)} %fusion.31), channel_id=1, source_target_pairs={{0,2},{2,0},{4,6},{6,4},{8,10},{10,8},{12,14},{14,12},{1,3},{3,1},... | collective-permute-start | bytes 393224 | tf_op jit(solution)/shard_map/ppermute | solution.py:58
  51.8 7.5 %collective-permute-start.1 = (f32[32,1024]{1,0:T(8,128)S(1)}, f32[32,1024]{1,0:T(8,128)S(1)}, u32[]{:S(2)}, u32[]{:S(2)}) collective-permute-start(f32[32,1024]{1,0:T(8,128)S(1)} %fusion.32), channel_id=1, source_target_pairs={{0,4},{2,6},{4,0},{6,2},{8,12},{10,14},{12,8},{14,10},{1,5},{3,7},... | collective-permute-start | bytes 393224 | tf_op jit(solution)/shard_map/ppermute | solution.py:58
  53.5 32.3 %collective-permute-start.23 = (f32[32,512]{1,0:T(8,128)S(1)}, f32[32,512]{1,0:T(8,128)S(1)}, u32[]{:S(2)}, u32[]{:S(2)}) collective-permute-start(f32[32,512]{1,0:T(8,128)S(1)} %slice_select_fusion), channel_id=1, source_target_pairs={{0,8},{2,10},{4,12},{6,14},{8,0},{10,2},{12,4},{14,6},{1,9},{3,11}... | collective-permute-start | bytes 196616 | tf_op jit(solution)/shard_map/ppermute | solution.py:58
  56.2 29.5 %collective-permute-start.20 = (f32[32,512]{1,0:T(8,128)S(1)}, f32[32,512]{1,0:T(8,128)S(1)}, u32[]{:S(2)}, u32[]{:S(2)}) collective-permute-start(f32[32,512]{1,0:T(8,128)S(1)} %slice_select_fusion.1), channel_id=1, source_target_pairs={{0,8},{2,10},{4,12},{6,14},{8,0},{10,2},{12,4},{14,6},{1,9},{3,11}... | collective-permute-start | bytes 196616 | tf_op jit(solution)/shard_map/ppermute | solution.py:58
  56.7 29.0 %collective-permute-start.17 = (f32[32,512]{1,0:T(8,128)S(1)}, f32[32,512]{1,0:T(8,128)S(1)}, u32[]{:S(2)}, u32[]{:S(2)}) collective-permute-start(f32[32,512]{1,0:T(8,128)S(1)} %slice_select_fusion.2), channel_id=1, source_target_pairs={{0,8},{2,10},{4,12},{6,14},{8,0},{10,2},{12,4},{14,6},{1,9},{3,11}... | collective-permute-start | bytes 196616 | tf_op jit(solution)/shard_map/ppermute | solution.py:58
  59.3 26.3 %collective-permute-start.14 = (f32[32,512]{1,0:T(8,128)S(1)}, f32[32,512]{1,0:T(8,128)S(1)}, u32[]{:S(2)}, u32[]{:S(2)}) collective-permute-start(f32[32,512]{1,0:T(8,128)S(1)} %slice_select_fusion.3), channel_id=1, source_target_pairs={{0,8},{2,10},{4,12},{6,14},{8,0},{10,2},{12,4},{14,6},{1,9},{3,11}... | collective-permute-start | bytes 196616 | tf_op jit(solution)/shard_map/ppermute | solution.py:58
  60.7 7.9 %collective-permute-start.2 = (f32[32,512]{1,0:T(8,128)S(1)}, f32[32,512]{1,0:T(8,128)S(1)}, u32[]{:S(2)}, u32[]{:S(2)}) collective-permute-start(f32[32,512]{1,0:T(8,128)S(1)} %slice_select_fusion.7), channel_id=1, source_target_pairs={{0,8},{2,10},{4,12},{6,14},{8,0},{10,2},{12,4},{14,6},{1,9},{3,11}... | collective-permute-start | bytes 196616 | tf_op jit(solution)/shard_map/ppermute | solution.py:58
  68.6 6.1 %collective-permute-start.5 = (f32[32,512]{1,0:T(8,128)S(1)}, f32[32,512]{1,0:T(8,128)S(1)}, u32[]{:S(2)}, u32[]{:S(2)}) collective-permute-start(f32[32,512]{1,0:T(8,128)S(1)} %slice_select_fusion.6), channel_id=1, source_target_pairs={{0,8},{2,10},{4,12},{6,14},{8,0},{10,2},{12,4},{14,6},{1,9},{3,11}... | collective-permute-start | bytes 196616 | tf_op jit(solution)/shard_map/ppermute | solution.py:58
  74.7 5.8 %collective-permute-start.8 = (f32[32,512]{1,0:T(8,128)S(1)}, f32[32,512]{1,0:T(8,128)S(1)}, u32[]{:S(2)}, u32[]{:S(2)}) collective-permute-start(f32[32,512]{1,0:T(8,128)S(1)} %slice_select_fusion.5), channel_id=1, source_target_pairs={{0,8},{2,10},{4,12},{6,14},{8,0},{10,2},{12,4},{14,6},{1,9},{3,11}... | collective-permute-start | bytes 196616 | tf_op jit(solution)/shard_map/ppermute | solution.py:58
  80.4 5.2 %collective-permute-start.11 = (f32[32,512]{1,0:T(8,128)S(1)}, f32[32,512]{1,0:T(8,128)S(1)}, u32[]{:S(2)}, u32[]{:S(2)}) collective-permute-start(f32[32,512]{1,0:T(8,128)S(1)} %slice_select_fusion.4), channel_id=1, source_target_pairs={{0,8},{2,10},{4,12},{6,14},{8,0},{10,2},{12,4},{14,6},{1,9},{3,11}... | collective-permute-start | bytes 196616 | tf_op jit(solution)/shard_map/ppermute | solution.py:58
  89.2 3.7 %collective-permute-start.25 = (f32[]{:T(128)}, f32[]{:T(128)}, u32[]{:S(2)}, u32[]{:S(2)}) collective-permute-start(f32[]{:T(128)} %add.126), channel_id=1, source_target_pairs={{0,1},{1,0},{2,3},{3,2},{4,5},{5,4},{6,7},{7,6},{8,9},{9,8},{10,11... | collective-permute-start | bytes 20 | tf_op jit(solution)/shard_map/ppermute | solution.py:33
  102.2 4.7 %collective-permute-start.28 = (f32[]{:T(128)}, f32[]{:T(128)}, u32[]{:S(2)}, u32[]{:S(2)}) collective-permute-start(f32[]{:T(128)} %add.129), channel_id=1, source_target_pairs={{0,8},{2,10},{4,12},{6,14},{8,0},{10,2},{12,4},{14,6},{1,9},{3,11}... | collective-permute-start | bytes 20 | tf_op jit(solution)/shard_map/ppermute | solution.py:33
  108.0 9.3 %collective-permute-start.29 = (bf16[512,128]{0,1:T(8,128)(2,1)S(1)}, bf16[512,128]{0,1:T(8,128)(2,1)S(1)}, u32[]{:S(2)}, u32[]{:S(2)}) collective-permute-start(bf16[512,128]{0,1:T(8,128)(2,1)S(1)} %slice.592), channel_id=1, source_target_pairs={{0,8},{2,10},{4,12},{6,14},{8,0},{10,2},{12,4},{14,6},{1,9},{3,11}... | collective-permute-start | bytes 393224 | tf_op jit(solution)/shard_map/ppermute | solution.py:72
  117.4 6.5 %collective-permute-start.32 = (bf16[512,128]{0,1:T(8,128)(2,1)S(1)}, bf16[512,128]{0,1:T(8,128)(2,1)S(1)}, u32[]{:S(2)}, u32[]{:S(2)}) collective-permute-start(bf16[512,128]{0,1:T(8,128)(2,1)S(1)} %get-tuple-element.65), channel_id=1, source_target_pairs={{0,8},{2,10},{4,12},{6,14},{8,0},{10,2},{12,4},{14,6},{1,9},{3,11}... | collective-permute-start | bytes 393224 | tf_op jit(solution)/shard_map/ppermute | solution.py:72
  117.5 8.4 %collective-permute-start.30 = (bf16[2,512,128]{1,2,0:T(8,128)(2,1)S(1)}, bf16[2,512,128]{1,2,0:T(8,128)(2,1)S(1)}, u32[]{:S(2)}, u32[]{:S(2)}) collective-permute-start(bf16[2,512,128]{1,2,0:T(8,128)(2,1)S(1)} %pad_maximum_fusion.18), channel_id=1, source_target_pairs={{0,4},{2,6},{4,0},{6,2},{8,12},{10,14},{12,8},{14,10},{1,5},{3,7},... | collective-permute-start | bytes 786440 | tf_op jit(solution)/shard_map/ppermute | solution.py:72
  124.0 7.4 %collective-permute-start.33 = (bf16[2,512,128]{1,2,0:T(8,128)(2,1)S(1)}, bf16[2,512,128]{1,2,0:T(8,128)(2,1)S(1)}, u32[]{:S(2)}, u32[]{:S(2)}) collective-permute-start(bf16[2,512,128]{1,2,0:T(8,128)(2,1)S(1)} %pad_maximum_fusion.19), channel_id=1, source_target_pairs={{0,2},{2,0},{4,6},{6,4},{8,10},{10,8},{12,14},{14,12},{1,3},{3,1},... | collective-permute-start | bytes 786440 | tf_op jit(solution)/shard_map/ppermute | solution.py:72
  126.0 11.0 %collective-permute-start.31 = (bf16[2,2,512,128]{2,3,1,0:T(8,128)(2,1)S(1)}, bf16[2,2,512,128]{2,3,1,0:T(8,128)(2,1)S(1)}, u32[]{:S(2)}, u32[]{:S(2)}) collective-permute-start(bf16[2,2,512,128]{2,3,1,0:T(8,128)(2,1)S(1)} %pad_maximum_fusion), channel_id=1, source_target_pairs={{0,2},{2,0},{4,6},{6,4},{8,10},{10,8},{12,14},{14,12},{1,3},{3,1},... | collective-permute-start | bytes 1572872 | tf_op jit(solution)/shard_map/ppermute | solution.py:72
  132.3 9.4 %collective-permute-start.34 = (bf16[2,2,512,128]{2,3,1,0:T(8,128)(2,1)}, bf16[2,2,512,128]{2,3,1,0:T(8,128)(2,1)S(1)}, u32[]{:S(2)}, u32[]{:S(2)}) collective-permute-start(bf16[2,2,512,128]{2,3,1,0:T(8,128)(2,1)} %pad_maximum_fusion.1), channel_id=1, source_target_pairs={{0,4},{2,6},{4,0},{6,2},{8,12},{10,14},{12,8},{14,10},{1,5},{3,7},... | collective-permute-start | bytes 1572872 | tf_op jit(solution)/shard_map/ppermute | solution.py:72
  (53 other events, 500.6 us)

commit v8 on v6

--- a/solution.py
+++ b/solution.py
@@ -62,21 +62,22 @@
 
 def doubling_gather(part, axis, order):
     size = lax.axis_size(axis)
-    levels = size.bit_length() - 1
     index = lax.axis_index(axis)
-    placed = []
-    current = part
+    width = part.shape[1]
+    held = [0]
+    blocks = part
     for bit in order:
         mine = (index >> bit) & 1
         pairs = [(i, i ^ (1 << bit)) for i in range(size)]
-        other = lax.ppermute(current, axis, pairs)
-        low = jnp.where(mine == 1, other, current)
-        high = jnp.where(mine == 1, current, other)
-        current = jnp.stack([low, high], axis=0)
-        placed.insert(0, bit)
-    perm = [placed.index(bit) for bit in range(levels - 1, -1, -1)]
-    current = jnp.transpose(current, perm + list(range(levels, current.ndim)))
-    return current.reshape((-1,) + part.shape[1:])
+        other = lax.ppermute(blocks, axis, pairs)
+        low = jnp.where(mine == 1, other, blocks)
+        high = jnp.where(mine == 1, blocks, other)
+        merged = sorted([(block, 0, k) for k, block in enumerate(held)] + [(block | (1 << bit), 1, k) for k, block in enumerate(held)])
+        blocks = jnp.concatenate(
+            [(high if side else low)[:, k * width:(k + 1) * width] for _, side, k in merged], axis=1
+        )
+        held = [block for block, _, _ in merged]
+    return blocks
 
 
 def scatter_rows(partial_t, axis, parts=4):
@@ -95,20 +96,20 @@
     )
 
 
-def gather_rows(part, axis):
+def gather_rows(part_t, axis, parts=4):
     size = lax.axis_size(axis)
-    cols = part.shape[1]
-    if size & (size - 1) or size == 1 or cols % 2:
-        return lax.all_gather(part, axis, axis=0, tiled=True)
-    first, second = bit_orders(size)
-    half = cols // 2
+    cols = part_t.shape[0]
+    if size & (size - 1) or size == 1 or cols % (16 * parts):
+        return lax.all_gather(part_t.T, axis, axis=0, tiled=True)
+    orders = bit_orders(size)
+    width = cols // parts
     return jnp.concatenate(
         [
-            doubling_gather(part[:, :half], axis, first[::-1]),
-            doubling_gather(part[:, half:], axis, second[::-1]),
+            doubling_gather(part_t[k * width:(k + 1) * width], axis, orders[k % 2][::-1])
+            for k in range(parts)
         ],
-        axis=1,
-    )
+        axis=0,
+    ).T
 
 
 def local(normed_input, key_grad, live_slots, master, first_moment, second_moment):
@@ -129,7 +130,7 @@
         moment1 / FIRST_CORRECTION / (jnp.sqrt(moment2 / SECOND_CORRECTION) + EPSILON)
         + WEIGHT_DECAY * master[0].T
     )
-    return gather_rows(update.astype(jnp.bfloat16).T, "dp")[None]
+    return gather_rows(update.astype(jnp.bfloat16), "dp")[None]
 
 
 def solution(mesh):

time: 131 us -> 142 us (1.084)
  other arithmetic: 14.5 us -> 22.3 us
  starting transfers between devices: 30.7 us -> 37.7 us
  waiting for transfers between devices: 64.5 us -> 58.2 us
  local copies, waits for them, and re-layouts: 9.88 us -> 11.3 us
    broadcast_in_dim x1, other arithmetic: 1.55 us -> 10.1 us  [local(): return gather_rows(update.astype(jnp.bfloat16), 'dp')[None]]
    ppermute x6 -> x12, starting transfers between devices: 5.38 us -> 12.4 us  [doubling_gather(): other = lax.ppermute(blocks, axis, pairs)]
    ppermute x6 -> x12, waiting for transfers between devices: 26.7 us -> 20.5 us  [doubling_gather(): other = lax.ppermute(blocks, axis, pairs)]
    broadcast_in_dim x0 -> x1, local copies, waits for them, and re-layouts: none -> 2.46 us  [local(): return gather_rows(update.astype(jnp.bfloat16), 'dp')[None]]
    unnamed x43 -> x57, local copies, waits for them, and re-layouts: 6.54 us -> 6.67 us
  transfers between devices with their start and end apart: 23 -> 29, of which waited for: 20 -> 21; matrix products, arithmetic and copies ran while one was open for 12% -> 11% of each run, Pallas kernels for 0% -> 0%
where the time goes in v8:
time: 142 us; the launch traced here: 141 us
  waiting for transfers between devices  58.2 us (41%)
  starting transfers between devices  37.7 us (27%)
  other arithmetic  22.3 us (16%)
  local copies, waits for them, and re-layouts  11.3 us (8%)
  matrix products  6.18 us (4%)
  between operations  5.24 us (4%)
    ppermute x12, waiting for transfers between devices, halving_scatter(): blocks = keep + lax.ppermute(send, axis, pairs)  29.9 us
    ppermute x12, waiting for transfers between devices, doubling_gather(): other = lax.ppermute(blocks, axis, pairs)  20.5 us
    ppermute x12, starting transfers between devices, halving_scatter(): blocks = keep + lax.ppermute(send, axis, pairs)  16.7 us
    ppermute x12, starting transfers between devices, doubling_gather(): other = lax.ppermute(blocks, axis, pairs)  12.4 us
    broadcast_in_dim x1, other arithmetic, local(): return gather_rows(update.astype(jnp.bfloat16), 'dp')[None]  10.1 us
    ppermute x5, starting transfers between devices, butterfly_sum(): value = value + lax.ppermute(value, axis, pairs)  8.59 us
    ppermute x5, waiting for transfers between devices, butterfly_sum(): value = value + lax.ppermute(value, axis, pairs)  7.85 us
    unnamed x57, local copies, waits for them, and re-layouts  6.67 us
  transfers between devices with their start and end apart: 29, of which 21 were waited for; matrix products, arithmetic and copies ran while one was open for 11% of the time, Pallas kernels for 0%

profile of v8, /device:TPU:0, one launch (start us, length us, event | category | flops | bytes accessed | tf_op | source)
XLA Modules:
  0.0 141.0 jit_solution(15900020080272867845)
XLA Ops:
  1.4 6.2 %fusion.2 = f32[256,4096]{1,0:T(8,128)S(1)} fusion(bf16[1,8,128,4096]{3,2,1,0:T(8,128)(2,1)} %param.6, bf16[1,8,128,256]{3,2,1,0:T(8,128)(2,1)} %param.7, bf16[8]{0:T(256)(128)(2,1)S(1)} %get-tuple-element.100), kind=kOutput, calls=%fused_computation.2 | convolution fusion | flops 2147745792 | bytes 13107216 | tf_op jit(solution)/shard_map/dot_general | solution.py:19
  7.6 2.0 %copy-done = f32[256,4096]{1,0:T(8,128)} copy-done((f32[256,4096]{1,0:T(8,128)}, f32[256,4096]{1,0:T(8,128)S(1)}, u32[]{:S(2)}) %copy-start) | copy-done | bytes 4194328
  10.9 2.9 %collective-permute-start = (f32[64,2048]{1,0:T(8,128)}, f32[64,2048]{1,0:T(8,128)}, u32[]{:S(2)}, u32[]{:S(2)}) collective-permute-start(f32[64,2048]{1,0:T(8,128)} %fusion.18), channel_id=1, source_target_pairs={{0,2},{2,0},{4,6},{6,4},{8,10},{10,8},{12,14},{14,12},{1,3},{3,1},... | collective-permute-start | bytes 1572872 | tf_op jit(solution)/shard_map/ppermute | solution.py:58
  13.9 1.6 %fusion.25 = (f32[64,1024]{1,0:T(8,128)S(1)}, f32[64,1024]{1,0:T(8,128)S(1)}, f32[64,1024]{1,0:T(8,128)S(1)}, f32[64,1024]{1,0:T(8,128)S(1)}, f32[64,1024]{1,0:T...) fusion(f32[256,4096]{1,0:T(8,128)} %copy-done), kind=kLoop, calls=%fused_computation.109 | loop fusion | bytes 4194304 | tf_op jit(solution)/shard_map/slice | solution.py:54
  16.4 1.6 %collective-permute-start.3 = (f32[64,2048]{1,0:T(8,128)}, f32[64,2048]{1,0:T(8,128)}, u32[]{:S(2)}, u32[]{:S(2)}) collective-permute-start(f32[64,2048]{1,0:T(8,128)} %fusion.16), channel_id=1, source_target_pairs={{0,4},{2,6},{4,0},{6,2},{8,12},{10,14},{12,8},{14,10},{1,5},{3,7},... | collective-permute-start | bytes 1572872 | tf_op jit(solution)/shard_map/ppermute | solution.py:58
  23.5 2.0 %copy.9 = f32[1,512,256]{1,2,0:T(8,128)} copy(f32[1,512,256]{2,1,0:T(8,128)} %param.11) | data formatting | bytes 1048576 | tf_op args[5]
  28.4 2.2 %collective-permute-start.1 = (f32[64,1024]{1,0:T(8,128)S(1)}, f32[64,1024]{1,0:T(8,128)S(1)}, u32[]{:S(2)}, u32[]{:S(2)}) collective-permute-start(f32[64,1024]{1,0:T(8,128)S(1)} %fusion.23), channel_id=1, source_target_pairs={{0,4},{2,6},{4,0},{6,2},{8,12},{10,14},{12,8},{14,10},{1,5},{3,7},... | collective-permute-start | bytes 786440 | tf_op jit(solution)/shard_map/ppermute | solution.py:58
  33.4 4.7 %collective-permute-done.6 = f32[64,2048]{1,0:T(8,128)} collective-permute-done((f32[64,2048]{1,0:T(8,128)}, f32[64,2048]{1,0:T(8,128)}, u32[]{:S(2)}, u32[]{:S(2)}) %collective-permute-start.6) | collective-permute-done | bytes 524320 | tf_op jit(solution)/shard_map/ppermute | solution.py:58
  39.4 2.2 %collective-permute-start.7 = (f32[64,1024]{1,0:T(8,128)S(1)}, f32[64,1024]{1,0:T(8,128)S(1)}, u32[]{:S(2)}, u32[]{:S(2)}) collective-permute-start(f32[64,1024]{1,0:T(8,128)S(1)} %fusion.21), channel_id=1, source_target_pairs={{0,4},{2,6},{4,0},{6,2},{8,12},{10,14},{12,8},{14,10},{1,5},{3,7},... | collective-permute-start | bytes 786440 | tf_op jit(solution)/shard_map/ppermute | solution.py:58
  44.4 3.9 %collective-permute-done.1 = f32[64,1024]{1,0:T(8,128)S(1)} collective-permute-done((f32[64,1024]{1,0:T(8,128)S(1)}, f32[64,1024]{1,0:T(8,128)S(1)}, u32[]{:S(2)}, u32[]{:S(2)}) %collective-permute-start.1) | collective-permute-done | bytes 262176 | tf_op jit(solution)/shard_map/ppermute | solution.py:58
  48.4 2.7 %collective-permute-start.2 = (f32[64,512]{1,0:T(8,128)S(1)}, f32[64,512]{1,0:T(8,128)S(1)}, u32[]{:S(2)}, u32[]{:S(2)}) collective-permute-start(f32[64,512]{1,0:T(8,128)S(1)} %slice_select_fusion.3), channel_id=1, source_target_pairs={{0,8},{2,10},{4,12},{6,14},{8,0},{10,2},{12,4},{14,6},{1,9},{3,11}... | collective-permute-start | bytes 393224 | tf_op jit(solution)/shard_map/ppermute | solution.py:58
  51.5 5.3 %collective-permute-done.7 = f32[64,1024]{1,0:T(8,128)S(1)} collective-permute-done((f32[64,1024]{1,0:T(8,128)S(1)}, f32[64,1024]{1,0:T(8,128)S(1)}, u32[]{:S(2)}, u32[]{:S(2)}) %collective-permute-start.7) | collective-permute-done | bytes 262176 | tf_op jit(solution)/shard_map/ppermute | solution.py:58
  57.5 2.5 %collective-permute-start.11 = (f32[64,512]{1,0:T(8,128)S(1)}, f32[64,512]{1,0:T(8,128)S(1)}, u32[]{:S(2)}, u32[]{:S(2)}) collective-permute-start(f32[64,512]{1,0:T(8,128)S(1)} %slice_select_fusion), channel_id=1, source_target_pairs={{0,8},{2,10},{4,12},{6,14},{8,0},{10,2},{12,4},{14,6},{1,9},{3,11}... | collective-permute-start | bytes 393224 | tf_op jit(solution)/shard_map/ppermute | solution.py:58
  60.1 8.2 %collective-permute-done.5 = f32[64,512]{1,0:T(8,128)S(1)} collective-permute-done((f32[64,512]{1,0:T(8,128)S(1)}, f32[64,512]{1,0:T(8,128)S(1)}, u32[]{:S(2)}, u32[]{:S(2)}) %collective-permute-start.5) | collective-permute-done | bytes 131104 | tf_op jit(solution)/shard_map/ppermute | solution.py:58
  68.3 2.8 %collective-permute-done.8 = f32[64,512]{1,0:T(8,128)S(1)} collective-permute-done((f32[64,512]{1,0:T(8,128)S(1)}, f32[64,512]{1,0:T(8,128)S(1)}, u32[]{:S(2)}, u32[]{:S(2)}) %collective-permute-start.8) | collective-permute-done | bytes 131104 | tf_op jit(solution)/shard_map/ppermute | solution.py:58
  71.1 1.6 %collective-permute-done.11 = f32[64,512]{1,0:T(8,128)S(1)} collective-permute-done((f32[64,512]{1,0:T(8,128)S(1)}, f32[64,512]{1,0:T(8,128)S(1)}, u32[]{:S(2)}, u32[]{:S(2)}) %collective-permute-start.11) | collective-permute-done | bytes 131104 | tf_op jit(solution)/shard_map/ppermute | solution.py:58
  76.1 2.9 %collective-permute-start.13 = (f32[]{:T(128)}, f32[]{:T(128)}, u32[]{:S(2)}, u32[]{:S(2)}) collective-permute-start(f32[]{:T(128)} %add.78), channel_id=1, source_target_pairs={{0,1},{1,0},{2,3},{3,2},{4,5},{5,4},{6,7},{7,6},{8,9},{9,8},{10,11... | collective-permute-start | bytes 20 | tf_op jit(solution)/shard_map/ppermute | solution.py:33
  80.2 1.9 %collective-permute-start.14 = (f32[]{:T(128)}, f32[]{:T(128)}, u32[]{:S(2)}, u32[]{:S(2)}) collective-permute-start(f32[]{:T(128)} %add.79), channel_id=1, source_target_pairs={{0,2},{2,0},{4,6},{6,4},{8,10},{10,8},{12,14},{14,12},{1,3},{3,1},... | collective-permute-start | bytes 20 | tf_op jit(solution)/shard_map/ppermute | solution.py:33
  82.1 1.7 %collective-permute-done.14 = f32[]{:T(128)} collective-permute-done((f32[]{:T(128)}, f32[]{:T(128)}, u32[]{:S(2)}, u32[]{:S(2)}) %collective-permute-start.14) | collective-permute-done | bytes 36 | tf_op jit(solution)/shard_map/ppermute | solution.py:33
  85.8 2.2 %collective-permute-done.15 = f32[]{:T(128)} collective-permute-done((f32[]{:T(128)}, f32[]{:T(128)}, u32[]{:S(2)}, u32[]{:S(2)}) %collective-permute-start.15) | collective-permute-done | bytes 36 | tf_op jit(solution)/shard_map/ppermute | solution.py:33
  88.6 2.5 %collective-permute-start.16 = (f32[]{:T(128)}, f32[]{:T(128)}, u32[]{:S(2)}, u32[]{:S(2)}) collective-permute-start(f32[]{:T(128)} %add.81), channel_id=1, source_target_pairs={{0,8},{2,10},{4,12},{6,14},{8,0},{10,2},{12,4},{14,6},{1,9},{3,11}... | collective-permute-start | bytes 20 | tf_op jit(solution)/shard_map/ppermute | solution.py:33
  91.1 2.0 %collective-permute-done.16 = f32[]{:T(128)} collective-permute-done((f32[]{:T(128)}, f32[]{:T(128)}, u32[]{:S(2)}, u32[]{:S(2)}) %collective-permute-start.16) | collective-permute-done | bytes 36 | tf_op jit(solution)/shard_map/ppermute | solution.py:33
  95.4 7.3 %collective-permute-done.17 = bf16[64,512]{1,0:T(8,128)(2,1)S(1)} collective-permute-done((bf16[64,512]{1,0:T(8,128)(2,1)S(1)}, bf16[64,512]{1,0:T(8,128)(2,1)S(1)}, u32[]{:S(2)}, u32[]{:S(2)}) %collective-permute-start.17) | collective-permute-done | bytes 65568 | tf_op jit(solution)/shard_map/ppermute | solution.py:72
  102.8 2.9 %collective-permute-start.23 = (bf16[64,512]{1,0:T(8,128)(2,1)S(1)}, bf16[64,512]{1,0:T(8,128)(2,1)S(1)}, u32[]{:S(2)}, u32[]{:S(2)}) collective-permute-start(bf16[64,512]{1,0:T(8,128)(2,1)S(1)} %get-tuple-element.64), channel_id=1, source_target_pairs={{0,8},{2,10},{4,12},{6,14},{8,0},{10,2},{12,4},{14,6},{1,9},{3,11}... | collective-permute-start | bytes 196616 | tf_op jit(solution)/shard_map/ppermute | solution.py:72
  105.8 2.6 %collective-permute-start.18 = (bf16[64,1024]{1,0:T(8,128)(2,1)S(1)}, bf16[64,1024]{1,0:T(8,128)(2,1)S(1)}, u32[]{:S(2)}, u32[]{:S(2)}) collective-permute-start(bf16[64,1024]{1,0:T(8,128)(2,1)S(1)} %pad_maximum_fusion.20), channel_id=1, source_target_pairs={{0,4},{2,6},{4,0},{6,2},{8,12},{10,14},{12,8},{14,10},{1,5},{3,7},... | collective-permute-start | bytes 393224 | tf_op jit(solution)/shard_map/ppermute | solution.py:72
  108.8 2.7 %collective-permute-done.26 = bf16[64,512]{1,0:T(8,128)(2,1)S(1)} collective-permute-done((bf16[64,512]{1,0:T(8,128)(2,1)S(1)}, bf16[64,512]{1,0:T(8,128)(2,1)S(1)}, u32[]{:S(2)}, u32[]{:S(2)}) %collective-permute-start.26) | collective-permute-done | bytes 65568 | tf_op jit(solution)/shard_map/ppermute | solution.py:72
  114.6 3.5 %collective-permute-done.24 = bf16[64,1024]{1,0:T(8,128)(2,1)S(1)} collective-permute-done((bf16[64,1024]{1,0:T(8,128)(2,1)S(1)}, bf16[64,1024]{1,0:T(8,128)(2,1)S(1)}, u32[]{:S(2)}, u32[]{:S(2)}) %collective-permute-start.24) | collective-permute-done | bytes 131104 | tf_op jit(solution)/shard_map/ppermute | solution.py:72
  119.1 2.1 %collective-permute-start.28 = (bf16[64,2048]{1,0:T(8,128)(2,1)S(1)}, bf16[64,2048]{1,0:T(8,128)(2,1)S(1)}, u32[]{:S(2)}, u32[]{:S(2)}) collective-permute-start(bf16[64,2048]{1,0:T(8,128)(2,1)S(1)} %pad_maximum_fusion.19), channel_id=1, source_target_pairs={{0,4},{2,6},{4,0},{6,2},{8,12},{10,14},{12,8},{14,10},{1,5},{3,7},... | collective-permute-start | bytes 786440 | tf_op jit(solution)/shard_map/ppermute | solution.py:72
  121.4 3.2 %collective-permute-done.25 = bf16[64,2048]{1,0:T(8,128)(2,1)S(1)} collective-permute-done((bf16[64,2048]{1,0:T(8,128)(2,1)S(1)}, bf16[64,2048]{1,0:T(8,128)(2,1)S(1)}, u32[]{:S(2)}, u32[]{:S(2)}) %collective-permute-start.25) | collective-permute-done | bytes 262176 | tf_op jit(solution)/shard_map/ppermute | solution.py:72
  125.4 2.8 %collective-permute-done.28 = bf16[64,2048]{1,0:T(8,128)(2,1)S(1)} collective-permute-done((bf16[64,2048]{1,0:T(8,128)(2,1)S(1)}, bf16[64,2048]{1,0:T(8,128)(2,1)S(1)}, u32[]{:S(2)}, u32[]{:S(2)}) %collective-permute-start.28) | collective-permute-done | bytes 262176 | tf_op jit(solution)/shard_map/ppermute | solution.py:72
  128.5 10.1 %maximum_bitcast_fusion = bf16[1,4096,256]{1,2,0:T(8,128)(2,1)S(1)} fusion(bf16[64,1024]{1,0:T(8,128)(2,1)S(1)} %get-tuple-element.81, bf16[64,1024]{1,0:T(8,128)(2,1)S(1)} %get-tuple-element.79, bf16[64,1024]{1,0:T(8,128)(2,1)S(1)} %get-tuple-element.80, bf16[64,1024]{1,0:T(8,128)(2,1)S(1)} %get-tuple-element.78, ...), kind=kLoop, calls=%fused_computation.3 | loop fusion | flops 20971520 | bytes 4194304 | tf_op jit(solution)/shard_map/broadcast_in_dim | solution.py:133
  138.6 2.5 %copy.11 = bf16[1,4096,256]{2,1,0:T(8,128)(2,1)} copy(bf16[1,4096,256]{1,2,0:T(8,128)(2,1)S(1)} %maximum_bitcast_fusion) | data formatting | bytes 4194304 | tf_op jit(solution)/shard_map/broadcast_in_dim | solution.py:133
  (149 shorter events, 30.6 us)
Async XLA Ops:
  10.9 16.0 %collective-permute-start = (f32[64,2048]{1,0:T(8,128)}, f32[64,2048]{1,0:T(8,128)}, u32[]{:S(2)}, u32[]{:S(2)}) collective-permute-start(f32[64,2048]{1,0:T(8,128)} %fusion.18), channel_id=1, source_target_pairs={{0,2},{2,0},{4,6},{6,4},{8,10},{10,8},{12,14},{14,12},{1,3},{3,1},... | collective-permute-start | bytes 1572872 | tf_op jit(solution)/shard_map/ppermute | solution.py:58
  16.4 15.2 %collective-permute-start.3 = (f32[64,2048]{1,0:T(8,128)}, f32[64,2048]{1,0:T(8,128)}, u32[]{:S(2)}, u32[]{:S(2)}) collective-permute-start(f32[64,2048]{1,0:T(8,128)} %fusion.16), channel_id=1, source_target_pairs={{0,4},{2,6},{4,0},{6,2},{8,12},{10,14},{12,8},{14,10},{1,5},{3,7},... | collective-permute-start | bytes 1572872 | tf_op jit(solution)/shard_map/ppermute | solution.py:58
  18.9 19.3 %collective-permute-start.6 = (f32[64,2048]{1,0:T(8,128)}, f32[64,2048]{1,0:T(8,128)}, u32[]{:S(2)}, u32[]{:S(2)}) collective-permute-start(f32[64,2048]{1,0:T(8,128)} %fusion.17), channel_id=1, source_target_pairs={{0,2},{2,0},{4,6},{6,4},{8,10},{10,8},{12,14},{14,12},{1,3},{3,1},... | collective-permute-start | bytes 1572872 | tf_op jit(solution)/shard_map/ppermute | solution.py:58
  20.4 22.4 %collective-permute-start.9 = (f32[64,2048]{1,0:T(8,128)}, f32[64,2048]{1,0:T(8,128)}, u32[]{:S(2)}, u32[]{:S(2)}) collective-permute-start(f32[64,2048]{1,0:T(8,128)} %fusion.15), channel_id=1, source_target_pairs={{0,4},{2,6},{4,0},{6,2},{8,12},{10,14},{12,8},{14,10},{1,5},{3,7},... | collective-permute-start | bytes 1572872 | tf_op jit(solution)/shard_map/ppermute | solution.py:58
  25.6 12.6 %copy-start.9 = (f32[64,512]{1,0:T(8,128)S(1)}, f32[64,512]{1,0:T(8,128)}, u32[]{:S(2)}) copy-start(f32[64,512]{1,0:T(8,128)} %copy-done.8) | copy-start | bytes 393220
  25.6 12.6 %copy-start.11 = (f32[64,512]{1,0:T(8,128)S(1)}, f32[64,512]{1,0:T(8,128)}, u32[]{:S(2)}) copy-start(f32[64,512]{1,0:T(8,128)} %copy-done.10) | copy-start | bytes 393220
  28.4 19.9 %collective-permute-start.1 = (f32[64,1024]{1,0:T(8,128)S(1)}, f32[64,1024]{1,0:T(8,128)S(1)}, u32[]{:S(2)}, u32[]{:S(2)}) collective-permute-start(f32[64,1024]{1,0:T(8,128)S(1)} %fusion.23), channel_id=1, source_target_pairs={{0,4},{2,6},{4,0},{6,2},{8,12},{10,14},{12,8},{14,10},{1,5},{3,7},... | collective-permute-start | bytes 786440 | tf_op jit(solution)/shard_map/ppermute | solution.py:58
  32.8 18.3 %collective-permute-start.4 = (f32[64,1024]{1,0:T(8,128)S(1)}, f32[64,1024]{1,0:T(8,128)S(1)}, u32[]{:S(2)}, u32[]{:S(2)}) collective-permute-start(f32[64,1024]{1,0:T(8,128)S(1)} %fusion.22), channel_id=1, source_target_pairs={{0,2},{2,0},{4,6},{6,4},{8,10},{10,8},{12,14},{14,12},{1,3},{3,1},... | collective-permute-start | bytes 786440 | tf_op jit(solution)/shard_map/ppermute | solution.py:58
  39.4 17.4 %collective-permute-start.7 = (f32[64,1024]{1,0:T(8,128)S(1)}, f32[64,1024]{1,0:T(8,128)S(1)}, u32[]{:S(2)}, u32[]{:S(2)}) collective-permute-start(f32[64,1024]{1,0:T(8,128)S(1)} %fusion.21), channel_id=1, source_target_pairs={{0,4},{2,6},{4,0},{6,2},{8,12},{10,14},{12,8},{14,10},{1,5},{3,7},... | collective-permute-start | bytes 786440 | tf_op jit(solution)/shard_map/ppermute | solution.py:58
  44.0 49.7 %copy-start.1 = (f32[1,512,256]{1,2,0:T(8,128)S(1)}, f32[1,512,256]{1,2,0:T(8,128)}, u32[]{:S(2)}) copy-start(f32[1,512,256]{1,2,0:T(8,128)} %copy.9) | copy-start | bytes 1572868
  44.0 13.4 %collective-permute-start.10 = (f32[64,1024]{1,0:T(8,128)S(1)}, f32[64,1024]{1,0:T(8,128)S(1)}, u32[]{:S(2)}, u32[]{:S(2)}) collective-permute-start(f32[64,1024]{1,0:T(8,128)S(1)} %fusion.20), channel_id=1, source_target_pairs={{0,2},{2,0},{4,6},{6,4},{8,10},{10,8},{12,14},{14,12},{1,3},{3,1},... | collective-permute-start | bytes 786440 | tf_op jit(solution)/shard_map/ppermute | solution.py:58
  48.4 11.7 %collective-permute-start.2 = (f32[64,512]{1,0:T(8,128)S(1)}, f32[64,512]{1,0:T(8,128)S(1)}, u32[]{:S(2)}, u32[]{:S(2)}) collective-permute-start(f32[64,512]{1,0:T(8,128)S(1)} %slice_select_fusion.3), channel_id=1, source_target_pairs={{0,8},{2,10},{4,12},{6,14},{8,0},{10,2},{12,4},{14,6},{1,9},{3,11}... | collective-permute-start | bytes 393224 | tf_op jit(solution)/shard_map/ppermute | solution.py:58
  51.1 17.1 %collective-permute-start.5 = (f32[64,512]{1,0:T(8,128)S(1)}, f32[64,512]{1,0:T(8,128)S(1)}, u32[]{:S(2)}, u32[]{:S(2)}) collective-permute-start(f32[64,512]{1,0:T(8,128)S(1)} %slice_select_fusion.2), channel_id=1, source_target_pairs={{0,8},{2,10},{4,12},{6,14},{8,0},{10,2},{12,4},{14,6},{1,9},{3,11}... | collective-permute-start | bytes 393224 | tf_op jit(solution)/shard_map/ppermute | solution.py:58
  56.9 14.1 %collective-permute-start.8 = (f32[64,512]{1,0:T(8,128)S(1)}, f32[64,512]{1,0:T(8,128)S(1)}, u32[]{:S(2)}, u32[]{:S(2)}) collective-permute-start(f32[64,512]{1,0:T(8,128)S(1)} %slice_select_fusion.1), channel_id=1, source_target_pairs={{0,8},{2,10},{4,12},{6,14},{8,0},{10,2},{12,4},{14,6},{1,9},{3,11}... | collective-permute-start | bytes 393224 | tf_op jit(solution)/shard_map/ppermute | solution.py:58
  57.5 15.1 %collective-permute-start.11 = (f32[64,512]{1,0:T(8,128)S(1)}, f32[64,512]{1,0:T(8,128)S(1)}, u32[]{:S(2)}, u32[]{:S(2)}) collective-permute-start(f32[64,512]{1,0:T(8,128)S(1)} %slice_select_fusion), channel_id=1, source_target_pairs={{0,8},{2,10},{4,12},{6,14},{8,0},{10,2},{12,4},{14,6},{1,9},{3,11}... | collective-permute-start | bytes 393224 | tf_op jit(solution)/shard_map/ppermute | solution.py:58
  73.5 1.3 collective-permute-start.12
  76.1 3.6 %collective-permute-start.13 = (f32[]{:T(128)}, f32[]{:T(128)}, u32[]{:S(2)}, u32[]{:S(2)}) collective-permute-start(f32[]{:T(128)} %add.78), channel_id=1, source_target_pairs={{0,1},{1,0},{2,3},{3,2},{4,5},{5,4},{6,7},{7,6},{8,9},{9,8},{10,11... | collective-permute-start | bytes 20 | tf_op jit(solution)/shard_map/ppermute | solution.py:33
  80.2 3.6 %collective-permute-start.14 = (f32[]{:T(128)}, f32[]{:T(128)}, u32[]{:S(2)}, u32[]{:S(2)}) collective-permute-start(f32[]{:T(128)} %add.79), channel_id=1, source_target_pairs={{0,2},{2,0},{4,6},{6,4},{8,10},{10,8},{12,14},{14,12},{1,3},{3,1},... | collective-permute-start | bytes 20 | tf_op jit(solution)/shard_map/ppermute | solution.py:33
  84.4 3.6 %collective-permute-start.15 = (f32[]{:T(128)}, f32[]{:T(128)}, u32[]{:S(2)}, u32[]{:S(2)}) collective-permute-start(f32[]{:T(128)} %add.80), channel_id=1, source_target_pairs={{0,4},{2,6},{4,0},{6,2},{8,12},{10,14},{12,8},{14,10},{1,5},{3,7},... | collective-permute-start | bytes 20 | tf_op jit(solution)/shard_map/ppermute | solution.py:33
  88.6 4.5 %collective-permute-start.16 = (f32[]{:T(128)}, f32[]{:T(128)}, u32[]{:S(2)}, u32[]{:S(2)}) collective-permute-start(f32[]{:T(128)} %add.81), channel_id=1, source_target_pairs={{0,8},{2,10},{4,12},{6,14},{8,0},{10,2},{12,4},{14,6},{1,9},{3,11}... | collective-permute-start | bytes 20 | tf_op jit(solution)/shard_map/ppermute | solution.py:33
  94.2 8.5 %collective-permute-start.17 = (bf16[64,512]{1,0:T(8,128)(2,1)S(1)}, bf16[64,512]{1,0:T(8,128)(2,1)S(1)}, u32[]{:S(2)}, u32[]{:S(2)}) collective-permute-start(bf16[64,512]{1,0:T(8,128)(2,1)S(1)} %slice.484), channel_id=1, source_target_pairs={{0,8},{2,10},{4,12},{6,14},{8,0},{10,2},{12,4},{14,6},{1,9},{3,11}... | collective-permute-start | bytes 196616 | tf_op jit(solution)/shard_map/ppermute | solution.py:72
  102.7 5.7 %collective-permute-start.20 = (bf16[64,512]{1,0:T(8,128)(2,1)S(1)}, bf16[64,512]{1,0:T(8,128)(2,1)S(1)}, u32[]{:S(2)}, u32[]{:S(2)}) collective-permute-start(bf16[64,512]{1,0:T(8,128)(2,1)S(1)} %get-tuple-element.65), channel_id=1, source_target_pairs={{0,8},{2,10},{4,12},{6,14},{8,0},{10,2},{12,4},{14,6},{1,9},{3,11}... | collective-permute-start | bytes 196616 | tf_op jit(solution)/shard_map/ppermute | solution.py:72
  102.8 6.0 %collective-permute-start.23 = (bf16[64,512]{1,0:T(8,128)(2,1)S(1)}, bf16[64,512]{1,0:T(8,128)(2,1)S(1)}, u32[]{:S(2)}, u32[]{:S(2)}) collective-permute-start(bf16[64,512]{1,0:T(8,128)(2,1)S(1)} %get-tuple-element.64), channel_id=1, source_target_pairs={{0,8},{2,10},{4,12},{6,14},{8,0},{10,2},{12,4},{14,6},{1,9},{3,11}... | collective-permute-start | bytes 196616 | tf_op jit(solution)/shard_map/ppermute | solution.py:72
  105.7 5.8 %collective-permute-start.26 = (bf16[64,512]{1,0:T(8,128)(2,1)S(1)}, bf16[64,512]{1,0:T(8,128)(2,1)S(1)}, u32[]{:S(2)}, u32[]{:S(2)}) collective-permute-start(bf16[64,512]{1,0:T(8,128)(2,1)S(1)} %get-tuple-element.63), channel_id=1, source_target_pairs={{0,8},{2,10},{4,12},{6,14},{8,0},{10,2},{12,4},{14,6},{1,9},{3,11}... | collective-permute-start | bytes 196616 | tf_op jit(solution)/shard_map/ppermute | solution.py:72
  105.8 8.1 %collective-permute-start.18 = (bf16[64,1024]{1,0:T(8,128)(2,1)S(1)}, bf16[64,1024]{1,0:T(8,128)(2,1)S(1)}, u32[]{:S(2)}, u32[]{:S(2)}) collective-permute-start(bf16[64,1024]{1,0:T(8,128)(2,1)S(1)} %pad_maximum_fusion.20), channel_id=1, source_target_pairs={{0,4},{2,6},{4,0},{6,2},{8,12},{10,14},{12,8},{14,10},{1,5},{3,7},... | collective-permute-start | bytes 393224 | tf_op jit(solution)/shard_map/ppermute | solution.py:72
  111.6 6.5 %collective-permute-start.24 = (bf16[64,1024]{1,0:T(8,128)(2,1)S(1)}, bf16[64,1024]{1,0:T(8,128)(2,1)S(1)}, u32[]{:S(2)}, u32[]{:S(2)}) collective-permute-start(bf16[64,1024]{1,0:T(8,128)(2,1)S(1)} %pad_maximum_fusion.22), channel_id=1, source_target_pairs={{0,4},{2,6},{4,0},{6,2},{8,12},{10,14},{12,8},{14,10},{1,5},{3,7},... | collective-permute-start | bytes 393224 | tf_op jit(solution)/shard_map/ppermute | solution.py:72
  111.7 7.1 %collective-permute-start.21 = (bf16[64,1024]{1,0:T(8,128)(2,1)S(1)}, bf16[64,1024]{1,0:T(8,128)(2,1)S(1)}, u32[]{:S(2)}, u32[]{:S(2)}) collective-permute-start(bf16[64,1024]{1,0:T(8,128)(2,1)S(1)} %pad_maximum_fusion.21), channel_id=1, source_target_pairs={{0,2},{2,0},{4,6},{6,4},{8,10},{10,8},{12,14},{14,12},{1,3},{3,1},... | collective-permute-start | bytes 393224 | tf_op jit(solution)/shard_map/ppermute | solution.py:72
  112.3 6.7 %collective-permute-start.27 = (bf16[64,1024]{1,0:T(8,128)(2,1)S(1)}, bf16[64,1024]{1,0:T(8,128)(2,1)S(1)}, u32[]{:S(2)}, u32[]{:S(2)}) collective-permute-start(bf16[64,1024]{1,0:T(8,128)(2,1)S(1)} %pad_maximum_fusion.23), channel_id=1, source_target_pairs={{0,2},{2,0},{4,6},{6,4},{8,10},{10,8},{12,14},{14,12},{1,3},{3,1},... | collective-permute-start | bytes 393224 | tf_op jit(solution)/shard_map/ppermute | solution.py:72
  114.0 7.2 %collective-permute-start.19 = (bf16[64,2048]{1,0:T(8,128)(2,1)S(1)}, bf16[64,2048]{1,0:T(8,128)(2,1)S(1)}, u32[]{:S(2)}, u32[]{:S(2)}) collective-permute-start(bf16[64,2048]{1,0:T(8,128)(2,1)S(1)} %pad_maximum_fusion.16), channel_id=1, source_target_pairs={{0,2},{2,0},{4,6},{6,4},{8,10},{10,8},{12,14},{14,12},{1,3},{3,1},... | collective-permute-start | bytes 786440 | tf_op jit(solution)/shard_map/ppermute | solution.py:72
  118.2 6.4 %collective-permute-start.25 = (bf16[64,2048]{1,0:T(8,128)(2,1)S(1)}, bf16[64,2048]{1,0:T(8,128)(2,1)S(1)}, u32[]{:S(2)}, u32[]{:S(2)}) collective-permute-start(bf16[64,2048]{1,0:T(8,128)(2,1)S(1)} %pad_maximum_fusion.18), channel_id=1, source_target_pairs={{0,2},{2,0},{4,6},{6,4},{8,10},{10,8},{12,14},{14,12},{1,3},{3,1},... | collective-permute-start | bytes 786440 | tf_op jit(solution)/shard_map/ppermute | solution.py:72
  118.9 6.4 %collective-permute-start.22 = (bf16[64,2048]{1,0:T(8,128)(2,1)S(1)}, bf16[64,2048]{1,0:T(8,128)(2,1)S(1)}, u32[]{:S(2)}, u32[]{:S(2)}) collective-permute-start(bf16[64,2048]{1,0:T(8,128)(2,1)S(1)} %pad_maximum_fusion.17), channel_id=1, source_target_pairs={{0,4},{2,6},{4,0},{6,2},{8,12},{10,14},{12,8},{14,10},{1,5},{3,7},... | collective-permute-start | bytes 786440 | tf_op jit(solution)/shard_map/ppermute | solution.py:72
  119.1 9.0 %collective-permute-start.28 = (bf16[64,2048]{1,0:T(8,128)(2,1)S(1)}, bf16[64,2048]{1,0:T(8,128)(2,1)S(1)}, u32[]{:S(2)}, u32[]{:S(2)}) collective-permute-start(bf16[64,2048]{1,0:T(8,128)(2,1)S(1)} %pad_maximum_fusion.19), channel_id=1, source_target_pairs={{0,4},{2,6},{4,0},{6,2},{8,12},{10,14},{12,8},{14,10},{1,5},{3,7},... | collective-permute-start | bytes 786440 | tf_op jit(solution)/shard_map/ppermute | solution.py:72
  (17 other events, 132.7 us)

commit v9 on v6

--- a/solution.py
+++ b/solution.py
@@ -88,7 +88,7 @@
     width = cols // parts
     return jnp.concatenate(
         [
-            halving_scatter(partial_t[k * width:(k + 1) * width], axis, orders[k % 2])
+            halving_scatter(partial_t[k * width:(k + 1) * width], axis, orders[int(k % 4 == 1)])
             for k in range(parts)
         ],
         axis=0,

time: 131 us -> 137 us (1.046)
  starting transfers between devices: 30.7 us -> 38.3 us
    ppermute x12, starting transfers between devices: 16.7 us -> 23.2 us  [halving_scatter(): blocks = keep + lax.ppermute(send, axis, pairs)]
    unnamed x43 -> x57, local copies, waits for them, and re-layouts: 6.54 us -> 5.54 us
  transfers between devices with their start and end apart: 23 -> 23, of which waited for: 20 -> 19; matrix products, arithmetic and copies ran while one was open for 12% -> 11% of each run, Pallas kernels for 0% -> 0%
where the time goes in v9:
time: 137 us; the launch traced here: 136 us
  waiting for transfers between devices  63.4 us (46%)
  starting transfers between devices  38.3 us (28%)
  other arithmetic  14.5 us (11%)
  local copies, waits for them, and re-layouts  8.59 us (6%)
  matrix products  6.18 us (5%)
  between operations  5.16 us (4%)
    ppermute x12, waiting for transfers between devices, halving_scatter(): blocks = keep + lax.ppermute(send, axis, pairs)  29.5 us
    ppermute x6, waiting for transfers between devices, doubling_gather(): other = lax.ppermute(current, axis, pairs)  25.8 us
    ppermute x12, starting transfers between devices, halving_scatter(): blocks = keep + lax.ppermute(send, axis, pairs)  23.2 us
    ppermute x5, starting transfers between devices, butterfly_sum(): value = value + lax.ppermute(value, axis, pairs)  9.05 us
    ppermute x5, waiting for transfers between devices, butterfly_sum(): value = value + lax.ppermute(value, axis, pairs)  8.13 us
    dot_general x1, matrix products, slot_term(): lax.dot_general(weighted, columns, (((0,), (0,)), ((), ())), preferred_el...  6.18 us
    ppermute x6, starting transfers between devices, doubling_gather(): other = lax.ppermute(current, axis, pairs)  6.12 us
    unnamed x57, local copies, waits for them, and re-layouts  5.54 us
  transfers between devices with their start and end apart: 23, of which 19 were waited for; matrix products, arithmetic and copies ran while one was open for 11% of the time, Pallas kernels for 0%

profile of v9, /device:TPU:0, one launch (start us, length us, event | category | flops | bytes accessed | tf_op | source)
XLA Modules:
  0.0 136.2 jit_solution(6274360407834804246)
XLA Ops:
  1.4 6.2 %fusion.2 = f32[256,4096]{1,0:T(8,128)S(1)} fusion(bf16[1,8,128,4096]{3,2,1,0:T(8,128)(2,1)} %param.6, bf16[1,8,128,256]{3,2,1,0:T(8,128)(2,1)} %param.7, bf16[8]{0:T(256)(128)(2,1)S(1)} %get-tuple-element.62), kind=kOutput, calls=%fused_computation.2 | convolution fusion | flops 2147745792 | bytes 13107216 | tf_op jit(solution)/shard_map/dot_general | solution.py:19
  7.8 1.7 %copy-done = f32[256,4096]{1,0:T(8,128)} copy-done((f32[256,4096]{1,0:T(8,128)}, f32[256,4096]{1,0:T(8,128)S(1)}, u32[]{:S(2)}) %copy-start) | copy-done | bytes 4194328
  10.8 2.9 %collective-permute-start = (f32[64,2048]{1,0:T(8,128)}, f32[64,2048]{1,0:T(8,128)}, u32[]{:S(2)}, u32[]{:S(2)}) collective-permute-start(f32[64,2048]{1,0:T(8,128)} %fusion.18), channel_id=1, source_target_pairs={{0,2},{2,0},{4,6},{6,4},{8,10},{10,8},{12,14},{14,12},{1,3},{3,1},... | collective-permute-start | bytes 1572872 | tf_op jit(solution)/shard_map/ppermute | solution.py:58
  15.9 1.6 %collective-permute-start.3 = (f32[64,2048]{1,0:T(8,128)}, f32[64,2048]{1,0:T(8,128)}, u32[]{:S(2)}, u32[]{:S(2)}) collective-permute-start(f32[64,2048]{1,0:T(8,128)} %fusion.15), channel_id=1, source_target_pairs={{0,4},{2,6},{4,0},{6,2},{8,12},{10,14},{12,8},{14,10},{1,5},{3,7},... | collective-permute-start | bytes 1572872 | tf_op jit(solution)/shard_map/ppermute | solution.py:58
  19.8 1.6 %collective-permute-start.9 = (f32[64,2048]{1,0:T(8,128)}, f32[64,2048]{1,0:T(8,128)}, u32[]{:S(2)}, u32[]{:S(2)}) collective-permute-start(f32[64,2048]{1,0:T(8,128)} %fusion.16), channel_id=1, source_target_pairs={{0,2},{2,0},{4,6},{6,4},{8,10},{10,8},{12,14},{14,12},{1,3},{3,1},... | collective-permute-start | bytes 1572872 | tf_op jit(solution)/shard_map/ppermute | solution.py:58
  28.4 2.2 %collective-permute-start.1 = (f32[64,1024]{1,0:T(8,128)S(1)}, f32[64,1024]{1,0:T(8,128)S(1)}, u32[]{:S(2)}, u32[]{:S(2)}) collective-permute-start(f32[64,1024]{1,0:T(8,128)S(1)} %fusion.24), channel_id=1, source_target_pairs={{0,4},{2,6},{4,0},{6,2},{8,12},{10,14},{12,8},{14,10},{1,5},{3,7},... | collective-permute-start | bytes 786440 | tf_op jit(solution)/shard_map/ppermute | solution.py:58
  31.8 1.6 %collective-permute-start.4 = (f32[64,1024]{1,0:T(8,128)S(1)}, f32[64,1024]{1,0:T(8,128)S(1)}, u32[]{:S(2)}, u32[]{:S(2)}) collective-permute-start(f32[64,1024]{1,0:T(8,128)S(1)} %fusion.23), channel_id=1, source_target_pairs={{0,2},{2,0},{4,6},{6,4},{8,10},{10,8},{12,14},{14,12},{1,3},{3,1},... | collective-permute-start | bytes 786440 | tf_op jit(solution)/shard_map/ppermute | solution.py:58
  33.3 4.7 %collective-permute-done.6 = f32[64,2048]{1,0:T(8,128)} collective-permute-done((f32[64,2048]{1,0:T(8,128)}, f32[64,2048]{1,0:T(8,128)}, u32[]{:S(2)}, u32[]{:S(2)}) %collective-permute-start.6) | collective-permute-done | bytes 524320 | tf_op jit(solution)/shard_map/ppermute | solution.py:58
  39.4 2.2 %collective-permute-start.7 = (f32[64,1024]{1,0:T(8,128)S(1)}, f32[64,1024]{1,0:T(8,128)S(1)}, u32[]{:S(2)}, u32[]{:S(2)}) collective-permute-start(f32[64,1024]{1,0:T(8,128)S(1)} %fusion.22), channel_id=1, source_target_pairs={{0,4},{2,6},{4,0},{6,2},{8,12},{10,14},{12,8},{14,10},{1,5},{3,7},... | collective-permute-start | bytes 786440 | tf_op jit(solution)/shard_map/ppermute | solution.py:58
  41.6 7.7 %collective-permute-done.9 = f32[64,2048]{1,0:T(8,128)} collective-permute-done((f32[64,2048]{1,0:T(8,128)}, f32[64,2048]{1,0:T(8,128)}, u32[]{:S(2)}, u32[]{:S(2)}) %collective-permute-start.9) | collective-permute-done | bytes 524320 | tf_op jit(solution)/shard_map/ppermute | solution.py:58
  50.5 2.2 %collective-permute-start.10 = (f32[64,1024]{1,0:T(8,128)S(1)}, f32[64,1024]{1,0:T(8,128)S(1)}, u32[]{:S(2)}, u32[]{:S(2)}) collective-permute-start(f32[64,1024]{1,0:T(8,128)S(1)} %fusion.21), channel_id=1, source_target_pairs={{0,4},{2,6},{4,0},{6,2},{8,12},{10,14},{12,8},{14,10},{1,5},{3,7},... | collective-permute-start | bytes 786440 | tf_op jit(solution)/shard_map/ppermute | solution.py:58
  52.8 2.6 %collective-permute-start.2 = (f32[64,512]{1,0:T(8,128)S(1)}, f32[64,512]{1,0:T(8,128)S(1)}, u32[]{:S(2)}, u32[]{:S(2)}) collective-permute-start(f32[64,512]{1,0:T(8,128)S(1)} %slice_select_fusion.3), channel_id=1, source_target_pairs={{0,8},{2,10},{4,12},{6,14},{8,0},{10,2},{12,4},{14,6},{1,9},{3,11}... | collective-permute-start | bytes 393224 | tf_op jit(solution)/shard_map/ppermute | solution.py:58
  57.1 1.6 %collective-permute-start.8 = (f32[64,512]{1,0:T(8,128)S(1)}, f32[64,512]{1,0:T(8,128)S(1)}, u32[]{:S(2)}, u32[]{:S(2)}) collective-permute-start(f32[64,512]{1,0:T(8,128)S(1)} %slice_select_fusion.1), channel_id=1, source_target_pairs={{0,8},{2,10},{4,12},{6,14},{8,0},{10,2},{12,4},{14,6},{1,9},{3,11}... | collective-permute-start | bytes 393224 | tf_op jit(solution)/shard_map/ppermute | solution.py:58
  58.7 1.7 %collective-permute-done.10 = f32[64,1024]{1,0:T(8,128)S(1)} collective-permute-done((f32[64,1024]{1,0:T(8,128)S(1)}, f32[64,1024]{1,0:T(8,128)S(1)}, u32[]{:S(2)}, u32[]{:S(2)}) %collective-permute-start.10) | collective-permute-done | bytes 262176 | tf_op jit(solution)/shard_map/ppermute | solution.py:58
  60.5 2.6 %collective-permute-start.11 = (f32[64,512]{1,0:T(8,128)S(1)}, f32[64,512]{1,0:T(8,128)S(1)}, u32[]{:S(2)}, u32[]{:S(2)}) collective-permute-start(f32[64,512]{1,0:T(8,128)S(1)} %slice_select_fusion), channel_id=1, source_target_pairs={{0,8},{2,10},{4,12},{6,14},{8,0},{10,2},{12,4},{14,6},{1,9},{3,11}... | collective-permute-start | bytes 393224 | tf_op jit(solution)/shard_map/ppermute | solution.py:58
  63.1 7.6 %collective-permute-done.2 = f32[64,512]{1,0:T(8,128)S(1)} collective-permute-done((f32[64,512]{1,0:T(8,128)S(1)}, f32[64,512]{1,0:T(8,128)S(1)}, u32[]{:S(2)}, u32[]{:S(2)}) %collective-permute-start.2) | collective-permute-done | bytes 131104 | tf_op jit(solution)/shard_map/ppermute | solution.py:58
  70.7 2.8 %collective-permute-done.5 = f32[64,512]{1,0:T(8,128)S(1)} collective-permute-done((f32[64,512]{1,0:T(8,128)S(1)}, f32[64,512]{1,0:T(8,128)S(1)}, u32[]{:S(2)}, u32[]{:S(2)}) %collective-permute-start.5) | collective-permute-done | bytes 131104 | tf_op jit(solution)/shard_map/ppermute | solution.py:58
  73.6 2.6 %collective-permute-done.8 = f32[64,512]{1,0:T(8,128)S(1)} collective-permute-done((f32[64,512]{1,0:T(8,128)S(1)}, f32[64,512]{1,0:T(8,128)S(1)}, u32[]{:S(2)}, u32[]{:S(2)}) %collective-permute-start.8) | collective-permute-done | bytes 131104 | tf_op jit(solution)/shard_map/ppermute | solution.py:58
  81.0 2.8 %collective-permute-start.13 = (f32[]{:T(128)}, f32[]{:T(128)}, u32[]{:S(2)}, u32[]{:S(2)}) collective-permute-start(f32[]{:T(128)} %add.78), channel_id=1, source_target_pairs={{0,1},{1,0},{2,3},{3,2},{4,5},{5,4},{6,7},{7,6},{8,9},{9,8},{10,11... | collective-permute-start | bytes 20 | tf_op jit(solution)/shard_map/ppermute | solution.py:33
  85.3 2.8 %collective-permute-start.14 = (f32[]{:T(128)}, f32[]{:T(128)}, u32[]{:S(2)}, u32[]{:S(2)}) collective-permute-start(f32[]{:T(128)} %add.79), channel_id=1, source_target_pairs={{0,2},{2,0},{4,6},{6,4},{8,10},{10,8},{12,14},{14,12},{1,3},{3,1},... | collective-permute-start | bytes 20 | tf_op jit(solution)/shard_map/ppermute | solution.py:33
  91.0 2.3 %collective-permute-done.15 = f32[]{:T(128)} collective-permute-done((f32[]{:T(128)}, f32[]{:T(128)}, u32[]{:S(2)}, u32[]{:S(2)}) %collective-permute-start.15) | collective-permute-done | bytes 36 | tf_op jit(solution)/shard_map/ppermute | solution.py:33
  94.0 2.0 %collective-permute-start.16 = (f32[]{:T(128)}, f32[]{:T(128)}, u32[]{:S(2)}, u32[]{:S(2)}) collective-permute-start(f32[]{:T(128)} %add.81), channel_id=1, source_target_pairs={{0,8},{2,10},{4,12},{6,14},{8,0},{10,2},{12,4},{14,6},{1,9},{3,11}... | collective-permute-start | bytes 20 | tf_op jit(solution)/shard_map/ppermute | solution.py:33
  96.1 2.6 %collective-permute-done.16 = f32[]{:T(128)} collective-permute-done((f32[]{:T(128)}, f32[]{:T(128)}, u32[]{:S(2)}, u32[]{:S(2)}) %collective-permute-start.16) | collective-permute-done | bytes 36 | tf_op jit(solution)/shard_map/ppermute | solution.py:33
  100.5 9.0 %collective-permute-done.17 = bf16[512,128]{0,1:T(8,128)(2,1)S(1)} collective-permute-done((bf16[512,128]{0,1:T(8,128)(2,1)S(1)}, bf16[512,128]{0,1:T(8,128)(2,1)S(1)}, u32[]{:S(2)}, u32[]{:S(2)}) %collective-permute-start.17) | collective-permute-done | bytes 131104 | tf_op jit(solution)/shard_map/ppermute | solution.py:72
  109.6 2.3 %collective-permute-start.18 = (bf16[2,512,128]{1,2,0:T(8,128)(2,1)S(1)}, bf16[2,512,128]{1,2,0:T(8,128)(2,1)S(1)}, u32[]{:S(2)}, u32[]{:S(2)}) collective-permute-start(bf16[2,512,128]{1,2,0:T(8,128)(2,1)S(1)} %pad_maximum_fusion.18), channel_id=1, source_target_pairs={{0,4},{2,6},{4,0},{6,2},{8,12},{10,14},{12,8},{14,10},{1,5},{3,7},... | collective-permute-start | bytes 786440 | tf_op jit(solution)/shard_map/ppermute | solution.py:72
  112.0 3.8 %collective-permute-done.20 = bf16[512,128]{0,1:T(8,128)(2,1)S(1)} collective-permute-done((bf16[512,128]{0,1:T(8,128)(2,1)S(1)}, bf16[512,128]{0,1:T(8,128)(2,1)S(1)}, u32[]{:S(2)}, u32[]{:S(2)}) %collective-permute-start.20) | collective-permute-done | bytes 131104 | tf_op jit(solution)/shard_map/ppermute | solution.py:72
  115.8 1.5 %collective-permute-start.21 = (bf16[2,512,128]{1,2,0:T(8,128)(2,1)S(1)}, bf16[2,512,128]{1,2,0:T(8,128)(2,1)S(1)}, u32[]{:S(2)}, u32[]{:S(2)}) collective-permute-start(bf16[2,512,128]{1,2,0:T(8,128)(2,1)S(1)} %pad_maximum_fusion.19), channel_id=1, source_target_pairs={{0,2},{2,0},{4,6},{6,4},{8,10},{10,8},{12,14},{14,12},{1,3},{3,1},... | collective-permute-start | bytes 786440 | tf_op jit(solution)/shard_map/ppermute | solution.py:72
  117.8 1.5 %collective-permute-start.19 = (bf16[2,2,512,128]{2,3,1,0:T(8,128)(2,1)S(1)}, bf16[2,2,512,128]{2,3,1,0:T(8,128)(2,1)S(1)}, u32[]{:S(2)}, u32[]{:S(2)}) collective-permute-start(bf16[2,2,512,128]{2,3,1,0:T(8,128)(2,1)S(1)} %pad_maximum_fusion.8), channel_id=1, source_target_pairs={{0,2},{2,0},{4,6},{6,4},{8,10},{10,8},{12,14},{14,12},{1,3},{3,1},... | collective-permute-start | bytes 1572872 | tf_op jit(solution)/shard_map/ppermute | solution.py:72
  119.3 4.1 %collective-permute-done.21 = bf16[2,512,128]{1,2,0:T(8,128)(2,1)S(1)} collective-permute-done((bf16[2,512,128]{1,2,0:T(8,128)(2,1)S(1)}, bf16[2,512,128]{1,2,0:T(8,128)(2,1)S(1)}, u32[]{:S(2)}, u32[]{:S(2)}) %collective-permute-start.21) | collective-permute-done | bytes 262176 | tf_op jit(solution)/shard_map/ppermute | solution.py:72
  124.4 4.7 %collective-permute-done.19 = bf16[2,2,512,128]{2,3,1,0:T(8,128)(2,1)S(1)} collective-permute-done((bf16[2,2,512,128]{2,3,1,0:T(8,128)(2,1)S(1)}, bf16[2,2,512,128]{2,3,1,0:T(8,128)(2,1)S(1)}, u32[]{:S(2)}, u32[]{:S(2)}) %collective-permute-start.19) | collective-permute-done | bytes 524320 | tf_op jit(solution)/shard_map/ppermute | solution.py:72
  129.9 3.8 %collective-permute-done.22 = bf16[2,2,512,128]{2,3,1,0:T(8,128)(2,1)S(1)} collective-permute-done((bf16[2,2,512,128]{2,3,1,0:T(8,128)(2,1)}, bf16[2,2,512,128]{2,3,1,0:T(8,128)(2,1)S(1)}, u32[]{:S(2)}, u32[]{:S(2)}) %collective-permute-start.22) | collective-permute-done | bytes 524320 | tf_op jit(solution)/shard_map/ppermute | solution.py:72
  134.6 1.5 %maximum_bitcast_fusion = bf16[1,4096,256]{2,1,0:T(8,128)(2,1)} fusion(bf16[4096,128]{1,0:T(8,128)(2,1)S(1)} %bitcast.75, bf16[4096,128]{1,0:T(8,128)(2,1)S(1)} %bitcast.74), kind=kLoop, calls=%fused_computation.3 | loop fusion | flops 4194304 | bytes 4194304 | tf_op jit(solution)/shard_map/broadcast_in_dim | solution.py:132
  (122 shorter events, 29.8 us)
Async XLA Ops:
  9.6 13.6 %copy-start.19 = (f32[64,512]{1,0:T(8,128)}, f32[64,512]{1,0:T(8,128)S(1)}, u32[]{:S(2)}) copy-start(f32[64,512]{1,0:T(8,128)S(1)} %get-tuple-element.5) | copy-start | bytes 393220
  9.6 13.6 %copy-start.20 = (f32[64,512]{1,0:T(8,128)}, f32[64,512]{1,0:T(8,128)S(1)}, u32[]{:S(2)}) copy-start(f32[64,512]{1,0:T(8,128)S(1)} %get-tuple-element.22) | copy-start | bytes 393220
  9.6 13.6 %copy-start.21 = (f32[64,512]{1,0:T(8,128)}, f32[64,512]{1,0:T(8,128)S(1)}, u32[]{:S(2)}) copy-start(f32[64,512]{1,0:T(8,128)S(1)} %get-tuple-element.23) | copy-start | bytes 393220
  10.8 16.0 %collective-permute-start = (f32[64,2048]{1,0:T(8,128)}, f32[64,2048]{1,0:T(8,128)}, u32[]{:S(2)}, u32[]{:S(2)}) collective-permute-start(f32[64,2048]{1,0:T(8,128)} %fusion.18), channel_id=1, source_target_pairs={{0,2},{2,0},{4,6},{6,4},{8,10},{10,8},{12,14},{14,12},{1,3},{3,1},... | collective-permute-start | bytes 1572872 | tf_op jit(solution)/shard_map/ppermute | solution.py:58
  15.9 14.6 %collective-permute-start.3 = (f32[64,2048]{1,0:T(8,128)}, f32[64,2048]{1,0:T(8,128)}, u32[]{:S(2)}, u32[]{:S(2)}) collective-permute-start(f32[64,2048]{1,0:T(8,128)} %fusion.15), channel_id=1, source_target_pairs={{0,4},{2,6},{4,0},{6,2},{8,12},{10,14},{12,8},{14,10},{1,5},{3,7},... | collective-permute-start | bytes 1572872 | tf_op jit(solution)/shard_map/ppermute | solution.py:58
  18.4 19.7 %collective-permute-start.6 = (f32[64,2048]{1,0:T(8,128)}, f32[64,2048]{1,0:T(8,128)}, u32[]{:S(2)}, u32[]{:S(2)}) collective-permute-start(f32[64,2048]{1,0:T(8,128)} %fusion.17), channel_id=1, source_target_pairs={{0,2},{2,0},{4,6},{6,4},{8,10},{10,8},{12,14},{14,12},{1,3},{3,1},... | collective-permute-start | bytes 1572872 | tf_op jit(solution)/shard_map/ppermute | solution.py:58
  19.8 29.5 %collective-permute-start.9 = (f32[64,2048]{1,0:T(8,128)}, f32[64,2048]{1,0:T(8,128)}, u32[]{:S(2)}, u32[]{:S(2)}) collective-permute-start(f32[64,2048]{1,0:T(8,128)} %fusion.16), channel_id=1, source_target_pairs={{0,2},{2,0},{4,6},{6,4},{8,10},{10,8},{12,14},{14,12},{1,3},{3,1},... | collective-permute-start | bytes 1572872 | tf_op jit(solution)/shard_map/ppermute | solution.py:58
  25.8 12.3 %copy-start.4 = (f32[64,512]{1,0:T(8,128)S(1)}, f32[64,512]{1,0:T(8,128)}, u32[]{:S(2)}) copy-start(f32[64,512]{1,0:T(8,128)} %copy-done.3) | copy-start | bytes 393220
  25.8 12.3 %copy-start.6 = (f32[64,512]{1,0:T(8,128)S(1)}, f32[64,512]{1,0:T(8,128)}, u32[]{:S(2)}) copy-start(f32[64,512]{1,0:T(8,128)} %copy-done.5) | copy-start | bytes 393220
  25.8 12.3 %copy-start.8 = (f32[64,512]{1,0:T(8,128)S(1)}, f32[64,512]{1,0:T(8,128)}, u32[]{:S(2)}) copy-start(f32[64,512]{1,0:T(8,128)} %copy-done.7) | copy-start | bytes 393220
  25.8 12.3 %copy-start.10 = (f32[64,512]{1,0:T(8,128)S(1)}, f32[64,512]{1,0:T(8,128)}, u32[]{:S(2)}) copy-start(f32[64,512]{1,0:T(8,128)} %copy-done.9) | copy-start | bytes 393220
  25.8 12.3 %copy-start.12 = (f32[64,512]{1,0:T(8,128)S(1)}, f32[64,512]{1,0:T(8,128)}, u32[]{:S(2)}) copy-start(f32[64,512]{1,0:T(8,128)} %copy-done.11) | copy-start | bytes 393220
  28.3 21.0 %copy-start.2 = (f32[64,512]{1,0:T(8,128)S(1)}, f32[64,512]{1,0:T(8,128)}, u32[]{:S(2)}) copy-start(f32[64,512]{1,0:T(8,128)} %copy-done.1) | copy-start | bytes 393220
  28.4 24.4 %collective-permute-start.1 = (f32[64,1024]{1,0:T(8,128)S(1)}, f32[64,1024]{1,0:T(8,128)S(1)}, u32[]{:S(2)}, u32[]{:S(2)}) collective-permute-start(f32[64,1024]{1,0:T(8,128)S(1)} %fusion.24), channel_id=1, source_target_pairs={{0,4},{2,6},{4,0},{6,2},{8,12},{10,14},{12,8},{14,10},{1,5},{3,7},... | collective-permute-start | bytes 786440 | tf_op jit(solution)/shard_map/ppermute | solution.py:58
  31.8 23.7 %collective-permute-start.4 = (f32[64,1024]{1,0:T(8,128)S(1)}, f32[64,1024]{1,0:T(8,128)S(1)}, u32[]{:S(2)}, u32[]{:S(2)}) collective-permute-start(f32[64,1024]{1,0:T(8,128)S(1)} %fusion.23), channel_id=1, source_target_pairs={{0,2},{2,0},{4,6},{6,4},{8,10},{10,8},{12,14},{14,12},{1,3},{3,1},... | collective-permute-start | bytes 786440 | tf_op jit(solution)/shard_map/ppermute | solution.py:58
  39.4 17.6 %collective-permute-start.7 = (f32[64,1024]{1,0:T(8,128)S(1)}, f32[64,1024]{1,0:T(8,128)S(1)}, u32[]{:S(2)}, u32[]{:S(2)}) collective-permute-start(f32[64,1024]{1,0:T(8,128)S(1)} %fusion.22), channel_id=1, source_target_pairs={{0,4},{2,6},{4,0},{6,2},{8,12},{10,14},{12,8},{14,10},{1,5},{3,7},... | collective-permute-start | bytes 786440 | tf_op jit(solution)/shard_map/ppermute | solution.py:58
  50.5 9.9 %collective-permute-start.10 = (f32[64,1024]{1,0:T(8,128)S(1)}, f32[64,1024]{1,0:T(8,128)S(1)}, u32[]{:S(2)}, u32[]{:S(2)}) collective-permute-start(f32[64,1024]{1,0:T(8,128)S(1)} %fusion.21), channel_id=1, source_target_pairs={{0,4},{2,6},{4,0},{6,2},{8,12},{10,14},{12,8},{14,10},{1,5},{3,7},... | collective-permute-start | bytes 786440 | tf_op jit(solution)/shard_map/ppermute | solution.py:58
  52.8 17.9 %collective-permute-start.2 = (f32[64,512]{1,0:T(8,128)S(1)}, f32[64,512]{1,0:T(8,128)S(1)}, u32[]{:S(2)}, u32[]{:S(2)}) collective-permute-start(f32[64,512]{1,0:T(8,128)S(1)} %slice_select_fusion.3), channel_id=1, source_target_pairs={{0,8},{2,10},{4,12},{6,14},{8,0},{10,2},{12,4},{14,6},{1,9},{3,11}... | collective-permute-start | bytes 393224 | tf_op jit(solution)/shard_map/ppermute | solution.py:58
  55.5 18.0 %collective-permute-start.5 = (f32[64,512]{1,0:T(8,128)S(1)}, f32[64,512]{1,0:T(8,128)S(1)}, u32[]{:S(2)}, u32[]{:S(2)}) collective-permute-start(f32[64,512]{1,0:T(8,128)S(1)} %slice_select_fusion.2), channel_id=1, source_target_pairs={{0,8},{2,10},{4,12},{6,14},{8,0},{10,2},{12,4},{14,6},{1,9},{3,11}... | collective-permute-start | bytes 393224 | tf_op jit(solution)/shard_map/ppermute | solution.py:58
  57.1 19.1 %collective-permute-start.8 = (f32[64,512]{1,0:T(8,128)S(1)}, f32[64,512]{1,0:T(8,128)S(1)}, u32[]{:S(2)}, u32[]{:S(2)}) collective-permute-start(f32[64,512]{1,0:T(8,128)S(1)} %slice_select_fusion.1), channel_id=1, source_target_pairs={{0,8},{2,10},{4,12},{6,14},{8,0},{10,2},{12,4},{14,6},{1,9},{3,11}... | collective-permute-start | bytes 393224 | tf_op jit(solution)/shard_map/ppermute | solution.py:58
  60.5 17.0 %collective-permute-start.11 = (f32[64,512]{1,0:T(8,128)S(1)}, f32[64,512]{1,0:T(8,128)S(1)}, u32[]{:S(2)}, u32[]{:S(2)}) collective-permute-start(f32[64,512]{1,0:T(8,128)S(1)} %slice_select_fusion), channel_id=1, source_target_pairs={{0,8},{2,10},{4,12},{6,14},{8,0},{10,2},{12,4},{14,6},{1,9},{3,11}... | collective-permute-start | bytes 393224 | tf_op jit(solution)/shard_map/ppermute | solution.py:58
  78.3 1.4 %collective-permute-start.12 = (f32[]{:T(128)}, f32[]{:T(128)}, u32[]{:S(2)}, u32[]{:S(2)}) collective-permute-start(f32[]{:T(128)} %multiply_reduce_fusion), channel_id=1, source_target_pairs={{0,16},{16,0},{1,17},{17,1},{2,18},{18,2},{3,19},{19,3},{4,20},{20... | collective-permute-start | bytes 20 | tf_op jit(solution)/shard_map/ppermute | solution.py:33
  81.0 3.7 %collective-permute-start.13 = (f32[]{:T(128)}, f32[]{:T(128)}, u32[]{:S(2)}, u32[]{:S(2)}) collective-permute-start(f32[]{:T(128)} %add.78), channel_id=1, source_target_pairs={{0,1},{1,0},{2,3},{3,2},{4,5},{5,4},{6,7},{7,6},{8,9},{9,8},{10,11... | collective-permute-start | bytes 20 | tf_op jit(solution)/shard_map/ppermute | solution.py:33
  85.3 3.7 %collective-permute-start.14 = (f32[]{:T(128)}, f32[]{:T(128)}, u32[]{:S(2)}, u32[]{:S(2)}) collective-permute-start(f32[]{:T(128)} %add.79), channel_id=1, source_target_pairs={{0,2},{2,0},{4,6},{6,4},{8,10},{10,8},{12,14},{14,12},{1,3},{3,1},... | collective-permute-start | bytes 20 | tf_op jit(solution)/shard_map/ppermute | solution.py:33
  89.7 3.7 %collective-permute-start.15 = (f32[]{:T(128)}, f32[]{:T(128)}, u32[]{:S(2)}, u32[]{:S(2)}) collective-permute-start(f32[]{:T(128)} %add.80), channel_id=1, source_target_pairs={{0,4},{2,6},{4,0},{6,2},{8,12},{10,14},{12,8},{14,10},{1,5},{3,7},... | collective-permute-start | bytes 20 | tf_op jit(solution)/shard_map/ppermute | solution.py:33
  94.0 4.7 %collective-permute-start.16 = (f32[]{:T(128)}, f32[]{:T(128)}, u32[]{:S(2)}, u32[]{:S(2)}) collective-permute-start(f32[]{:T(128)} %add.81), channel_id=1, source_target_pairs={{0,8},{2,10},{4,12},{6,14},{8,0},{10,2},{12,4},{14,6},{1,9},{3,11}... | collective-permute-start | bytes 20 | tf_op jit(solution)/shard_map/ppermute | solution.py:33
  99.8 9.6 %collective-permute-start.17 = (bf16[512,128]{0,1:T(8,128)(2,1)S(1)}, bf16[512,128]{0,1:T(8,128)(2,1)S(1)}, u32[]{:S(2)}, u32[]{:S(2)}) collective-permute-start(bf16[512,128]{0,1:T(8,128)(2,1)S(1)} %slice.312), channel_id=1, source_target_pairs={{0,8},{2,10},{4,12},{6,14},{8,0},{10,2},{12,4},{14,6},{1,9},{3,11}... | collective-permute-start | bytes 393224 | tf_op jit(solution)/shard_map/ppermute | solution.py:72
  109.5 6.2 %collective-permute-start.20 = (bf16[512,128]{0,1:T(8,128)(2,1)S(1)}, bf16[512,128]{0,1:T(8,128)(2,1)S(1)}, u32[]{:S(2)}, u32[]{:S(2)}) collective-permute-start(bf16[512,128]{0,1:T(8,128)(2,1)S(1)} %get-tuple-element.61), channel_id=1, source_target_pairs={{0,8},{2,10},{4,12},{6,14},{8,0},{10,2},{12,4},{14,6},{1,9},{3,11}... | collective-permute-start | bytes 393224 | tf_op jit(solution)/shard_map/ppermute | solution.py:72
  109.6 8.1 %collective-permute-start.18 = (bf16[2,512,128]{1,2,0:T(8,128)(2,1)S(1)}, bf16[2,512,128]{1,2,0:T(8,128)(2,1)S(1)}, u32[]{:S(2)}, u32[]{:S(2)}) collective-permute-start(bf16[2,512,128]{1,2,0:T(8,128)(2,1)S(1)} %pad_maximum_fusion.18), channel_id=1, source_target_pairs={{0,4},{2,6},{4,0},{6,2},{8,12},{10,14},{12,8},{14,10},{1,5},{3,7},... | collective-permute-start | bytes 786440 | tf_op jit(solution)/shard_map/ppermute | solution.py:72
  115.8 7.7 %collective-permute-start.21 = (bf16[2,512,128]{1,2,0:T(8,128)(2,1)S(1)}, bf16[2,512,128]{1,2,0:T(8,128)(2,1)S(1)}, u32[]{:S(2)}, u32[]{:S(2)}) collective-permute-start(bf16[2,512,128]{1,2,0:T(8,128)(2,1)S(1)} %pad_maximum_fusion.19), channel_id=1, source_target_pairs={{0,2},{2,0},{4,6},{6,4},{8,10},{10,8},{12,14},{14,12},{1,3},{3,1},... | collective-permute-start | bytes 786440 | tf_op jit(solution)/shard_map/ppermute | solution.py:72
  117.8 11.3 %collective-permute-start.19 = (bf16[2,2,512,128]{2,3,1,0:T(8,128)(2,1)S(1)}, bf16[2,2,512,128]{2,3,1,0:T(8,128)(2,1)S(1)}, u32[]{:S(2)}, u32[]{:S(2)}) collective-permute-start(bf16[2,2,512,128]{2,3,1,0:T(8,128)(2,1)S(1)} %pad_maximum_fusion.8), channel_id=1, source_target_pairs={{0,2},{2,0},{4,6},{6,4},{8,10},{10,8},{12,14},{14,12},{1,3},{3,1},... | collective-permute-start | bytes 1572872 | tf_op jit(solution)/shard_map/ppermute | solution.py:72
  124.4 9.4 %collective-permute-start.22 = (bf16[2,2,512,128]{2,3,1,0:T(8,128)(2,1)}, bf16[2,2,512,128]{2,3,1,0:T(8,128)(2,1)S(1)}, u32[]{:S(2)}, u32[]{:S(2)}) collective-permute-start(bf16[2,2,512,128]{2,3,1,0:T(8,128)(2,1)} %pad_maximum_fusion.9), channel_id=1, source_target_pairs={{0,4},{2,6},{4,0},{6,2},{8,12},{10,14},{12,8},{14,10},{1,5},{3,7},... | collective-permute-start | bytes 1572872 | tf_op jit(solution)/shard_map/ppermute | solution.py:72
  (18 other events, 150.9 us)

commit v10 on v6

--- a/solution.py
+++ b/solution.py
@@ -24,7 +24,7 @@
 def butterfly_sum(value, axes):
     for axis in axes:
         size = lax.axis_size(axis)
-        if size & (size - 1):
+        if size & (size - 1) or axis == "pipe":
             value = lax.psum(value, axis)
             continue
         bit = 1

time: 131 us -> 134 us (1.023)
  blocking collectives: 0 us -> 3.11 us
  waiting for transfers between devices: 64.5 us -> 66.7 us
  starting transfers between devices: 30.7 us -> 29.3 us
    psum x0 -> x1, blocking collectives: none -> 3.11 us  [butterfly_sum(): value = lax.psum(value, axis)]
    ppermute x12, waiting for transfers between devices: 29.9 us -> 32.1 us  [halving_scatter(): blocks = keep + lax.ppermute(send, axis, pairs)]
    ppermute x5 -> x4, starting transfers between devices: 8.59 us -> 7.24 us  [butterfly_sum(): value = value + lax.ppermute(value, axis, pairs)]
    unnamed x43 -> x41, local copies, waits for them, and re-layouts: 6.54 us -> 5.75 us
    ppermute x5 -> x4, waiting for transfers between devices: 7.85 us -> 7.95 us  [butterfly_sum(): value = value + lax.ppermute(value, axis, pairs)]
  transfers between devices with their start and end apart: 23 -> 22, of which waited for: 20 -> 19; matrix products, arithmetic and copies ran while one was open for 12% -> 11% of each run, Pallas kernels for 0% -> 0%
where the time goes in v10:
time: 134 us; the launch traced here: 133 us
  waiting for transfers between devices  66.7 us (50%)
  starting transfers between devices  29.3 us (22%)
  other arithmetic  14.5 us (11%)
  local copies, waits for them, and re-layouts  9.09 us (7%)
  matrix products  6.18 us (5%)
  between operations  4.48 us (3%)
  blocking collectives  3.11 us (2%)
    ppermute x12, waiting for transfers between devices, halving_scatter(): blocks = keep + lax.ppermute(send, axis, pairs)  32.1 us
    ppermute x6, waiting for transfers between devices, doubling_gather(): other = lax.ppermute(current, axis, pairs)  26.7 us
    ppermute x12, starting transfers between devices, halving_scatter(): blocks = keep + lax.ppermute(send, axis, pairs)  16.7 us
    ppermute x4, waiting for transfers between devices, butterfly_sum(): value = value + lax.ppermute(value, axis, pairs)  7.95 us
    ppermute x4, starting transfers between devices, butterfly_sum(): value = value + lax.ppermute(value, axis, pairs)  7.24 us
    dot_general x1, matrix products, slot_term(): lax.dot_general(weighted, columns, (((0,), (0,)), ((), ())), preferred_el...  6.18 us
    unnamed x41, local copies, waits for them, and re-layouts  5.75 us
    ppermute x6, starting transfers between devices, doubling_gather(): other = lax.ppermute(current, axis, pairs)  5.41 us
  transfers between devices with their start and end apart: 22, of which 19 were waited for; matrix products, arithmetic and copies ran while one was open for 11% of the time, Pallas kernels for 0%

profile of v10, /device:TPU:0, one launch (start us, length us, event | category | flops | bytes accessed | tf_op | source)
XLA Modules:
  0.0 133.3 jit_solution(14633539032516352005)
XLA Ops:
  1.4 6.2 %fusion.2 = f32[256,4096]{1,0:T(8,128)S(1)} fusion(bf16[1,8,128,4096]{3,2,1,0:T(8,128)(2,1)} %param.6, bf16[1,8,128,256]{3,2,1,0:T(8,128)(2,1)} %param.7, bf16[8]{0:T(256)(128)(2,1)S(1)} %get-tuple-element.58), kind=kOutput, calls=%fused_computation.2 | convolution fusion | flops 2147745792 | bytes 13107216 | tf_op jit(solution)/shard_map/dot_general | solution.py:19
  7.6 2.0 %copy-done = f32[256,4096]{1,0:T(8,128)} copy-done((f32[256,4096]{1,0:T(8,128)}, f32[256,4096]{1,0:T(8,128)S(1)}, u32[]{:S(2)}) %copy-start) | copy-done | bytes 4194328
  10.9 2.9 %collective-permute-start = (f32[64,2048]{1,0:T(8,128)}, f32[64,2048]{1,0:T(8,128)}, u32[]{:S(2)}, u32[]{:S(2)}) collective-permute-start(f32[64,2048]{1,0:T(8,128)} %fusion.18), channel_id=1, source_target_pairs={{0,2},{2,0},{4,6},{6,4},{8,10},{10,8},{12,14},{14,12},{1,3},{3,1},... | collective-permute-start | bytes 1572872 | tf_op jit(solution)/shard_map/ppermute | solution.py:58
  13.9 1.6 %fusion.26 = (f32[64,1024]{1,0:T(8,128)S(1)}, f32[64,1024]{1,0:T(8,128)S(1)}, f32[64,1024]{1,0:T(8,128)S(1)}, f32[64,1024]{1,0:T(8,128)S(1)}, f32[64,1024]{1,0:T...) fusion(f32[256,4096]{1,0:T(8,128)} %copy-done), kind=kLoop, calls=%fused_computation.80 | loop fusion | bytes 4194304 | tf_op jit(solution)/shard_map/slice | solution.py:54
  16.4 1.6 %collective-permute-start.3 = (f32[64,2048]{1,0:T(8,128)}, f32[64,2048]{1,0:T(8,128)}, u32[]{:S(2)}, u32[]{:S(2)}) collective-permute-start(f32[64,2048]{1,0:T(8,128)} %fusion.16), channel_id=1, source_target_pairs={{0,4},{2,6},{4,0},{6,2},{8,12},{10,14},{12,8},{14,10},{1,5},{3,7},... | collective-permute-start | bytes 1572872 | tf_op jit(solution)/shard_map/ppermute | solution.py:58
  23.5 3.5 %collective-permute-done = f32[64,2048]{1,0:T(8,128)} collective-permute-done((f32[64,2048]{1,0:T(8,128)}, f32[64,2048]{1,0:T(8,128)}, u32[]{:S(2)}, u32[]{:S(2)}) %collective-permute-start) | collective-permute-done | bytes 524320 | tf_op jit(solution)/shard_map/ppermute | solution.py:58
  26.9 1.4 %select_add_fusion.3 = f32[64,2048]{1,0:T(8,128)S(1)} fusion(f32[64,2048]{1,0:T(8,128)} %collective-permute-done, f32[64,512]{1,0:T(8,128)} %copy-done.12, f32[64,512]{1,0:T(8,128)} %copy-done.13, f32[64,512]{1,0:T(8,128)} %copy-done.14, f32[64,512]{1,0:T(8,128)} %copy-done.15, f32[64,512]{1,0:T(8,128)} %copy-done.16, f32[64,512]{1,0:T(8,128)} %copy-done.17, ...), kind=kLoop, calls=%fused_computation.35 | loop fusion | flops 1048576 | bytes 2097153 | tf_op jit(solution)/shard_map/add | solution.py:58
  28.4 2.2 %collective-permute-start.1 = (f32[64,1024]{1,0:T(8,128)S(1)}, f32[64,1024]{1,0:T(8,128)S(1)}, u32[]{:S(2)}, u32[]{:S(2)}) collective-permute-start(f32[64,1024]{1,0:T(8,128)S(1)} %fusion.24), channel_id=1, source_target_pairs={{0,4},{2,6},{4,0},{6,2},{8,12},{10,14},{12,8},{14,10},{1,5},{3,7},... | collective-permute-start | bytes 786440 | tf_op jit(solution)/shard_map/ppermute | solution.py:58
  33.4 4.7 %collective-permute-done.6 = f32[64,2048]{1,0:T(8,128)} collective-permute-done((f32[64,2048]{1,0:T(8,128)}, f32[64,2048]{1,0:T(8,128)}, u32[]{:S(2)}, u32[]{:S(2)}) %collective-permute-start.6) | collective-permute-done | bytes 524320 | tf_op jit(solution)/shard_map/ppermute | solution.py:58
  39.4 2.2 %collective-permute-start.7 = (f32[64,1024]{1,0:T(8,128)S(1)}, f32[64,1024]{1,0:T(8,128)S(1)}, u32[]{:S(2)}, u32[]{:S(2)}) collective-permute-start(f32[64,1024]{1,0:T(8,128)S(1)} %fusion.22), channel_id=1, source_target_pairs={{0,4},{2,6},{4,0},{6,2},{8,12},{10,14},{12,8},{14,10},{1,5},{3,7},... | collective-permute-start | bytes 786440 | tf_op jit(solution)/shard_map/ppermute | solution.py:58
  44.4 3.9 %collective-permute-done.1 = f32[64,1024]{1,0:T(8,128)S(1)} collective-permute-done((f32[64,1024]{1,0:T(8,128)S(1)}, f32[64,1024]{1,0:T(8,128)S(1)}, u32[]{:S(2)}, u32[]{:S(2)}) %collective-permute-start.1) | collective-permute-done | bytes 262176 | tf_op jit(solution)/shard_map/ppermute | solution.py:58
  48.4 2.7 %collective-permute-start.2 = (f32[64,512]{1,0:T(8,128)S(1)}, f32[64,512]{1,0:T(8,128)S(1)}, u32[]{:S(2)}, u32[]{:S(2)}) collective-permute-start(f32[64,512]{1,0:T(8,128)S(1)} %slice_select_fusion.3), channel_id=1, source_target_pairs={{0,8},{2,10},{4,12},{6,14},{8,0},{10,2},{12,4},{14,6},{1,9},{3,11}... | collective-permute-start | bytes 393224 | tf_op jit(solution)/shard_map/ppermute | solution.py:58
  51.5 5.3 %collective-permute-done.7 = f32[64,1024]{1,0:T(8,128)S(1)} collective-permute-done((f32[64,1024]{1,0:T(8,128)S(1)}, f32[64,1024]{1,0:T(8,128)S(1)}, u32[]{:S(2)}, u32[]{:S(2)}) %collective-permute-start.7) | collective-permute-done | bytes 262176 | tf_op jit(solution)/shard_map/ppermute | solution.py:58
  57.6 2.5 %collective-permute-start.11 = (f32[64,512]{1,0:T(8,128)S(1)}, f32[64,512]{1,0:T(8,128)S(1)}, u32[]{:S(2)}, u32[]{:S(2)}) collective-permute-start(f32[64,512]{1,0:T(8,128)S(1)} %slice_select_fusion), channel_id=1, source_target_pairs={{0,8},{2,10},{4,12},{6,14},{8,0},{10,2},{12,4},{14,6},{1,9},{3,11}... | collective-permute-start | bytes 393224 | tf_op jit(solution)/shard_map/ppermute | solution.py:58
  60.1 8.2 %collective-permute-done.5 = f32[64,512]{1,0:T(8,128)S(1)} collective-permute-done((f32[64,512]{1,0:T(8,128)S(1)}, f32[64,512]{1,0:T(8,128)S(1)}, u32[]{:S(2)}, u32[]{:S(2)}) %collective-permute-start.5) | collective-permute-done | bytes 131104 | tf_op jit(solution)/shard_map/ppermute | solution.py:58
  68.3 2.8 %collective-permute-done.8 = f32[64,512]{1,0:T(8,128)S(1)} collective-permute-done((f32[64,512]{1,0:T(8,128)S(1)}, f32[64,512]{1,0:T(8,128)S(1)}, u32[]{:S(2)}, u32[]{:S(2)}) %collective-permute-start.8) | collective-permute-done | bytes 131104 | tf_op jit(solution)/shard_map/ppermute | solution.py:58
  71.1 1.6 %collective-permute-done.11 = f32[64,512]{1,0:T(8,128)S(1)} collective-permute-done((f32[64,512]{1,0:T(8,128)S(1)}, f32[64,512]{1,0:T(8,128)S(1)}, u32[]{:S(2)}, u32[]{:S(2)}) %collective-permute-start.11) | collective-permute-done | bytes 131104 | tf_op jit(solution)/shard_map/ppermute | solution.py:58
  74.7 3.1 %psum.7 = f32[]{:T(128)} all-reduce(f32[]{:T(128)} %multiply_reduce_fusion), channel_id=1, replica_groups=mesh['pipe'=2,'dp'=8,'tensor'=2] {'pipe'}, use_global_device_ids=true, to_apply=%region_2.3 | all-reduce | flops 1 | bytes 8 | tf_op jit(solution)/shard_map/psum | solution.py:28
  77.8 1.5 %collective-permute-start.12 = (f32[]{:T(128)}, f32[]{:T(128)}, u32[]{:S(2)}, u32[]{:S(2)}) collective-permute-start(f32[]{:T(128)} %psum.7), channel_id=1, source_target_pairs={{0,1},{1,0},{2,3},{3,2},{4,5},{5,4},{6,7},{7,6},{8,9},{9,8},{10,11... | collective-permute-start | bytes 20 | tf_op jit(solution)/shard_map/ppermute | solution.py:33
  79.3 2.1 %collective-permute-done.12 = f32[]{:T(128)} collective-permute-done((f32[]{:T(128)}, f32[]{:T(128)}, u32[]{:S(2)}, u32[]{:S(2)}) %collective-permute-start.12) | collective-permute-done | bytes 36 | tf_op jit(solution)/shard_map/ppermute | solution.py:33
  82.8 1.9 %collective-permute-start.13 = (f32[]{:T(128)}, f32[]{:T(128)}, u32[]{:S(2)}, u32[]{:S(2)}) collective-permute-start(f32[]{:T(128)} %add.77), channel_id=1, source_target_pairs={{0,2},{2,0},{4,6},{6,4},{8,10},{10,8},{12,14},{14,12},{1,3},{3,1},... | collective-permute-start | bytes 20 | tf_op jit(solution)/shard_map/ppermute | solution.py:33
  84.7 1.7 %collective-permute-done.13 = f32[]{:T(128)} collective-permute-done((f32[]{:T(128)}, f32[]{:T(128)}, u32[]{:S(2)}, u32[]{:S(2)}) %collective-permute-start.13) | collective-permute-done | bytes 36 | tf_op jit(solution)/shard_map/ppermute | solution.py:33
  88.4 2.2 %collective-permute-done.14 = f32[]{:T(128)} collective-permute-done((f32[]{:T(128)}, f32[]{:T(128)}, u32[]{:S(2)}, u32[]{:S(2)}) %collective-permute-start.14) | collective-permute-done | bytes 36 | tf_op jit(solution)/shard_map/ppermute | solution.py:33
  91.2 2.5 %collective-permute-start.15 = (f32[]{:T(128)}, f32[]{:T(128)}, u32[]{:S(2)}, u32[]{:S(2)}) collective-permute-start(f32[]{:T(128)} %add.79), channel_id=1, source_target_pairs={{0,8},{2,10},{4,12},{6,14},{8,0},{10,2},{12,4},{14,6},{1,9},{3,11}... | collective-permute-start | bytes 20 | tf_op jit(solution)/shard_map/ppermute | solution.py:33
  93.7 2.0 %collective-permute-done.15 = f32[]{:T(128)} collective-permute-done((f32[]{:T(128)}, f32[]{:T(128)}, u32[]{:S(2)}, u32[]{:S(2)}) %collective-permute-start.15) | collective-permute-done | bytes 36 | tf_op jit(solution)/shard_map/ppermute | solution.py:33
  98.0 8.6 %collective-permute-done.16 = bf16[512,128]{0,1:T(8,128)(2,1)S(1)} collective-permute-done((bf16[512,128]{0,1:T(8,128)(2,1)S(1)}, bf16[512,128]{0,1:T(8,128)(2,1)S(1)}, u32[]{:S(2)}, u32[]{:S(2)}) %collective-permute-start.16) | collective-permute-done | bytes 131104 | tf_op jit(solution)/shard_map/ppermute | solution.py:72
  106.8 3.0 %collective-permute-start.17 = (bf16[2,512,128]{1,2,0:T(8,128)(2,1)S(1)}, bf16[2,512,128]{1,2,0:T(8,128)(2,1)S(1)}, u32[]{:S(2)}, u32[]{:S(2)}) collective-permute-start(bf16[2,512,128]{1,2,0:T(8,128)(2,1)S(1)} %pad_maximum_fusion.18), channel_id=1, source_target_pairs={{0,4},{2,6},{4,0},{6,2},{8,12},{10,14},{12,8},{14,10},{1,5},{3,7},... | collective-permute-start | bytes 786440 | tf_op jit(solution)/shard_map/ppermute | solution.py:72
  109.8 3.8 %collective-permute-done.19 = bf16[512,128]{0,1:T(8,128)(2,1)S(1)} collective-permute-done((bf16[512,128]{0,1:T(8,128)(2,1)S(1)}, bf16[512,128]{0,1:T(8,128)(2,1)S(1)}, u32[]{:S(2)}, u32[]{:S(2)}) %collective-permute-start.19) | collective-permute-done | bytes 131104 | tf_op jit(solution)/shard_map/ppermute | solution.py:72
  116.2 4.4 %collective-permute-done.20 = bf16[2,512,128]{1,2,0:T(8,128)(2,1)S(1)} collective-permute-done((bf16[2,512,128]{1,2,0:T(8,128)(2,1)S(1)}, bf16[2,512,128]{1,2,0:T(8,128)(2,1)S(1)}, u32[]{:S(2)}, u32[]{:S(2)}) %collective-permute-start.20) | collective-permute-done | bytes 262176 | tf_op jit(solution)/shard_map/ppermute | solution.py:72
  121.6 4.7 %collective-permute-done.18 = bf16[2,2,512,128]{2,3,1,0:T(8,128)(2,1)S(1)} collective-permute-done((bf16[2,2,512,128]{2,3,1,0:T(8,128)(2,1)S(1)}, bf16[2,2,512,128]{2,3,1,0:T(8,128)(2,1)S(1)}, u32[]{:S(2)}, u32[]{:S(2)}) %collective-permute-start.18) | collective-permute-done | bytes 524320 | tf_op jit(solution)/shard_map/ppermute | solution.py:72
  127.1 3.8 %collective-permute-done.21 = bf16[2,2,512,128]{2,3,1,0:T(8,128)(2,1)S(1)} collective-permute-done((bf16[2,2,512,128]{2,3,1,0:T(8,128)(2,1)}, bf16[2,2,512,128]{2,3,1,0:T(8,128)(2,1)S(1)}, u32[]{:S(2)}, u32[]{:S(2)}) %collective-permute-start.21) | collective-permute-done | bytes 524320 | tf_op jit(solution)/shard_map/ppermute | solution.py:72
  131.8 1.5 %maximum_bitcast_fusion = bf16[1,4096,256]{2,1,0:T(8,128)(2,1)} fusion(bf16[4096,128]{1,0:T(8,128)(2,1)S(1)} %bitcast.75, bf16[4096,128]{1,0:T(8,128)(2,1)S(1)} %bitcast.74), kind=kLoop, calls=%fused_computation.3 | loop fusion | flops 4194304 | bytes 4194304 | tf_op jit(solution)/shard_map/broadcast_in_dim | solution.py:132
  (104 shorter events, 26.8 us)
Async XLA Ops:
  9.8 9.1 %copy-start.1 = (f32[64,512]{1,0:T(8,128)}, f32[64,512]{1,0:T(8,128)S(1)}, u32[]{:S(2)}) copy-start(f32[64,512]{1,0:T(8,128)S(1)} %get-tuple-element.9) | copy-start | bytes 393220
  9.8 9.1 %copy-start.3 = (f32[64,512]{1,0:T(8,128)}, f32[64,512]{1,0:T(8,128)S(1)}, u32[]{:S(2)}) copy-start(f32[64,512]{1,0:T(8,128)S(1)} %get-tuple-element.10) | copy-start | bytes 393220
  9.8 11.1 %copy-start.11 = (f32[64,512]{1,0:T(8,128)}, f32[64,512]{1,0:T(8,128)S(1)}, u32[]{:S(2)}) copy-start(f32[64,512]{1,0:T(8,128)S(1)} %get-tuple-element.5) | copy-start | bytes 393220
  9.8 11.1 %copy-start.12 = (f32[64,512]{1,0:T(8,128)}, f32[64,512]{1,0:T(8,128)S(1)}, u32[]{:S(2)}) copy-start(f32[64,512]{1,0:T(8,128)S(1)} %get-tuple-element.14) | copy-start | bytes 393220
  9.8 11.1 %copy-start.13 = (f32[64,512]{1,0:T(8,128)}, f32[64,512]{1,0:T(8,128)S(1)}, u32[]{:S(2)}) copy-start(f32[64,512]{1,0:T(8,128)S(1)} %get-tuple-element.15) | copy-start | bytes 393220
  10.9 16.0 %collective-permute-start = (f32[64,2048]{1,0:T(8,128)}, f32[64,2048]{1,0:T(8,128)}, u32[]{:S(2)}, u32[]{:S(2)}) collective-permute-start(f32[64,2048]{1,0:T(8,128)} %fusion.18), channel_id=1, source_target_pairs={{0,2},{2,0},{4,6},{6,4},{8,10},{10,8},{12,14},{14,12},{1,3},{3,1},... | collective-permute-start | bytes 1572872 | tf_op jit(solution)/shard_map/ppermute | solution.py:58
  16.4 15.2 %collective-permute-start.3 = (f32[64,2048]{1,0:T(8,128)}, f32[64,2048]{1,0:T(8,128)}, u32[]{:S(2)}, u32[]{:S(2)}) collective-permute-start(f32[64,2048]{1,0:T(8,128)} %fusion.16), channel_id=1, source_target_pairs={{0,4},{2,6},{4,0},{6,2},{8,12},{10,14},{12,8},{14,10},{1,5},{3,7},... | collective-permute-start | bytes 1572872 | tf_op jit(solution)/shard_map/ppermute | solution.py:58
  18.9 19.3 %collective-permute-start.6 = (f32[64,2048]{1,0:T(8,128)}, f32[64,2048]{1,0:T(8,128)}, u32[]{:S(2)}, u32[]{:S(2)}) collective-permute-start(f32[64,2048]{1,0:T(8,128)} %fusion.17), channel_id=1, source_target_pairs={{0,2},{2,0},{4,6},{6,4},{8,10},{10,8},{12,14},{14,12},{1,3},{3,1},... | collective-permute-start | bytes 1572872 | tf_op jit(solution)/shard_map/ppermute | solution.py:58
  20.3 22.5 %collective-permute-start.9 = (f32[64,2048]{1,0:T(8,128)}, f32[64,2048]{1,0:T(8,128)}, u32[]{:S(2)}, u32[]{:S(2)}) collective-permute-start(f32[64,2048]{1,0:T(8,128)} %fusion.15), channel_id=1, source_target_pairs={{0,4},{2,6},{4,0},{6,2},{8,12},{10,14},{12,8},{14,10},{1,5},{3,7},... | collective-permute-start | bytes 1572872 | tf_op jit(solution)/shard_map/ppermute | solution.py:58
  23.4 14.8 %copy-start.2 = (f32[64,512]{1,0:T(8,128)S(1)}, f32[64,512]{1,0:T(8,128)}, u32[]{:S(2)}) copy-start(f32[64,512]{1,0:T(8,128)} %copy-done.1) | copy-start | bytes 393220
  23.4 14.8 %copy-start.4 = (f32[64,512]{1,0:T(8,128)S(1)}, f32[64,512]{1,0:T(8,128)}, u32[]{:S(2)}) copy-start(f32[64,512]{1,0:T(8,128)} %copy-done.3) | copy-start | bytes 393220
  23.4 14.7 %copy-start.6 = (f32[64,512]{1,0:T(8,128)S(1)}, f32[64,512]{1,0:T(8,128)}, u32[]{:S(2)}) copy-start(f32[64,512]{1,0:T(8,128)} %copy-done.5) | copy-start | bytes 393220
  23.4 14.7 %copy-start.8 = (f32[64,512]{1,0:T(8,128)S(1)}, f32[64,512]{1,0:T(8,128)}, u32[]{:S(2)}) copy-start(f32[64,512]{1,0:T(8,128)} %copy-done.7) | copy-start | bytes 393220
  23.4 14.7 %copy-start.10 = (f32[64,512]{1,0:T(8,128)S(1)}, f32[64,512]{1,0:T(8,128)}, u32[]{:S(2)}) copy-start(f32[64,512]{1,0:T(8,128)} %copy-done.9) | copy-start | bytes 393220
  28.4 19.9 %collective-permute-start.1 = (f32[64,1024]{1,0:T(8,128)S(1)}, f32[64,1024]{1,0:T(8,128)S(1)}, u32[]{:S(2)}, u32[]{:S(2)}) collective-permute-start(f32[64,1024]{1,0:T(8,128)S(1)} %fusion.24), channel_id=1, source_target_pairs={{0,4},{2,6},{4,0},{6,2},{8,12},{10,14},{12,8},{14,10},{1,5},{3,7},... | collective-permute-start | bytes 786440 | tf_op jit(solution)/shard_map/ppermute | solution.py:58
  32.8 18.3 %collective-permute-start.4 = (f32[64,1024]{1,0:T(8,128)S(1)}, f32[64,1024]{1,0:T(8,128)S(1)}, u32[]{:S(2)}, u32[]{:S(2)}) collective-permute-start(f32[64,1024]{1,0:T(8,128)S(1)} %fusion.23), channel_id=1, source_target_pairs={{0,2},{2,0},{4,6},{6,4},{8,10},{10,8},{12,14},{14,12},{1,3},{3,1},... | collective-permute-start | bytes 786440 | tf_op jit(solution)/shard_map/ppermute | solution.py:58
  39.4 17.4 %collective-permute-start.7 = (f32[64,1024]{1,0:T(8,128)S(1)}, f32[64,1024]{1,0:T(8,128)S(1)}, u32[]{:S(2)}, u32[]{:S(2)}) collective-permute-start(f32[64,1024]{1,0:T(8,128)S(1)} %fusion.22), channel_id=1, source_target_pairs={{0,4},{2,6},{4,0},{6,2},{8,12},{10,14},{12,8},{14,10},{1,5},{3,7},... | collective-permute-start | bytes 786440 | tf_op jit(solution)/shard_map/ppermute | solution.py:58
  44.0 13.4 %collective-permute-start.10 = (f32[64,1024]{1,0:T(8,128)S(1)}, f32[64,1024]{1,0:T(8,128)S(1)}, u32[]{:S(2)}, u32[]{:S(2)}) collective-permute-start(f32[64,1024]{1,0:T(8,128)S(1)} %fusion.21), channel_id=1, source_target_pairs={{0,2},{2,0},{4,6},{6,4},{8,10},{10,8},{12,14},{14,12},{1,3},{3,1},... | collective-permute-start | bytes 786440 | tf_op jit(solution)/shard_map/ppermute | solution.py:58
  48.4 11.7 %collective-permute-start.2 = (f32[64,512]{1,0:T(8,128)S(1)}, f32[64,512]{1,0:T(8,128)S(1)}, u32[]{:S(2)}, u32[]{:S(2)}) collective-permute-start(f32[64,512]{1,0:T(8,128)S(1)} %slice_select_fusion.3), channel_id=1, source_target_pairs={{0,8},{2,10},{4,12},{6,14},{8,0},{10,2},{12,4},{14,6},{1,9},{3,11}... | collective-permute-start | bytes 393224 | tf_op jit(solution)/shard_map/ppermute | solution.py:58
  51.1 17.1 %collective-permute-start.5 = (f32[64,512]{1,0:T(8,128)S(1)}, f32[64,512]{1,0:T(8,128)S(1)}, u32[]{:S(2)}, u32[]{:S(2)}) collective-permute-start(f32[64,512]{1,0:T(8,128)S(1)} %slice_select_fusion.2), channel_id=1, source_target_pairs={{0,8},{2,10},{4,12},{6,14},{8,0},{10,2},{12,4},{14,6},{1,9},{3,11}... | collective-permute-start | bytes 393224 | tf_op jit(solution)/shard_map/ppermute | solution.py:58
  56.9 14.2 %collective-permute-start.8 = (f32[64,512]{1,0:T(8,128)S(1)}, f32[64,512]{1,0:T(8,128)S(1)}, u32[]{:S(2)}, u32[]{:S(2)}) collective-permute-start(f32[64,512]{1,0:T(8,128)S(1)} %slice_select_fusion.1), channel_id=1, source_target_pairs={{0,8},{2,10},{4,12},{6,14},{8,0},{10,2},{12,4},{14,6},{1,9},{3,11}... | collective-permute-start | bytes 393224 | tf_op jit(solution)/shard_map/ppermute | solution.py:58
  57.6 15.1 %collective-permute-start.11 = (f32[64,512]{1,0:T(8,128)S(1)}, f32[64,512]{1,0:T(8,128)S(1)}, u32[]{:S(2)}, u32[]{:S(2)}) collective-permute-start(f32[64,512]{1,0:T(8,128)S(1)} %slice_select_fusion), channel_id=1, source_target_pairs={{0,8},{2,10},{4,12},{6,14},{8,0},{10,2},{12,4},{14,6},{1,9},{3,11}... | collective-permute-start | bytes 393224 | tf_op jit(solution)/shard_map/ppermute | solution.py:58
  77.8 3.6 %collective-permute-start.12 = (f32[]{:T(128)}, f32[]{:T(128)}, u32[]{:S(2)}, u32[]{:S(2)}) collective-permute-start(f32[]{:T(128)} %psum.7), channel_id=1, source_target_pairs={{0,1},{1,0},{2,3},{3,2},{4,5},{5,4},{6,7},{7,6},{8,9},{9,8},{10,11... | collective-permute-start | bytes 20 | tf_op jit(solution)/shard_map/ppermute | solution.py:33
  82.8 3.6 %collective-permute-start.13 = (f32[]{:T(128)}, f32[]{:T(128)}, u32[]{:S(2)}, u32[]{:S(2)}) collective-permute-start(f32[]{:T(128)} %add.77), channel_id=1, source_target_pairs={{0,2},{2,0},{4,6},{6,4},{8,10},{10,8},{12,14},{14,12},{1,3},{3,1},... | collective-permute-start | bytes 20 | tf_op jit(solution)/shard_map/ppermute | solution.py:33
  87.0 3.6 %collective-permute-start.14 = (f32[]{:T(128)}, f32[]{:T(128)}, u32[]{:S(2)}, u32[]{:S(2)}) collective-permute-start(f32[]{:T(128)} %add.78), channel_id=1, source_target_pairs={{0,4},{2,6},{4,0},{6,2},{8,12},{10,14},{12,8},{14,10},{1,5},{3,7},... | collective-permute-start | bytes 20 | tf_op jit(solution)/shard_map/ppermute | solution.py:33
  91.2 4.5 %collective-permute-start.15 = (f32[]{:T(128)}, f32[]{:T(128)}, u32[]{:S(2)}, u32[]{:S(2)}) collective-permute-start(f32[]{:T(128)} %add.79), channel_id=1, source_target_pairs={{0,8},{2,10},{4,12},{6,14},{8,0},{10,2},{12,4},{14,6},{1,9},{3,11}... | collective-permute-start | bytes 20 | tf_op jit(solution)/shard_map/ppermute | solution.py:33
  96.9 9.8 %collective-permute-start.16 = (bf16[512,128]{0,1:T(8,128)(2,1)S(1)}, bf16[512,128]{0,1:T(8,128)(2,1)S(1)}, u32[]{:S(2)}, u32[]{:S(2)}) collective-permute-start(bf16[512,128]{0,1:T(8,128)(2,1)S(1)} %slice.300), channel_id=1, source_target_pairs={{0,8},{2,10},{4,12},{6,14},{8,0},{10,2},{12,4},{14,6},{1,9},{3,11}... | collective-permute-start | bytes 393224 | tf_op jit(solution)/shard_map/ppermute | solution.py:72
  106.7 6.9 %collective-permute-start.19 = (bf16[512,128]{0,1:T(8,128)(2,1)S(1)}, bf16[512,128]{0,1:T(8,128)(2,1)S(1)}, u32[]{:S(2)}, u32[]{:S(2)}) collective-permute-start(bf16[512,128]{0,1:T(8,128)(2,1)S(1)} %get-tuple-element.57), channel_id=1, source_target_pairs={{0,8},{2,10},{4,12},{6,14},{8,0},{10,2},{12,4},{14,6},{1,9},{3,11}... | collective-permute-start | bytes 393224 | tf_op jit(solution)/shard_map/ppermute | solution.py:72
  106.8 8.7 %collective-permute-start.17 = (bf16[2,512,128]{1,2,0:T(8,128)(2,1)S(1)}, bf16[2,512,128]{1,2,0:T(8,128)(2,1)S(1)}, u32[]{:S(2)}, u32[]{:S(2)}) collective-permute-start(bf16[2,512,128]{1,2,0:T(8,128)(2,1)S(1)} %pad_maximum_fusion.18), channel_id=1, source_target_pairs={{0,4},{2,6},{4,0},{6,2},{8,12},{10,14},{12,8},{14,10},{1,5},{3,7},... | collective-permute-start | bytes 786440 | tf_op jit(solution)/shard_map/ppermute | solution.py:72
  113.6 7.0 %collective-permute-start.20 = (bf16[2,512,128]{1,2,0:T(8,128)(2,1)S(1)}, bf16[2,512,128]{1,2,0:T(8,128)(2,1)S(1)}, u32[]{:S(2)}, u32[]{:S(2)}) collective-permute-start(bf16[2,512,128]{1,2,0:T(8,128)(2,1)S(1)} %pad_maximum_fusion.19), channel_id=1, source_target_pairs={{0,2},{2,0},{4,6},{6,4},{8,10},{10,8},{12,14},{14,12},{1,3},{3,1},... | collective-permute-start | bytes 786440 | tf_op jit(solution)/shard_map/ppermute | solution.py:72
  115.6 10.7 %collective-permute-start.18 = (bf16[2,2,512,128]{2,3,1,0:T(8,128)(2,1)S(1)}, bf16[2,2,512,128]{2,3,1,0:T(8,128)(2,1)S(1)}, u32[]{:S(2)}, u32[]{:S(2)}) collective-permute-start(bf16[2,2,512,128]{2,3,1,0:T(8,128)(2,1)S(1)} %pad_maximum_fusion.8), channel_id=1, source_target_pairs={{0,2},{2,0},{4,6},{6,4},{8,10},{10,8},{12,14},{14,12},{1,3},{3,1},... | collective-permute-start | bytes 1572872 | tf_op jit(solution)/shard_map/ppermute | solution.py:72
  121.6 9.4 %collective-permute-start.21 = (bf16[2,2,512,128]{2,3,1,0:T(8,128)(2,1)}, bf16[2,2,512,128]{2,3,1,0:T(8,128)(2,1)S(1)}, u32[]{:S(2)}, u32[]{:S(2)}) collective-permute-start(bf16[2,2,512,128]{2,3,1,0:T(8,128)(2,1)} %pad_maximum_fusion.9), channel_id=1, source_target_pairs={{0,4},{2,6},{4,0},{6,2},{8,12},{10,14},{12,8},{14,10},{1,5},{3,7},... | collective-permute-start | bytes 1572872 | tf_op jit(solution)/shard_map/ppermute | solution.py:72
  (9 other events, 49.7 us)

commit v11 on v9

--- a/solution.py
+++ b/solution.py
@@ -37,7 +37,7 @@
 
 def bit_orders(size):
     bits = list(range(size.bit_length() - 1))
-    return bits, bits[1:2] + bits[:1] + bits[2:]
+    return bits, bits[1:2] + bits[:1] + bits[2:], bits[:1] + bits[2:3] + bits[1:2] + bits[3:]
 
 
 def halving_scatter(partial, axis, order):
@@ -88,7 +88,7 @@
     width = cols // parts
     return jnp.concatenate(
         [
-            halving_scatter(partial_t[k * width:(k + 1) * width], axis, orders[int(k % 4 == 1)])
+            halving_scatter(partial_t[k * width:(k + 1) * width], axis, orders[(0, 1, 2, 1)[k % 4]])
             for k in range(parts)
         ],
         axis=0,
@@ -100,7 +100,7 @@
     cols = part.shape[1]
     if size & (size - 1) or size == 1 or cols % 2:
         return lax.all_gather(part, axis, axis=0, tiled=True)
-    first, second = bit_orders(size)
+    first, second = bit_orders(size)[:2]
     half = cols // 2
     return jnp.concatenate(
         [

time: 137 us -> 131 us (0.956)
  starting transfers between devices: 38.3 us -> 30.5 us
    ppermute x12, starting transfers between devices: 23.2 us -> 18 us  [halving_scatter(): blocks = keep + lax.ppermute(send, axis, pairs)]
    ppermute x12, waiting for transfers between devices: 29.5 us -> 27.5 us  [halving_scatter(): blocks = keep + lax.ppermute(send, axis, pairs)]
    ppermute x6, starting transfers between devices: 6.12 us -> 4.59 us  [doubling_gather(): other = lax.ppermute(current, axis, pairs)]
    ppermute x6, waiting for transfers between devices: 25.8 us -> 27.3 us  [doubling_gather(): other = lax.ppermute(current, axis, pairs)]
    unnamed x57 -> x43, local copies, waits for them, and re-layouts: 5.54 us -> 6.55 us
  transfers between devices with their start and end apart: 23 -> 23, of which waited for: 19 -> 19; matrix products, arithmetic and copies ran while one was open for 11% -> 12% of each run, Pallas kernels for 0% -> 0%
where the time goes in v11:
time: 131 us; the launch traced here: 130 us
  waiting for transfers between devices  64 us (49%)
  starting transfers between devices  30.5 us (23%)
  other arithmetic  14.5 us (11%)
  local copies, waits for them, and re-layouts  9.85 us (8%)
  matrix products  6.18 us (5%)
  between operations  5.04 us (4%)
    ppermute x12, waiting for transfers between devices, halving_scatter(): blocks = keep + lax.ppermute(send, axis, pairs)  27.5 us
    ppermute x6, waiting for transfers between devices, doubling_gather(): other = lax.ppermute(current, axis, pairs)  27.3 us
    ppermute x12, starting transfers between devices, halving_scatter(): blocks = keep + lax.ppermute(send, axis, pairs)  18 us
    ppermute x5, waiting for transfers between devices, butterfly_sum(): value = value + lax.ppermute(value, axis, pairs)  9.17 us
    ppermute x5, starting transfers between devices, butterfly_sum(): value = value + lax.ppermute(value, axis, pairs)  7.88 us
    unnamed x43, local copies, waits for them, and re-layouts  6.55 us
    dot_general x1, matrix products, slot_term(): lax.dot_general(weighted, columns, (((0,), (0,)), ((), ())), preferred_el...  6.18 us
    add x12, other arithmetic, halving_scatter(): blocks = keep + lax.ppermute(send, axis, pairs)  5.12 us
  transfers between devices with their start and end apart: 23, of which 19 were waited for; matrix products, arithmetic and copies ran while one was open for 12% of the time, Pallas kernels for 0%

profile of v11, /device:TPU:0, one launch (start us, length us, event | category | flops | bytes accessed | tf_op | source)
XLA Modules:
  0.0 130.1 jit_solution(16450309621199365273)
XLA Ops:
  0.0 1.4 %convert_bitcast_fusion = (bf16[8]{0:T(256)(128)(2,1)S(1)}, s32[]{:T(128)}) fusion(s32[1,8]{1,0:T(1,128)} %param.8), kind=kLoop, calls=%fused_computation.76 | loop fusion | flops 15 | bytes 52 | tf_op jit(solution)/shard_map/convert_element_type | solution.py:16
  1.4 6.2 %fusion.2 = f32[256,4096]{1,0:T(8,128)S(1)} fusion(bf16[1,8,128,4096]{3,2,1,0:T(8,128)(2,1)} %param.6, bf16[1,8,128,256]{3,2,1,0:T(8,128)(2,1)} %param.7, bf16[8]{0:T(256)(128)(2,1)S(1)} %get-tuple-element.54), kind=kOutput, calls=%fused_computation.2 | convolution fusion | flops 2147745792 | bytes 13107216 | tf_op jit(solution)/shard_map/dot_general | solution.py:19
  7.6 1.9 %copy-done = f32[256,4096]{1,0:T(8,128)} copy-done((f32[256,4096]{1,0:T(8,128)}, f32[256,4096]{1,0:T(8,128)S(1)}, u32[]{:S(2)}) %copy-start) | copy-done | bytes 4194328
  10.9 2.9 %collective-permute-start = (f32[64,2048]{1,0:T(8,128)}, f32[64,2048]{1,0:T(8,128)}, u32[]{:S(2)}, u32[]{:S(2)}) collective-permute-start(f32[64,2048]{1,0:T(8,128)} %fusion.18), channel_id=1, source_target_pairs={{0,2},{2,0},{4,6},{6,4},{8,10},{10,8},{12,14},{14,12},{1,3},{3,1},... | collective-permute-start | bytes 1572872 | tf_op jit(solution)/shard_map/ppermute | solution.py:58
  13.9 1.6 %fusion.25 = (f32[64,1024]{1,0:T(8,128)S(1)}, f32[64,1024]{1,0:T(8,128)S(1)}, f32[64,1024]{1,0:T(8,128)S(1)}, f32[64,1024]{1,0:T(8,128)S(1)}, f32[64,1024]{1,0:T...) fusion(f32[256,4096]{1,0:T(8,128)} %copy-done), kind=kLoop, calls=%fused_computation.78 | loop fusion | bytes 4194304 | tf_op jit(solution)/shard_map/slice | solution.py:54
  16.4 1.6 %collective-permute-start.3 = (f32[64,2048]{1,0:T(8,128)}, f32[64,2048]{1,0:T(8,128)}, u32[]{:S(2)}, u32[]{:S(2)}) collective-permute-start(f32[64,2048]{1,0:T(8,128)} %fusion.16), channel_id=1, source_target_pairs={{0,4},{2,6},{4,0},{6,2},{8,12},{10,14},{12,8},{14,10},{1,5},{3,7},... | collective-permute-start | bytes 1572872 | tf_op jit(solution)/shard_map/ppermute | solution.py:58
  23.5 2.0 %copy.14 = f32[1,512,256]{1,2,0:T(8,128)} copy(f32[1,512,256]{2,1,0:T(8,128)} %param.9) | data formatting | bytes 1048576 | tf_op args[3]
  26.9 1.4 %select_add_fusion.3 = f32[64,2048]{1,0:T(8,128)S(1)} fusion(f32[64,2048]{1,0:T(8,128)} %collective-permute-done, f32[64,512]{1,0:T(8,128)} %copy-done.13, f32[64,512]{1,0:T(8,128)} %copy-done.14, f32[64,512]{1,0:T(8,128)} %copy-done.15, f32[64,512]{1,0:T(8,128)} %copy-done.16, f32[64,512]{1,0:T(8,128)} %copy-done.17, f32[64,512]{1,0:T(8,128)} %copy-done.18, ...), kind=kLoop, calls=%fused_computation.35 | loop fusion | flops 1048576 | bytes 2097153 | tf_op jit(solution)/shard_map/add | solution.py:58
  28.4 2.2 %collective-permute-start.1 = (f32[64,1024]{1,0:T(8,128)S(1)}, f32[64,1024]{1,0:T(8,128)S(1)}, u32[]{:S(2)}, u32[]{:S(2)}) collective-permute-start(f32[64,1024]{1,0:T(8,128)S(1)} %fusion.23), channel_id=1, source_target_pairs={{0,4},{2,6},{4,0},{6,2},{8,12},{10,14},{12,8},{14,10},{1,5},{3,7},... | collective-permute-start | bytes 786440 | tf_op jit(solution)/shard_map/ppermute | solution.py:58
  33.4 4.7 %collective-permute-done.6 = f32[64,2048]{1,0:T(8,128)} collective-permute-done((f32[64,2048]{1,0:T(8,128)}, f32[64,2048]{1,0:T(8,128)}, u32[]{:S(2)}, u32[]{:S(2)}) %collective-permute-start.6) | collective-permute-done | bytes 524320 | tf_op jit(solution)/shard_map/ppermute | solution.py:58
  39.4 3.2 %collective-permute-start.7 = (f32[64,1024]{1,0:T(8,128)S(1)}, f32[64,1024]{1,0:T(8,128)S(1)}, u32[]{:S(2)}, u32[]{:S(2)}) collective-permute-start(f32[64,1024]{1,0:T(8,128)S(1)} %slice_select_fusion), channel_id=1, source_target_pairs={{0,8},{2,10},{4,12},{6,14},{8,0},{10,2},{12,4},{14,6},{1,9},{3,11}... | collective-permute-start | bytes 786440 | tf_op jit(solution)/shard_map/ppermute | solution.py:58
  42.6 5.8 %collective-permute-done.9 = f32[64,2048]{1,0:T(8,128)} collective-permute-done((f32[64,2048]{1,0:T(8,128)}, f32[64,2048]{1,0:T(8,128)}, u32[]{:S(2)}, u32[]{:S(2)}) %collective-permute-start.9) | collective-permute-done | bytes 524320 | tf_op jit(solution)/shard_map/ppermute | solution.py:58
  49.7 2.7 %collective-permute-done.1 = f32[64,1024]{1,0:T(8,128)S(1)} collective-permute-done((f32[64,1024]{1,0:T(8,128)S(1)}, f32[64,1024]{1,0:T(8,128)S(1)}, u32[]{:S(2)}, u32[]{:S(2)}) %collective-permute-start.1) | collective-permute-done | bytes 262176 | tf_op jit(solution)/shard_map/ppermute | solution.py:58
  53.8 1.9 %collective-permute-start.5 = (f32[64,512]{1,0:T(8,128)S(1)}, f32[64,512]{1,0:T(8,128)S(1)}, u32[]{:S(2)}, u32[]{:S(2)}) collective-permute-start(f32[64,512]{1,0:T(8,128)S(1)} %slice_select_fusion.3), channel_id=1, source_target_pairs={{0,8},{2,10},{4,12},{6,14},{8,0},{10,2},{12,4},{14,6},{1,9},{3,11}... | collective-permute-start | bytes 393224 | tf_op jit(solution)/shard_map/ppermute | solution.py:58
  56.6 3.0 %collective-permute-start.11 = (f32[64,512]{1,0:T(8,128)S(1)}, f32[64,512]{1,0:T(8,128)S(1)}, u32[]{:S(2)}, u32[]{:S(2)}) collective-permute-start(f32[64,512]{1,0:T(8,128)S(1)} %slice_select_fusion.1), channel_id=1, source_target_pairs={{0,8},{2,10},{4,12},{6,14},{8,0},{10,2},{12,4},{14,6},{1,9},{3,11}... | collective-permute-start | bytes 393224 | tf_op jit(solution)/shard_map/ppermute | solution.py:58
  59.6 6.0 %collective-permute-done.2 = f32[64,512]{1,0:T(8,128)S(1)} collective-permute-done((f32[64,512]{1,0:T(8,128)S(1)}, f32[64,512]{1,0:T(8,128)S(1)}, u32[]{:S(2)}, u32[]{:S(2)}) %collective-permute-start.2) | collective-permute-done | bytes 131104 | tf_op jit(solution)/shard_map/ppermute | solution.py:58
  65.6 4.2 %collective-permute-done.5 = f32[64,512]{1,0:T(8,128)S(1)} collective-permute-done((f32[64,512]{1,0:T(8,128)S(1)}, f32[64,512]{1,0:T(8,128)S(1)}, u32[]{:S(2)}, u32[]{:S(2)}) %collective-permute-start.5) | collective-permute-done | bytes 131104 | tf_op jit(solution)/shard_map/ppermute | solution.py:58
  69.9 1.7 %collective-permute-done.11 = f32[64,512]{1,0:T(8,128)S(1)} collective-permute-done((f32[64,512]{1,0:T(8,128)S(1)}, f32[64,512]{1,0:T(8,128)S(1)}, u32[]{:S(2)}, u32[]{:S(2)}) %collective-permute-start.11) | collective-permute-done | bytes 131104 | tf_op jit(solution)/shard_map/ppermute | solution.py:58
  75.0 2.9 %collective-permute-start.13 = (f32[]{:T(128)}, f32[]{:T(128)}, u32[]{:S(2)}, u32[]{:S(2)}) collective-permute-start(f32[]{:T(128)} %add.78), channel_id=1, source_target_pairs={{0,1},{1,0},{2,3},{3,2},{4,5},{5,4},{6,7},{7,6},{8,9},{9,8},{10,11... | collective-permute-start | bytes 20 | tf_op jit(solution)/shard_map/ppermute | solution.py:33
  79.4 1.7 %collective-permute-start.14 = (f32[]{:T(128)}, f32[]{:T(128)}, u32[]{:S(2)}, u32[]{:S(2)}) collective-permute-start(f32[]{:T(128)} %add.79), channel_id=1, source_target_pairs={{0,2},{2,0},{4,6},{6,4},{8,10},{10,8},{12,14},{14,12},{1,3},{3,1},... | collective-permute-start | bytes 20 | tf_op jit(solution)/shard_map/ppermute | solution.py:33
  81.1 2.0 %collective-permute-done.14 = f32[]{:T(128)} collective-permute-done((f32[]{:T(128)}, f32[]{:T(128)}, u32[]{:S(2)}, u32[]{:S(2)}) %collective-permute-start.14) | collective-permute-done | bytes 36 | tf_op jit(solution)/shard_map/ppermute | solution.py:33
  83.7 1.4 %collective-permute-start.15 = (f32[]{:T(128)}, f32[]{:T(128)}, u32[]{:S(2)}, u32[]{:S(2)}) collective-permute-start(f32[]{:T(128)} %add.80), channel_id=1, source_target_pairs={{0,4},{2,6},{4,0},{6,2},{8,12},{10,14},{12,8},{14,10},{1,5},{3,7},... | collective-permute-start | bytes 20 | tf_op jit(solution)/shard_map/ppermute | solution.py:33
  85.1 2.3 %collective-permute-done.15 = f32[]{:T(128)} collective-permute-done((f32[]{:T(128)}, f32[]{:T(128)}, u32[]{:S(2)}, u32[]{:S(2)}) %collective-permute-start.15) | collective-permute-done | bytes 36 | tf_op jit(solution)/shard_map/ppermute | solution.py:33
  88.1 1.9 %collective-permute-start.16 = (f32[]{:T(128)}, f32[]{:T(128)}, u32[]{:S(2)}, u32[]{:S(2)}) collective-permute-start(f32[]{:T(128)} %add.81), channel_id=1, source_target_pairs={{0,8},{2,10},{4,12},{6,14},{8,0},{10,2},{12,4},{14,6},{1,9},{3,11}... | collective-permute-start | bytes 20 | tf_op jit(solution)/shard_map/ppermute | solution.py:33
  90.0 2.7 %collective-permute-done.16 = f32[]{:T(128)} collective-permute-done((f32[]{:T(128)}, f32[]{:T(128)}, u32[]{:S(2)}, u32[]{:S(2)}) %collective-permute-start.16) | collective-permute-done | bytes 36 | tf_op jit(solution)/shard_map/ppermute | solution.py:33
  94.4 9.0 %collective-permute-done.17 = bf16[512,128]{0,1:T(8,128)(2,1)S(1)} collective-permute-done((bf16[512,128]{0,1:T(8,128)(2,1)S(1)}, bf16[512,128]{0,1:T(8,128)(2,1)S(1)}, u32[]{:S(2)}, u32[]{:S(2)}) %collective-permute-start.17) | collective-permute-done | bytes 131104 | tf_op jit(solution)/shard_map/ppermute | solution.py:72
  103.6 2.4 %collective-permute-start.18 = (bf16[2,512,128]{1,2,0:T(8,128)(2,1)S(1)}, bf16[2,512,128]{1,2,0:T(8,128)(2,1)S(1)}, u32[]{:S(2)}, u32[]{:S(2)}) collective-permute-start(bf16[2,512,128]{1,2,0:T(8,128)(2,1)S(1)} %pad_maximum_fusion.16), channel_id=1, source_target_pairs={{0,4},{2,6},{4,0},{6,2},{8,12},{10,14},{12,8},{14,10},{1,5},{3,7},... | collective-permute-start | bytes 786440 | tf_op jit(solution)/shard_map/ppermute | solution.py:72
  106.0 3.8 %collective-permute-done.20 = bf16[512,128]{0,1:T(8,128)(2,1)S(1)} collective-permute-done((bf16[512,128]{0,1:T(8,128)(2,1)S(1)}, bf16[512,128]{0,1:T(8,128)(2,1)S(1)}, u32[]{:S(2)}, u32[]{:S(2)}) %collective-permute-start.20) | collective-permute-done | bytes 131104 | tf_op jit(solution)/shard_map/ppermute | solution.py:72
  112.6 4.9 %collective-permute-done.21 = bf16[2,512,128]{1,2,0:T(8,128)(2,1)S(1)} collective-permute-done((bf16[2,512,128]{1,2,0:T(8,128)(2,1)S(1)}, bf16[2,512,128]{1,2,0:T(8,128)(2,1)S(1)}, u32[]{:S(2)}, u32[]{:S(2)}) %collective-permute-start.21) | collective-permute-done | bytes 262176 | tf_op jit(solution)/shard_map/ppermute | solution.py:72
  118.3 4.7 %collective-permute-done.19 = bf16[2,2,512,128]{2,3,1,0:T(8,128)(2,1)S(1)} collective-permute-done((bf16[2,2,512,128]{2,3,1,0:T(8,128)(2,1)S(1)}, bf16[2,2,512,128]{2,3,1,0:T(8,128)(2,1)S(1)}, u32[]{:S(2)}, u32[]{:S(2)}) %collective-permute-start.19) | collective-permute-done | bytes 524320 | tf_op jit(solution)/shard_map/ppermute | solution.py:72
  123.9 3.8 %collective-permute-done.22 = bf16[2,2,512,128]{2,3,1,0:T(8,128)(2,1)S(1)} collective-permute-done((bf16[2,2,512,128]{2,3,1,0:T(8,128)(2,1)}, bf16[2,2,512,128]{2,3,1,0:T(8,128)(2,1)S(1)}, u32[]{:S(2)}, u32[]{:S(2)}) %collective-permute-start.22) | collective-permute-done | bytes 524320 | tf_op jit(solution)/shard_map/ppermute | solution.py:72
  128.6 1.5 %maximum_bitcast_fusion = bf16[1,4096,256]{2,1,0:T(8,128)(2,1)} fusion(bf16[4096,128]{1,0:T(8,128)(2,1)S(1)} %bitcast.75, bf16[4096,128]{1,0:T(8,128)(2,1)S(1)} %bitcast.74), kind=kLoop, calls=%fused_computation.3 | loop fusion | flops 4194304 | bytes 4194304 | tf_op jit(solution)/shard_map/broadcast_in_dim | solution.py:132
  (106 shorter events, 25.4 us)
Async XLA Ops:
  9.8 11.2 %copy-start.12 = (f32[64,512]{1,0:T(8,128)}, f32[64,512]{1,0:T(8,128)S(1)}, u32[]{:S(2)}) copy-start(f32[64,512]{1,0:T(8,128)S(1)} %get-tuple-element.5) | copy-start | bytes 393220
  9.8 11.2 %copy-start.13 = (f32[64,512]{1,0:T(8,128)}, f32[64,512]{1,0:T(8,128)S(1)}, u32[]{:S(2)}) copy-start(f32[64,512]{1,0:T(8,128)S(1)} %get-tuple-element.14) | copy-start | bytes 393220
  9.8 11.2 %copy-start.14 = (f32[64,512]{1,0:T(8,128)}, f32[64,512]{1,0:T(8,128)S(1)}, u32[]{:S(2)}) copy-start(f32[64,512]{1,0:T(8,128)S(1)} %get-tuple-element.15) | copy-start | bytes 393220
  10.9 16.0 %collective-permute-start = (f32[64,2048]{1,0:T(8,128)}, f32[64,2048]{1,0:T(8,128)}, u32[]{:S(2)}, u32[]{:S(2)}) collective-permute-start(f32[64,2048]{1,0:T(8,128)} %fusion.18), channel_id=1, source_target_pairs={{0,2},{2,0},{4,6},{6,4},{8,10},{10,8},{12,14},{14,12},{1,3},{3,1},... | collective-permute-start | bytes 1572872 | tf_op jit(solution)/shard_map/ppermute | solution.py:58
  16.4 15.2 %collective-permute-start.3 = (f32[64,2048]{1,0:T(8,128)}, f32[64,2048]{1,0:T(8,128)}, u32[]{:S(2)}, u32[]{:S(2)}) collective-permute-start(f32[64,2048]{1,0:T(8,128)} %fusion.16), channel_id=1, source_target_pairs={{0,4},{2,6},{4,0},{6,2},{8,12},{10,14},{12,8},{14,10},{1,5},{3,7},... | collective-permute-start | bytes 1572872 | tf_op jit(solution)/shard_map/ppermute | solution.py:58
  18.9 19.3 %collective-permute-start.6 = (f32[64,2048]{1,0:T(8,128)}, f32[64,2048]{1,0:T(8,128)}, u32[]{:S(2)}, u32[]{:S(2)}) collective-permute-start(f32[64,2048]{1,0:T(8,128)} %fusion.17), channel_id=1, source_target_pairs={{0,2},{2,0},{4,6},{6,4},{8,10},{10,8},{12,14},{14,12},{1,3},{3,1},... | collective-permute-start | bytes 1572872 | tf_op jit(solution)/shard_map/ppermute | solution.py:58
  20.3 28.1 %collective-permute-start.9 = (f32[64,2048]{1,0:T(8,128)}, f32[64,2048]{1,0:T(8,128)}, u32[]{:S(2)}, u32[]{:S(2)}) collective-permute-start(f32[64,2048]{1,0:T(8,128)} %fusion.15), channel_id=1, source_target_pairs={{0,4},{2,6},{4,0},{6,2},{8,12},{10,14},{12,8},{14,10},{1,5},{3,7},... | collective-permute-start | bytes 1572872 | tf_op jit(solution)/shard_map/ppermute | solution.py:58
  25.6 12.6 %copy-start.3 = (f32[64,512]{1,0:T(8,128)S(1)}, f32[64,512]{1,0:T(8,128)}, u32[]{:S(2)}) copy-start(f32[64,512]{1,0:T(8,128)} %copy-done.2) | copy-start | bytes 393220
  25.6 12.6 %copy-start.5 = (f32[64,512]{1,0:T(8,128)S(1)}, f32[64,512]{1,0:T(8,128)}, u32[]{:S(2)}) copy-start(f32[64,512]{1,0:T(8,128)} %copy-done.4) | copy-start | bytes 393220
  25.6 12.6 %copy-start.7 = (f32[64,512]{1,0:T(8,128)S(1)}, f32[64,512]{1,0:T(8,128)}, u32[]{:S(2)}) copy-start(f32[64,512]{1,0:T(8,128)} %copy-done.6) | copy-start | bytes 393220
  25.6 12.6 %copy-start.9 = (f32[64,512]{1,0:T(8,128)S(1)}, f32[64,512]{1,0:T(8,128)}, u32[]{:S(2)}) copy-start(f32[64,512]{1,0:T(8,128)} %copy-done.8) | copy-start | bytes 393220
  25.6 12.6 %copy-start.11 = (f32[64,512]{1,0:T(8,128)S(1)}, f32[64,512]{1,0:T(8,128)}, u32[]{:S(2)}) copy-start(f32[64,512]{1,0:T(8,128)} %copy-done.10) | copy-start | bytes 393220
  28.4 24.0 %collective-permute-start.1 = (f32[64,1024]{1,0:T(8,128)S(1)}, f32[64,1024]{1,0:T(8,128)S(1)}, u32[]{:S(2)}, u32[]{:S(2)}) collective-permute-start(f32[64,1024]{1,0:T(8,128)S(1)} %fusion.23), channel_id=1, source_target_pairs={{0,4},{2,6},{4,0},{6,2},{8,12},{10,14},{12,8},{14,10},{1,5},{3,7},... | collective-permute-start | bytes 786440 | tf_op jit(solution)/shard_map/ppermute | solution.py:58
  32.8 20.9 %collective-permute-start.4 = (f32[64,1024]{1,0:T(8,128)S(1)}, f32[64,1024]{1,0:T(8,128)S(1)}, u32[]{:S(2)}, u32[]{:S(2)}) collective-permute-start(f32[64,1024]{1,0:T(8,128)S(1)} %fusion.22), channel_id=1, source_target_pairs={{0,2},{2,0},{4,6},{6,4},{8,10},{10,8},{12,14},{14,12},{1,3},{3,1},... | collective-permute-start | bytes 786440 | tf_op jit(solution)/shard_map/ppermute | solution.py:58
  39.4 16.3 %collective-permute-start.7 = (f32[64,1024]{1,0:T(8,128)S(1)}, f32[64,1024]{1,0:T(8,128)S(1)}, u32[]{:S(2)}, u32[]{:S(2)}) collective-permute-start(f32[64,1024]{1,0:T(8,128)S(1)} %slice_select_fusion), channel_id=1, source_target_pairs={{0,8},{2,10},{4,12},{6,14},{8,0},{10,2},{12,4},{14,6},{1,9},{3,11}... | collective-permute-start | bytes 786440 | tf_op jit(solution)/shard_map/ppermute | solution.py:58
  49.6 43.7 %copy-start.1 = (f32[1,512,256]{1,2,0:T(8,128)S(1)}, f32[1,512,256]{1,2,0:T(8,128)}, u32[]{:S(2)}) copy-start(f32[1,512,256]{1,2,0:T(8,128)} %copy.14) | copy-start | bytes 1572868
  49.6 6.9 %collective-permute-start.10 = (f32[64,1024]{1,0:T(8,128)S(1)}, f32[64,1024]{1,0:T(8,128)S(1)}, u32[]{:S(2)}, u32[]{:S(2)}) collective-permute-start(f32[64,1024]{1,0:T(8,128)S(1)} %fusion.21), channel_id=1, source_target_pairs={{0,2},{2,0},{4,6},{6,4},{8,10},{10,8},{12,14},{14,12},{1,3},{3,1},... | collective-permute-start | bytes 786440 | tf_op jit(solution)/shard_map/ppermute | solution.py:58
  52.5 13.0 %collective-permute-start.2 = (f32[64,512]{1,0:T(8,128)S(1)}, f32[64,512]{1,0:T(8,128)S(1)}, u32[]{:S(2)}, u32[]{:S(2)}) collective-permute-start(f32[64,512]{1,0:T(8,128)S(1)} %slice_select_fusion.4), channel_id=1, source_target_pairs={{0,8},{2,10},{4,12},{6,14},{8,0},{10,2},{12,4},{14,6},{1,9},{3,11}... | collective-permute-start | bytes 393224 | tf_op jit(solution)/shard_map/ppermute | solution.py:58
  53.8 16.0 %collective-permute-start.5 = (f32[64,512]{1,0:T(8,128)S(1)}, f32[64,512]{1,0:T(8,128)S(1)}, u32[]{:S(2)}, u32[]{:S(2)}) collective-permute-start(f32[64,512]{1,0:T(8,128)S(1)} %slice_select_fusion.3), channel_id=1, source_target_pairs={{0,8},{2,10},{4,12},{6,14},{8,0},{10,2},{12,4},{14,6},{1,9},{3,11}... | collective-permute-start | bytes 393224 | tf_op jit(solution)/shard_map/ppermute | solution.py:58
  55.8 14.1 %collective-permute-start.8 = (f32[64,512]{1,0:T(8,128)S(1)}, f32[64,512]{1,0:T(8,128)S(1)}, u32[]{:S(2)}, u32[]{:S(2)}) collective-permute-start(f32[64,512]{1,0:T(8,128)S(1)} %slice_select_fusion.2), channel_id=1, source_target_pairs={{0,4},{2,6},{4,0},{6,2},{8,12},{10,14},{12,8},{14,10},{1,5},{3,7},... | collective-permute-start | bytes 393224 | tf_op jit(solution)/shard_map/ppermute | solution.py:58
  56.6 15.0 %collective-permute-start.11 = (f32[64,512]{1,0:T(8,128)S(1)}, f32[64,512]{1,0:T(8,128)S(1)}, u32[]{:S(2)}, u32[]{:S(2)}) collective-permute-start(f32[64,512]{1,0:T(8,128)S(1)} %slice_select_fusion.1), channel_id=1, source_target_pairs={{0,8},{2,10},{4,12},{6,14},{8,0},{10,2},{12,4},{14,6},{1,9},{3,11}... | collective-permute-start | bytes 393224 | tf_op jit(solution)/shard_map/ppermute | solution.py:58
  72.4 1.3 %collective-permute-start.12 = (f32[]{:T(128)}, f32[]{:T(128)}, u32[]{:S(2)}, u32[]{:S(2)}) collective-permute-start(f32[]{:T(128)} %multiply_reduce_fusion), channel_id=1, source_target_pairs={{0,16},{16,0},{1,17},{17,1},{2,18},{18,2},{3,19},{19,3},{4,20},{20... | collective-permute-start | bytes 20 | tf_op jit(solution)/shard_map/ppermute | solution.py:33
  75.0 3.7 %collective-permute-start.13 = (f32[]{:T(128)}, f32[]{:T(128)}, u32[]{:S(2)}, u32[]{:S(2)}) collective-permute-start(f32[]{:T(128)} %add.78), channel_id=1, source_target_pairs={{0,1},{1,0},{2,3},{3,2},{4,5},{5,4},{6,7},{7,6},{8,9},{9,8},{10,11... | collective-permute-start | bytes 20 | tf_op jit(solution)/shard_map/ppermute | solution.py:33
  79.4 3.7 %collective-permute-start.14 = (f32[]{:T(128)}, f32[]{:T(128)}, u32[]{:S(2)}, u32[]{:S(2)}) collective-permute-start(f32[]{:T(128)} %add.79), channel_id=1, source_target_pairs={{0,2},{2,0},{4,6},{6,4},{8,10},{10,8},{12,14},{14,12},{1,3},{3,1},... | collective-permute-start | bytes 20 | tf_op jit(solution)/shard_map/ppermute | solution.py:33
  83.7 3.7 %collective-permute-start.15 = (f32[]{:T(128)}, f32[]{:T(128)}, u32[]{:S(2)}, u32[]{:S(2)}) collective-permute-start(f32[]{:T(128)} %add.80), channel_id=1, source_target_pairs={{0,4},{2,6},{4,0},{6,2},{8,12},{10,14},{12,8},{14,10},{1,5},{3,7},... | collective-permute-start | bytes 20 | tf_op jit(solution)/shard_map/ppermute | solution.py:33
  88.1 4.6 %collective-permute-start.16 = (f32[]{:T(128)}, f32[]{:T(128)}, u32[]{:S(2)}, u32[]{:S(2)}) collective-permute-start(f32[]{:T(128)} %add.81), channel_id=1, source_target_pairs={{0,8},{2,10},{4,12},{6,14},{8,0},{10,2},{12,4},{14,6},{1,9},{3,11}... | collective-permute-start | bytes 20 | tf_op jit(solution)/shard_map/ppermute | solution.py:33
  93.8 9.6 %collective-permute-start.17 = (bf16[512,128]{0,1:T(8,128)(2,1)S(1)}, bf16[512,128]{0,1:T(8,128)(2,1)S(1)}, u32[]{:S(2)}, u32[]{:S(2)}) collective-permute-start(bf16[512,128]{0,1:T(8,128)(2,1)S(1)} %slice.286), channel_id=1, source_target_pairs={{0,8},{2,10},{4,12},{6,14},{8,0},{10,2},{12,4},{14,6},{1,9},{3,11}... | collective-permute-start | bytes 393224 | tf_op jit(solution)/shard_map/ppermute | solution.py:72
  103.5 6.3 %collective-permute-start.20 = (bf16[512,128]{0,1:T(8,128)(2,1)S(1)}, bf16[512,128]{0,1:T(8,128)(2,1)S(1)}, u32[]{:S(2)}, u32[]{:S(2)}) collective-permute-start(bf16[512,128]{0,1:T(8,128)(2,1)S(1)} %get-tuple-element.53), channel_id=1, source_target_pairs={{0,8},{2,10},{4,12},{6,14},{8,0},{10,2},{12,4},{14,6},{1,9},{3,11}... | collective-permute-start | bytes 393224 | tf_op jit(solution)/shard_map/ppermute | solution.py:72
  103.6 8.2 %collective-permute-start.18 = (bf16[2,512,128]{1,2,0:T(8,128)(2,1)S(1)}, bf16[2,512,128]{1,2,0:T(8,128)(2,1)S(1)}, u32[]{:S(2)}, u32[]{:S(2)}) collective-permute-start(bf16[2,512,128]{1,2,0:T(8,128)(2,1)S(1)} %pad_maximum_fusion.16), channel_id=1, source_target_pairs={{0,4},{2,6},{4,0},{6,2},{8,12},{10,14},{12,8},{14,10},{1,5},{3,7},... | collective-permute-start | bytes 786440 | tf_op jit(solution)/shard_map/ppermute | solution.py:72
  109.8 7.6 %collective-permute-start.21 = (bf16[2,512,128]{1,2,0:T(8,128)(2,1)S(1)}, bf16[2,512,128]{1,2,0:T(8,128)(2,1)S(1)}, u32[]{:S(2)}, u32[]{:S(2)}) collective-permute-start(bf16[2,512,128]{1,2,0:T(8,128)(2,1)S(1)} %pad_maximum_fusion.17), channel_id=1, source_target_pairs={{0,2},{2,0},{4,6},{6,4},{8,10},{10,8},{12,14},{14,12},{1,3},{3,1},... | collective-permute-start | bytes 786440 | tf_op jit(solution)/shard_map/ppermute | solution.py:72
  111.8 11.2 %collective-permute-start.19 = (bf16[2,2,512,128]{2,3,1,0:T(8,128)(2,1)S(1)}, bf16[2,2,512,128]{2,3,1,0:T(8,128)(2,1)S(1)}, u32[]{:S(2)}, u32[]{:S(2)}) collective-permute-start(bf16[2,2,512,128]{2,3,1,0:T(8,128)(2,1)S(1)} %pad_maximum_fusion.8), channel_id=1, source_target_pairs={{0,2},{2,0},{4,6},{6,4},{8,10},{10,8},{12,14},{14,12},{1,3},{3,1},... | collective-permute-start | bytes 1572872 | tf_op jit(solution)/shard_map/ppermute | solution.py:72
  118.3 9.4 %collective-permute-start.22 = (bf16[2,2,512,128]{2,3,1,0:T(8,128)(2,1)}, bf16[2,2,512,128]{2,3,1,0:T(8,128)(2,1)S(1)}, u32[]{:S(2)}, u32[]{:S(2)}) collective-permute-start(bf16[2,2,512,128]{2,3,1,0:T(8,128)(2,1)} %pad_maximum_fusion.9), channel_id=1, source_target_pairs={{0,4},{2,6},{4,0},{6,2},{8,12},{10,14},{12,8},{14,10},{1,5},{3,7},... | collective-permute-start | bytes 1572872 | tf_op jit(solution)/shard_map/ppermute | solution.py:72
  (11 other events, 67.9 us)

commit v12 on v11

--- a/solution.py
+++ b/solution.py
@@ -97,18 +97,20 @@
 
 def gather_rows(part, axis):
     size = lax.axis_size(axis)
-    cols = part.shape[1]
-    if size & (size - 1) or size == 1 or cols % 2:
+    rows, cols = part.shape
+    if size & (size - 1) or size == 1 or cols % 256 or rows % 32:
         return lax.all_gather(part, axis, axis=0, tiled=True)
     first, second = bit_orders(size)[:2]
-    half = cols // 2
-    return jnp.concatenate(
-        [
-            doubling_gather(part[:, :half], axis, first[::-1]),
-            doubling_gather(part[:, half:], axis, second[::-1]),
-        ],
-        axis=1,
-    )
+    half_rows, half_cols = rows // 2, cols // 2
+    columns = []
+    for h in range(2):
+        gathered = []
+        for r in range(2):
+            piece = part[r * half_rows:(r + 1) * half_rows, h * half_cols:(h + 1) * half_cols]
+            order = (first, second)[(h + r) % 2][::-1]
+            gathered.append(doubling_gather(piece, axis, order).reshape(size, half_rows, half_cols))
+        columns.append(jnp.stack(gathered, axis=1).reshape(size * rows, half_cols))
+    return jnp.concatenate(columns, axis=1)
 
 
 def local(normed_input, key_grad, live_slots, master, first_moment, second_moment):

time: 131 us -> 131 us (level)
  waiting for transfers between devices: 64 us -> 54.7 us
  starting transfers between devices: 30.5 us -> 38.8 us
  other arithmetic: 14.5 us -> 15.9 us
    ppermute x6 -> x12, waiting for transfers between devices: 27.3 us -> 18 us  [doubling_gather(): other = lax.ppermute(current, axis, pairs)]
    ppermute x6 -> x12, starting transfers between devices: 4.59 us -> 12.8 us  [doubling_gather(): other = lax.ppermute(current, axis, pairs)]
  transfers between devices with their start and end apart: 23 -> 29, of which waited for: 19 -> 20; matrix products, arithmetic and copies ran while one was open for 12% -> 14% of each run, Pallas kernels for 0% -> 0%
where the time goes in v12:
time: 131 us; the launch traced here: 130 us
  waiting for transfers between devices  54.7 us (42%)
  starting transfers between devices  38.8 us (30%)
  other arithmetic  15.9 us (12%)
  local copies, waits for them, and re-layouts  9.8 us (7%)
  matrix products  6.18 us (5%)
  between operations  5.21 us (4%)
    ppermute x12, waiting for transfers between devices, halving_scatter(): blocks = keep + lax.ppermute(send, axis, pairs)  27.5 us
    ppermute x12, starting transfers between devices, halving_scatter(): blocks = keep + lax.ppermute(send, axis, pairs)  18 us
    ppermute x12, waiting for transfers between devices, doubling_gather(): other = lax.ppermute(current, axis, pairs)  18 us
    ppermute x12, starting transfers between devices, doubling_gather(): other = lax.ppermute(current, axis, pairs)  12.8 us
    ppermute x5, waiting for transfers between devices, butterfly_sum(): value = value + lax.ppermute(value, axis, pairs)  9.17 us
    ppermute x5, starting transfers between devices, butterfly_sum(): value = value + lax.ppermute(value, axis, pairs)  7.87 us
    unnamed x43, local copies, waits for them, and re-layouts  6.58 us
    dot_general x1, matrix products, slot_term(): lax.dot_general(weighted, columns, (((0,), (0,)), ((), ())), preferred_el...  6.18 us
  transfers between devices with their start and end apart: 29, of which 20 were waited for; matrix products, arithmetic and copies ran while one was open for 14% of the time, Pallas kernels for 0%

profile of v12, /device:TPU:0, one launch (start us, length us, event | category | flops | bytes accessed | tf_op | source)
XLA Modules:
  0.0 130.5 jit_solution(16654544955621878952)
XLA Ops:
  1.4 6.2 %fusion.2 = f32[256,4096]{1,0:T(8,128)S(1)} fusion(bf16[1,8,128,4096]{3,2,1,0:T(8,128)(2,1)} %param.6, bf16[1,8,128,256]{3,2,1,0:T(8,128)(2,1)} %param.7, bf16[8]{0:T(256)(128)(2,1)S(1)} %get-tuple-element.72), kind=kOutput, calls=%fused_computation.2 | convolution fusion | flops 2147745792 | bytes 13107216 | tf_op jit(solution)/shard_map/dot_general | solution.py:19
  7.6 2.0 %copy-done = f32[256,4096]{1,0:T(8,128)} copy-done((f32[256,4096]{1,0:T(8,128)}, f32[256,4096]{1,0:T(8,128)S(1)}, u32[]{:S(2)}) %copy-start) | copy-done | bytes 4194328
  10.9 2.9 %collective-permute-start = (f32[64,2048]{1,0:T(8,128)}, f32[64,2048]{1,0:T(8,128)}, u32[]{:S(2)}, u32[]{:S(2)}) collective-permute-start(f32[64,2048]{1,0:T(8,128)} %fusion.18), channel_id=1, source_target_pairs={{0,2},{2,0},{4,6},{6,4},{8,10},{10,8},{12,14},{14,12},{1,3},{3,1},... | collective-permute-start | bytes 1572872 | tf_op jit(solution)/shard_map/ppermute | solution.py:58
  13.9 1.6 %fusion.25 = (f32[64,1024]{1,0:T(8,128)S(1)}, f32[64,1024]{1,0:T(8,128)S(1)}, f32[64,1024]{1,0:T(8,128)S(1)}, f32[64,1024]{1,0:T(8,128)S(1)}, f32[64,1024]{1,0:T...) fusion(f32[256,4096]{1,0:T(8,128)} %copy-done), kind=kLoop, calls=%fused_computation.98 | loop fusion | bytes 4194304 | tf_op jit(solution)/shard_map/slice | solution.py:54
  16.4 1.6 %collective-permute-start.3 = (f32[64,2048]{1,0:T(8,128)}, f32[64,2048]{1,0:T(8,128)}, u32[]{:S(2)}, u32[]{:S(2)}) collective-permute-start(f32[64,2048]{1,0:T(8,128)} %fusion.16), channel_id=1, source_target_pairs={{0,4},{2,6},{4,0},{6,2},{8,12},{10,14},{12,8},{14,10},{1,5},{3,7},... | collective-permute-start | bytes 1572872 | tf_op jit(solution)/shard_map/ppermute | solution.py:58
  23.5 2.0 %copy.22 = f32[1,512,256]{1,2,0:T(8,128)} copy(f32[1,512,256]{2,1,0:T(8,128)} %param.9) | data formatting | bytes 1048576 | tf_op args[3]
  26.9 1.4 %select_add_fusion.3 = f32[64,2048]{1,0:T(8,128)S(1)} fusion(f32[64,2048]{1,0:T(8,128)} %collective-permute-done, f32[64,512]{1,0:T(8,128)} %copy-done.13, f32[64,512]{1,0:T(8,128)} %copy-done.14, f32[64,512]{1,0:T(8,128)} %copy-done.15, f32[64,512]{1,0:T(8,128)} %copy-done.16, f32[64,512]{1,0:T(8,128)} %copy-done.17, f32[64,512]{1,0:T(8,128)} %copy-done.18, ...), kind=kLoop, calls=%fused_computation.33 | loop fusion | flops 1048576 | bytes 2097153 | tf_op jit(solution)/shard_map/add | solution.py:58
  28.4 2.2 %collective-permute-start.1 = (f32[64,1024]{1,0:T(8,128)S(1)}, f32[64,1024]{1,0:T(8,128)S(1)}, u32[]{:S(2)}, u32[]{:S(2)}) collective-permute-start(f32[64,1024]{1,0:T(8,128)S(1)} %fusion.23), channel_id=1, source_target_pairs={{0,4},{2,6},{4,0},{6,2},{8,12},{10,14},{12,8},{14,10},{1,5},{3,7},... | collective-permute-start | bytes 786440 | tf_op jit(solution)/shard_map/ppermute | solution.py:58
  33.4 4.7 %collective-permute-done.6 = f32[64,2048]{1,0:T(8,128)} collective-permute-done((f32[64,2048]{1,0:T(8,128)}, f32[64,2048]{1,0:T(8,128)}, u32[]{:S(2)}, u32[]{:S(2)}) %collective-permute-start.6) | collective-permute-done | bytes 524320 | tf_op jit(solution)/shard_map/ppermute | solution.py:58
  39.4 3.2 %collective-permute-start.7 = (f32[64,1024]{1,0:T(8,128)S(1)}, f32[64,1024]{1,0:T(8,128)S(1)}, u32[]{:S(2)}, u32[]{:S(2)}) collective-permute-start(f32[64,1024]{1,0:T(8,128)S(1)} %slice_select_fusion), channel_id=1, source_target_pairs={{0,8},{2,10},{4,12},{6,14},{8,0},{10,2},{12,4},{14,6},{1,9},{3,11}... | collective-permute-start | bytes 786440 | tf_op jit(solution)/shard_map/ppermute | solution.py:58
  42.6 5.8 %collective-permute-done.9 = f32[64,2048]{1,0:T(8,128)} collective-permute-done((f32[64,2048]{1,0:T(8,128)}, f32[64,2048]{1,0:T(8,128)}, u32[]{:S(2)}, u32[]{:S(2)}) %collective-permute-start.9) | collective-permute-done | bytes 524320 | tf_op jit(solution)/shard_map/ppermute | solution.py:58
  49.7 2.7 %collective-permute-done.1 = f32[64,1024]{1,0:T(8,128)S(1)} collective-permute-done((f32[64,1024]{1,0:T(8,128)S(1)}, f32[64,1024]{1,0:T(8,128)S(1)}, u32[]{:S(2)}, u32[]{:S(2)}) %collective-permute-start.1) | collective-permute-done | bytes 262176 | tf_op jit(solution)/shard_map/ppermute | solution.py:58
  53.8 1.9 %collective-permute-start.5 = (f32[64,512]{1,0:T(8,128)S(1)}, f32[64,512]{1,0:T(8,128)S(1)}, u32[]{:S(2)}, u32[]{:S(2)}) collective-permute-start(f32[64,512]{1,0:T(8,128)S(1)} %slice_select_fusion.3), channel_id=1, source_target_pairs={{0,8},{2,10},{4,12},{6,14},{8,0},{10,2},{12,4},{14,6},{1,9},{3,11}... | collective-permute-start | bytes 393224 | tf_op jit(solution)/shard_map/ppermute | solution.py:58
  56.6 3.0 %collective-permute-start.11 = (f32[64,512]{1,0:T(8,128)S(1)}, f32[64,512]{1,0:T(8,128)S(1)}, u32[]{:S(2)}, u32[]{:S(2)}) collective-permute-start(f32[64,512]{1,0:T(8,128)S(1)} %slice_select_fusion.1), channel_id=1, source_target_pairs={{0,8},{2,10},{4,12},{6,14},{8,0},{10,2},{12,4},{14,6},{1,9},{3,11}... | collective-permute-start | bytes 393224 | tf_op jit(solution)/shard_map/ppermute | solution.py:58
  59.6 6.0 %collective-permute-done.2 = f32[64,512]{1,0:T(8,128)S(1)} collective-permute-done((f32[64,512]{1,0:T(8,128)S(1)}, f32[64,512]{1,0:T(8,128)S(1)}, u32[]{:S(2)}, u32[]{:S(2)}) %collective-permute-start.2) | collective-permute-done | bytes 131104 | tf_op jit(solution)/shard_map/ppermute | solution.py:58
  65.6 4.2 %collective-permute-done.5 = f32[64,512]{1,0:T(8,128)S(1)} collective-permute-done((f32[64,512]{1,0:T(8,128)S(1)}, f32[64,512]{1,0:T(8,128)S(1)}, u32[]{:S(2)}, u32[]{:S(2)}) %collective-permute-start.5) | collective-permute-done | bytes 131104 | tf_op jit(solution)/shard_map/ppermute | solution.py:58
  69.8 1.7 %collective-permute-done.11 = f32[64,512]{1,0:T(8,128)S(1)} collective-permute-done((f32[64,512]{1,0:T(8,128)S(1)}, f32[64,512]{1,0:T(8,128)S(1)}, u32[]{:S(2)}, u32[]{:S(2)}) %collective-permute-start.11) | collective-permute-done | bytes 131104 | tf_op jit(solution)/shard_map/ppermute | solution.py:58
  75.0 2.9 %collective-permute-start.13 = (f32[]{:T(128)}, f32[]{:T(128)}, u32[]{:S(2)}, u32[]{:S(2)}) collective-permute-start(f32[]{:T(128)} %add.78), channel_id=1, source_target_pairs={{0,1},{1,0},{2,3},{3,2},{4,5},{5,4},{6,7},{7,6},{8,9},{9,8},{10,11... | collective-permute-start | bytes 20 | tf_op jit(solution)/shard_map/ppermute | solution.py:33
  79.4 1.7 %collective-permute-start.14 = (f32[]{:T(128)}, f32[]{:T(128)}, u32[]{:S(2)}, u32[]{:S(2)}) collective-permute-start(f32[]{:T(128)} %add.79), channel_id=1, source_target_pairs={{0,2},{2,0},{4,6},{6,4},{8,10},{10,8},{12,14},{14,12},{1,3},{3,1},... | collective-permute-start | bytes 20 | tf_op jit(solution)/shard_map/ppermute | solution.py:33
  81.1 2.0 %collective-permute-done.14 = f32[]{:T(128)} collective-permute-done((f32[]{:T(128)}, f32[]{:T(128)}, u32[]{:S(2)}, u32[]{:S(2)}) %collective-permute-start.14) | collective-permute-done | bytes 36 | tf_op jit(solution)/shard_map/ppermute | solution.py:33
  85.1 2.3 %collective-permute-done.15 = f32[]{:T(128)} collective-permute-done((f32[]{:T(128)}, f32[]{:T(128)}, u32[]{:S(2)}, u32[]{:S(2)}) %collective-permute-start.15) | collective-permute-done | bytes 36 | tf_op jit(solution)/shard_map/ppermute | solution.py:33
  88.1 1.9 %collective-permute-start.16 = (f32[]{:T(128)}, f32[]{:T(128)}, u32[]{:S(2)}, u32[]{:S(2)}) collective-permute-start(f32[]{:T(128)} %add.81), channel_id=1, source_target_pairs={{0,8},{2,10},{4,12},{6,14},{8,0},{10,2},{12,4},{14,6},{1,9},{3,11}... | collective-permute-start | bytes 20 | tf_op jit(solution)/shard_map/ppermute | solution.py:33
  90.0 2.7 %collective-permute-done.16 = f32[]{:T(128)} collective-permute-done((f32[]{:T(128)}, f32[]{:T(128)}, u32[]{:S(2)}, u32[]{:S(2)}) %collective-permute-start.16) | collective-permute-done | bytes 36 | tf_op jit(solution)/shard_map/ppermute | solution.py:33
  94.5 7.1 %collective-permute-done.17 = bf16[256,128]{0,1:T(8,128)(2,1)S(1)} collective-permute-done((bf16[256,128]{0,1:T(8,128)(2,1)S(1)}, bf16[256,128]{0,1:T(8,128)(2,1)S(1)}, u32[]{:S(2)}, u32[]{:S(2)}) %collective-permute-start.17) | collective-permute-done | bytes 65568 | tf_op jit(solution)/shard_map/ppermute | solution.py:72
  101.7 2.9 %collective-permute-start.23 = (bf16[256,128]{0,1:T(8,128)(2,1)S(1)}, bf16[256,128]{0,1:T(8,128)(2,1)S(1)}, u32[]{:S(2)}, u32[]{:S(2)}) collective-permute-start(bf16[256,128]{0,1:T(8,128)(2,1)S(1)} %get-tuple-element.60), channel_id=1, source_target_pairs={{0,8},{2,10},{4,12},{6,14},{8,0},{10,2},{12,4},{14,6},{1,9},{3,11}... | collective-permute-start | bytes 196616 | tf_op jit(solution)/shard_map/ppermute | solution.py:72
  104.7 2.6 %collective-permute-start.18 = (bf16[2,256,128]{1,2,0:T(8,128)(2,1)S(1)}, bf16[2,256,128]{1,2,0:T(8,128)(2,1)S(1)}, u32[]{:S(2)}, u32[]{:S(2)}) collective-permute-start(bf16[2,256,128]{1,2,0:T(8,128)(2,1)S(1)} %pad_maximum_fusion.20), channel_id=1, source_target_pairs={{0,4},{2,6},{4,0},{6,2},{8,12},{10,14},{12,8},{14,10},{1,5},{3,7},... | collective-permute-start | bytes 393224 | tf_op jit(solution)/shard_map/ppermute | solution.py:72
  107.7 2.7 %collective-permute-done.26 = bf16[256,128]{0,1:T(8,128)(2,1)S(1)} collective-permute-done((bf16[256,128]{0,1:T(8,128)(2,1)S(1)}, bf16[256,128]{0,1:T(8,128)(2,1)S(1)}, u32[]{:S(2)}, u32[]{:S(2)}) %collective-permute-start.26) | collective-permute-done | bytes 65568 | tf_op jit(solution)/shard_map/ppermute | solution.py:72
  113.9 2.2 %collective-permute-done.21 = bf16[2,256,128]{1,2,0:T(8,128)(2,1)S(1)} collective-permute-done((bf16[2,256,128]{1,2,0:T(8,128)(2,1)S(1)}, bf16[2,256,128]{1,2,0:T(8,128)(2,1)S(1)}, u32[]{:S(2)}, u32[]{:S(2)}) %collective-permute-start.21) | collective-permute-done | bytes 131104 | tf_op jit(solution)/shard_map/ppermute | solution.py:72
  116.2 1.4 %collective-permute-done.24 = bf16[2,256,128]{1,2,0:T(8,128)(2,1)S(1)} collective-permute-done((bf16[2,256,128]{1,2,0:T(8,128)(2,1)S(1)}, bf16[2,256,128]{1,2,0:T(8,128)(2,1)S(1)}, u32[]{:S(2)}, u32[]{:S(2)}) %collective-permute-start.24) | collective-permute-done | bytes 131104 | tf_op jit(solution)/shard_map/ppermute | solution.py:72
  118.1 1.8 %collective-permute-start.25 = (bf16[2,2,256,128]{2,3,1,0:T(8,128)(2,1)S(1)}, bf16[2,2,256,128]{2,3,1,0:T(8,128)(2,1)}, u32[]{:S(2)}, u32[]{:S(2)}) collective-permute-start(bf16[2,2,256,128]{2,3,1,0:T(8,128)(2,1)S(1)} %pad_maximum_fusion.18), channel_id=1, source_target_pairs={{0,4},{2,6},{4,0},{6,2},{8,12},{10,14},{12,8},{14,10},{1,5},{3,7},... | collective-permute-start | bytes 786440 | tf_op jit(solution)/shard_map/ppermute | solution.py:72
  121.4 2.8 %collective-permute-done.22 = bf16[2,2,256,128]{2,3,1,0:T(8,128)(2,1)} collective-permute-done((bf16[2,2,256,128]{2,3,1,0:T(8,128)(2,1)S(1)}, bf16[2,2,256,128]{2,3,1,0:T(8,128)(2,1)}, u32[]{:S(2)}, u32[]{:S(2)}) %collective-permute-start.22) | collective-permute-done | bytes 262176 | tf_op jit(solution)/shard_map/ppermute | solution.py:72
  128.9 1.5 %maximum_bitcast_fusion = bf16[1,4096,256]{2,1,0:T(8,128)(2,1)} fusion(bf16[4096,128]{1,0:T(8,128)(2,1)S(1)} %bitcast.107, bf16[4096,128]{1,0:T(8,128)(2,1)S(1)} %bitcast.106), kind=kLoop, calls=%fused_computation.3 | loop fusion | flops 4194304 | bytes 4194304 | tf_op jit(solution)/shard_map/broadcast_in_dim | solution.py:134
  (133 shorter events, 33.3 us)
Async XLA Ops:
  10.9 16.0 %collective-permute-start = (f32[64,2048]{1,0:T(8,128)}, f32[64,2048]{1,0:T(8,128)}, u32[]{:S(2)}, u32[]{:S(2)}) collective-permute-start(f32[64,2048]{1,0:T(8,128)} %fusion.18), channel_id=1, source_target_pairs={{0,2},{2,0},{4,6},{6,4},{8,10},{10,8},{12,14},{14,12},{1,3},{3,1},... | collective-permute-start | bytes 1572872 | tf_op jit(solution)/shard_map/ppermute | solution.py:58
  16.4 15.2 %collective-permute-start.3 = (f32[64,2048]{1,0:T(8,128)}, f32[64,2048]{1,0:T(8,128)}, u32[]{:S(2)}, u32[]{:S(2)}) collective-permute-start(f32[64,2048]{1,0:T(8,128)} %fusion.16), channel_id=1, source_target_pairs={{0,4},{2,6},{4,0},{6,2},{8,12},{10,14},{12,8},{14,10},{1,5},{3,7},... | collective-permute-start | bytes 1572872 | tf_op jit(solution)/shard_map/ppermute | solution.py:58
  18.9 19.3 %collective-permute-start.6 = (f32[64,2048]{1,0:T(8,128)}, f32[64,2048]{1,0:T(8,128)}, u32[]{:S(2)}, u32[]{:S(2)}) collective-permute-start(f32[64,2048]{1,0:T(8,128)} %fusion.17), channel_id=1, source_target_pairs={{0,2},{2,0},{4,6},{6,4},{8,10},{10,8},{12,14},{14,12},{1,3},{3,1},... | collective-permute-start | bytes 1572872 | tf_op jit(solution)/shard_map/ppermute | solution.py:58
  20.4 28.1 %collective-permute-start.9 = (f32[64,2048]{1,0:T(8,128)}, f32[64,2048]{1,0:T(8,128)}, u32[]{:S(2)}, u32[]{:S(2)}) collective-permute-start(f32[64,2048]{1,0:T(8,128)} %fusion.15), channel_id=1, source_target_pairs={{0,4},{2,6},{4,0},{6,2},{8,12},{10,14},{12,8},{14,10},{1,5},{3,7},... | collective-permute-start | bytes 1572872 | tf_op jit(solution)/shard_map/ppermute | solution.py:58
  25.5 12.6 %copy-start.9 = (f32[64,512]{1,0:T(8,128)S(1)}, f32[64,512]{1,0:T(8,128)}, u32[]{:S(2)}) copy-start(f32[64,512]{1,0:T(8,128)} %copy-done.8) | copy-start | bytes 393220
  25.6 12.6 %copy-start.11 = (f32[64,512]{1,0:T(8,128)S(1)}, f32[64,512]{1,0:T(8,128)}, u32[]{:S(2)}) copy-start(f32[64,512]{1,0:T(8,128)} %copy-done.10) | copy-start | bytes 393220
  28.4 24.0 %collective-permute-start.1 = (f32[64,1024]{1,0:T(8,128)S(1)}, f32[64,1024]{1,0:T(8,128)S(1)}, u32[]{:S(2)}, u32[]{:S(2)}) collective-permute-start(f32[64,1024]{1,0:T(8,128)S(1)} %fusion.23), channel_id=1, source_target_pairs={{0,4},{2,6},{4,0},{6,2},{8,12},{10,14},{12,8},{14,10},{1,5},{3,7},... | collective-permute-start | bytes 786440 | tf_op jit(solution)/shard_map/ppermute | solution.py:58
  32.8 20.9 %collective-permute-start.4 = (f32[64,1024]{1,0:T(8,128)S(1)}, f32[64,1024]{1,0:T(8,128)S(1)}, u32[]{:S(2)}, u32[]{:S(2)}) collective-permute-start(f32[64,1024]{1,0:T(8,128)S(1)} %fusion.22), channel_id=1, source_target_pairs={{0,2},{2,0},{4,6},{6,4},{8,10},{10,8},{12,14},{14,12},{1,3},{3,1},... | collective-permute-start | bytes 786440 | tf_op jit(solution)/shard_map/ppermute | solution.py:58
  39.4 16.3 %collective-permute-start.7 = (f32[64,1024]{1,0:T(8,128)S(1)}, f32[64,1024]{1,0:T(8,128)S(1)}, u32[]{:S(2)}, u32[]{:S(2)}) collective-permute-start(f32[64,1024]{1,0:T(8,128)S(1)} %slice_select_fusion), channel_id=1, source_target_pairs={{0,8},{2,10},{4,12},{6,14},{8,0},{10,2},{12,4},{14,6},{1,9},{3,11}... | collective-permute-start | bytes 786440 | tf_op jit(solution)/shard_map/ppermute | solution.py:58
  49.6 43.8 %copy-start.1 = (f32[1,512,256]{1,2,0:T(8,128)S(1)}, f32[1,512,256]{1,2,0:T(8,128)}, u32[]{:S(2)}) copy-start(f32[1,512,256]{1,2,0:T(8,128)} %copy.22) | copy-start | bytes 1572868
  49.6 6.9 %collective-permute-start.10 = (f32[64,1024]{1,0:T(8,128)S(1)}, f32[64,1024]{1,0:T(8,128)S(1)}, u32[]{:S(2)}, u32[]{:S(2)}) collective-permute-start(f32[64,1024]{1,0:T(8,128)S(1)} %fusion.21), channel_id=1, source_target_pairs={{0,2},{2,0},{4,6},{6,4},{8,10},{10,8},{12,14},{14,12},{1,3},{3,1},... | collective-permute-start | bytes 786440 | tf_op jit(solution)/shard_map/ppermute | solution.py:58
  52.5 13.0 %collective-permute-start.2 = (f32[64,512]{1,0:T(8,128)S(1)}, f32[64,512]{1,0:T(8,128)S(1)}, u32[]{:S(2)}, u32[]{:S(2)}) collective-permute-start(f32[64,512]{1,0:T(8,128)S(1)} %slice_select_fusion.4), channel_id=1, source_target_pairs={{0,8},{2,10},{4,12},{6,14},{8,0},{10,2},{12,4},{14,6},{1,9},{3,11}... | collective-permute-start | bytes 393224 | tf_op jit(solution)/shard_map/ppermute | solution.py:58
  53.8 16.0 %collective-permute-start.5 = (f32[64,512]{1,0:T(8,128)S(1)}, f32[64,512]{1,0:T(8,128)S(1)}, u32[]{:S(2)}, u32[]{:S(2)}) collective-permute-start(f32[64,512]{1,0:T(8,128)S(1)} %slice_select_fusion.3), channel_id=1, source_target_pairs={{0,8},{2,10},{4,12},{6,14},{8,0},{10,2},{12,4},{14,6},{1,9},{3,11}... | collective-permute-start | bytes 393224 | tf_op jit(solution)/shard_map/ppermute | solution.py:58
  55.8 14.0 %collective-permute-start.8 = (f32[64,512]{1,0:T(8,128)S(1)}, f32[64,512]{1,0:T(8,128)S(1)}, u32[]{:S(2)}, u32[]{:S(2)}) collective-permute-start(f32[64,512]{1,0:T(8,128)S(1)} %slice_select_fusion.2), channel_id=1, source_target_pairs={{0,4},{2,6},{4,0},{6,2},{8,12},{10,14},{12,8},{14,10},{1,5},{3,7},... | collective-permute-start | bytes 393224 | tf_op jit(solution)/shard_map/ppermute | solution.py:58
  56.6 15.0 %collective-permute-start.11 = (f32[64,512]{1,0:T(8,128)S(1)}, f32[64,512]{1,0:T(8,128)S(1)}, u32[]{:S(2)}, u32[]{:S(2)}) collective-permute-start(f32[64,512]{1,0:T(8,128)S(1)} %slice_select_fusion.1), channel_id=1, source_target_pairs={{0,8},{2,10},{4,12},{6,14},{8,0},{10,2},{12,4},{14,6},{1,9},{3,11}... | collective-permute-start | bytes 393224 | tf_op jit(solution)/shard_map/ppermute | solution.py:58
  72.4 1.3 %collective-permute-start.12 = (f32[]{:T(128)}, f32[]{:T(128)}, u32[]{:S(2)}, u32[]{:S(2)}) collective-permute-start(f32[]{:T(128)} %multiply_reduce_fusion), channel_id=1, source_target_pairs={{0,16},{16,0},{1,17},{17,1},{2,18},{18,2},{3,19},{19,3},{4,20},{20... | collective-permute-start | bytes 20 | tf_op jit(solution)/shard_map/ppermute | solution.py:33
  75.0 3.7 %collective-permute-start.13 = (f32[]{:T(128)}, f32[]{:T(128)}, u32[]{:S(2)}, u32[]{:S(2)}) collective-permute-start(f32[]{:T(128)} %add.78), channel_id=1, source_target_pairs={{0,1},{1,0},{2,3},{3,2},{4,5},{5,4},{6,7},{7,6},{8,9},{9,8},{10,11... | collective-permute-start | bytes 20 | tf_op jit(solution)/shard_map/ppermute | solution.py:33
  79.4 3.7 %collective-permute-start.14 = (f32[]{:T(128)}, f32[]{:T(128)}, u32[]{:S(2)}, u32[]{:S(2)}) collective-permute-start(f32[]{:T(128)} %add.79), channel_id=1, source_target_pairs={{0,2},{2,0},{4,6},{6,4},{8,10},{10,8},{12,14},{14,12},{1,3},{3,1},... | collective-permute-start | bytes 20 | tf_op jit(solution)/shard_map/ppermute | solution.py:33
  83.8 3.7 %collective-permute-start.15 = (f32[]{:T(128)}, f32[]{:T(128)}, u32[]{:S(2)}, u32[]{:S(2)}) collective-permute-start(f32[]{:T(128)} %add.80), channel_id=1, source_target_pairs={{0,4},{2,6},{4,0},{6,2},{8,12},{10,14},{12,8},{14,10},{1,5},{3,7},... | collective-permute-start | bytes 20 | tf_op jit(solution)/shard_map/ppermute | solution.py:33
  88.1 4.6 %collective-permute-start.16 = (f32[]{:T(128)}, f32[]{:T(128)}, u32[]{:S(2)}, u32[]{:S(2)}) collective-permute-start(f32[]{:T(128)} %add.81), channel_id=1, source_target_pairs={{0,8},{2,10},{4,12},{6,14},{8,0},{10,2},{12,4},{14,6},{1,9},{3,11}... | collective-permute-start | bytes 20 | tf_op jit(solution)/shard_map/ppermute | solution.py:33
  93.9 7.7 %collective-permute-start.17 = (bf16[256,128]{0,1:T(8,128)(2,1)S(1)}, bf16[256,128]{0,1:T(8,128)(2,1)S(1)}, u32[]{:S(2)}, u32[]{:S(2)}) collective-permute-start(bf16[256,128]{0,1:T(8,128)(2,1)S(1)} %slice.294), channel_id=1, source_target_pairs={{0,8},{2,10},{4,12},{6,14},{8,0},{10,2},{12,4},{14,6},{1,9},{3,11}... | collective-permute-start | bytes 196616 | tf_op jit(solution)/shard_map/ppermute | solution.py:72
  101.6 5.7 %collective-permute-start.20 = (bf16[256,128]{0,1:T(8,128)(2,1)S(1)}, bf16[256,128]{0,1:T(8,128)(2,1)S(1)}, u32[]{:S(2)}, u32[]{:S(2)}) collective-permute-start(bf16[256,128]{0,1:T(8,128)(2,1)S(1)} %get-tuple-element.61), channel_id=1, source_target_pairs={{0,8},{2,10},{4,12},{6,14},{8,0},{10,2},{12,4},{14,6},{1,9},{3,11}... | collective-permute-start | bytes 196616 | tf_op jit(solution)/shard_map/ppermute | solution.py:72
  101.7 6.0 %collective-permute-start.23 = (bf16[256,128]{0,1:T(8,128)(2,1)S(1)}, bf16[256,128]{0,1:T(8,128)(2,1)S(1)}, u32[]{:S(2)}, u32[]{:S(2)}) collective-permute-start(bf16[256,128]{0,1:T(8,128)(2,1)S(1)} %get-tuple-element.60), channel_id=1, source_target_pairs={{0,8},{2,10},{4,12},{6,14},{8,0},{10,2},{12,4},{14,6},{1,9},{3,11}... | collective-permute-start | bytes 196616 | tf_op jit(solution)/shard_map/ppermute | solution.py:72
  104.6 5.8 %collective-permute-start.26 = (bf16[256,128]{0,1:T(8,128)(2,1)S(1)}, bf16[256,128]{0,1:T(8,128)(2,1)S(1)}, u32[]{:S(2)}, u32[]{:S(2)}) collective-permute-start(bf16[256,128]{0,1:T(8,128)(2,1)S(1)} %get-tuple-element.59), channel_id=1, source_target_pairs={{0,8},{2,10},{4,12},{6,14},{8,0},{10,2},{12,4},{14,6},{1,9},{3,11}... | collective-permute-start | bytes 196616 | tf_op jit(solution)/shard_map/ppermute | solution.py:72
  104.7 8.0 %collective-permute-start.18 = (bf16[2,256,128]{1,2,0:T(8,128)(2,1)S(1)}, bf16[2,256,128]{1,2,0:T(8,128)(2,1)S(1)}, u32[]{:S(2)}, u32[]{:S(2)}) collective-permute-start(bf16[2,256,128]{1,2,0:T(8,128)(2,1)S(1)} %pad_maximum_fusion.20), channel_id=1, source_target_pairs={{0,4},{2,6},{4,0},{6,2},{8,12},{10,14},{12,8},{14,10},{1,5},{3,7},... | collective-permute-start | bytes 393224 | tf_op jit(solution)/shard_map/ppermute | solution.py:72
  110.5 5.7 %collective-permute-start.21 = (bf16[2,256,128]{1,2,0:T(8,128)(2,1)S(1)}, bf16[2,256,128]{1,2,0:T(8,128)(2,1)S(1)}, u32[]{:S(2)}, u32[]{:S(2)}) collective-permute-start(bf16[2,256,128]{1,2,0:T(8,128)(2,1)S(1)} %pad_maximum_fusion.21), channel_id=1, source_target_pairs={{0,2},{2,0},{4,6},{6,4},{8,10},{10,8},{12,14},{14,12},{1,3},{3,1},... | collective-permute-start | bytes 393224 | tf_op jit(solution)/shard_map/ppermute | solution.py:72
  111.6 6.0 %collective-permute-start.24 = (bf16[2,256,128]{1,2,0:T(8,128)(2,1)S(1)}, bf16[2,256,128]{1,2,0:T(8,128)(2,1)S(1)}, u32[]{:S(2)}, u32[]{:S(2)}) collective-permute-start(bf16[2,256,128]{1,2,0:T(8,128)(2,1)S(1)} %pad_maximum_fusion.22), channel_id=1, source_target_pairs={{0,2},{2,0},{4,6},{6,4},{8,10},{10,8},{12,14},{14,12},{1,3},{3,1},... | collective-permute-start | bytes 393224 | tf_op jit(solution)/shard_map/ppermute | solution.py:72
  112.6 7.2 %collective-permute-start.27 = (bf16[2,256,128]{1,2,0:T(8,128)(2,1)S(1)}, bf16[2,256,128]{1,2,0:T(8,128)(2,1)S(1)}, u32[]{:S(2)}, u32[]{:S(2)}) collective-permute-start(bf16[2,256,128]{1,2,0:T(8,128)(2,1)S(1)} %pad_maximum_fusion.23), channel_id=1, source_target_pairs={{0,4},{2,6},{4,0},{6,2},{8,12},{10,14},{12,8},{14,10},{1,5},{3,7},... | collective-permute-start | bytes 393224 | tf_op jit(solution)/shard_map/ppermute | solution.py:72
  112.8 8.2 %collective-permute-start.19 = (bf16[2,2,256,128]{2,3,1,0:T(8,128)(2,1)S(1)}, bf16[2,2,256,128]{2,3,1,0:T(8,128)(2,1)S(1)}, u32[]{:S(2)}, u32[]{:S(2)}) collective-permute-start(bf16[2,2,256,128]{2,3,1,0:T(8,128)(2,1)S(1)} %pad_maximum_fusion.16), channel_id=1, source_target_pairs={{0,2},{2,0},{4,6},{6,4},{8,10},{10,8},{12,14},{14,12},{1,3},{3,1},... | collective-permute-start | bytes 786440 | tf_op jit(solution)/shard_map/ppermute | solution.py:72
  117.7 6.5 %collective-permute-start.22 = (bf16[2,2,256,128]{2,3,1,0:T(8,128)(2,1)S(1)}, bf16[2,2,256,128]{2,3,1,0:T(8,128)(2,1)}, u32[]{:S(2)}, u32[]{:S(2)}) collective-permute-start(bf16[2,2,256,128]{2,3,1,0:T(8,128)(2,1)S(1)} %pad_maximum_fusion.17), channel_id=1, source_target_pairs={{0,4},{2,6},{4,0},{6,2},{8,12},{10,14},{12,8},{14,10},{1,5},{3,7},... | collective-permute-start | bytes 786440 | tf_op jit(solution)/shard_map/ppermute | solution.py:72
  118.1 8.9 %collective-permute-start.25 = (bf16[2,2,256,128]{2,3,1,0:T(8,128)(2,1)S(1)}, bf16[2,2,256,128]{2,3,1,0:T(8,128)(2,1)}, u32[]{:S(2)}, u32[]{:S(2)}) collective-permute-start(bf16[2,2,256,128]{2,3,1,0:T(8,128)(2,1)S(1)} %pad_maximum_fusion.18), channel_id=1, source_target_pairs={{0,4},{2,6},{4,0},{6,2},{8,12},{10,14},{12,8},{14,10},{1,5},{3,7},... | collective-permute-start | bytes 786440 | tf_op jit(solution)/shard_map/ppermute | solution.py:72
  119.9 8.4 %collective-permute-start.28 = (bf16[2,2,256,128]{2,3,1,0:T(8,128)(2,1)S(1)}, bf16[2,2,256,128]{2,3,1,0:T(8,128)(2,1)S(1)}, u32[]{:S(2)}, u32[]{:S(2)}) collective-permute-start(bf16[2,2,256,128]{2,3,1,0:T(8,128)(2,1)S(1)} %pad_maximum_fusion.19), channel_id=1, source_target_pairs={{0,2},{2,0},{4,6},{6,4},{8,10},{10,8},{12,14},{14,12},{1,3},{3,1},... | collective-permute-start | bytes 786440 | tf_op jit(solution)/shard_map/ppermute | solution.py:72
  (17 other events, 132.4 us)

commit v13 on v11

--- a/solution.py
+++ b/solution.py
@@ -105,7 +105,7 @@
     return jnp.concatenate(
         [
             doubling_gather(part[:, :half], axis, first[::-1]),
-            doubling_gather(part[:, half:], axis, second[::-1]),
+            doubling_gather(part[:, half:], axis, bit_orders(size)[2]),
         ],
         axis=1,
     )

time: 131 us -> 130 us (level)
  waiting for transfers between devices: 64 us -> 60.8 us
  starting transfers between devices: 30.5 us -> 33.2 us
    ppermute x6, waiting for transfers between devices: 27.3 us -> 24.1 us  [doubling_gather(): other = lax.ppermute(current, axis, pairs)]
    ppermute x6, starting transfers between devices: 4.59 us -> 7.25 us  [doubling_gather(): other = lax.ppermute(current, axis, pairs)]
  transfers between devices with their start and end apart: 23 -> 23, of which waited for: 19 -> 17; matrix products, arithmetic and copies ran while one was open for 12% -> 12% of each run, Pallas kernels for 0% -> 0%
where the time goes in v13:
time: 130 us
  waiting for transfers between devices  60.8 us (47%)
  starting transfers between devices  33.2 us (26%)
  other arithmetic  14.5 us (11%)
  local copies, waits for them, and re-layouts  9.86 us (8%)
  matrix products  6.18 us (5%)
  between operations  5.05 us (4%)
    ppermute x12, waiting for transfers between devices, halving_scatter(): blocks = keep + lax.ppermute(send, axis, pairs)  27.5 us
    ppermute x6, waiting for transfers between devices, doubling_gather(): other = lax.ppermute(current, axis, pairs)  24.1 us
    ppermute x12, starting transfers between devices, halving_scatter(): blocks = keep + lax.ppermute(send, axis, pairs)  18 us
    ppermute x5, waiting for transfers between devices, butterfly_sum(): value = value + lax.ppermute(value, axis, pairs)  9.18 us
    ppermute x5, starting transfers between devices, butterfly_sum(): value = value + lax.ppermute(value, axis, pairs)  7.88 us
    ppermute x6, starting transfers between devices, doubling_gather(): other = lax.ppermute(current, axis, pairs)  7.25 us
    unnamed x43, local copies, waits for them, and re-layouts  6.55 us
    dot_general x1, matrix products, slot_term(): lax.dot_general(weighted, columns, (((0,), (0,)), ((), ())), preferred_el...  6.18 us
  transfers between devices with their start and end apart: 23, of which 17 were waited for; matrix products, arithmetic and copies ran while one was open for 12% of the time, Pallas kernels for 0%

profile of v13, /device:TPU:0, one launch (start us, length us, event | category | flops | bytes accessed | tf_op | source)
XLA Modules:
  0.0 129.6 jit_solution(13189395300573710963)
XLA Ops:
  0.0 1.4 %convert_bitcast_fusion = (bf16[8]{0:T(256)(128)(2,1)S(1)}, s32[]{:T(128)}) fusion(s32[1,8]{1,0:T(1,128)} %param.8), kind=kLoop, calls=%fused_computation.76 | loop fusion | flops 15 | bytes 52 | tf_op jit(solution)/shard_map/convert_element_type | solution.py:16
  1.4 6.2 %fusion.2 = f32[256,4096]{1,0:T(8,128)S(1)} fusion(bf16[1,8,128,4096]{3,2,1,0:T(8,128)(2,1)} %param.6, bf16[1,8,128,256]{3,2,1,0:T(8,128)(2,1)} %param.7, bf16[8]{0:T(256)(128)(2,1)S(1)} %get-tuple-element.57), kind=kOutput, calls=%fused_computation.2 | convolution fusion | flops 2147745792 | bytes 13107216 | tf_op jit(solution)/shard_map/dot_general | solution.py:19
  7.6 1.9 %copy-done = f32[256,4096]{1,0:T(8,128)} copy-done((f32[256,4096]{1,0:T(8,128)}, f32[256,4096]{1,0:T(8,128)S(1)}, u32[]{:S(2)}) %copy-start) | copy-done | bytes 4194328
  10.9 2.9 %collective-permute-start = (f32[64,2048]{1,0:T(8,128)}, f32[64,2048]{1,0:T(8,128)}, u32[]{:S(2)}, u32[]{:S(2)}) collective-permute-start(f32[64,2048]{1,0:T(8,128)} %fusion.18), channel_id=1, source_target_pairs={{0,2},{2,0},{4,6},{6,4},{8,10},{10,8},{12,14},{14,12},{1,3},{3,1},... | collective-permute-start | bytes 1572872 | tf_op jit(solution)/shard_map/ppermute | solution.py:58
  13.9 1.6 %fusion.25 = (f32[64,1024]{1,0:T(8,128)S(1)}, f32[64,1024]{1,0:T(8,128)S(1)}, f32[64,1024]{1,0:T(8,128)S(1)}, f32[64,1024]{1,0:T(8,128)S(1)}, f32[64,1024]{1,0:T...) fusion(f32[256,4096]{1,0:T(8,128)} %copy-done), kind=kLoop, calls=%fused_computation.78 | loop fusion | bytes 4194304 | tf_op jit(solution)/shard_map/slice | solution.py:54
  16.4 1.6 %collective-permute-start.3 = (f32[64,2048]{1,0:T(8,128)}, f32[64,2048]{1,0:T(8,128)}, u32[]{:S(2)}, u32[]{:S(2)}) collective-permute-start(f32[64,2048]{1,0:T(8,128)} %fusion.16), channel_id=1, source_target_pairs={{0,4},{2,6},{4,0},{6,2},{8,12},{10,14},{12,8},{14,10},{1,5},{3,7},... | collective-permute-start | bytes 1572872 | tf_op jit(solution)/shard_map/ppermute | solution.py:58
  23.5 2.0 %copy.14 = f32[1,512,256]{1,2,0:T(8,128)} copy(f32[1,512,256]{2,1,0:T(8,128)} %param.9) | data formatting | bytes 1048576 | tf_op args[3]
  25.6 1.3 %collective-permute-done = f32[64,2048]{1,0:T(8,128)} collective-permute-done((f32[64,2048]{1,0:T(8,128)}, f32[64,2048]{1,0:T(8,128)}, u32[]{:S(2)}, u32[]{:S(2)}) %collective-permute-start) | collective-permute-done | bytes 524320 | tf_op jit(solution)/shard_map/ppermute | solution.py:58
  26.9 1.4 %select_add_fusion.3 = f32[64,2048]{1,0:T(8,128)S(1)} fusion(f32[64,2048]{1,0:T(8,128)} %collective-permute-done, f32[64,512]{1,0:T(8,128)} %copy-done.13, f32[64,512]{1,0:T(8,128)} %copy-done.14, f32[64,512]{1,0:T(8,128)} %copy-done.15, f32[64,512]{1,0:T(8,128)} %copy-done.16, f32[64,512]{1,0:T(8,128)} %copy-done.17, f32[64,512]{1,0:T(8,128)} %copy-done.18, ...), kind=kLoop, calls=%fused_computation.35 | loop fusion | flops 1048576 | bytes 2097153 | tf_op jit(solution)/shard_map/add | solution.py:58
  28.4 2.2 %collective-permute-start.1 = (f32[64,1024]{1,0:T(8,128)S(1)}, f32[64,1024]{1,0:T(8,128)S(1)}, u32[]{:S(2)}, u32[]{:S(2)}) collective-permute-start(f32[64,1024]{1,0:T(8,128)S(1)} %fusion.23), channel_id=1, source_target_pairs={{0,4},{2,6},{4,0},{6,2},{8,12},{10,14},{12,8},{14,10},{1,5},{3,7},... | collective-permute-start | bytes 786440 | tf_op jit(solution)/shard_map/ppermute | solution.py:58
  33.4 4.7 %collective-permute-done.6 = f32[64,2048]{1,0:T(8,128)} collective-permute-done((f32[64,2048]{1,0:T(8,128)}, f32[64,2048]{1,0:T(8,128)}, u32[]{:S(2)}, u32[]{:S(2)}) %collective-permute-start.6) | collective-permute-done | bytes 524320 | tf_op jit(solution)/shard_map/ppermute | solution.py:58
  39.4 3.2 %collective-permute-start.7 = (f32[64,1024]{1,0:T(8,128)S(1)}, f32[64,1024]{1,0:T(8,128)S(1)}, u32[]{:S(2)}, u32[]{:S(2)}) collective-permute-start(f32[64,1024]{1,0:T(8,128)S(1)} %slice_select_fusion), channel_id=1, source_target_pairs={{0,8},{2,10},{4,12},{6,14},{8,0},{10,2},{12,4},{14,6},{1,9},{3,11}... | collective-permute-start | bytes 786440 | tf_op jit(solution)/shard_map/ppermute | solution.py:58
  42.6 5.8 %collective-permute-done.9 = f32[64,2048]{1,0:T(8,128)} collective-permute-done((f32[64,2048]{1,0:T(8,128)}, f32[64,2048]{1,0:T(8,128)}, u32[]{:S(2)}, u32[]{:S(2)}) %collective-permute-start.9) | collective-permute-done | bytes 524320 | tf_op jit(solution)/shard_map/ppermute | solution.py:58
  49.7 2.7 %collective-permute-done.1 = f32[64,1024]{1,0:T(8,128)S(1)} collective-permute-done((f32[64,1024]{1,0:T(8,128)S(1)}, f32[64,1024]{1,0:T(8,128)S(1)}, u32[]{:S(2)}, u32[]{:S(2)}) %collective-permute-start.1) | collective-permute-done | bytes 262176 | tf_op jit(solution)/shard_map/ppermute | solution.py:58
  53.8 1.9 %collective-permute-start.5 = (f32[64,512]{1,0:T(8,128)S(1)}, f32[64,512]{1,0:T(8,128)S(1)}, u32[]{:S(2)}, u32[]{:S(2)}) collective-permute-start(f32[64,512]{1,0:T(8,128)S(1)} %slice_select_fusion.3), channel_id=1, source_target_pairs={{0,8},{2,10},{4,12},{6,14},{8,0},{10,2},{12,4},{14,6},{1,9},{3,11}... | collective-permute-start | bytes 393224 | tf_op jit(solution)/shard_map/ppermute | solution.py:58
  56.6 3.0 %collective-permute-start.11 = (f32[64,512]{1,0:T(8,128)S(1)}, f32[64,512]{1,0:T(8,128)S(1)}, u32[]{:S(2)}, u32[]{:S(2)}) collective-permute-start(f32[64,512]{1,0:T(8,128)S(1)} %slice_select_fusion.1), channel_id=1, source_target_pairs={{0,8},{2,10},{4,12},{6,14},{8,0},{10,2},{12,4},{14,6},{1,9},{3,11}... | collective-permute-start | bytes 393224 | tf_op jit(solution)/shard_map/ppermute | solution.py:58
  59.6 6.0 %collective-permute-done.2 = f32[64,512]{1,0:T(8,128)S(1)} collective-permute-done((f32[64,512]{1,0:T(8,128)S(1)}, f32[64,512]{1,0:T(8,128)S(1)}, u32[]{:S(2)}, u32[]{:S(2)}) %collective-permute-start.2) | collective-permute-done | bytes 131104 | tf_op jit(solution)/shard_map/ppermute | solution.py:58
  65.6 4.2 %collective-permute-done.5 = f32[64,512]{1,0:T(8,128)S(1)} collective-permute-done((f32[64,512]{1,0:T(8,128)S(1)}, f32[64,512]{1,0:T(8,128)S(1)}, u32[]{:S(2)}, u32[]{:S(2)}) %collective-permute-start.5) | collective-permute-done | bytes 131104 | tf_op jit(solution)/shard_map/ppermute | solution.py:58
  69.9 1.7 %collective-permute-done.11 = f32[64,512]{1,0:T(8,128)S(1)} collective-permute-done((f32[64,512]{1,0:T(8,128)S(1)}, f32[64,512]{1,0:T(8,128)S(1)}, u32[]{:S(2)}, u32[]{:S(2)}) %collective-permute-start.11) | collective-permute-done | bytes 131104 | tf_op jit(solution)/shard_map/ppermute | solution.py:58
  75.0 2.9 %collective-permute-start.13 = (f32[]{:T(128)}, f32[]{:T(128)}, u32[]{:S(2)}, u32[]{:S(2)}) collective-permute-start(f32[]{:T(128)} %add.78), channel_id=1, source_target_pairs={{0,1},{1,0},{2,3},{3,2},{4,5},{5,4},{6,7},{7,6},{8,9},{9,8},{10,11... | collective-permute-start | bytes 20 | tf_op jit(solution)/shard_map/ppermute | solution.py:33
  79.4 1.7 %collective-permute-start.14 = (f32[]{:T(128)}, f32[]{:T(128)}, u32[]{:S(2)}, u32[]{:S(2)}) collective-permute-start(f32[]{:T(128)} %add.79), channel_id=1, source_target_pairs={{0,2},{2,0},{4,6},{6,4},{8,10},{10,8},{12,14},{14,12},{1,3},{3,1},... | collective-permute-start | bytes 20 | tf_op jit(solution)/shard_map/ppermute | solution.py:33
  81.1 2.0 %collective-permute-done.14 = f32[]{:T(128)} collective-permute-done((f32[]{:T(128)}, f32[]{:T(128)}, u32[]{:S(2)}, u32[]{:S(2)}) %collective-permute-start.14) | collective-permute-done | bytes 36 | tf_op jit(solution)/shard_map/ppermute | solution.py:33
  83.7 1.4 %collective-permute-start.15 = (f32[]{:T(128)}, f32[]{:T(128)}, u32[]{:S(2)}, u32[]{:S(2)}) collective-permute-start(f32[]{:T(128)} %add.80), channel_id=1, source_target_pairs={{0,4},{2,6},{4,0},{6,2},{8,12},{10,14},{12,8},{14,10},{1,5},{3,7},... | collective-permute-start | bytes 20 | tf_op jit(solution)/shard_map/ppermute | solution.py:33
  85.1 2.3 %collective-permute-done.15 = f32[]{:T(128)} collective-permute-done((f32[]{:T(128)}, f32[]{:T(128)}, u32[]{:S(2)}, u32[]{:S(2)}) %collective-permute-start.15) | collective-permute-done | bytes 36 | tf_op jit(solution)/shard_map/ppermute | solution.py:33
  88.1 1.9 %collective-permute-start.16 = (f32[]{:T(128)}, f32[]{:T(128)}, u32[]{:S(2)}, u32[]{:S(2)}) collective-permute-start(f32[]{:T(128)} %add.81), channel_id=1, source_target_pairs={{0,8},{2,10},{4,12},{6,14},{8,0},{10,2},{12,4},{14,6},{1,9},{3,11}... | collective-permute-start | bytes 20 | tf_op jit(solution)/shard_map/ppermute | solution.py:33
  90.0 2.7 %collective-permute-done.16 = f32[]{:T(128)} collective-permute-done((f32[]{:T(128)}, f32[]{:T(128)}, u32[]{:S(2)}, u32[]{:S(2)}) %collective-permute-start.16) | collective-permute-done | bytes 36 | tf_op jit(solution)/shard_map/ppermute | solution.py:33
  95.6 9.5 %collective-permute-done.17 = bf16[512,128]{0,1:T(8,128)(2,1)S(1)} collective-permute-done((bf16[512,128]{0,1:T(8,128)(2,1)S(1)}, bf16[512,128]{0,1:T(8,128)(2,1)S(1)}, u32[]{:S(2)}, u32[]{:S(2)}) %collective-permute-start.17) | collective-permute-done | bytes 131104 | tf_op jit(solution)/shard_map/ppermute | solution.py:72
  105.3 2.6 %collective-permute-start.21 = (bf16[2,512,128]{1,2,0:T(8,128)(2,1)S(1)}, bf16[2,512,128]{1,2,0:T(8,128)(2,1)S(1)}, u32[]{:S(2)}, u32[]{:S(2)}) collective-permute-start(bf16[2,512,128]{1,2,0:T(8,128)(2,1)S(1)} %pad_maximum_fusion.17), channel_id=1, source_target_pairs={{0,8},{2,10},{4,12},{6,14},{8,0},{10,2},{12,4},{14,6},{1,9},{3,11}... | collective-permute-start | bytes 786440 | tf_op jit(solution)/shard_map/ppermute | solution.py:72
  107.9 8.2 %collective-permute-done.18 = bf16[2,512,128]{1,2,0:T(8,128)(2,1)S(1)} collective-permute-done((bf16[2,512,128]{1,2,0:T(8,128)(2,1)S(1)}, bf16[2,512,128]{1,2,0:T(8,128)(2,1)S(1)}, u32[]{:S(2)}, u32[]{:S(2)}) %collective-permute-start.18) | collective-permute-done | bytes 262176 | tf_op jit(solution)/shard_map/ppermute | solution.py:72
  117.1 2.7 %collective-permute-start.22 = (bf16[2,2,512,128]{2,3,1,0:T(8,128)(2,1)}, bf16[2,2,512,128]{2,3,1,0:T(8,128)(2,1)S(1)}, u32[]{:S(2)}, u32[]{:S(2)}) collective-permute-start(bf16[2,2,512,128]{2,3,1,0:T(8,128)(2,1)} %pad_maximum_fusion.9), channel_id=1, source_target_pairs={{0,4},{2,6},{4,0},{6,2},{8,12},{10,14},{12,8},{14,10},{1,5},{3,7},... | collective-permute-start | bytes 1572872 | tf_op jit(solution)/shard_map/ppermute | solution.py:72
  119.9 5.6 %collective-permute-done.19 = bf16[2,2,512,128]{2,3,1,0:T(8,128)(2,1)S(1)} collective-permute-done((bf16[2,2,512,128]{2,3,1,0:T(8,128)(2,1)S(1)}, bf16[2,2,512,128]{2,3,1,0:T(8,128)(2,1)S(1)}, u32[]{:S(2)}, u32[]{:S(2)}) %collective-permute-start.19) | collective-permute-done | bytes 524320 | tf_op jit(solution)/shard_map/ppermute | solution.py:72
  128.1 1.5 %maximum_bitcast_fusion = bf16[1,4096,256]{2,1,0:T(8,128)(2,1)} fusion(bf16[4096,128]{1,0:T(8,128)(2,1)S(1)} %bitcast.75, bf16[4096,128]{1,0:T(8,128)(2,1)S(1)} %bitcast.74), kind=kLoop, calls=%fused_computation.3 | loop fusion | flops 4194304 | bytes 4194304 | tf_op jit(solution)/shard_map/broadcast_in_dim | solution.py:132
  (105 shorter events, 23.6 us)
Async XLA Ops:
  9.8 11.2 %copy-start.12 = (f32[64,512]{1,0:T(8,128)}, f32[64,512]{1,0:T(8,128)S(1)}, u32[]{:S(2)}) copy-start(f32[64,512]{1,0:T(8,128)S(1)} %get-tuple-element.5) | copy-start | bytes 393220
  9.8 11.2 %copy-start.13 = (f32[64,512]{1,0:T(8,128)}, f32[64,512]{1,0:T(8,128)S(1)}, u32[]{:S(2)}) copy-start(f32[64,512]{1,0:T(8,128)S(1)} %get-tuple-element.14) | copy-start | bytes 393220
  9.8 11.2 %copy-start.14 = (f32[64,512]{1,0:T(8,128)}, f32[64,512]{1,0:T(8,128)S(1)}, u32[]{:S(2)}) copy-start(f32[64,512]{1,0:T(8,128)S(1)} %get-tuple-element.15) | copy-start | bytes 393220
  10.9 16.0 %collective-permute-start = (f32[64,2048]{1,0:T(8,128)}, f32[64,2048]{1,0:T(8,128)}, u32[]{:S(2)}, u32[]{:S(2)}) collective-permute-start(f32[64,2048]{1,0:T(8,128)} %fusion.18), channel_id=1, source_target_pairs={{0,2},{2,0},{4,6},{6,4},{8,10},{10,8},{12,14},{14,12},{1,3},{3,1},... | collective-permute-start | bytes 1572872 | tf_op jit(solution)/shard_map/ppermute | solution.py:58
  16.4 15.2 %collective-permute-start.3 = (f32[64,2048]{1,0:T(8,128)}, f32[64,2048]{1,0:T(8,128)}, u32[]{:S(2)}, u32[]{:S(2)}) collective-permute-start(f32[64,2048]{1,0:T(8,128)} %fusion.16), channel_id=1, source_target_pairs={{0,4},{2,6},{4,0},{6,2},{8,12},{10,14},{12,8},{14,10},{1,5},{3,7},... | collective-permute-start | bytes 1572872 | tf_op jit(solution)/shard_map/ppermute | solution.py:58
  18.9 19.3 %collective-permute-start.6 = (f32[64,2048]{1,0:T(8,128)}, f32[64,2048]{1,0:T(8,128)}, u32[]{:S(2)}, u32[]{:S(2)}) collective-permute-start(f32[64,2048]{1,0:T(8,128)} %fusion.17), channel_id=1, source_target_pairs={{0,2},{2,0},{4,6},{6,4},{8,10},{10,8},{12,14},{14,12},{1,3},{3,1},... | collective-permute-start | bytes 1572872 | tf_op jit(solution)/shard_map/ppermute | solution.py:58
  20.3 28.1 %collective-permute-start.9 = (f32[64,2048]{1,0:T(8,128)}, f32[64,2048]{1,0:T(8,128)}, u32[]{:S(2)}, u32[]{:S(2)}) collective-permute-start(f32[64,2048]{1,0:T(8,128)} %fusion.15), channel_id=1, source_target_pairs={{0,4},{2,6},{4,0},{6,2},{8,12},{10,14},{12,8},{14,10},{1,5},{3,7},... | collective-permute-start | bytes 1572872 | tf_op jit(solution)/shard_map/ppermute | solution.py:58
  25.6 12.6 %copy-start.3 = (f32[64,512]{1,0:T(8,128)S(1)}, f32[64,512]{1,0:T(8,128)}, u32[]{:S(2)}) copy-start(f32[64,512]{1,0:T(8,128)} %copy-done.2) | copy-start | bytes 393220
  25.6 12.6 %copy-start.5 = (f32[64,512]{1,0:T(8,128)S(1)}, f32[64,512]{1,0:T(8,128)}, u32[]{:S(2)}) copy-start(f32[64,512]{1,0:T(8,128)} %copy-done.4) | copy-start | bytes 393220
  25.6 12.6 %copy-start.7 = (f32[64,512]{1,0:T(8,128)S(1)}, f32[64,512]{1,0:T(8,128)}, u32[]{:S(2)}) copy-start(f32[64,512]{1,0:T(8,128)} %copy-done.6) | copy-start | bytes 393220
  25.6 12.6 %copy-start.9 = (f32[64,512]{1,0:T(8,128)S(1)}, f32[64,512]{1,0:T(8,128)}, u32[]{:S(2)}) copy-start(f32[64,512]{1,0:T(8,128)} %copy-done.8) | copy-start | bytes 393220
  25.6 12.6 %copy-start.11 = (f32[64,512]{1,0:T(8,128)S(1)}, f32[64,512]{1,0:T(8,128)}, u32[]{:S(2)}) copy-start(f32[64,512]{1,0:T(8,128)} %copy-done.10) | copy-start | bytes 393220
  28.4 24.0 %collective-permute-start.1 = (f32[64,1024]{1,0:T(8,128)S(1)}, f32[64,1024]{1,0:T(8,128)S(1)}, u32[]{:S(2)}, u32[]{:S(2)}) collective-permute-start(f32[64,1024]{1,0:T(8,128)S(1)} %fusion.23), channel_id=1, source_target_pairs={{0,4},{2,6},{4,0},{6,2},{8,12},{10,14},{12,8},{14,10},{1,5},{3,7},... | collective-permute-start | bytes 786440 | tf_op jit(solution)/shard_map/ppermute | solution.py:58
  32.8 20.9 %collective-permute-start.4 = (f32[64,1024]{1,0:T(8,128)S(1)}, f32[64,1024]{1,0:T(8,128)S(1)}, u32[]{:S(2)}, u32[]{:S(2)}) collective-permute-start(f32[64,1024]{1,0:T(8,128)S(1)} %fusion.22), channel_id=1, source_target_pairs={{0,2},{2,0},{4,6},{6,4},{8,10},{10,8},{12,14},{14,12},{1,3},{3,1},... | collective-permute-start | bytes 786440 | tf_op jit(solution)/shard_map/ppermute | solution.py:58
  39.4 16.3 %collective-permute-start.7 = (f32[64,1024]{1,0:T(8,128)S(1)}, f32[64,1024]{1,0:T(8,128)S(1)}, u32[]{:S(2)}, u32[]{:S(2)}) collective-permute-start(f32[64,1024]{1,0:T(8,128)S(1)} %slice_select_fusion), channel_id=1, source_target_pairs={{0,8},{2,10},{4,12},{6,14},{8,0},{10,2},{12,4},{14,6},{1,9},{3,11}... | collective-permute-start | bytes 786440 | tf_op jit(solution)/shard_map/ppermute | solution.py:58
  49.6 43.7 %copy-start.1 = (f32[1,512,256]{1,2,0:T(8,128)S(1)}, f32[1,512,256]{1,2,0:T(8,128)}, u32[]{:S(2)}) copy-start(f32[1,512,256]{1,2,0:T(8,128)} %copy.14) | copy-start | bytes 1572868
  49.6 6.9 %collective-permute-start.10 = (f32[64,1024]{1,0:T(8,128)S(1)}, f32[64,1024]{1,0:T(8,128)S(1)}, u32[]{:S(2)}, u32[]{:S(2)}) collective-permute-start(f32[64,1024]{1,0:T(8,128)S(1)} %fusion.21), channel_id=1, source_target_pairs={{0,2},{2,0},{4,6},{6,4},{8,10},{10,8},{12,14},{14,12},{1,3},{3,1},... | collective-permute-start | bytes 786440 | tf_op jit(solution)/shard_map/ppermute | solution.py:58
  52.5 13.0 %collective-permute-start.2 = (f32[64,512]{1,0:T(8,128)S(1)}, f32[64,512]{1,0:T(8,128)S(1)}, u32[]{:S(2)}, u32[]{:S(2)}) collective-permute-start(f32[64,512]{1,0:T(8,128)S(1)} %slice_select_fusion.4), channel_id=1, source_target_pairs={{0,8},{2,10},{4,12},{6,14},{8,0},{10,2},{12,4},{14,6},{1,9},{3,11}... | collective-permute-start | bytes 393224 | tf_op jit(solution)/shard_map/ppermute | solution.py:58
  53.8 16.0 %collective-permute-start.5 = (f32[64,512]{1,0:T(8,128)S(1)}, f32[64,512]{1,0:T(8,128)S(1)}, u32[]{:S(2)}, u32[]{:S(2)}) collective-permute-start(f32[64,512]{1,0:T(8,128)S(1)} %slice_select_fusion.3), channel_id=1, source_target_pairs={{0,8},{2,10},{4,12},{6,14},{8,0},{10,2},{12,4},{14,6},{1,9},{3,11}... | collective-permute-start | bytes 393224 | tf_op jit(solution)/shard_map/ppermute | solution.py:58
  55.8 14.1 %collective-permute-start.8 = (f32[64,512]{1,0:T(8,128)S(1)}, f32[64,512]{1,0:T(8,128)S(1)}, u32[]{:S(2)}, u32[]{:S(2)}) collective-permute-start(f32[64,512]{1,0:T(8,128)S(1)} %slice_select_fusion.2), channel_id=1, source_target_pairs={{0,4},{2,6},{4,0},{6,2},{8,12},{10,14},{12,8},{14,10},{1,5},{3,7},... | collective-permute-start | bytes 393224 | tf_op jit(solution)/shard_map/ppermute | solution.py:58
  56.6 15.0 %collective-permute-start.11 = (f32[64,512]{1,0:T(8,128)S(1)}, f32[64,512]{1,0:T(8,128)S(1)}, u32[]{:S(2)}, u32[]{:S(2)}) collective-permute-start(f32[64,512]{1,0:T(8,128)S(1)} %slice_select_fusion.1), channel_id=1, source_target_pairs={{0,8},{2,10},{4,12},{6,14},{8,0},{10,2},{12,4},{14,6},{1,9},{3,11}... | collective-permute-start | bytes 393224 | tf_op jit(solution)/shard_map/ppermute | solution.py:58
  72.4 1.3 %collective-permute-start.12 = (f32[]{:T(128)}, f32[]{:T(128)}, u32[]{:S(2)}, u32[]{:S(2)}) collective-permute-start(f32[]{:T(128)} %multiply_reduce_fusion), channel_id=1, source_target_pairs={{0,16},{16,0},{1,17},{17,1},{2,18},{18,2},{3,19},{19,3},{4,20},{20... | collective-permute-start | bytes 20 | tf_op jit(solution)/shard_map/ppermute | solution.py:33
  75.0 3.7 %collective-permute-start.13 = (f32[]{:T(128)}, f32[]{:T(128)}, u32[]{:S(2)}, u32[]{:S(2)}) collective-permute-start(f32[]{:T(128)} %add.78), channel_id=1, source_target_pairs={{0,1},{1,0},{2,3},{3,2},{4,5},{5,4},{6,7},{7,6},{8,9},{9,8},{10,11... | collective-permute-start | bytes 20 | tf_op jit(solution)/shard_map/ppermute | solution.py:33
  79.4 3.7 %collective-permute-start.14 = (f32[]{:T(128)}, f32[]{:T(128)}, u32[]{:S(2)}, u32[]{:S(2)}) collective-permute-start(f32[]{:T(128)} %add.79), channel_id=1, source_target_pairs={{0,2},{2,0},{4,6},{6,4},{8,10},{10,8},{12,14},{14,12},{1,3},{3,1},... | collective-permute-start | bytes 20 | tf_op jit(solution)/shard_map/ppermute | solution.py:33
  83.7 3.7 %collective-permute-start.15 = (f32[]{:T(128)}, f32[]{:T(128)}, u32[]{:S(2)}, u32[]{:S(2)}) collective-permute-start(f32[]{:T(128)} %add.80), channel_id=1, source_target_pairs={{0,4},{2,6},{4,0},{6,2},{8,12},{10,14},{12,8},{14,10},{1,5},{3,7},... | collective-permute-start | bytes 20 | tf_op jit(solution)/shard_map/ppermute | solution.py:33
  88.1 4.6 %collective-permute-start.16 = (f32[]{:T(128)}, f32[]{:T(128)}, u32[]{:S(2)}, u32[]{:S(2)}) collective-permute-start(f32[]{:T(128)} %add.81), channel_id=1, source_target_pairs={{0,8},{2,10},{4,12},{6,14},{8,0},{10,2},{12,4},{14,6},{1,9},{3,11}... | collective-permute-start | bytes 20 | tf_op jit(solution)/shard_map/ppermute | solution.py:33
  93.8 11.2 %collective-permute-start.17 = (bf16[512,128]{0,1:T(8,128)(2,1)S(1)}, bf16[512,128]{0,1:T(8,128)(2,1)S(1)}, u32[]{:S(2)}, u32[]{:S(2)}) collective-permute-start(bf16[512,128]{0,1:T(8,128)(2,1)S(1)} %get-tuple-element.55), channel_id=1, source_target_pairs={{0,8},{2,10},{4,12},{6,14},{8,0},{10,2},{12,4},{14,6},{1,9},{3,11}... | collective-permute-start | bytes 393224 | tf_op jit(solution)/shard_map/ppermute | solution.py:72
  94.5 10.6 %collective-permute-start.20 = (bf16[512,128]{0,1:T(8,128)(2,1)S(1)}, bf16[512,128]{0,1:T(8,128)(2,1)S(1)}, u32[]{:S(2)}, u32[]{:S(2)}) collective-permute-start(bf16[512,128]{0,1:T(8,128)(2,1)S(1)} %get-tuple-element.56), channel_id=1, source_target_pairs={{0,2},{2,0},{4,6},{6,4},{8,10},{10,8},{12,14},{14,12},{1,3},{3,1},... | collective-permute-start | bytes 393224 | tf_op jit(solution)/shard_map/ppermute | solution.py:72
  105.2 10.9 %collective-permute-start.18 = (bf16[2,512,128]{1,2,0:T(8,128)(2,1)S(1)}, bf16[2,512,128]{1,2,0:T(8,128)(2,1)S(1)}, u32[]{:S(2)}, u32[]{:S(2)}) collective-permute-start(bf16[2,512,128]{1,2,0:T(8,128)(2,1)S(1)} %pad_maximum_fusion.16), channel_id=1, source_target_pairs={{0,4},{2,6},{4,0},{6,2},{8,12},{10,14},{12,8},{14,10},{1,5},{3,7},... | collective-permute-start | bytes 786440 | tf_op jit(solution)/shard_map/ppermute | solution.py:72
  105.3 11.0 %collective-permute-start.21 = (bf16[2,512,128]{1,2,0:T(8,128)(2,1)S(1)}, bf16[2,512,128]{1,2,0:T(8,128)(2,1)S(1)}, u32[]{:S(2)}, u32[]{:S(2)}) collective-permute-start(bf16[2,512,128]{1,2,0:T(8,128)(2,1)S(1)} %pad_maximum_fusion.17), channel_id=1, source_target_pairs={{0,8},{2,10},{4,12},{6,14},{8,0},{10,2},{12,4},{14,6},{1,9},{3,11}... | collective-permute-start | bytes 786440 | tf_op jit(solution)/shard_map/ppermute | solution.py:72
  116.2 9.2 %collective-permute-start.19 = (bf16[2,2,512,128]{2,3,1,0:T(8,128)(2,1)S(1)}, bf16[2,2,512,128]{2,3,1,0:T(8,128)(2,1)S(1)}, u32[]{:S(2)}, u32[]{:S(2)}) collective-permute-start(bf16[2,2,512,128]{2,3,1,0:T(8,128)(2,1)S(1)} %pad_maximum_fusion.8), channel_id=1, source_target_pairs={{0,2},{2,0},{4,6},{6,4},{8,10},{10,8},{12,14},{14,12},{1,3},{3,1},... | collective-permute-start | bytes 1572872 | tf_op jit(solution)/shard_map/ppermute | solution.py:72
  117.1 10.1 %collective-permute-start.22 = (bf16[2,2,512,128]{2,3,1,0:T(8,128)(2,1)}, bf16[2,2,512,128]{2,3,1,0:T(8,128)(2,1)S(1)}, u32[]{:S(2)}, u32[]{:S(2)}) collective-permute-start(bf16[2,2,512,128]{2,3,1,0:T(8,128)(2,1)} %pad_maximum_fusion.9), channel_id=1, source_target_pairs={{0,4},{2,6},{4,0},{6,2},{8,12},{10,14},{12,8},{14,10},{1,5},{3,7},... | collective-permute-start | bytes 1572872 | tf_op jit(solution)/shard_map/ppermute | solution.py:72
  (11 other events, 67.9 us)

commit v14 on v13

--- a/solution.py
+++ b/solution.py
@@ -62,21 +62,22 @@
 
 def doubling_gather(part, axis, order):
     size = lax.axis_size(axis)
-    levels = size.bit_length() - 1
     index = lax.axis_index(axis)
-    placed = []
-    current = part
+    height = part.shape[0]
+    held = [0]
+    blocks = part
     for bit in order:
         mine = (index >> bit) & 1
         pairs = [(i, i ^ (1 << bit)) for i in range(size)]
-        other = lax.ppermute(current, axis, pairs)
-        low = jnp.where(mine == 1, other, current)
-        high = jnp.where(mine == 1, current, other)
-        current = jnp.stack([low, high], axis=0)
-        placed.insert(0, bit)
-    perm = [placed.index(bit) for bit in range(levels - 1, -1, -1)]
-    current = jnp.transpose(current, perm + list(range(levels, current.ndim)))
-    return current.reshape((-1,) + part.shape[1:])
+        other = lax.ppermute(blocks, axis, pairs)
+        low = jnp.where(mine == 1, other, blocks)
+        high = jnp.where(mine == 1, blocks, other)
+        merged = sorted([(block, 0, k) for k, block in enumerate(held)] + [(block | (1 << bit), 1, k) for k, block in enumerate(held)])
+        blocks = jnp.concatenate(
+            [(high if side else low)[k * height:(k + 1) * height] for _, side, k in merged], axis=0
+        )
+        held = [block for block, _, _ in merged]
+    return blocks
 
 
 def scatter_rows(partial_t, axis, parts=4):

time: 130 us -> 139 us (1.069)
  other arithmetic: 14.5 us -> 20.3 us
    broadcast_in_dim x1, other arithmetic: 1.55 us -> 7.89 us  [local(): return gather_rows(update.astype(jnp.bfloat16).T, 'dp')[None]]
    broadcast_in_dim x0 -> x1, local copies, waits for them, and re-layouts: none -> 2.46 us  [local(): return gather_rows(update.astype(jnp.bfloat16).T, 'dp')[None]]
    unnamed x43 -> x50, local copies, waits for them, and re-layouts: 6.55 us -> 6.63 us
  transfers between devices with their start and end apart: 23 -> 23, of which waited for: 17 -> 17; matrix products, arithmetic and copies ran while one was open for 12% -> 11% of each run, Pallas kernels for 0% -> 0%
where the time goes in v14:
time: 139 us; the launch traced here: 138 us
  waiting for transfers between devices  62 us (45%)
  starting transfers between devices  33.2 us (24%)
  other arithmetic  20.3 us (15%)
  local copies, waits for them, and re-layouts  11.2 us (8%)
  matrix products  6.18 us (4%)
  between operations  5.12 us (4%)
    ppermute x12, waiting for transfers between devices, halving_scatter(): blocks = keep + lax.ppermute(send, axis, pairs)  27.5 us
    ppermute x6, waiting for transfers between devices, doubling_gather(): other = lax.ppermute(blocks, axis, pairs)  25.3 us
    ppermute x12, starting transfers between devices, halving_scatter(): blocks = keep + lax.ppermute(send, axis, pairs)  18.1 us
    ppermute x5, waiting for transfers between devices, butterfly_sum(): value = value + lax.ppermute(value, axis, pairs)  9.22 us
    broadcast_in_dim x1, other arithmetic, local(): return gather_rows(update.astype(jnp.bfloat16).T, 'dp')[None]  7.89 us
    ppermute x5, starting transfers between devices, butterfly_sum(): value = value + lax.ppermute(value, axis, pairs)  7.84 us
    ppermute x6, starting transfers between devices, doubling_gather(): other = lax.ppermute(blocks, axis, pairs)  7.31 us
    unnamed x50, local copies, waits for them, and re-layouts  6.63 us
  transfers between devices with their start and end apart: 23, of which 17 were waited for; matrix products, arithmetic and copies ran while one was open for 11% of the time, Pallas kernels for 0%

profile of v14, /device:TPU:0, one launch (start us, length us, event | category | flops | bytes accessed | tf_op | source)
XLA Modules:
  0.0 138.0 jit_solution(12670010721198433412)
XLA Ops:
  1.4 6.2 %fusion.2 = f32[256,4096]{1,0:T(8,128)S(1)} fusion(bf16[1,8,128,4096]{3,2,1,0:T(8,128)(2,1)} %param.6, bf16[1,8,128,256]{3,2,1,0:T(8,128)(2,1)} %param.7, bf16[8]{0:T(256)(128)(2,1)S(1)} %get-tuple-element.65), kind=kOutput, calls=%fused_computation.2 | convolution fusion | flops 2147745792 | bytes 13107216 | tf_op jit(solution)/shard_map/dot_general | solution.py:19
  7.6 2.0 %copy-done = f32[256,4096]{1,0:T(8,128)} copy-done((f32[256,4096]{1,0:T(8,128)}, f32[256,4096]{1,0:T(8,128)S(1)}, u32[]{:S(2)}) %copy-start) | copy-done | bytes 4194328
  10.9 2.9 %collective-permute-start = (f32[64,2048]{1,0:T(8,128)}, f32[64,2048]{1,0:T(8,128)}, u32[]{:S(2)}, u32[]{:S(2)}) collective-permute-start(f32[64,2048]{1,0:T(8,128)} %fusion.18), channel_id=1, source_target_pairs={{0,2},{2,0},{4,6},{6,4},{8,10},{10,8},{12,14},{14,12},{1,3},{3,1},... | collective-permute-start | bytes 1572872 | tf_op jit(solution)/shard_map/ppermute | solution.py:58
  13.9 1.6 %fusion.25 = (f32[64,1024]{1,0:T(8,128)S(1)}, f32[64,1024]{1,0:T(8,128)S(1)}, f32[64,1024]{1,0:T(8,128)S(1)}, f32[64,1024]{1,0:T(8,128)S(1)}, f32[64,1024]{1,0:T...) fusion(f32[256,4096]{1,0:T(8,128)} %copy-done), kind=kLoop, calls=%fused_computation.84 | loop fusion | bytes 4194304 | tf_op jit(solution)/shard_map/slice | solution.py:54
  16.4 1.6 %collective-permute-start.3 = (f32[64,2048]{1,0:T(8,128)}, f32[64,2048]{1,0:T(8,128)}, u32[]{:S(2)}, u32[]{:S(2)}) collective-permute-start(f32[64,2048]{1,0:T(8,128)} %fusion.16), channel_id=1, source_target_pairs={{0,4},{2,6},{4,0},{6,2},{8,12},{10,14},{12,8},{14,10},{1,5},{3,7},... | collective-permute-start | bytes 1572872 | tf_op jit(solution)/shard_map/ppermute | solution.py:58
  23.5 2.0 %copy.9 = f32[1,512,256]{1,2,0:T(8,128)} copy(f32[1,512,256]{2,1,0:T(8,128)} %param.11) | data formatting | bytes 1048576 | tf_op args[5]
  25.6 1.4 %collective-permute-done = f32[64,2048]{1,0:T(8,128)} collective-permute-done((f32[64,2048]{1,0:T(8,128)}, f32[64,2048]{1,0:T(8,128)}, u32[]{:S(2)}, u32[]{:S(2)}) %collective-permute-start) | collective-permute-done | bytes 524320 | tf_op jit(solution)/shard_map/ppermute | solution.py:58
  26.9 1.4 %select_add_fusion.3 = f32[64,2048]{1,0:T(8,128)S(1)} fusion(f32[64,2048]{1,0:T(8,128)} %collective-permute-done, f32[64,512]{1,0:T(8,128)} %copy-done.13, f32[64,512]{1,0:T(8,128)} %copy-done.14, f32[64,512]{1,0:T(8,128)} %copy-done.15, f32[64,512]{1,0:T(8,128)} %copy-done.16, f32[64,512]{1,0:T(8,128)} %copy-done.17, f32[64,512]{1,0:T(8,128)} %copy-done.18, ...), kind=kLoop, calls=%fused_computation.29 | loop fusion | flops 1048576 | bytes 2097153 | tf_op jit(solution)/shard_map/add | solution.py:58
  28.5 2.2 %collective-permute-start.1 = (f32[64,1024]{1,0:T(8,128)S(1)}, f32[64,1024]{1,0:T(8,128)S(1)}, u32[]{:S(2)}, u32[]{:S(2)}) collective-permute-start(f32[64,1024]{1,0:T(8,128)S(1)} %fusion.23), channel_id=1, source_target_pairs={{0,4},{2,6},{4,0},{6,2},{8,12},{10,14},{12,8},{14,10},{1,5},{3,7},... | collective-permute-start | bytes 786440 | tf_op jit(solution)/shard_map/ppermute | solution.py:58
  33.4 4.7 %collective-permute-done.6 = f32[64,2048]{1,0:T(8,128)} collective-permute-done((f32[64,2048]{1,0:T(8,128)}, f32[64,2048]{1,0:T(8,128)}, u32[]{:S(2)}, u32[]{:S(2)}) %collective-permute-start.6) | collective-permute-done | bytes 524320 | tf_op jit(solution)/shard_map/ppermute | solution.py:58
  39.4 3.2 %collective-permute-start.7 = (f32[64,1024]{1,0:T(8,128)S(1)}, f32[64,1024]{1,0:T(8,128)S(1)}, u32[]{:S(2)}, u32[]{:S(2)}) collective-permute-start(f32[64,1024]{1,0:T(8,128)S(1)} %slice_select_fusion), channel_id=1, source_target_pairs={{0,8},{2,10},{4,12},{6,14},{8,0},{10,2},{12,4},{14,6},{1,9},{3,11}... | collective-permute-start | bytes 786440 | tf_op jit(solution)/shard_map/ppermute | solution.py:58
  42.6 5.8 %collective-permute-done.9 = f32[64,2048]{1,0:T(8,128)} collective-permute-done((f32[64,2048]{1,0:T(8,128)}, f32[64,2048]{1,0:T(8,128)}, u32[]{:S(2)}, u32[]{:S(2)}) %collective-permute-start.9) | collective-permute-done | bytes 524320 | tf_op jit(solution)/shard_map/ppermute | solution.py:58
  49.7 2.7 %collective-permute-done.1 = f32[64,1024]{1,0:T(8,128)S(1)} collective-permute-done((f32[64,1024]{1,0:T(8,128)S(1)}, f32[64,1024]{1,0:T(8,128)S(1)}, u32[]{:S(2)}, u32[]{:S(2)}) %collective-permute-start.1) | collective-permute-done | bytes 262176 | tf_op jit(solution)/shard_map/ppermute | solution.py:58
  53.8 1.9 %collective-permute-start.5 = (f32[64,512]{1,0:T(8,128)S(1)}, f32[64,512]{1,0:T(8,128)S(1)}, u32[]{:S(2)}, u32[]{:S(2)}) collective-permute-start(f32[64,512]{1,0:T(8,128)S(1)} %slice_select_fusion.3), channel_id=1, source_target_pairs={{0,8},{2,10},{4,12},{6,14},{8,0},{10,2},{12,4},{14,6},{1,9},{3,11}... | collective-permute-start | bytes 393224 | tf_op jit(solution)/shard_map/ppermute | solution.py:58
  56.6 3.0 %collective-permute-start.11 = (f32[64,512]{1,0:T(8,128)S(1)}, f32[64,512]{1,0:T(8,128)S(1)}, u32[]{:S(2)}, u32[]{:S(2)}) collective-permute-start(f32[64,512]{1,0:T(8,128)S(1)} %slice_select_fusion.1), channel_id=1, source_target_pairs={{0,8},{2,10},{4,12},{6,14},{8,0},{10,2},{12,4},{14,6},{1,9},{3,11}... | collective-permute-start | bytes 393224 | tf_op jit(solution)/shard_map/ppermute | solution.py:58
  59.6 6.0 %collective-permute-done.2 = f32[64,512]{1,0:T(8,128)S(1)} collective-permute-done((f32[64,512]{1,0:T(8,128)S(1)}, f32[64,512]{1,0:T(8,128)S(1)}, u32[]{:S(2)}, u32[]{:S(2)}) %collective-permute-start.2) | collective-permute-done | bytes 131104 | tf_op jit(solution)/shard_map/ppermute | solution.py:58
  65.6 4.2 %collective-permute-done.5 = f32[64,512]{1,0:T(8,128)S(1)} collective-permute-done((f32[64,512]{1,0:T(8,128)S(1)}, f32[64,512]{1,0:T(8,128)S(1)}, u32[]{:S(2)}, u32[]{:S(2)}) %collective-permute-start.5) | collective-permute-done | bytes 131104 | tf_op jit(solution)/shard_map/ppermute | solution.py:58
  69.9 1.7 %collective-permute-done.11 = f32[64,512]{1,0:T(8,128)S(1)} collective-permute-done((f32[64,512]{1,0:T(8,128)S(1)}, f32[64,512]{1,0:T(8,128)S(1)}, u32[]{:S(2)}, u32[]{:S(2)}) %collective-permute-start.11) | collective-permute-done | bytes 131104 | tf_op jit(solution)/shard_map/ppermute | solution.py:58
  75.0 2.9 %collective-permute-start.13 = (f32[]{:T(128)}, f32[]{:T(128)}, u32[]{:S(2)}, u32[]{:S(2)}) collective-permute-start(f32[]{:T(128)} %add.78), channel_id=1, source_target_pairs={{0,1},{1,0},{2,3},{3,2},{4,5},{5,4},{6,7},{7,6},{8,9},{9,8},{10,11... | collective-permute-start | bytes 20 | tf_op jit(solution)/shard_map/ppermute | solution.py:33
  79.4 1.7 %collective-permute-start.14 = (f32[]{:T(128)}, f32[]{:T(128)}, u32[]{:S(2)}, u32[]{:S(2)}) collective-permute-start(f32[]{:T(128)} %add.79), channel_id=1, source_target_pairs={{0,2},{2,0},{4,6},{6,4},{8,10},{10,8},{12,14},{14,12},{1,3},{3,1},... | collective-permute-start | bytes 20 | tf_op jit(solution)/shard_map/ppermute | solution.py:33
  81.0 2.0 %collective-permute-done.14 = f32[]{:T(128)} collective-permute-done((f32[]{:T(128)}, f32[]{:T(128)}, u32[]{:S(2)}, u32[]{:S(2)}) %collective-permute-start.14) | collective-permute-done | bytes 36 | tf_op jit(solution)/shard_map/ppermute | solution.py:33
  83.7 1.4 collective-permute-start.15
  85.1 2.3 %collective-permute-done.15 = f32[]{:T(128)} collective-permute-done((f32[]{:T(128)}, f32[]{:T(128)}, u32[]{:S(2)}, u32[]{:S(2)}) %collective-permute-start.15) | collective-permute-done | bytes 36 | tf_op jit(solution)/shard_map/ppermute | solution.py:33
  88.1 1.9 %collective-permute-start.16 = (f32[]{:T(128)}, f32[]{:T(128)}, u32[]{:S(2)}, u32[]{:S(2)}) collective-permute-start(f32[]{:T(128)} %add.81), channel_id=1, source_target_pairs={{0,8},{2,10},{4,12},{6,14},{8,0},{10,2},{12,4},{14,6},{1,9},{3,11}... | collective-permute-start | bytes 20 | tf_op jit(solution)/shard_map/ppermute | solution.py:33
  90.0 2.7 %collective-permute-done.16 = f32[]{:T(128)} collective-permute-done((f32[]{:T(128)}, f32[]{:T(128)}, u32[]{:S(2)}, u32[]{:S(2)}) %collective-permute-start.16) | collective-permute-done | bytes 36 | tf_op jit(solution)/shard_map/ppermute | solution.py:33
  95.6 9.5 %collective-permute-done.17 = bf16[512,128]{0,1:T(8,128)(2,1)S(1)} collective-permute-done((bf16[512,128]{0,1:T(8,128)(2,1)S(1)}, bf16[512,128]{0,1:T(8,128)(2,1)S(1)}, u32[]{:S(2)}, u32[]{:S(2)}) %collective-permute-start.17) | collective-permute-done | bytes 131104 | tf_op jit(solution)/shard_map/ppermute | solution.py:72
  105.3 2.6 %collective-permute-start.21 = (bf16[1024,128]{0,1:T(8,128)(2,1)S(1)}, bf16[1024,128]{0,1:T(8,128)(2,1)S(1)}, u32[]{:S(2)}, u32[]{:S(2)}) collective-permute-start(bf16[1024,128]{0,1:T(8,128)(2,1)S(1)} %pad_maximum_fusion.17), channel_id=1, source_target_pairs={{0,8},{2,10},{4,12},{6,14},{8,0},{10,2},{12,4},{14,6},{1,9},{3,11}... | collective-permute-start | bytes 786440 | tf_op jit(solution)/shard_map/ppermute | solution.py:72
  107.9 9.0 %collective-permute-done.18 = bf16[1024,128]{0,1:T(8,128)(2,1)S(1)} collective-permute-done((bf16[1024,128]{0,1:T(8,128)(2,1)S(1)}, bf16[1024,128]{0,1:T(8,128)(2,1)S(1)}, u32[]{:S(2)}, u32[]{:S(2)}) %collective-permute-start.18) | collective-permute-done | bytes 262176 | tf_op jit(solution)/shard_map/ppermute | solution.py:72
  117.4 2.8 %collective-permute-start.22 = (bf16[2048,128]{0,1:T(8,128)(2,1)S(1)}, bf16[2048,128]{0,1:T(8,128)(2,1)S(1)}, u32[]{:S(2)}, u32[]{:S(2)}) collective-permute-start(bf16[2048,128]{0,1:T(8,128)(2,1)S(1)} %pad_maximum_fusion.9), channel_id=1, source_target_pairs={{0,4},{2,6},{4,0},{6,2},{8,12},{10,14},{12,8},{14,10},{1,5},{3,7},... | collective-permute-start | bytes 1572872 | tf_op jit(solution)/shard_map/ppermute | solution.py:72
  120.2 6.2 %collective-permute-done.19 = bf16[2048,128]{0,1:T(8,128)(2,1)S(1)} collective-permute-done((bf16[2048,128]{0,1:T(8,128)(2,1)S(1)}, bf16[2048,128]{0,1:T(8,128)(2,1)S(1)}, u32[]{:S(2)}, u32[]{:S(2)}) %collective-permute-start.19) | collective-permute-done | bytes 524320 | tf_op jit(solution)/shard_map/ppermute | solution.py:72
  127.7 7.9 %maximum_bitcast_fusion = bf16[1,4096,256]{1,2,0:T(8,128)(2,1)S(1)} fusion(bf16[1024,128]{0,1:T(8,128)(2,1)S(1)} %get-tuple-element.67, bf16[1024,128]{0,1:T(8,128)(2,1)S(1)} %get-tuple-element.36, bf16[1024,128]{0,1:T(8,128)(2,1)S(1)} %get-tuple-element.68, bf16[1024,128]{0,1:T(8,128)(2,1)S(1)} %get-tuple-element.35, ...), kind=kLoop, calls=%fused_computation.3 | loop fusion | flops 10485760 | bytes 4194304 | tf_op jit(solution)/shard_map/broadcast_in_dim | solution.py:133
  135.6 2.5 %copy.11 = bf16[1,4096,256]{2,1,0:T(8,128)(2,1)} copy(bf16[1,4096,256]{1,2,0:T(8,128)(2,1)S(1)} %maximum_bitcast_fusion) | data formatting | bytes 4194304 | tf_op jit(solution)/shard_map/broadcast_in_dim | solution.py:133
  (112 shorter events, 22.9 us)
Async XLA Ops:
  9.8 9.1 %copy-start.2 = (f32[64,512]{1,0:T(8,128)}, f32[64,512]{1,0:T(8,128)S(1)}, u32[]{:S(2)}) copy-start(f32[64,512]{1,0:T(8,128)S(1)} %get-tuple-element.9) | copy-start | bytes 393220
  9.8 9.1 %copy-start.4 = (f32[64,512]{1,0:T(8,128)}, f32[64,512]{1,0:T(8,128)S(1)}, u32[]{:S(2)}) copy-start(f32[64,512]{1,0:T(8,128)S(1)} %get-tuple-element.10) | copy-start | bytes 393220
  9.8 9.0 %copy-start.6 = (f32[64,512]{1,0:T(8,128)}, f32[64,512]{1,0:T(8,128)S(1)}, u32[]{:S(2)}) copy-start(f32[64,512]{1,0:T(8,128)S(1)} %get-tuple-element.11) | copy-start | bytes 393220
  10.9 16.0 %collective-permute-start = (f32[64,2048]{1,0:T(8,128)}, f32[64,2048]{1,0:T(8,128)}, u32[]{:S(2)}, u32[]{:S(2)}) collective-permute-start(f32[64,2048]{1,0:T(8,128)} %fusion.18), channel_id=1, source_target_pairs={{0,2},{2,0},{4,6},{6,4},{8,10},{10,8},{12,14},{14,12},{1,3},{3,1},... | collective-permute-start | bytes 1572872 | tf_op jit(solution)/shard_map/ppermute | solution.py:58
  16.4 15.2 %collective-permute-start.3 = (f32[64,2048]{1,0:T(8,128)}, f32[64,2048]{1,0:T(8,128)}, u32[]{:S(2)}, u32[]{:S(2)}) collective-permute-start(f32[64,2048]{1,0:T(8,128)} %fusion.16), channel_id=1, source_target_pairs={{0,4},{2,6},{4,0},{6,2},{8,12},{10,14},{12,8},{14,10},{1,5},{3,7},... | collective-permute-start | bytes 1572872 | tf_op jit(solution)/shard_map/ppermute | solution.py:58
  18.9 19.3 %collective-permute-start.6 = (f32[64,2048]{1,0:T(8,128)}, f32[64,2048]{1,0:T(8,128)}, u32[]{:S(2)}, u32[]{:S(2)}) collective-permute-start(f32[64,2048]{1,0:T(8,128)} %fusion.17), channel_id=1, source_target_pairs={{0,2},{2,0},{4,6},{6,4},{8,10},{10,8},{12,14},{14,12},{1,3},{3,1},... | collective-permute-start | bytes 1572872 | tf_op jit(solution)/shard_map/ppermute | solution.py:58
  20.4 28.1 %collective-permute-start.9 = (f32[64,2048]{1,0:T(8,128)}, f32[64,2048]{1,0:T(8,128)}, u32[]{:S(2)}, u32[]{:S(2)}) collective-permute-start(f32[64,2048]{1,0:T(8,128)} %fusion.15), channel_id=1, source_target_pairs={{0,4},{2,6},{4,0},{6,2},{8,12},{10,14},{12,8},{14,10},{1,5},{3,7},... | collective-permute-start | bytes 1572872 | tf_op jit(solution)/shard_map/ppermute | solution.py:58
  25.5 12.6 %copy-start.3 = (f32[64,512]{1,0:T(8,128)S(1)}, f32[64,512]{1,0:T(8,128)}, u32[]{:S(2)}) copy-start(f32[64,512]{1,0:T(8,128)} %copy-done.2) | copy-start | bytes 393220
  25.5 12.6 %copy-start.5 = (f32[64,512]{1,0:T(8,128)S(1)}, f32[64,512]{1,0:T(8,128)}, u32[]{:S(2)}) copy-start(f32[64,512]{1,0:T(8,128)} %copy-done.4) | copy-start | bytes 393220
  25.5 12.6 %copy-start.7 = (f32[64,512]{1,0:T(8,128)S(1)}, f32[64,512]{1,0:T(8,128)}, u32[]{:S(2)}) copy-start(f32[64,512]{1,0:T(8,128)} %copy-done.6) | copy-start | bytes 393220
  25.5 12.6 %copy-start.9 = (f32[64,512]{1,0:T(8,128)S(1)}, f32[64,512]{1,0:T(8,128)}, u32[]{:S(2)}) copy-start(f32[64,512]{1,0:T(8,128)} %copy-done.8) | copy-start | bytes 393220
  25.6 12.6 %copy-start.11 = (f32[64,512]{1,0:T(8,128)S(1)}, f32[64,512]{1,0:T(8,128)}, u32[]{:S(2)}) copy-start(f32[64,512]{1,0:T(8,128)} %copy-done.10) | copy-start | bytes 393220
  28.5 24.0 %collective-permute-start.1 = (f32[64,1024]{1,0:T(8,128)S(1)}, f32[64,1024]{1,0:T(8,128)S(1)}, u32[]{:S(2)}, u32[]{:S(2)}) collective-permute-start(f32[64,1024]{1,0:T(8,128)S(1)} %fusion.23), channel_id=1, source_target_pairs={{0,4},{2,6},{4,0},{6,2},{8,12},{10,14},{12,8},{14,10},{1,5},{3,7},... | collective-permute-start | bytes 786440 | tf_op jit(solution)/shard_map/ppermute | solution.py:58
  32.8 20.9 %collective-permute-start.4 = (f32[64,1024]{1,0:T(8,128)S(1)}, f32[64,1024]{1,0:T(8,128)S(1)}, u32[]{:S(2)}, u32[]{:S(2)}) collective-permute-start(f32[64,1024]{1,0:T(8,128)S(1)} %fusion.22), channel_id=1, source_target_pairs={{0,2},{2,0},{4,6},{6,4},{8,10},{10,8},{12,14},{14,12},{1,3},{3,1},... | collective-permute-start | bytes 786440 | tf_op jit(solution)/shard_map/ppermute | solution.py:58
  39.4 16.3 %collective-permute-start.7 = (f32[64,1024]{1,0:T(8,128)S(1)}, f32[64,1024]{1,0:T(8,128)S(1)}, u32[]{:S(2)}, u32[]{:S(2)}) collective-permute-start(f32[64,1024]{1,0:T(8,128)S(1)} %slice_select_fusion), channel_id=1, source_target_pairs={{0,8},{2,10},{4,12},{6,14},{8,0},{10,2},{12,4},{14,6},{1,9},{3,11}... | collective-permute-start | bytes 786440 | tf_op jit(solution)/shard_map/ppermute | solution.py:58
  49.6 43.7 %copy-start.1 = (f32[1,512,256]{1,2,0:T(8,128)S(1)}, f32[1,512,256]{1,2,0:T(8,128)}, u32[]{:S(2)}) copy-start(f32[1,512,256]{1,2,0:T(8,128)} %copy.9) | copy-start | bytes 1572868
  49.7 6.9 %collective-permute-start.10 = (f32[64,1024]{1,0:T(8,128)S(1)}, f32[64,1024]{1,0:T(8,128)S(1)}, u32[]{:S(2)}, u32[]{:S(2)}) collective-permute-start(f32[64,1024]{1,0:T(8,128)S(1)} %fusion.21), channel_id=1, source_target_pairs={{0,2},{2,0},{4,6},{6,4},{8,10},{10,8},{12,14},{14,12},{1,3},{3,1},... | collective-permute-start | bytes 786440 | tf_op jit(solution)/shard_map/ppermute | solution.py:58
  52.6 13.0 %collective-permute-start.2 = (f32[64,512]{1,0:T(8,128)S(1)}, f32[64,512]{1,0:T(8,128)S(1)}, u32[]{:S(2)}, u32[]{:S(2)}) collective-permute-start(f32[64,512]{1,0:T(8,128)S(1)} %slice_select_fusion.4), channel_id=1, source_target_pairs={{0,8},{2,10},{4,12},{6,14},{8,0},{10,2},{12,4},{14,6},{1,9},{3,11}... | collective-permute-start | bytes 393224 | tf_op jit(solution)/shard_map/ppermute | solution.py:58
  53.8 16.0 %collective-permute-start.5 = (f32[64,512]{1,0:T(8,128)S(1)}, f32[64,512]{1,0:T(8,128)S(1)}, u32[]{:S(2)}, u32[]{:S(2)}) collective-permute-start(f32[64,512]{1,0:T(8,128)S(1)} %slice_select_fusion.3), channel_id=1, source_target_pairs={{0,8},{2,10},{4,12},{6,14},{8,0},{10,2},{12,4},{14,6},{1,9},{3,11}... | collective-permute-start | bytes 393224 | tf_op jit(solution)/shard_map/ppermute | solution.py:58
  55.8 14.0 %collective-permute-start.8 = (f32[64,512]{1,0:T(8,128)S(1)}, f32[64,512]{1,0:T(8,128)S(1)}, u32[]{:S(2)}, u32[]{:S(2)}) collective-permute-start(f32[64,512]{1,0:T(8,128)S(1)} %slice_select_fusion.2), channel_id=1, source_target_pairs={{0,4},{2,6},{4,0},{6,2},{8,12},{10,14},{12,8},{14,10},{1,5},{3,7},... | collective-permute-start | bytes 393224 | tf_op jit(solution)/shard_map/ppermute | solution.py:58
  56.6 15.0 %collective-permute-start.11 = (f32[64,512]{1,0:T(8,128)S(1)}, f32[64,512]{1,0:T(8,128)S(1)}, u32[]{:S(2)}, u32[]{:S(2)}) collective-permute-start(f32[64,512]{1,0:T(8,128)S(1)} %slice_select_fusion.1), channel_id=1, source_target_pairs={{0,8},{2,10},{4,12},{6,14},{8,0},{10,2},{12,4},{14,6},{1,9},{3,11}... | collective-permute-start | bytes 393224 | tf_op jit(solution)/shard_map/ppermute | solution.py:58
  72.4 1.3 collective-permute-start.12
  75.0 3.7 %collective-permute-start.13 = (f32[]{:T(128)}, f32[]{:T(128)}, u32[]{:S(2)}, u32[]{:S(2)}) collective-permute-start(f32[]{:T(128)} %add.78), channel_id=1, source_target_pairs={{0,1},{1,0},{2,3},{3,2},{4,5},{5,4},{6,7},{7,6},{8,9},{9,8},{10,11... | collective-permute-start | bytes 20 | tf_op jit(solution)/shard_map/ppermute | solution.py:33
  79.4 3.7 %collective-permute-start.14 = (f32[]{:T(128)}, f32[]{:T(128)}, u32[]{:S(2)}, u32[]{:S(2)}) collective-permute-start(f32[]{:T(128)} %add.79), channel_id=1, source_target_pairs={{0,2},{2,0},{4,6},{6,4},{8,10},{10,8},{12,14},{14,12},{1,3},{3,1},... | collective-permute-start | bytes 20 | tf_op jit(solution)/shard_map/ppermute | solution.py:33
  83.7 3.7 %collective-permute-start.15 = (f32[]{:T(128)}, f32[]{:T(128)}, u32[]{:S(2)}, u32[]{:S(2)}) collective-permute-start(f32[]{:T(128)} %add.80), channel_id=1, source_target_pairs={{0,4},{2,6},{4,0},{6,2},{8,12},{10,14},{12,8},{14,10},{1,5},{3,7},... | collective-permute-start | bytes 20 | tf_op jit(solution)/shard_map/ppermute | solution.py:33
  88.1 4.6 %collective-permute-start.16 = (f32[]{:T(128)}, f32[]{:T(128)}, u32[]{:S(2)}, u32[]{:S(2)}) collective-permute-start(f32[]{:T(128)} %add.81), channel_id=1, source_target_pairs={{0,8},{2,10},{4,12},{6,14},{8,0},{10,2},{12,4},{14,6},{1,9},{3,11}... | collective-permute-start | bytes 20 | tf_op jit(solution)/shard_map/ppermute | solution.py:33
  93.8 11.2 %collective-permute-start.17 = (bf16[512,128]{0,1:T(8,128)(2,1)S(1)}, bf16[512,128]{0,1:T(8,128)(2,1)S(1)}, u32[]{:S(2)}, u32[]{:S(2)}) collective-permute-start(bf16[512,128]{0,1:T(8,128)(2,1)S(1)} %get-tuple-element.63), channel_id=1, source_target_pairs={{0,8},{2,10},{4,12},{6,14},{8,0},{10,2},{12,4},{14,6},{1,9},{3,11}... | collective-permute-start | bytes 393224 | tf_op jit(solution)/shard_map/ppermute | solution.py:72
  94.4 10.7 %collective-permute-start.20 = (bf16[512,128]{0,1:T(8,128)(2,1)S(1)}, bf16[512,128]{0,1:T(8,128)(2,1)S(1)}, u32[]{:S(2)}, u32[]{:S(2)}) collective-permute-start(bf16[512,128]{0,1:T(8,128)(2,1)S(1)} %get-tuple-element.64), channel_id=1, source_target_pairs={{0,2},{2,0},{4,6},{6,4},{8,10},{10,8},{12,14},{14,12},{1,3},{3,1},... | collective-permute-start | bytes 393224 | tf_op jit(solution)/shard_map/ppermute | solution.py:72
  105.2 11.7 %collective-permute-start.18 = (bf16[1024,128]{0,1:T(8,128)(2,1)S(1)}, bf16[1024,128]{0,1:T(8,128)(2,1)S(1)}, u32[]{:S(2)}, u32[]{:S(2)}) collective-permute-start(bf16[1024,128]{0,1:T(8,128)(2,1)S(1)} %pad_maximum_fusion.16), channel_id=1, source_target_pairs={{0,4},{2,6},{4,0},{6,2},{8,12},{10,14},{12,8},{14,10},{1,5},{3,7},... | collective-permute-start | bytes 786440 | tf_op jit(solution)/shard_map/ppermute | solution.py:72
  105.3 11.9 %collective-permute-start.21 = (bf16[1024,128]{0,1:T(8,128)(2,1)S(1)}, bf16[1024,128]{0,1:T(8,128)(2,1)S(1)}, u32[]{:S(2)}, u32[]{:S(2)}) collective-permute-start(bf16[1024,128]{0,1:T(8,128)(2,1)S(1)} %pad_maximum_fusion.17), channel_id=1, source_target_pairs={{0,8},{2,10},{4,12},{6,14},{8,0},{10,2},{12,4},{14,6},{1,9},{3,11}... | collective-permute-start | bytes 786440 | tf_op jit(solution)/shard_map/ppermute | solution.py:72
  117.1 9.2 %collective-permute-start.19 = (bf16[2048,128]{0,1:T(8,128)(2,1)S(1)}, bf16[2048,128]{0,1:T(8,128)(2,1)S(1)}, u32[]{:S(2)}, u32[]{:S(2)}) collective-permute-start(bf16[2048,128]{0,1:T(8,128)(2,1)S(1)} %pad_maximum_fusion.8), channel_id=1, source_target_pairs={{0,2},{2,0},{4,6},{6,4},{8,10},{10,8},{12,14},{14,12},{1,3},{3,1},... | collective-permute-start | bytes 1572872 | tf_op jit(solution)/shard_map/ppermute | solution.py:72
  117.4 10.0 %collective-permute-start.22 = (bf16[2048,128]{0,1:T(8,128)(2,1)S(1)}, bf16[2048,128]{0,1:T(8,128)(2,1)S(1)}, u32[]{:S(2)}, u32[]{:S(2)}) collective-permute-start(bf16[2048,128]{0,1:T(8,128)(2,1)S(1)} %pad_maximum_fusion.9), channel_id=1, source_target_pairs={{0,4},{2,6},{4,0},{6,2},{8,12},{10,14},{12,8},{14,10},{1,5},{3,7},... | collective-permute-start | bytes 1572872 | tf_op jit(solution)/shard_map/ppermute | solution.py:72
  (11 other events, 67.8 us)

commit v15 on v13

--- a/solution.py
+++ b/solution.py
@@ -13,8 +13,8 @@
 
 
 def slot_term(inputs, key_grads, live_row, column_count):
-    keep_mask = live_row.astype(key_grads.dtype)
-    weighted = (key_grads * keep_mask[:, None, None]).reshape(-1, key_grads.shape[2])
+    live = live_row[:, None, None] == 1
+    weighted = jnp.where(live, key_grads, jnp.zeros_like(key_grads)).reshape(-1, key_grads.shape[2])
     columns = inputs.reshape(-1, column_count)
     return lax.dot_general(
         weighted, columns, (((0,), (0,)), ((), ())), preferred_element_type=jnp.float32

time: 130 us -> 129 us (level)
    convert_element_type x1 -> x0, other arithmetic: 1.37 us -> none  [slot_term(): keep_mask = live_row.astype(key_grads.dtype)]
    unnamed x43 -> x45, local copies, waits for them, and re-layouts: 6.55 us -> 6.55 us
  transfers between devices with their start and end apart: 23 -> 23, of which waited for: 17 -> 17; matrix products, arithmetic and copies ran while one was open for 12% -> 13% of each run, Pallas kernels for 0% -> 0%
where the time goes in v15:
time: 129 us
  waiting for transfers between devices  60.2 us (47%)
  starting transfers between devices  33.2 us (26%)
  other arithmetic  14.5 us (11%)
  local copies, waits for them, and re-layouts  9.86 us (8%)
  matrix products  6.18 us (5%)
  between operations  5.06 us (4%)
    ppermute x12, waiting for transfers between devices, halving_scatter(): blocks = keep + lax.ppermute(send, axis, pairs)  26.9 us
    ppermute x6, waiting for transfers between devices, doubling_gather(): other = lax.ppermute(current, axis, pairs)  24.2 us
    ppermute x12, starting transfers between devices, halving_scatter(): blocks = keep + lax.ppermute(send, axis, pairs)  18.1 us
    ppermute x5, waiting for transfers between devices, butterfly_sum(): value = value + lax.ppermute(value, axis, pairs)  9.19 us
    ppermute x5, starting transfers between devices, butterfly_sum(): value = value + lax.ppermute(value, axis, pairs)  7.87 us
    ppermute x6, starting transfers between devices, doubling_gather(): other = lax.ppermute(current, axis, pairs)  7.25 us
    unnamed x45, local copies, waits for them, and re-layouts  6.55 us
    dot_general x1, matrix products, slot_term(): lax.dot_general(weighted, columns, (((0,), (0,)), ((), ())), preferred_el...  6.18 us
  transfers between devices with their start and end apart: 23, of which 17 were waited for; matrix products, arithmetic and copies ran while one was open for 13% of the time, Pallas kernels for 0%

profile of v15, /device:TPU:0, one launch (start us, length us, event | category | flops | bytes accessed | tf_op | source)
XLA Modules:
  0.0 128.9 jit_solution(13792682343329960973)
XLA Ops:
  0.7 6.2 %fusion.2 = f32[256,4096]{1,0:T(8,128)S(1)} fusion(bf16[1,8,128,4096]{3,2,1,0:T(8,128)(2,1)} %param.6, bf16[1,8,128,256]{3,2,1,0:T(8,128)(2,1)} %param.7, pred[8]{0:T(512)(128)(4,1)S(1)} %compare_bitcast_fusion), kind=kOutput, calls=%fused_computation.2 | convolution fusion | flops 2147745792 | bytes 13107208 | tf_op jit(solution)/shard_map/dot_general | solution.py:19
  6.9 1.9 %copy-done = f32[256,4096]{1,0:T(8,128)} copy-done((f32[256,4096]{1,0:T(8,128)}, f32[256,4096]{1,0:T(8,128)S(1)}, u32[]{:S(2)}) %copy-start) | copy-done | bytes 4194328
  10.2 2.9 %collective-permute-start = (f32[64,2048]{1,0:T(8,128)}, f32[64,2048]{1,0:T(8,128)}, u32[]{:S(2)}, u32[]{:S(2)}) collective-permute-start(f32[64,2048]{1,0:T(8,128)} %fusion.19), channel_id=1, source_target_pairs={{0,2},{2,0},{4,6},{6,4},{8,10},{10,8},{12,14},{14,12},{1,3},{3,1},... | collective-permute-start | bytes 1572872 | tf_op jit(solution)/shard_map/ppermute | solution.py:58
  13.2 1.6 %fusion.27 = (f32[64,1024]{1,0:T(8,128)S(1)}, f32[64,1024]{1,0:T(8,128)S(1)}, f32[64,1024]{1,0:T(8,128)S(1)}, f32[64,1024]{1,0:T(8,128)S(1)}, f32[64,1024]{1,0:T...) fusion(f32[256,4096]{1,0:T(8,128)} %copy-done), kind=kLoop, calls=%fused_computation.80 | loop fusion | bytes 4194304 | tf_op jit(solution)/shard_map/slice | solution.py:54
  15.7 1.6 %collective-permute-start.3 = (f32[64,2048]{1,0:T(8,128)}, f32[64,2048]{1,0:T(8,128)}, u32[]{:S(2)}, u32[]{:S(2)}) collective-permute-start(f32[64,2048]{1,0:T(8,128)} %fusion.17), channel_id=1, source_target_pairs={{0,4},{2,6},{4,0},{6,2},{8,12},{10,14},{12,8},{14,10},{1,5},{3,7},... | collective-permute-start | bytes 1572872 | tf_op jit(solution)/shard_map/ppermute | solution.py:58
  22.2 1.2 copy.13
  23.5 2.0 %copy.14 = f32[1,512,256]{1,2,0:T(8,128)} copy(f32[1,512,256]{2,1,0:T(8,128)} %param.9) | data formatting | bytes 1048576 | tf_op args[3]
  26.2 1.4 %select_add_fusion.3 = f32[64,2048]{1,0:T(8,128)S(1)} fusion(f32[64,2048]{1,0:T(8,128)} %collective-permute-done, f32[64,512]{1,0:T(8,128)} %copy-done.13, f32[64,512]{1,0:T(8,128)} %copy-done.14, f32[64,512]{1,0:T(8,128)} %copy-done.15, f32[64,512]{1,0:T(8,128)} %copy-done.16, f32[64,512]{1,0:T(8,128)} %copy-done.17, f32[64,512]{1,0:T(8,128)} %copy-done.18, ...), kind=kLoop, calls=%fused_computation.35 | loop fusion | flops 1048576 | bytes 2097153 | tf_op jit(solution)/shard_map/add | solution.py:58
  27.7 2.2 %collective-permute-start.1 = (f32[64,1024]{1,0:T(8,128)S(1)}, f32[64,1024]{1,0:T(8,128)S(1)}, u32[]{:S(2)}, u32[]{:S(2)}) collective-permute-start(f32[64,1024]{1,0:T(8,128)S(1)} %fusion.24), channel_id=1, source_target_pairs={{0,4},{2,6},{4,0},{6,2},{8,12},{10,14},{12,8},{14,10},{1,5},{3,7},... | collective-permute-start | bytes 786440 | tf_op jit(solution)/shard_map/ppermute | solution.py:58
  32.7 4.7 %collective-permute-done.6 = f32[64,2048]{1,0:T(8,128)} collective-permute-done((f32[64,2048]{1,0:T(8,128)}, f32[64,2048]{1,0:T(8,128)}, u32[]{:S(2)}, u32[]{:S(2)}) %collective-permute-start.6) | collective-permute-done | bytes 524320 | tf_op jit(solution)/shard_map/ppermute | solution.py:58
  38.7 3.2 %collective-permute-start.7 = (f32[64,1024]{1,0:T(8,128)S(1)}, f32[64,1024]{1,0:T(8,128)S(1)}, u32[]{:S(2)}, u32[]{:S(2)}) collective-permute-start(f32[64,1024]{1,0:T(8,128)S(1)} %slice_select_fusion), channel_id=1, source_target_pairs={{0,8},{2,10},{4,12},{6,14},{8,0},{10,2},{12,4},{14,6},{1,9},{3,11}... | collective-permute-start | bytes 786440 | tf_op jit(solution)/shard_map/ppermute | solution.py:58
  41.9 5.8 %collective-permute-done.9 = f32[64,2048]{1,0:T(8,128)} collective-permute-done((f32[64,2048]{1,0:T(8,128)}, f32[64,2048]{1,0:T(8,128)}, u32[]{:S(2)}, u32[]{:S(2)}) %collective-permute-start.9) | collective-permute-done | bytes 524320 | tf_op jit(solution)/shard_map/ppermute | solution.py:58
  49.0 2.7 %collective-permute-done.1 = f32[64,1024]{1,0:T(8,128)S(1)} collective-permute-done((f32[64,1024]{1,0:T(8,128)S(1)}, f32[64,1024]{1,0:T(8,128)S(1)}, u32[]{:S(2)}, u32[]{:S(2)}) %collective-permute-start.1) | collective-permute-done | bytes 262176 | tf_op jit(solution)/shard_map/ppermute | solution.py:58
  53.1 1.9 %collective-permute-start.5 = (f32[64,512]{1,0:T(8,128)S(1)}, f32[64,512]{1,0:T(8,128)S(1)}, u32[]{:S(2)}, u32[]{:S(2)}) collective-permute-start(f32[64,512]{1,0:T(8,128)S(1)} %slice_select_fusion.3), channel_id=1, source_target_pairs={{0,8},{2,10},{4,12},{6,14},{8,0},{10,2},{12,4},{14,6},{1,9},{3,11}... | collective-permute-start | bytes 393224 | tf_op jit(solution)/shard_map/ppermute | solution.py:58
  55.9 3.0 %collective-permute-start.11 = (f32[64,512]{1,0:T(8,128)S(1)}, f32[64,512]{1,0:T(8,128)S(1)}, u32[]{:S(2)}, u32[]{:S(2)}) collective-permute-start(f32[64,512]{1,0:T(8,128)S(1)} %slice_select_fusion.1), channel_id=1, source_target_pairs={{0,8},{2,10},{4,12},{6,14},{8,0},{10,2},{12,4},{14,6},{1,9},{3,11}... | collective-permute-start | bytes 393224 | tf_op jit(solution)/shard_map/ppermute | solution.py:58
  58.9 6.0 %collective-permute-done.2 = f32[64,512]{1,0:T(8,128)S(1)} collective-permute-done((f32[64,512]{1,0:T(8,128)S(1)}, f32[64,512]{1,0:T(8,128)S(1)}, u32[]{:S(2)}, u32[]{:S(2)}) %collective-permute-start.2) | collective-permute-done | bytes 131104 | tf_op jit(solution)/shard_map/ppermute | solution.py:58
  64.9 4.2 %collective-permute-done.5 = f32[64,512]{1,0:T(8,128)S(1)} collective-permute-done((f32[64,512]{1,0:T(8,128)S(1)}, f32[64,512]{1,0:T(8,128)S(1)}, u32[]{:S(2)}, u32[]{:S(2)}) %collective-permute-start.5) | collective-permute-done | bytes 131104 | tf_op jit(solution)/shard_map/ppermute | solution.py:58
  69.2 1.7 %collective-permute-done.11 = f32[64,512]{1,0:T(8,128)S(1)} collective-permute-done((f32[64,512]{1,0:T(8,128)S(1)}, f32[64,512]{1,0:T(8,128)S(1)}, u32[]{:S(2)}, u32[]{:S(2)}) %collective-permute-start.11) | collective-permute-done | bytes 131104 | tf_op jit(solution)/shard_map/ppermute | solution.py:58
  71.7 1.3 %collective-permute-done.12 = f32[]{:T(128)} collective-permute-done((f32[]{:T(128)}, f32[]{:T(128)}, u32[]{:S(2)}, u32[]{:S(2)}) %collective-permute-start.12) | collective-permute-done | bytes 36 | tf_op jit(solution)/shard_map/ppermute | solution.py:33
  74.3 2.9 %collective-permute-start.13 = (f32[]{:T(128)}, f32[]{:T(128)}, u32[]{:S(2)}, u32[]{:S(2)}) collective-permute-start(f32[]{:T(128)} %add.78), channel_id=1, source_target_pairs={{0,1},{1,0},{2,3},{3,2},{4,5},{5,4},{6,7},{7,6},{8,9},{9,8},{10,11... | collective-permute-start | bytes 20 | tf_op jit(solution)/shard_map/ppermute | solution.py:33
  78.7 1.7 %collective-permute-start.14 = (f32[]{:T(128)}, f32[]{:T(128)}, u32[]{:S(2)}, u32[]{:S(2)}) collective-permute-start(f32[]{:T(128)} %add.79), channel_id=1, source_target_pairs={{0,2},{2,0},{4,6},{6,4},{8,10},{10,8},{12,14},{14,12},{1,3},{3,1},... | collective-permute-start | bytes 20 | tf_op jit(solution)/shard_map/ppermute | solution.py:33
  80.4 2.0 %collective-permute-done.14 = f32[]{:T(128)} collective-permute-done((f32[]{:T(128)}, f32[]{:T(128)}, u32[]{:S(2)}, u32[]{:S(2)}) %collective-permute-start.14) | collective-permute-done | bytes 36 | tf_op jit(solution)/shard_map/ppermute | solution.py:33
  83.0 1.4 %collective-permute-start.15 = (f32[]{:T(128)}, f32[]{:T(128)}, u32[]{:S(2)}, u32[]{:S(2)}) collective-permute-start(f32[]{:T(128)} %add.80), channel_id=1, source_target_pairs={{0,4},{2,6},{4,0},{6,2},{8,12},{10,14},{12,8},{14,10},{1,5},{3,7},... | collective-permute-start | bytes 20 | tf_op jit(solution)/shard_map/ppermute | solution.py:33
  84.4 2.3 %collective-permute-done.15 = f32[]{:T(128)} collective-permute-done((f32[]{:T(128)}, f32[]{:T(128)}, u32[]{:S(2)}, u32[]{:S(2)}) %collective-permute-start.15) | collective-permute-done | bytes 36 | tf_op jit(solution)/shard_map/ppermute | solution.py:33
  87.4 1.9 %collective-permute-start.16 = (f32[]{:T(128)}, f32[]{:T(128)}, u32[]{:S(2)}, u32[]{:S(2)}) collective-permute-start(f32[]{:T(128)} %add.81), channel_id=1, source_target_pairs={{0,8},{2,10},{4,12},{6,14},{8,0},{10,2},{12,4},{14,6},{1,9},{3,11}... | collective-permute-start | bytes 20 | tf_op jit(solution)/shard_map/ppermute | solution.py:33
  89.3 2.7 %collective-permute-done.16 = f32[]{:T(128)} collective-permute-done((f32[]{:T(128)}, f32[]{:T(128)}, u32[]{:S(2)}, u32[]{:S(2)}) %collective-permute-start.16) | collective-permute-done | bytes 36 | tf_op jit(solution)/shard_map/ppermute | solution.py:33
  94.9 9.5 %collective-permute-done.17 = bf16[512,128]{0,1:T(8,128)(2,1)S(1)} collective-permute-done((bf16[512,128]{0,1:T(8,128)(2,1)S(1)}, bf16[512,128]{0,1:T(8,128)(2,1)S(1)}, u32[]{:S(2)}, u32[]{:S(2)}) %collective-permute-start.17) | collective-permute-done | bytes 131104 | tf_op jit(solution)/shard_map/ppermute | solution.py:72
  104.6 2.6 %collective-permute-start.21 = (bf16[2,512,128]{1,2,0:T(8,128)(2,1)S(1)}, bf16[2,512,128]{1,2,0:T(8,128)(2,1)S(1)}, u32[]{:S(2)}, u32[]{:S(2)}) collective-permute-start(bf16[2,512,128]{1,2,0:T(8,128)(2,1)S(1)} %pad_maximum_fusion.17), channel_id=1, source_target_pairs={{0,8},{2,10},{4,12},{6,14},{8,0},{10,2},{12,4},{14,6},{1,9},{3,11}... | collective-permute-start | bytes 786440 | tf_op jit(solution)/shard_map/ppermute | solution.py:72
  107.2 8.2 %collective-permute-done.18 = bf16[2,512,128]{1,2,0:T(8,128)(2,1)S(1)} collective-permute-done((bf16[2,512,128]{1,2,0:T(8,128)(2,1)S(1)}, bf16[2,512,128]{1,2,0:T(8,128)(2,1)S(1)}, u32[]{:S(2)}, u32[]{:S(2)}) %collective-permute-start.18) | collective-permute-done | bytes 262176 | tf_op jit(solution)/shard_map/ppermute | solution.py:72
  116.5 2.7 %collective-permute-start.22 = (bf16[2,2,512,128]{2,3,1,0:T(8,128)(2,1)}, bf16[2,2,512,128]{2,3,1,0:T(8,128)(2,1)S(1)}, u32[]{:S(2)}, u32[]{:S(2)}) collective-permute-start(bf16[2,2,512,128]{2,3,1,0:T(8,128)(2,1)} %pad_maximum_fusion.9), channel_id=1, source_target_pairs={{0,4},{2,6},{4,0},{6,2},{8,12},{10,14},{12,8},{14,10},{1,5},{3,7},... | collective-permute-start | bytes 1572872 | tf_op jit(solution)/shard_map/ppermute | solution.py:72
  119.2 5.5 %collective-permute-done.19 = bf16[2,2,512,128]{2,3,1,0:T(8,128)(2,1)S(1)} collective-permute-done((bf16[2,2,512,128]{2,3,1,0:T(8,128)(2,1)S(1)}, bf16[2,2,512,128]{2,3,1,0:T(8,128)(2,1)S(1)}, u32[]{:S(2)}, u32[]{:S(2)}) %collective-permute-start.19) | collective-permute-done | bytes 524320 | tf_op jit(solution)/shard_map/ppermute | solution.py:72
  127.4 1.5 %maximum_bitcast_fusion = bf16[1,4096,256]{2,1,0:T(8,128)(2,1)} fusion(bf16[4096,128]{1,0:T(8,128)(2,1)S(1)} %bitcast.75, bf16[4096,128]{1,0:T(8,128)(2,1)S(1)} %bitcast.74), kind=kLoop, calls=%fused_computation.3 | loop fusion | flops 4194304 | bytes 4194304 | tf_op jit(solution)/shard_map/broadcast_in_dim | solution.py:132
  (108 shorter events, 23.1 us)
Async XLA Ops:
  9.1 11.8 %copy-start.12 = (f32[64,512]{1,0:T(8,128)}, f32[64,512]{1,0:T(8,128)S(1)}, u32[]{:S(2)}) copy-start(f32[64,512]{1,0:T(8,128)S(1)} %get-tuple-element.5) | copy-start | bytes 393220
  9.1 11.8 %copy-start.13 = (f32[64,512]{1,0:T(8,128)}, f32[64,512]{1,0:T(8,128)S(1)}, u32[]{:S(2)}) copy-start(f32[64,512]{1,0:T(8,128)S(1)} %get-tuple-element.14) | copy-start | bytes 393220
  9.1 11.8 %copy-start.14 = (f32[64,512]{1,0:T(8,128)}, f32[64,512]{1,0:T(8,128)S(1)}, u32[]{:S(2)}) copy-start(f32[64,512]{1,0:T(8,128)S(1)} %get-tuple-element.15) | copy-start | bytes 393220
  10.2 16.0 %collective-permute-start = (f32[64,2048]{1,0:T(8,128)}, f32[64,2048]{1,0:T(8,128)}, u32[]{:S(2)}, u32[]{:S(2)}) collective-permute-start(f32[64,2048]{1,0:T(8,128)} %fusion.19), channel_id=1, source_target_pairs={{0,2},{2,0},{4,6},{6,4},{8,10},{10,8},{12,14},{14,12},{1,3},{3,1},... | collective-permute-start | bytes 1572872 | tf_op jit(solution)/shard_map/ppermute | solution.py:58
  15.7 15.2 %collective-permute-start.3 = (f32[64,2048]{1,0:T(8,128)}, f32[64,2048]{1,0:T(8,128)}, u32[]{:S(2)}, u32[]{:S(2)}) collective-permute-start(f32[64,2048]{1,0:T(8,128)} %fusion.17), channel_id=1, source_target_pairs={{0,4},{2,6},{4,0},{6,2},{8,12},{10,14},{12,8},{14,10},{1,5},{3,7},... | collective-permute-start | bytes 1572872 | tf_op jit(solution)/shard_map/ppermute | solution.py:58
  18.2 19.3 %collective-permute-start.6 = (f32[64,2048]{1,0:T(8,128)}, f32[64,2048]{1,0:T(8,128)}, u32[]{:S(2)}, u32[]{:S(2)}) collective-permute-start(f32[64,2048]{1,0:T(8,128)} %fusion.18), channel_id=1, source_target_pairs={{0,2},{2,0},{4,6},{6,4},{8,10},{10,8},{12,14},{14,12},{1,3},{3,1},... | collective-permute-start | bytes 1572872 | tf_op jit(solution)/shard_map/ppermute | solution.py:58
  19.6 28.1 %collective-permute-start.9 = (f32[64,2048]{1,0:T(8,128)}, f32[64,2048]{1,0:T(8,128)}, u32[]{:S(2)}, u32[]{:S(2)}) collective-permute-start(f32[64,2048]{1,0:T(8,128)} %fusion.16), channel_id=1, source_target_pairs={{0,4},{2,6},{4,0},{6,2},{8,12},{10,14},{12,8},{14,10},{1,5},{3,7},... | collective-permute-start | bytes 1572872 | tf_op jit(solution)/shard_map/ppermute | solution.py:58
  25.5 12.0 %copy-start.3 = (f32[64,512]{1,0:T(8,128)S(1)}, f32[64,512]{1,0:T(8,128)}, u32[]{:S(2)}) copy-start(f32[64,512]{1,0:T(8,128)} %copy-done.2) | copy-start | bytes 393220
  25.5 12.0 %copy-start.5 = (f32[64,512]{1,0:T(8,128)S(1)}, f32[64,512]{1,0:T(8,128)}, u32[]{:S(2)}) copy-start(f32[64,512]{1,0:T(8,128)} %copy-done.4) | copy-start | bytes 393220
  25.5 12.0 %copy-start.7 = (f32[64,512]{1,0:T(8,128)S(1)}, f32[64,512]{1,0:T(8,128)}, u32[]{:S(2)}) copy-start(f32[64,512]{1,0:T(8,128)} %copy-done.6) | copy-start | bytes 393220
  25.5 12.0 %copy-start.9 = (f32[64,512]{1,0:T(8,128)S(1)}, f32[64,512]{1,0:T(8,128)}, u32[]{:S(2)}) copy-start(f32[64,512]{1,0:T(8,128)} %copy-done.8) | copy-start | bytes 393220
  25.5 12.0 %copy-start.11 = (f32[64,512]{1,0:T(8,128)S(1)}, f32[64,512]{1,0:T(8,128)}, u32[]{:S(2)}) copy-start(f32[64,512]{1,0:T(8,128)} %copy-done.10) | copy-start | bytes 393220
  27.7 24.1 %collective-permute-start.1 = (f32[64,1024]{1,0:T(8,128)S(1)}, f32[64,1024]{1,0:T(8,128)S(1)}, u32[]{:S(2)}, u32[]{:S(2)}) collective-permute-start(f32[64,1024]{1,0:T(8,128)S(1)} %fusion.24), channel_id=1, source_target_pairs={{0,4},{2,6},{4,0},{6,2},{8,12},{10,14},{12,8},{14,10},{1,5},{3,7},... | collective-permute-start | bytes 786440 | tf_op jit(solution)/shard_map/ppermute | solution.py:58
  32.1 21.0 %collective-permute-start.4 = (f32[64,1024]{1,0:T(8,128)S(1)}, f32[64,1024]{1,0:T(8,128)S(1)}, u32[]{:S(2)}, u32[]{:S(2)}) collective-permute-start(f32[64,1024]{1,0:T(8,128)S(1)} %fusion.23), channel_id=1, source_target_pairs={{0,2},{2,0},{4,6},{6,4},{8,10},{10,8},{12,14},{14,12},{1,3},{3,1},... | collective-permute-start | bytes 786440 | tf_op jit(solution)/shard_map/ppermute | solution.py:58
  38.7 16.3 %collective-permute-start.7 = (f32[64,1024]{1,0:T(8,128)S(1)}, f32[64,1024]{1,0:T(8,128)S(1)}, u32[]{:S(2)}, u32[]{:S(2)}) collective-permute-start(f32[64,1024]{1,0:T(8,128)S(1)} %slice_select_fusion), channel_id=1, source_target_pairs={{0,8},{2,10},{4,12},{6,14},{8,0},{10,2},{12,4},{14,6},{1,9},{3,11}... | collective-permute-start | bytes 786440 | tf_op jit(solution)/shard_map/ppermute | solution.py:58
  48.9 43.7 %copy-start.1 = (f32[1,512,256]{1,2,0:T(8,128)S(1)}, f32[1,512,256]{1,2,0:T(8,128)}, u32[]{:S(2)}) copy-start(f32[1,512,256]{1,2,0:T(8,128)} %copy.14) | copy-start | bytes 1572868
  49.0 6.9 %collective-permute-start.10 = (f32[64,1024]{1,0:T(8,128)S(1)}, f32[64,1024]{1,0:T(8,128)S(1)}, u32[]{:S(2)}, u32[]{:S(2)}) collective-permute-start(f32[64,1024]{1,0:T(8,128)S(1)} %fusion.22), channel_id=1, source_target_pairs={{0,2},{2,0},{4,6},{6,4},{8,10},{10,8},{12,14},{14,12},{1,3},{3,1},... | collective-permute-start | bytes 786440 | tf_op jit(solution)/shard_map/ppermute | solution.py:58
  51.8 13.0 %collective-permute-start.2 = (f32[64,512]{1,0:T(8,128)S(1)}, f32[64,512]{1,0:T(8,128)S(1)}, u32[]{:S(2)}, u32[]{:S(2)}) collective-permute-start(f32[64,512]{1,0:T(8,128)S(1)} %slice_select_fusion.4), channel_id=1, source_target_pairs={{0,8},{2,10},{4,12},{6,14},{8,0},{10,2},{12,4},{14,6},{1,9},{3,11}... | collective-permute-start | bytes 393224 | tf_op jit(solution)/shard_map/ppermute | solution.py:58
  53.1 16.0 %collective-permute-start.5 = (f32[64,512]{1,0:T(8,128)S(1)}, f32[64,512]{1,0:T(8,128)S(1)}, u32[]{:S(2)}, u32[]{:S(2)}) collective-permute-start(f32[64,512]{1,0:T(8,128)S(1)} %slice_select_fusion.3), channel_id=1, source_target_pairs={{0,8},{2,10},{4,12},{6,14},{8,0},{10,2},{12,4},{14,6},{1,9},{3,11}... | collective-permute-start | bytes 393224 | tf_op jit(solution)/shard_map/ppermute | solution.py:58
  55.1 14.1 %collective-permute-start.8 = (f32[64,512]{1,0:T(8,128)S(1)}, f32[64,512]{1,0:T(8,128)S(1)}, u32[]{:S(2)}, u32[]{:S(2)}) collective-permute-start(f32[64,512]{1,0:T(8,128)S(1)} %slice_select_fusion.2), channel_id=1, source_target_pairs={{0,4},{2,6},{4,0},{6,2},{8,12},{10,14},{12,8},{14,10},{1,5},{3,7},... | collective-permute-start | bytes 393224 | tf_op jit(solution)/shard_map/ppermute | solution.py:58
  55.9 15.0 %collective-permute-start.11 = (f32[64,512]{1,0:T(8,128)S(1)}, f32[64,512]{1,0:T(8,128)S(1)}, u32[]{:S(2)}, u32[]{:S(2)}) collective-permute-start(f32[64,512]{1,0:T(8,128)S(1)} %slice_select_fusion.1), channel_id=1, source_target_pairs={{0,8},{2,10},{4,12},{6,14},{8,0},{10,2},{12,4},{14,6},{1,9},{3,11}... | collective-permute-start | bytes 393224 | tf_op jit(solution)/shard_map/ppermute | solution.py:58
  71.7 1.3 %collective-permute-start.12 = (f32[]{:T(128)}, f32[]{:T(128)}, u32[]{:S(2)}, u32[]{:S(2)}) collective-permute-start(f32[]{:T(128)} %multiply_reduce_fusion), channel_id=1, source_target_pairs={{0,16},{16,0},{1,17},{17,1},{2,18},{18,2},{3,19},{19,3},{4,20},{20... | collective-permute-start | bytes 20 | tf_op jit(solution)/shard_map/ppermute | solution.py:33
  74.3 3.7 %collective-permute-start.13 = (f32[]{:T(128)}, f32[]{:T(128)}, u32[]{:S(2)}, u32[]{:S(2)}) collective-permute-start(f32[]{:T(128)} %add.78), channel_id=1, source_target_pairs={{0,1},{1,0},{2,3},{3,2},{4,5},{5,4},{6,7},{7,6},{8,9},{9,8},{10,11... | collective-permute-start | bytes 20 | tf_op jit(solution)/shard_map/ppermute | solution.py:33
  78.7 3.7 %collective-permute-start.14 = (f32[]{:T(128)}, f32[]{:T(128)}, u32[]{:S(2)}, u32[]{:S(2)}) collective-permute-start(f32[]{:T(128)} %add.79), channel_id=1, source_target_pairs={{0,2},{2,0},{4,6},{6,4},{8,10},{10,8},{12,14},{14,12},{1,3},{3,1},... | collective-permute-start | bytes 20 | tf_op jit(solution)/shard_map/ppermute | solution.py:33
  83.0 3.7 %collective-permute-start.15 = (f32[]{:T(128)}, f32[]{:T(128)}, u32[]{:S(2)}, u32[]{:S(2)}) collective-permute-start(f32[]{:T(128)} %add.80), channel_id=1, source_target_pairs={{0,4},{2,6},{4,0},{6,2},{8,12},{10,14},{12,8},{14,10},{1,5},{3,7},... | collective-permute-start | bytes 20 | tf_op jit(solution)/shard_map/ppermute | solution.py:33
  87.4 4.6 %collective-permute-start.16 = (f32[]{:T(128)}, f32[]{:T(128)}, u32[]{:S(2)}, u32[]{:S(2)}) collective-permute-start(f32[]{:T(128)} %add.81), channel_id=1, source_target_pairs={{0,8},{2,10},{4,12},{6,14},{8,0},{10,2},{12,4},{14,6},{1,9},{3,11}... | collective-permute-start | bytes 20 | tf_op jit(solution)/shard_map/ppermute | solution.py:33
  93.1 11.2 %collective-permute-start.17 = (bf16[512,128]{0,1:T(8,128)(2,1)S(1)}, bf16[512,128]{0,1:T(8,128)(2,1)S(1)}, u32[]{:S(2)}, u32[]{:S(2)}) collective-permute-start(bf16[512,128]{0,1:T(8,128)(2,1)S(1)} %get-tuple-element.55), channel_id=1, source_target_pairs={{0,8},{2,10},{4,12},{6,14},{8,0},{10,2},{12,4},{14,6},{1,9},{3,11}... | collective-permute-start | bytes 393224 | tf_op jit(solution)/shard_map/ppermute | solution.py:72
  93.8 10.6 %collective-permute-start.20 = (bf16[512,128]{0,1:T(8,128)(2,1)S(1)}, bf16[512,128]{0,1:T(8,128)(2,1)S(1)}, u32[]{:S(2)}, u32[]{:S(2)}) collective-permute-start(bf16[512,128]{0,1:T(8,128)(2,1)S(1)} %get-tuple-element.56), channel_id=1, source_target_pairs={{0,2},{2,0},{4,6},{6,4},{8,10},{10,8},{12,14},{14,12},{1,3},{3,1},... | collective-permute-start | bytes 393224 | tf_op jit(solution)/shard_map/ppermute | solution.py:72
  104.5 10.9 %collective-permute-start.18 = (bf16[2,512,128]{1,2,0:T(8,128)(2,1)S(1)}, bf16[2,512,128]{1,2,0:T(8,128)(2,1)S(1)}, u32[]{:S(2)}, u32[]{:S(2)}) collective-permute-start(bf16[2,512,128]{1,2,0:T(8,128)(2,1)S(1)} %pad_maximum_fusion.16), channel_id=1, source_target_pairs={{0,4},{2,6},{4,0},{6,2},{8,12},{10,14},{12,8},{14,10},{1,5},{3,7},... | collective-permute-start | bytes 786440 | tf_op jit(solution)/shard_map/ppermute | solution.py:72
  104.6 11.0 %collective-permute-start.21 = (bf16[2,512,128]{1,2,0:T(8,128)(2,1)S(1)}, bf16[2,512,128]{1,2,0:T(8,128)(2,1)S(1)}, u32[]{:S(2)}, u32[]{:S(2)}) collective-permute-start(bf16[2,512,128]{1,2,0:T(8,128)(2,1)S(1)} %pad_maximum_fusion.17), channel_id=1, source_target_pairs={{0,8},{2,10},{4,12},{6,14},{8,0},{10,2},{12,4},{14,6},{1,9},{3,11}... | collective-permute-start | bytes 786440 | tf_op jit(solution)/shard_map/ppermute | solution.py:72
  115.5 9.2 %collective-permute-start.19 = (bf16[2,2,512,128]{2,3,1,0:T(8,128)(2,1)S(1)}, bf16[2,2,512,128]{2,3,1,0:T(8,128)(2,1)S(1)}, u32[]{:S(2)}, u32[]{:S(2)}) collective-permute-start(bf16[2,2,512,128]{2,3,1,0:T(8,128)(2,1)S(1)} %pad_maximum_fusion.8), channel_id=1, source_target_pairs={{0,2},{2,0},{4,6},{6,4},{8,10},{10,8},{12,14},{14,12},{1,3},{3,1},... | collective-permute-start | bytes 1572872 | tf_op jit(solution)/shard_map/ppermute | solution.py:72
  116.5 10.1 %collective-permute-start.22 = (bf16[2,2,512,128]{2,3,1,0:T(8,128)(2,1)}, bf16[2,2,512,128]{2,3,1,0:T(8,128)(2,1)S(1)}, u32[]{:S(2)}, u32[]{:S(2)}) collective-permute-start(bf16[2,2,512,128]{2,3,1,0:T(8,128)(2,1)} %pad_maximum_fusion.9), channel_id=1, source_target_pairs={{0,4},{2,6},{4,0},{6,2},{8,12},{10,14},{12,8},{14,10},{1,5},{3,7},... | collective-permute-start | bytes 1572872 | tf_op jit(solution)/shard_map/ppermute | solution.py:72
  (12 other events, 74.4 us)

commit v16 on v15

--- a/solution.py
+++ b/solution.py
@@ -120,7 +120,7 @@
     summed = scatter_rows(slot_term(inputs, key_grads, live_row, features), "dp")
     tokens_total = (live_count * (inputs.shape[1] * lax.axis_size("dp"))).astype(jnp.float32)
     grad_shard = summed / tokens_total
-    squares = butterfly_sum(jnp.sum(grad_shard * grad_shard), ("pipe", "tensor", "dp"))
+    squares = butterfly_sum(jnp.sum(grad_shard * grad_shard), ("dp", "tensor", "pipe"))
     clip_factor = jnp.minimum(1.0, CLIP_NORM / jnp.sqrt(squares))
     clipped = clip_factor * grad_shard
     moment1 = MOMENT_DECAY * first_moment[0].T + (1.0 - MOMENT_DECAY) * clipped

time: 129 us -> 133 us (1.031)
  waiting for transfers between devices: 60.2 us -> 65.8 us
  starting transfers between devices: 33.2 us -> 31.1 us
    ppermute x6, waiting for transfers between devices: 24.2 us -> 29.5 us  [doubling_gather(): other = lax.ppermute(current, axis, pairs)]
    ppermute x6, starting transfers between devices: 7.25 us -> 5.56 us  [doubling_gather(): other = lax.ppermute(current, axis, pairs)]
  transfers between devices with their start and end apart: 23 -> 23, of which waited for: 17 -> 18; matrix products, arithmetic and copies ran while one was open for 13% -> 13% of each run, Pallas kernels for 0% -> 0%
where the time goes in v16:
time: 133 us
  waiting for transfers between devices  65.8 us (49%)
  starting transfers between devices  31.1 us (23%)
  other arithmetic  14.5 us (11%)
  local copies, waits for them, and re-layouts  9.86 us (7%)
  matrix products  6.18 us (5%)
  between operations  5.04 us (4%)
    ppermute x6, waiting for transfers between devices, doubling_gather(): other = lax.ppermute(current, axis, pairs)  29.5 us
    ppermute x12, waiting for transfers between devices, halving_scatter(): blocks = keep + lax.ppermute(send, axis, pairs)  26.9 us
    ppermute x12, starting transfers between devices, halving_scatter(): blocks = keep + lax.ppermute(send, axis, pairs)  18.1 us
    ppermute x5, waiting for transfers between devices, butterfly_sum(): value = value + lax.ppermute(value, axis, pairs)  9.52 us
    ppermute x5, starting transfers between devices, butterfly_sum(): value = value + lax.ppermute(value, axis, pairs)  7.53 us
    unnamed x45, local copies, waits for them, and re-layouts  6.55 us
    dot_general x1, matrix products, slot_term(): lax.dot_general(weighted, columns, (((0,), (0,)), ((), ())), preferred_el...  6.18 us
    ppermute x6, starting transfers between devices, doubling_gather(): other = lax.ppermute(current, axis, pairs)  5.56 us
  transfers between devices with their start and end apart: 23, of which 18 were waited for; matrix products, arithmetic and copies ran while one was open for 13% of the time, Pallas kernels for 0%

profile of v16, /device:TPU:0, one launch (start us, length us, event | category | flops | bytes accessed | tf_op | source)
XLA Modules:
  0.0 132.5 jit_solution(2714484806936780112)
XLA Ops:
  0.7 6.2 %fusion.2 = f32[256,4096]{1,0:T(8,128)S(1)} fusion(bf16[1,8,128,4096]{3,2,1,0:T(8,128)(2,1)} %param.6, bf16[1,8,128,256]{3,2,1,0:T(8,128)(2,1)} %param.7, pred[8]{0:T(512)(128)(4,1)S(1)} %compare_bitcast_fusion), kind=kOutput, calls=%fused_computation.2 | convolution fusion | flops 2147745792 | bytes 13107208 | tf_op jit(solution)/shard_map/dot_general | solution.py:19
  6.9 1.9 %copy-done = f32[256,4096]{1,0:T(8,128)} copy-done((f32[256,4096]{1,0:T(8,128)}, f32[256,4096]{1,0:T(8,128)S(1)}, u32[]{:S(2)}) %copy-start) | copy-done | bytes 4194328
  10.2 2.9 %collective-permute-start = (f32[64,2048]{1,0:T(8,128)}, f32[64,2048]{1,0:T(8,128)}, u32[]{:S(2)}, u32[]{:S(2)}) collective-permute-start(f32[64,2048]{1,0:T(8,128)} %fusion.19), channel_id=1, source_target_pairs={{0,2},{2,0},{4,6},{6,4},{8,10},{10,8},{12,14},{14,12},{1,3},{3,1},... | collective-permute-start | bytes 1572872 | tf_op jit(solution)/shard_map/ppermute | solution.py:58
  13.2 1.6 %fusion.27 = (f32[64,1024]{1,0:T(8,128)S(1)}, f32[64,1024]{1,0:T(8,128)S(1)}, f32[64,1024]{1,0:T(8,128)S(1)}, f32[64,1024]{1,0:T(8,128)S(1)}, f32[64,1024]{1,0:T...) fusion(f32[256,4096]{1,0:T(8,128)} %copy-done), kind=kLoop, calls=%fused_computation.80 | loop fusion | bytes 4194304 | tf_op jit(solution)/shard_map/slice | solution.py:54
  15.7 1.6 %collective-permute-start.3 = (f32[64,2048]{1,0:T(8,128)}, f32[64,2048]{1,0:T(8,128)}, u32[]{:S(2)}, u32[]{:S(2)}) collective-permute-start(f32[64,2048]{1,0:T(8,128)} %fusion.17), channel_id=1, source_target_pairs={{0,4},{2,6},{4,0},{6,2},{8,12},{10,14},{12,8},{14,10},{1,5},{3,7},... | collective-permute-start | bytes 1572872 | tf_op jit(solution)/shard_map/ppermute | solution.py:58
  21.0 1.2 copy.11
  22.2 1.2 copy.13
  23.5 2.0 %copy.14 = f32[1,512,256]{1,2,0:T(8,128)} copy(f32[1,512,256]{2,1,0:T(8,128)} %param.9) | data formatting | bytes 1048576 | tf_op args[3]
  26.2 1.4 %select_add_fusion.3 = f32[64,2048]{1,0:T(8,128)S(1)} fusion(f32[64,2048]{1,0:T(8,128)} %collective-permute-done, f32[64,512]{1,0:T(8,128)} %copy-done.13, f32[64,512]{1,0:T(8,128)} %copy-done.14, f32[64,512]{1,0:T(8,128)} %copy-done.15, f32[64,512]{1,0:T(8,128)} %copy-done.16, f32[64,512]{1,0:T(8,128)} %copy-done.17, f32[64,512]{1,0:T(8,128)} %copy-done.18, ...), kind=kLoop, calls=%fused_computation.35 | loop fusion | flops 1048576 | bytes 2097153 | tf_op jit(solution)/shard_map/add | solution.py:58
  27.7 2.2 %collective-permute-start.1 = (f32[64,1024]{1,0:T(8,128)S(1)}, f32[64,1024]{1,0:T(8,128)S(1)}, u32[]{:S(2)}, u32[]{:S(2)}) collective-permute-start(f32[64,1024]{1,0:T(8,128)S(1)} %fusion.24), channel_id=1, source_target_pairs={{0,4},{2,6},{4,0},{6,2},{8,12},{10,14},{12,8},{14,10},{1,5},{3,7},... | collective-permute-start | bytes 786440 | tf_op jit(solution)/shard_map/ppermute | solution.py:58
  32.7 4.7 %collective-permute-done.6 = f32[64,2048]{1,0:T(8,128)} collective-permute-done((f32[64,2048]{1,0:T(8,128)}, f32[64,2048]{1,0:T(8,128)}, u32[]{:S(2)}, u32[]{:S(2)}) %collective-permute-start.6) | collective-permute-done | bytes 524320 | tf_op jit(solution)/shard_map/ppermute | solution.py:58
  37.5 1.2 select_add_fusion.1
  38.7 3.2 %collective-permute-start.7 = (f32[64,1024]{1,0:T(8,128)S(1)}, f32[64,1024]{1,0:T(8,128)S(1)}, u32[]{:S(2)}, u32[]{:S(2)}) collective-permute-start(f32[64,1024]{1,0:T(8,128)S(1)} %slice_select_fusion), channel_id=1, source_target_pairs={{0,8},{2,10},{4,12},{6,14},{8,0},{10,2},{12,4},{14,6},{1,9},{3,11}... | collective-permute-start | bytes 786440 | tf_op jit(solution)/shard_map/ppermute | solution.py:58
  41.9 5.8 %collective-permute-done.9 = f32[64,2048]{1,0:T(8,128)} collective-permute-done((f32[64,2048]{1,0:T(8,128)}, f32[64,2048]{1,0:T(8,128)}, u32[]{:S(2)}, u32[]{:S(2)}) %collective-permute-start.9) | collective-permute-done | bytes 524320 | tf_op jit(solution)/shard_map/ppermute | solution.py:58
  49.0 2.7 %collective-permute-done.1 = f32[64,1024]{1,0:T(8,128)S(1)} collective-permute-done((f32[64,1024]{1,0:T(8,128)S(1)}, f32[64,1024]{1,0:T(8,128)S(1)}, u32[]{:S(2)}, u32[]{:S(2)}) %collective-permute-start.1) | collective-permute-done | bytes 262176 | tf_op jit(solution)/shard_map/ppermute | solution.py:58
  51.8 1.2 collective-permute-start.2
  53.1 1.9 %collective-permute-start.5 = (f32[64,512]{1,0:T(8,128)S(1)}, f32[64,512]{1,0:T(8,128)S(1)}, u32[]{:S(2)}, u32[]{:S(2)}) collective-permute-start(f32[64,512]{1,0:T(8,128)S(1)} %slice_select_fusion.3), channel_id=1, source_target_pairs={{0,8},{2,10},{4,12},{6,14},{8,0},{10,2},{12,4},{14,6},{1,9},{3,11}... | collective-permute-start | bytes 393224 | tf_op jit(solution)/shard_map/ppermute | solution.py:58
  55.9 3.0 %collective-permute-start.11 = (f32[64,512]{1,0:T(8,128)S(1)}, f32[64,512]{1,0:T(8,128)S(1)}, u32[]{:S(2)}, u32[]{:S(2)}) collective-permute-start(f32[64,512]{1,0:T(8,128)S(1)} %slice_select_fusion.1), channel_id=1, source_target_pairs={{0,8},{2,10},{4,12},{6,14},{8,0},{10,2},{12,4},{14,6},{1,9},{3,11}... | collective-permute-start | bytes 393224 | tf_op jit(solution)/shard_map/ppermute | solution.py:58
  58.9 6.0 %collective-permute-done.2 = f32[64,512]{1,0:T(8,128)S(1)} collective-permute-done((f32[64,512]{1,0:T(8,128)S(1)}, f32[64,512]{1,0:T(8,128)S(1)}, u32[]{:S(2)}, u32[]{:S(2)}) %collective-permute-start.2) | collective-permute-done | bytes 131104 | tf_op jit(solution)/shard_map/ppermute | solution.py:58
  64.9 4.2 %collective-permute-done.5 = f32[64,512]{1,0:T(8,128)S(1)} collective-permute-done((f32[64,512]{1,0:T(8,128)S(1)}, f32[64,512]{1,0:T(8,128)S(1)}, u32[]{:S(2)}, u32[]{:S(2)}) %collective-permute-start.5) | collective-permute-done | bytes 131104 | tf_op jit(solution)/shard_map/ppermute | solution.py:58
  69.2 1.7 %collective-permute-done.11 = f32[64,512]{1,0:T(8,128)S(1)} collective-permute-done((f32[64,512]{1,0:T(8,128)S(1)}, f32[64,512]{1,0:T(8,128)S(1)}, u32[]{:S(2)}, u32[]{:S(2)}) %collective-permute-start.11) | collective-permute-done | bytes 131104 | tf_op jit(solution)/shard_map/ppermute | solution.py:58
  72.1 3.4 %collective-permute-done.12 = f32[]{:T(128)} collective-permute-done((f32[]{:T(128)}, f32[]{:T(128)}, u32[]{:S(2)}, u32[]{:S(2)}) %collective-permute-start.12) | collective-permute-done | bytes 36 | tf_op jit(solution)/shard_map/ppermute | solution.py:33
  76.7 1.4 %collective-permute-start.13 = (f32[]{:T(128)}, f32[]{:T(128)}, u32[]{:S(2)}, u32[]{:S(2)}) collective-permute-start(f32[]{:T(128)} %add.78), channel_id=1, source_target_pairs={{0,4},{2,6},{4,0},{6,2},{8,12},{10,14},{12,8},{14,10},{1,5},{3,7},... | collective-permute-start | bytes 20 | tf_op jit(solution)/shard_map/ppermute | solution.py:33
  78.1 2.3 %collective-permute-done.13 = f32[]{:T(128)} collective-permute-done((f32[]{:T(128)}, f32[]{:T(128)}, u32[]{:S(2)}, u32[]{:S(2)}) %collective-permute-start.13) | collective-permute-done | bytes 36 | tf_op jit(solution)/shard_map/ppermute | solution.py:33
  81.1 1.9 %collective-permute-start.14 = (f32[]{:T(128)}, f32[]{:T(128)}, u32[]{:S(2)}, u32[]{:S(2)}) collective-permute-start(f32[]{:T(128)} %add.79), channel_id=1, source_target_pairs={{0,8},{2,10},{4,12},{6,14},{8,0},{10,2},{12,4},{14,6},{1,9},{3,11}... | collective-permute-start | bytes 20 | tf_op jit(solution)/shard_map/ppermute | solution.py:33
  83.0 2.7 %collective-permute-done.14 = f32[]{:T(128)} collective-permute-done((f32[]{:T(128)}, f32[]{:T(128)}, u32[]{:S(2)}, u32[]{:S(2)}) %collective-permute-start.14) | collective-permute-done | bytes 36 | tf_op jit(solution)/shard_map/ppermute | solution.py:33
  86.3 2.9 %collective-permute-start.15 = (f32[]{:T(128)}, f32[]{:T(128)}, u32[]{:S(2)}, u32[]{:S(2)}) collective-permute-start(f32[]{:T(128)} %add.80), channel_id=1, source_target_pairs={{0,1},{1,0},{2,3},{3,2},{4,5},{5,4},{6,7},{7,6},{8,9},{9,8},{10,11... | collective-permute-start | bytes 20 | tf_op jit(solution)/shard_map/ppermute | solution.py:33
  94.9 7.1 %collective-permute-done.17 = bf16[512,128]{0,1:T(8,128)(2,1)S(1)} collective-permute-done((bf16[512,128]{0,1:T(8,128)(2,1)S(1)}, bf16[512,128]{0,1:T(8,128)(2,1)S(1)}, u32[]{:S(2)}, u32[]{:S(2)}) %collective-permute-start.17) | collective-permute-done | bytes 131104 | tf_op jit(solution)/shard_map/ppermute | solution.py:72
  102.2 2.6 %collective-permute-start.21 = (bf16[2,512,128]{1,2,0:T(8,128)(2,1)S(1)}, bf16[2,512,128]{1,2,0:T(8,128)(2,1)S(1)}, u32[]{:S(2)}, u32[]{:S(2)}) collective-permute-start(bf16[2,512,128]{1,2,0:T(8,128)(2,1)S(1)} %pad_maximum_fusion.17), channel_id=1, source_target_pairs={{0,8},{2,10},{4,12},{6,14},{8,0},{10,2},{12,4},{14,6},{1,9},{3,11}... | collective-permute-start | bytes 786440 | tf_op jit(solution)/shard_map/ppermute | solution.py:72
  104.8 10.5 %collective-permute-done.18 = bf16[2,512,128]{1,2,0:T(8,128)(2,1)S(1)} collective-permute-done((bf16[2,512,128]{1,2,0:T(8,128)(2,1)S(1)}, bf16[2,512,128]{1,2,0:T(8,128)(2,1)S(1)}, u32[]{:S(2)}, u32[]{:S(2)}) %collective-permute-start.18) | collective-permute-done | bytes 262176 | tf_op jit(solution)/shard_map/ppermute | solution.py:72
  117.9 10.6 %collective-permute-done.19 = bf16[2,2,512,128]{2,3,1,0:T(8,128)(2,1)S(1)} collective-permute-done((bf16[2,2,512,128]{2,3,1,0:T(8,128)(2,1)S(1)}, bf16[2,2,512,128]{2,3,1,0:T(8,128)(2,1)S(1)}, u32[]{:S(2)}, u32[]{:S(2)}) %collective-permute-start.19) | collective-permute-done | bytes 524320 | tf_op jit(solution)/shard_map/ppermute | solution.py:72
  131.0 1.5 %maximum_bitcast_fusion = bf16[1,4096,256]{2,1,0:T(8,128)(2,1)} fusion(bf16[4096,128]{1,0:T(8,128)(2,1)S(1)} %bitcast.75, bf16[4096,128]{1,0:T(8,128)(2,1)S(1)} %bitcast.74), kind=kLoop, calls=%fused_computation.3 | loop fusion | flops 4194304 | bytes 4194304 | tf_op jit(solution)/shard_map/broadcast_in_dim | solution.py:132
  (108 shorter events, 22.5 us)
Async XLA Ops:
  9.1 11.8 %copy-start.12 = (f32[64,512]{1,0:T(8,128)}, f32[64,512]{1,0:T(8,128)S(1)}, u32[]{:S(2)}) copy-start(f32[64,512]{1,0:T(8,128)S(1)} %get-tuple-element.5) | copy-start | bytes 393220
  9.1 11.8 %copy-start.13 = (f32[64,512]{1,0:T(8,128)}, f32[64,512]{1,0:T(8,128)S(1)}, u32[]{:S(2)}) copy-start(f32[64,512]{1,0:T(8,128)S(1)} %get-tuple-element.14) | copy-start | bytes 393220
  9.1 11.8 %copy-start.14 = (f32[64,512]{1,0:T(8,128)}, f32[64,512]{1,0:T(8,128)S(1)}, u32[]{:S(2)}) copy-start(f32[64,512]{1,0:T(8,128)S(1)} %get-tuple-element.15) | copy-start | bytes 393220
  10.2 16.0 %collective-permute-start = (f32[64,2048]{1,0:T(8,128)}, f32[64,2048]{1,0:T(8,128)}, u32[]{:S(2)}, u32[]{:S(2)}) collective-permute-start(f32[64,2048]{1,0:T(8,128)} %fusion.19), channel_id=1, source_target_pairs={{0,2},{2,0},{4,6},{6,4},{8,10},{10,8},{12,14},{14,12},{1,3},{3,1},... | collective-permute-start | bytes 1572872 | tf_op jit(solution)/shard_map/ppermute | solution.py:58
  15.7 15.2 %collective-permute-start.3 = (f32[64,2048]{1,0:T(8,128)}, f32[64,2048]{1,0:T(8,128)}, u32[]{:S(2)}, u32[]{:S(2)}) collective-permute-start(f32[64,2048]{1,0:T(8,128)} %fusion.17), channel_id=1, source_target_pairs={{0,4},{2,6},{4,0},{6,2},{8,12},{10,14},{12,8},{14,10},{1,5},{3,7},... | collective-permute-start | bytes 1572872 | tf_op jit(solution)/shard_map/ppermute | solution.py:58
  18.2 19.3 %collective-permute-start.6 = (f32[64,2048]{1,0:T(8,128)}, f32[64,2048]{1,0:T(8,128)}, u32[]{:S(2)}, u32[]{:S(2)}) collective-permute-start(f32[64,2048]{1,0:T(8,128)} %fusion.18), channel_id=1, source_target_pairs={{0,2},{2,0},{4,6},{6,4},{8,10},{10,8},{12,14},{14,12},{1,3},{3,1},... | collective-permute-start | bytes 1572872 | tf_op jit(solution)/shard_map/ppermute | solution.py:58
  19.6 28.1 %collective-permute-start.9 = (f32[64,2048]{1,0:T(8,128)}, f32[64,2048]{1,0:T(8,128)}, u32[]{:S(2)}, u32[]{:S(2)}) collective-permute-start(f32[64,2048]{1,0:T(8,128)} %fusion.16), channel_id=1, source_target_pairs={{0,4},{2,6},{4,0},{6,2},{8,12},{10,14},{12,8},{14,10},{1,5},{3,7},... | collective-permute-start | bytes 1572872 | tf_op jit(solution)/shard_map/ppermute | solution.py:58
  25.5 12.0 %copy-start.3 = (f32[64,512]{1,0:T(8,128)S(1)}, f32[64,512]{1,0:T(8,128)}, u32[]{:S(2)}) copy-start(f32[64,512]{1,0:T(8,128)} %copy-done.2) | copy-start | bytes 393220
  25.5 12.0 %copy-start.5 = (f32[64,512]{1,0:T(8,128)S(1)}, f32[64,512]{1,0:T(8,128)}, u32[]{:S(2)}) copy-start(f32[64,512]{1,0:T(8,128)} %copy-done.4) | copy-start | bytes 393220
  25.5 12.0 %copy-start.7 = (f32[64,512]{1,0:T(8,128)S(1)}, f32[64,512]{1,0:T(8,128)}, u32[]{:S(2)}) copy-start(f32[64,512]{1,0:T(8,128)} %copy-done.6) | copy-start | bytes 393220
  25.5 12.0 %copy-start.9 = (f32[64,512]{1,0:T(8,128)S(1)}, f32[64,512]{1,0:T(8,128)}, u32[]{:S(2)}) copy-start(f32[64,512]{1,0:T(8,128)} %copy-done.8) | copy-start | bytes 393220
  25.5 12.0 %copy-start.11 = (f32[64,512]{1,0:T(8,128)S(1)}, f32[64,512]{1,0:T(8,128)}, u32[]{:S(2)}) copy-start(f32[64,512]{1,0:T(8,128)} %copy-done.10) | copy-start | bytes 393220
  27.7 24.1 %collective-permute-start.1 = (f32[64,1024]{1,0:T(8,128)S(1)}, f32[64,1024]{1,0:T(8,128)S(1)}, u32[]{:S(2)}, u32[]{:S(2)}) collective-permute-start(f32[64,1024]{1,0:T(8,128)S(1)} %fusion.24), channel_id=1, source_target_pairs={{0,4},{2,6},{4,0},{6,2},{8,12},{10,14},{12,8},{14,10},{1,5},{3,7},... | collective-permute-start | bytes 786440 | tf_op jit(solution)/shard_map/ppermute | solution.py:58
  32.1 21.0 %collective-permute-start.4 = (f32[64,1024]{1,0:T(8,128)S(1)}, f32[64,1024]{1,0:T(8,128)S(1)}, u32[]{:S(2)}, u32[]{:S(2)}) collective-permute-start(f32[64,1024]{1,0:T(8,128)S(1)} %fusion.23), channel_id=1, source_target_pairs={{0,2},{2,0},{4,6},{6,4},{8,10},{10,8},{12,14},{14,12},{1,3},{3,1},... | collective-permute-start | bytes 786440 | tf_op jit(solution)/shard_map/ppermute | solution.py:58
  38.7 16.3 %collective-permute-start.7 = (f32[64,1024]{1,0:T(8,128)S(1)}, f32[64,1024]{1,0:T(8,128)S(1)}, u32[]{:S(2)}, u32[]{:S(2)}) collective-permute-start(f32[64,1024]{1,0:T(8,128)S(1)} %slice_select_fusion), channel_id=1, source_target_pairs={{0,8},{2,10},{4,12},{6,14},{8,0},{10,2},{12,4},{14,6},{1,9},{3,11}... | collective-permute-start | bytes 786440 | tf_op jit(solution)/shard_map/ppermute | solution.py:58
  48.9 43.7 %copy-start.1 = (f32[1,512,256]{1,2,0:T(8,128)S(1)}, f32[1,512,256]{1,2,0:T(8,128)}, u32[]{:S(2)}) copy-start(f32[1,512,256]{1,2,0:T(8,128)} %copy.14) | copy-start | bytes 1572868
  49.0 6.9 %collective-permute-start.10 = (f32[64,1024]{1,0:T(8,128)S(1)}, f32[64,1024]{1,0:T(8,128)S(1)}, u32[]{:S(2)}, u32[]{:S(2)}) collective-permute-start(f32[64,1024]{1,0:T(8,128)S(1)} %fusion.22), channel_id=1, source_target_pairs={{0,2},{2,0},{4,6},{6,4},{8,10},{10,8},{12,14},{14,12},{1,3},{3,1},... | collective-permute-start | bytes 786440 | tf_op jit(solution)/shard_map/ppermute | solution.py:58
  51.8 13.0 %collective-permute-start.2 = (f32[64,512]{1,0:T(8,128)S(1)}, f32[64,512]{1,0:T(8,128)S(1)}, u32[]{:S(2)}, u32[]{:S(2)}) collective-permute-start(f32[64,512]{1,0:T(8,128)S(1)} %slice_select_fusion.4), channel_id=1, source_target_pairs={{0,8},{2,10},{4,12},{6,14},{8,0},{10,2},{12,4},{14,6},{1,9},{3,11}... | collective-permute-start | bytes 393224 | tf_op jit(solution)/shard_map/ppermute | solution.py:58
  53.1 16.0 %collective-permute-start.5 = (f32[64,512]{1,0:T(8,128)S(1)}, f32[64,512]{1,0:T(8,128)S(1)}, u32[]{:S(2)}, u32[]{:S(2)}) collective-permute-start(f32[64,512]{1,0:T(8,128)S(1)} %slice_select_fusion.3), channel_id=1, source_target_pairs={{0,8},{2,10},{4,12},{6,14},{8,0},{10,2},{12,4},{14,6},{1,9},{3,11}... | collective-permute-start | bytes 393224 | tf_op jit(solution)/shard_map/ppermute | solution.py:58
  55.1 14.1 %collective-permute-start.8 = (f32[64,512]{1,0:T(8,128)S(1)}, f32[64,512]{1,0:T(8,128)S(1)}, u32[]{:S(2)}, u32[]{:S(2)}) collective-permute-start(f32[64,512]{1,0:T(8,128)S(1)} %slice_select_fusion.2), channel_id=1, source_target_pairs={{0,4},{2,6},{4,0},{6,2},{8,12},{10,14},{12,8},{14,10},{1,5},{3,7},... | collective-permute-start | bytes 393224 | tf_op jit(solution)/shard_map/ppermute | solution.py:58
  55.9 15.0 %collective-permute-start.11 = (f32[64,512]{1,0:T(8,128)S(1)}, f32[64,512]{1,0:T(8,128)S(1)}, u32[]{:S(2)}, u32[]{:S(2)}) collective-permute-start(f32[64,512]{1,0:T(8,128)S(1)} %slice_select_fusion.1), channel_id=1, source_target_pairs={{0,8},{2,10},{4,12},{6,14},{8,0},{10,2},{12,4},{14,6},{1,9},{3,11}... | collective-permute-start | bytes 393224 | tf_op jit(solution)/shard_map/ppermute | solution.py:58
  71.7 3.7 %collective-permute-start.12 = (f32[]{:T(128)}, f32[]{:T(128)}, u32[]{:S(2)}, u32[]{:S(2)}) collective-permute-start(f32[]{:T(128)} %multiply_reduce_fusion), channel_id=1, source_target_pairs={{0,2},{2,0},{4,6},{6,4},{8,10},{10,8},{12,14},{14,12},{1,3},{3,1},... | collective-permute-start | bytes 20 | tf_op jit(solution)/shard_map/ppermute | solution.py:33
  76.7 3.7 %collective-permute-start.13 = (f32[]{:T(128)}, f32[]{:T(128)}, u32[]{:S(2)}, u32[]{:S(2)}) collective-permute-start(f32[]{:T(128)} %add.78), channel_id=1, source_target_pairs={{0,4},{2,6},{4,0},{6,2},{8,12},{10,14},{12,8},{14,10},{1,5},{3,7},... | collective-permute-start | bytes 20 | tf_op jit(solution)/shard_map/ppermute | solution.py:33
  81.1 4.6 %collective-permute-start.14 = (f32[]{:T(128)}, f32[]{:T(128)}, u32[]{:S(2)}, u32[]{:S(2)}) collective-permute-start(f32[]{:T(128)} %add.79), channel_id=1, source_target_pairs={{0,8},{2,10},{4,12},{6,14},{8,0},{10,2},{12,4},{14,6},{1,9},{3,11}... | collective-permute-start | bytes 20 | tf_op jit(solution)/shard_map/ppermute | solution.py:33
  86.3 3.7 %collective-permute-start.15 = (f32[]{:T(128)}, f32[]{:T(128)}, u32[]{:S(2)}, u32[]{:S(2)}) collective-permute-start(f32[]{:T(128)} %add.80), channel_id=1, source_target_pairs={{0,1},{1,0},{2,3},{3,2},{4,5},{5,4},{6,7},{7,6},{8,9},{9,8},{10,11... | collective-permute-start | bytes 20 | tf_op jit(solution)/shard_map/ppermute | solution.py:33
  90.7 1.3 collective-permute-start.16
  93.1 8.8 %collective-permute-start.17 = (bf16[512,128]{0,1:T(8,128)(2,1)S(1)}, bf16[512,128]{0,1:T(8,128)(2,1)S(1)}, u32[]{:S(2)}, u32[]{:S(2)}) collective-permute-start(bf16[512,128]{0,1:T(8,128)(2,1)S(1)} %get-tuple-element.55), channel_id=1, source_target_pairs={{0,8},{2,10},{4,12},{6,14},{8,0},{10,2},{12,4},{14,6},{1,9},{3,11}... | collective-permute-start | bytes 393224 | tf_op jit(solution)/shard_map/ppermute | solution.py:72
  93.8 8.2 %collective-permute-start.20 = (bf16[512,128]{0,1:T(8,128)(2,1)S(1)}, bf16[512,128]{0,1:T(8,128)(2,1)S(1)}, u32[]{:S(2)}, u32[]{:S(2)}) collective-permute-start(bf16[512,128]{0,1:T(8,128)(2,1)S(1)} %get-tuple-element.56), channel_id=1, source_target_pairs={{0,2},{2,0},{4,6},{6,4},{8,10},{10,8},{12,14},{14,12},{1,3},{3,1},... | collective-permute-start | bytes 393224 | tf_op jit(solution)/shard_map/ppermute | solution.py:72
  102.0 13.3 %collective-permute-start.18 = (bf16[2,512,128]{1,2,0:T(8,128)(2,1)S(1)}, bf16[2,512,128]{1,2,0:T(8,128)(2,1)S(1)}, u32[]{:S(2)}, u32[]{:S(2)}) collective-permute-start(bf16[2,512,128]{1,2,0:T(8,128)(2,1)S(1)} %pad_maximum_fusion.16), channel_id=1, source_target_pairs={{0,4},{2,6},{4,0},{6,2},{8,12},{10,14},{12,8},{14,10},{1,5},{3,7},... | collective-permute-start | bytes 786440 | tf_op jit(solution)/shard_map/ppermute | solution.py:72
  102.2 14.9 %collective-permute-start.21 = (bf16[2,512,128]{1,2,0:T(8,128)(2,1)S(1)}, bf16[2,512,128]{1,2,0:T(8,128)(2,1)S(1)}, u32[]{:S(2)}, u32[]{:S(2)}) collective-permute-start(bf16[2,512,128]{1,2,0:T(8,128)(2,1)S(1)} %pad_maximum_fusion.17), channel_id=1, source_target_pairs={{0,8},{2,10},{4,12},{6,14},{8,0},{10,2},{12,4},{14,6},{1,9},{3,11}... | collective-permute-start | bytes 786440 | tf_op jit(solution)/shard_map/ppermute | solution.py:72
  115.4 13.1 %collective-permute-start.19 = (bf16[2,2,512,128]{2,3,1,0:T(8,128)(2,1)S(1)}, bf16[2,2,512,128]{2,3,1,0:T(8,128)(2,1)S(1)}, u32[]{:S(2)}, u32[]{:S(2)}) collective-permute-start(bf16[2,2,512,128]{2,3,1,0:T(8,128)(2,1)S(1)} %pad_maximum_fusion.8), channel_id=1, source_target_pairs={{0,2},{2,0},{4,6},{6,4},{8,10},{10,8},{12,14},{14,12},{1,3},{3,1},... | collective-permute-start | bytes 1572872 | tf_op jit(solution)/shard_map/ppermute | solution.py:72
  117.9 12.2 %collective-permute-start.22 = (bf16[2,2,512,128]{2,3,1,0:T(8,128)(2,1)}, bf16[2,2,512,128]{2,3,1,0:T(8,128)(2,1)S(1)}, u32[]{:S(2)}, u32[]{:S(2)}) collective-permute-start(bf16[2,2,512,128]{2,3,1,0:T(8,128)(2,1)} %pad_maximum_fusion.9), channel_id=1, source_target_pairs={{0,4},{2,6},{4,0},{6,2},{8,12},{10,14},{12,8},{14,10},{1,5},{3,7},... | collective-permute-start | bytes 1572872 | tf_op jit(solution)/shard_map/ppermute | solution.py:72
  (12 other events, 74.4 us)

commit v17 on v16

--- a/solution.py
+++ b/solution.py
@@ -120,7 +120,7 @@
     summed = scatter_rows(slot_term(inputs, key_grads, live_row, features), "dp")
     tokens_total = (live_count * (inputs.shape[1] * lax.axis_size("dp"))).astype(jnp.float32)
     grad_shard = summed / tokens_total
-    squares = butterfly_sum(jnp.sum(grad_shard * grad_shard), ("dp", "tensor", "pipe"))
+    squares = butterfly_sum(jnp.sum(grad_shard * grad_shard), ("tensor", "pipe", "dp"))
     clip_factor = jnp.minimum(1.0, CLIP_NORM / jnp.sqrt(squares))
     clipped = clip_factor * grad_shard
     moment1 = MOMENT_DECAY * first_moment[0].T + (1.0 - MOMENT_DECAY) * clipped

time: 133 us -> 126 us (0.947)
  waiting for transfers between devices: 65.8 us -> 59.1 us
    ppermute x6, waiting for transfers between devices: 29.5 us -> 22.7 us  [doubling_gather(): other = lax.ppermute(current, axis, pairs)]
  transfers between devices with their start and end apart: 23 -> 23, of which waited for: 18 -> 17; matrix products, arithmetic and copies ran while one was open for 13% -> 13% of each run, Pallas kernels for 0% -> 0%
where the time goes in v17:
time: 126 us; the launch traced here: 125 us
  waiting for transfers between devices  59.1 us (47%)
  starting transfers between devices  30.7 us (24%)
  other arithmetic  14.5 us (12%)
  local copies, waits for them, and re-layouts  9.86 us (8%)
  matrix products  6.18 us (5%)
  between operations  5.04 us (4%)
    ppermute x12, waiting for transfers between devices, halving_scatter(): blocks = keep + lax.ppermute(send, axis, pairs)  26.9 us
    ppermute x6, waiting for transfers between devices, doubling_gather(): other = lax.ppermute(current, axis, pairs)  22.7 us
    ppermute x12, starting transfers between devices, halving_scatter(): blocks = keep + lax.ppermute(send, axis, pairs)  18.1 us
    ppermute x5, waiting for transfers between devices, butterfly_sum(): value = value + lax.ppermute(value, axis, pairs)  9.52 us
    ppermute x5, starting transfers between devices, butterfly_sum(): value = value + lax.ppermute(value, axis, pairs)  7.53 us
    unnamed x45, local copies, waits for them, and re-layouts  6.55 us
    dot_general x1, matrix products, slot_term(): lax.dot_general(weighted, columns, (((0,), (0,)), ((), ())), preferred_el...  6.18 us
    ppermute x6, starting transfers between devices, doubling_gather(): other = lax.ppermute(current, axis, pairs)  5.14 us
  transfers between devices with their start and end apart: 23, of which 17 were waited for; matrix products, arithmetic and copies ran while one was open for 13% of the time, Pallas kernels for 0%

profile of v17, /device:TPU:0, one launch (start us, length us, event | category | flops | bytes accessed | tf_op | source)
XLA Modules:
  0.0 125.3 jit_solution(11246238359965276132)
XLA Ops:
  0.7 6.2 %fusion.2 = f32[256,4096]{1,0:T(8,128)S(1)} fusion(bf16[1,8,128,4096]{3,2,1,0:T(8,128)(2,1)} %param.6, bf16[1,8,128,256]{3,2,1,0:T(8,128)(2,1)} %param.7, pred[8]{0:T(512)(128)(4,1)S(1)} %compare_bitcast_fusion), kind=kOutput, calls=%fused_computation.2 | convolution fusion | flops 2147745792 | bytes 13107208 | tf_op jit(solution)/shard_map/dot_general | solution.py:19
  6.9 1.9 %copy-done = f32[256,4096]{1,0:T(8,128)} copy-done((f32[256,4096]{1,0:T(8,128)}, f32[256,4096]{1,0:T(8,128)S(1)}, u32[]{:S(2)}) %copy-start) | copy-done | bytes 4194328
  10.2 2.9 %collective-permute-start = (f32[64,2048]{1,0:T(8,128)}, f32[64,2048]{1,0:T(8,128)}, u32[]{:S(2)}, u32[]{:S(2)}) collective-permute-start(f32[64,2048]{1,0:T(8,128)} %fusion.19), channel_id=1, source_target_pairs={{0,2},{2,0},{4,6},{6,4},{8,10},{10,8},{12,14},{14,12},{1,3},{3,1},... | collective-permute-start | bytes 1572872 | tf_op jit(solution)/shard_map/ppermute | solution.py:58
  13.2 1.6 %fusion.27 = (f32[64,1024]{1,0:T(8,128)S(1)}, f32[64,1024]{1,0:T(8,128)S(1)}, f32[64,1024]{1,0:T(8,128)S(1)}, f32[64,1024]{1,0:T(8,128)S(1)}, f32[64,1024]{1,0:T...) fusion(f32[256,4096]{1,0:T(8,128)} %copy-done), kind=kLoop, calls=%fused_computation.80 | loop fusion | bytes 4194304 | tf_op jit(solution)/shard_map/slice | solution.py:54
  15.7 1.6 %collective-permute-start.3 = (f32[64,2048]{1,0:T(8,128)}, f32[64,2048]{1,0:T(8,128)}, u32[]{:S(2)}, u32[]{:S(2)}) collective-permute-start(f32[64,2048]{1,0:T(8,128)} %fusion.17), channel_id=1, source_target_pairs={{0,4},{2,6},{4,0},{6,2},{8,12},{10,14},{12,8},{14,10},{1,5},{3,7},... | collective-permute-start | bytes 1572872 | tf_op jit(solution)/shard_map/ppermute | solution.py:58
  21.0 1.2 copy.11
  22.2 1.2 copy.13
  23.5 2.0 %copy.14 = f32[1,512,256]{1,2,0:T(8,128)} copy(f32[1,512,256]{2,1,0:T(8,128)} %param.9) | data formatting | bytes 1048576 | tf_op args[3]
  26.2 1.4 %select_add_fusion.3 = f32[64,2048]{1,0:T(8,128)S(1)} fusion(f32[64,2048]{1,0:T(8,128)} %collective-permute-done, f32[64,512]{1,0:T(8,128)} %copy-done.13, f32[64,512]{1,0:T(8,128)} %copy-done.14, f32[64,512]{1,0:T(8,128)} %copy-done.15, f32[64,512]{1,0:T(8,128)} %copy-done.16, f32[64,512]{1,0:T(8,128)} %copy-done.17, f32[64,512]{1,0:T(8,128)} %copy-done.18, ...), kind=kLoop, calls=%fused_computation.35 | loop fusion | flops 1048576 | bytes 2097153 | tf_op jit(solution)/shard_map/add | solution.py:58
  27.7 2.2 %collective-permute-start.1 = (f32[64,1024]{1,0:T(8,128)S(1)}, f32[64,1024]{1,0:T(8,128)S(1)}, u32[]{:S(2)}, u32[]{:S(2)}) collective-permute-start(f32[64,1024]{1,0:T(8,128)S(1)} %fusion.24), channel_id=1, source_target_pairs={{0,4},{2,6},{4,0},{6,2},{8,12},{10,14},{12,8},{14,10},{1,5},{3,7},... | collective-permute-start | bytes 786440 | tf_op jit(solution)/shard_map/ppermute | solution.py:58
  32.7 4.7 %collective-permute-done.6 = f32[64,2048]{1,0:T(8,128)} collective-permute-done((f32[64,2048]{1,0:T(8,128)}, f32[64,2048]{1,0:T(8,128)}, u32[]{:S(2)}, u32[]{:S(2)}) %collective-permute-start.6) | collective-permute-done | bytes 524320 | tf_op jit(solution)/shard_map/ppermute | solution.py:58
  38.7 3.2 %collective-permute-start.7 = (f32[64,1024]{1,0:T(8,128)S(1)}, f32[64,1024]{1,0:T(8,128)S(1)}, u32[]{:S(2)}, u32[]{:S(2)}) collective-permute-start(f32[64,1024]{1,0:T(8,128)S(1)} %slice_select_fusion), channel_id=1, source_target_pairs={{0,8},{2,10},{4,12},{6,14},{8,0},{10,2},{12,4},{14,6},{1,9},{3,11}... | collective-permute-start | bytes 786440 | tf_op jit(solution)/shard_map/ppermute | solution.py:58
  41.9 5.8 %collective-permute-done.9 = f32[64,2048]{1,0:T(8,128)} collective-permute-done((f32[64,2048]{1,0:T(8,128)}, f32[64,2048]{1,0:T(8,128)}, u32[]{:S(2)}, u32[]{:S(2)}) %collective-permute-start.9) | collective-permute-done | bytes 524320 | tf_op jit(solution)/shard_map/ppermute | solution.py:58
  49.0 2.7 %collective-permute-done.1 = f32[64,1024]{1,0:T(8,128)S(1)} collective-permute-done((f32[64,1024]{1,0:T(8,128)S(1)}, f32[64,1024]{1,0:T(8,128)S(1)}, u32[]{:S(2)}, u32[]{:S(2)}) %collective-permute-start.1) | collective-permute-done | bytes 262176 | tf_op jit(solution)/shard_map/ppermute | solution.py:58
  53.1 1.9 %collective-permute-start.5 = (f32[64,512]{1,0:T(8,128)S(1)}, f32[64,512]{1,0:T(8,128)S(1)}, u32[]{:S(2)}, u32[]{:S(2)}) collective-permute-start(f32[64,512]{1,0:T(8,128)S(1)} %slice_select_fusion.3), channel_id=1, source_target_pairs={{0,8},{2,10},{4,12},{6,14},{8,0},{10,2},{12,4},{14,6},{1,9},{3,11}... | collective-permute-start | bytes 393224 | tf_op jit(solution)/shard_map/ppermute | solution.py:58
  55.9 3.0 %collective-permute-start.11 = (f32[64,512]{1,0:T(8,128)S(1)}, f32[64,512]{1,0:T(8,128)S(1)}, u32[]{:S(2)}, u32[]{:S(2)}) collective-permute-start(f32[64,512]{1,0:T(8,128)S(1)} %slice_select_fusion.1), channel_id=1, source_target_pairs={{0,8},{2,10},{4,12},{6,14},{8,0},{10,2},{12,4},{14,6},{1,9},{3,11}... | collective-permute-start | bytes 393224 | tf_op jit(solution)/shard_map/ppermute | solution.py:58
  58.9 6.0 %collective-permute-done.2 = f32[64,512]{1,0:T(8,128)S(1)} collective-permute-done((f32[64,512]{1,0:T(8,128)S(1)}, f32[64,512]{1,0:T(8,128)S(1)}, u32[]{:S(2)}, u32[]{:S(2)}) %collective-permute-start.2) | collective-permute-done | bytes 131104 | tf_op jit(solution)/shard_map/ppermute | solution.py:58
  64.9 4.2 %collective-permute-done.5 = f32[64,512]{1,0:T(8,128)S(1)} collective-permute-done((f32[64,512]{1,0:T(8,128)S(1)}, f32[64,512]{1,0:T(8,128)S(1)}, u32[]{:S(2)}, u32[]{:S(2)}) %collective-permute-start.5) | collective-permute-done | bytes 131104 | tf_op jit(solution)/shard_map/ppermute | solution.py:58
  69.2 1.7 %collective-permute-done.11 = f32[64,512]{1,0:T(8,128)S(1)} collective-permute-done((f32[64,512]{1,0:T(8,128)S(1)}, f32[64,512]{1,0:T(8,128)S(1)}, u32[]{:S(2)}, u32[]{:S(2)}) %collective-permute-start.11) | collective-permute-done | bytes 131104 | tf_op jit(solution)/shard_map/ppermute | solution.py:58
  71.7 1.5 %collective-permute-start.12 = (f32[]{:T(128)}, f32[]{:T(128)}, u32[]{:S(2)}, u32[]{:S(2)}) collective-permute-start(f32[]{:T(128)} %multiply_reduce_fusion), channel_id=1, source_target_pairs={{0,1},{1,0},{2,3},{3,2},{4,5},{5,4},{6,7},{7,6},{8,9},{9,8},{10,11... | collective-permute-start | bytes 20 | tf_op jit(solution)/shard_map/ppermute | solution.py:33
  73.3 2.2 %collective-permute-done.12 = f32[]{:T(128)} collective-permute-done((f32[]{:T(128)}, f32[]{:T(128)}, u32[]{:S(2)}, u32[]{:S(2)}) %collective-permute-start.12) | collective-permute-done | bytes 36 | tf_op jit(solution)/shard_map/ppermute | solution.py:33
  78.7 1.7 %collective-permute-start.14 = (f32[]{:T(128)}, f32[]{:T(128)}, u32[]{:S(2)}, u32[]{:S(2)}) collective-permute-start(f32[]{:T(128)} %add.79), channel_id=1, source_target_pairs={{0,2},{2,0},{4,6},{6,4},{8,10},{10,8},{12,14},{14,12},{1,3},{3,1},... | collective-permute-start | bytes 20 | tf_op jit(solution)/shard_map/ppermute | solution.py:33
  80.4 2.0 %collective-permute-done.14 = f32[]{:T(128)} collective-permute-done((f32[]{:T(128)}, f32[]{:T(128)}, u32[]{:S(2)}, u32[]{:S(2)}) %collective-permute-start.14) | collective-permute-done | bytes 36 | tf_op jit(solution)/shard_map/ppermute | solution.py:33
  83.0 1.4 %collective-permute-start.15 = (f32[]{:T(128)}, f32[]{:T(128)}, u32[]{:S(2)}, u32[]{:S(2)}) collective-permute-start(f32[]{:T(128)} %add.80), channel_id=1, source_target_pairs={{0,4},{2,6},{4,0},{6,2},{8,12},{10,14},{12,8},{14,10},{1,5},{3,7},... | collective-permute-start | bytes 20 | tf_op jit(solution)/shard_map/ppermute | solution.py:33
  84.4 2.3 %collective-permute-done.15 = f32[]{:T(128)} collective-permute-done((f32[]{:T(128)}, f32[]{:T(128)}, u32[]{:S(2)}, u32[]{:S(2)}) %collective-permute-start.15) | collective-permute-done | bytes 36 | tf_op jit(solution)/shard_map/ppermute | solution.py:33
  87.4 1.9 %collective-permute-start.16 = (f32[]{:T(128)}, f32[]{:T(128)}, u32[]{:S(2)}, u32[]{:S(2)}) collective-permute-start(f32[]{:T(128)} %add.81), channel_id=1, source_target_pairs={{0,8},{2,10},{4,12},{6,14},{8,0},{10,2},{12,4},{14,6},{1,9},{3,11}... | collective-permute-start | bytes 20 | tf_op jit(solution)/shard_map/ppermute | solution.py:33
  89.3 2.7 %collective-permute-done.16 = f32[]{:T(128)} collective-permute-done((f32[]{:T(128)}, f32[]{:T(128)}, u32[]{:S(2)}, u32[]{:S(2)}) %collective-permute-start.16) | collective-permute-done | bytes 36 | tf_op jit(solution)/shard_map/ppermute | solution.py:33
  94.9 5.9 %collective-permute-done.17 = bf16[512,128]{0,1:T(8,128)(2,1)S(1)} collective-permute-done((bf16[512,128]{0,1:T(8,128)(2,1)S(1)}, bf16[512,128]{0,1:T(8,128)(2,1)S(1)}, u32[]{:S(2)}, u32[]{:S(2)}) %collective-permute-start.17) | collective-permute-done | bytes 131104 | tf_op jit(solution)/shard_map/ppermute | solution.py:72
  101.0 2.6 %collective-permute-start.21 = (bf16[2,512,128]{1,2,0:T(8,128)(2,1)S(1)}, bf16[2,512,128]{1,2,0:T(8,128)(2,1)S(1)}, u32[]{:S(2)}, u32[]{:S(2)}) collective-permute-start(bf16[2,512,128]{1,2,0:T(8,128)(2,1)S(1)} %pad_maximum_fusion.17), channel_id=1, source_target_pairs={{0,8},{2,10},{4,12},{6,14},{8,0},{10,2},{12,4},{14,6},{1,9},{3,11}... | collective-permute-start | bytes 786440 | tf_op jit(solution)/shard_map/ppermute | solution.py:72
  103.6 8.3 %collective-permute-done.18 = bf16[2,512,128]{1,2,0:T(8,128)(2,1)S(1)} collective-permute-done((bf16[2,512,128]{1,2,0:T(8,128)(2,1)S(1)}, bf16[2,512,128]{1,2,0:T(8,128)(2,1)S(1)}, u32[]{:S(2)}, u32[]{:S(2)}) %collective-permute-start.18) | collective-permute-done | bytes 262176 | tf_op jit(solution)/shard_map/ppermute | solution.py:72
  113.5 7.7 %collective-permute-done.19 = bf16[2,2,512,128]{2,3,1,0:T(8,128)(2,1)S(1)} collective-permute-done((bf16[2,2,512,128]{2,3,1,0:T(8,128)(2,1)S(1)}, bf16[2,2,512,128]{2,3,1,0:T(8,128)(2,1)S(1)}, u32[]{:S(2)}, u32[]{:S(2)}) %collective-permute-start.19) | collective-permute-done | bytes 524320 | tf_op jit(solution)/shard_map/ppermute | solution.py:72
  123.8 1.5 %maximum_bitcast_fusion = bf16[1,4096,256]{2,1,0:T(8,128)(2,1)} fusion(bf16[4096,128]{1,0:T(8,128)(2,1)S(1)} %bitcast.75, bf16[4096,128]{1,0:T(8,128)(2,1)S(1)} %bitcast.74), kind=kLoop, calls=%fused_computation.3 | loop fusion | flops 4194304 | bytes 4194304 | tf_op jit(solution)/shard_map/broadcast_in_dim | solution.py:132
  (108 shorter events, 22.8 us)
Async XLA Ops:
  9.1 11.8 %copy-start.12 = (f32[64,512]{1,0:T(8,128)}, f32[64,512]{1,0:T(8,128)S(1)}, u32[]{:S(2)}) copy-start(f32[64,512]{1,0:T(8,128)S(1)} %get-tuple-element.5) | copy-start | bytes 393220
  9.1 11.8 %copy-start.13 = (f32[64,512]{1,0:T(8,128)}, f32[64,512]{1,0:T(8,128)S(1)}, u32[]{:S(2)}) copy-start(f32[64,512]{1,0:T(8,128)S(1)} %get-tuple-element.14) | copy-start | bytes 393220
  9.1 11.8 %copy-start.14 = (f32[64,512]{1,0:T(8,128)}, f32[64,512]{1,0:T(8,128)S(1)}, u32[]{:S(2)}) copy-start(f32[64,512]{1,0:T(8,128)S(1)} %get-tuple-element.15) | copy-start | bytes 393220
  10.2 16.0 %collective-permute-start = (f32[64,2048]{1,0:T(8,128)}, f32[64,2048]{1,0:T(8,128)}, u32[]{:S(2)}, u32[]{:S(2)}) collective-permute-start(f32[64,2048]{1,0:T(8,128)} %fusion.19), channel_id=1, source_target_pairs={{0,2},{2,0},{4,6},{6,4},{8,10},{10,8},{12,14},{14,12},{1,3},{3,1},... | collective-permute-start | bytes 1572872 | tf_op jit(solution)/shard_map/ppermute | solution.py:58
  15.7 15.2 %collective-permute-start.3 = (f32[64,2048]{1,0:T(8,128)}, f32[64,2048]{1,0:T(8,128)}, u32[]{:S(2)}, u32[]{:S(2)}) collective-permute-start(f32[64,2048]{1,0:T(8,128)} %fusion.17), channel_id=1, source_target_pairs={{0,4},{2,6},{4,0},{6,2},{8,12},{10,14},{12,8},{14,10},{1,5},{3,7},... | collective-permute-start | bytes 1572872 | tf_op jit(solution)/shard_map/ppermute | solution.py:58
  18.2 19.3 %collective-permute-start.6 = (f32[64,2048]{1,0:T(8,128)}, f32[64,2048]{1,0:T(8,128)}, u32[]{:S(2)}, u32[]{:S(2)}) collective-permute-start(f32[64,2048]{1,0:T(8,128)} %fusion.18), channel_id=1, source_target_pairs={{0,2},{2,0},{4,6},{6,4},{8,10},{10,8},{12,14},{14,12},{1,3},{3,1},... | collective-permute-start | bytes 1572872 | tf_op jit(solution)/shard_map/ppermute | solution.py:58
  19.6 28.1 %collective-permute-start.9 = (f32[64,2048]{1,0:T(8,128)}, f32[64,2048]{1,0:T(8,128)}, u32[]{:S(2)}, u32[]{:S(2)}) collective-permute-start(f32[64,2048]{1,0:T(8,128)} %fusion.16), channel_id=1, source_target_pairs={{0,4},{2,6},{4,0},{6,2},{8,12},{10,14},{12,8},{14,10},{1,5},{3,7},... | collective-permute-start | bytes 1572872 | tf_op jit(solution)/shard_map/ppermute | solution.py:58
  25.5 12.0 %copy-start.3 = (f32[64,512]{1,0:T(8,128)S(1)}, f32[64,512]{1,0:T(8,128)}, u32[]{:S(2)}) copy-start(f32[64,512]{1,0:T(8,128)} %copy-done.2) | copy-start | bytes 393220
  25.5 12.0 %copy-start.5 = (f32[64,512]{1,0:T(8,128)S(1)}, f32[64,512]{1,0:T(8,128)}, u32[]{:S(2)}) copy-start(f32[64,512]{1,0:T(8,128)} %copy-done.4) | copy-start | bytes 393220
  25.5 12.0 %copy-start.7 = (f32[64,512]{1,0:T(8,128)S(1)}, f32[64,512]{1,0:T(8,128)}, u32[]{:S(2)}) copy-start(f32[64,512]{1,0:T(8,128)} %copy-done.6) | copy-start | bytes 393220
  25.5 12.0 %copy-start.9 = (f32[64,512]{1,0:T(8,128)S(1)}, f32[64,512]{1,0:T(8,128)}, u32[]{:S(2)}) copy-start(f32[64,512]{1,0:T(8,128)} %copy-done.8) | copy-start | bytes 393220
  25.5 12.0 %copy-start.11 = (f32[64,512]{1,0:T(8,128)S(1)}, f32[64,512]{1,0:T(8,128)}, u32[]{:S(2)}) copy-start(f32[64,512]{1,0:T(8,128)} %copy-done.10) | copy-start | bytes 393220
  27.7 24.1 %collective-permute-start.1 = (f32[64,1024]{1,0:T(8,128)S(1)}, f32[64,1024]{1,0:T(8,128)S(1)}, u32[]{:S(2)}, u32[]{:S(2)}) collective-permute-start(f32[64,1024]{1,0:T(8,128)S(1)} %fusion.24), channel_id=1, source_target_pairs={{0,4},{2,6},{4,0},{6,2},{8,12},{10,14},{12,8},{14,10},{1,5},{3,7},... | collective-permute-start | bytes 786440 | tf_op jit(solution)/shard_map/ppermute | solution.py:58
  32.1 21.0 %collective-permute-start.4 = (f32[64,1024]{1,0:T(8,128)S(1)}, f32[64,1024]{1,0:T(8,128)S(1)}, u32[]{:S(2)}, u32[]{:S(2)}) collective-permute-start(f32[64,1024]{1,0:T(8,128)S(1)} %fusion.23), channel_id=1, source_target_pairs={{0,2},{2,0},{4,6},{6,4},{8,10},{10,8},{12,14},{14,12},{1,3},{3,1},... | collective-permute-start | bytes 786440 | tf_op jit(solution)/shard_map/ppermute | solution.py:58
  38.7 16.3 %collective-permute-start.7 = (f32[64,1024]{1,0:T(8,128)S(1)}, f32[64,1024]{1,0:T(8,128)S(1)}, u32[]{:S(2)}, u32[]{:S(2)}) collective-permute-start(f32[64,1024]{1,0:T(8,128)S(1)} %slice_select_fusion), channel_id=1, source_target_pairs={{0,8},{2,10},{4,12},{6,14},{8,0},{10,2},{12,4},{14,6},{1,9},{3,11}... | collective-permute-start | bytes 786440 | tf_op jit(solution)/shard_map/ppermute | solution.py:58
  48.9 43.7 %copy-start.1 = (f32[1,512,256]{1,2,0:T(8,128)S(1)}, f32[1,512,256]{1,2,0:T(8,128)}, u32[]{:S(2)}) copy-start(f32[1,512,256]{1,2,0:T(8,128)} %copy.14) | copy-start | bytes 1572868
  49.0 6.9 %collective-permute-start.10 = (f32[64,1024]{1,0:T(8,128)S(1)}, f32[64,1024]{1,0:T(8,128)S(1)}, u32[]{:S(2)}, u32[]{:S(2)}) collective-permute-start(f32[64,1024]{1,0:T(8,128)S(1)} %fusion.22), channel_id=1, source_target_pairs={{0,2},{2,0},{4,6},{6,4},{8,10},{10,8},{12,14},{14,12},{1,3},{3,1},... | collective-permute-start | bytes 786440 | tf_op jit(solution)/shard_map/ppermute | solution.py:58
  51.8 13.0 %collective-permute-start.2 = (f32[64,512]{1,0:T(8,128)S(1)}, f32[64,512]{1,0:T(8,128)S(1)}, u32[]{:S(2)}, u32[]{:S(2)}) collective-permute-start(f32[64,512]{1,0:T(8,128)S(1)} %slice_select_fusion.4), channel_id=1, source_target_pairs={{0,8},{2,10},{4,12},{6,14},{8,0},{10,2},{12,4},{14,6},{1,9},{3,11}... | collective-permute-start | bytes 393224 | tf_op jit(solution)/shard_map/ppermute | solution.py:58
  53.1 16.0 %collective-permute-start.5 = (f32[64,512]{1,0:T(8,128)S(1)}, f32[64,512]{1,0:T(8,128)S(1)}, u32[]{:S(2)}, u32[]{:S(2)}) collective-permute-start(f32[64,512]{1,0:T(8,128)S(1)} %slice_select_fusion.3), channel_id=1, source_target_pairs={{0,8},{2,10},{4,12},{6,14},{8,0},{10,2},{12,4},{14,6},{1,9},{3,11}... | collective-permute-start | bytes 393224 | tf_op jit(solution)/shard_map/ppermute | solution.py:58
  55.1 14.1 %collective-permute-start.8 = (f32[64,512]{1,0:T(8,128)S(1)}, f32[64,512]{1,0:T(8,128)S(1)}, u32[]{:S(2)}, u32[]{:S(2)}) collective-permute-start(f32[64,512]{1,0:T(8,128)S(1)} %slice_select_fusion.2), channel_id=1, source_target_pairs={{0,4},{2,6},{4,0},{6,2},{8,12},{10,14},{12,8},{14,10},{1,5},{3,7},... | collective-permute-start | bytes 393224 | tf_op jit(solution)/shard_map/ppermute | solution.py:58
  55.9 15.0 %collective-permute-start.11 = (f32[64,512]{1,0:T(8,128)S(1)}, f32[64,512]{1,0:T(8,128)S(1)}, u32[]{:S(2)}, u32[]{:S(2)}) collective-permute-start(f32[64,512]{1,0:T(8,128)S(1)} %slice_select_fusion.1), channel_id=1, source_target_pairs={{0,8},{2,10},{4,12},{6,14},{8,0},{10,2},{12,4},{14,6},{1,9},{3,11}... | collective-permute-start | bytes 393224 | tf_op jit(solution)/shard_map/ppermute | solution.py:58
  71.7 3.7 %collective-permute-start.12 = (f32[]{:T(128)}, f32[]{:T(128)}, u32[]{:S(2)}, u32[]{:S(2)}) collective-permute-start(f32[]{:T(128)} %multiply_reduce_fusion), channel_id=1, source_target_pairs={{0,1},{1,0},{2,3},{3,2},{4,5},{5,4},{6,7},{7,6},{8,9},{9,8},{10,11... | collective-permute-start | bytes 20 | tf_op jit(solution)/shard_map/ppermute | solution.py:33
  76.7 1.3 %collective-permute-start.13 = (f32[]{:T(128)}, f32[]{:T(128)}, u32[]{:S(2)}, u32[]{:S(2)}) collective-permute-start(f32[]{:T(128)} %add.78), channel_id=1, source_target_pairs={{0,16},{16,0},{1,17},{17,1},{2,18},{18,2},{3,19},{19,3},{4,20},{20... | collective-permute-start | bytes 20 | tf_op jit(solution)/shard_map/ppermute | solution.py:33
  78.7 3.7 %collective-permute-start.14 = (f32[]{:T(128)}, f32[]{:T(128)}, u32[]{:S(2)}, u32[]{:S(2)}) collective-permute-start(f32[]{:T(128)} %add.79), channel_id=1, source_target_pairs={{0,2},{2,0},{4,6},{6,4},{8,10},{10,8},{12,14},{14,12},{1,3},{3,1},... | collective-permute-start | bytes 20 | tf_op jit(solution)/shard_map/ppermute | solution.py:33
  83.0 3.7 %collective-permute-start.15 = (f32[]{:T(128)}, f32[]{:T(128)}, u32[]{:S(2)}, u32[]{:S(2)}) collective-permute-start(f32[]{:T(128)} %add.80), channel_id=1, source_target_pairs={{0,4},{2,6},{4,0},{6,2},{8,12},{10,14},{12,8},{14,10},{1,5},{3,7},... | collective-permute-start | bytes 20 | tf_op jit(solution)/shard_map/ppermute | solution.py:33
  87.4 4.6 %collective-permute-start.16 = (f32[]{:T(128)}, f32[]{:T(128)}, u32[]{:S(2)}, u32[]{:S(2)}) collective-permute-start(f32[]{:T(128)} %add.81), channel_id=1, source_target_pairs={{0,8},{2,10},{4,12},{6,14},{8,0},{10,2},{12,4},{14,6},{1,9},{3,11}... | collective-permute-start | bytes 20 | tf_op jit(solution)/shard_map/ppermute | solution.py:33
  93.1 7.6 %collective-permute-start.17 = (bf16[512,128]{0,1:T(8,128)(2,1)S(1)}, bf16[512,128]{0,1:T(8,128)(2,1)S(1)}, u32[]{:S(2)}, u32[]{:S(2)}) collective-permute-start(bf16[512,128]{0,1:T(8,128)(2,1)S(1)} %get-tuple-element.55), channel_id=1, source_target_pairs={{0,8},{2,10},{4,12},{6,14},{8,0},{10,2},{12,4},{14,6},{1,9},{3,11}... | collective-permute-start | bytes 393224 | tf_op jit(solution)/shard_map/ppermute | solution.py:72
  93.8 7.0 %collective-permute-start.20 = (bf16[512,128]{0,1:T(8,128)(2,1)S(1)}, bf16[512,128]{0,1:T(8,128)(2,1)S(1)}, u32[]{:S(2)}, u32[]{:S(2)}) collective-permute-start(bf16[512,128]{0,1:T(8,128)(2,1)S(1)} %get-tuple-element.56), channel_id=1, source_target_pairs={{0,2},{2,0},{4,6},{6,4},{8,10},{10,8},{12,14},{14,12},{1,3},{3,1},... | collective-permute-start | bytes 393224 | tf_op jit(solution)/shard_map/ppermute | solution.py:72
  100.8 11.0 %collective-permute-start.18 = (bf16[2,512,128]{1,2,0:T(8,128)(2,1)S(1)}, bf16[2,512,128]{1,2,0:T(8,128)(2,1)S(1)}, u32[]{:S(2)}, u32[]{:S(2)}) collective-permute-start(bf16[2,512,128]{1,2,0:T(8,128)(2,1)S(1)} %pad_maximum_fusion.16), channel_id=1, source_target_pairs={{0,4},{2,6},{4,0},{6,2},{8,12},{10,14},{12,8},{14,10},{1,5},{3,7},... | collective-permute-start | bytes 786440 | tf_op jit(solution)/shard_map/ppermute | solution.py:72
  101.0 11.7 %collective-permute-start.21 = (bf16[2,512,128]{1,2,0:T(8,128)(2,1)S(1)}, bf16[2,512,128]{1,2,0:T(8,128)(2,1)S(1)}, u32[]{:S(2)}, u32[]{:S(2)}) collective-permute-start(bf16[2,512,128]{1,2,0:T(8,128)(2,1)S(1)} %pad_maximum_fusion.17), channel_id=1, source_target_pairs={{0,8},{2,10},{4,12},{6,14},{8,0},{10,2},{12,4},{14,6},{1,9},{3,11}... | collective-permute-start | bytes 786440 | tf_op jit(solution)/shard_map/ppermute | solution.py:72
  112.0 9.2 %collective-permute-start.19 = (bf16[2,2,512,128]{2,3,1,0:T(8,128)(2,1)S(1)}, bf16[2,2,512,128]{2,3,1,0:T(8,128)(2,1)S(1)}, u32[]{:S(2)}, u32[]{:S(2)}) collective-permute-start(bf16[2,2,512,128]{2,3,1,0:T(8,128)(2,1)S(1)} %pad_maximum_fusion.8), channel_id=1, source_target_pairs={{0,2},{2,0},{4,6},{6,4},{8,10},{10,8},{12,14},{14,12},{1,3},{3,1},... | collective-permute-start | bytes 1572872 | tf_op jit(solution)/shard_map/ppermute | solution.py:72
  113.5 9.4 %collective-permute-start.22 = (bf16[2,2,512,128]{2,3,1,0:T(8,128)(2,1)}, bf16[2,2,512,128]{2,3,1,0:T(8,128)(2,1)S(1)}, u32[]{:S(2)}, u32[]{:S(2)}) collective-permute-start(bf16[2,2,512,128]{2,3,1,0:T(8,128)(2,1)} %pad_maximum_fusion.9), channel_id=1, source_target_pairs={{0,4},{2,6},{4,0},{6,2},{8,12},{10,14},{12,8},{14,10},{1,5},{3,7},... | collective-permute-start | bytes 1572872 | tf_op jit(solution)/shard_map/ppermute | solution.py:72
  (12 other events, 74.4 us)

commit v18 on v17

--- a/solution.py
+++ b/solution.py
@@ -120,7 +120,7 @@
     summed = scatter_rows(slot_term(inputs, key_grads, live_row, features), "dp")
     tokens_total = (live_count * (inputs.shape[1] * lax.axis_size("dp"))).astype(jnp.float32)
     grad_shard = summed / tokens_total
-    squares = butterfly_sum(jnp.sum(grad_shard * grad_shard), ("tensor", "pipe", "dp"))
+    squares = butterfly_sum(jnp.sum(grad_shard * grad_shard), ("tensor", "dp", "pipe"))
     clip_factor = jnp.minimum(1.0, CLIP_NORM / jnp.sqrt(squares))
     clipped = clip_factor * grad_shard
     moment1 = MOMENT_DECAY * first_moment[0].T + (1.0 - MOMENT_DECAY) * clipped

time: 126 us -> 133 us (1.056)
  waiting for transfers between devices: 59.1 us -> 65.8 us
    ppermute x6, waiting for transfers between devices: 22.7 us -> 29.5 us  [doubling_gather(): other = lax.ppermute(current, axis, pairs)]
  transfers between devices with their start and end apart: 23 -> 23, of which waited for: 17 -> 18; matrix products, arithmetic and copies ran while one was open for 13% -> 13% of each run, Pallas kernels for 0% -> 0%
where the time goes in v18:
time: 133 us
  waiting for transfers between devices  65.8 us (49%)
  starting transfers between devices  31.1 us (23%)
  other arithmetic  14.5 us (11%)
  local copies, waits for them, and re-layouts  9.86 us (7%)
  matrix products  6.18 us (5%)
  between operations  5.04 us (4%)
    ppermute x6, waiting for transfers between devices, doubling_gather(): other = lax.ppermute(current, axis, pairs)  29.5 us
    ppermute x12, waiting for transfers between devices, halving_scatter(): blocks = keep + lax.ppermute(send, axis, pairs)  26.9 us
    ppermute x12, starting transfers between devices, halving_scatter(): blocks = keep + lax.ppermute(send, axis, pairs)  18.1 us
    ppermute x5, waiting for transfers between devices, butterfly_sum(): value = value + lax.ppermute(value, axis, pairs)  9.52 us
    ppermute x5, starting transfers between devices, butterfly_sum(): value = value + lax.ppermute(value, axis, pairs)  7.53 us
    unnamed x45, local copies, waits for them, and re-layouts  6.55 us
    dot_general x1, matrix products, slot_term(): lax.dot_general(weighted, columns, (((0,), (0,)), ((), ())), preferred_el...  6.18 us
    ppermute x6, starting transfers between devices, doubling_gather(): other = lax.ppermute(current, axis, pairs)  5.56 us
  transfers between devices with their start and end apart: 23, of which 18 were waited for; matrix products, arithmetic and copies ran while one was open for 13% of the time, Pallas kernels for 0%

profile of v18, /device:TPU:0, one launch (start us, length us, event | category | flops | bytes accessed | tf_op | source)
XLA Modules:
  0.0 132.5 jit_solution(10438691959504578665)
XLA Ops:
  0.7 6.2 %fusion.2 = f32[256,4096]{1,0:T(8,128)S(1)} fusion(bf16[1,8,128,4096]{3,2,1,0:T(8,128)(2,1)} %param.6, bf16[1,8,128,256]{3,2,1,0:T(8,128)(2,1)} %param.7, pred[8]{0:T(512)(128)(4,1)S(1)} %compare_bitcast_fusion), kind=kOutput, calls=%fused_computation.2 | convolution fusion | flops 2147745792 | bytes 13107208 | tf_op jit(solution)/shard_map/dot_general | solution.py:19
  6.9 1.9 %copy-done = f32[256,4096]{1,0:T(8,128)} copy-done((f32[256,4096]{1,0:T(8,128)}, f32[256,4096]{1,0:T(8,128)S(1)}, u32[]{:S(2)}) %copy-start) | copy-done | bytes 4194328
  10.2 2.9 %collective-permute-start = (f32[64,2048]{1,0:T(8,128)}, f32[64,2048]{1,0:T(8,128)}, u32[]{:S(2)}, u32[]{:S(2)}) collective-permute-start(f32[64,2048]{1,0:T(8,128)} %fusion.19), channel_id=1, source_target_pairs={{0,2},{2,0},{4,6},{6,4},{8,10},{10,8},{12,14},{14,12},{1,3},{3,1},... | collective-permute-start | bytes 1572872 | tf_op jit(solution)/shard_map/ppermute | solution.py:58
  13.2 1.6 %fusion.27 = (f32[64,1024]{1,0:T(8,128)S(1)}, f32[64,1024]{1,0:T(8,128)S(1)}, f32[64,1024]{1,0:T(8,128)S(1)}, f32[64,1024]{1,0:T(8,128)S(1)}, f32[64,1024]{1,0:T...) fusion(f32[256,4096]{1,0:T(8,128)} %copy-done), kind=kLoop, calls=%fused_computation.80 | loop fusion | bytes 4194304 | tf_op jit(solution)/shard_map/slice | solution.py:54
  15.7 1.6 %collective-permute-start.3 = (f32[64,2048]{1,0:T(8,128)}, f32[64,2048]{1,0:T(8,128)}, u32[]{:S(2)}, u32[]{:S(2)}) collective-permute-start(f32[64,2048]{1,0:T(8,128)} %fusion.17), channel_id=1, source_target_pairs={{0,4},{2,6},{4,0},{6,2},{8,12},{10,14},{12,8},{14,10},{1,5},{3,7},... | collective-permute-start | bytes 1572872 | tf_op jit(solution)/shard_map/ppermute | solution.py:58
  21.0 1.2 copy.11
  22.2 1.2 copy.13
  23.5 2.0 %copy.14 = f32[1,512,256]{1,2,0:T(8,128)} copy(f32[1,512,256]{2,1,0:T(8,128)} %param.9) | data formatting | bytes 1048576 | tf_op args[3]
  26.2 1.4 %select_add_fusion.3 = f32[64,2048]{1,0:T(8,128)S(1)} fusion(f32[64,2048]{1,0:T(8,128)} %collective-permute-done, f32[64,512]{1,0:T(8,128)} %copy-done.13, f32[64,512]{1,0:T(8,128)} %copy-done.14, f32[64,512]{1,0:T(8,128)} %copy-done.15, f32[64,512]{1,0:T(8,128)} %copy-done.16, f32[64,512]{1,0:T(8,128)} %copy-done.17, f32[64,512]{1,0:T(8,128)} %copy-done.18, ...), kind=kLoop, calls=%fused_computation.35 | loop fusion | flops 1048576 | bytes 2097153 | tf_op jit(solution)/shard_map/add | solution.py:58
  27.7 2.2 %collective-permute-start.1 = (f32[64,1024]{1,0:T(8,128)S(1)}, f32[64,1024]{1,0:T(8,128)S(1)}, u32[]{:S(2)}, u32[]{:S(2)}) collective-permute-start(f32[64,1024]{1,0:T(8,128)S(1)} %fusion.24), channel_id=1, source_target_pairs={{0,4},{2,6},{4,0},{6,2},{8,12},{10,14},{12,8},{14,10},{1,5},{3,7},... | collective-permute-start | bytes 786440 | tf_op jit(solution)/shard_map/ppermute | solution.py:58
  32.7 4.7 %collective-permute-done.6 = f32[64,2048]{1,0:T(8,128)} collective-permute-done((f32[64,2048]{1,0:T(8,128)}, f32[64,2048]{1,0:T(8,128)}, u32[]{:S(2)}, u32[]{:S(2)}) %collective-permute-start.6) | collective-permute-done | bytes 524320 | tf_op jit(solution)/shard_map/ppermute | solution.py:58
  38.7 3.2 %collective-permute-start.7 = (f32[64,1024]{1,0:T(8,128)S(1)}, f32[64,1024]{1,0:T(8,128)S(1)}, u32[]{:S(2)}, u32[]{:S(2)}) collective-permute-start(f32[64,1024]{1,0:T(8,128)S(1)} %slice_select_fusion), channel_id=1, source_target_pairs={{0,8},{2,10},{4,12},{6,14},{8,0},{10,2},{12,4},{14,6},{1,9},{3,11}... | collective-permute-start | bytes 786440 | tf_op jit(solution)/shard_map/ppermute | solution.py:58
  41.9 5.8 %collective-permute-done.9 = f32[64,2048]{1,0:T(8,128)} collective-permute-done((f32[64,2048]{1,0:T(8,128)}, f32[64,2048]{1,0:T(8,128)}, u32[]{:S(2)}, u32[]{:S(2)}) %collective-permute-start.9) | collective-permute-done | bytes 524320 | tf_op jit(solution)/shard_map/ppermute | solution.py:58
  49.0 2.7 %collective-permute-done.1 = f32[64,1024]{1,0:T(8,128)S(1)} collective-permute-done((f32[64,1024]{1,0:T(8,128)S(1)}, f32[64,1024]{1,0:T(8,128)S(1)}, u32[]{:S(2)}, u32[]{:S(2)}) %collective-permute-start.1) | collective-permute-done | bytes 262176 | tf_op jit(solution)/shard_map/ppermute | solution.py:58
  53.1 1.9 %collective-permute-start.5 = (f32[64,512]{1,0:T(8,128)S(1)}, f32[64,512]{1,0:T(8,128)S(1)}, u32[]{:S(2)}, u32[]{:S(2)}) collective-permute-start(f32[64,512]{1,0:T(8,128)S(1)} %slice_select_fusion.3), channel_id=1, source_target_pairs={{0,8},{2,10},{4,12},{6,14},{8,0},{10,2},{12,4},{14,6},{1,9},{3,11}... | collective-permute-start | bytes 393224 | tf_op jit(solution)/shard_map/ppermute | solution.py:58
  55.9 3.0 %collective-permute-start.11 = (f32[64,512]{1,0:T(8,128)S(1)}, f32[64,512]{1,0:T(8,128)S(1)}, u32[]{:S(2)}, u32[]{:S(2)}) collective-permute-start(f32[64,512]{1,0:T(8,128)S(1)} %slice_select_fusion.1), channel_id=1, source_target_pairs={{0,8},{2,10},{4,12},{6,14},{8,0},{10,2},{12,4},{14,6},{1,9},{3,11}... | collective-permute-start | bytes 393224 | tf_op jit(solution)/shard_map/ppermute | solution.py:58
  58.9 6.0 %collective-permute-done.2 = f32[64,512]{1,0:T(8,128)S(1)} collective-permute-done((f32[64,512]{1,0:T(8,128)S(1)}, f32[64,512]{1,0:T(8,128)S(1)}, u32[]{:S(2)}, u32[]{:S(2)}) %collective-permute-start.2) | collective-permute-done | bytes 131104 | tf_op jit(solution)/shard_map/ppermute | solution.py:58
  64.9 4.2 %collective-permute-done.5 = f32[64,512]{1,0:T(8,128)S(1)} collective-permute-done((f32[64,512]{1,0:T(8,128)S(1)}, f32[64,512]{1,0:T(8,128)S(1)}, u32[]{:S(2)}, u32[]{:S(2)}) %collective-permute-start.5) | collective-permute-done | bytes 131104 | tf_op jit(solution)/shard_map/ppermute | solution.py:58
  69.2 1.7 %collective-permute-done.11 = f32[64,512]{1,0:T(8,128)S(1)} collective-permute-done((f32[64,512]{1,0:T(8,128)S(1)}, f32[64,512]{1,0:T(8,128)S(1)}, u32[]{:S(2)}, u32[]{:S(2)}) %collective-permute-start.11) | collective-permute-done | bytes 131104 | tf_op jit(solution)/shard_map/ppermute | solution.py:58
  71.7 1.5 %collective-permute-start.12 = (f32[]{:T(128)}, f32[]{:T(128)}, u32[]{:S(2)}, u32[]{:S(2)}) collective-permute-start(f32[]{:T(128)} %multiply_reduce_fusion), channel_id=1, source_target_pairs={{0,1},{1,0},{2,3},{3,2},{4,5},{5,4},{6,7},{7,6},{8,9},{9,8},{10,11... | collective-permute-start | bytes 20 | tf_op jit(solution)/shard_map/ppermute | solution.py:33
  73.3 2.2 %collective-permute-done.12 = f32[]{:T(128)} collective-permute-done((f32[]{:T(128)}, f32[]{:T(128)}, u32[]{:S(2)}, u32[]{:S(2)}) %collective-permute-start.12) | collective-permute-done | bytes 36 | tf_op jit(solution)/shard_map/ppermute | solution.py:33
  76.7 1.7 %collective-permute-start.13 = (f32[]{:T(128)}, f32[]{:T(128)}, u32[]{:S(2)}, u32[]{:S(2)}) collective-permute-start(f32[]{:T(128)} %add.78), channel_id=1, source_target_pairs={{0,2},{2,0},{4,6},{6,4},{8,10},{10,8},{12,14},{14,12},{1,3},{3,1},... | collective-permute-start | bytes 20 | tf_op jit(solution)/shard_map/ppermute | solution.py:33
  78.4 2.0 %collective-permute-done.13 = f32[]{:T(128)} collective-permute-done((f32[]{:T(128)}, f32[]{:T(128)}, u32[]{:S(2)}, u32[]{:S(2)}) %collective-permute-start.13) | collective-permute-done | bytes 36 | tf_op jit(solution)/shard_map/ppermute | solution.py:33
  81.1 1.4 %collective-permute-start.14 = (f32[]{:T(128)}, f32[]{:T(128)}, u32[]{:S(2)}, u32[]{:S(2)}) collective-permute-start(f32[]{:T(128)} %add.79), channel_id=1, source_target_pairs={{0,4},{2,6},{4,0},{6,2},{8,12},{10,14},{12,8},{14,10},{1,5},{3,7},... | collective-permute-start | bytes 20 | tf_op jit(solution)/shard_map/ppermute | solution.py:33
  82.4 2.3 %collective-permute-done.14 = f32[]{:T(128)} collective-permute-done((f32[]{:T(128)}, f32[]{:T(128)}, u32[]{:S(2)}, u32[]{:S(2)}) %collective-permute-start.14) | collective-permute-done | bytes 36 | tf_op jit(solution)/shard_map/ppermute | solution.py:33
  85.4 1.9 %collective-permute-start.15 = (f32[]{:T(128)}, f32[]{:T(128)}, u32[]{:S(2)}, u32[]{:S(2)}) collective-permute-start(f32[]{:T(128)} %add.80), channel_id=1, source_target_pairs={{0,8},{2,10},{4,12},{6,14},{8,0},{10,2},{12,4},{14,6},{1,9},{3,11}... | collective-permute-start | bytes 20 | tf_op jit(solution)/shard_map/ppermute | solution.py:33
  87.3 2.7 %collective-permute-done.15 = f32[]{:T(128)} collective-permute-done((f32[]{:T(128)}, f32[]{:T(128)}, u32[]{:S(2)}, u32[]{:S(2)}) %collective-permute-start.15) | collective-permute-done | bytes 36 | tf_op jit(solution)/shard_map/ppermute | solution.py:33
  94.9 7.1 %collective-permute-done.17 = bf16[512,128]{0,1:T(8,128)(2,1)S(1)} collective-permute-done((bf16[512,128]{0,1:T(8,128)(2,1)S(1)}, bf16[512,128]{0,1:T(8,128)(2,1)S(1)}, u32[]{:S(2)}, u32[]{:S(2)}) %collective-permute-start.17) | collective-permute-done | bytes 131104 | tf_op jit(solution)/shard_map/ppermute | solution.py:72
  102.2 2.6 %collective-permute-start.21 = (bf16[2,512,128]{1,2,0:T(8,128)(2,1)S(1)}, bf16[2,512,128]{1,2,0:T(8,128)(2,1)S(1)}, u32[]{:S(2)}, u32[]{:S(2)}) collective-permute-start(bf16[2,512,128]{1,2,0:T(8,128)(2,1)S(1)} %pad_maximum_fusion.17), channel_id=1, source_target_pairs={{0,8},{2,10},{4,12},{6,14},{8,0},{10,2},{12,4},{14,6},{1,9},{3,11}... | collective-permute-start | bytes 786440 | tf_op jit(solution)/shard_map/ppermute | solution.py:72
  104.8 10.5 %collective-permute-done.18 = bf16[2,512,128]{1,2,0:T(8,128)(2,1)S(1)} collective-permute-done((bf16[2,512,128]{1,2,0:T(8,128)(2,1)S(1)}, bf16[2,512,128]{1,2,0:T(8,128)(2,1)S(1)}, u32[]{:S(2)}, u32[]{:S(2)}) %collective-permute-start.18) | collective-permute-done | bytes 262176 | tf_op jit(solution)/shard_map/ppermute | solution.py:72
  117.9 10.6 %collective-permute-done.19 = bf16[2,2,512,128]{2,3,1,0:T(8,128)(2,1)S(1)} collective-permute-done((bf16[2,2,512,128]{2,3,1,0:T(8,128)(2,1)S(1)}, bf16[2,2,512,128]{2,3,1,0:T(8,128)(2,1)S(1)}, u32[]{:S(2)}, u32[]{:S(2)}) %collective-permute-start.19) | collective-permute-done | bytes 524320 | tf_op jit(solution)/shard_map/ppermute | solution.py:72
  131.0 1.5 %maximum_bitcast_fusion = bf16[1,4096,256]{2,1,0:T(8,128)(2,1)} fusion(bf16[4096,128]{1,0:T(8,128)(2,1)S(1)} %bitcast.75, bf16[4096,128]{1,0:T(8,128)(2,1)S(1)} %bitcast.74), kind=kLoop, calls=%fused_computation.3 | loop fusion | flops 4194304 | bytes 4194304 | tf_op jit(solution)/shard_map/broadcast_in_dim | solution.py:132
  (108 shorter events, 23.7 us)
Async XLA Ops:
  9.1 11.8 %copy-start.12 = (f32[64,512]{1,0:T(8,128)}, f32[64,512]{1,0:T(8,128)S(1)}, u32[]{:S(2)}) copy-start(f32[64,512]{1,0:T(8,128)S(1)} %get-tuple-element.5) | copy-start | bytes 393220
  9.1 11.8 %copy-start.13 = (f32[64,512]{1,0:T(8,128)}, f32[64,512]{1,0:T(8,128)S(1)}, u32[]{:S(2)}) copy-start(f32[64,512]{1,0:T(8,128)S(1)} %get-tuple-element.14) | copy-start | bytes 393220
  9.1 11.8 %copy-start.14 = (f32[64,512]{1,0:T(8,128)}, f32[64,512]{1,0:T(8,128)S(1)}, u32[]{:S(2)}) copy-start(f32[64,512]{1,0:T(8,128)S(1)} %get-tuple-element.15) | copy-start | bytes 393220
  10.2 16.0 %collective-permute-start = (f32[64,2048]{1,0:T(8,128)}, f32[64,2048]{1,0:T(8,128)}, u32[]{:S(2)}, u32[]{:S(2)}) collective-permute-start(f32[64,2048]{1,0:T(8,128)} %fusion.19), channel_id=1, source_target_pairs={{0,2},{2,0},{4,6},{6,4},{8,10},{10,8},{12,14},{14,12},{1,3},{3,1},... | collective-permute-start | bytes 1572872 | tf_op jit(solution)/shard_map/ppermute | solution.py:58
  15.7 15.2 %collective-permute-start.3 = (f32[64,2048]{1,0:T(8,128)}, f32[64,2048]{1,0:T(8,128)}, u32[]{:S(2)}, u32[]{:S(2)}) collective-permute-start(f32[64,2048]{1,0:T(8,128)} %fusion.17), channel_id=1, source_target_pairs={{0,4},{2,6},{4,0},{6,2},{8,12},{10,14},{12,8},{14,10},{1,5},{3,7},... | collective-permute-start | bytes 1572872 | tf_op jit(solution)/shard_map/ppermute | solution.py:58
  18.2 19.3 %collective-permute-start.6 = (f32[64,2048]{1,0:T(8,128)}, f32[64,2048]{1,0:T(8,128)}, u32[]{:S(2)}, u32[]{:S(2)}) collective-permute-start(f32[64,2048]{1,0:T(8,128)} %fusion.18), channel_id=1, source_target_pairs={{0,2},{2,0},{4,6},{6,4},{8,10},{10,8},{12,14},{14,12},{1,3},{3,1},... | collective-permute-start | bytes 1572872 | tf_op jit(solution)/shard_map/ppermute | solution.py:58
  19.6 28.1 %collective-permute-start.9 = (f32[64,2048]{1,0:T(8,128)}, f32[64,2048]{1,0:T(8,128)}, u32[]{:S(2)}, u32[]{:S(2)}) collective-permute-start(f32[64,2048]{1,0:T(8,128)} %fusion.16), channel_id=1, source_target_pairs={{0,4},{2,6},{4,0},{6,2},{8,12},{10,14},{12,8},{14,10},{1,5},{3,7},... | collective-permute-start | bytes 1572872 | tf_op jit(solution)/shard_map/ppermute | solution.py:58
  25.5 12.0 %copy-start.3 = (f32[64,512]{1,0:T(8,128)S(1)}, f32[64,512]{1,0:T(8,128)}, u32[]{:S(2)}) copy-start(f32[64,512]{1,0:T(8,128)} %copy-done.2) | copy-start | bytes 393220
  25.5 12.0 %copy-start.5 = (f32[64,512]{1,0:T(8,128)S(1)}, f32[64,512]{1,0:T(8,128)}, u32[]{:S(2)}) copy-start(f32[64,512]{1,0:T(8,128)} %copy-done.4) | copy-start | bytes 393220
  25.5 12.0 %copy-start.7 = (f32[64,512]{1,0:T(8,128)S(1)}, f32[64,512]{1,0:T(8,128)}, u32[]{:S(2)}) copy-start(f32[64,512]{1,0:T(8,128)} %copy-done.6) | copy-start | bytes 393220
  25.5 12.0 %copy-start.9 = (f32[64,512]{1,0:T(8,128)S(1)}, f32[64,512]{1,0:T(8,128)}, u32[]{:S(2)}) copy-start(f32[64,512]{1,0:T(8,128)} %copy-done.8) | copy-start | bytes 393220
  25.5 12.0 %copy-start.11 = (f32[64,512]{1,0:T(8,128)S(1)}, f32[64,512]{1,0:T(8,128)}, u32[]{:S(2)}) copy-start(f32[64,512]{1,0:T(8,128)} %copy-done.10) | copy-start | bytes 393220
  27.7 24.1 %collective-permute-start.1 = (f32[64,1024]{1,0:T(8,128)S(1)}, f32[64,1024]{1,0:T(8,128)S(1)}, u32[]{:S(2)}, u32[]{:S(2)}) collective-permute-start(f32[64,1024]{1,0:T(8,128)S(1)} %fusion.24), channel_id=1, source_target_pairs={{0,4},{2,6},{4,0},{6,2},{8,12},{10,14},{12,8},{14,10},{1,5},{3,7},... | collective-permute-start | bytes 786440 | tf_op jit(solution)/shard_map/ppermute | solution.py:58
  32.1 21.0 %collective-permute-start.4 = (f32[64,1024]{1,0:T(8,128)S(1)}, f32[64,1024]{1,0:T(8,128)S(1)}, u32[]{:S(2)}, u32[]{:S(2)}) collective-permute-start(f32[64,1024]{1,0:T(8,128)S(1)} %fusion.23), channel_id=1, source_target_pairs={{0,2},{2,0},{4,6},{6,4},{8,10},{10,8},{12,14},{14,12},{1,3},{3,1},... | collective-permute-start | bytes 786440 | tf_op jit(solution)/shard_map/ppermute | solution.py:58
  38.7 16.3 %collective-permute-start.7 = (f32[64,1024]{1,0:T(8,128)S(1)}, f32[64,1024]{1,0:T(8,128)S(1)}, u32[]{:S(2)}, u32[]{:S(2)}) collective-permute-start(f32[64,1024]{1,0:T(8,128)S(1)} %slice_select_fusion), channel_id=1, source_target_pairs={{0,8},{2,10},{4,12},{6,14},{8,0},{10,2},{12,4},{14,6},{1,9},{3,11}... | collective-permute-start | bytes 786440 | tf_op jit(solution)/shard_map/ppermute | solution.py:58
  48.9 43.7 %copy-start.1 = (f32[1,512,256]{1,2,0:T(8,128)S(1)}, f32[1,512,256]{1,2,0:T(8,128)}, u32[]{:S(2)}) copy-start(f32[1,512,256]{1,2,0:T(8,128)} %copy.14) | copy-start | bytes 1572868
  49.0 6.9 %collective-permute-start.10 = (f32[64,1024]{1,0:T(8,128)S(1)}, f32[64,1024]{1,0:T(8,128)S(1)}, u32[]{:S(2)}, u32[]{:S(2)}) collective-permute-start(f32[64,1024]{1,0:T(8,128)S(1)} %fusion.22), channel_id=1, source_target_pairs={{0,2},{2,0},{4,6},{6,4},{8,10},{10,8},{12,14},{14,12},{1,3},{3,1},... | collective-permute-start | bytes 786440 | tf_op jit(solution)/shard_map/ppermute | solution.py:58
  51.8 13.0 %collective-permute-start.2 = (f32[64,512]{1,0:T(8,128)S(1)}, f32[64,512]{1,0:T(8,128)S(1)}, u32[]{:S(2)}, u32[]{:S(2)}) collective-permute-start(f32[64,512]{1,0:T(8,128)S(1)} %slice_select_fusion.4), channel_id=1, source_target_pairs={{0,8},{2,10},{4,12},{6,14},{8,0},{10,2},{12,4},{14,6},{1,9},{3,11}... | collective-permute-start | bytes 393224 | tf_op jit(solution)/shard_map/ppermute | solution.py:58
  53.1 16.0 %collective-permute-start.5 = (f32[64,512]{1,0:T(8,128)S(1)}, f32[64,512]{1,0:T(8,128)S(1)}, u32[]{:S(2)}, u32[]{:S(2)}) collective-permute-start(f32[64,512]{1,0:T(8,128)S(1)} %slice_select_fusion.3), channel_id=1, source_target_pairs={{0,8},{2,10},{4,12},{6,14},{8,0},{10,2},{12,4},{14,6},{1,9},{3,11}... | collective-permute-start | bytes 393224 | tf_op jit(solution)/shard_map/ppermute | solution.py:58
  55.1 14.1 %collective-permute-start.8 = (f32[64,512]{1,0:T(8,128)S(1)}, f32[64,512]{1,0:T(8,128)S(1)}, u32[]{:S(2)}, u32[]{:S(2)}) collective-permute-start(f32[64,512]{1,0:T(8,128)S(1)} %slice_select_fusion.2), channel_id=1, source_target_pairs={{0,4},{2,6},{4,0},{6,2},{8,12},{10,14},{12,8},{14,10},{1,5},{3,7},... | collective-permute-start | bytes 393224 | tf_op jit(solution)/shard_map/ppermute | solution.py:58
  55.9 15.0 %collective-permute-start.11 = (f32[64,512]{1,0:T(8,128)S(1)}, f32[64,512]{1,0:T(8,128)S(1)}, u32[]{:S(2)}, u32[]{:S(2)}) collective-permute-start(f32[64,512]{1,0:T(8,128)S(1)} %slice_select_fusion.1), channel_id=1, source_target_pairs={{0,8},{2,10},{4,12},{6,14},{8,0},{10,2},{12,4},{14,6},{1,9},{3,11}... | collective-permute-start | bytes 393224 | tf_op jit(solution)/shard_map/ppermute | solution.py:58
  71.7 3.7 %collective-permute-start.12 = (f32[]{:T(128)}, f32[]{:T(128)}, u32[]{:S(2)}, u32[]{:S(2)}) collective-permute-start(f32[]{:T(128)} %multiply_reduce_fusion), channel_id=1, source_target_pairs={{0,1},{1,0},{2,3},{3,2},{4,5},{5,4},{6,7},{7,6},{8,9},{9,8},{10,11... | collective-permute-start | bytes 20 | tf_op jit(solution)/shard_map/ppermute | solution.py:33
  76.7 3.7 %collective-permute-start.13 = (f32[]{:T(128)}, f32[]{:T(128)}, u32[]{:S(2)}, u32[]{:S(2)}) collective-permute-start(f32[]{:T(128)} %add.78), channel_id=1, source_target_pairs={{0,2},{2,0},{4,6},{6,4},{8,10},{10,8},{12,14},{14,12},{1,3},{3,1},... | collective-permute-start | bytes 20 | tf_op jit(solution)/shard_map/ppermute | solution.py:33
  81.1 3.7 %collective-permute-start.14 = (f32[]{:T(128)}, f32[]{:T(128)}, u32[]{:S(2)}, u32[]{:S(2)}) collective-permute-start(f32[]{:T(128)} %add.79), channel_id=1, source_target_pairs={{0,4},{2,6},{4,0},{6,2},{8,12},{10,14},{12,8},{14,10},{1,5},{3,7},... | collective-permute-start | bytes 20 | tf_op jit(solution)/shard_map/ppermute | solution.py:33
  85.4 4.6 %collective-permute-start.15 = (f32[]{:T(128)}, f32[]{:T(128)}, u32[]{:S(2)}, u32[]{:S(2)}) collective-permute-start(f32[]{:T(128)} %add.80), channel_id=1, source_target_pairs={{0,8},{2,10},{4,12},{6,14},{8,0},{10,2},{12,4},{14,6},{1,9},{3,11}... | collective-permute-start | bytes 20 | tf_op jit(solution)/shard_map/ppermute | solution.py:33
  90.7 1.3 collective-permute-start.16
  93.1 8.8 %collective-permute-start.17 = (bf16[512,128]{0,1:T(8,128)(2,1)S(1)}, bf16[512,128]{0,1:T(8,128)(2,1)S(1)}, u32[]{:S(2)}, u32[]{:S(2)}) collective-permute-start(bf16[512,128]{0,1:T(8,128)(2,1)S(1)} %get-tuple-element.55), channel_id=1, source_target_pairs={{0,8},{2,10},{4,12},{6,14},{8,0},{10,2},{12,4},{14,6},{1,9},{3,11}... | collective-permute-start | bytes 393224 | tf_op jit(solution)/shard_map/ppermute | solution.py:72
  93.8 8.2 %collective-permute-start.20 = (bf16[512,128]{0,1:T(8,128)(2,1)S(1)}, bf16[512,128]{0,1:T(8,128)(2,1)S(1)}, u32[]{:S(2)}, u32[]{:S(2)}) collective-permute-start(bf16[512,128]{0,1:T(8,128)(2,1)S(1)} %get-tuple-element.56), channel_id=1, source_target_pairs={{0,2},{2,0},{4,6},{6,4},{8,10},{10,8},{12,14},{14,12},{1,3},{3,1},... | collective-permute-start | bytes 393224 | tf_op jit(solution)/shard_map/ppermute | solution.py:72
  102.0 13.3 %collective-permute-start.18 = (bf16[2,512,128]{1,2,0:T(8,128)(2,1)S(1)}, bf16[2,512,128]{1,2,0:T(8,128)(2,1)S(1)}, u32[]{:S(2)}, u32[]{:S(2)}) collective-permute-start(bf16[2,512,128]{1,2,0:T(8,128)(2,1)S(1)} %pad_maximum_fusion.16), channel_id=1, source_target_pairs={{0,4},{2,6},{4,0},{6,2},{8,12},{10,14},{12,8},{14,10},{1,5},{3,7},... | collective-permute-start | bytes 786440 | tf_op jit(solution)/shard_map/ppermute | solution.py:72
  102.2 14.9 %collective-permute-start.21 = (bf16[2,512,128]{1,2,0:T(8,128)(2,1)S(1)}, bf16[2,512,128]{1,2,0:T(8,128)(2,1)S(1)}, u32[]{:S(2)}, u32[]{:S(2)}) collective-permute-start(bf16[2,512,128]{1,2,0:T(8,128)(2,1)S(1)} %pad_maximum_fusion.17), channel_id=1, source_target_pairs={{0,8},{2,10},{4,12},{6,14},{8,0},{10,2},{12,4},{14,6},{1,9},{3,11}... | collective-permute-start | bytes 786440 | tf_op jit(solution)/shard_map/ppermute | solution.py:72
  115.4 13.1 %collective-permute-start.19 = (bf16[2,2,512,128]{2,3,1,0:T(8,128)(2,1)S(1)}, bf16[2,2,512,128]{2,3,1,0:T(8,128)(2,1)S(1)}, u32[]{:S(2)}, u32[]{:S(2)}) collective-permute-start(bf16[2,2,512,128]{2,3,1,0:T(8,128)(2,1)S(1)} %pad_maximum_fusion.8), channel_id=1, source_target_pairs={{0,2},{2,0},{4,6},{6,4},{8,10},{10,8},{12,14},{14,12},{1,3},{3,1},... | collective-permute-start | bytes 1572872 | tf_op jit(solution)/shard_map/ppermute | solution.py:72
  117.9 12.2 %collective-permute-start.22 = (bf16[2,2,512,128]{2,3,1,0:T(8,128)(2,1)}, bf16[2,2,512,128]{2,3,1,0:T(8,128)(2,1)S(1)}, u32[]{:S(2)}, u32[]{:S(2)}) collective-permute-start(bf16[2,2,512,128]{2,3,1,0:T(8,128)(2,1)} %pad_maximum_fusion.9), channel_id=1, source_target_pairs={{0,4},{2,6},{4,0},{6,2},{8,12},{10,14},{12,8},{14,10},{1,5},{3,7},... | collective-permute-start | bytes 1572872 | tf_op jit(solution)/shard_map/ppermute | solution.py:72
  (12 other events, 74.4 us)

commit v19 on v17

--- a/solution.py
+++ b/solution.py
@@ -27,11 +27,11 @@
         if size & (size - 1):
             value = lax.psum(value, axis)
             continue
-        bit = 1
-        while bit < size:
+        bit = size // 2
+        while bit >= 1:
             pairs = [(i, i ^ bit) for i in range(size)]
             value = value + lax.ppermute(value, axis, pairs)
-            bit *= 2
+            bit //= 2
     return value
 
 

time: 126 us -> 126 us (level)
  no operation moved by 1% of the time
where the time goes in v19:
time: 126 us; the launch traced here: 125 us
  waiting for transfers between devices  59.6 us (47%)
  starting transfers between devices  30.2 us (24%)
  other arithmetic  14.5 us (12%)
  local copies, waits for them, and re-layouts  9.86 us (8%)
  matrix products  6.18 us (5%)
  between operations  5.04 us (4%)
    ppermute x12, waiting for transfers between devices, halving_scatter(): blocks = keep + lax.ppermute(send, axis, pairs)  26.9 us
    ppermute x6, waiting for transfers between devices, doubling_gather(): other = lax.ppermute(current, axis, pairs)  22.7 us
    ppermute x12, starting transfers between devices, halving_scatter(): blocks = keep + lax.ppermute(send, axis, pairs)  18.1 us
    ppermute x5, waiting for transfers between devices, butterfly_sum(): value = value + lax.ppermute(value, axis, pairs)  10.1 us
    ppermute x5, starting transfers between devices, butterfly_sum(): value = value + lax.ppermute(value, axis, pairs)  6.96 us
    unnamed x45, local copies, waits for them, and re-layouts  6.55 us
    dot_general x1, matrix products, slot_term(): lax.dot_general(weighted, columns, (((0,), (0,)), ((), ())), preferred_el...  6.18 us
    ppermute x6, starting transfers between devices, doubling_gather(): other = lax.ppermute(current, axis, pairs)  5.14 us
  transfers between devices with their start and end apart: 23, of which 17 were waited for; matrix products, arithmetic and copies ran while one was open for 13% of the time, Pallas kernels for 0%

profile of v19, /device:TPU:0, one launch (start us, length us, event | category | flops | bytes accessed | tf_op | source)
XLA Modules:
  0.0 125.3 jit_solution(8462278182139626437)
XLA Ops:
  0.7 6.2 %fusion.2 = f32[256,4096]{1,0:T(8,128)S(1)} fusion(bf16[1,8,128,4096]{3,2,1,0:T(8,128)(2,1)} %param.6, bf16[1,8,128,256]{3,2,1,0:T(8,128)(2,1)} %param.7, pred[8]{0:T(512)(128)(4,1)S(1)} %compare_bitcast_fusion), kind=kOutput, calls=%fused_computation.2 | convolution fusion | flops 2147745792 | bytes 13107208 | tf_op jit(solution)/shard_map/dot_general | solution.py:19
  6.9 1.9 %copy-done = f32[256,4096]{1,0:T(8,128)} copy-done((f32[256,4096]{1,0:T(8,128)}, f32[256,4096]{1,0:T(8,128)S(1)}, u32[]{:S(2)}) %copy-start) | copy-done | bytes 4194328
  10.2 2.9 %collective-permute-start = (f32[64,2048]{1,0:T(8,128)}, f32[64,2048]{1,0:T(8,128)}, u32[]{:S(2)}, u32[]{:S(2)}) collective-permute-start(f32[64,2048]{1,0:T(8,128)} %fusion.19), channel_id=1, source_target_pairs={{0,2},{2,0},{4,6},{6,4},{8,10},{10,8},{12,14},{14,12},{1,3},{3,1},... | collective-permute-start | bytes 1572872 | tf_op jit(solution)/shard_map/ppermute | solution.py:58
  13.2 1.6 %fusion.27 = (f32[64,1024]{1,0:T(8,128)S(1)}, f32[64,1024]{1,0:T(8,128)S(1)}, f32[64,1024]{1,0:T(8,128)S(1)}, f32[64,1024]{1,0:T(8,128)S(1)}, f32[64,1024]{1,0:T...) fusion(f32[256,4096]{1,0:T(8,128)} %copy-done), kind=kLoop, calls=%fused_computation.80 | loop fusion | bytes 4194304 | tf_op jit(solution)/shard_map/slice | solution.py:54
  15.7 1.6 %collective-permute-start.3 = (f32[64,2048]{1,0:T(8,128)}, f32[64,2048]{1,0:T(8,128)}, u32[]{:S(2)}, u32[]{:S(2)}) collective-permute-start(f32[64,2048]{1,0:T(8,128)} %fusion.17), channel_id=1, source_target_pairs={{0,4},{2,6},{4,0},{6,2},{8,12},{10,14},{12,8},{14,10},{1,5},{3,7},... | collective-permute-start | bytes 1572872 | tf_op jit(solution)/shard_map/ppermute | solution.py:58
  21.0 1.2 copy.11
  22.2 1.2 copy.13
  23.5 2.0 %copy.14 = f32[1,512,256]{1,2,0:T(8,128)} copy(f32[1,512,256]{2,1,0:T(8,128)} %param.9) | data formatting | bytes 1048576 | tf_op args[3]
  26.2 1.4 %select_add_fusion.3 = f32[64,2048]{1,0:T(8,128)S(1)} fusion(f32[64,2048]{1,0:T(8,128)} %collective-permute-done, f32[64,512]{1,0:T(8,128)} %copy-done.13, f32[64,512]{1,0:T(8,128)} %copy-done.14, f32[64,512]{1,0:T(8,128)} %copy-done.15, f32[64,512]{1,0:T(8,128)} %copy-done.16, f32[64,512]{1,0:T(8,128)} %copy-done.17, f32[64,512]{1,0:T(8,128)} %copy-done.18, ...), kind=kLoop, calls=%fused_computation.35 | loop fusion | flops 1048576 | bytes 2097153 | tf_op jit(solution)/shard_map/add | solution.py:58
  27.7 2.2 %collective-permute-start.1 = (f32[64,1024]{1,0:T(8,128)S(1)}, f32[64,1024]{1,0:T(8,128)S(1)}, u32[]{:S(2)}, u32[]{:S(2)}) collective-permute-start(f32[64,1024]{1,0:T(8,128)S(1)} %fusion.24), channel_id=1, source_target_pairs={{0,4},{2,6},{4,0},{6,2},{8,12},{10,14},{12,8},{14,10},{1,5},{3,7},... | collective-permute-start | bytes 786440 | tf_op jit(solution)/shard_map/ppermute | solution.py:58
  32.7 4.7 %collective-permute-done.6 = f32[64,2048]{1,0:T(8,128)} collective-permute-done((f32[64,2048]{1,0:T(8,128)}, f32[64,2048]{1,0:T(8,128)}, u32[]{:S(2)}, u32[]{:S(2)}) %collective-permute-start.6) | collective-permute-done | bytes 524320 | tf_op jit(solution)/shard_map/ppermute | solution.py:58
  38.7 3.2 %collective-permute-start.7 = (f32[64,1024]{1,0:T(8,128)S(1)}, f32[64,1024]{1,0:T(8,128)S(1)}, u32[]{:S(2)}, u32[]{:S(2)}) collective-permute-start(f32[64,1024]{1,0:T(8,128)S(1)} %slice_select_fusion), channel_id=1, source_target_pairs={{0,8},{2,10},{4,12},{6,14},{8,0},{10,2},{12,4},{14,6},{1,9},{3,11}... | collective-permute-start | bytes 786440 | tf_op jit(solution)/shard_map/ppermute | solution.py:58
  41.9 5.8 %collective-permute-done.9 = f32[64,2048]{1,0:T(8,128)} collective-permute-done((f32[64,2048]{1,0:T(8,128)}, f32[64,2048]{1,0:T(8,128)}, u32[]{:S(2)}, u32[]{:S(2)}) %collective-permute-start.9) | collective-permute-done | bytes 524320 | tf_op jit(solution)/shard_map/ppermute | solution.py:58
  49.0 2.7 %collective-permute-done.1 = f32[64,1024]{1,0:T(8,128)S(1)} collective-permute-done((f32[64,1024]{1,0:T(8,128)S(1)}, f32[64,1024]{1,0:T(8,128)S(1)}, u32[]{:S(2)}, u32[]{:S(2)}) %collective-permute-start.1) | collective-permute-done | bytes 262176 | tf_op jit(solution)/shard_map/ppermute | solution.py:58
  53.1 1.9 %collective-permute-start.5 = (f32[64,512]{1,0:T(8,128)S(1)}, f32[64,512]{1,0:T(8,128)S(1)}, u32[]{:S(2)}, u32[]{:S(2)}) collective-permute-start(f32[64,512]{1,0:T(8,128)S(1)} %slice_select_fusion.3), channel_id=1, source_target_pairs={{0,8},{2,10},{4,12},{6,14},{8,0},{10,2},{12,4},{14,6},{1,9},{3,11}... | collective-permute-start | bytes 393224 | tf_op jit(solution)/shard_map/ppermute | solution.py:58
  55.9 3.0 %collective-permute-start.11 = (f32[64,512]{1,0:T(8,128)S(1)}, f32[64,512]{1,0:T(8,128)S(1)}, u32[]{:S(2)}, u32[]{:S(2)}) collective-permute-start(f32[64,512]{1,0:T(8,128)S(1)} %slice_select_fusion.1), channel_id=1, source_target_pairs={{0,8},{2,10},{4,12},{6,14},{8,0},{10,2},{12,4},{14,6},{1,9},{3,11}... | collective-permute-start | bytes 393224 | tf_op jit(solution)/shard_map/ppermute | solution.py:58
  58.9 6.0 %collective-permute-done.2 = f32[64,512]{1,0:T(8,128)S(1)} collective-permute-done((f32[64,512]{1,0:T(8,128)S(1)}, f32[64,512]{1,0:T(8,128)S(1)}, u32[]{:S(2)}, u32[]{:S(2)}) %collective-permute-start.2) | collective-permute-done | bytes 131104 | tf_op jit(solution)/shard_map/ppermute | solution.py:58
  64.9 4.2 %collective-permute-done.5 = f32[64,512]{1,0:T(8,128)S(1)} collective-permute-done((f32[64,512]{1,0:T(8,128)S(1)}, f32[64,512]{1,0:T(8,128)S(1)}, u32[]{:S(2)}, u32[]{:S(2)}) %collective-permute-start.5) | collective-permute-done | bytes 131104 | tf_op jit(solution)/shard_map/ppermute | solution.py:58
  69.2 1.7 %collective-permute-done.11 = f32[64,512]{1,0:T(8,128)S(1)} collective-permute-done((f32[64,512]{1,0:T(8,128)S(1)}, f32[64,512]{1,0:T(8,128)S(1)}, u32[]{:S(2)}, u32[]{:S(2)}) %collective-permute-start.11) | collective-permute-done | bytes 131104 | tf_op jit(solution)/shard_map/ppermute | solution.py:58
  71.7 1.5 %collective-permute-start.12 = (f32[]{:T(128)}, f32[]{:T(128)}, u32[]{:S(2)}, u32[]{:S(2)}) collective-permute-start(f32[]{:T(128)} %multiply_reduce_fusion), channel_id=1, source_target_pairs={{0,1},{1,0},{2,3},{3,2},{4,5},{5,4},{6,7},{7,6},{8,9},{9,8},{10,11... | collective-permute-start | bytes 20 | tf_op jit(solution)/shard_map/ppermute | solution.py:33
  73.3 2.2 %collective-permute-done.12 = f32[]{:T(128)} collective-permute-done((f32[]{:T(128)}, f32[]{:T(128)}, u32[]{:S(2)}, u32[]{:S(2)}) %collective-permute-start.12) | collective-permute-done | bytes 36 | tf_op jit(solution)/shard_map/ppermute | solution.py:33
  78.7 1.4 %collective-permute-start.14 = (f32[]{:T(128)}, f32[]{:T(128)}, u32[]{:S(2)}, u32[]{:S(2)}) collective-permute-start(f32[]{:T(128)} %add.79), channel_id=1, source_target_pairs={{0,8},{2,10},{4,12},{6,14},{8,0},{10,2},{12,4},{14,6},{1,9},{3,11}... | collective-permute-start | bytes 20 | tf_op jit(solution)/shard_map/ppermute | solution.py:33
  80.0 3.2 %collective-permute-done.14 = f32[]{:T(128)} collective-permute-done((f32[]{:T(128)}, f32[]{:T(128)}, u32[]{:S(2)}, u32[]{:S(2)}) %collective-permute-start.14) | collective-permute-done | bytes 36 | tf_op jit(solution)/shard_map/ppermute | solution.py:33
  83.9 1.4 %collective-permute-start.15 = (f32[]{:T(128)}, f32[]{:T(128)}, u32[]{:S(2)}, u32[]{:S(2)}) collective-permute-start(f32[]{:T(128)} %add.80), channel_id=1, source_target_pairs={{0,4},{2,6},{4,0},{6,2},{8,12},{10,14},{12,8},{14,10},{1,5},{3,7},... | collective-permute-start | bytes 20 | tf_op jit(solution)/shard_map/ppermute | solution.py:33
  85.3 2.3 %collective-permute-done.15 = f32[]{:T(128)} collective-permute-done((f32[]{:T(128)}, f32[]{:T(128)}, u32[]{:S(2)}, u32[]{:S(2)}) %collective-permute-start.15) | collective-permute-done | bytes 36 | tf_op jit(solution)/shard_map/ppermute | solution.py:33
  88.3 1.7 %collective-permute-start.16 = (f32[]{:T(128)}, f32[]{:T(128)}, u32[]{:S(2)}, u32[]{:S(2)}) collective-permute-start(f32[]{:T(128)} %add.81), channel_id=1, source_target_pairs={{0,2},{2,0},{4,6},{6,4},{8,10},{10,8},{12,14},{14,12},{1,3},{3,1},... | collective-permute-start | bytes 20 | tf_op jit(solution)/shard_map/ppermute | solution.py:33
  90.0 2.0 %collective-permute-done.16 = f32[]{:T(128)} collective-permute-done((f32[]{:T(128)}, f32[]{:T(128)}, u32[]{:S(2)}, u32[]{:S(2)}) %collective-permute-start.16) | collective-permute-done | bytes 36 | tf_op jit(solution)/shard_map/ppermute | solution.py:33
  94.9 5.9 %collective-permute-done.17 = bf16[512,128]{0,1:T(8,128)(2,1)S(1)} collective-permute-done((bf16[512,128]{0,1:T(8,128)(2,1)S(1)}, bf16[512,128]{0,1:T(8,128)(2,1)S(1)}, u32[]{:S(2)}, u32[]{:S(2)}) %collective-permute-start.17) | collective-permute-done | bytes 131104 | tf_op jit(solution)/shard_map/ppermute | solution.py:72
  101.0 2.6 %collective-permute-start.21 = (bf16[2,512,128]{1,2,0:T(8,128)(2,1)S(1)}, bf16[2,512,128]{1,2,0:T(8,128)(2,1)S(1)}, u32[]{:S(2)}, u32[]{:S(2)}) collective-permute-start(bf16[2,512,128]{1,2,0:T(8,128)(2,1)S(1)} %pad_maximum_fusion.17), channel_id=1, source_target_pairs={{0,8},{2,10},{4,12},{6,14},{8,0},{10,2},{12,4},{14,6},{1,9},{3,11}... | collective-permute-start | bytes 786440 | tf_op jit(solution)/shard_map/ppermute | solution.py:72
  103.6 8.3 %collective-permute-done.18 = bf16[2,512,128]{1,2,0:T(8,128)(2,1)S(1)} collective-permute-done((bf16[2,512,128]{1,2,0:T(8,128)(2,1)S(1)}, bf16[2,512,128]{1,2,0:T(8,128)(2,1)S(1)}, u32[]{:S(2)}, u32[]{:S(2)}) %collective-permute-start.18) | collective-permute-done | bytes 262176 | tf_op jit(solution)/shard_map/ppermute | solution.py:72
  113.5 7.7 %collective-permute-done.19 = bf16[2,2,512,128]{2,3,1,0:T(8,128)(2,1)S(1)} collective-permute-done((bf16[2,2,512,128]{2,3,1,0:T(8,128)(2,1)S(1)}, bf16[2,2,512,128]{2,3,1,0:T(8,128)(2,1)S(1)}, u32[]{:S(2)}, u32[]{:S(2)}) %collective-permute-start.19) | collective-permute-done | bytes 524320 | tf_op jit(solution)/shard_map/ppermute | solution.py:72
  123.8 1.5 %maximum_bitcast_fusion = bf16[1,4096,256]{2,1,0:T(8,128)(2,1)} fusion(bf16[4096,128]{1,0:T(8,128)(2,1)S(1)} %bitcast.75, bf16[4096,128]{1,0:T(8,128)(2,1)S(1)} %bitcast.74), kind=kLoop, calls=%fused_computation.3 | loop fusion | flops 4194304 | bytes 4194304 | tf_op jit(solution)/shard_map/broadcast_in_dim | solution.py:132
  (108 shorter events, 22.8 us)
Async XLA Ops:
  9.1 11.8 %copy-start.12 = (f32[64,512]{1,0:T(8,128)}, f32[64,512]{1,0:T(8,128)S(1)}, u32[]{:S(2)}) copy-start(f32[64,512]{1,0:T(8,128)S(1)} %get-tuple-element.5) | copy-start | bytes 393220
  9.1 11.8 %copy-start.13 = (f32[64,512]{1,0:T(8,128)}, f32[64,512]{1,0:T(8,128)S(1)}, u32[]{:S(2)}) copy-start(f32[64,512]{1,0:T(8,128)S(1)} %get-tuple-element.14) | copy-start | bytes 393220
  9.1 11.8 %copy-start.14 = (f32[64,512]{1,0:T(8,128)}, f32[64,512]{1,0:T(8,128)S(1)}, u32[]{:S(2)}) copy-start(f32[64,512]{1,0:T(8,128)S(1)} %get-tuple-element.15) | copy-start | bytes 393220
  10.2 16.0 %collective-permute-start = (f32[64,2048]{1,0:T(8,128)}, f32[64,2048]{1,0:T(8,128)}, u32[]{:S(2)}, u32[]{:S(2)}) collective-permute-start(f32[64,2048]{1,0:T(8,128)} %fusion.19), channel_id=1, source_target_pairs={{0,2},{2,0},{4,6},{6,4},{8,10},{10,8},{12,14},{14,12},{1,3},{3,1},... | collective-permute-start | bytes 1572872 | tf_op jit(solution)/shard_map/ppermute | solution.py:58
  15.7 15.2 %collective-permute-start.3 = (f32[64,2048]{1,0:T(8,128)}, f32[64,2048]{1,0:T(8,128)}, u32[]{:S(2)}, u32[]{:S(2)}) collective-permute-start(f32[64,2048]{1,0:T(8,128)} %fusion.17), channel_id=1, source_target_pairs={{0,4},{2,6},{4,0},{6,2},{8,12},{10,14},{12,8},{14,10},{1,5},{3,7},... | collective-permute-start | bytes 1572872 | tf_op jit(solution)/shard_map/ppermute | solution.py:58
  18.2 19.3 %collective-permute-start.6 = (f32[64,2048]{1,0:T(8,128)}, f32[64,2048]{1,0:T(8,128)}, u32[]{:S(2)}, u32[]{:S(2)}) collective-permute-start(f32[64,2048]{1,0:T(8,128)} %fusion.18), channel_id=1, source_target_pairs={{0,2},{2,0},{4,6},{6,4},{8,10},{10,8},{12,14},{14,12},{1,3},{3,1},... | collective-permute-start | bytes 1572872 | tf_op jit(solution)/shard_map/ppermute | solution.py:58
  19.6 28.1 %collective-permute-start.9 = (f32[64,2048]{1,0:T(8,128)}, f32[64,2048]{1,0:T(8,128)}, u32[]{:S(2)}, u32[]{:S(2)}) collective-permute-start(f32[64,2048]{1,0:T(8,128)} %fusion.16), channel_id=1, source_target_pairs={{0,4},{2,6},{4,0},{6,2},{8,12},{10,14},{12,8},{14,10},{1,5},{3,7},... | collective-permute-start | bytes 1572872 | tf_op jit(solution)/shard_map/ppermute | solution.py:58
  25.5 12.0 %copy-start.3 = (f32[64,512]{1,0:T(8,128)S(1)}, f32[64,512]{1,0:T(8,128)}, u32[]{:S(2)}) copy-start(f32[64,512]{1,0:T(8,128)} %copy-done.2) | copy-start | bytes 393220
  25.5 12.0 %copy-start.5 = (f32[64,512]{1,0:T(8,128)S(1)}, f32[64,512]{1,0:T(8,128)}, u32[]{:S(2)}) copy-start(f32[64,512]{1,0:T(8,128)} %copy-done.4) | copy-start | bytes 393220
  25.5 12.0 %copy-start.7 = (f32[64,512]{1,0:T(8,128)S(1)}, f32[64,512]{1,0:T(8,128)}, u32[]{:S(2)}) copy-start(f32[64,512]{1,0:T(8,128)} %copy-done.6) | copy-start | bytes 393220
  25.5 12.0 %copy-start.9 = (f32[64,512]{1,0:T(8,128)S(1)}, f32[64,512]{1,0:T(8,128)}, u32[]{:S(2)}) copy-start(f32[64,512]{1,0:T(8,128)} %copy-done.8) | copy-start | bytes 393220
  25.5 12.0 %copy-start.11 = (f32[64,512]{1,0:T(8,128)S(1)}, f32[64,512]{1,0:T(8,128)}, u32[]{:S(2)}) copy-start(f32[64,512]{1,0:T(8,128)} %copy-done.10) | copy-start | bytes 393220
  27.7 24.1 %collective-permute-start.1 = (f32[64,1024]{1,0:T(8,128)S(1)}, f32[64,1024]{1,0:T(8,128)S(1)}, u32[]{:S(2)}, u32[]{:S(2)}) collective-permute-start(f32[64,1024]{1,0:T(8,128)S(1)} %fusion.24), channel_id=1, source_target_pairs={{0,4},{2,6},{4,0},{6,2},{8,12},{10,14},{12,8},{14,10},{1,5},{3,7},... | collective-permute-start | bytes 786440 | tf_op jit(solution)/shard_map/ppermute | solution.py:58
  32.1 21.0 %collective-permute-start.4 = (f32[64,1024]{1,0:T(8,128)S(1)}, f32[64,1024]{1,0:T(8,128)S(1)}, u32[]{:S(2)}, u32[]{:S(2)}) collective-permute-start(f32[64,1024]{1,0:T(8,128)S(1)} %fusion.23), channel_id=1, source_target_pairs={{0,2},{2,0},{4,6},{6,4},{8,10},{10,8},{12,14},{14,12},{1,3},{3,1},... | collective-permute-start | bytes 786440 | tf_op jit(solution)/shard_map/ppermute | solution.py:58
  38.7 16.3 %collective-permute-start.7 = (f32[64,1024]{1,0:T(8,128)S(1)}, f32[64,1024]{1,0:T(8,128)S(1)}, u32[]{:S(2)}, u32[]{:S(2)}) collective-permute-start(f32[64,1024]{1,0:T(8,128)S(1)} %slice_select_fusion), channel_id=1, source_target_pairs={{0,8},{2,10},{4,12},{6,14},{8,0},{10,2},{12,4},{14,6},{1,9},{3,11}... | collective-permute-start | bytes 786440 | tf_op jit(solution)/shard_map/ppermute | solution.py:58
  48.9 43.7 %copy-start.1 = (f32[1,512,256]{1,2,0:T(8,128)S(1)}, f32[1,512,256]{1,2,0:T(8,128)}, u32[]{:S(2)}) copy-start(f32[1,512,256]{1,2,0:T(8,128)} %copy.14) | copy-start | bytes 1572868
  49.0 6.9 %collective-permute-start.10 = (f32[64,1024]{1,0:T(8,128)S(1)}, f32[64,1024]{1,0:T(8,128)S(1)}, u32[]{:S(2)}, u32[]{:S(2)}) collective-permute-start(f32[64,1024]{1,0:T(8,128)S(1)} %fusion.22), channel_id=1, source_target_pairs={{0,2},{2,0},{4,6},{6,4},{8,10},{10,8},{12,14},{14,12},{1,3},{3,1},... | collective-permute-start | bytes 786440 | tf_op jit(solution)/shard_map/ppermute | solution.py:58
  51.8 13.0 %collective-permute-start.2 = (f32[64,512]{1,0:T(8,128)S(1)}, f32[64,512]{1,0:T(8,128)S(1)}, u32[]{:S(2)}, u32[]{:S(2)}) collective-permute-start(f32[64,512]{1,0:T(8,128)S(1)} %slice_select_fusion.4), channel_id=1, source_target_pairs={{0,8},{2,10},{4,12},{6,14},{8,0},{10,2},{12,4},{14,6},{1,9},{3,11}... | collective-permute-start | bytes 393224 | tf_op jit(solution)/shard_map/ppermute | solution.py:58
  53.1 16.0 %collective-permute-start.5 = (f32[64,512]{1,0:T(8,128)S(1)}, f32[64,512]{1,0:T(8,128)S(1)}, u32[]{:S(2)}, u32[]{:S(2)}) collective-permute-start(f32[64,512]{1,0:T(8,128)S(1)} %slice_select_fusion.3), channel_id=1, source_target_pairs={{0,8},{2,10},{4,12},{6,14},{8,0},{10,2},{12,4},{14,6},{1,9},{3,11}... | collective-permute-start | bytes 393224 | tf_op jit(solution)/shard_map/ppermute | solution.py:58
  55.1 14.1 %collective-permute-start.8 = (f32[64,512]{1,0:T(8,128)S(1)}, f32[64,512]{1,0:T(8,128)S(1)}, u32[]{:S(2)}, u32[]{:S(2)}) collective-permute-start(f32[64,512]{1,0:T(8,128)S(1)} %slice_select_fusion.2), channel_id=1, source_target_pairs={{0,4},{2,6},{4,0},{6,2},{8,12},{10,14},{12,8},{14,10},{1,5},{3,7},... | collective-permute-start | bytes 393224 | tf_op jit(solution)/shard_map/ppermute | solution.py:58
  55.9 15.0 %collective-permute-start.11 = (f32[64,512]{1,0:T(8,128)S(1)}, f32[64,512]{1,0:T(8,128)S(1)}, u32[]{:S(2)}, u32[]{:S(2)}) collective-permute-start(f32[64,512]{1,0:T(8,128)S(1)} %slice_select_fusion.1), channel_id=1, source_target_pairs={{0,8},{2,10},{4,12},{6,14},{8,0},{10,2},{12,4},{14,6},{1,9},{3,11}... | collective-permute-start | bytes 393224 | tf_op jit(solution)/shard_map/ppermute | solution.py:58
  71.7 3.7 %collective-permute-start.12 = (f32[]{:T(128)}, f32[]{:T(128)}, u32[]{:S(2)}, u32[]{:S(2)}) collective-permute-start(f32[]{:T(128)} %multiply_reduce_fusion), channel_id=1, source_target_pairs={{0,1},{1,0},{2,3},{3,2},{4,5},{5,4},{6,7},{7,6},{8,9},{9,8},{10,11... | collective-permute-start | bytes 20 | tf_op jit(solution)/shard_map/ppermute | solution.py:33
  76.7 1.3 %collective-permute-start.13 = (f32[]{:T(128)}, f32[]{:T(128)}, u32[]{:S(2)}, u32[]{:S(2)}) collective-permute-start(f32[]{:T(128)} %add.78), channel_id=1, source_target_pairs={{0,16},{16,0},{1,17},{17,1},{2,18},{18,2},{3,19},{19,3},{4,20},{20... | collective-permute-start | bytes 20 | tf_op jit(solution)/shard_map/ppermute | solution.py:33
  78.7 4.6 %collective-permute-start.14 = (f32[]{:T(128)}, f32[]{:T(128)}, u32[]{:S(2)}, u32[]{:S(2)}) collective-permute-start(f32[]{:T(128)} %add.79), channel_id=1, source_target_pairs={{0,8},{2,10},{4,12},{6,14},{8,0},{10,2},{12,4},{14,6},{1,9},{3,11}... | collective-permute-start | bytes 20 | tf_op jit(solution)/shard_map/ppermute | solution.py:33
  83.9 3.7 %collective-permute-start.15 = (f32[]{:T(128)}, f32[]{:T(128)}, u32[]{:S(2)}, u32[]{:S(2)}) collective-permute-start(f32[]{:T(128)} %add.80), channel_id=1, source_target_pairs={{0,4},{2,6},{4,0},{6,2},{8,12},{10,14},{12,8},{14,10},{1,5},{3,7},... | collective-permute-start | bytes 20 | tf_op jit(solution)/shard_map/ppermute | solution.py:33
  88.3 3.7 %collective-permute-start.16 = (f32[]{:T(128)}, f32[]{:T(128)}, u32[]{:S(2)}, u32[]{:S(2)}) collective-permute-start(f32[]{:T(128)} %add.81), channel_id=1, source_target_pairs={{0,2},{2,0},{4,6},{6,4},{8,10},{10,8},{12,14},{14,12},{1,3},{3,1},... | collective-permute-start | bytes 20 | tf_op jit(solution)/shard_map/ppermute | solution.py:33
  93.1 7.6 %collective-permute-start.17 = (bf16[512,128]{0,1:T(8,128)(2,1)S(1)}, bf16[512,128]{0,1:T(8,128)(2,1)S(1)}, u32[]{:S(2)}, u32[]{:S(2)}) collective-permute-start(bf16[512,128]{0,1:T(8,128)(2,1)S(1)} %get-tuple-element.55), channel_id=1, source_target_pairs={{0,8},{2,10},{4,12},{6,14},{8,0},{10,2},{12,4},{14,6},{1,9},{3,11}... | collective-permute-start | bytes 393224 | tf_op jit(solution)/shard_map/ppermute | solution.py:72
  93.8 7.0 %collective-permute-start.20 = (bf16[512,128]{0,1:T(8,128)(2,1)S(1)}, bf16[512,128]{0,1:T(8,128)(2,1)S(1)}, u32[]{:S(2)}, u32[]{:S(2)}) collective-permute-start(bf16[512,128]{0,1:T(8,128)(2,1)S(1)} %get-tuple-element.56), channel_id=1, source_target_pairs={{0,2},{2,0},{4,6},{6,4},{8,10},{10,8},{12,14},{14,12},{1,3},{3,1},... | collective-permute-start | bytes 393224 | tf_op jit(solution)/shard_map/ppermute | solution.py:72
  100.8 11.0 %collective-permute-start.18 = (bf16[2,512,128]{1,2,0:T(8,128)(2,1)S(1)}, bf16[2,512,128]{1,2,0:T(8,128)(2,1)S(1)}, u32[]{:S(2)}, u32[]{:S(2)}) collective-permute-start(bf16[2,512,128]{1,2,0:T(8,128)(2,1)S(1)} %pad_maximum_fusion.16), channel_id=1, source_target_pairs={{0,4},{2,6},{4,0},{6,2},{8,12},{10,14},{12,8},{14,10},{1,5},{3,7},... | collective-permute-start | bytes 786440 | tf_op jit(solution)/shard_map/ppermute | solution.py:72
  101.0 11.7 %collective-permute-start.21 = (bf16[2,512,128]{1,2,0:T(8,128)(2,1)S(1)}, bf16[2,512,128]{1,2,0:T(8,128)(2,1)S(1)}, u32[]{:S(2)}, u32[]{:S(2)}) collective-permute-start(bf16[2,512,128]{1,2,0:T(8,128)(2,1)S(1)} %pad_maximum_fusion.17), channel_id=1, source_target_pairs={{0,8},{2,10},{4,12},{6,14},{8,0},{10,2},{12,4},{14,6},{1,9},{3,11}... | collective-permute-start | bytes 786440 | tf_op jit(solution)/shard_map/ppermute | solution.py:72
  112.0 9.2 %collective-permute-start.19 = (bf16[2,2,512,128]{2,3,1,0:T(8,128)(2,1)S(1)}, bf16[2,2,512,128]{2,3,1,0:T(8,128)(2,1)S(1)}, u32[]{:S(2)}, u32[]{:S(2)}) collective-permute-start(bf16[2,2,512,128]{2,3,1,0:T(8,128)(2,1)S(1)} %pad_maximum_fusion.8), channel_id=1, source_target_pairs={{0,2},{2,0},{4,6},{6,4},{8,10},{10,8},{12,14},{14,12},{1,3},{3,1},... | collective-permute-start | bytes 1572872 | tf_op jit(solution)/shard_map/ppermute | solution.py:72
  113.5 9.4 %collective-permute-start.22 = (bf16[2,2,512,128]{2,3,1,0:T(8,128)(2,1)}, bf16[2,2,512,128]{2,3,1,0:T(8,128)(2,1)S(1)}, u32[]{:S(2)}, u32[]{:S(2)}) collective-permute-start(bf16[2,2,512,128]{2,3,1,0:T(8,128)(2,1)} %pad_maximum_fusion.9), channel_id=1, source_target_pairs={{0,4},{2,6},{4,0},{6,2},{8,12},{10,14},{12,8},{14,10},{1,5},{3,7},... | collective-permute-start | bytes 1572872 | tf_op jit(solution)/shard_map/ppermute | solution.py:72
  (12 other events, 74.4 us)

commit v20 on v19

--- a/solution.py
+++ b/solution.py
@@ -88,7 +88,7 @@
     width = cols // parts
     return jnp.concatenate(
         [
-            halving_scatter(partial_t[k * width:(k + 1) * width], axis, orders[(0, 1, 2, 1)[k % 4]])
+            halving_scatter(partial_t[k * width:(k + 1) * width], axis, orders[(1, 0, 1, 2)[k % 4]])
             for k in range(parts)
         ],
         axis=0,

time: 126 us -> 130 us (1.032)
  starting transfers between devices: 30.2 us -> 33.4 us
  local copies, waits for them, and re-layouts: 9.86 us -> 7.16 us
  waiting for transfers between devices: 59.6 us -> 62.2 us
    ppermute x12, waiting for transfers between devices: 26.9 us -> 31.2 us  [halving_scatter(): blocks = keep + lax.ppermute(send, axis, pairs)]
    ppermute x5, waiting for transfers between devices: 10.1 us -> 8.01 us  [butterfly_sum(): value = value + lax.ppermute(value, axis, pairs)]
    ppermute x6, starting transfers between devices: 5.14 us -> 7.16 us  [doubling_gather(): other = lax.ppermute(current, axis, pairs)]
    unnamed x45 -> x33, local copies, waits for them, and re-layouts: 6.55 us -> 4.58 us
    ppermute x5, starting transfers between devices: 6.96 us -> 8.43 us  [butterfly_sum(): value = value + lax.ppermute(value, axis, pairs)]
  transfers between devices with their start and end apart: 23 -> 23, of which waited for: 17 -> 19; matrix products, arithmetic and copies ran while one was open for 13% -> 13% of each run, Pallas kernels for 0% -> 0%
where the time goes in v20:
time: 130 us
  waiting for transfers between devices  62.2 us (48%)
  starting transfers between devices  33.4 us (26%)
  other arithmetic  15.7 us (12%)
  local copies, waits for them, and re-layouts  7.16 us (6%)
  matrix products  6.18 us (5%)
  between operations  4.92 us (4%)
    ppermute x12, waiting for transfers between devices, halving_scatter(): blocks = keep + lax.ppermute(send, axis, pairs)  31.2 us
    ppermute x6, waiting for transfers between devices, doubling_gather(): other = lax.ppermute(current, axis, pairs)  23 us
    ppermute x12, starting transfers between devices, halving_scatter(): blocks = keep + lax.ppermute(send, axis, pairs)  17.9 us
    ppermute x5, starting transfers between devices, butterfly_sum(): value = value + lax.ppermute(value, axis, pairs)  8.43 us
    ppermute x5, waiting for transfers between devices, butterfly_sum(): value = value + lax.ppermute(value, axis, pairs)  8.01 us
    ppermute x6, starting transfers between devices, doubling_gather(): other = lax.ppermute(current, axis, pairs)  7.16 us
    dot_general x1, matrix products, slot_term(): lax.dot_general(weighted, columns, (((0,), (0,)), ((), ())), preferred_el...  6.18 us
    select_n x12, other arithmetic, halving_scatter(): send = jnp.where(mine == 1, low_part, high_part)  5.14 us
  transfers between devices with their start and end apart: 23, of which 19 were waited for; matrix products, arithmetic and copies ran while one was open for 13% of the time, Pallas kernels for 0%

profile of v20, /device:TPU:0, one launch (start us, length us, event | category | flops | bytes accessed | tf_op | source)
XLA Modules:
  0.0 129.6 jit_solution(12138449129414691299)
XLA Ops:
  0.7 6.2 %fusion.2 = f32[256,4096]{1,0:T(8,128)S(1)} fusion(bf16[1,8,128,4096]{3,2,1,0:T(8,128)(2,1)} %param.6, bf16[1,8,128,256]{3,2,1,0:T(8,128)(2,1)} %param.7, pred[8]{0:T(512)(128)(4,1)S(1)} %compare_bitcast_fusion), kind=kOutput, calls=%fused_computation.2 | convolution fusion | flops 2147745792 | bytes 13107208 | tf_op jit(solution)/shard_map/dot_general | solution.py:19
  7.9 3.0 %collective-permute-start = (f32[64,2048]{1,0:T(8,128)}, f32[64,2048]{1,0:T(8,128)}, u32[]{:S(2)}, u32[]{:S(2)}) collective-permute-start(f32[64,2048]{1,0:T(8,128)} %fusion.17), channel_id=1, source_target_pairs={{0,4},{2,6},{4,0},{6,2},{8,12},{10,14},{12,8},{14,10},{1,5},{3,7},... | collective-permute-start | bytes 1572872 | tf_op jit(solution)/shard_map/ppermute | solution.py:58
  11.9 2.3 %fusion.19 = f32[64,2048]{1,0:T(8,128)} fusion(f32[64,512]{1,0:T(8,128)S(1)} %get-tuple-element.22, f32[64,512]{1,0:T(8,128)S(1)} %get-tuple-element.23, f32[64,512]{1,0:T(8,128)} %get-tuple-element.24, f32[64,512]{1,0:T(8,128)} %get-tuple-element.25, f32[64,512]{1,0:T(8,128)} %get-tuple-element.26, f32[64,512]{1,0:T(8,128)} %get-tuple-element.27, ...), kind=kLoop, calls=%fused_computation.42 | loop fusion | flops 917504 | bytes 1572865 | tf_op jit(solution)/shard_map/jit(_where)/select_n | solution.py:56
  14.3 1.5 %collective-permute-start.3 = (f32[64,2048]{1,0:T(8,128)}, f32[64,2048]{1,0:T(8,128)}, u32[]{:S(2)}, u32[]{:S(2)}) collective-permute-start(f32[64,2048]{1,0:T(8,128)} %fusion.19), channel_id=1, source_target_pairs={{0,2},{2,0},{4,6},{6,4},{8,10},{10,8},{12,14},{14,12},{1,3},{3,1},... | collective-permute-start | bytes 1572872 | tf_op jit(solution)/shard_map/ppermute | solution.py:58
  21.9 2.0 %copy.14 = f32[1,512,256]{1,2,0:T(8,128)} copy(f32[1,512,256]{2,1,0:T(8,128)} %param.9) | data formatting | bytes 1048576 | tf_op args[3]
  25.2 2.0 %collective-permute-start.1 = (f32[64,1024]{1,0:T(8,128)S(1)}, f32[64,1024]{1,0:T(8,128)S(1)}, u32[]{:S(2)}, u32[]{:S(2)}) collective-permute-start(f32[64,1024]{1,0:T(8,128)S(1)} %fusion.24), channel_id=1, source_target_pairs={{0,2},{2,0},{4,6},{6,4},{8,10},{10,8},{12,14},{14,12},{1,3},{3,1},... | collective-permute-start | bytes 786440 | tf_op jit(solution)/shard_map/ppermute | solution.py:58
  27.3 2.2 %collective-permute-done.3 = f32[64,2048]{1,0:T(8,128)} collective-permute-done((f32[64,2048]{1,0:T(8,128)}, f32[64,2048]{1,0:T(8,128)}, u32[]{:S(2)}, u32[]{:S(2)}) %collective-permute-start.3) | collective-permute-done | bytes 524320 | tf_op jit(solution)/shard_map/ppermute | solution.py:58
  31.0 4.2 %collective-permute-done.6 = f32[64,2048]{1,0:T(8,128)} collective-permute-done((f32[64,2048]{1,0:T(8,128)}, f32[64,2048]{1,0:T(8,128)}, u32[]{:S(2)}, u32[]{:S(2)}) %collective-permute-start.6) | collective-permute-done | bytes 524320 | tf_op jit(solution)/shard_map/ppermute | solution.py:58
  36.4 2.0 %collective-permute-start.7 = (f32[64,1024]{1,0:T(8,128)S(1)}, f32[64,1024]{1,0:T(8,128)S(1)}, u32[]{:S(2)}, u32[]{:S(2)}) collective-permute-start(f32[64,1024]{1,0:T(8,128)S(1)} %fusion.22), channel_id=1, source_target_pairs={{0,2},{2,0},{4,6},{6,4},{8,10},{10,8},{12,14},{14,12},{1,3},{3,1},... | collective-permute-start | bytes 786440 | tf_op jit(solution)/shard_map/ppermute | solution.py:58
  38.5 2.2 %collective-permute-done.9 = f32[64,2048]{1,0:T(8,128)} collective-permute-done((f32[64,2048]{1,0:T(8,128)}, f32[64,2048]{1,0:T(8,128)}, u32[]{:S(2)}, u32[]{:S(2)}) %collective-permute-start.9) | collective-permute-done | bytes 524320 | tf_op jit(solution)/shard_map/ppermute | solution.py:58
  41.9 2.7 %collective-permute-start.10 = (f32[64,1024]{1,0:T(8,128)S(1)}, f32[64,1024]{1,0:T(8,128)S(1)}, u32[]{:S(2)}, u32[]{:S(2)}) collective-permute-start(f32[64,1024]{1,0:T(8,128)S(1)} %slice_select_fusion), channel_id=1, source_target_pairs={{0,8},{2,10},{4,12},{6,14},{8,0},{10,2},{12,4},{14,6},{1,9},{3,11}... | collective-permute-start | bytes 786440 | tf_op jit(solution)/shard_map/ppermute | solution.py:58
  44.6 1.6 %collective-permute-done.1 = f32[64,1024]{1,0:T(8,128)S(1)} collective-permute-done((f32[64,1024]{1,0:T(8,128)S(1)}, f32[64,1024]{1,0:T(8,128)S(1)}, u32[]{:S(2)}, u32[]{:S(2)}) %collective-permute-start.1) | collective-permute-done | bytes 262176 | tf_op jit(solution)/shard_map/ppermute | solution.py:58
  46.3 2.7 %collective-permute-start.2 = (f32[64,512]{1,0:T(8,128)S(1)}, f32[64,512]{1,0:T(8,128)S(1)}, u32[]{:S(2)}, u32[]{:S(2)}) collective-permute-start(f32[64,512]{1,0:T(8,128)S(1)} %slice_select_fusion.4), channel_id=1, source_target_pairs={{0,8},{2,10},{4,12},{6,14},{8,0},{10,2},{12,4},{14,6},{1,9},{3,11}... | collective-permute-start | bytes 393224 | tf_op jit(solution)/shard_map/ppermute | solution.py:58
  50.4 2.7 %collective-permute-start.8 = (f32[64,512]{1,0:T(8,128)S(1)}, f32[64,512]{1,0:T(8,128)S(1)}, u32[]{:S(2)}, u32[]{:S(2)}) collective-permute-start(f32[64,512]{1,0:T(8,128)S(1)} %slice_select_fusion.2), channel_id=1, source_target_pairs={{0,8},{2,10},{4,12},{6,14},{8,0},{10,2},{12,4},{14,6},{1,9},{3,11}... | collective-permute-start | bytes 393224 | tf_op jit(solution)/shard_map/ppermute | solution.py:58
  53.1 9.8 %collective-permute-done.10 = f32[64,1024]{1,0:T(8,128)S(1)} collective-permute-done((f32[64,1024]{1,0:T(8,128)S(1)}, f32[64,1024]{1,0:T(8,128)S(1)}, u32[]{:S(2)}, u32[]{:S(2)}) %collective-permute-start.10) | collective-permute-done | bytes 262176 | tf_op jit(solution)/shard_map/ppermute | solution.py:58
  63.3 2.5 %collective-permute-done.2 = f32[64,512]{1,0:T(8,128)S(1)} collective-permute-done((f32[64,512]{1,0:T(8,128)S(1)}, f32[64,512]{1,0:T(8,128)S(1)}, u32[]{:S(2)}, u32[]{:S(2)}) %collective-permute-start.2) | collective-permute-done | bytes 131104 | tf_op jit(solution)/shard_map/ppermute | solution.py:58
  65.8 2.8 %collective-permute-done.5 = f32[64,512]{1,0:T(8,128)S(1)} collective-permute-done((f32[64,512]{1,0:T(8,128)S(1)}, f32[64,512]{1,0:T(8,128)S(1)}, u32[]{:S(2)}, u32[]{:S(2)}) %collective-permute-start.5) | collective-permute-done | bytes 131104 | tf_op jit(solution)/shard_map/ppermute | solution.py:58
  68.6 2.2 %collective-permute-done.8 = f32[64,512]{1,0:T(8,128)S(1)} collective-permute-done((f32[64,512]{1,0:T(8,128)S(1)}, f32[64,512]{1,0:T(8,128)S(1)}, u32[]{:S(2)}, u32[]{:S(2)}) %collective-permute-start.8) | collective-permute-done | bytes 131104 | tf_op jit(solution)/shard_map/ppermute | solution.py:58
  70.9 2.7 %collective-permute-done.11 = f32[64,512]{1,0:T(8,128)S(1)} collective-permute-done((f32[64,512]{1,0:T(8,128)S(1)}, f32[64,512]{1,0:T(8,128)S(1)}, u32[]{:S(2)}, u32[]{:S(2)}) %collective-permute-start.11) | collective-permute-done | bytes 131104 | tf_op jit(solution)/shard_map/ppermute | solution.py:58
  75.7 2.3 %collective-permute-done.12 = f32[]{:T(128)} collective-permute-done((f32[]{:T(128)}, f32[]{:T(128)}, u32[]{:S(2)}, u32[]{:S(2)}) %collective-permute-start.12) | collective-permute-done | bytes 36 | tf_op jit(solution)/shard_map/ppermute | solution.py:33
  81.1 1.9 %collective-permute-start.14 = (f32[]{:T(128)}, f32[]{:T(128)}, u32[]{:S(2)}, u32[]{:S(2)}) collective-permute-start(f32[]{:T(128)} %add.79), channel_id=1, source_target_pairs={{0,8},{2,10},{4,12},{6,14},{8,0},{10,2},{12,4},{14,6},{1,9},{3,11}... | collective-permute-start | bytes 20 | tf_op jit(solution)/shard_map/ppermute | solution.py:33
  83.0 2.5 %collective-permute-done.14 = f32[]{:T(128)} collective-permute-done((f32[]{:T(128)}, f32[]{:T(128)}, u32[]{:S(2)}, u32[]{:S(2)}) %collective-permute-start.14) | collective-permute-done | bytes 36 | tf_op jit(solution)/shard_map/ppermute | solution.py:33
  86.2 1.5 %collective-permute-start.15 = (f32[]{:T(128)}, f32[]{:T(128)}, u32[]{:S(2)}, u32[]{:S(2)}) collective-permute-start(f32[]{:T(128)} %add.80), channel_id=1, source_target_pairs={{0,4},{2,6},{4,0},{6,2},{8,12},{10,14},{12,8},{14,10},{1,5},{3,7},... | collective-permute-start | bytes 20 | tf_op jit(solution)/shard_map/ppermute | solution.py:33
  87.6 2.1 %collective-permute-done.15 = f32[]{:T(128)} collective-permute-done((f32[]{:T(128)}, f32[]{:T(128)}, u32[]{:S(2)}, u32[]{:S(2)}) %collective-permute-start.15) | collective-permute-done | bytes 36 | tf_op jit(solution)/shard_map/ppermute | solution.py:33
  90.4 2.7 %collective-permute-start.16 = (f32[]{:T(128)}, f32[]{:T(128)}, u32[]{:S(2)}, u32[]{:S(2)}) collective-permute-start(f32[]{:T(128)} %add.81), channel_id=1, source_target_pairs={{0,2},{2,0},{4,6},{6,4},{8,10},{10,8},{12,14},{14,12},{1,3},{3,1},... | collective-permute-start | bytes 20 | tf_op jit(solution)/shard_map/ppermute | solution.py:33
  96.1 1.5 %collective-permute-start.20 = (bf16[512,128]{0,1:T(8,128)(2,1)S(1)}, bf16[512,128]{0,1:T(8,128)(2,1)S(1)}, u32[]{:S(2)}, u32[]{:S(2)}) collective-permute-start(bf16[512,128]{0,1:T(8,128)(2,1)S(1)} %get-tuple-element.56), channel_id=1, source_target_pairs={{0,2},{2,0},{4,6},{6,4},{8,10},{10,8},{12,14},{14,12},{1,3},{3,1},... | collective-permute-start | bytes 393224 | tf_op jit(solution)/shard_map/ppermute | solution.py:72
  97.6 4.4 %collective-permute-done.17 = bf16[512,128]{0,1:T(8,128)(2,1)S(1)} collective-permute-done((bf16[512,128]{0,1:T(8,128)(2,1)S(1)}, bf16[512,128]{0,1:T(8,128)(2,1)S(1)}, u32[]{:S(2)}, u32[]{:S(2)}) %collective-permute-start.17) | collective-permute-done | bytes 131104 | tf_op jit(solution)/shard_map/ppermute | solution.py:72
  103.3 1.9 %collective-permute-start.21 = (bf16[2,512,128]{1,2,0:T(8,128)(2,1)S(1)}, bf16[2,512,128]{1,2,0:T(8,128)(2,1)S(1)}, u32[]{:S(2)}, u32[]{:S(2)}) collective-permute-start(bf16[2,512,128]{1,2,0:T(8,128)(2,1)S(1)} %pad_maximum_fusion.17), channel_id=1, source_target_pairs={{0,8},{2,10},{4,12},{6,14},{8,0},{10,2},{12,4},{14,6},{1,9},{3,11}... | collective-permute-start | bytes 786440 | tf_op jit(solution)/shard_map/ppermute | solution.py:72
  105.2 7.2 %collective-permute-done.18 = bf16[2,512,128]{1,2,0:T(8,128)(2,1)S(1)} collective-permute-done((bf16[2,512,128]{1,2,0:T(8,128)(2,1)S(1)}, bf16[2,512,128]{1,2,0:T(8,128)(2,1)S(1)}, u32[]{:S(2)}, u32[]{:S(2)}) %collective-permute-start.18) | collective-permute-done | bytes 262176 | tf_op jit(solution)/shard_map/ppermute | solution.py:72
  112.5 1.5 %collective-permute-start.19 = (bf16[2,2,512,128]{2,3,1,0:T(8,128)(2,1)S(1)}, bf16[2,2,512,128]{2,3,1,0:T(8,128)(2,1)S(1)}, u32[]{:S(2)}, u32[]{:S(2)}) collective-permute-start(bf16[2,2,512,128]{2,3,1,0:T(8,128)(2,1)S(1)} %pad_maximum_fusion.8), channel_id=1, source_target_pairs={{0,2},{2,0},{4,6},{6,4},{8,10},{10,8},{12,14},{14,12},{1,3},{3,1},... | collective-permute-start | bytes 1572872 | tf_op jit(solution)/shard_map/ppermute | solution.py:72
  115.0 9.9 %collective-permute-done.19 = bf16[2,2,512,128]{2,3,1,0:T(8,128)(2,1)S(1)} collective-permute-done((bf16[2,2,512,128]{2,3,1,0:T(8,128)(2,1)S(1)}, bf16[2,2,512,128]{2,3,1,0:T(8,128)(2,1)S(1)}, u32[]{:S(2)}, u32[]{:S(2)}) %collective-permute-start.19) | collective-permute-done | bytes 524320 | tf_op jit(solution)/shard_map/ppermute | solution.py:72
  128.0 1.5 %maximum_bitcast_fusion = bf16[1,4096,256]{2,1,0:T(8,128)(2,1)} fusion(bf16[4096,128]{1,0:T(8,128)(2,1)S(1)} %bitcast.75, bf16[4096,128]{1,0:T(8,128)(2,1)S(1)} %bitcast.74), kind=kLoop, calls=%fused_computation.3 | loop fusion | flops 4194304 | bytes 4194304 | tf_op jit(solution)/shard_map/broadcast_in_dim | solution.py:132
  (96 shorter events, 26.2 us)
Async XLA Ops:
  7.9 10.2 %copy-start.14 = (s32[1,8]{1,0:T(1,128)S(1)}, s32[1,8]{1,0:T(1,128)}, u32[]{:S(2)}) copy-start(s32[1,8]{1,0:T(1,128)} %param.8) | copy-start | bytes 100
  7.9 16.1 %collective-permute-start = (f32[64,2048]{1,0:T(8,128)}, f32[64,2048]{1,0:T(8,128)}, u32[]{:S(2)}, u32[]{:S(2)}) collective-permute-start(f32[64,2048]{1,0:T(8,128)} %fusion.17), channel_id=1, source_target_pairs={{0,4},{2,6},{4,0},{6,2},{8,12},{10,14},{12,8},{14,10},{1,5},{3,7},... | collective-permute-start | bytes 1572872 | tf_op jit(solution)/shard_map/ppermute | solution.py:58
  11.9 7.5 %copy-start.9 = (f32[64,512]{1,0:T(8,128)}, f32[64,512]{1,0:T(8,128)S(1)}, u32[]{:S(2)}) copy-start(f32[64,512]{1,0:T(8,128)S(1)} %get-tuple-element.21) | copy-start | bytes 393220
  11.9 7.5 %copy-start.11 = (f32[64,512]{1,0:T(8,128)}, f32[64,512]{1,0:T(8,128)S(1)}, u32[]{:S(2)}) copy-start(f32[64,512]{1,0:T(8,128)S(1)} %get-tuple-element.13) | copy-start | bytes 393220
  14.3 15.2 %collective-permute-start.3 = (f32[64,2048]{1,0:T(8,128)}, f32[64,2048]{1,0:T(8,128)}, u32[]{:S(2)}, u32[]{:S(2)}) collective-permute-start(f32[64,2048]{1,0:T(8,128)} %fusion.19), channel_id=1, source_target_pairs={{0,2},{2,0},{4,6},{6,4},{8,10},{10,8},{12,14},{14,12},{1,3},{3,1},... | collective-permute-start | bytes 1572872 | tf_op jit(solution)/shard_map/ppermute | solution.py:58
  16.6 18.6 %collective-permute-start.6 = (f32[64,2048]{1,0:T(8,128)}, f32[64,2048]{1,0:T(8,128)}, u32[]{:S(2)}, u32[]{:S(2)}) collective-permute-start(f32[64,2048]{1,0:T(8,128)} %fusion.16), channel_id=1, source_target_pairs={{0,4},{2,6},{4,0},{6,2},{8,12},{10,14},{12,8},{14,10},{1,5},{3,7},... | collective-permute-start | bytes 1572872 | tf_op jit(solution)/shard_map/ppermute | solution.py:58
  17.9 22.8 %collective-permute-start.9 = (f32[64,2048]{1,0:T(8,128)}, f32[64,2048]{1,0:T(8,128)}, u32[]{:S(2)}, u32[]{:S(2)}) collective-permute-start(f32[64,2048]{1,0:T(8,128)} %fusion.18), channel_id=1, source_target_pairs={{0,2},{2,0},{4,6},{6,4},{8,10},{10,8},{12,14},{14,12},{1,3},{3,1},... | collective-permute-start | bytes 1572872 | tf_op jit(solution)/shard_map/ppermute | solution.py:58
  25.1 15.6 %copy-start.2 = (f32[64,512]{1,0:T(8,128)S(1)}, f32[64,512]{1,0:T(8,128)}, u32[]{:S(2)}) copy-start(f32[64,512]{1,0:T(8,128)} %copy-done.1) | copy-start | bytes 393220
  25.1 15.5 %copy-start.4 = (f32[64,512]{1,0:T(8,128)S(1)}, f32[64,512]{1,0:T(8,128)}, u32[]{:S(2)}) copy-start(f32[64,512]{1,0:T(8,128)} %copy-done.3) | copy-start | bytes 393220
  25.2 15.5 %copy-start.6 = (f32[64,512]{1,0:T(8,128)S(1)}, f32[64,512]{1,0:T(8,128)}, u32[]{:S(2)}) copy-start(f32[64,512]{1,0:T(8,128)} %copy-done.5) | copy-start | bytes 393220
  25.2 15.5 %copy-start.8 = (f32[64,512]{1,0:T(8,128)S(1)}, f32[64,512]{1,0:T(8,128)}, u32[]{:S(2)}) copy-start(f32[64,512]{1,0:T(8,128)} %copy-done.7) | copy-start | bytes 393220
  25.2 15.5 %copy-start.10 = (f32[64,512]{1,0:T(8,128)S(1)}, f32[64,512]{1,0:T(8,128)}, u32[]{:S(2)}) copy-start(f32[64,512]{1,0:T(8,128)} %copy-done.9) | copy-start | bytes 393220
  25.2 21.0 %collective-permute-start.1 = (f32[64,1024]{1,0:T(8,128)S(1)}, f32[64,1024]{1,0:T(8,128)S(1)}, u32[]{:S(2)}, u32[]{:S(2)}) collective-permute-start(f32[64,1024]{1,0:T(8,128)S(1)} %fusion.24), channel_id=1, source_target_pairs={{0,2},{2,0},{4,6},{6,4},{8,10},{10,8},{12,14},{14,12},{1,3},{3,1},... | collective-permute-start | bytes 786440 | tf_op jit(solution)/shard_map/ppermute | solution.py:58
  31.0 18.0 %collective-permute-start.4 = (f32[64,1024]{1,0:T(8,128)S(1)}, f32[64,1024]{1,0:T(8,128)S(1)}, u32[]{:S(2)}, u32[]{:S(2)}) collective-permute-start(f32[64,1024]{1,0:T(8,128)S(1)} %fusion.23), channel_id=1, source_target_pairs={{0,4},{2,6},{4,0},{6,2},{8,12},{10,14},{12,8},{14,10},{1,5},{3,7},... | collective-permute-start | bytes 786440 | tf_op jit(solution)/shard_map/ppermute | solution.py:58
  36.4 13.9 %collective-permute-start.7 = (f32[64,1024]{1,0:T(8,128)S(1)}, f32[64,1024]{1,0:T(8,128)S(1)}, u32[]{:S(2)}, u32[]{:S(2)}) collective-permute-start(f32[64,1024]{1,0:T(8,128)S(1)} %fusion.22), channel_id=1, source_target_pairs={{0,2},{2,0},{4,6},{6,4},{8,10},{10,8},{12,14},{14,12},{1,3},{3,1},... | collective-permute-start | bytes 786440 | tf_op jit(solution)/shard_map/ppermute | solution.py:58
  41.9 52.7 %copy-start = (f32[1,512,256]{1,2,0:T(8,128)S(1)}, f32[1,512,256]{1,2,0:T(8,128)}, u32[]{:S(2)}) copy-start(f32[1,512,256]{1,2,0:T(8,128)} %copy.14) | copy-start | bytes 1572868
  41.9 21.0 %collective-permute-start.10 = (f32[64,1024]{1,0:T(8,128)S(1)}, f32[64,1024]{1,0:T(8,128)S(1)}, u32[]{:S(2)}, u32[]{:S(2)}) collective-permute-start(f32[64,1024]{1,0:T(8,128)S(1)} %slice_select_fusion), channel_id=1, source_target_pairs={{0,8},{2,10},{4,12},{6,14},{8,0},{10,2},{12,4},{14,6},{1,9},{3,11}... | collective-permute-start | bytes 786440 | tf_op jit(solution)/shard_map/ppermute | solution.py:58
  46.3 19.5 %collective-permute-start.2 = (f32[64,512]{1,0:T(8,128)S(1)}, f32[64,512]{1,0:T(8,128)S(1)}, u32[]{:S(2)}, u32[]{:S(2)}) collective-permute-start(f32[64,512]{1,0:T(8,128)S(1)} %slice_select_fusion.4), channel_id=1, source_target_pairs={{0,8},{2,10},{4,12},{6,14},{8,0},{10,2},{12,4},{14,6},{1,9},{3,11}... | collective-permute-start | bytes 393224 | tf_op jit(solution)/shard_map/ppermute | solution.py:58
  49.0 19.6 %collective-permute-start.5 = (f32[64,512]{1,0:T(8,128)S(1)}, f32[64,512]{1,0:T(8,128)S(1)}, u32[]{:S(2)}, u32[]{:S(2)}) collective-permute-start(f32[64,512]{1,0:T(8,128)S(1)} %slice_select_fusion.3), channel_id=1, source_target_pairs={{0,8},{2,10},{4,12},{6,14},{8,0},{10,2},{12,4},{14,6},{1,9},{3,11}... | collective-permute-start | bytes 393224 | tf_op jit(solution)/shard_map/ppermute | solution.py:58
  50.4 20.4 %collective-permute-start.8 = (f32[64,512]{1,0:T(8,128)S(1)}, f32[64,512]{1,0:T(8,128)S(1)}, u32[]{:S(2)}, u32[]{:S(2)}) collective-permute-start(f32[64,512]{1,0:T(8,128)S(1)} %slice_select_fusion.2), channel_id=1, source_target_pairs={{0,8},{2,10},{4,12},{6,14},{8,0},{10,2},{12,4},{14,6},{1,9},{3,11}... | collective-permute-start | bytes 393224 | tf_op jit(solution)/shard_map/ppermute | solution.py:58
  63.0 10.6 %collective-permute-start.11 = (f32[64,512]{1,0:T(8,128)S(1)}, f32[64,512]{1,0:T(8,128)S(1)}, u32[]{:S(2)}, u32[]{:S(2)}) collective-permute-start(f32[64,512]{1,0:T(8,128)S(1)} %slice_select_fusion.1), channel_id=1, source_target_pairs={{0,4},{2,6},{4,0},{6,2},{8,12},{10,14},{12,8},{14,10},{1,5},{3,7},... | collective-permute-start | bytes 393224 | tf_op jit(solution)/shard_map/ppermute | solution.py:58
  74.3 3.7 %collective-permute-start.12 = (f32[]{:T(128)}, f32[]{:T(128)}, u32[]{:S(2)}, u32[]{:S(2)}) collective-permute-start(f32[]{:T(128)} %multiply_reduce_fusion), channel_id=1, source_target_pairs={{0,1},{1,0},{2,3},{3,2},{4,5},{5,4},{6,7},{7,6},{8,9},{9,8},{10,11... | collective-permute-start | bytes 20 | tf_op jit(solution)/shard_map/ppermute | solution.py:33
  79.3 1.2 collective-permute-start.13
  81.1 4.5 %collective-permute-start.14 = (f32[]{:T(128)}, f32[]{:T(128)}, u32[]{:S(2)}, u32[]{:S(2)}) collective-permute-start(f32[]{:T(128)} %add.79), channel_id=1, source_target_pairs={{0,8},{2,10},{4,12},{6,14},{8,0},{10,2},{12,4},{14,6},{1,9},{3,11}... | collective-permute-start | bytes 20 | tf_op jit(solution)/shard_map/ppermute | solution.py:33
  86.2 3.6 %collective-permute-start.15 = (f32[]{:T(128)}, f32[]{:T(128)}, u32[]{:S(2)}, u32[]{:S(2)}) collective-permute-start(f32[]{:T(128)} %add.80), channel_id=1, source_target_pairs={{0,4},{2,6},{4,0},{6,2},{8,12},{10,14},{12,8},{14,10},{1,5},{3,7},... | collective-permute-start | bytes 20 | tf_op jit(solution)/shard_map/ppermute | solution.py:33
  90.4 3.6 %collective-permute-start.16 = (f32[]{:T(128)}, f32[]{:T(128)}, u32[]{:S(2)}, u32[]{:S(2)}) collective-permute-start(f32[]{:T(128)} %add.81), channel_id=1, source_target_pairs={{0,2},{2,0},{4,6},{6,4},{8,10},{10,8},{12,14},{14,12},{1,3},{3,1},... | collective-permute-start | bytes 20 | tf_op jit(solution)/shard_map/ppermute | solution.py:33
  95.1 7.0 %collective-permute-start.17 = (bf16[512,128]{0,1:T(8,128)(2,1)S(1)}, bf16[512,128]{0,1:T(8,128)(2,1)S(1)}, u32[]{:S(2)}, u32[]{:S(2)}) collective-permute-start(bf16[512,128]{0,1:T(8,128)(2,1)S(1)} %get-tuple-element.55), channel_id=1, source_target_pairs={{0,8},{2,10},{4,12},{6,14},{8,0},{10,2},{12,4},{14,6},{1,9},{3,11}... | collective-permute-start | bytes 393224 | tf_op jit(solution)/shard_map/ppermute | solution.py:72
  96.1 5.9 %collective-permute-start.20 = (bf16[512,128]{0,1:T(8,128)(2,1)S(1)}, bf16[512,128]{0,1:T(8,128)(2,1)S(1)}, u32[]{:S(2)}, u32[]{:S(2)}) collective-permute-start(bf16[512,128]{0,1:T(8,128)(2,1)S(1)} %get-tuple-element.56), channel_id=1, source_target_pairs={{0,2},{2,0},{4,6},{6,4},{8,10},{10,8},{12,14},{14,12},{1,3},{3,1},... | collective-permute-start | bytes 393224 | tf_op jit(solution)/shard_map/ppermute | solution.py:72
  102.1 10.3 %collective-permute-start.18 = (bf16[2,512,128]{1,2,0:T(8,128)(2,1)S(1)}, bf16[2,512,128]{1,2,0:T(8,128)(2,1)S(1)}, u32[]{:S(2)}, u32[]{:S(2)}) collective-permute-start(bf16[2,512,128]{1,2,0:T(8,128)(2,1)S(1)} %pad_maximum_fusion.16), channel_id=1, source_target_pairs={{0,4},{2,6},{4,0},{6,2},{8,12},{10,14},{12,8},{14,10},{1,5},{3,7},... | collective-permute-start | bytes 786440 | tf_op jit(solution)/shard_map/ppermute | solution.py:72
  103.3 10.8 %collective-permute-start.21 = (bf16[2,512,128]{1,2,0:T(8,128)(2,1)S(1)}, bf16[2,512,128]{1,2,0:T(8,128)(2,1)S(1)}, u32[]{:S(2)}, u32[]{:S(2)}) collective-permute-start(bf16[2,512,128]{1,2,0:T(8,128)(2,1)S(1)} %pad_maximum_fusion.17), channel_id=1, source_target_pairs={{0,8},{2,10},{4,12},{6,14},{8,0},{10,2},{12,4},{14,6},{1,9},{3,11}... | collective-permute-start | bytes 786440 | tf_op jit(solution)/shard_map/ppermute | solution.py:72
  112.5 12.3 %collective-permute-start.19 = (bf16[2,2,512,128]{2,3,1,0:T(8,128)(2,1)S(1)}, bf16[2,2,512,128]{2,3,1,0:T(8,128)(2,1)S(1)}, u32[]{:S(2)}, u32[]{:S(2)}) collective-permute-start(bf16[2,2,512,128]{2,3,1,0:T(8,128)(2,1)S(1)} %pad_maximum_fusion.8), channel_id=1, source_target_pairs={{0,2},{2,0},{4,6},{6,4},{8,10},{10,8},{12,14},{14,12},{1,3},{3,1},... | collective-permute-start | bytes 1572872 | tf_op jit(solution)/shard_map/ppermute | solution.py:72
  115.0 12.2 %collective-permute-start.22 = (bf16[2,2,512,128]{2,3,1,0:T(8,128)(2,1)}, bf16[2,2,512,128]{2,3,1,0:T(8,128)(2,1)S(1)}, u32[]{:S(2)}, u32[]{:S(2)}) collective-permute-start(bf16[2,2,512,128]{2,3,1,0:T(8,128)(2,1)} %pad_maximum_fusion.9), channel_id=1, source_target_pairs={{0,4},{2,6},{4,0},{6,2},{8,12},{10,14},{12,8},{14,10},{1,5},{3,7},... | collective-permute-start | bytes 1572872 | tf_op jit(solution)/shard_map/ppermute | solution.py:72
  (6 other events, 44.7 us)

commit v21 on v19

--- a/solution.py
+++ b/solution.py
@@ -104,8 +104,8 @@
     half = cols // 2
     return jnp.concatenate(
         [
-            doubling_gather(part[:, :half], axis, first[::-1]),
-            doubling_gather(part[:, half:], axis, bit_orders(size)[2]),
+            doubling_gather(part[:, :half], axis, bit_orders(size)[2]),
+            doubling_gather(part[:, half:], axis, first[::-1]),
         ],
         axis=1,
     )

time: 126 us -> 131 us (1.040)
  waiting for transfers between devices: 59.6 us -> 64.3 us
    ppermute x6, waiting for transfers between devices: 22.7 us -> 27.3 us  [doubling_gather(): other = lax.ppermute(current, axis, pairs)]
  transfers between devices with their start and end apart: 23 -> 23, of which waited for: 17 -> 19; matrix products, arithmetic and copies ran while one was open for 13% -> 13% of each run, Pallas kernels for 0% -> 0%
where the time goes in v21:
time: 131 us
  waiting for transfers between devices  64.3 us (49%)
  starting transfers between devices  30.8 us (24%)
  other arithmetic  14.5 us (11%)
  local copies, waits for them, and re-layouts  9.86 us (8%)
  matrix products  6.18 us (5%)
  between operations  5.05 us (4%)
    ppermute x6, waiting for transfers between devices, doubling_gather(): other = lax.ppermute(current, axis, pairs)  27.3 us
    ppermute x12, waiting for transfers between devices, halving_scatter(): blocks = keep + lax.ppermute(send, axis, pairs)  26.9 us
    ppermute x12, starting transfers between devices, halving_scatter(): blocks = keep + lax.ppermute(send, axis, pairs)  18.1 us
    ppermute x5, waiting for transfers between devices, butterfly_sum(): value = value + lax.ppermute(value, axis, pairs)  10.1 us
    ppermute x5, starting transfers between devices, butterfly_sum(): value = value + lax.ppermute(value, axis, pairs)  6.96 us
    unnamed x45, local copies, waits for them, and re-layouts  6.55 us
    dot_general x1, matrix products, slot_term(): lax.dot_general(weighted, columns, (((0,), (0,)), ((), ())), preferred_el...  6.18 us
    ppermute x6, starting transfers between devices, doubling_gather(): other = lax.ppermute(current, axis, pairs)  5.74 us
  transfers between devices with their start and end apart: 23, of which 19 were waited for; matrix products, arithmetic and copies ran while one was open for 13% of the time, Pallas kernels for 0%

profile of v21, /device:TPU:0, one launch (start us, length us, event | category | flops | bytes accessed | tf_op | source)
XLA Modules:
  0.0 130.6 jit_solution(4025078631405602841)
XLA Ops:
  0.7 6.2 %fusion.2 = f32[256,4096]{1,0:T(8,128)S(1)} fusion(bf16[1,8,128,4096]{3,2,1,0:T(8,128)(2,1)} %param.6, bf16[1,8,128,256]{3,2,1,0:T(8,128)(2,1)} %param.7, pred[8]{0:T(512)(128)(4,1)S(1)} %compare_bitcast_fusion), kind=kOutput, calls=%fused_computation.2 | convolution fusion | flops 2147745792 | bytes 13107208 | tf_op jit(solution)/shard_map/dot_general | solution.py:19
  6.9 1.9 %copy-done = f32[256,4096]{1,0:T(8,128)} copy-done((f32[256,4096]{1,0:T(8,128)}, f32[256,4096]{1,0:T(8,128)S(1)}, u32[]{:S(2)}) %copy-start) | copy-done | bytes 4194328
  10.2 2.9 %collective-permute-start = (f32[64,2048]{1,0:T(8,128)}, f32[64,2048]{1,0:T(8,128)}, u32[]{:S(2)}, u32[]{:S(2)}) collective-permute-start(f32[64,2048]{1,0:T(8,128)} %fusion.19), channel_id=1, source_target_pairs={{0,2},{2,0},{4,6},{6,4},{8,10},{10,8},{12,14},{14,12},{1,3},{3,1},... | collective-permute-start | bytes 1572872 | tf_op jit(solution)/shard_map/ppermute | solution.py:58
  13.2 1.6 %fusion.27 = (f32[64,1024]{1,0:T(8,128)S(1)}, f32[64,1024]{1,0:T(8,128)S(1)}, f32[64,1024]{1,0:T(8,128)S(1)}, f32[64,1024]{1,0:T(8,128)S(1)}, f32[64,1024]{1,0:T...) fusion(f32[256,4096]{1,0:T(8,128)} %copy-done), kind=kLoop, calls=%fused_computation.80 | loop fusion | bytes 4194304 | tf_op jit(solution)/shard_map/slice | solution.py:54
  15.7 1.6 %collective-permute-start.3 = (f32[64,2048]{1,0:T(8,128)}, f32[64,2048]{1,0:T(8,128)}, u32[]{:S(2)}, u32[]{:S(2)}) collective-permute-start(f32[64,2048]{1,0:T(8,128)} %fusion.17), channel_id=1, source_target_pairs={{0,4},{2,6},{4,0},{6,2},{8,12},{10,14},{12,8},{14,10},{1,5},{3,7},... | collective-permute-start | bytes 1572872 | tf_op jit(solution)/shard_map/ppermute | solution.py:58
  23.5 2.0 %copy.14 = f32[1,512,256]{1,2,0:T(8,128)} copy(f32[1,512,256]{2,1,0:T(8,128)} %param.9) | data formatting | bytes 1048576 | tf_op args[3]
  26.2 1.4 %select_add_fusion.3 = f32[64,2048]{1,0:T(8,128)S(1)} fusion(f32[64,2048]{1,0:T(8,128)} %collective-permute-done, f32[64,512]{1,0:T(8,128)} %copy-done.13, f32[64,512]{1,0:T(8,128)} %copy-done.14, f32[64,512]{1,0:T(8,128)} %copy-done.15, f32[64,512]{1,0:T(8,128)} %copy-done.16, f32[64,512]{1,0:T(8,128)} %copy-done.17, f32[64,512]{1,0:T(8,128)} %copy-done.18, ...), kind=kLoop, calls=%fused_computation.35 | loop fusion | flops 1048576 | bytes 2097153 | tf_op jit(solution)/shard_map/add | solution.py:58
  27.7 2.2 %collective-permute-start.1 = (f32[64,1024]{1,0:T(8,128)S(1)}, f32[64,1024]{1,0:T(8,128)S(1)}, u32[]{:S(2)}, u32[]{:S(2)}) collective-permute-start(f32[64,1024]{1,0:T(8,128)S(1)} %fusion.24), channel_id=1, source_target_pairs={{0,4},{2,6},{4,0},{6,2},{8,12},{10,14},{12,8},{14,10},{1,5},{3,7},... | collective-permute-start | bytes 786440 | tf_op jit(solution)/shard_map/ppermute | solution.py:58
  32.7 4.7 %collective-permute-done.6 = f32[64,2048]{1,0:T(8,128)} collective-permute-done((f32[64,2048]{1,0:T(8,128)}, f32[64,2048]{1,0:T(8,128)}, u32[]{:S(2)}, u32[]{:S(2)}) %collective-permute-start.6) | collective-permute-done | bytes 524320 | tf_op jit(solution)/shard_map/ppermute | solution.py:58
  38.7 3.2 %collective-permute-start.7 = (f32[64,1024]{1,0:T(8,128)S(1)}, f32[64,1024]{1,0:T(8,128)S(1)}, u32[]{:S(2)}, u32[]{:S(2)}) collective-permute-start(f32[64,1024]{1,0:T(8,128)S(1)} %slice_select_fusion), channel_id=1, source_target_pairs={{0,8},{2,10},{4,12},{6,14},{8,0},{10,2},{12,4},{14,6},{1,9},{3,11}... | collective-permute-start | bytes 786440 | tf_op jit(solution)/shard_map/ppermute | solution.py:58
  41.9 5.8 %collective-permute-done.9 = f32[64,2048]{1,0:T(8,128)} collective-permute-done((f32[64,2048]{1,0:T(8,128)}, f32[64,2048]{1,0:T(8,128)}, u32[]{:S(2)}, u32[]{:S(2)}) %collective-permute-start.9) | collective-permute-done | bytes 524320 | tf_op jit(solution)/shard_map/ppermute | solution.py:58
  49.0 2.7 %collective-permute-done.1 = f32[64,1024]{1,0:T(8,128)S(1)} collective-permute-done((f32[64,1024]{1,0:T(8,128)S(1)}, f32[64,1024]{1,0:T(8,128)S(1)}, u32[]{:S(2)}, u32[]{:S(2)}) %collective-permute-start.1) | collective-permute-done | bytes 262176 | tf_op jit(solution)/shard_map/ppermute | solution.py:58
  53.1 1.9 %collective-permute-start.5 = (f32[64,512]{1,0:T(8,128)S(1)}, f32[64,512]{1,0:T(8,128)S(1)}, u32[]{:S(2)}, u32[]{:S(2)}) collective-permute-start(f32[64,512]{1,0:T(8,128)S(1)} %slice_select_fusion.3), channel_id=1, source_target_pairs={{0,8},{2,10},{4,12},{6,14},{8,0},{10,2},{12,4},{14,6},{1,9},{3,11}... | collective-permute-start | bytes 393224 | tf_op jit(solution)/shard_map/ppermute | solution.py:58
  55.9 3.0 %collective-permute-start.11 = (f32[64,512]{1,0:T(8,128)S(1)}, f32[64,512]{1,0:T(8,128)S(1)}, u32[]{:S(2)}, u32[]{:S(2)}) collective-permute-start(f32[64,512]{1,0:T(8,128)S(1)} %slice_select_fusion.1), channel_id=1, source_target_pairs={{0,8},{2,10},{4,12},{6,14},{8,0},{10,2},{12,4},{14,6},{1,9},{3,11}... | collective-permute-start | bytes 393224 | tf_op jit(solution)/shard_map/ppermute | solution.py:58
  58.9 6.0 %collective-permute-done.2 = f32[64,512]{1,0:T(8,128)S(1)} collective-permute-done((f32[64,512]{1,0:T(8,128)S(1)}, f32[64,512]{1,0:T(8,128)S(1)}, u32[]{:S(2)}, u32[]{:S(2)}) %collective-permute-start.2) | collective-permute-done | bytes 131104 | tf_op jit(solution)/shard_map/ppermute | solution.py:58
  64.9 4.2 %collective-permute-done.5 = f32[64,512]{1,0:T(8,128)S(1)} collective-permute-done((f32[64,512]{1,0:T(8,128)S(1)}, f32[64,512]{1,0:T(8,128)S(1)}, u32[]{:S(2)}, u32[]{:S(2)}) %collective-permute-start.5) | collective-permute-done | bytes 131104 | tf_op jit(solution)/shard_map/ppermute | solution.py:58
  69.2 1.7 %collective-permute-done.11 = f32[64,512]{1,0:T(8,128)S(1)} collective-permute-done((f32[64,512]{1,0:T(8,128)S(1)}, f32[64,512]{1,0:T(8,128)S(1)}, u32[]{:S(2)}, u32[]{:S(2)}) %collective-permute-start.11) | collective-permute-done | bytes 131104 | tf_op jit(solution)/shard_map/ppermute | solution.py:58
  71.7 1.5 %collective-permute-start.12 = (f32[]{:T(128)}, f32[]{:T(128)}, u32[]{:S(2)}, u32[]{:S(2)}) collective-permute-start(f32[]{:T(128)} %multiply_reduce_fusion), channel_id=1, source_target_pairs={{0,1},{1,0},{2,3},{3,2},{4,5},{5,4},{6,7},{7,6},{8,9},{9,8},{10,11... | collective-permute-start | bytes 20 | tf_op jit(solution)/shard_map/ppermute | solution.py:33
  73.3 2.2 %collective-permute-done.12 = f32[]{:T(128)} collective-permute-done((f32[]{:T(128)}, f32[]{:T(128)}, u32[]{:S(2)}, u32[]{:S(2)}) %collective-permute-start.12) | collective-permute-done | bytes 36 | tf_op jit(solution)/shard_map/ppermute | solution.py:33
  80.0 3.2 %collective-permute-done.14 = f32[]{:T(128)} collective-permute-done((f32[]{:T(128)}, f32[]{:T(128)}, u32[]{:S(2)}, u32[]{:S(2)}) %collective-permute-start.14) | collective-permute-done | bytes 36 | tf_op jit(solution)/shard_map/ppermute | solution.py:33
  85.3 2.3 %collective-permute-done.15 = f32[]{:T(128)} collective-permute-done((f32[]{:T(128)}, f32[]{:T(128)}, u32[]{:S(2)}, u32[]{:S(2)}) %collective-permute-start.15) | collective-permute-done | bytes 36 | tf_op jit(solution)/shard_map/ppermute | solution.py:33
  88.3 1.7 %collective-permute-start.16 = (f32[]{:T(128)}, f32[]{:T(128)}, u32[]{:S(2)}, u32[]{:S(2)}) collective-permute-start(f32[]{:T(128)} %add.81), channel_id=1, source_target_pairs={{0,2},{2,0},{4,6},{6,4},{8,10},{10,8},{12,14},{14,12},{1,3},{3,1},... | collective-permute-start | bytes 20 | tf_op jit(solution)/shard_map/ppermute | solution.py:33
  90.0 2.0 %collective-permute-done.16 = f32[]{:T(128)} collective-permute-done((f32[]{:T(128)}, f32[]{:T(128)}, u32[]{:S(2)}, u32[]{:S(2)}) %collective-permute-start.16) | collective-permute-done | bytes 36 | tf_op jit(solution)/shard_map/ppermute | solution.py:33
  93.5 1.4 %collective-permute-start.20 = (bf16[512,128]{0,1:T(8,128)(2,1)S(1)}, bf16[512,128]{0,1:T(8,128)(2,1)S(1)}, u32[]{:S(2)}, u32[]{:S(2)}) collective-permute-start(bf16[512,128]{0,1:T(8,128)(2,1)S(1)} %get-tuple-element.56), channel_id=1, source_target_pairs={{0,8},{2,10},{4,12},{6,14},{8,0},{10,2},{12,4},{14,6},{1,9},{3,11}... | collective-permute-start | bytes 393224 | tf_op jit(solution)/shard_map/ppermute | solution.py:72
  94.9 3.3 %collective-permute-done.17 = bf16[512,128]{0,1:T(8,128)(2,1)S(1)} collective-permute-done((bf16[512,128]{0,1:T(8,128)(2,1)S(1)}, bf16[512,128]{0,1:T(8,128)(2,1)S(1)}, u32[]{:S(2)}, u32[]{:S(2)}) %collective-permute-start.17) | collective-permute-done | bytes 131104 | tf_op jit(solution)/shard_map/ppermute | solution.py:72
  98.2 6.8 %collective-permute-done.20 = bf16[512,128]{0,1:T(8,128)(2,1)S(1)} collective-permute-done((bf16[512,128]{0,1:T(8,128)(2,1)S(1)}, bf16[512,128]{0,1:T(8,128)(2,1)S(1)}, u32[]{:S(2)}, u32[]{:S(2)}) %collective-permute-start.20) | collective-permute-done | bytes 131104 | tf_op jit(solution)/shard_map/ppermute | solution.py:72
  105.1 2.9 %collective-permute-start.21 = (bf16[2,512,128]{1,2,0:T(8,128)(2,1)S(1)}, bf16[2,512,128]{1,2,0:T(8,128)(2,1)S(1)}, u32[]{:S(2)}, u32[]{:S(2)}) collective-permute-start(bf16[2,512,128]{1,2,0:T(8,128)(2,1)S(1)} %pad_maximum_fusion.17), channel_id=1, source_target_pairs={{0,4},{2,6},{4,0},{6,2},{8,12},{10,14},{12,8},{14,10},{1,5},{3,7},... | collective-permute-start | bytes 786440 | tf_op jit(solution)/shard_map/ppermute | solution.py:72
  108.0 6.6 %collective-permute-done.18 = bf16[2,512,128]{1,2,0:T(8,128)(2,1)S(1)} collective-permute-done((bf16[2,512,128]{1,2,0:T(8,128)(2,1)S(1)}, bf16[2,512,128]{1,2,0:T(8,128)(2,1)S(1)}, u32[]{:S(2)}, u32[]{:S(2)}) %collective-permute-start.18) | collective-permute-done | bytes 262176 | tf_op jit(solution)/shard_map/ppermute | solution.py:72
  114.7 3.2 %collective-permute-done.21 = bf16[2,512,128]{1,2,0:T(8,128)(2,1)S(1)} collective-permute-done((bf16[2,512,128]{1,2,0:T(8,128)(2,1)S(1)}, bf16[2,512,128]{1,2,0:T(8,128)(2,1)S(1)}, u32[]{:S(2)}, u32[]{:S(2)}) %collective-permute-start.21) | collective-permute-done | bytes 262176 | tf_op jit(solution)/shard_map/ppermute | solution.py:72
  119.7 6.1 %collective-permute-done.19 = bf16[2,2,512,128]{2,3,1,0:T(8,128)(2,1)S(1)} collective-permute-done((bf16[2,2,512,128]{2,3,1,0:T(8,128)(2,1)S(1)}, bf16[2,2,512,128]{2,3,1,0:T(8,128)(2,1)S(1)}, u32[]{:S(2)}, u32[]{:S(2)}) %collective-permute-start.19) | collective-permute-done | bytes 524320 | tf_op jit(solution)/shard_map/ppermute | solution.py:72
  126.7 1.4 %collective-permute-done.22 = bf16[2,2,512,128]{2,3,1,0:T(8,128)(2,1)S(1)} collective-permute-done((bf16[2,2,512,128]{2,3,1,0:T(8,128)(2,1)}, bf16[2,2,512,128]{2,3,1,0:T(8,128)(2,1)S(1)}, u32[]{:S(2)}, u32[]{:S(2)}) %collective-permute-start.22) | collective-permute-done | bytes 524320 | tf_op jit(solution)/shard_map/ppermute | solution.py:72
  129.0 1.5 %maximum_bitcast_fusion = bf16[1,4096,256]{2,1,0:T(8,128)(2,1)} fusion(bf16[4096,128]{1,0:T(8,128)(2,1)S(1)} %bitcast.75, bf16[4096,128]{1,0:T(8,128)(2,1)S(1)} %bitcast.74), kind=kLoop, calls=%fused_computation.3 | loop fusion | flops 4194304 | bytes 4194304 | tf_op jit(solution)/shard_map/broadcast_in_dim | solution.py:132
  (108 shorter events, 26.2 us)
Async XLA Ops:
  9.1 11.8 %copy-start.12 = (f32[64,512]{1,0:T(8,128)}, f32[64,512]{1,0:T(8,128)S(1)}, u32[]{:S(2)}) copy-start(f32[64,512]{1,0:T(8,128)S(1)} %get-tuple-element.5) | copy-start | bytes 393220
  9.1 11.8 %copy-start.13 = (f32[64,512]{1,0:T(8,128)}, f32[64,512]{1,0:T(8,128)S(1)}, u32[]{:S(2)}) copy-start(f32[64,512]{1,0:T(8,128)S(1)} %get-tuple-element.14) | copy-start | bytes 393220
  9.1 11.8 %copy-start.14 = (f32[64,512]{1,0:T(8,128)}, f32[64,512]{1,0:T(8,128)S(1)}, u32[]{:S(2)}) copy-start(f32[64,512]{1,0:T(8,128)S(1)} %get-tuple-element.15) | copy-start | bytes 393220
  10.2 16.0 %collective-permute-start = (f32[64,2048]{1,0:T(8,128)}, f32[64,2048]{1,0:T(8,128)}, u32[]{:S(2)}, u32[]{:S(2)}) collective-permute-start(f32[64,2048]{1,0:T(8,128)} %fusion.19), channel_id=1, source_target_pairs={{0,2},{2,0},{4,6},{6,4},{8,10},{10,8},{12,14},{14,12},{1,3},{3,1},... | collective-permute-start | bytes 1572872 | tf_op jit(solution)/shard_map/ppermute | solution.py:58
  15.7 15.2 %collective-permute-start.3 = (f32[64,2048]{1,0:T(8,128)}, f32[64,2048]{1,0:T(8,128)}, u32[]{:S(2)}, u32[]{:S(2)}) collective-permute-start(f32[64,2048]{1,0:T(8,128)} %fusion.17), channel_id=1, source_target_pairs={{0,4},{2,6},{4,0},{6,2},{8,12},{10,14},{12,8},{14,10},{1,5},{3,7},... | collective-permute-start | bytes 1572872 | tf_op jit(solution)/shard_map/ppermute | solution.py:58
  18.2 19.3 %collective-permute-start.6 = (f32[64,2048]{1,0:T(8,128)}, f32[64,2048]{1,0:T(8,128)}, u32[]{:S(2)}, u32[]{:S(2)}) collective-permute-start(f32[64,2048]{1,0:T(8,128)} %fusion.18), channel_id=1, source_target_pairs={{0,2},{2,0},{4,6},{6,4},{8,10},{10,8},{12,14},{14,12},{1,3},{3,1},... | collective-permute-start | bytes 1572872 | tf_op jit(solution)/shard_map/ppermute | solution.py:58
  19.6 28.1 %collective-permute-start.9 = (f32[64,2048]{1,0:T(8,128)}, f32[64,2048]{1,0:T(8,128)}, u32[]{:S(2)}, u32[]{:S(2)}) collective-permute-start(f32[64,2048]{1,0:T(8,128)} %fusion.16), channel_id=1, source_target_pairs={{0,4},{2,6},{4,0},{6,2},{8,12},{10,14},{12,8},{14,10},{1,5},{3,7},... | collective-permute-start | bytes 1572872 | tf_op jit(solution)/shard_map/ppermute | solution.py:58
  25.5 12.0 %copy-start.3 = (f32[64,512]{1,0:T(8,128)S(1)}, f32[64,512]{1,0:T(8,128)}, u32[]{:S(2)}) copy-start(f32[64,512]{1,0:T(8,128)} %copy-done.2) | copy-start | bytes 393220
  25.5 12.0 %copy-start.5 = (f32[64,512]{1,0:T(8,128)S(1)}, f32[64,512]{1,0:T(8,128)}, u32[]{:S(2)}) copy-start(f32[64,512]{1,0:T(8,128)} %copy-done.4) | copy-start | bytes 393220
  25.5 12.0 %copy-start.7 = (f32[64,512]{1,0:T(8,128)S(1)}, f32[64,512]{1,0:T(8,128)}, u32[]{:S(2)}) copy-start(f32[64,512]{1,0:T(8,128)} %copy-done.6) | copy-start | bytes 393220
  25.5 12.0 %copy-start.9 = (f32[64,512]{1,0:T(8,128)S(1)}, f32[64,512]{1,0:T(8,128)}, u32[]{:S(2)}) copy-start(f32[64,512]{1,0:T(8,128)} %copy-done.8) | copy-start | bytes 393220
  25.5 12.0 %copy-start.11 = (f32[64,512]{1,0:T(8,128)S(1)}, f32[64,512]{1,0:T(8,128)}, u32[]{:S(2)}) copy-start(f32[64,512]{1,0:T(8,128)} %copy-done.10) | copy-start | bytes 393220
  27.7 24.1 %collective-permute-start.1 = (f32[64,1024]{1,0:T(8,128)S(1)}, f32[64,1024]{1,0:T(8,128)S(1)}, u32[]{:S(2)}, u32[]{:S(2)}) collective-permute-start(f32[64,1024]{1,0:T(8,128)S(1)} %fusion.24), channel_id=1, source_target_pairs={{0,4},{2,6},{4,0},{6,2},{8,12},{10,14},{12,8},{14,10},{1,5},{3,7},... | collective-permute-start | bytes 786440 | tf_op jit(solution)/shard_map/ppermute | solution.py:58
  32.1 21.0 %collective-permute-start.4 = (f32[64,1024]{1,0:T(8,128)S(1)}, f32[64,1024]{1,0:T(8,128)S(1)}, u32[]{:S(2)}, u32[]{:S(2)}) collective-permute-start(f32[64,1024]{1,0:T(8,128)S(1)} %fusion.23), channel_id=1, source_target_pairs={{0,2},{2,0},{4,6},{6,4},{8,10},{10,8},{12,14},{14,12},{1,3},{3,1},... | collective-permute-start | bytes 786440 | tf_op jit(solution)/shard_map/ppermute | solution.py:58
  38.7 16.3 %collective-permute-start.7 = (f32[64,1024]{1,0:T(8,128)S(1)}, f32[64,1024]{1,0:T(8,128)S(1)}, u32[]{:S(2)}, u32[]{:S(2)}) collective-permute-start(f32[64,1024]{1,0:T(8,128)S(1)} %slice_select_fusion), channel_id=1, source_target_pairs={{0,8},{2,10},{4,12},{6,14},{8,0},{10,2},{12,4},{14,6},{1,9},{3,11}... | collective-permute-start | bytes 786440 | tf_op jit(solution)/shard_map/ppermute | solution.py:58
  48.9 43.7 %copy-start.1 = (f32[1,512,256]{1,2,0:T(8,128)S(1)}, f32[1,512,256]{1,2,0:T(8,128)}, u32[]{:S(2)}) copy-start(f32[1,512,256]{1,2,0:T(8,128)} %copy.14) | copy-start | bytes 1572868
  49.0 6.9 %collective-permute-start.10 = (f32[64,1024]{1,0:T(8,128)S(1)}, f32[64,1024]{1,0:T(8,128)S(1)}, u32[]{:S(2)}, u32[]{:S(2)}) collective-permute-start(f32[64,1024]{1,0:T(8,128)S(1)} %fusion.22), channel_id=1, source_target_pairs={{0,2},{2,0},{4,6},{6,4},{8,10},{10,8},{12,14},{14,12},{1,3},{3,1},... | collective-permute-start | bytes 786440 | tf_op jit(solution)/shard_map/ppermute | solution.py:58
  51.8 13.0 %collective-permute-start.2 = (f32[64,512]{1,0:T(8,128)S(1)}, f32[64,512]{1,0:T(8,128)S(1)}, u32[]{:S(2)}, u32[]{:S(2)}) collective-permute-start(f32[64,512]{1,0:T(8,128)S(1)} %slice_select_fusion.4), channel_id=1, source_target_pairs={{0,8},{2,10},{4,12},{6,14},{8,0},{10,2},{12,4},{14,6},{1,9},{3,11}... | collective-permute-start | bytes 393224 | tf_op jit(solution)/shard_map/ppermute | solution.py:58
  53.1 16.0 %collective-permute-start.5 = (f32[64,512]{1,0:T(8,128)S(1)}, f32[64,512]{1,0:T(8,128)S(1)}, u32[]{:S(2)}, u32[]{:S(2)}) collective-permute-start(f32[64,512]{1,0:T(8,128)S(1)} %slice_select_fusion.3), channel_id=1, source_target_pairs={{0,8},{2,10},{4,12},{6,14},{8,0},{10,2},{12,4},{14,6},{1,9},{3,11}... | collective-permute-start | bytes 393224 | tf_op jit(solution)/shard_map/ppermute | solution.py:58
  55.1 14.1 %collective-permute-start.8 = (f32[64,512]{1,0:T(8,128)S(1)}, f32[64,512]{1,0:T(8,128)S(1)}, u32[]{:S(2)}, u32[]{:S(2)}) collective-permute-start(f32[64,512]{1,0:T(8,128)S(1)} %slice_select_fusion.2), channel_id=1, source_target_pairs={{0,4},{2,6},{4,0},{6,2},{8,12},{10,14},{12,8},{14,10},{1,5},{3,7},... | collective-permute-start | bytes 393224 | tf_op jit(solution)/shard_map/ppermute | solution.py:58
  55.9 15.0 %collective-permute-start.11 = (f32[64,512]{1,0:T(8,128)S(1)}, f32[64,512]{1,0:T(8,128)S(1)}, u32[]{:S(2)}, u32[]{:S(2)}) collective-permute-start(f32[64,512]{1,0:T(8,128)S(1)} %slice_select_fusion.1), channel_id=1, source_target_pairs={{0,8},{2,10},{4,12},{6,14},{8,0},{10,2},{12,4},{14,6},{1,9},{3,11}... | collective-permute-start | bytes 393224 | tf_op jit(solution)/shard_map/ppermute | solution.py:58
  71.7 3.7 %collective-permute-start.12 = (f32[]{:T(128)}, f32[]{:T(128)}, u32[]{:S(2)}, u32[]{:S(2)}) collective-permute-start(f32[]{:T(128)} %multiply_reduce_fusion), channel_id=1, source_target_pairs={{0,1},{1,0},{2,3},{3,2},{4,5},{5,4},{6,7},{7,6},{8,9},{9,8},{10,11... | collective-permute-start | bytes 20 | tf_op jit(solution)/shard_map/ppermute | solution.py:33
  76.7 1.3 %collective-permute-start.13 = (f32[]{:T(128)}, f32[]{:T(128)}, u32[]{:S(2)}, u32[]{:S(2)}) collective-permute-start(f32[]{:T(128)} %add.78), channel_id=1, source_target_pairs={{0,16},{16,0},{1,17},{17,1},{2,18},{18,2},{3,19},{19,3},{4,20},{20... | collective-permute-start | bytes 20 | tf_op jit(solution)/shard_map/ppermute | solution.py:33
  78.7 4.6 %collective-permute-start.14 = (f32[]{:T(128)}, f32[]{:T(128)}, u32[]{:S(2)}, u32[]{:S(2)}) collective-permute-start(f32[]{:T(128)} %add.79), channel_id=1, source_target_pairs={{0,8},{2,10},{4,12},{6,14},{8,0},{10,2},{12,4},{14,6},{1,9},{3,11}... | collective-permute-start | bytes 20 | tf_op jit(solution)/shard_map/ppermute | solution.py:33
  83.9 3.7 %collective-permute-start.15 = (f32[]{:T(128)}, f32[]{:T(128)}, u32[]{:S(2)}, u32[]{:S(2)}) collective-permute-start(f32[]{:T(128)} %add.80), channel_id=1, source_target_pairs={{0,4},{2,6},{4,0},{6,2},{8,12},{10,14},{12,8},{14,10},{1,5},{3,7},... | collective-permute-start | bytes 20 | tf_op jit(solution)/shard_map/ppermute | solution.py:33
  88.3 3.7 %collective-permute-start.16 = (f32[]{:T(128)}, f32[]{:T(128)}, u32[]{:S(2)}, u32[]{:S(2)}) collective-permute-start(f32[]{:T(128)} %add.81), channel_id=1, source_target_pairs={{0,2},{2,0},{4,6},{6,4},{8,10},{10,8},{12,14},{14,12},{1,3},{3,1},... | collective-permute-start | bytes 20 | tf_op jit(solution)/shard_map/ppermute | solution.py:33
  93.1 5.0 %collective-permute-start.17 = (bf16[512,128]{0,1:T(8,128)(2,1)S(1)}, bf16[512,128]{0,1:T(8,128)(2,1)S(1)}, u32[]{:S(2)}, u32[]{:S(2)}) collective-permute-start(bf16[512,128]{0,1:T(8,128)(2,1)S(1)} %get-tuple-element.55), channel_id=1, source_target_pairs={{0,2},{2,0},{4,6},{6,4},{8,10},{10,8},{12,14},{14,12},{1,3},{3,1},... | collective-permute-start | bytes 393224 | tf_op jit(solution)/shard_map/ppermute | solution.py:72
  93.5 11.4 %collective-permute-start.20 = (bf16[512,128]{0,1:T(8,128)(2,1)S(1)}, bf16[512,128]{0,1:T(8,128)(2,1)S(1)}, u32[]{:S(2)}, u32[]{:S(2)}) collective-permute-start(bf16[512,128]{0,1:T(8,128)(2,1)S(1)} %get-tuple-element.56), channel_id=1, source_target_pairs={{0,8},{2,10},{4,12},{6,14},{8,0},{10,2},{12,4},{14,6},{1,9},{3,11}... | collective-permute-start | bytes 393224 | tf_op jit(solution)/shard_map/ppermute | solution.py:72
  105.0 9.5 %collective-permute-start.18 = (bf16[2,512,128]{1,2,0:T(8,128)(2,1)S(1)}, bf16[2,512,128]{1,2,0:T(8,128)(2,1)S(1)}, u32[]{:S(2)}, u32[]{:S(2)}) collective-permute-start(bf16[2,512,128]{1,2,0:T(8,128)(2,1)S(1)} %pad_maximum_fusion.16), channel_id=1, source_target_pairs={{0,8},{2,10},{4,12},{6,14},{8,0},{10,2},{12,4},{14,6},{1,9},{3,11}... | collective-permute-start | bytes 786440 | tf_op jit(solution)/shard_map/ppermute | solution.py:72
  105.1 12.8 %collective-permute-start.21 = (bf16[2,512,128]{1,2,0:T(8,128)(2,1)S(1)}, bf16[2,512,128]{1,2,0:T(8,128)(2,1)S(1)}, u32[]{:S(2)}, u32[]{:S(2)}) collective-permute-start(bf16[2,512,128]{1,2,0:T(8,128)(2,1)S(1)} %pad_maximum_fusion.17), channel_id=1, source_target_pairs={{0,4},{2,6},{4,0},{6,2},{8,12},{10,14},{12,8},{14,10},{1,5},{3,7},... | collective-permute-start | bytes 786440 | tf_op jit(solution)/shard_map/ppermute | solution.py:72
  114.7 11.2 %collective-permute-start.19 = (bf16[2,2,512,128]{2,3,1,0:T(8,128)(2,1)S(1)}, bf16[2,2,512,128]{2,3,1,0:T(8,128)(2,1)S(1)}, u32[]{:S(2)}, u32[]{:S(2)}) collective-permute-start(bf16[2,2,512,128]{2,3,1,0:T(8,128)(2,1)S(1)} %pad_maximum_fusion.8), channel_id=1, source_target_pairs={{0,4},{2,6},{4,0},{6,2},{8,12},{10,14},{12,8},{14,10},{1,5},{3,7},... | collective-permute-start | bytes 1572872 | tf_op jit(solution)/shard_map/ppermute | solution.py:72
  118.8 9.4 %collective-permute-start.22 = (bf16[2,2,512,128]{2,3,1,0:T(8,128)(2,1)}, bf16[2,2,512,128]{2,3,1,0:T(8,128)(2,1)S(1)}, u32[]{:S(2)}, u32[]{:S(2)}) collective-permute-start(bf16[2,2,512,128]{2,3,1,0:T(8,128)(2,1)} %pad_maximum_fusion.9), channel_id=1, source_target_pairs={{0,2},{2,0},{4,6},{6,4},{8,10},{10,8},{12,14},{14,12},{1,3},{3,1},... | collective-permute-start | bytes 1572872 | tf_op jit(solution)/shard_map/ppermute | solution.py:72
  (12 other events, 74.4 us)

commit v22 on v19

--- a/solution.py
+++ b/solution.py
@@ -120,7 +120,7 @@
     summed = scatter_rows(slot_term(inputs, key_grads, live_row, features), "dp")
     tokens_total = (live_count * (inputs.shape[1] * lax.axis_size("dp"))).astype(jnp.float32)
     grad_shard = summed / tokens_total
-    squares = butterfly_sum(jnp.sum(grad_shard * grad_shard), ("tensor", "pipe", "dp"))
+    squares = butterfly_sum(jnp.sum(grad_shard * grad_shard), ("pipe", "dp", "tensor"))
     clip_factor = jnp.minimum(1.0, CLIP_NORM / jnp.sqrt(squares))
     clipped = clip_factor * grad_shard
     moment1 = MOMENT_DECAY * first_moment[0].T + (1.0 - MOMENT_DECAY) * clipped

time: 126 us -> 129 us (1.024)
  starting transfers between devices: 30.2 us -> 32.6 us
    ppermute x6, starting transfers between devices: 5.14 us -> 7.26 us  [doubling_gather(): other = lax.ppermute(current, axis, pairs)]
    ppermute x6, waiting for transfers between devices: 22.7 us -> 24.1 us  [doubling_gather(): other = lax.ppermute(current, axis, pairs)]
where the time goes in v22:
time: 129 us
  waiting for transfers between devices  60.8 us (47%)
  starting transfers between devices  32.6 us (25%)
  other arithmetic  14.5 us (11%)
  local copies, waits for them, and re-layouts  9.86 us (8%)
  matrix products  6.18 us (5%)
  between operations  5.06 us (4%)
    ppermute x12, waiting for transfers between devices, halving_scatter(): blocks = keep + lax.ppermute(send, axis, pairs)  26.9 us
    ppermute x6, waiting for transfers between devices, doubling_gather(): other = lax.ppermute(current, axis, pairs)  24.1 us
    ppermute x12, starting transfers between devices, halving_scatter(): blocks = keep + lax.ppermute(send, axis, pairs)  18.1 us
    ppermute x5, waiting for transfers between devices, butterfly_sum(): value = value + lax.ppermute(value, axis, pairs)  9.74 us
    ppermute x5, starting transfers between devices, butterfly_sum(): value = value + lax.ppermute(value, axis, pairs)  7.3 us
    ppermute x6, starting transfers between devices, doubling_gather(): other = lax.ppermute(current, axis, pairs)  7.26 us
    unnamed x45, local copies, waits for them, and re-layouts  6.55 us
    dot_general x1, matrix products, slot_term(): lax.dot_general(weighted, columns, (((0,), (0,)), ((), ())), preferred_el...  6.18 us
  transfers between devices with their start and end apart: 23, of which 17 were waited for; matrix products, arithmetic and copies ran while one was open for 13% of the time, Pallas kernels for 0%

profile of v22, /device:TPU:0, one launch (start us, length us, event | category | flops | bytes accessed | tf_op | source)
XLA Modules:
  0.0 128.9 jit_solution(15667658044740777045)
XLA Ops:
  0.7 6.2 %fusion.2 = f32[256,4096]{1,0:T(8,128)S(1)} fusion(bf16[1,8,128,4096]{3,2,1,0:T(8,128)(2,1)} %param.6, bf16[1,8,128,256]{3,2,1,0:T(8,128)(2,1)} %param.7, pred[8]{0:T(512)(128)(4,1)S(1)} %compare_bitcast_fusion), kind=kOutput, calls=%fused_computation.2 | convolution fusion | flops 2147745792 | bytes 13107208 | tf_op jit(solution)/shard_map/dot_general | solution.py:19
  6.9 1.9 %copy-done = f32[256,4096]{1,0:T(8,128)} copy-done((f32[256,4096]{1,0:T(8,128)}, f32[256,4096]{1,0:T(8,128)S(1)}, u32[]{:S(2)}) %copy-start) | copy-done | bytes 4194328
  10.2 2.9 %collective-permute-start = (f32[64,2048]{1,0:T(8,128)}, f32[64,2048]{1,0:T(8,128)}, u32[]{:S(2)}, u32[]{:S(2)}) collective-permute-start(f32[64,2048]{1,0:T(8,128)} %fusion.19), channel_id=1, source_target_pairs={{0,2},{2,0},{4,6},{6,4},{8,10},{10,8},{12,14},{14,12},{1,3},{3,1},... | collective-permute-start | bytes 1572872 | tf_op jit(solution)/shard_map/ppermute | solution.py:58
  13.2 1.6 %fusion.27 = (f32[64,1024]{1,0:T(8,128)S(1)}, f32[64,1024]{1,0:T(8,128)S(1)}, f32[64,1024]{1,0:T(8,128)S(1)}, f32[64,1024]{1,0:T(8,128)S(1)}, f32[64,1024]{1,0:T...) fusion(f32[256,4096]{1,0:T(8,128)} %copy-done), kind=kLoop, calls=%fused_computation.80 | loop fusion | bytes 4194304 | tf_op jit(solution)/shard_map/slice | solution.py:54
  15.7 1.6 %collective-permute-start.3 = (f32[64,2048]{1,0:T(8,128)}, f32[64,2048]{1,0:T(8,128)}, u32[]{:S(2)}, u32[]{:S(2)}) collective-permute-start(f32[64,2048]{1,0:T(8,128)} %fusion.17), channel_id=1, source_target_pairs={{0,4},{2,6},{4,0},{6,2},{8,12},{10,14},{12,8},{14,10},{1,5},{3,7},... | collective-permute-start | bytes 1572872 | tf_op jit(solution)/shard_map/ppermute | solution.py:58
  22.2 1.2 copy.13
  23.5 2.0 %copy.14 = f32[1,512,256]{1,2,0:T(8,128)} copy(f32[1,512,256]{2,1,0:T(8,128)} %param.9) | data formatting | bytes 1048576 | tf_op args[3]
  26.2 1.4 %select_add_fusion.3 = f32[64,2048]{1,0:T(8,128)S(1)} fusion(f32[64,2048]{1,0:T(8,128)} %collective-permute-done, f32[64,512]{1,0:T(8,128)} %copy-done.13, f32[64,512]{1,0:T(8,128)} %copy-done.14, f32[64,512]{1,0:T(8,128)} %copy-done.15, f32[64,512]{1,0:T(8,128)} %copy-done.16, f32[64,512]{1,0:T(8,128)} %copy-done.17, f32[64,512]{1,0:T(8,128)} %copy-done.18, ...), kind=kLoop, calls=%fused_computation.35 | loop fusion | flops 1048576 | bytes 2097153 | tf_op jit(solution)/shard_map/add | solution.py:58
  27.7 2.2 %collective-permute-start.1 = (f32[64,1024]{1,0:T(8,128)S(1)}, f32[64,1024]{1,0:T(8,128)S(1)}, u32[]{:S(2)}, u32[]{:S(2)}) collective-permute-start(f32[64,1024]{1,0:T(8,128)S(1)} %fusion.24), channel_id=1, source_target_pairs={{0,4},{2,6},{4,0},{6,2},{8,12},{10,14},{12,8},{14,10},{1,5},{3,7},... | collective-permute-start | bytes 786440 | tf_op jit(solution)/shard_map/ppermute | solution.py:58
  32.7 4.7 %collective-permute-done.6 = f32[64,2048]{1,0:T(8,128)} collective-permute-done((f32[64,2048]{1,0:T(8,128)}, f32[64,2048]{1,0:T(8,128)}, u32[]{:S(2)}, u32[]{:S(2)}) %collective-permute-start.6) | collective-permute-done | bytes 524320 | tf_op jit(solution)/shard_map/ppermute | solution.py:58
  38.7 3.2 %collective-permute-start.7 = (f32[64,1024]{1,0:T(8,128)S(1)}, f32[64,1024]{1,0:T(8,128)S(1)}, u32[]{:S(2)}, u32[]{:S(2)}) collective-permute-start(f32[64,1024]{1,0:T(8,128)S(1)} %slice_select_fusion), channel_id=1, source_target_pairs={{0,8},{2,10},{4,12},{6,14},{8,0},{10,2},{12,4},{14,6},{1,9},{3,11}... | collective-permute-start | bytes 786440 | tf_op jit(solution)/shard_map/ppermute | solution.py:58
  41.9 5.8 %collective-permute-done.9 = f32[64,2048]{1,0:T(8,128)} collective-permute-done((f32[64,2048]{1,0:T(8,128)}, f32[64,2048]{1,0:T(8,128)}, u32[]{:S(2)}, u32[]{:S(2)}) %collective-permute-start.9) | collective-permute-done | bytes 524320 | tf_op jit(solution)/shard_map/ppermute | solution.py:58
  49.0 2.7 %collective-permute-done.1 = f32[64,1024]{1,0:T(8,128)S(1)} collective-permute-done((f32[64,1024]{1,0:T(8,128)S(1)}, f32[64,1024]{1,0:T(8,128)S(1)}, u32[]{:S(2)}, u32[]{:S(2)}) %collective-permute-start.1) | collective-permute-done | bytes 262176 | tf_op jit(solution)/shard_map/ppermute | solution.py:58
  53.1 1.9 %collective-permute-start.5 = (f32[64,512]{1,0:T(8,128)S(1)}, f32[64,512]{1,0:T(8,128)S(1)}, u32[]{:S(2)}, u32[]{:S(2)}) collective-permute-start(f32[64,512]{1,0:T(8,128)S(1)} %slice_select_fusion.3), channel_id=1, source_target_pairs={{0,8},{2,10},{4,12},{6,14},{8,0},{10,2},{12,4},{14,6},{1,9},{3,11}... | collective-permute-start | bytes 393224 | tf_op jit(solution)/shard_map/ppermute | solution.py:58
  55.9 3.0 %collective-permute-start.11 = (f32[64,512]{1,0:T(8,128)S(1)}, f32[64,512]{1,0:T(8,128)S(1)}, u32[]{:S(2)}, u32[]{:S(2)}) collective-permute-start(f32[64,512]{1,0:T(8,128)S(1)} %slice_select_fusion.1), channel_id=1, source_target_pairs={{0,8},{2,10},{4,12},{6,14},{8,0},{10,2},{12,4},{14,6},{1,9},{3,11}... | collective-permute-start | bytes 393224 | tf_op jit(solution)/shard_map/ppermute | solution.py:58
  58.9 6.0 %collective-permute-done.2 = f32[64,512]{1,0:T(8,128)S(1)} collective-permute-done((f32[64,512]{1,0:T(8,128)S(1)}, f32[64,512]{1,0:T(8,128)S(1)}, u32[]{:S(2)}, u32[]{:S(2)}) %collective-permute-start.2) | collective-permute-done | bytes 131104 | tf_op jit(solution)/shard_map/ppermute | solution.py:58
  64.9 4.2 %collective-permute-done.5 = f32[64,512]{1,0:T(8,128)S(1)} collective-permute-done((f32[64,512]{1,0:T(8,128)S(1)}, f32[64,512]{1,0:T(8,128)S(1)}, u32[]{:S(2)}, u32[]{:S(2)}) %collective-permute-start.5) | collective-permute-done | bytes 131104 | tf_op jit(solution)/shard_map/ppermute | solution.py:58
  69.2 1.7 %collective-permute-done.11 = f32[64,512]{1,0:T(8,128)S(1)} collective-permute-done((f32[64,512]{1,0:T(8,128)S(1)}, f32[64,512]{1,0:T(8,128)S(1)}, u32[]{:S(2)}, u32[]{:S(2)}) %collective-permute-start.11) | collective-permute-done | bytes 131104 | tf_op jit(solution)/shard_map/ppermute | solution.py:58
  71.7 1.3 %collective-permute-done.12 = f32[]{:T(128)} collective-permute-done((f32[]{:T(128)}, f32[]{:T(128)}, u32[]{:S(2)}, u32[]{:S(2)}) %collective-permute-start.12) | collective-permute-done | bytes 36 | tf_op jit(solution)/shard_map/ppermute | solution.py:33
  74.3 1.4 %collective-permute-start.13 = (f32[]{:T(128)}, f32[]{:T(128)}, u32[]{:S(2)}, u32[]{:S(2)}) collective-permute-start(f32[]{:T(128)} %add.78), channel_id=1, source_target_pairs={{0,8},{2,10},{4,12},{6,14},{8,0},{10,2},{12,4},{14,6},{1,9},{3,11}... | collective-permute-start | bytes 20 | tf_op jit(solution)/shard_map/ppermute | solution.py:33
  75.7 3.2 %collective-permute-done.13 = f32[]{:T(128)} collective-permute-done((f32[]{:T(128)}, f32[]{:T(128)}, u32[]{:S(2)}, u32[]{:S(2)}) %collective-permute-start.13) | collective-permute-done | bytes 36 | tf_op jit(solution)/shard_map/ppermute | solution.py:33
  79.6 1.4 %collective-permute-start.14 = (f32[]{:T(128)}, f32[]{:T(128)}, u32[]{:S(2)}, u32[]{:S(2)}) collective-permute-start(f32[]{:T(128)} %add.79), channel_id=1, source_target_pairs={{0,4},{2,6},{4,0},{6,2},{8,12},{10,14},{12,8},{14,10},{1,5},{3,7},... | collective-permute-start | bytes 20 | tf_op jit(solution)/shard_map/ppermute | solution.py:33
  80.9 2.3 %collective-permute-done.14 = f32[]{:T(128)} collective-permute-done((f32[]{:T(128)}, f32[]{:T(128)}, u32[]{:S(2)}, u32[]{:S(2)}) %collective-permute-start.14) | collective-permute-done | bytes 36 | tf_op jit(solution)/shard_map/ppermute | solution.py:33
  83.9 1.7 %collective-permute-start.15 = (f32[]{:T(128)}, f32[]{:T(128)}, u32[]{:S(2)}, u32[]{:S(2)}) collective-permute-start(f32[]{:T(128)} %add.80), channel_id=1, source_target_pairs={{0,2},{2,0},{4,6},{6,4},{8,10},{10,8},{12,14},{14,12},{1,3},{3,1},... | collective-permute-start | bytes 20 | tf_op jit(solution)/shard_map/ppermute | solution.py:33
  85.6 2.0 %collective-permute-done.15 = f32[]{:T(128)} collective-permute-done((f32[]{:T(128)}, f32[]{:T(128)}, u32[]{:S(2)}, u32[]{:S(2)}) %collective-permute-start.15) | collective-permute-done | bytes 36 | tf_op jit(solution)/shard_map/ppermute | solution.py:33
  88.3 2.9 %collective-permute-start.16 = (f32[]{:T(128)}, f32[]{:T(128)}, u32[]{:S(2)}, u32[]{:S(2)}) collective-permute-start(f32[]{:T(128)} %add.81), channel_id=1, source_target_pairs={{0,1},{1,0},{2,3},{3,2},{4,5},{5,4},{6,7},{7,6},{8,9},{9,8},{10,11... | collective-permute-start | bytes 20 | tf_op jit(solution)/shard_map/ppermute | solution.py:33
  94.9 9.5 %collective-permute-done.17 = bf16[512,128]{0,1:T(8,128)(2,1)S(1)} collective-permute-done((bf16[512,128]{0,1:T(8,128)(2,1)S(1)}, bf16[512,128]{0,1:T(8,128)(2,1)S(1)}, u32[]{:S(2)}, u32[]{:S(2)}) %collective-permute-start.17) | collective-permute-done | bytes 131104 | tf_op jit(solution)/shard_map/ppermute | solution.py:72
  104.6 2.6 %collective-permute-start.21 = (bf16[2,512,128]{1,2,0:T(8,128)(2,1)S(1)}, bf16[2,512,128]{1,2,0:T(8,128)(2,1)S(1)}, u32[]{:S(2)}, u32[]{:S(2)}) collective-permute-start(bf16[2,512,128]{1,2,0:T(8,128)(2,1)S(1)} %pad_maximum_fusion.17), channel_id=1, source_target_pairs={{0,8},{2,10},{4,12},{6,14},{8,0},{10,2},{12,4},{14,6},{1,9},{3,11}... | collective-permute-start | bytes 786440 | tf_op jit(solution)/shard_map/ppermute | solution.py:72
  107.2 8.2 %collective-permute-done.18 = bf16[2,512,128]{1,2,0:T(8,128)(2,1)S(1)} collective-permute-done((bf16[2,512,128]{1,2,0:T(8,128)(2,1)S(1)}, bf16[2,512,128]{1,2,0:T(8,128)(2,1)S(1)}, u32[]{:S(2)}, u32[]{:S(2)}) %collective-permute-start.18) | collective-permute-done | bytes 262176 | tf_op jit(solution)/shard_map/ppermute | solution.py:72
  116.5 2.7 %collective-permute-start.22 = (bf16[2,2,512,128]{2,3,1,0:T(8,128)(2,1)}, bf16[2,2,512,128]{2,3,1,0:T(8,128)(2,1)S(1)}, u32[]{:S(2)}, u32[]{:S(2)}) collective-permute-start(bf16[2,2,512,128]{2,3,1,0:T(8,128)(2,1)} %pad_maximum_fusion.9), channel_id=1, source_target_pairs={{0,4},{2,6},{4,0},{6,2},{8,12},{10,14},{12,8},{14,10},{1,5},{3,7},... | collective-permute-start | bytes 1572872 | tf_op jit(solution)/shard_map/ppermute | solution.py:72
  119.2 5.5 %collective-permute-done.19 = bf16[2,2,512,128]{2,3,1,0:T(8,128)(2,1)S(1)} collective-permute-done((bf16[2,2,512,128]{2,3,1,0:T(8,128)(2,1)S(1)}, bf16[2,2,512,128]{2,3,1,0:T(8,128)(2,1)S(1)}, u32[]{:S(2)}, u32[]{:S(2)}) %collective-permute-start.19) | collective-permute-done | bytes 524320 | tf_op jit(solution)/shard_map/ppermute | solution.py:72
  127.4 1.5 %maximum_bitcast_fusion = bf16[1,4096,256]{2,1,0:T(8,128)(2,1)} fusion(bf16[4096,128]{1,0:T(8,128)(2,1)S(1)} %bitcast.75, bf16[4096,128]{1,0:T(8,128)(2,1)S(1)} %bitcast.74), kind=kLoop, calls=%fused_computation.3 | loop fusion | flops 4194304 | bytes 4194304 | tf_op jit(solution)/shard_map/broadcast_in_dim | solution.py:132
  (108 shorter events, 23.1 us)
Async XLA Ops:
  9.1 11.8 %copy-start.12 = (f32[64,512]{1,0:T(8,128)}, f32[64,512]{1,0:T(8,128)S(1)}, u32[]{:S(2)}) copy-start(f32[64,512]{1,0:T(8,128)S(1)} %get-tuple-element.5) | copy-start | bytes 393220
  9.1 11.8 %copy-start.13 = (f32[64,512]{1,0:T(8,128)}, f32[64,512]{1,0:T(8,128)S(1)}, u32[]{:S(2)}) copy-start(f32[64,512]{1,0:T(8,128)S(1)} %get-tuple-element.14) | copy-start | bytes 393220
  9.1 11.8 %copy-start.14 = (f32[64,512]{1,0:T(8,128)}, f32[64,512]{1,0:T(8,128)S(1)}, u32[]{:S(2)}) copy-start(f32[64,512]{1,0:T(8,128)S(1)} %get-tuple-element.15) | copy-start | bytes 393220
  10.2 16.0 %collective-permute-start = (f32[64,2048]{1,0:T(8,128)}, f32[64,2048]{1,0:T(8,128)}, u32[]{:S(2)}, u32[]{:S(2)}) collective-permute-start(f32[64,2048]{1,0:T(8,128)} %fusion.19), channel_id=1, source_target_pairs={{0,2},{2,0},{4,6},{6,4},{8,10},{10,8},{12,14},{14,12},{1,3},{3,1},... | collective-permute-start | bytes 1572872 | tf_op jit(solution)/shard_map/ppermute | solution.py:58
  15.7 15.2 %collective-permute-start.3 = (f32[64,2048]{1,0:T(8,128)}, f32[64,2048]{1,0:T(8,128)}, u32[]{:S(2)}, u32[]{:S(2)}) collective-permute-start(f32[64,2048]{1,0:T(8,128)} %fusion.17), channel_id=1, source_target_pairs={{0,4},{2,6},{4,0},{6,2},{8,12},{10,14},{12,8},{14,10},{1,5},{3,7},... | collective-permute-start | bytes 1572872 | tf_op jit(solution)/shard_map/ppermute | solution.py:58
  18.2 19.3 %collective-permute-start.6 = (f32[64,2048]{1,0:T(8,128)}, f32[64,2048]{1,0:T(8,128)}, u32[]{:S(2)}, u32[]{:S(2)}) collective-permute-start(f32[64,2048]{1,0:T(8,128)} %fusion.18), channel_id=1, source_target_pairs={{0,2},{2,0},{4,6},{6,4},{8,10},{10,8},{12,14},{14,12},{1,3},{3,1},... | collective-permute-start | bytes 1572872 | tf_op jit(solution)/shard_map/ppermute | solution.py:58
  19.6 28.1 %collective-permute-start.9 = (f32[64,2048]{1,0:T(8,128)}, f32[64,2048]{1,0:T(8,128)}, u32[]{:S(2)}, u32[]{:S(2)}) collective-permute-start(f32[64,2048]{1,0:T(8,128)} %fusion.16), channel_id=1, source_target_pairs={{0,4},{2,6},{4,0},{6,2},{8,12},{10,14},{12,8},{14,10},{1,5},{3,7},... | collective-permute-start | bytes 1572872 | tf_op jit(solution)/shard_map/ppermute | solution.py:58
  25.5 12.0 %copy-start.3 = (f32[64,512]{1,0:T(8,128)S(1)}, f32[64,512]{1,0:T(8,128)}, u32[]{:S(2)}) copy-start(f32[64,512]{1,0:T(8,128)} %copy-done.2) | copy-start | bytes 393220
  25.5 12.0 %copy-start.5 = (f32[64,512]{1,0:T(8,128)S(1)}, f32[64,512]{1,0:T(8,128)}, u32[]{:S(2)}) copy-start(f32[64,512]{1,0:T(8,128)} %copy-done.4) | copy-start | bytes 393220
  25.5 12.0 %copy-start.7 = (f32[64,512]{1,0:T(8,128)S(1)}, f32[64,512]{1,0:T(8,128)}, u32[]{:S(2)}) copy-start(f32[64,512]{1,0:T(8,128)} %copy-done.6) | copy-start | bytes 393220
  25.5 12.0 %copy-start.9 = (f32[64,512]{1,0:T(8,128)S(1)}, f32[64,512]{1,0:T(8,128)}, u32[]{:S(2)}) copy-start(f32[64,512]{1,0:T(8,128)} %copy-done.8) | copy-start | bytes 393220
  25.5 12.0 %copy-start.11 = (f32[64,512]{1,0:T(8,128)S(1)}, f32[64,512]{1,0:T(8,128)}, u32[]{:S(2)}) copy-start(f32[64,512]{1,0:T(8,128)} %copy-done.10) | copy-start | bytes 393220
  27.7 24.1 %collective-permute-start.1 = (f32[64,1024]{1,0:T(8,128)S(1)}, f32[64,1024]{1,0:T(8,128)S(1)}, u32[]{:S(2)}, u32[]{:S(2)}) collective-permute-start(f32[64,1024]{1,0:T(8,128)S(1)} %fusion.24), channel_id=1, source_target_pairs={{0,4},{2,6},{4,0},{6,2},{8,12},{10,14},{12,8},{14,10},{1,5},{3,7},... | collective-permute-start | bytes 786440 | tf_op jit(solution)/shard_map/ppermute | solution.py:58
  32.1 21.0 %collective-permute-start.4 = (f32[64,1024]{1,0:T(8,128)S(1)}, f32[64,1024]{1,0:T(8,128)S(1)}, u32[]{:S(2)}, u32[]{:S(2)}) collective-permute-start(f32[64,1024]{1,0:T(8,128)S(1)} %fusion.23), channel_id=1, source_target_pairs={{0,2},{2,0},{4,6},{6,4},{8,10},{10,8},{12,14},{14,12},{1,3},{3,1},... | collective-permute-start | bytes 786440 | tf_op jit(solution)/shard_map/ppermute | solution.py:58
  38.7 16.3 %collective-permute-start.7 = (f32[64,1024]{1,0:T(8,128)S(1)}, f32[64,1024]{1,0:T(8,128)S(1)}, u32[]{:S(2)}, u32[]{:S(2)}) collective-permute-start(f32[64,1024]{1,0:T(8,128)S(1)} %slice_select_fusion), channel_id=1, source_target_pairs={{0,8},{2,10},{4,12},{6,14},{8,0},{10,2},{12,4},{14,6},{1,9},{3,11}... | collective-permute-start | bytes 786440 | tf_op jit(solution)/shard_map/ppermute | solution.py:58
  48.9 43.7 %copy-start.1 = (f32[1,512,256]{1,2,0:T(8,128)S(1)}, f32[1,512,256]{1,2,0:T(8,128)}, u32[]{:S(2)}) copy-start(f32[1,512,256]{1,2,0:T(8,128)} %copy.14) | copy-start | bytes 1572868
  49.0 6.9 %collective-permute-start.10 = (f32[64,1024]{1,0:T(8,128)S(1)}, f32[64,1024]{1,0:T(8,128)S(1)}, u32[]{:S(2)}, u32[]{:S(2)}) collective-permute-start(f32[64,1024]{1,0:T(8,128)S(1)} %fusion.22), channel_id=1, source_target_pairs={{0,2},{2,0},{4,6},{6,4},{8,10},{10,8},{12,14},{14,12},{1,3},{3,1},... | collective-permute-start | bytes 786440 | tf_op jit(solution)/shard_map/ppermute | solution.py:58
  51.8 13.0 %collective-permute-start.2 = (f32[64,512]{1,0:T(8,128)S(1)}, f32[64,512]{1,0:T(8,128)S(1)}, u32[]{:S(2)}, u32[]{:S(2)}) collective-permute-start(f32[64,512]{1,0:T(8,128)S(1)} %slice_select_fusion.4), channel_id=1, source_target_pairs={{0,8},{2,10},{4,12},{6,14},{8,0},{10,2},{12,4},{14,6},{1,9},{3,11}... | collective-permute-start | bytes 393224 | tf_op jit(solution)/shard_map/ppermute | solution.py:58
  53.1 16.0 %collective-permute-start.5 = (f32[64,512]{1,0:T(8,128)S(1)}, f32[64,512]{1,0:T(8,128)S(1)}, u32[]{:S(2)}, u32[]{:S(2)}) collective-permute-start(f32[64,512]{1,0:T(8,128)S(1)} %slice_select_fusion.3), channel_id=1, source_target_pairs={{0,8},{2,10},{4,12},{6,14},{8,0},{10,2},{12,4},{14,6},{1,9},{3,11}... | collective-permute-start | bytes 393224 | tf_op jit(solution)/shard_map/ppermute | solution.py:58
  55.1 14.1 %collective-permute-start.8 = (f32[64,512]{1,0:T(8,128)S(1)}, f32[64,512]{1,0:T(8,128)S(1)}, u32[]{:S(2)}, u32[]{:S(2)}) collective-permute-start(f32[64,512]{1,0:T(8,128)S(1)} %slice_select_fusion.2), channel_id=1, source_target_pairs={{0,4},{2,6},{4,0},{6,2},{8,12},{10,14},{12,8},{14,10},{1,5},{3,7},... | collective-permute-start | bytes 393224 | tf_op jit(solution)/shard_map/ppermute | solution.py:58
  55.9 15.0 %collective-permute-start.11 = (f32[64,512]{1,0:T(8,128)S(1)}, f32[64,512]{1,0:T(8,128)S(1)}, u32[]{:S(2)}, u32[]{:S(2)}) collective-permute-start(f32[64,512]{1,0:T(8,128)S(1)} %slice_select_fusion.1), channel_id=1, source_target_pairs={{0,8},{2,10},{4,12},{6,14},{8,0},{10,2},{12,4},{14,6},{1,9},{3,11}... | collective-permute-start | bytes 393224 | tf_op jit(solution)/shard_map/ppermute | solution.py:58
  71.7 1.3 %collective-permute-start.12 = (f32[]{:T(128)}, f32[]{:T(128)}, u32[]{:S(2)}, u32[]{:S(2)}) collective-permute-start(f32[]{:T(128)} %multiply_reduce_fusion), channel_id=1, source_target_pairs={{0,16},{16,0},{1,17},{17,1},{2,18},{18,2},{3,19},{19,3},{4,20},{20... | collective-permute-start | bytes 20 | tf_op jit(solution)/shard_map/ppermute | solution.py:33
  74.3 4.6 %collective-permute-start.13 = (f32[]{:T(128)}, f32[]{:T(128)}, u32[]{:S(2)}, u32[]{:S(2)}) collective-permute-start(f32[]{:T(128)} %add.78), channel_id=1, source_target_pairs={{0,8},{2,10},{4,12},{6,14},{8,0},{10,2},{12,4},{14,6},{1,9},{3,11}... | collective-permute-start | bytes 20 | tf_op jit(solution)/shard_map/ppermute | solution.py:33
  79.6 3.7 %collective-permute-start.14 = (f32[]{:T(128)}, f32[]{:T(128)}, u32[]{:S(2)}, u32[]{:S(2)}) collective-permute-start(f32[]{:T(128)} %add.79), channel_id=1, source_target_pairs={{0,4},{2,6},{4,0},{6,2},{8,12},{10,14},{12,8},{14,10},{1,5},{3,7},... | collective-permute-start | bytes 20 | tf_op jit(solution)/shard_map/ppermute | solution.py:33
  83.9 3.7 %collective-permute-start.15 = (f32[]{:T(128)}, f32[]{:T(128)}, u32[]{:S(2)}, u32[]{:S(2)}) collective-permute-start(f32[]{:T(128)} %add.80), channel_id=1, source_target_pairs={{0,2},{2,0},{4,6},{6,4},{8,10},{10,8},{12,14},{14,12},{1,3},{3,1},... | collective-permute-start | bytes 20 | tf_op jit(solution)/shard_map/ppermute | solution.py:33
  88.3 3.7 %collective-permute-start.16 = (f32[]{:T(128)}, f32[]{:T(128)}, u32[]{:S(2)}, u32[]{:S(2)}) collective-permute-start(f32[]{:T(128)} %add.81), channel_id=1, source_target_pairs={{0,1},{1,0},{2,3},{3,2},{4,5},{5,4},{6,7},{7,6},{8,9},{9,8},{10,11... | collective-permute-start | bytes 20 | tf_op jit(solution)/shard_map/ppermute | solution.py:33
  93.1 11.2 %collective-permute-start.17 = (bf16[512,128]{0,1:T(8,128)(2,1)S(1)}, bf16[512,128]{0,1:T(8,128)(2,1)S(1)}, u32[]{:S(2)}, u32[]{:S(2)}) collective-permute-start(bf16[512,128]{0,1:T(8,128)(2,1)S(1)} %get-tuple-element.55), channel_id=1, source_target_pairs={{0,8},{2,10},{4,12},{6,14},{8,0},{10,2},{12,4},{14,6},{1,9},{3,11}... | collective-permute-start | bytes 393224 | tf_op jit(solution)/shard_map/ppermute | solution.py:72
  93.8 10.6 %collective-permute-start.20 = (bf16[512,128]{0,1:T(8,128)(2,1)S(1)}, bf16[512,128]{0,1:T(8,128)(2,1)S(1)}, u32[]{:S(2)}, u32[]{:S(2)}) collective-permute-start(bf16[512,128]{0,1:T(8,128)(2,1)S(1)} %get-tuple-element.56), channel_id=1, source_target_pairs={{0,2},{2,0},{4,6},{6,4},{8,10},{10,8},{12,14},{14,12},{1,3},{3,1},... | collective-permute-start | bytes 393224 | tf_op jit(solution)/shard_map/ppermute | solution.py:72
  104.5 10.9 %collective-permute-start.18 = (bf16[2,512,128]{1,2,0:T(8,128)(2,1)S(1)}, bf16[2,512,128]{1,2,0:T(8,128)(2,1)S(1)}, u32[]{:S(2)}, u32[]{:S(2)}) collective-permute-start(bf16[2,512,128]{1,2,0:T(8,128)(2,1)S(1)} %pad_maximum_fusion.16), channel_id=1, source_target_pairs={{0,4},{2,6},{4,0},{6,2},{8,12},{10,14},{12,8},{14,10},{1,5},{3,7},... | collective-permute-start | bytes 786440 | tf_op jit(solution)/shard_map/ppermute | solution.py:72
  104.6 11.0 %collective-permute-start.21 = (bf16[2,512,128]{1,2,0:T(8,128)(2,1)S(1)}, bf16[2,512,128]{1,2,0:T(8,128)(2,1)S(1)}, u32[]{:S(2)}, u32[]{:S(2)}) collective-permute-start(bf16[2,512,128]{1,2,0:T(8,128)(2,1)S(1)} %pad_maximum_fusion.17), channel_id=1, source_target_pairs={{0,8},{2,10},{4,12},{6,14},{8,0},{10,2},{12,4},{14,6},{1,9},{3,11}... | collective-permute-start | bytes 786440 | tf_op jit(solution)/shard_map/ppermute | solution.py:72
  115.5 9.2 %collective-permute-start.19 = (bf16[2,2,512,128]{2,3,1,0:T(8,128)(2,1)S(1)}, bf16[2,2,512,128]{2,3,1,0:T(8,128)(2,1)S(1)}, u32[]{:S(2)}, u32[]{:S(2)}) collective-permute-start(bf16[2,2,512,128]{2,3,1,0:T(8,128)(2,1)S(1)} %pad_maximum_fusion.8), channel_id=1, source_target_pairs={{0,2},{2,0},{4,6},{6,4},{8,10},{10,8},{12,14},{14,12},{1,3},{3,1},... | collective-permute-start | bytes 1572872 | tf_op jit(solution)/shard_map/ppermute | solution.py:72
  116.5 10.1 %collective-permute-start.22 = (bf16[2,2,512,128]{2,3,1,0:T(8,128)(2,1)}, bf16[2,2,512,128]{2,3,1,0:T(8,128)(2,1)S(1)}, u32[]{:S(2)}, u32[]{:S(2)}) collective-permute-start(bf16[2,2,512,128]{2,3,1,0:T(8,128)(2,1)} %pad_maximum_fusion.9), channel_id=1, source_target_pairs={{0,4},{2,6},{4,0},{6,2},{8,12},{10,14},{12,8},{14,10},{1,5},{3,7},... | collective-permute-start | bytes 1572872 | tf_op jit(solution)/shard_map/ppermute | solution.py:72
  (12 other events, 74.4 us)

commit v23 on v20

--- a/solution.py
+++ b/solution.py
@@ -88,7 +88,7 @@
     width = cols // parts
     return jnp.concatenate(
         [
-            halving_scatter(partial_t[k * width:(k + 1) * width], axis, orders[(1, 0, 1, 2)[k % 4]])
+            halving_scatter(partial_t[k * width:(k + 1) * width], axis, orders[(2, 1, 0, 1)[k % 4]])
             for k in range(parts)
         ],
         axis=0,

time: 130 us -> 126 us (0.969)
  waiting for transfers between devices: 62.2 us -> 54.7 us
  local copies, waits for them, and re-layouts: 7.16 us -> 9.86 us
  starting transfers between devices: 33.4 us -> 34.8 us
    ppermute x12, waiting for transfers between devices: 31.2 us -> 25.3 us  [halving_scatter(): blocks = keep + lax.ppermute(send, axis, pairs)]
    unnamed x33 -> x45, local copies, waits for them, and re-layouts: 4.58 us -> 6.55 us
    ppermute x6, waiting for transfers between devices: 23 us -> 21 us  [doubling_gather(): other = lax.ppermute(current, axis, pairs)]
  transfers between devices with their start and end apart: 23 -> 23, of which waited for: 19 -> 16; matrix products, arithmetic and copies ran while one was open for 13% -> 13% of each run, Pallas kernels for 0% -> 0%
where the time goes in v23:
time: 126 us; the launch traced here: 125 us
  waiting for transfers between devices  54.7 us (43%)
  starting transfers between devices  34.8 us (28%)
  other arithmetic  14.5 us (12%)
  local copies, waits for them, and re-layouts  9.86 us (8%)
  matrix products  6.18 us (5%)
  between operations  5.05 us (4%)
    ppermute x12, waiting for transfers between devices, halving_scatter(): blocks = keep + lax.ppermute(send, axis, pairs)  25.3 us
    ppermute x6, waiting for transfers between devices, doubling_gather(): other = lax.ppermute(current, axis, pairs)  21 us
    ppermute x12, starting transfers between devices, halving_scatter(): blocks = keep + lax.ppermute(send, axis, pairs)  18.2 us
    ppermute x5, starting transfers between devices, butterfly_sum(): value = value + lax.ppermute(value, axis, pairs)  8.64 us
    ppermute x5, waiting for transfers between devices, butterfly_sum(): value = value + lax.ppermute(value, axis, pairs)  8.4 us
    ppermute x6, starting transfers between devices, doubling_gather(): other = lax.ppermute(current, axis, pairs)  7.92 us
    unnamed x45, local copies, waits for them, and re-layouts  6.55 us
    dot_general x1, matrix products, slot_term(): lax.dot_general(weighted, columns, (((0,), (0,)), ((), ())), preferred_el...  6.18 us
  transfers between devices with their start and end apart: 23, of which 16 were waited for; matrix products, arithmetic and copies ran while one was open for 13% of the time, Pallas kernels for 0%

profile of v23, /device:TPU:0, one launch (start us, length us, event | category | flops | bytes accessed | tf_op | source)
XLA Modules:
  0.0 125.1 jit_solution(15291056867955325366)
XLA Ops:
  0.7 6.2 %fusion.2 = f32[256,4096]{1,0:T(8,128)S(1)} fusion(bf16[1,8,128,4096]{3,2,1,0:T(8,128)(2,1)} %param.6, bf16[1,8,128,256]{3,2,1,0:T(8,128)(2,1)} %param.7, pred[8]{0:T(512)(128)(4,1)S(1)} %compare_bitcast_fusion), kind=kOutput, calls=%fused_computation.2 | convolution fusion | flops 2147745792 | bytes 13107208 | tf_op jit(solution)/shard_map/dot_general | solution.py:19
  6.9 1.9 %copy-done = f32[256,4096]{1,0:T(8,128)} copy-done((f32[256,4096]{1,0:T(8,128)}, f32[256,4096]{1,0:T(8,128)S(1)}, u32[]{:S(2)}) %copy-start) | copy-done | bytes 4194328
  10.2 2.9 %collective-permute-start = (f32[64,2048]{1,0:T(8,128)}, f32[64,2048]{1,0:T(8,128)}, u32[]{:S(2)}, u32[]{:S(2)}) collective-permute-start(f32[64,2048]{1,0:T(8,128)} %fusion.19), channel_id=1, source_target_pairs={{0,2},{2,0},{4,6},{6,4},{8,10},{10,8},{12,14},{14,12},{1,3},{3,1},... | collective-permute-start | bytes 1572872 | tf_op jit(solution)/shard_map/ppermute | solution.py:58
  13.2 1.6 %fusion.27 = (f32[64,1024]{1,0:T(8,128)S(1)}, f32[64,1024]{1,0:T(8,128)S(1)}, f32[64,1024]{1,0:T(8,128)S(1)}, f32[64,1024]{1,0:T(8,128)S(1)}, f32[64,1024]{1,0:T...) fusion(f32[256,4096]{1,0:T(8,128)} %copy-done), kind=kLoop, calls=%fused_computation.80 | loop fusion | bytes 4194304 | tf_op jit(solution)/shard_map/slice | solution.py:54
  15.7 1.6 %collective-permute-start.3 = (f32[64,2048]{1,0:T(8,128)}, f32[64,2048]{1,0:T(8,128)}, u32[]{:S(2)}, u32[]{:S(2)}) collective-permute-start(f32[64,2048]{1,0:T(8,128)} %fusion.17), channel_id=1, source_target_pairs={{0,4},{2,6},{4,0},{6,2},{8,12},{10,14},{12,8},{14,10},{1,5},{3,7},... | collective-permute-start | bytes 1572872 | tf_op jit(solution)/shard_map/ppermute | solution.py:58
  23.5 2.0 %copy.14 = f32[1,512,256]{1,2,0:T(8,128)} copy(f32[1,512,256]{2,1,0:T(8,128)} %param.9) | data formatting | bytes 1048576 | tf_op args[3]
  26.2 1.4 %select_add_fusion.3 = f32[64,2048]{1,0:T(8,128)S(1)} fusion(f32[64,2048]{1,0:T(8,128)} %collective-permute-done, f32[64,512]{1,0:T(8,128)} %copy-done.13, f32[64,512]{1,0:T(8,128)} %copy-done.14, f32[64,512]{1,0:T(8,128)} %copy-done.15, f32[64,512]{1,0:T(8,128)} %copy-done.16, f32[64,512]{1,0:T(8,128)} %copy-done.17, f32[64,512]{1,0:T(8,128)} %copy-done.18, ...), kind=kLoop, calls=%fused_computation.35 | loop fusion | flops 1048576 | bytes 2097153 | tf_op jit(solution)/shard_map/add | solution.py:58
  27.7 3.2 %collective-permute-start.1 = (f32[64,1024]{1,0:T(8,128)S(1)}, f32[64,1024]{1,0:T(8,128)S(1)}, u32[]{:S(2)}, u32[]{:S(2)}) collective-permute-start(f32[64,1024]{1,0:T(8,128)S(1)} %slice_select_fusion), channel_id=1, source_target_pairs={{0,8},{2,10},{4,12},{6,14},{8,0},{10,2},{12,4},{14,6},{1,9},{3,11}... | collective-permute-start | bytes 786440 | tf_op jit(solution)/shard_map/ppermute | solution.py:58
  30.9 5.6 %collective-permute-done.3 = f32[64,2048]{1,0:T(8,128)} collective-permute-done((f32[64,2048]{1,0:T(8,128)}, f32[64,2048]{1,0:T(8,128)}, u32[]{:S(2)}, u32[]{:S(2)}) %collective-permute-start.3) | collective-permute-done | bytes 524320 | tf_op jit(solution)/shard_map/ppermute | solution.py:58
  39.1 1.9 %collective-permute-start.7 = (f32[64,1024]{1,0:T(8,128)S(1)}, f32[64,1024]{1,0:T(8,128)S(1)}, u32[]{:S(2)}, u32[]{:S(2)}) collective-permute-start(f32[64,1024]{1,0:T(8,128)S(1)} %fusion.23), channel_id=1, source_target_pairs={{0,4},{2,6},{4,0},{6,2},{8,12},{10,14},{12,8},{14,10},{1,5},{3,7},... | collective-permute-start | bytes 786440 | tf_op jit(solution)/shard_map/ppermute | solution.py:58
  40.9 6.8 %collective-permute-done.9 = f32[64,2048]{1,0:T(8,128)} collective-permute-done((f32[64,2048]{1,0:T(8,128)}, f32[64,2048]{1,0:T(8,128)}, u32[]{:S(2)}, u32[]{:S(2)}) %collective-permute-start.9) | collective-permute-done | bytes 524320 | tf_op jit(solution)/shard_map/ppermute | solution.py:58
  50.4 3.6 %collective-permute-start.5 = (f32[64,512]{1,0:T(8,128)S(1)}, f32[64,512]{1,0:T(8,128)S(1)}, u32[]{:S(2)}, u32[]{:S(2)}) collective-permute-start(f32[64,512]{1,0:T(8,128)S(1)} %slice_select_fusion.3), channel_id=1, source_target_pairs={{0,8},{2,10},{4,12},{6,14},{8,0},{10,2},{12,4},{14,6},{1,9},{3,11}... | collective-permute-start | bytes 393224 | tf_op jit(solution)/shard_map/ppermute | solution.py:58
  54.0 2.1 %collective-permute-done.7 = f32[64,1024]{1,0:T(8,128)S(1)} collective-permute-done((f32[64,1024]{1,0:T(8,128)S(1)}, f32[64,1024]{1,0:T(8,128)S(1)}, u32[]{:S(2)}, u32[]{:S(2)}) %collective-permute-start.7) | collective-permute-done | bytes 262176 | tf_op jit(solution)/shard_map/ppermute | solution.py:58
  56.6 2.7 %collective-permute-start.11 = (f32[64,512]{1,0:T(8,128)S(1)}, f32[64,512]{1,0:T(8,128)S(1)}, u32[]{:S(2)}, u32[]{:S(2)}) collective-permute-start(f32[64,512]{1,0:T(8,128)S(1)} %slice_select_fusion.1), channel_id=1, source_target_pairs={{0,8},{2,10},{4,12},{6,14},{8,0},{10,2},{12,4},{14,6},{1,9},{3,11}... | collective-permute-start | bytes 393224 | tf_op jit(solution)/shard_map/ppermute | solution.py:58
  59.4 7.0 %collective-permute-done.5 = f32[64,512]{1,0:T(8,128)S(1)} collective-permute-done((f32[64,512]{1,0:T(8,128)S(1)}, f32[64,512]{1,0:T(8,128)S(1)}, u32[]{:S(2)}, u32[]{:S(2)}) %collective-permute-start.5) | collective-permute-done | bytes 131104 | tf_op jit(solution)/shard_map/ppermute | solution.py:58
  66.4 1.7 %collective-permute-done.8 = f32[64,512]{1,0:T(8,128)S(1)} collective-permute-done((f32[64,512]{1,0:T(8,128)S(1)}, f32[64,512]{1,0:T(8,128)S(1)}, u32[]{:S(2)}, u32[]{:S(2)}) %collective-permute-start.8) | collective-permute-done | bytes 131104 | tf_op jit(solution)/shard_map/ppermute | solution.py:58
  68.2 1.4 %collective-permute-done.11 = f32[64,512]{1,0:T(8,128)S(1)} collective-permute-done((f32[64,512]{1,0:T(8,128)S(1)}, f32[64,512]{1,0:T(8,128)S(1)}, u32[]{:S(2)}, u32[]{:S(2)}) %collective-permute-start.11) | collective-permute-done | bytes 131104 | tf_op jit(solution)/shard_map/ppermute | solution.py:58
  70.4 1.5 %collective-permute-start.12 = (f32[]{:T(128)}, f32[]{:T(128)}, u32[]{:S(2)}, u32[]{:S(2)}) collective-permute-start(f32[]{:T(128)} %multiply_reduce_fusion), channel_id=1, source_target_pairs={{0,1},{1,0},{2,3},{3,2},{4,5},{5,4},{6,7},{7,6},{8,9},{9,8},{10,11... | collective-permute-start | bytes 20 | tf_op jit(solution)/shard_map/ppermute | solution.py:33
  71.9 2.2 %collective-permute-done.12 = f32[]{:T(128)} collective-permute-done((f32[]{:T(128)}, f32[]{:T(128)}, u32[]{:S(2)}, u32[]{:S(2)}) %collective-permute-start.12) | collective-permute-done | bytes 36 | tf_op jit(solution)/shard_map/ppermute | solution.py:33
  77.3 1.4 %collective-permute-start.14 = (f32[]{:T(128)}, f32[]{:T(128)}, u32[]{:S(2)}, u32[]{:S(2)}) collective-permute-start(f32[]{:T(128)} %add.79), channel_id=1, source_target_pairs={{0,8},{2,10},{4,12},{6,14},{8,0},{10,2},{12,4},{14,6},{1,9},{3,11}... | collective-permute-start | bytes 20 | tf_op jit(solution)/shard_map/ppermute | solution.py:33
  78.7 3.2 %collective-permute-done.14 = f32[]{:T(128)} collective-permute-done((f32[]{:T(128)}, f32[]{:T(128)}, u32[]{:S(2)}, u32[]{:S(2)}) %collective-permute-start.14) | collective-permute-done | bytes 36 | tf_op jit(solution)/shard_map/ppermute | solution.py:33
  82.6 2.0 %collective-permute-start.15 = (f32[]{:T(128)}, f32[]{:T(128)}, u32[]{:S(2)}, u32[]{:S(2)}) collective-permute-start(f32[]{:T(128)} %add.80), channel_id=1, source_target_pairs={{0,4},{2,6},{4,0},{6,2},{8,12},{10,14},{12,8},{14,10},{1,5},{3,7},... | collective-permute-start | bytes 20 | tf_op jit(solution)/shard_map/ppermute | solution.py:33
  84.6 1.7 %collective-permute-done.15 = f32[]{:T(128)} collective-permute-done((f32[]{:T(128)}, f32[]{:T(128)}, u32[]{:S(2)}, u32[]{:S(2)}) %collective-permute-start.15) | collective-permute-done | bytes 36 | tf_op jit(solution)/shard_map/ppermute | solution.py:33
  86.9 2.7 %collective-permute-start.16 = (f32[]{:T(128)}, f32[]{:T(128)}, u32[]{:S(2)}, u32[]{:S(2)}) collective-permute-start(f32[]{:T(128)} %add.81), channel_id=1, source_target_pairs={{0,2},{2,0},{4,6},{6,4},{8,10},{10,8},{12,14},{14,12},{1,3},{3,1},... | collective-permute-start | bytes 20 | tf_op jit(solution)/shard_map/ppermute | solution.py:33
  91.8 1.6 %collective-permute-start.17 = (bf16[512,128]{0,1:T(8,128)(2,1)S(1)}, bf16[512,128]{0,1:T(8,128)(2,1)S(1)}, u32[]{:S(2)}, u32[]{:S(2)}) collective-permute-start(bf16[512,128]{0,1:T(8,128)(2,1)S(1)} %get-tuple-element.55), channel_id=1, source_target_pairs={{0,8},{2,10},{4,12},{6,14},{8,0},{10,2},{12,4},{14,6},{1,9},{3,11}... | collective-permute-start | bytes 393224 | tf_op jit(solution)/shard_map/ppermute | solution.py:72
  93.9 5.7 %collective-permute-done.17 = bf16[512,128]{0,1:T(8,128)(2,1)S(1)} collective-permute-done((bf16[512,128]{0,1:T(8,128)(2,1)S(1)}, bf16[512,128]{0,1:T(8,128)(2,1)S(1)}, u32[]{:S(2)}, u32[]{:S(2)}) %collective-permute-start.17) | collective-permute-done | bytes 131104 | tf_op jit(solution)/shard_map/ppermute | solution.py:72
  100.5 2.7 %collective-permute-start.21 = (bf16[2,512,128]{1,2,0:T(8,128)(2,1)S(1)}, bf16[2,512,128]{1,2,0:T(8,128)(2,1)S(1)}, u32[]{:S(2)}, u32[]{:S(2)}) collective-permute-start(bf16[2,512,128]{1,2,0:T(8,128)(2,1)S(1)} %pad_maximum_fusion.17), channel_id=1, source_target_pairs={{0,8},{2,10},{4,12},{6,14},{8,0},{10,2},{12,4},{14,6},{1,9},{3,11}... | collective-permute-start | bytes 786440 | tf_op jit(solution)/shard_map/ppermute | solution.py:72
  103.2 6.8 %collective-permute-done.18 = bf16[2,512,128]{1,2,0:T(8,128)(2,1)S(1)} collective-permute-done((bf16[2,512,128]{1,2,0:T(8,128)(2,1)S(1)}, bf16[2,512,128]{1,2,0:T(8,128)(2,1)S(1)}, u32[]{:S(2)}, u32[]{:S(2)}) %collective-permute-start.18) | collective-permute-done | bytes 262176 | tf_op jit(solution)/shard_map/ppermute | solution.py:72
  110.1 2.3 %collective-permute-start.19 = (bf16[2,2,512,128]{2,3,1,0:T(8,128)(2,1)S(1)}, bf16[2,2,512,128]{2,3,1,0:T(8,128)(2,1)S(1)}, u32[]{:S(2)}, u32[]{:S(2)}) collective-permute-start(bf16[2,2,512,128]{2,3,1,0:T(8,128)(2,1)S(1)} %pad_maximum_fusion.8), channel_id=1, source_target_pairs={{0,2},{2,0},{4,6},{6,4},{8,10},{10,8},{12,14},{14,12},{1,3},{3,1},... | collective-permute-start | bytes 1572872 | tf_op jit(solution)/shard_map/ppermute | solution.py:72
  113.3 6.3 %collective-permute-done.19 = bf16[2,2,512,128]{2,3,1,0:T(8,128)(2,1)S(1)} collective-permute-done((bf16[2,2,512,128]{2,3,1,0:T(8,128)(2,1)S(1)}, bf16[2,2,512,128]{2,3,1,0:T(8,128)(2,1)S(1)}, u32[]{:S(2)}, u32[]{:S(2)}) %collective-permute-start.19) | collective-permute-done | bytes 524320 | tf_op jit(solution)/shard_map/ppermute | solution.py:72
  120.4 2.3 %collective-permute-done.22 = bf16[2,2,512,128]{2,3,1,0:T(8,128)(2,1)S(1)} collective-permute-done((bf16[2,2,512,128]{2,3,1,0:T(8,128)(2,1)}, bf16[2,2,512,128]{2,3,1,0:T(8,128)(2,1)S(1)}, u32[]{:S(2)}, u32[]{:S(2)}) %collective-permute-start.22) | collective-permute-done | bytes 524320 | tf_op jit(solution)/shard_map/ppermute | solution.py:72
  123.5 1.5 %maximum_bitcast_fusion = bf16[1,4096,256]{2,1,0:T(8,128)(2,1)} fusion(bf16[4096,128]{1,0:T(8,128)(2,1)S(1)} %bitcast.75, bf16[4096,128]{1,0:T(8,128)(2,1)S(1)} %bitcast.74), kind=kLoop, calls=%fused_computation.3 | loop fusion | flops 4194304 | bytes 4194304 | tf_op jit(solution)/shard_map/broadcast_in_dim | solution.py:132
  (108 shorter events, 22.5 us)
Async XLA Ops:
  9.1 11.8 %copy-start.12 = (f32[64,512]{1,0:T(8,128)}, f32[64,512]{1,0:T(8,128)S(1)}, u32[]{:S(2)}) copy-start(f32[64,512]{1,0:T(8,128)S(1)} %get-tuple-element.5) | copy-start | bytes 393220
  9.1 11.8 %copy-start.13 = (f32[64,512]{1,0:T(8,128)}, f32[64,512]{1,0:T(8,128)S(1)}, u32[]{:S(2)}) copy-start(f32[64,512]{1,0:T(8,128)S(1)} %get-tuple-element.14) | copy-start | bytes 393220
  9.1 11.8 %copy-start.14 = (f32[64,512]{1,0:T(8,128)}, f32[64,512]{1,0:T(8,128)S(1)}, u32[]{:S(2)}) copy-start(f32[64,512]{1,0:T(8,128)S(1)} %get-tuple-element.15) | copy-start | bytes 393220
  10.2 16.0 %collective-permute-start = (f32[64,2048]{1,0:T(8,128)}, f32[64,2048]{1,0:T(8,128)}, u32[]{:S(2)}, u32[]{:S(2)}) collective-permute-start(f32[64,2048]{1,0:T(8,128)} %fusion.19), channel_id=1, source_target_pairs={{0,2},{2,0},{4,6},{6,4},{8,10},{10,8},{12,14},{14,12},{1,3},{3,1},... | collective-permute-start | bytes 1572872 | tf_op jit(solution)/shard_map/ppermute | solution.py:58
  15.7 20.8 %collective-permute-start.3 = (f32[64,2048]{1,0:T(8,128)}, f32[64,2048]{1,0:T(8,128)}, u32[]{:S(2)}, u32[]{:S(2)}) collective-permute-start(f32[64,2048]{1,0:T(8,128)} %fusion.17), channel_id=1, source_target_pairs={{0,4},{2,6},{4,0},{6,2},{8,12},{10,14},{12,8},{14,10},{1,5},{3,7},... | collective-permute-start | bytes 1572872 | tf_op jit(solution)/shard_map/ppermute | solution.py:58
  18.2 19.6 %collective-permute-start.6 = (f32[64,2048]{1,0:T(8,128)}, f32[64,2048]{1,0:T(8,128)}, u32[]{:S(2)}, u32[]{:S(2)}) collective-permute-start(f32[64,2048]{1,0:T(8,128)} %fusion.18), channel_id=1, source_target_pairs={{0,2},{2,0},{4,6},{6,4},{8,10},{10,8},{12,14},{14,12},{1,3},{3,1},... | collective-permute-start | bytes 1572872 | tf_op jit(solution)/shard_map/ppermute | solution.py:58
  19.6 28.1 %collective-permute-start.9 = (f32[64,2048]{1,0:T(8,128)}, f32[64,2048]{1,0:T(8,128)}, u32[]{:S(2)}, u32[]{:S(2)}) collective-permute-start(f32[64,2048]{1,0:T(8,128)} %fusion.16), channel_id=1, source_target_pairs={{0,4},{2,6},{4,0},{6,2},{8,12},{10,14},{12,8},{14,10},{1,5},{3,7},... | collective-permute-start | bytes 1572872 | tf_op jit(solution)/shard_map/ppermute | solution.py:58
  25.5 12.3 %copy-start.3 = (f32[64,512]{1,0:T(8,128)S(1)}, f32[64,512]{1,0:T(8,128)}, u32[]{:S(2)}) copy-start(f32[64,512]{1,0:T(8,128)} %copy-done.2) | copy-start | bytes 393220
  25.5 12.3 %copy-start.5 = (f32[64,512]{1,0:T(8,128)S(1)}, f32[64,512]{1,0:T(8,128)}, u32[]{:S(2)}) copy-start(f32[64,512]{1,0:T(8,128)} %copy-done.4) | copy-start | bytes 393220
  25.5 12.3 %copy-start.7 = (f32[64,512]{1,0:T(8,128)S(1)}, f32[64,512]{1,0:T(8,128)}, u32[]{:S(2)}) copy-start(f32[64,512]{1,0:T(8,128)} %copy-done.6) | copy-start | bytes 393220
  25.5 12.3 %copy-start.9 = (f32[64,512]{1,0:T(8,128)S(1)}, f32[64,512]{1,0:T(8,128)}, u32[]{:S(2)}) copy-start(f32[64,512]{1,0:T(8,128)} %copy-done.8) | copy-start | bytes 393220
  25.5 12.3 %copy-start.11 = (f32[64,512]{1,0:T(8,128)S(1)}, f32[64,512]{1,0:T(8,128)}, u32[]{:S(2)}) copy-start(f32[64,512]{1,0:T(8,128)} %copy-done.10) | copy-start | bytes 393220
  27.7 21.4 %collective-permute-start.1 = (f32[64,1024]{1,0:T(8,128)S(1)}, f32[64,1024]{1,0:T(8,128)S(1)}, u32[]{:S(2)}, u32[]{:S(2)}) collective-permute-start(f32[64,1024]{1,0:T(8,128)S(1)} %slice_select_fusion), channel_id=1, source_target_pairs={{0,8},{2,10},{4,12},{6,14},{8,0},{10,2},{12,4},{14,6},{1,9},{3,11}... | collective-permute-start | bytes 786440 | tf_op jit(solution)/shard_map/ppermute | solution.py:58
  37.7 12.7 %collective-permute-start.4 = (f32[64,1024]{1,0:T(8,128)S(1)}, f32[64,1024]{1,0:T(8,128)S(1)}, u32[]{:S(2)}, u32[]{:S(2)}) collective-permute-start(f32[64,1024]{1,0:T(8,128)S(1)} %fusion.24), channel_id=1, source_target_pairs={{0,2},{2,0},{4,6},{6,4},{8,10},{10,8},{12,14},{14,12},{1,3},{3,1},... | collective-permute-start | bytes 786440 | tf_op jit(solution)/shard_map/ppermute | solution.py:58
  39.1 17.0 %collective-permute-start.7 = (f32[64,1024]{1,0:T(8,128)S(1)}, f32[64,1024]{1,0:T(8,128)S(1)}, u32[]{:S(2)}, u32[]{:S(2)}) collective-permute-start(f32[64,1024]{1,0:T(8,128)S(1)} %fusion.23), channel_id=1, source_target_pairs={{0,4},{2,6},{4,0},{6,2},{8,12},{10,14},{12,8},{14,10},{1,5},{3,7},... | collective-permute-start | bytes 786440 | tf_op jit(solution)/shard_map/ppermute | solution.py:58
  48.9 42.4 %copy-start.1 = (f32[1,512,256]{1,2,0:T(8,128)S(1)}, f32[1,512,256]{1,2,0:T(8,128)}, u32[]{:S(2)}) copy-start(f32[1,512,256]{1,2,0:T(8,128)} %copy.14) | copy-start | bytes 1572868
  49.0 7.6 %collective-permute-start.10 = (f32[64,1024]{1,0:T(8,128)S(1)}, f32[64,1024]{1,0:T(8,128)S(1)}, u32[]{:S(2)}, u32[]{:S(2)}) collective-permute-start(f32[64,1024]{1,0:T(8,128)S(1)} %fusion.22), channel_id=1, source_target_pairs={{0,2},{2,0},{4,6},{6,4},{8,10},{10,8},{12,14},{14,12},{1,3},{3,1},... | collective-permute-start | bytes 786440 | tf_op jit(solution)/shard_map/ppermute | solution.py:58
  49.1 10.2 %collective-permute-start.2 = (f32[64,512]{1,0:T(8,128)S(1)}, f32[64,512]{1,0:T(8,128)S(1)}, u32[]{:S(2)}, u32[]{:S(2)}) collective-permute-start(f32[64,512]{1,0:T(8,128)S(1)} %slice_select_fusion.4), channel_id=1, source_target_pairs={{0,4},{2,6},{4,0},{6,2},{8,12},{10,14},{12,8},{14,10},{1,5},{3,7},... | collective-permute-start | bytes 393224 | tf_op jit(solution)/shard_map/ppermute | solution.py:58
  50.4 16.0 %collective-permute-start.5 = (f32[64,512]{1,0:T(8,128)S(1)}, f32[64,512]{1,0:T(8,128)S(1)}, u32[]{:S(2)}, u32[]{:S(2)}) collective-permute-start(f32[64,512]{1,0:T(8,128)S(1)} %slice_select_fusion.3), channel_id=1, source_target_pairs={{0,8},{2,10},{4,12},{6,14},{8,0},{10,2},{12,4},{14,6},{1,9},{3,11}... | collective-permute-start | bytes 393224 | tf_op jit(solution)/shard_map/ppermute | solution.py:58
  56.2 11.9 %collective-permute-start.8 = (f32[64,512]{1,0:T(8,128)S(1)}, f32[64,512]{1,0:T(8,128)S(1)}, u32[]{:S(2)}, u32[]{:S(2)}) collective-permute-start(f32[64,512]{1,0:T(8,128)S(1)} %slice_select_fusion.2), channel_id=1, source_target_pairs={{0,8},{2,10},{4,12},{6,14},{8,0},{10,2},{12,4},{14,6},{1,9},{3,11}... | collective-permute-start | bytes 393224 | tf_op jit(solution)/shard_map/ppermute | solution.py:58
  56.6 12.9 %collective-permute-start.11 = (f32[64,512]{1,0:T(8,128)S(1)}, f32[64,512]{1,0:T(8,128)S(1)}, u32[]{:S(2)}, u32[]{:S(2)}) collective-permute-start(f32[64,512]{1,0:T(8,128)S(1)} %slice_select_fusion.1), channel_id=1, source_target_pairs={{0,8},{2,10},{4,12},{6,14},{8,0},{10,2},{12,4},{14,6},{1,9},{3,11}... | collective-permute-start | bytes 393224 | tf_op jit(solution)/shard_map/ppermute | solution.py:58
  70.4 3.7 %collective-permute-start.12 = (f32[]{:T(128)}, f32[]{:T(128)}, u32[]{:S(2)}, u32[]{:S(2)}) collective-permute-start(f32[]{:T(128)} %multiply_reduce_fusion), channel_id=1, source_target_pairs={{0,1},{1,0},{2,3},{3,2},{4,5},{5,4},{6,7},{7,6},{8,9},{9,8},{10,11... | collective-permute-start | bytes 20 | tf_op jit(solution)/shard_map/ppermute | solution.py:33
  75.4 1.3 %collective-permute-start.13 = (f32[]{:T(128)}, f32[]{:T(128)}, u32[]{:S(2)}, u32[]{:S(2)}) collective-permute-start(f32[]{:T(128)} %add.78), channel_id=1, source_target_pairs={{0,16},{16,0},{1,17},{17,1},{2,18},{18,2},{3,19},{19,3},{4,20},{20... | collective-permute-start | bytes 20 | tf_op jit(solution)/shard_map/ppermute | solution.py:33
  77.3 4.6 %collective-permute-start.14 = (f32[]{:T(128)}, f32[]{:T(128)}, u32[]{:S(2)}, u32[]{:S(2)}) collective-permute-start(f32[]{:T(128)} %add.79), channel_id=1, source_target_pairs={{0,8},{2,10},{4,12},{6,14},{8,0},{10,2},{12,4},{14,6},{1,9},{3,11}... | collective-permute-start | bytes 20 | tf_op jit(solution)/shard_map/ppermute | solution.py:33
  82.6 3.7 %collective-permute-start.15 = (f32[]{:T(128)}, f32[]{:T(128)}, u32[]{:S(2)}, u32[]{:S(2)}) collective-permute-start(f32[]{:T(128)} %add.80), channel_id=1, source_target_pairs={{0,4},{2,6},{4,0},{6,2},{8,12},{10,14},{12,8},{14,10},{1,5},{3,7},... | collective-permute-start | bytes 20 | tf_op jit(solution)/shard_map/ppermute | solution.py:33
  86.9 3.7 %collective-permute-start.16 = (f32[]{:T(128)}, f32[]{:T(128)}, u32[]{:S(2)}, u32[]{:S(2)}) collective-permute-start(f32[]{:T(128)} %add.81), channel_id=1, source_target_pairs={{0,2},{2,0},{4,6},{6,4},{8,10},{10,8},{12,14},{14,12},{1,3},{3,1},... | collective-permute-start | bytes 20 | tf_op jit(solution)/shard_map/ppermute | solution.py:33
  91.8 7.8 %collective-permute-start.17 = (bf16[512,128]{0,1:T(8,128)(2,1)S(1)}, bf16[512,128]{0,1:T(8,128)(2,1)S(1)}, u32[]{:S(2)}, u32[]{:S(2)}) collective-permute-start(bf16[512,128]{0,1:T(8,128)(2,1)S(1)} %get-tuple-element.55), channel_id=1, source_target_pairs={{0,8},{2,10},{4,12},{6,14},{8,0},{10,2},{12,4},{14,6},{1,9},{3,11}... | collective-permute-start | bytes 393224 | tf_op jit(solution)/shard_map/ppermute | solution.py:72
  93.4 6.2 %collective-permute-start.20 = (bf16[512,128]{0,1:T(8,128)(2,1)S(1)}, bf16[512,128]{0,1:T(8,128)(2,1)S(1)}, u32[]{:S(2)}, u32[]{:S(2)}) collective-permute-start(bf16[512,128]{0,1:T(8,128)(2,1)S(1)} %get-tuple-element.56), channel_id=1, source_target_pairs={{0,2},{2,0},{4,6},{6,4},{8,10},{10,8},{12,14},{14,12},{1,3},{3,1},... | collective-permute-start | bytes 393224 | tf_op jit(solution)/shard_map/ppermute | solution.py:72
  99.7 10.4 %collective-permute-start.18 = (bf16[2,512,128]{1,2,0:T(8,128)(2,1)S(1)}, bf16[2,512,128]{1,2,0:T(8,128)(2,1)S(1)}, u32[]{:S(2)}, u32[]{:S(2)}) collective-permute-start(bf16[2,512,128]{1,2,0:T(8,128)(2,1)S(1)} %pad_maximum_fusion.16), channel_id=1, source_target_pairs={{0,4},{2,6},{4,0},{6,2},{8,12},{10,14},{12,8},{14,10},{1,5},{3,7},... | collective-permute-start | bytes 786440 | tf_op jit(solution)/shard_map/ppermute | solution.py:72
  100.5 11.9 %collective-permute-start.21 = (bf16[2,512,128]{1,2,0:T(8,128)(2,1)S(1)}, bf16[2,512,128]{1,2,0:T(8,128)(2,1)S(1)}, u32[]{:S(2)}, u32[]{:S(2)}) collective-permute-start(bf16[2,512,128]{1,2,0:T(8,128)(2,1)S(1)} %pad_maximum_fusion.17), channel_id=1, source_target_pairs={{0,8},{2,10},{4,12},{6,14},{8,0},{10,2},{12,4},{14,6},{1,9},{3,11}... | collective-permute-start | bytes 786440 | tf_op jit(solution)/shard_map/ppermute | solution.py:72
  110.1 9.4 %collective-permute-start.19 = (bf16[2,2,512,128]{2,3,1,0:T(8,128)(2,1)S(1)}, bf16[2,2,512,128]{2,3,1,0:T(8,128)(2,1)S(1)}, u32[]{:S(2)}, u32[]{:S(2)}) collective-permute-start(bf16[2,2,512,128]{2,3,1,0:T(8,128)(2,1)S(1)} %pad_maximum_fusion.8), channel_id=1, source_target_pairs={{0,2},{2,0},{4,6},{6,4},{8,10},{10,8},{12,14},{14,12},{1,3},{3,1},... | collective-permute-start | bytes 1572872 | tf_op jit(solution)/shard_map/ppermute | solution.py:72
  113.3 9.4 %collective-permute-start.22 = (bf16[2,2,512,128]{2,3,1,0:T(8,128)(2,1)}, bf16[2,2,512,128]{2,3,1,0:T(8,128)(2,1)S(1)}, u32[]{:S(2)}, u32[]{:S(2)}) collective-permute-start(bf16[2,2,512,128]{2,3,1,0:T(8,128)(2,1)} %pad_maximum_fusion.9), channel_id=1, source_target_pairs={{0,4},{2,6},{4,0},{6,2},{8,12},{10,14},{12,8},{14,10},{1,5},{3,7},... | collective-permute-start | bytes 1572872 | tf_op jit(solution)/shard_map/ppermute | solution.py:72
  (12 other events, 74.4 us)

commit v24 on v23

--- a/solution.py
+++ b/solution.py
@@ -88,7 +88,7 @@
     width = cols // parts
     return jnp.concatenate(
         [
-            halving_scatter(partial_t[k * width:(k + 1) * width], axis, orders[(2, 1, 0, 1)[k % 4]])
+            halving_scatter(partial_t[k * width:(k + 1) * width], axis, orders[(2, 0, 1, 1)[k % 4]])
             for k in range(parts)
         ],
         axis=0,

time: 126 us -> 128 us (1.016)
  starting transfers between devices: 34.8 us -> 38.5 us
    ppermute x12, starting transfers between devices: 18.2 us -> 20.1 us  [halving_scatter(): blocks = keep + lax.ppermute(send, axis, pairs)]
    ppermute x12, waiting for transfers between devices: 25.3 us -> 26.9 us  [halving_scatter(): blocks = keep + lax.ppermute(send, axis, pairs)]
    unnamed x45 -> x37, local copies, waits for them, and re-layouts: 6.55 us -> 5.5 us
  transfers between devices with their start and end apart: 23 -> 23, of which waited for: 16 -> 17; matrix products, arithmetic and copies ran while one was open for 13% -> 12% of each run, Pallas kernels for 0% -> 0%
where the time goes in v24:
time: 128 us; the launch traced here: 127 us
  waiting for transfers between devices  53.9 us (42%)
  starting transfers between devices  38.5 us (30%)
  other arithmetic  14.5 us (11%)
  local copies, waits for them, and re-layouts  8.81 us (7%)
  matrix products  6.18 us (5%)
  between operations  5.14 us (4%)
    ppermute x12, waiting for transfers between devices, halving_scatter(): blocks = keep + lax.ppermute(send, axis, pairs)  26.9 us
    ppermute x12, starting transfers between devices, halving_scatter(): blocks = keep + lax.ppermute(send, axis, pairs)  20.1 us
    ppermute x6, waiting for transfers between devices, doubling_gather(): other = lax.ppermute(current, axis, pairs)  19.9 us
    ppermute x5, starting transfers between devices, butterfly_sum(): value = value + lax.ppermute(value, axis, pairs)  9.26 us
    ppermute x6, starting transfers between devices, doubling_gather(): other = lax.ppermute(current, axis, pairs)  9.15 us
    ppermute x5, waiting for transfers between devices, butterfly_sum(): value = value + lax.ppermute(value, axis, pairs)  7.17 us
    dot_general x1, matrix products, slot_term(): lax.dot_general(weighted, columns, (((0,), (0,)), ((), ())), preferred_el...  6.18 us
    unnamed x37, local copies, waits for them, and re-layouts  5.5 us
  transfers between devices with their start and end apart: 23, of which 17 were waited for; matrix products, arithmetic and copies ran while one was open for 12% of the time, Pallas kernels for 0%

profile of v24, /device:TPU:0, one launch (start us, length us, event | category | flops | bytes accessed | tf_op | source)
XLA Modules:
  0.0 127.1 jit_solution(9013192465995196121)
XLA Ops:
  0.7 6.2 %fusion.2 = f32[256,4096]{1,0:T(8,128)S(1)} fusion(bf16[1,8,128,4096]{3,2,1,0:T(8,128)(2,1)} %param.6, bf16[1,8,128,256]{3,2,1,0:T(8,128)(2,1)} %param.7, pred[8]{0:T(512)(128)(4,1)S(1)} %compare_bitcast_fusion), kind=kOutput, calls=%fused_computation.2 | convolution fusion | flops 2147745792 | bytes 13107208 | tf_op jit(solution)/shard_map/dot_general | solution.py:19
  6.9 2.0 %copy-done = f32[256,4096]{1,0:T(8,128)} copy-done((f32[256,4096]{1,0:T(8,128)}, f32[256,4096]{1,0:T(8,128)S(1)}, u32[]{:S(2)}) %copy-start) | copy-done | bytes 4194328
  10.2 2.9 %collective-permute-start = (f32[64,2048]{1,0:T(8,128)}, f32[64,2048]{1,0:T(8,128)}, u32[]{:S(2)}, u32[]{:S(2)}) collective-permute-start(f32[64,2048]{1,0:T(8,128)} %fusion.19), channel_id=1, source_target_pairs={{0,2},{2,0},{4,6},{6,4},{8,10},{10,8},{12,14},{14,12},{1,3},{3,1},... | collective-permute-start | bytes 1572872 | tf_op jit(solution)/shard_map/ppermute | solution.py:58
  14.2 1.6 %fusion.27 = (f32[64,1024]{1,0:T(8,128)S(1)}, f32[64,1024]{1,0:T(8,128)S(1)}, f32[64,1024]{1,0:T(8,128)S(1)}, f32[64,1024]{1,0:T(8,128)S(1)}, f32[64,1024]{1,0:T...) fusion(f32[256,4096]{1,0:T(8,128)} %copy-done), kind=kLoop, calls=%fused_computation.80 | loop fusion | bytes 4194304 | tf_op jit(solution)/shard_map/slice | solution.py:54
  16.7 2.1 %collective-permute-start.6 = (f32[64,2048]{1,0:T(8,128)}, f32[64,2048]{1,0:T(8,128)}, u32[]{:S(2)}, u32[]{:S(2)}) collective-permute-start(f32[64,2048]{1,0:T(8,128)} %fusion.17), channel_id=1, source_target_pairs={{0,4},{2,6},{4,0},{6,2},{8,12},{10,14},{12,8},{14,10},{1,5},{3,7},... | collective-permute-start | bytes 1572872 | tf_op jit(solution)/shard_map/ppermute | solution.py:58
  22.4 2.0 %copy.14 = f32[1,512,256]{1,2,0:T(8,128)} copy(f32[1,512,256]{2,1,0:T(8,128)} %param.9) | data formatting | bytes 1048576 | tf_op args[3]
  24.5 1.7 %collective-permute-done = f32[64,2048]{1,0:T(8,128)} collective-permute-done((f32[64,2048]{1,0:T(8,128)}, f32[64,2048]{1,0:T(8,128)}, u32[]{:S(2)}, u32[]{:S(2)}) %collective-permute-start) | collective-permute-done | bytes 524320 | tf_op jit(solution)/shard_map/ppermute | solution.py:58
  27.7 3.2 %collective-permute-start.1 = (f32[64,1024]{1,0:T(8,128)S(1)}, f32[64,1024]{1,0:T(8,128)S(1)}, u32[]{:S(2)}, u32[]{:S(2)}) collective-permute-start(f32[64,1024]{1,0:T(8,128)S(1)} %slice_select_fusion), channel_id=1, source_target_pairs={{0,8},{2,10},{4,12},{6,14},{8,0},{10,2},{12,4},{14,6},{1,9},{3,11}... | collective-permute-start | bytes 786440 | tf_op jit(solution)/shard_map/ppermute | solution.py:58
  30.9 5.7 %collective-permute-done.3 = f32[64,2048]{1,0:T(8,128)} collective-permute-done((f32[64,2048]{1,0:T(8,128)}, f32[64,2048]{1,0:T(8,128)}, u32[]{:S(2)}, u32[]{:S(2)}) %collective-permute-start.3) | collective-permute-done | bytes 524320 | tf_op jit(solution)/shard_map/ppermute | solution.py:58
  38.0 1.9 %collective-permute-start.4 = (f32[64,1024]{1,0:T(8,128)S(1)}, f32[64,1024]{1,0:T(8,128)S(1)}, u32[]{:S(2)}, u32[]{:S(2)}) collective-permute-start(f32[64,1024]{1,0:T(8,128)S(1)} %fusion.24), channel_id=1, source_target_pairs={{0,4},{2,6},{4,0},{6,2},{8,12},{10,14},{12,8},{14,10},{1,5},{3,7},... | collective-permute-start | bytes 786440 | tf_op jit(solution)/shard_map/ppermute | solution.py:58
  41.1 1.6 %collective-permute-start.7 = (f32[64,1024]{1,0:T(8,128)S(1)}, f32[64,1024]{1,0:T(8,128)S(1)}, u32[]{:S(2)}, u32[]{:S(2)}) collective-permute-start(f32[64,1024]{1,0:T(8,128)S(1)} %fusion.23), channel_id=1, source_target_pairs={{0,2},{2,0},{4,6},{6,4},{8,10},{10,8},{12,14},{14,12},{1,3},{3,1},... | collective-permute-start | bytes 786440 | tf_op jit(solution)/shard_map/ppermute | solution.py:58
  42.7 6.2 %collective-permute-done.9 = f32[64,2048]{1,0:T(8,128)} collective-permute-done((f32[64,2048]{1,0:T(8,128)}, f32[64,2048]{1,0:T(8,128)}, u32[]{:S(2)}, u32[]{:S(2)}) %collective-permute-start.9) | collective-permute-done | bytes 524320 | tf_op jit(solution)/shard_map/ppermute | solution.py:58
  50.1 2.0 %collective-permute-start.10 = (f32[64,1024]{1,0:T(8,128)S(1)}, f32[64,1024]{1,0:T(8,128)S(1)}, u32[]{:S(2)}, u32[]{:S(2)}) collective-permute-start(f32[64,1024]{1,0:T(8,128)S(1)} %fusion.22), channel_id=1, source_target_pairs={{0,2},{2,0},{4,6},{6,4},{8,10},{10,8},{12,14},{14,12},{1,3},{3,1},... | collective-permute-start | bytes 786440 | tf_op jit(solution)/shard_map/ppermute | solution.py:58
  52.2 2.1 %collective-permute-done.4 = f32[64,1024]{1,0:T(8,128)S(1)} collective-permute-done((f32[64,1024]{1,0:T(8,128)S(1)}, f32[64,1024]{1,0:T(8,128)S(1)}, u32[]{:S(2)}, u32[]{:S(2)}) %collective-permute-start.4) | collective-permute-done | bytes 262176 | tf_op jit(solution)/shard_map/ppermute | solution.py:58
  54.4 3.2 %collective-permute-start.5 = (f32[64,512]{1,0:T(8,128)S(1)}, f32[64,512]{1,0:T(8,128)S(1)}, u32[]{:S(2)}, u32[]{:S(2)}) collective-permute-start(f32[64,512]{1,0:T(8,128)S(1)} %slice_select_fusion.3), channel_id=1, source_target_pairs={{0,8},{2,10},{4,12},{6,14},{8,0},{10,2},{12,4},{14,6},{1,9},{3,11}... | collective-permute-start | bytes 393224 | tf_op jit(solution)/shard_map/ppermute | solution.py:58
  57.8 3.0 %collective-permute-start.11 = (f32[64,512]{1,0:T(8,128)S(1)}, f32[64,512]{1,0:T(8,128)S(1)}, u32[]{:S(2)}, u32[]{:S(2)}) collective-permute-start(f32[64,512]{1,0:T(8,128)S(1)} %slice_select_fusion.1), channel_id=1, source_target_pairs={{0,8},{2,10},{4,12},{6,14},{8,0},{10,2},{12,4},{14,6},{1,9},{3,11}... | collective-permute-start | bytes 393224 | tf_op jit(solution)/shard_map/ppermute | solution.py:58
  60.8 7.9 %collective-permute-done.5 = f32[64,512]{1,0:T(8,128)S(1)} collective-permute-done((f32[64,512]{1,0:T(8,128)S(1)}, f32[64,512]{1,0:T(8,128)S(1)}, u32[]{:S(2)}, u32[]{:S(2)}) %collective-permute-start.5) | collective-permute-done | bytes 131104 | tf_op jit(solution)/shard_map/ppermute | solution.py:58
  68.7 1.9 %collective-permute-done.8 = f32[64,512]{1,0:T(8,128)S(1)} collective-permute-done((f32[64,512]{1,0:T(8,128)S(1)}, f32[64,512]{1,0:T(8,128)S(1)}, u32[]{:S(2)}, u32[]{:S(2)}) %collective-permute-start.8) | collective-permute-done | bytes 131104 | tf_op jit(solution)/shard_map/ppermute | solution.py:58
  74.2 2.2 %collective-permute-done.12 = f32[]{:T(128)} collective-permute-done((f32[]{:T(128)}, f32[]{:T(128)}, u32[]{:S(2)}, u32[]{:S(2)}) %collective-permute-start.12) | collective-permute-done | bytes 36 | tf_op jit(solution)/shard_map/ppermute | solution.py:33
  80.9 3.1 %collective-permute-done.14 = f32[]{:T(128)} collective-permute-done((f32[]{:T(128)}, f32[]{:T(128)}, u32[]{:S(2)}, u32[]{:S(2)}) %collective-permute-start.14) | collective-permute-done | bytes 36 | tf_op jit(solution)/shard_map/ppermute | solution.py:33
  84.7 2.5 %collective-permute-start.15 = (f32[]{:T(128)}, f32[]{:T(128)}, u32[]{:S(2)}, u32[]{:S(2)}) collective-permute-start(f32[]{:T(128)} %add.80), channel_id=1, source_target_pairs={{0,4},{2,6},{4,0},{6,2},{8,12},{10,14},{12,8},{14,10},{1,5},{3,7},... | collective-permute-start | bytes 20 | tf_op jit(solution)/shard_map/ppermute | solution.py:33
  88.9 3.1 %collective-permute-start.16 = (f32[]{:T(128)}, f32[]{:T(128)}, u32[]{:S(2)}, u32[]{:S(2)}) collective-permute-start(f32[]{:T(128)} %add.81), channel_id=1, source_target_pairs={{0,2},{2,0},{4,6},{6,4},{8,10},{10,8},{12,14},{14,12},{1,3},{3,1},... | collective-permute-start | bytes 20 | tf_op jit(solution)/shard_map/ppermute | solution.py:33
  93.7 2.1 %collective-permute-start.17 = (bf16[512,128]{0,1:T(8,128)(2,1)S(1)}, bf16[512,128]{0,1:T(8,128)(2,1)S(1)}, u32[]{:S(2)}, u32[]{:S(2)}) collective-permute-start(bf16[512,128]{0,1:T(8,128)(2,1)S(1)} %get-tuple-element.55), channel_id=1, source_target_pairs={{0,8},{2,10},{4,12},{6,14},{8,0},{10,2},{12,4},{14,6},{1,9},{3,11}... | collective-permute-start | bytes 393224 | tf_op jit(solution)/shard_map/ppermute | solution.py:72
  95.7 1.5 %collective-permute-start.20 = (bf16[512,128]{0,1:T(8,128)(2,1)S(1)}, bf16[512,128]{0,1:T(8,128)(2,1)S(1)}, u32[]{:S(2)}, u32[]{:S(2)}) collective-permute-start(bf16[512,128]{0,1:T(8,128)(2,1)S(1)} %get-tuple-element.56), channel_id=1, source_target_pairs={{0,2},{2,0},{4,6},{6,4},{8,10},{10,8},{12,14},{14,12},{1,3},{3,1},... | collective-permute-start | bytes 393224 | tf_op jit(solution)/shard_map/ppermute | solution.py:72
  97.2 3.9 %collective-permute-done.17 = bf16[512,128]{0,1:T(8,128)(2,1)S(1)} collective-permute-done((bf16[512,128]{0,1:T(8,128)(2,1)S(1)}, bf16[512,128]{0,1:T(8,128)(2,1)S(1)}, u32[]{:S(2)}, u32[]{:S(2)}) %collective-permute-start.17) | collective-permute-done | bytes 131104 | tf_op jit(solution)/shard_map/ppermute | solution.py:72
  101.2 1.7 %collective-permute-start.18 = (bf16[2,512,128]{1,2,0:T(8,128)(2,1)S(1)}, bf16[2,512,128]{1,2,0:T(8,128)(2,1)S(1)}, u32[]{:S(2)}, u32[]{:S(2)}) collective-permute-start(bf16[2,512,128]{1,2,0:T(8,128)(2,1)S(1)} %pad_maximum_fusion.16), channel_id=1, source_target_pairs={{0,4},{2,6},{4,0},{6,2},{8,12},{10,14},{12,8},{14,10},{1,5},{3,7},... | collective-permute-start | bytes 786440 | tf_op jit(solution)/shard_map/ppermute | solution.py:72
  102.9 1.9 %collective-permute-start.21 = (bf16[2,512,128]{1,2,0:T(8,128)(2,1)S(1)}, bf16[2,512,128]{1,2,0:T(8,128)(2,1)S(1)}, u32[]{:S(2)}, u32[]{:S(2)}) collective-permute-start(bf16[2,512,128]{1,2,0:T(8,128)(2,1)S(1)} %pad_maximum_fusion.17), channel_id=1, source_target_pairs={{0,8},{2,10},{4,12},{6,14},{8,0},{10,2},{12,4},{14,6},{1,9},{3,11}... | collective-permute-start | bytes 786440 | tf_op jit(solution)/shard_map/ppermute | solution.py:72
  104.8 6.3 %collective-permute-done.18 = bf16[2,512,128]{1,2,0:T(8,128)(2,1)S(1)} collective-permute-done((bf16[2,512,128]{1,2,0:T(8,128)(2,1)S(1)}, bf16[2,512,128]{1,2,0:T(8,128)(2,1)S(1)}, u32[]{:S(2)}, u32[]{:S(2)}) %collective-permute-start.18) | collective-permute-done | bytes 262176 | tf_op jit(solution)/shard_map/ppermute | solution.py:72
  111.2 2.0 %collective-permute-start.19 = (bf16[2,2,512,128]{2,3,1,0:T(8,128)(2,1)S(1)}, bf16[2,2,512,128]{2,3,1,0:T(8,128)(2,1)S(1)}, u32[]{:S(2)}, u32[]{:S(2)}) collective-permute-start(bf16[2,2,512,128]{2,3,1,0:T(8,128)(2,1)S(1)} %pad_maximum_fusion.8), channel_id=1, source_target_pairs={{0,2},{2,0},{4,6},{6,4},{8,10},{10,8},{12,14},{14,12},{1,3},{3,1},... | collective-permute-start | bytes 1572872 | tf_op jit(solution)/shard_map/ppermute | solution.py:72
  114.4 7.3 %collective-permute-done.19 = bf16[2,2,512,128]{2,3,1,0:T(8,128)(2,1)S(1)} collective-permute-done((bf16[2,2,512,128]{2,3,1,0:T(8,128)(2,1)S(1)}, bf16[2,2,512,128]{2,3,1,0:T(8,128)(2,1)S(1)}, u32[]{:S(2)}, u32[]{:S(2)}) %collective-permute-start.19) | collective-permute-done | bytes 524320 | tf_op jit(solution)/shard_map/ppermute | solution.py:72
  122.5 2.2 %collective-permute-done.22 = bf16[2,2,512,128]{2,3,1,0:T(8,128)(2,1)S(1)} collective-permute-done((bf16[2,2,512,128]{2,3,1,0:T(8,128)(2,1)}, bf16[2,2,512,128]{2,3,1,0:T(8,128)(2,1)S(1)}, u32[]{:S(2)}, u32[]{:S(2)}) %collective-permute-start.22) | collective-permute-done | bytes 524320 | tf_op jit(solution)/shard_map/ppermute | solution.py:72
  125.5 1.5 %maximum_bitcast_fusion = bf16[1,4096,256]{2,1,0:T(8,128)(2,1)} fusion(bf16[4096,128]{1,0:T(8,128)(2,1)S(1)} %bitcast.75, bf16[4096,128]{1,0:T(8,128)(2,1)S(1)} %bitcast.74), kind=kLoop, calls=%fused_computation.3 | loop fusion | flops 4194304 | bytes 4194304 | tf_op jit(solution)/shard_map/broadcast_in_dim | solution.py:132
  (100 shorter events, 23.6 us)
Async XLA Ops:
  9.0 5.0 %copy-start.2 = (f32[64,512]{1,0:T(8,128)}, f32[64,512]{1,0:T(8,128)S(1)}, u32[]{:S(2)}) copy-start(f32[64,512]{1,0:T(8,128)S(1)} %get-tuple-element.9) | copy-start | bytes 393220
  9.0 5.0 %copy-start.3 = (f32[64,512]{1,0:T(8,128)}, f32[64,512]{1,0:T(8,128)S(1)}, u32[]{:S(2)}) copy-start(f32[64,512]{1,0:T(8,128)S(1)} %get-tuple-element.10) | copy-start | bytes 393220
  9.0 5.0 %copy-start.4 = (f32[64,512]{1,0:T(8,128)}, f32[64,512]{1,0:T(8,128)S(1)}, u32[]{:S(2)}) copy-start(f32[64,512]{1,0:T(8,128)S(1)} %get-tuple-element.11) | copy-start | bytes 393220
  9.1 5.0 %copy-start.5 = (f32[64,512]{1,0:T(8,128)}, f32[64,512]{1,0:T(8,128)S(1)}, u32[]{:S(2)}) copy-start(f32[64,512]{1,0:T(8,128)S(1)} %get-tuple-element.12) | copy-start | bytes 393220
  9.1 5.0 %copy-start.6 = (f32[64,512]{1,0:T(8,128)}, f32[64,512]{1,0:T(8,128)S(1)}, u32[]{:S(2)}) copy-start(f32[64,512]{1,0:T(8,128)S(1)} %get-tuple-element.13) | copy-start | bytes 393220
  9.1 5.0 %copy-start.7 = (f32[64,512]{1,0:T(8,128)}, f32[64,512]{1,0:T(8,128)S(1)}, u32[]{:S(2)}) copy-start(f32[64,512]{1,0:T(8,128)S(1)} %get-tuple-element.5) | copy-start | bytes 393220
  10.2 16.0 %collective-permute-start = (f32[64,2048]{1,0:T(8,128)}, f32[64,2048]{1,0:T(8,128)}, u32[]{:S(2)}, u32[]{:S(2)}) collective-permute-start(f32[64,2048]{1,0:T(8,128)} %fusion.19), channel_id=1, source_target_pairs={{0,2},{2,0},{4,6},{6,4},{8,10},{10,8},{12,14},{14,12},{1,3},{3,1},... | collective-permute-start | bytes 1572872 | tf_op jit(solution)/shard_map/ppermute | solution.py:58
  13.1 6.5 %copy-start.16 = (s32[1,8]{1,0:T(1,128)S(1)}, s32[1,8]{1,0:T(1,128)}, u32[]{:S(2)}) copy-start(s32[1,8]{1,0:T(1,128)} %param.8) | copy-start | bytes 100
  13.1 7.8 %copy-start.15 = (f32[1,512,256]{2,1,0:T(8,128)S(1)}, f32[1,512,256]{2,1,0:T(8,128)}, u32[]{:S(2)}) copy-start(f32[1,512,256]{2,1,0:T(8,128)} %param.10) | copy-start | bytes 1572868
  14.1 22.5 %collective-permute-start.3 = (f32[64,2048]{1,0:T(8,128)}, f32[64,2048]{1,0:T(8,128)}, u32[]{:S(2)}, u32[]{:S(2)}) collective-permute-start(f32[64,2048]{1,0:T(8,128)} %fusion.18), channel_id=1, source_target_pairs={{0,2},{2,0},{4,6},{6,4},{8,10},{10,8},{12,14},{14,12},{1,3},{3,1},... | collective-permute-start | bytes 1572872 | tf_op jit(solution)/shard_map/ppermute | solution.py:58
  16.7 23.2 %collective-permute-start.6 = (f32[64,2048]{1,0:T(8,128)}, f32[64,2048]{1,0:T(8,128)}, u32[]{:S(2)}, u32[]{:S(2)}) collective-permute-start(f32[64,2048]{1,0:T(8,128)} %fusion.17), channel_id=1, source_target_pairs={{0,4},{2,6},{4,0},{6,2},{8,12},{10,14},{12,8},{14,10},{1,5},{3,7},... | collective-permute-start | bytes 1572872 | tf_op jit(solution)/shard_map/ppermute | solution.py:58
  19.7 29.1 %collective-permute-start.9 = (f32[64,2048]{1,0:T(8,128)}, f32[64,2048]{1,0:T(8,128)}, u32[]{:S(2)}, u32[]{:S(2)}) collective-permute-start(f32[64,2048]{1,0:T(8,128)} %fusion.16), channel_id=1, source_target_pairs={{0,4},{2,6},{4,0},{6,2},{8,12},{10,14},{12,8},{14,10},{1,5},{3,7},... | collective-permute-start | bytes 1572872 | tf_op jit(solution)/shard_map/ppermute | solution.py:58
  27.7 24.4 %collective-permute-start.1 = (f32[64,1024]{1,0:T(8,128)S(1)}, f32[64,1024]{1,0:T(8,128)S(1)}, u32[]{:S(2)}, u32[]{:S(2)}) collective-permute-start(f32[64,1024]{1,0:T(8,128)S(1)} %slice_select_fusion), channel_id=1, source_target_pairs={{0,8},{2,10},{4,12},{6,14},{8,0},{10,2},{12,4},{14,6},{1,9},{3,11}... | collective-permute-start | bytes 786440 | tf_op jit(solution)/shard_map/ppermute | solution.py:58
  38.0 16.3 %collective-permute-start.4 = (f32[64,1024]{1,0:T(8,128)S(1)}, f32[64,1024]{1,0:T(8,128)S(1)}, u32[]{:S(2)}, u32[]{:S(2)}) collective-permute-start(f32[64,1024]{1,0:T(8,128)S(1)} %fusion.24), channel_id=1, source_target_pairs={{0,4},{2,6},{4,0},{6,2},{8,12},{10,14},{12,8},{14,10},{1,5},{3,7},... | collective-permute-start | bytes 786440 | tf_op jit(solution)/shard_map/ppermute | solution.py:58
  41.1 16.4 %collective-permute-start.7 = (f32[64,1024]{1,0:T(8,128)S(1)}, f32[64,1024]{1,0:T(8,128)S(1)}, u32[]{:S(2)}, u32[]{:S(2)}) collective-permute-start(f32[64,1024]{1,0:T(8,128)S(1)} %fusion.23), channel_id=1, source_target_pairs={{0,2},{2,0},{4,6},{6,4},{8,10},{10,8},{12,14},{14,12},{1,3},{3,1},... | collective-permute-start | bytes 786440 | tf_op jit(solution)/shard_map/ppermute | solution.py:58
  50.0 43.1 %copy-start.1 = (f32[1,512,256]{1,2,0:T(8,128)S(1)}, f32[1,512,256]{1,2,0:T(8,128)}, u32[]{:S(2)}) copy-start(f32[1,512,256]{1,2,0:T(8,128)} %copy.14) | copy-start | bytes 1572868
  50.1 7.7 %collective-permute-start.10 = (f32[64,1024]{1,0:T(8,128)S(1)}, f32[64,1024]{1,0:T(8,128)S(1)}, u32[]{:S(2)}, u32[]{:S(2)}) collective-permute-start(f32[64,1024]{1,0:T(8,128)S(1)} %fusion.22), channel_id=1, source_target_pairs={{0,2},{2,0},{4,6},{6,4},{8,10},{10,8},{12,14},{14,12},{1,3},{3,1},... | collective-permute-start | bytes 786440 | tf_op jit(solution)/shard_map/ppermute | solution.py:58
  52.1 8.6 %collective-permute-start.2 = (f32[64,512]{1,0:T(8,128)S(1)}, f32[64,512]{1,0:T(8,128)S(1)}, u32[]{:S(2)}, u32[]{:S(2)}) collective-permute-start(f32[64,512]{1,0:T(8,128)S(1)} %slice_select_fusion.4), channel_id=1, source_target_pairs={{0,4},{2,6},{4,0},{6,2},{8,12},{10,14},{12,8},{14,10},{1,5},{3,7},... | collective-permute-start | bytes 393224 | tf_op jit(solution)/shard_map/ppermute | solution.py:58
  54.4 14.3 %collective-permute-start.5 = (f32[64,512]{1,0:T(8,128)S(1)}, f32[64,512]{1,0:T(8,128)S(1)}, u32[]{:S(2)}, u32[]{:S(2)}) collective-permute-start(f32[64,512]{1,0:T(8,128)S(1)} %slice_select_fusion.3), channel_id=1, source_target_pairs={{0,8},{2,10},{4,12},{6,14},{8,0},{10,2},{12,4},{14,6},{1,9},{3,11}... | collective-permute-start | bytes 393224 | tf_op jit(solution)/shard_map/ppermute | solution.py:58
  57.6 13.0 %collective-permute-start.8 = (f32[64,512]{1,0:T(8,128)S(1)}, f32[64,512]{1,0:T(8,128)S(1)}, u32[]{:S(2)}, u32[]{:S(2)}) collective-permute-start(f32[64,512]{1,0:T(8,128)S(1)} %slice_select_fusion.2), channel_id=1, source_target_pairs={{0,8},{2,10},{4,12},{6,14},{8,0},{10,2},{12,4},{14,6},{1,9},{3,11}... | collective-permute-start | bytes 393224 | tf_op jit(solution)/shard_map/ppermute | solution.py:58
  57.8 14.2 %collective-permute-start.11 = (f32[64,512]{1,0:T(8,128)S(1)}, f32[64,512]{1,0:T(8,128)S(1)}, u32[]{:S(2)}, u32[]{:S(2)}) collective-permute-start(f32[64,512]{1,0:T(8,128)S(1)} %slice_select_fusion.1), channel_id=1, source_target_pairs={{0,8},{2,10},{4,12},{6,14},{8,0},{10,2},{12,4},{14,6},{1,9},{3,11}... | collective-permute-start | bytes 393224 | tf_op jit(solution)/shard_map/ppermute | solution.py:58
  72.8 3.7 %collective-permute-start.12 = (f32[]{:T(128)}, f32[]{:T(128)}, u32[]{:S(2)}, u32[]{:S(2)}) collective-permute-start(f32[]{:T(128)} %multiply_reduce_fusion), channel_id=1, source_target_pairs={{0,1},{1,0},{2,3},{3,2},{4,5},{5,4},{6,7},{7,6},{8,9},{9,8},{10,11... | collective-permute-start | bytes 20 | tf_op jit(solution)/shard_map/ppermute | solution.py:33
  77.7 1.2 collective-permute-start.13
  79.5 4.5 %collective-permute-start.14 = (f32[]{:T(128)}, f32[]{:T(128)}, u32[]{:S(2)}, u32[]{:S(2)}) collective-permute-start(f32[]{:T(128)} %add.79), channel_id=1, source_target_pairs={{0,8},{2,10},{4,12},{6,14},{8,0},{10,2},{12,4},{14,6},{1,9},{3,11}... | collective-permute-start | bytes 20 | tf_op jit(solution)/shard_map/ppermute | solution.py:33
  84.7 3.6 %collective-permute-start.15 = (f32[]{:T(128)}, f32[]{:T(128)}, u32[]{:S(2)}, u32[]{:S(2)}) collective-permute-start(f32[]{:T(128)} %add.80), channel_id=1, source_target_pairs={{0,4},{2,6},{4,0},{6,2},{8,12},{10,14},{12,8},{14,10},{1,5},{3,7},... | collective-permute-start | bytes 20 | tf_op jit(solution)/shard_map/ppermute | solution.py:33
  88.9 3.6 %collective-permute-start.16 = (f32[]{:T(128)}, f32[]{:T(128)}, u32[]{:S(2)}, u32[]{:S(2)}) collective-permute-start(f32[]{:T(128)} %add.81), channel_id=1, source_target_pairs={{0,2},{2,0},{4,6},{6,4},{8,10},{10,8},{12,14},{14,12},{1,3},{3,1},... | collective-permute-start | bytes 20 | tf_op jit(solution)/shard_map/ppermute | solution.py:33
  93.7 7.4 %collective-permute-start.17 = (bf16[512,128]{0,1:T(8,128)(2,1)S(1)}, bf16[512,128]{0,1:T(8,128)(2,1)S(1)}, u32[]{:S(2)}, u32[]{:S(2)}) collective-permute-start(bf16[512,128]{0,1:T(8,128)(2,1)S(1)} %get-tuple-element.55), channel_id=1, source_target_pairs={{0,8},{2,10},{4,12},{6,14},{8,0},{10,2},{12,4},{14,6},{1,9},{3,11}... | collective-permute-start | bytes 393224 | tf_op jit(solution)/shard_map/ppermute | solution.py:72
  95.7 5.4 %collective-permute-start.20 = (bf16[512,128]{0,1:T(8,128)(2,1)S(1)}, bf16[512,128]{0,1:T(8,128)(2,1)S(1)}, u32[]{:S(2)}, u32[]{:S(2)}) collective-permute-start(bf16[512,128]{0,1:T(8,128)(2,1)S(1)} %get-tuple-element.56), channel_id=1, source_target_pairs={{0,2},{2,0},{4,6},{6,4},{8,10},{10,8},{12,14},{14,12},{1,3},{3,1},... | collective-permute-start | bytes 393224 | tf_op jit(solution)/shard_map/ppermute | solution.py:72
  101.2 9.9 %collective-permute-start.18 = (bf16[2,512,128]{1,2,0:T(8,128)(2,1)S(1)}, bf16[2,512,128]{1,2,0:T(8,128)(2,1)S(1)}, u32[]{:S(2)}, u32[]{:S(2)}) collective-permute-start(bf16[2,512,128]{1,2,0:T(8,128)(2,1)S(1)} %pad_maximum_fusion.16), channel_id=1, source_target_pairs={{0,4},{2,6},{4,0},{6,2},{8,12},{10,14},{12,8},{14,10},{1,5},{3,7},... | collective-permute-start | bytes 786440 | tf_op jit(solution)/shard_map/ppermute | solution.py:72
  102.9 10.6 %collective-permute-start.21 = (bf16[2,512,128]{1,2,0:T(8,128)(2,1)S(1)}, bf16[2,512,128]{1,2,0:T(8,128)(2,1)S(1)}, u32[]{:S(2)}, u32[]{:S(2)}) collective-permute-start(bf16[2,512,128]{1,2,0:T(8,128)(2,1)S(1)} %pad_maximum_fusion.17), channel_id=1, source_target_pairs={{0,8},{2,10},{4,12},{6,14},{8,0},{10,2},{12,4},{14,6},{1,9},{3,11}... | collective-permute-start | bytes 786440 | tf_op jit(solution)/shard_map/ppermute | solution.py:72
  111.2 10.5 %collective-permute-start.19 = (bf16[2,2,512,128]{2,3,1,0:T(8,128)(2,1)S(1)}, bf16[2,2,512,128]{2,3,1,0:T(8,128)(2,1)S(1)}, u32[]{:S(2)}, u32[]{:S(2)}) collective-permute-start(bf16[2,2,512,128]{2,3,1,0:T(8,128)(2,1)S(1)} %pad_maximum_fusion.8), channel_id=1, source_target_pairs={{0,2},{2,0},{4,6},{6,4},{8,10},{10,8},{12,14},{14,12},{1,3},{3,1},... | collective-permute-start | bytes 1572872 | tf_op jit(solution)/shard_map/ppermute | solution.py:72
  114.4 10.3 %collective-permute-start.22 = (bf16[2,2,512,128]{2,3,1,0:T(8,128)(2,1)}, bf16[2,2,512,128]{2,3,1,0:T(8,128)(2,1)S(1)}, u32[]{:S(2)}, u32[]{:S(2)}) collective-permute-start(bf16[2,2,512,128]{2,3,1,0:T(8,128)(2,1)} %pad_maximum_fusion.9), channel_id=1, source_target_pairs={{0,4},{2,6},{4,0},{6,2},{8,12},{10,14},{12,8},{14,10},{1,5},{3,7},... | collective-permute-start | bytes 1572872 | tf_op jit(solution)/shard_map/ppermute | solution.py:72
  (8 other events, 36.9 us)

commit v25 on v24

--- a/solution.py
+++ b/solution.py
@@ -88,7 +88,7 @@
     width = cols // parts
     return jnp.concatenate(
         [
-            halving_scatter(partial_t[k * width:(k + 1) * width], axis, orders[(2, 0, 1, 1)[k % 4]])
+            halving_scatter(partial_t[k * width:(k + 1) * width], axis, orders[(2, 1, 1, 0)[k % 4]])
             for k in range(parts)
         ],
         axis=0,

time: 128 us -> 127 us (level)
  starting transfers between devices: 38.5 us -> 34.7 us
  waiting for transfers between devices: 53.9 us -> 56.2 us
    ppermute x12, starting transfers between devices: 20.1 us -> 15.2 us  [halving_scatter(): blocks = keep + lax.ppermute(send, axis, pairs)]
    ppermute x12, waiting for transfers between devices: 26.9 us -> 30 us  [halving_scatter(): blocks = keep + lax.ppermute(send, axis, pairs)]
    ppermute x6, waiting for transfers between devices: 19.9 us -> 18 us  [doubling_gather(): other = lax.ppermute(current, axis, pairs)]
    ppermute x6, starting transfers between devices: 9.15 us -> 10.7 us  [doubling_gather(): other = lax.ppermute(current, axis, pairs)]
    unnamed x37 -> x45, local copies, waits for them, and re-layouts: 5.5 us -> 6.56 us
  transfers between devices with their start and end apart: 23 -> 23, of which waited for: 17 -> 17; matrix products, arithmetic and copies ran while one was open for 12% -> 13% of each run, Pallas kernels for 0% -> 0%
where the time goes in v25:
time: 127 us
  waiting for transfers between devices  56.2 us (44%)
  starting transfers between devices  34.7 us (27%)
  other arithmetic  14.5 us (11%)
  local copies, waits for them, and re-layouts  9.86 us (8%)
  matrix products  6.18 us (5%)
  between operations  5.09 us (4%)
    ppermute x12, waiting for transfers between devices, halving_scatter(): blocks = keep + lax.ppermute(send, axis, pairs)  30 us
    ppermute x6, waiting for transfers between devices, doubling_gather(): other = lax.ppermute(current, axis, pairs)  18 us
    ppermute x12, starting transfers between devices, halving_scatter(): blocks = keep + lax.ppermute(send, axis, pairs)  15.2 us
    ppermute x6, starting transfers between devices, doubling_gather(): other = lax.ppermute(current, axis, pairs)  10.7 us
    ppermute x5, starting transfers between devices, butterfly_sum(): value = value + lax.ppermute(value, axis, pairs)  8.87 us
    ppermute x5, waiting for transfers between devices, butterfly_sum(): value = value + lax.ppermute(value, axis, pairs)  8.17 us
    unnamed x45, local copies, waits for them, and re-layouts  6.56 us
    dot_general x1, matrix products, slot_term(): lax.dot_general(weighted, columns, (((0,), (0,)), ((), ())), preferred_el...  6.18 us
  transfers between devices with their start and end apart: 23, of which 17 were waited for; matrix products, arithmetic and copies ran while one was open for 13% of the time, Pallas kernels for 0%

profile of v25, /device:TPU:0, one launch (start us, length us, event | category | flops | bytes accessed | tf_op | source)
XLA Modules:
  0.0 126.6 jit_solution(14079602656502079891)
XLA Ops:
  0.7 6.2 %fusion.2 = f32[256,4096]{1,0:T(8,128)S(1)} fusion(bf16[1,8,128,4096]{3,2,1,0:T(8,128)(2,1)} %param.6, bf16[1,8,128,256]{3,2,1,0:T(8,128)(2,1)} %param.7, pred[8]{0:T(512)(128)(4,1)S(1)} %compare_bitcast_fusion), kind=kOutput, calls=%fused_computation.2 | convolution fusion | flops 2147745792 | bytes 13107208 | tf_op jit(solution)/shard_map/dot_general | solution.py:19
  6.9 1.9 %copy-done = f32[256,4096]{1,0:T(8,128)} copy-done((f32[256,4096]{1,0:T(8,128)}, f32[256,4096]{1,0:T(8,128)S(1)}, u32[]{:S(2)}) %copy-start) | copy-done | bytes 4194328
  10.2 2.9 %collective-permute-start = (f32[64,2048]{1,0:T(8,128)}, f32[64,2048]{1,0:T(8,128)}, u32[]{:S(2)}, u32[]{:S(2)}) collective-permute-start(f32[64,2048]{1,0:T(8,128)} %fusion.19), channel_id=1, source_target_pairs={{0,2},{2,0},{4,6},{6,4},{8,10},{10,8},{12,14},{14,12},{1,3},{3,1},... | collective-permute-start | bytes 1572872 | tf_op jit(solution)/shard_map/ppermute | solution.py:58
  13.2 1.6 %fusion.27 = (f32[64,1024]{1,0:T(8,128)S(1)}, f32[64,1024]{1,0:T(8,128)S(1)}, f32[64,1024]{1,0:T(8,128)S(1)}, f32[64,1024]{1,0:T(8,128)S(1)}, f32[64,1024]{1,0:T...) fusion(f32[256,4096]{1,0:T(8,128)} %copy-done), kind=kLoop, calls=%fused_computation.80 | loop fusion | bytes 4194304 | tf_op jit(solution)/shard_map/slice | solution.py:54
  15.7 1.6 %collective-permute-start.3 = (f32[64,2048]{1,0:T(8,128)}, f32[64,2048]{1,0:T(8,128)}, u32[]{:S(2)}, u32[]{:S(2)}) collective-permute-start(f32[64,2048]{1,0:T(8,128)} %fusion.17), channel_id=1, source_target_pairs={{0,4},{2,6},{4,0},{6,2},{8,12},{10,14},{12,8},{14,10},{1,5},{3,7},... | collective-permute-start | bytes 1572872 | tf_op jit(solution)/shard_map/ppermute | solution.py:58
  23.4 2.0 %copy.14 = f32[1,512,256]{1,2,0:T(8,128)} copy(f32[1,512,256]{2,1,0:T(8,128)} %param.9) | data formatting | bytes 1048576 | tf_op args[3]
  26.2 1.4 %select_add_fusion.3 = f32[64,2048]{1,0:T(8,128)S(1)} fusion(f32[64,2048]{1,0:T(8,128)} %collective-permute-done, f32[64,512]{1,0:T(8,128)} %copy-done.13, f32[64,512]{1,0:T(8,128)} %copy-done.14, f32[64,512]{1,0:T(8,128)} %copy-done.15, f32[64,512]{1,0:T(8,128)} %copy-done.16, f32[64,512]{1,0:T(8,128)} %copy-done.17, f32[64,512]{1,0:T(8,128)} %copy-done.18, ...), kind=kLoop, calls=%fused_computation.35 | loop fusion | flops 1048576 | bytes 2097153 | tf_op jit(solution)/shard_map/add | solution.py:58
  27.7 3.2 %collective-permute-start.1 = (f32[64,1024]{1,0:T(8,128)S(1)}, f32[64,1024]{1,0:T(8,128)S(1)}, u32[]{:S(2)}, u32[]{:S(2)}) collective-permute-start(f32[64,1024]{1,0:T(8,128)S(1)} %slice_select_fusion), channel_id=1, source_target_pairs={{0,8},{2,10},{4,12},{6,14},{8,0},{10,2},{12,4},{14,6},{1,9},{3,11}... | collective-permute-start | bytes 786440 | tf_op jit(solution)/shard_map/ppermute | solution.py:58
  31.0 5.5 %collective-permute-done.3 = f32[64,2048]{1,0:T(8,128)} collective-permute-done((f32[64,2048]{1,0:T(8,128)}, f32[64,2048]{1,0:T(8,128)}, u32[]{:S(2)}, u32[]{:S(2)}) %collective-permute-start.3) | collective-permute-done | bytes 524320 | tf_op jit(solution)/shard_map/ppermute | solution.py:58
  37.8 8.5 %collective-permute-done.6 = f32[64,2048]{1,0:T(8,128)} collective-permute-done((f32[64,2048]{1,0:T(8,128)}, f32[64,2048]{1,0:T(8,128)}, u32[]{:S(2)}, u32[]{:S(2)}) %collective-permute-start.6) | collective-permute-done | bytes 524320 | tf_op jit(solution)/shard_map/ppermute | solution.py:58
  49.4 2.1 %collective-permute-start.2 = (f32[64,512]{1,0:T(8,128)S(1)}, f32[64,512]{1,0:T(8,128)S(1)}, u32[]{:S(2)}, u32[]{:S(2)}) collective-permute-start(f32[64,512]{1,0:T(8,128)S(1)} %slice_select_fusion.4), channel_id=1, source_target_pairs={{0,4},{2,6},{4,0},{6,2},{8,12},{10,14},{12,8},{14,10},{1,5},{3,7},... | collective-permute-start | bytes 393224 | tf_op jit(solution)/shard_map/ppermute | solution.py:58
  51.5 2.4 %collective-permute-start.5 = (f32[64,512]{1,0:T(8,128)S(1)}, f32[64,512]{1,0:T(8,128)S(1)}, u32[]{:S(2)}, u32[]{:S(2)}) collective-permute-start(f32[64,512]{1,0:T(8,128)S(1)} %slice_select_fusion.3), channel_id=1, source_target_pairs={{0,8},{2,10},{4,12},{6,14},{8,0},{10,2},{12,4},{14,6},{1,9},{3,11}... | collective-permute-start | bytes 393224 | tf_op jit(solution)/shard_map/ppermute | solution.py:58
  54.5 1.8 %collective-permute-start.8 = (f32[64,512]{1,0:T(8,128)S(1)}, f32[64,512]{1,0:T(8,128)S(1)}, u32[]{:S(2)}, u32[]{:S(2)}) collective-permute-start(f32[64,512]{1,0:T(8,128)S(1)} %slice_select_fusion.2), channel_id=1, source_target_pairs={{0,8},{2,10},{4,12},{6,14},{8,0},{10,2},{12,4},{14,6},{1,9},{3,11}... | collective-permute-start | bytes 393224 | tf_op jit(solution)/shard_map/ppermute | solution.py:58
  56.2 7.7 %collective-permute-done.10 = f32[64,1024]{1,0:T(8,128)S(1)} collective-permute-done((f32[64,1024]{1,0:T(8,128)S(1)}, f32[64,1024]{1,0:T(8,128)S(1)}, u32[]{:S(2)}, u32[]{:S(2)}) %collective-permute-start.10) | collective-permute-done | bytes 262176 | tf_op jit(solution)/shard_map/ppermute | solution.py:58
  65.4 4.4 %collective-permute-done.8 = f32[64,512]{1,0:T(8,128)S(1)} collective-permute-done((f32[64,512]{1,0:T(8,128)S(1)}, f32[64,512]{1,0:T(8,128)S(1)}, u32[]{:S(2)}, u32[]{:S(2)}) %collective-permute-start.8) | collective-permute-done | bytes 131104 | tf_op jit(solution)/shard_map/ppermute | solution.py:58
  69.9 1.4 %collective-permute-done.11 = f32[64,512]{1,0:T(8,128)S(1)} collective-permute-done((f32[64,512]{1,0:T(8,128)S(1)}, f32[64,512]{1,0:T(8,128)S(1)}, u32[]{:S(2)}, u32[]{:S(2)}) %collective-permute-start.11) | collective-permute-done | bytes 131104 | tf_op jit(solution)/shard_map/ppermute | solution.py:58
  72.1 1.5 %collective-permute-start.12 = (f32[]{:T(128)}, f32[]{:T(128)}, u32[]{:S(2)}, u32[]{:S(2)}) collective-permute-start(f32[]{:T(128)} %multiply_reduce_fusion), channel_id=1, source_target_pairs={{0,1},{1,0},{2,3},{3,2},{4,5},{5,4},{6,7},{7,6},{8,9},{9,8},{10,11... | collective-permute-start | bytes 20 | tf_op jit(solution)/shard_map/ppermute | solution.py:33
  73.6 2.2 %collective-permute-done.12 = f32[]{:T(128)} collective-permute-done((f32[]{:T(128)}, f32[]{:T(128)}, u32[]{:S(2)}, u32[]{:S(2)}) %collective-permute-start.12) | collective-permute-done | bytes 36 | tf_op jit(solution)/shard_map/ppermute | solution.py:33
  79.0 1.4 %collective-permute-start.14 = (f32[]{:T(128)}, f32[]{:T(128)}, u32[]{:S(2)}, u32[]{:S(2)}) collective-permute-start(f32[]{:T(128)} %add.79), channel_id=1, source_target_pairs={{0,8},{2,10},{4,12},{6,14},{8,0},{10,2},{12,4},{14,6},{1,9},{3,11}... | collective-permute-start | bytes 20 | tf_op jit(solution)/shard_map/ppermute | solution.py:33
  80.4 3.2 %collective-permute-done.14 = f32[]{:T(128)} collective-permute-done((f32[]{:T(128)}, f32[]{:T(128)}, u32[]{:S(2)}, u32[]{:S(2)}) %collective-permute-start.14) | collective-permute-done | bytes 36 | tf_op jit(solution)/shard_map/ppermute | solution.py:33
  84.3 2.4 %collective-permute-start.15 = (f32[]{:T(128)}, f32[]{:T(128)}, u32[]{:S(2)}, u32[]{:S(2)}) collective-permute-start(f32[]{:T(128)} %add.80), channel_id=1, source_target_pairs={{0,4},{2,6},{4,0},{6,2},{8,12},{10,14},{12,8},{14,10},{1,5},{3,7},... | collective-permute-start | bytes 20 | tf_op jit(solution)/shard_map/ppermute | solution.py:33
  86.6 1.3 %collective-permute-done.15 = f32[]{:T(128)} collective-permute-done((f32[]{:T(128)}, f32[]{:T(128)}, u32[]{:S(2)}, u32[]{:S(2)}) %collective-permute-start.15) | collective-permute-done | bytes 36 | tf_op jit(solution)/shard_map/ppermute | solution.py:33
  88.6 2.6 %collective-permute-start.16 = (f32[]{:T(128)}, f32[]{:T(128)}, u32[]{:S(2)}, u32[]{:S(2)}) collective-permute-start(f32[]{:T(128)} %add.81), channel_id=1, source_target_pairs={{0,2},{2,0},{4,6},{6,4},{8,10},{10,8},{12,14},{14,12},{1,3},{3,1},... | collective-permute-start | bytes 20 | tf_op jit(solution)/shard_map/ppermute | solution.py:33
  93.5 2.0 %collective-permute-start.17 = (bf16[512,128]{0,1:T(8,128)(2,1)S(1)}, bf16[512,128]{0,1:T(8,128)(2,1)S(1)}, u32[]{:S(2)}, u32[]{:S(2)}) collective-permute-start(bf16[512,128]{0,1:T(8,128)(2,1)S(1)} %get-tuple-element.55), channel_id=1, source_target_pairs={{0,8},{2,10},{4,12},{6,14},{8,0},{10,2},{12,4},{14,6},{1,9},{3,11}... | collective-permute-start | bytes 393224 | tf_op jit(solution)/shard_map/ppermute | solution.py:72
  96.2 4.8 %collective-permute-done.17 = bf16[512,128]{0,1:T(8,128)(2,1)S(1)} collective-permute-done((bf16[512,128]{0,1:T(8,128)(2,1)S(1)}, bf16[512,128]{0,1:T(8,128)(2,1)S(1)}, u32[]{:S(2)}, u32[]{:S(2)}) %collective-permute-start.17) | collective-permute-done | bytes 131104 | tf_op jit(solution)/shard_map/ppermute | solution.py:72
  101.0 1.6 %collective-permute-start.18 = (bf16[2,512,128]{1,2,0:T(8,128)(2,1)S(1)}, bf16[2,512,128]{1,2,0:T(8,128)(2,1)S(1)}, u32[]{:S(2)}, u32[]{:S(2)}) collective-permute-start(bf16[2,512,128]{1,2,0:T(8,128)(2,1)S(1)} %pad_maximum_fusion.16), channel_id=1, source_target_pairs={{0,4},{2,6},{4,0},{6,2},{8,12},{10,14},{12,8},{14,10},{1,5},{3,7},... | collective-permute-start | bytes 786440 | tf_op jit(solution)/shard_map/ppermute | solution.py:72
  102.6 2.7 %collective-permute-start.21 = (bf16[2,512,128]{1,2,0:T(8,128)(2,1)S(1)}, bf16[2,512,128]{1,2,0:T(8,128)(2,1)S(1)}, u32[]{:S(2)}, u32[]{:S(2)}) collective-permute-start(bf16[2,512,128]{1,2,0:T(8,128)(2,1)S(1)} %pad_maximum_fusion.17), channel_id=1, source_target_pairs={{0,8},{2,10},{4,12},{6,14},{8,0},{10,2},{12,4},{14,6},{1,9},{3,11}... | collective-permute-start | bytes 786440 | tf_op jit(solution)/shard_map/ppermute | solution.py:72
  105.3 4.7 %collective-permute-done.18 = bf16[2,512,128]{1,2,0:T(8,128)(2,1)S(1)} collective-permute-done((bf16[2,512,128]{1,2,0:T(8,128)(2,1)S(1)}, bf16[2,512,128]{1,2,0:T(8,128)(2,1)S(1)}, u32[]{:S(2)}, u32[]{:S(2)}) %collective-permute-start.18) | collective-permute-done | bytes 262176 | tf_op jit(solution)/shard_map/ppermute | solution.py:72
  110.1 3.8 %collective-permute-start.19 = (bf16[2,2,512,128]{2,3,1,0:T(8,128)(2,1)S(1)}, bf16[2,2,512,128]{2,3,1,0:T(8,128)(2,1)S(1)}, u32[]{:S(2)}, u32[]{:S(2)}) collective-permute-start(bf16[2,2,512,128]{2,3,1,0:T(8,128)(2,1)S(1)} %pad_maximum_fusion.8), channel_id=1, source_target_pairs={{0,2},{2,0},{4,6},{6,4},{8,10},{10,8},{12,14},{14,12},{1,3},{3,1},... | collective-permute-start | bytes 1572872 | tf_op jit(solution)/shard_map/ppermute | solution.py:72
  114.8 6.3 %collective-permute-done.19 = bf16[2,2,512,128]{2,3,1,0:T(8,128)(2,1)S(1)} collective-permute-done((bf16[2,2,512,128]{2,3,1,0:T(8,128)(2,1)S(1)}, bf16[2,2,512,128]{2,3,1,0:T(8,128)(2,1)S(1)}, u32[]{:S(2)}, u32[]{:S(2)}) %collective-permute-start.19) | collective-permute-done | bytes 524320 | tf_op jit(solution)/shard_map/ppermute | solution.py:72
  121.9 2.3 %collective-permute-done.22 = bf16[2,2,512,128]{2,3,1,0:T(8,128)(2,1)S(1)} collective-permute-done((bf16[2,2,512,128]{2,3,1,0:T(8,128)(2,1)}, bf16[2,2,512,128]{2,3,1,0:T(8,128)(2,1)S(1)}, u32[]{:S(2)}, u32[]{:S(2)}) %collective-permute-start.22) | collective-permute-done | bytes 524320 | tf_op jit(solution)/shard_map/ppermute | solution.py:72
  125.1 1.5 %maximum_bitcast_fusion = bf16[1,4096,256]{2,1,0:T(8,128)(2,1)} fusion(bf16[4096,128]{1,0:T(8,128)(2,1)S(1)} %bitcast.75, bf16[4096,128]{1,0:T(8,128)(2,1)S(1)} %bitcast.74), kind=kLoop, calls=%fused_computation.3 | loop fusion | flops 4194304 | bytes 4194304 | tf_op jit(solution)/shard_map/broadcast_in_dim | solution.py:132
  (108 shorter events, 22.6 us)
Async XLA Ops:
  9.1 11.8 %copy-start.12 = (f32[64,512]{1,0:T(8,128)}, f32[64,512]{1,0:T(8,128)S(1)}, u32[]{:S(2)}) copy-start(f32[64,512]{1,0:T(8,128)S(1)} %get-tuple-element.5) | copy-start | bytes 393220
  9.1 11.8 %copy-start.13 = (f32[64,512]{1,0:T(8,128)}, f32[64,512]{1,0:T(8,128)S(1)}, u32[]{:S(2)}) copy-start(f32[64,512]{1,0:T(8,128)S(1)} %get-tuple-element.14) | copy-start | bytes 393220
  9.1 11.8 %copy-start.14 = (f32[64,512]{1,0:T(8,128)}, f32[64,512]{1,0:T(8,128)S(1)}, u32[]{:S(2)}) copy-start(f32[64,512]{1,0:T(8,128)S(1)} %get-tuple-element.15) | copy-start | bytes 393220
  10.2 16.0 %collective-permute-start = (f32[64,2048]{1,0:T(8,128)}, f32[64,2048]{1,0:T(8,128)}, u32[]{:S(2)}, u32[]{:S(2)}) collective-permute-start(f32[64,2048]{1,0:T(8,128)} %fusion.19), channel_id=1, source_target_pairs={{0,2},{2,0},{4,6},{6,4},{8,10},{10,8},{12,14},{14,12},{1,3},{3,1},... | collective-permute-start | bytes 1572872 | tf_op jit(solution)/shard_map/ppermute | solution.py:58
  15.7 20.8 %collective-permute-start.3 = (f32[64,2048]{1,0:T(8,128)}, f32[64,2048]{1,0:T(8,128)}, u32[]{:S(2)}, u32[]{:S(2)}) collective-permute-start(f32[64,2048]{1,0:T(8,128)} %fusion.17), channel_id=1, source_target_pairs={{0,4},{2,6},{4,0},{6,2},{8,12},{10,14},{12,8},{14,10},{1,5},{3,7},... | collective-permute-start | bytes 1572872 | tf_op jit(solution)/shard_map/ppermute | solution.py:58
  18.2 28.1 %collective-permute-start.6 = (f32[64,2048]{1,0:T(8,128)}, f32[64,2048]{1,0:T(8,128)}, u32[]{:S(2)}, u32[]{:S(2)}) collective-permute-start(f32[64,2048]{1,0:T(8,128)} %fusion.16), channel_id=1, source_target_pairs={{0,4},{2,6},{4,0},{6,2},{8,12},{10,14},{12,8},{14,10},{1,5},{3,7},... | collective-permute-start | bytes 1572872 | tf_op jit(solution)/shard_map/ppermute | solution.py:58
  19.5 28.4 %collective-permute-start.9 = (f32[64,2048]{1,0:T(8,128)}, f32[64,2048]{1,0:T(8,128)}, u32[]{:S(2)}, u32[]{:S(2)}) collective-permute-start(f32[64,2048]{1,0:T(8,128)} %fusion.18), channel_id=1, source_target_pairs={{0,2},{2,0},{4,6},{6,4},{8,10},{10,8},{12,14},{14,12},{1,3},{3,1},... | collective-permute-start | bytes 1572872 | tf_op jit(solution)/shard_map/ppermute | solution.py:58
  27.6 20.3 %copy-start.3 = (f32[64,512]{1,0:T(8,128)S(1)}, f32[64,512]{1,0:T(8,128)}, u32[]{:S(2)}) copy-start(f32[64,512]{1,0:T(8,128)} %copy-done.2) | copy-start | bytes 393220
  27.7 20.3 %copy-start.5 = (f32[64,512]{1,0:T(8,128)S(1)}, f32[64,512]{1,0:T(8,128)}, u32[]{:S(2)}) copy-start(f32[64,512]{1,0:T(8,128)} %copy-done.4) | copy-start | bytes 393220
  27.7 20.3 %copy-start.7 = (f32[64,512]{1,0:T(8,128)S(1)}, f32[64,512]{1,0:T(8,128)}, u32[]{:S(2)}) copy-start(f32[64,512]{1,0:T(8,128)} %copy-done.6) | copy-start | bytes 393220
  27.7 20.3 %copy-start.9 = (f32[64,512]{1,0:T(8,128)S(1)}, f32[64,512]{1,0:T(8,128)}, u32[]{:S(2)}) copy-start(f32[64,512]{1,0:T(8,128)} %copy-done.8) | copy-start | bytes 393220
  27.7 20.3 %copy-start.11 = (f32[64,512]{1,0:T(8,128)S(1)}, f32[64,512]{1,0:T(8,128)}, u32[]{:S(2)}) copy-start(f32[64,512]{1,0:T(8,128)} %copy-done.10) | copy-start | bytes 393220
  27.7 21.6 %collective-permute-start.1 = (f32[64,1024]{1,0:T(8,128)S(1)}, f32[64,1024]{1,0:T(8,128)S(1)}, u32[]{:S(2)}, u32[]{:S(2)}) collective-permute-start(f32[64,1024]{1,0:T(8,128)S(1)} %slice_select_fusion), channel_id=1, source_target_pairs={{0,8},{2,10},{4,12},{6,14},{8,0},{10,2},{12,4},{14,6},{1,9},{3,11}... | collective-permute-start | bytes 786440 | tf_op jit(solution)/shard_map/ppermute | solution.py:58
  37.7 13.7 %collective-permute-start.4 = (f32[64,1024]{1,0:T(8,128)S(1)}, f32[64,1024]{1,0:T(8,128)S(1)}, u32[]{:S(2)}, u32[]{:S(2)}) collective-permute-start(f32[64,1024]{1,0:T(8,128)S(1)} %fusion.24), channel_id=1, source_target_pairs={{0,2},{2,0},{4,6},{6,4},{8,10},{10,8},{12,14},{14,12},{1,3},{3,1},... | collective-permute-start | bytes 786440 | tf_op jit(solution)/shard_map/ppermute | solution.py:58
  47.5 6.9 %collective-permute-start.7 = (f32[64,1024]{1,0:T(8,128)S(1)}, f32[64,1024]{1,0:T(8,128)S(1)}, u32[]{:S(2)}, u32[]{:S(2)}) collective-permute-start(f32[64,1024]{1,0:T(8,128)S(1)} %fusion.23), channel_id=1, source_target_pairs={{0,2},{2,0},{4,6},{6,4},{8,10},{10,8},{12,14},{14,12},{1,3},{3,1},... | collective-permute-start | bytes 786440 | tf_op jit(solution)/shard_map/ppermute | solution.py:58
  49.2 43.8 %copy-start.1 = (f32[1,512,256]{1,2,0:T(8,128)S(1)}, f32[1,512,256]{1,2,0:T(8,128)}, u32[]{:S(2)}) copy-start(f32[1,512,256]{1,2,0:T(8,128)} %copy.14) | copy-start | bytes 1572868
  49.2 14.7 %collective-permute-start.10 = (f32[64,1024]{1,0:T(8,128)S(1)}, f32[64,1024]{1,0:T(8,128)S(1)}, u32[]{:S(2)}, u32[]{:S(2)}) collective-permute-start(f32[64,1024]{1,0:T(8,128)S(1)} %fusion.22), channel_id=1, source_target_pairs={{0,4},{2,6},{4,0},{6,2},{8,12},{10,14},{12,8},{14,10},{1,5},{3,7},... | collective-permute-start | bytes 786440 | tf_op jit(solution)/shard_map/ppermute | solution.py:58
  49.4 16.0 %collective-permute-start.2 = (f32[64,512]{1,0:T(8,128)S(1)}, f32[64,512]{1,0:T(8,128)S(1)}, u32[]{:S(2)}, u32[]{:S(2)}) collective-permute-start(f32[64,512]{1,0:T(8,128)S(1)} %slice_select_fusion.4), channel_id=1, source_target_pairs={{0,4},{2,6},{4,0},{6,2},{8,12},{10,14},{12,8},{14,10},{1,5},{3,7},... | collective-permute-start | bytes 393224 | tf_op jit(solution)/shard_map/ppermute | solution.py:58
  51.5 13.8 %collective-permute-start.5 = (f32[64,512]{1,0:T(8,128)S(1)}, f32[64,512]{1,0:T(8,128)S(1)}, u32[]{:S(2)}, u32[]{:S(2)}) collective-permute-start(f32[64,512]{1,0:T(8,128)S(1)} %slice_select_fusion.3), channel_id=1, source_target_pairs={{0,8},{2,10},{4,12},{6,14},{8,0},{10,2},{12,4},{14,6},{1,9},{3,11}... | collective-permute-start | bytes 393224 | tf_op jit(solution)/shard_map/ppermute | solution.py:58
  54.5 15.4 %collective-permute-start.8 = (f32[64,512]{1,0:T(8,128)S(1)}, f32[64,512]{1,0:T(8,128)S(1)}, u32[]{:S(2)}, u32[]{:S(2)}) collective-permute-start(f32[64,512]{1,0:T(8,128)S(1)} %slice_select_fusion.2), channel_id=1, source_target_pairs={{0,8},{2,10},{4,12},{6,14},{8,0},{10,2},{12,4},{14,6},{1,9},{3,11}... | collective-permute-start | bytes 393224 | tf_op jit(solution)/shard_map/ppermute | solution.py:58
  64.0 7.2 %collective-permute-start.11 = (f32[64,512]{1,0:T(8,128)S(1)}, f32[64,512]{1,0:T(8,128)S(1)}, u32[]{:S(2)}, u32[]{:S(2)}) collective-permute-start(f32[64,512]{1,0:T(8,128)S(1)} %slice_select_fusion.1), channel_id=1, source_target_pairs={{0,8},{2,10},{4,12},{6,14},{8,0},{10,2},{12,4},{14,6},{1,9},{3,11}... | collective-permute-start | bytes 393224 | tf_op jit(solution)/shard_map/ppermute | solution.py:58
  72.1 3.7 %collective-permute-start.12 = (f32[]{:T(128)}, f32[]{:T(128)}, u32[]{:S(2)}, u32[]{:S(2)}) collective-permute-start(f32[]{:T(128)} %multiply_reduce_fusion), channel_id=1, source_target_pairs={{0,1},{1,0},{2,3},{3,2},{4,5},{5,4},{6,7},{7,6},{8,9},{9,8},{10,11... | collective-permute-start | bytes 20 | tf_op jit(solution)/shard_map/ppermute | solution.py:33
  77.1 1.3 %collective-permute-start.13 = (f32[]{:T(128)}, f32[]{:T(128)}, u32[]{:S(2)}, u32[]{:S(2)}) collective-permute-start(f32[]{:T(128)} %add.78), channel_id=1, source_target_pairs={{0,16},{16,0},{1,17},{17,1},{2,18},{18,2},{3,19},{19,3},{4,20},{20... | collective-permute-start | bytes 20 | tf_op jit(solution)/shard_map/ppermute | solution.py:33
  79.0 4.6 %collective-permute-start.14 = (f32[]{:T(128)}, f32[]{:T(128)}, u32[]{:S(2)}, u32[]{:S(2)}) collective-permute-start(f32[]{:T(128)} %add.79), channel_id=1, source_target_pairs={{0,8},{2,10},{4,12},{6,14},{8,0},{10,2},{12,4},{14,6},{1,9},{3,11}... | collective-permute-start | bytes 20 | tf_op jit(solution)/shard_map/ppermute | solution.py:33
  84.3 3.7 %collective-permute-start.15 = (f32[]{:T(128)}, f32[]{:T(128)}, u32[]{:S(2)}, u32[]{:S(2)}) collective-permute-start(f32[]{:T(128)} %add.80), channel_id=1, source_target_pairs={{0,4},{2,6},{4,0},{6,2},{8,12},{10,14},{12,8},{14,10},{1,5},{3,7},... | collective-permute-start | bytes 20 | tf_op jit(solution)/shard_map/ppermute | solution.py:33
  88.6 3.7 %collective-permute-start.16 = (f32[]{:T(128)}, f32[]{:T(128)}, u32[]{:S(2)}, u32[]{:S(2)}) collective-permute-start(f32[]{:T(128)} %add.81), channel_id=1, source_target_pairs={{0,2},{2,0},{4,6},{6,4},{8,10},{10,8},{12,14},{14,12},{1,3},{3,1},... | collective-permute-start | bytes 20 | tf_op jit(solution)/shard_map/ppermute | solution.py:33
  93.5 7.4 %collective-permute-start.17 = (bf16[512,128]{0,1:T(8,128)(2,1)S(1)}, bf16[512,128]{0,1:T(8,128)(2,1)S(1)}, u32[]{:S(2)}, u32[]{:S(2)}) collective-permute-start(bf16[512,128]{0,1:T(8,128)(2,1)S(1)} %get-tuple-element.55), channel_id=1, source_target_pairs={{0,8},{2,10},{4,12},{6,14},{8,0},{10,2},{12,4},{14,6},{1,9},{3,11}... | collective-permute-start | bytes 393224 | tf_op jit(solution)/shard_map/ppermute | solution.py:72
  95.5 5.5 %collective-permute-start.20 = (bf16[512,128]{0,1:T(8,128)(2,1)S(1)}, bf16[512,128]{0,1:T(8,128)(2,1)S(1)}, u32[]{:S(2)}, u32[]{:S(2)}) collective-permute-start(bf16[512,128]{0,1:T(8,128)(2,1)S(1)} %get-tuple-element.56), channel_id=1, source_target_pairs={{0,2},{2,0},{4,6},{6,4},{8,10},{10,8},{12,14},{14,12},{1,3},{3,1},... | collective-permute-start | bytes 393224 | tf_op jit(solution)/shard_map/ppermute | solution.py:72
  101.0 9.0 %collective-permute-start.18 = (bf16[2,512,128]{1,2,0:T(8,128)(2,1)S(1)}, bf16[2,512,128]{1,2,0:T(8,128)(2,1)S(1)}, u32[]{:S(2)}, u32[]{:S(2)}) collective-permute-start(bf16[2,512,128]{1,2,0:T(8,128)(2,1)S(1)} %pad_maximum_fusion.16), channel_id=1, source_target_pairs={{0,4},{2,6},{4,0},{6,2},{8,12},{10,14},{12,8},{14,10},{1,5},{3,7},... | collective-permute-start | bytes 786440 | tf_op jit(solution)/shard_map/ppermute | solution.py:72
  102.6 11.3 %collective-permute-start.21 = (bf16[2,512,128]{1,2,0:T(8,128)(2,1)S(1)}, bf16[2,512,128]{1,2,0:T(8,128)(2,1)S(1)}, u32[]{:S(2)}, u32[]{:S(2)}) collective-permute-start(bf16[2,512,128]{1,2,0:T(8,128)(2,1)S(1)} %pad_maximum_fusion.17), channel_id=1, source_target_pairs={{0,8},{2,10},{4,12},{6,14},{8,0},{10,2},{12,4},{14,6},{1,9},{3,11}... | collective-permute-start | bytes 786440 | tf_op jit(solution)/shard_map/ppermute | solution.py:72
  110.1 10.9 %collective-permute-start.19 = (bf16[2,2,512,128]{2,3,1,0:T(8,128)(2,1)S(1)}, bf16[2,2,512,128]{2,3,1,0:T(8,128)(2,1)S(1)}, u32[]{:S(2)}, u32[]{:S(2)}) collective-permute-start(bf16[2,2,512,128]{2,3,1,0:T(8,128)(2,1)S(1)} %pad_maximum_fusion.8), channel_id=1, source_target_pairs={{0,2},{2,0},{4,6},{6,4},{8,10},{10,8},{12,14},{14,12},{1,3},{3,1},... | collective-permute-start | bytes 1572872 | tf_op jit(solution)/shard_map/ppermute | solution.py:72
  114.8 9.4 %collective-permute-start.22 = (bf16[2,2,512,128]{2,3,1,0:T(8,128)(2,1)}, bf16[2,2,512,128]{2,3,1,0:T(8,128)(2,1)S(1)}, u32[]{:S(2)}, u32[]{:S(2)}) collective-permute-start(bf16[2,2,512,128]{2,3,1,0:T(8,128)(2,1)} %pad_maximum_fusion.9), channel_id=1, source_target_pairs={{0,4},{2,6},{4,0},{6,2},{8,12},{10,14},{12,8},{14,10},{1,5},{3,7},... | collective-permute-start | bytes 1572872 | tf_op jit(solution)/shard_map/ppermute | solution.py:72
  (12 other events, 76.7 us)
